TPU v7x, 32 devices: a whole 2x2x4 slice. The times are simulated.
32 devices in a mesh: light: 4 (over z), view: 4 (over x, core), across: 2 (over y).
Axes of the slice: x: 2, y: 2, z: 4, core: 2. Of those that a mesh axis runs over, the one named last changes fastest.
Arguments:
- density: float32 [64, 64, 512], P('light', 'across', 'view'), may hold values from 0 to 1
- labels: int32 [64, 64, 512], P('light', 'across', 'view'), may hold values from 0 to 15
- sunlight: float32 [3, 64, 512], P(None, 'across', 'view'), may hold values from 0.18 to 2.8
- opacity_table: float32 [16], replicated, may hold values from 0.5 to 8
- extinction_table: float32 [3, 16], replicated, may hold values from 0.02 to 4
- albedo_table: float32 [3, 16], replicated, may hold values from 0.2 to 1
Outputs:
- image: float32 [4, 64, 64], P(None, ('light', 'view'), 'across')
All inputs are finite; a program needn't handle non-finite values.
Results may differ from a plain program's by a relative error of at most 0.0003.
Values sent between devices are 32-bit elements; how exact they have to be, the bound alone decides.
No kernel may reach another device: no remote copies, remote signals or barrier semaphores. Data moves between devices by JAX's collectives and lax.ppermute only.
A program may use at most 64 MiB of HBM per device.

v0:
```python
import jax
import jax.numpy as jnp
from jax import lax
from jax.sharding import PartitionSpec as P

SLABS = 8


BLUR = 0.24
AMBIENT = 0.1
SOFTEN = 0.05


def padded_2(block, sides, width):
    for axis, dim in sides:
        count = lax.axis_size(axis)
        forward = [(i, i + 1) for i in range(count - 1)]
        backward = [(target, source) for source, target in forward]
        low = lax.ppermute(
            lax.slice_in_dim(block, block.shape[dim] - width, None, axis=dim), axis, forward
        )
        high = lax.ppermute(lax.slice_in_dim(block, 0, width, axis=dim), axis, backward)
        block = jnp.concatenate([low, block, high], axis=dim)
    return block


def from_behind(value, axis, steps):
    count = lax.axis_size(axis)
    leading, last = (max(0, -steps), min(count, count - steps))
    return lax.ppermute(value, axis, [(source, source + steps) for source in range(leading, last)])


def from_partner(block, axis, apart):
    count = lax.axis_size(axis)
    route = []
    for low in range(count):
        high = low | 1 << apart
        if high != low and high < count:
            route += [(low, high), (high, low)]
    return lax.ppermute(block, axis, route)


def shade_from(tensor):
    centre = tensor[:, 1:-1, 1:-1, 1:-1]
    smooth = (
        2.0 * centre
        + tensor[:, 2:, 1:-1, 1:-1]
        + tensor[:, :-2, 1:-1, 1:-1]
        + tensor[:, 1:-1, 2:, 1:-1]
        + tensor[:, 1:-1, :-2, 1:-1]
        + tensor[:, 1:-1, 1:-1, 2:]
        + tensor[:, 1:-1, 1:-1, :-2]
    ) * 0.125
    aligned = (
        0.64 * smooth[0]
        + 0.1296 * smooth[1]
        + 0.2304 * smooth[2]
        + 0.576 * smooth[3]
        + 0.768 * smooth[4]
        + 0.3456 * smooth[5]
    )
    trace_sum = smooth[0] + smooth[1] + smooth[2]
    return 0.25 + aligned / (trace_sum + SOFTEN)


def structure(window):
    slope_light = (window[2:, 1:-1, 1:-1] - window[:-2, 1:-1, 1:-1]) * 0.5
    slope_across = (window[1:-1, 2:, 1:-1] - window[1:-1, :-2, 1:-1]) * 0.5
    slope_view = (window[1:-1, 1:-1, 2:] - window[1:-1, 1:-1, :-2]) * 0.5
    return jnp.stack(
        [
            slope_light * slope_light,
            slope_across * slope_across,
            slope_view * slope_view,
            slope_light * slope_across,
            slope_light * slope_view,
            slope_across * slope_view,
        ]
    )


def rim_mask(position, devices, width, border):
    places = position * width - border + jnp.arange(width + 2 * border, dtype=jnp.int32)
    return ((places >= 0) & (places < devices * width)).astype(jnp.float32)


def propagate(current, depth_rim, plane_inside, brick_a, brick_v, light_step):
    starts = []
    for slab_num in range(SLABS):
        border = SLABS - slab_num
        starts.append(current[:, border : border + brick_a, border : border + brick_v])
        depth_here = depth_rim[
            :,
            slab_num,
            slab_num : slab_num + brick_a + 2 * border,
            slab_num : slab_num + brick_v + 2 * border,
        ]
        current = current * jnp.exp(-light_step * depth_here)
        centre = current[:, 1:-1, 1:-1]
        current = centre + BLUR * (
            current[:, :-2, 1:-1]
            + current[:, 2:, 1:-1]
            + current[:, 1:-1, :-2]
            + current[:, 1:-1, 2:]
            - 4.0 * centre
        )
        inner = border - 1
        current = (
            current
            * plane_inside[
                slab_num + 1 : slab_num + 1 + brick_a + 2 * inner,
                slab_num + 1 : slab_num + 1 + brick_v + 2 * inner,
            ][None]
        )
    return (current, jnp.stack(starts, axis=1))


def shards(density, labels, sunlight, opacity_table, extinction_table, albedo_table):
    brick_l, brick_a, brick_v = density.shape
    n_light = lax.axis_size("light")
    n_view = lax.axis_size("view")
    n_across = lax.axis_size("across")
    full_l = brick_l * n_light
    full_v = brick_v * n_view
    light_step = 10.0 / full_l
    view_step = 2.0 / full_v
    layer_rows = brick_l // SLABS
    light_idx = lax.axis_index("light")
    view_idx = lax.axis_index("view")
    across_idx = lax.axis_index("across")
    padded = padded_2(density, (("light", 0), ("view", 2), ("across", 1)), 2)
    inside = (
        rim_mask(light_idx, n_light, brick_l, 1)[:, None, None]
        * rim_mask(across_idx, n_across, brick_a, 1)[None, :, None]
        * rim_mask(view_idx, n_view, brick_v, 1)[None, None, :]
    )
    tensor_rim = structure(padded) * inside[None]
    shading = shade_from(tensor_rim)
    table_all = jnp.concatenate([opacity_table[None], extinction_table, albedo_table], axis=0)
    material_ids = jnp.arange(table_all.shape[1], dtype=jnp.int32)

    def lookup_row(row_labels):
        indicator = (row_labels.reshape(1, -1) == material_ids[:, None]).astype(jnp.float32)
        return jnp.dot(table_all, indicator, precision=lax.Precision.HIGHEST)

    looked = lax.map(lookup_row, labels)
    looked = looked.transpose(1, 0, 2).reshape(7, brick_l, brick_a, brick_v)
    extinct = looked[1:4] * density[None]
    extinct_slabs = extinct.reshape(3, SLABS, layer_rows, brick_a, brick_v)
    running = jnp.cumsum(extinct_slabs, axis=2) - extinct_slabs
    slab_depth = jnp.sum(extinct_slabs, axis=2)
    depth_rim = padded_2(slab_depth, (("view", 3), ("across", 2)), SLABS)
    plane_inside = (
        rim_mask(across_idx, n_across, brick_a, SLABS)[:, None]
        * rim_mask(view_idx, n_view, brick_v, SLABS)[None, :]
    )
    starts = None
    incoming = sunlight
    for section_num in range(n_light):
        current = padded_2(incoming, (("view", 2), ("across", 1)), SLABS)
        outgoing, starts = propagate(current, depth_rim, plane_inside, brick_a, brick_v, light_step)
        if section_num + 1 < n_light:
            arrived = from_behind(outgoing, "light", 1)
            incoming = jnp.where(light_idx == 0, sunlight, arrived)
    lighting = (starts[:, :, None] * jnp.exp(-light_step * running)).reshape(
        3, brick_l, brick_a, brick_v
    )
    optical = looked[0] * density * view_step
    colour = (1.0 - jnp.exp(-optical))[None] * looked[4:7] * (shading[None] * lighting + AMBIENT)
    upper = (jnp.arange(brick_v)[:, None] < jnp.arange(brick_v)[None, :]).astype(jnp.float32)
    before = jnp.dot(optical.reshape(-1, brick_v), upper, precision=lax.Precision.HIGHEST).reshape(
        brick_l, brick_a, brick_v
    )
    colour_sum = jnp.sum(colour * jnp.exp(-before)[None], axis=-1)
    transmit = jnp.exp(-jnp.sum(optical, axis=-1))
    pixels = brick_l * brick_a
    piece_len = pixels // n_view
    colour_now = colour_sum.reshape(3, n_view, piece_len)
    transmit_now = transmit.reshape(1, n_view, piece_len)
    bit_count = n_view.bit_length() - 1
    for bit_num in range(bit_count):
        kept = colour_now.shape[1]
        colour_pairs = colour_now.reshape(3, kept // 2, 2, piece_len)
        transmit_pairs = transmit_now.reshape(1, kept // 2, 2, piece_len)
        my_bit = view_idx // 2**bit_num % 2
        first_half = my_bit == 0
        keep_colour = jnp.where(first_half, colour_pairs[:, :, 0], colour_pairs[:, :, 1])
        send_colour = jnp.where(first_half, colour_pairs[:, :, 1], colour_pairs[:, :, 0])
        keep_transmit = jnp.where(first_half, transmit_pairs[:, :, 0], transmit_pairs[:, :, 1])
        send_transmit = jnp.where(first_half, transmit_pairs[:, :, 1], transmit_pairs[:, :, 0])
        got_colour, got_transmit = from_partner((send_colour, send_transmit), "view", bit_num)
        front_colour = jnp.where(first_half, keep_colour, got_colour)
        back_colour = jnp.where(first_half, got_colour, keep_colour)
        front_transmit = jnp.where(first_half, keep_transmit, got_transmit)
        colour_now = front_colour + front_transmit * back_colour
        transmit_now = keep_transmit * got_transmit
    final_colour = colour_now[:, 0]
    final_transmit = transmit_now[:, 0]
    rows_out = brick_l // n_view
    opacity = 1.0 - final_transmit.reshape(1, rows_out, brick_a)
    return jnp.concatenate([final_colour.reshape(3, rows_out, brick_a), opacity], axis=0)


def solution(mesh):
    in_specs = (
        P("light", "across", "view"),
        P("light", "across", "view"),
        P(None, "across", "view"),
        P(),
        P(),
        P(),
    )
    out_specs = P(None, ("light", "view"), "across")
    return jax.shard_map(shards, mesh=mesh, in_specs=in_specs, out_specs=out_specs, check_vma=False)
```

profile of v0, /device:TPU:16, one launch (start us, length us, event | category | flops | bytes accessed | tf_op | source)
XLA Modules:
  0.0 189.1 jit_solution(2398814531648516897)
XLA Ops:
  0.0 1.4 fusion.238
  1.4 3.5 %collective-permute-start = (f32[2,32,128]{2,1,0:T(8,128)}, f32[2,32,128]{2,1,0:T(8,128)}, u32[]{:S(2)}, u32[]{:S(2)}) collective-permute-start(f32[2,32,128]{2,1,0:T(8,128)} %get-tuple-element.87), channel_id=1, source_target_pairs={{0,8},{8,16},{16,24},{1,9},{9,17},{17,25},{2,10},{10,18},{18,26},{... | collective-permute-start | bytes 98312 | tf_op jit(solution)/shard_map/ppermute | solution.py:19
  4.9 2.4 %collective-permute-start.1 = (f32[2,32,128]{2,1,0:T(8,128)}, f32[2,32,128]{2,1,0:T(8,128)}, u32[]{:S(2)}, u32[]{:S(2)}) collective-permute-start(f32[2,32,128]{2,1,0:T(8,128)} %get-tuple-element.86), channel_id=1, source_target_pairs={{8,0},{16,8},{24,16},{9,1},{17,9},{25,17},{10,2},{18,10},{26,18},{... | collective-permute-start | bytes 98312 | tf_op jit(solution)/shard_map/ppermute | solution.py:22
  8.0 25.2 %while.11 = (s32[]{:T(128)}, f32[16,7,4096]{2,1,0:T(8,128)}, s32[16,32,128]{2,1,0:T(8,128)}, f32[7,16]{1,0:T(8,128)S(1)}, s32[]{:T(128)}) while((s32[]{:T(128)}, f32[16,7,4096]{2,1,0:T(8,128)}, s32[16,32,128]{2,1,0:T(8,128)}, f32[7,16]{1,0:T(8,128)S(1)}, s32[]{:T(128)}) %tuple.57), condition=%wide.region_1.2_spmd.clone, body=%wide.region_0.1_spmd.clone.sunk | while | flops 5570562 | bytes 181249 | solution.py:146
  8.7 0.9 fusion.250
  11.8 0.9 fusion.250
  15.0 0.9 fusion.250
  16.6 0.9 fusion.250
  21.3 0.9 fusion.250
  24.4 0.9 fusion.250
  27.6 0.9 fusion.250
  32.3 0.9 fusion.250
  33.1 3.8 %fusion.235 = (f32[3,16,4096]{2,0,1:T(4,128)}, f32[3,16,4096]{2,0,1:T(4,128)S(1)}) fusion(f32[7,16,4096]{2,0,1:T(8,128)} %bitcast.278), kind=kLoop, calls=%fused_computation.422 | loop fusion | bytes 3145728 | tf_op jit(solution)/shard_map/slice | solution.py:169
  38.0 1.0 fusion.236
  39.0 1.3 collective-permute-start.10
  40.4 4.1 %collective-permute-start.6 = (f32[3,32,8]{2,1,0:T(8,128)S(1)}, f32[3,32,8]{2,1,0:T(8,128)S(1)}, u32[]{:S(2)}, u32[]{:S(2)}) collective-permute-start(f32[3,32,8]{2,1,0:T(8,128)S(1)} %get-tuple-element.106), channel_id=1, source_target_pairs={{0,2},{2,4},{4,6},{1,3},{3,5},{5,7},{8,10},{10,12},{12,14},{9,11},... | collective-permute-start | bytes 9224 | tf_op jit(solution)/shard_map/ppermute | solution.py:19
  44.5 1.3 collective-permute-start.7
  45.8 1.8 slice.1007
  47.6 1.0 fusion.19
  48.7 1.0 fusion.5
  49.7 1.0 broadcast_multiply_fusion.1
  55.8 1.5 reshape.310
  57.3 1.5 reshape.308
  58.8 1.3 collective-permute-start.11
  60.8 4.0 %collective-permute-start.8 = (f32[3,8,144]{2,1,0:T(8,128)}, f32[3,8,144]{2,1,0:T(8,128)}, u32[]{:S(2)}, u32[]{:S(2)}) collective-permute-start(f32[3,8,144]{2,1,0:T(8,128)} %get-tuple-element.94), channel_id=1, source_target_pairs={{0,1},{2,3},{4,5},{6,7},{8,9},{10,11},{12,13},{14,15},{16,17},{18,... | collective-permute-start | bytes 41480 | tf_op jit(solution)/shard_map/ppermute | solution.py:19
  64.8 1.3 collective-permute-start.9
  66.4 5.1 %collective-permute-start.12 = (f32[3,8,8,144]{3,2,1,0:T(8,128)S(1)}, f32[3,8,8,144]{3,2,1,0:T(8,128)S(1)}, u32[]{:S(2)}, u32[]{:S(2)}) collective-permute-start(f32[3,8,8,144]{3,2,1,0:T(8,128)S(1)} %get-tuple-element.75), channel_id=1, source_target_pairs={{0,1},{2,3},{4,5},{6,7},{8,9},{10,11},{12,13},{14,15},{16,17},{18,... | collective-permute-start | bytes 331784 | tf_op jit(solution)/shard_map/ppermute | solution.py:19
  74.0 2.8 %collective-permute-start.2 = (f32[20,32,2]{2,1,0:T(8,128)S(1)}, f32[20,32,2]{2,1,0:T(8,128)S(1)}, u32[]{:S(2)}, u32[]{:S(2)}) collective-permute-start(f32[20,32,2]{2,1,0:T(8,128)S(1)} %get-tuple-element.83), channel_id=1, source_target_pairs={{0,2},{2,4},{4,6},{1,3},{3,5},{5,7},{8,10},{10,12},{12,14},{9,11},... | collective-permute-start | bytes 15368 | tf_op jit(solution)/shard_map/ppermute | solution.py:19
  76.9 1.3 collective-permute-start.3
  78.3 5.2 %collective-permute-start.30 = (f32[1,2,128]{2,1,0:T(2,128)S(1)}, f32[1,2,128]{2,1,0:T(2,128)S(1)}, u32[]{:S(2)}, u32[]{:S(2)}) collective-permute-start(f32[1,2,128]{2,1,0:T(2,128)S(1)} %bitcast.291), channel_id=1, source_target_pairs={{0,2},{2,0},{4,6},{6,4},{1,3},{3,1},{5,7},{7,5},{8,10},{10,8},{12,... | collective-permute-start | bytes 3080 | tf_op jit(solution)/shard_map/ppermute | solution.py:40
  83.6 1.3 collective-permute-start.4
  84.9 1.3 collective-permute-start.5
  86.8 1.3 collective-permute-start.13
  88.1 2.7 %collective-permute-done.5 = f32[20,2,132]{2,1,0:T(2,128)S(1)} collective-permute-done((f32[20,2,132]{2,1,0:T(2,128)S(1)}, f32[20,2,132]{2,1,0:T(2,128)S(1)}, u32[]{:S(2)}, u32[]{:S(2)}) %collective-permute-start.5) | collective-permute-done | bytes 21152 | tf_op jit(solution)/shard_map/ppermute | solution.py:22
  91.3 3.5 %collective-permute-done.13 = f32[3,8,8,144]{3,2,1,0:T(8,128)S(1)} collective-permute-done((f32[3,8,8,144]{3,2,1,0:T(8,128)S(1)}, f32[3,8,8,144]{3,2,1,0:T(8,128)S(1)}, u32[]{:S(2)}, u32[]{:S(2)}) %collective-permute-start.13) | collective-permute-done | bytes 110624 | tf_op jit(solution)/shard_map/ppermute | solution.py:22
  95.2 0.9 maximum_multiply_fusion
  99.0 4.1 %collective-permute-start.14 = (f32[3,32,128]{2,1,0:T(8,128)S(1)}, f32[3,32,128]{2,1,0:T(8,128)S(1)}, u32[]{:S(2)}, u32[]{:S(2)}) collective-permute-start(f32[3,32,128]{2,1,0:T(8,128)S(1)} %fusion.208), channel_id=1, source_target_pairs={{0,8},{8,16},{16,24},{1,9},{9,17},{17,25},{2,10},{10,18},{18,26},{... | collective-permute-start | bytes 147464 | tf_op jit(solution)/shard_map/ppermute | solution.py:30
  103.5 1.5 collective-permute-done.14
  105.0 3.7 %collective-permute-start.15 = (f32[3,32,8]{2,1,0:T(8,128)S(1)}, f32[3,32,8]{2,1,0:T(8,128)S(1)}, u32[]{:S(2)}, u32[]{:S(2)}) collective-permute-start(f32[3,32,8]{2,1,0:T(8,128)S(1)} %get-tuple-element.104), channel_id=1, source_target_pairs={{0,2},{2,4},{4,6},{1,3},{3,5},{5,7},{8,10},{10,12},{12,14},{9,11},... | collective-permute-start | bytes 9224 | tf_op jit(solution)/shard_map/ppermute | solution.py:19
  108.7 1.3 collective-permute-start.16
  110.8 2.8 %collective-permute-done.16 = f32[3,32,8]{2,1,0:T(8,128)S(1)} collective-permute-done((f32[3,32,8]{2,1,0:T(8,128)S(1)}, f32[3,32,8]{2,1,0:T(8,128)S(1)}, u32[]{:S(2)}, u32[]{:S(2)}) %collective-permute-start.16) | collective-permute-done | bytes 3104 | tf_op jit(solution)/shard_map/ppermute | solution.py:22
  113.8 1.4 collective-permute-start.17
  115.2 1.5 collective-permute-start.18
  117.0 4.0 %collective-permute-done.18 = f32[3,8,144]{2,1,0:T(8,128)S(1)} collective-permute-done((f32[3,8,144]{2,1,0:T(8,128)S(1)}, f32[3,8,144]{2,1,0:T(8,128)S(1)}, u32[]{:S(2)}, u32[]{:S(2)}) %collective-permute-start.18) | collective-permute-done | bytes 13856 | tf_op jit(solution)/shard_map/ppermute | solution.py:22
  122.8 4.1 %collective-permute-start.19 = (f32[3,32,128]{2,1,0:T(8,128)S(1)}, f32[3,32,128]{2,1,0:T(8,128)S(1)}, u32[]{:S(2)}, u32[]{:S(2)}) collective-permute-start(f32[3,32,128]{2,1,0:T(8,128)S(1)} %fusion.204), channel_id=1, source_target_pairs={{0,8},{8,16},{16,24},{1,9},{9,17},{17,25},{2,10},{10,18},{18,26},{... | collective-permute-start | bytes 147464 | tf_op jit(solution)/shard_map/ppermute | solution.py:30
  126.9 1.2 bitcast_dynamic-update-slice_fusion.2
  129.0 2.3 %collective-permute-start.20 = (f32[3,32,8]{2,1,0:T(8,128)S(1)}, f32[3,32,8]{2,1,0:T(8,128)S(1)}, u32[]{:S(2)}, u32[]{:S(2)}) collective-permute-start(f32[3,32,8]{2,1,0:T(8,128)S(1)} %get-tuple-element.102), channel_id=1, source_target_pairs={{0,2},{2,4},{4,6},{1,3},{3,5},{5,7},{8,10},{10,12},{12,14},{9,11},... | collective-permute-start | bytes 9224 | tf_op jit(solution)/shard_map/ppermute | solution.py:19
  131.3 1.3 collective-permute-start.21
  133.3 2.9 %collective-permute-done.21 = f32[3,32,8]{2,1,0:T(8,128)S(1)} collective-permute-done((f32[3,32,8]{2,1,0:T(8,128)S(1)}, f32[3,32,8]{2,1,0:T(8,128)S(1)}, u32[]{:S(2)}, u32[]{:S(2)}) %collective-permute-start.21) | collective-permute-done | bytes 3104 | tf_op jit(solution)/shard_map/ppermute | solution.py:22
  136.3 1.6 collective-permute-start.22
  137.9 1.3 collective-permute-start.23
  139.2 1.0 bitcast_dynamic-update-slice_fusion
  140.3 3.4 %collective-permute-done.23 = f32[3,8,144]{2,1,0:T(8,128)S(1)} collective-permute-done((f32[3,8,144]{2,1,0:T(8,128)S(1)}, f32[3,8,144]{2,1,0:T(8,128)S(1)}, u32[]{:S(2)}, u32[]{:S(2)}) %collective-permute-start.23) | collective-permute-done | bytes 13856 | tf_op jit(solution)/shard_map/ppermute | solution.py:22
  145.5 4.1 %collective-permute-start.24 = (f32[3,32,128]{2,1,0:T(8,128)S(1)}, f32[3,32,128]{2,1,0:T(8,128)S(1)}, u32[]{:S(2)}, u32[]{:S(2)}) collective-permute-start(f32[3,32,128]{2,1,0:T(8,128)S(1)} %fusion.200), channel_id=1, source_target_pairs={{0,8},{8,16},{16,24},{1,9},{9,17},{17,25},{2,10},{10,18},{18,26},{... | collective-permute-start | bytes 147464 | tf_op jit(solution)/shard_map/ppermute | solution.py:30
  149.6 2.4 %broadcast_multiply_fusion = f32[6,18,34,130]{3,2,1,0:T(8,128)} fusion(f32[6,18,34,130]{3,2,1,0:T(8,128)S(1)} %bitcast_dynamic-update-slice_fusion, f32[18,34,130]{2,1,0:T(8,128)S(1)} %copy-done.6), kind=kLoop, calls=%fused_computation.6 | loop fusion | flops 477360 | bytes 4137120 | tf_op jit(solution)/shard_map/mul | solution.py:137
  152.8 3.0 %collective-permute-start.25 = (f32[3,32,8]{2,1,0:T(8,128)S(1)}, f32[3,32,8]{2,1,0:T(8,128)S(1)}, u32[]{:S(2)}, u32[]{:S(2)}) collective-permute-start(f32[3,32,8]{2,1,0:T(8,128)S(1)} %get-tuple-element.100), channel_id=1, source_target_pairs={{0,2},{2,4},{4,6},{1,3},{3,5},{5,7},{8,10},{10,12},{12,14},{9,11},... | collective-permute-start | bytes 9224 | tf_op jit(solution)/shard_map/ppermute | solution.py:19
  155.7 1.3 collective-permute-start.26
  157.0 11.6 %fusion.4 = f32[6,16,32,128]{3,2,1,0:T(8,128)S(1)} fusion(f32[6,18,34,130]{3,2,1,0:T(8,128)} %broadcast_multiply_fusion), kind=kLoop, calls=%fused_computation.8 | loop fusion | flops 3145728 | bytes 12582912 | tf_op jit(solution)/shard_map/mul | solution.py:45
  168.7 2.1 %collective-permute-start.27 = (f32[3,8,144]{2,1,0:T(8,128)S(1)}, f32[3,8,144]{2,1,0:T(8,128)S(1)}, u32[]{:S(2)}, u32[]{:S(2)}) collective-permute-start(f32[3,8,144]{2,1,0:T(8,128)S(1)} %get-tuple-element.88), channel_id=1, source_target_pairs={{0,1},{2,3},{4,5},{6,7},{8,9},{10,11},{12,13},{14,15},{16,17},{18,... | collective-permute-start | bytes 41480 | tf_op jit(solution)/shard_map/ppermute | solution.py:19
  170.8 1.6 collective-permute-start.28
  172.7 4.0 %collective-permute-done.28 = f32[3,8,144]{2,1,0:T(8,128)S(1)} collective-permute-done((f32[3,8,144]{2,1,0:T(8,128)S(1)}, f32[3,8,144]{2,1,0:T(8,128)S(1)}, u32[]{:S(2)}, u32[]{:S(2)}) %collective-permute-start.28) | collective-permute-done | bytes 13856 | tf_op jit(solution)/shard_map/ppermute | solution.py:22
  181.6 3.1 %collective-permute-start.32 = (f32[1,1,128]{2,1,0:T(1,128)S(1)}, f32[1,1,128]{2,1,0:T(1,128)S(1)}, u32[]{:S(2)}, u32[]{:S(2)}) collective-permute-start(f32[1,1,128]{2,1,0:T(1,128)S(1)} %fusion.220), channel_id=1, source_target_pairs={{0,4},{4,0},{2,6},{6,2},{1,5},{5,1},{3,7},{7,3},{8,12},{12,8},{10,... | collective-permute-start | bytes 1544 | tf_op jit(solution)/shard_map/ppermute | solution.py:40
  184.8 1.1 collective-permute-start.31
  186.4 2.0 %collective-permute-done.31 = f32[3,1,128]{2,1,0:T(1,128)S(1)} collective-permute-done((f32[3,1,128]{2,1,0:T(1,128)S(1)}, f32[3,1,128]{2,1,0:T(1,128)S(1)}, u32[]{:S(2)}, u32[]{:S(2)}) %collective-permute-start.31) | collective-permute-done | bytes 1568 | tf_op jit(solution)/shard_map/ppermute | solution.py:40
  (230 shorter events, 47.0 us)
Async XLA Ops:
  1.4 70.1 %collective-permute-start = (f32[2,32,128]{2,1,0:T(8,128)}, f32[2,32,128]{2,1,0:T(8,128)}, u32[]{:S(2)}, u32[]{:S(2)}) collective-permute-start(f32[2,32,128]{2,1,0:T(8,128)} %get-tuple-element.87), channel_id=1, source_target_pairs={{0,8},{8,16},{16,24},{1,9},{9,17},{17,25},{2,10},{10,18},{18,26},{... | collective-permute-start | bytes 98312 | tf_op jit(solution)/shard_map/ppermute | solution.py:19
  4.9 68.2 %collective-permute-start.1 = (f32[2,32,128]{2,1,0:T(8,128)}, f32[2,32,128]{2,1,0:T(8,128)}, u32[]{:S(2)}, u32[]{:S(2)}) collective-permute-start(f32[2,32,128]{2,1,0:T(8,128)} %get-tuple-element.86), channel_id=1, source_target_pairs={{8,0},{16,8},{24,16},{9,1},{17,9},{25,17},{10,2},{18,10},{26,18},{... | collective-permute-start | bytes 98312 | tf_op jit(solution)/shard_map/ppermute | solution.py:22
  36.9 0.9 copy-start
  37.5 2.8 %copy-start.7 = (f32[3,32,128]{2,1,0:T(8,128)S(1)}, f32[3,32,128]{2,1,0:T(8,128)}, u32[]{:S(2)}) copy-start(f32[3,32,128]{2,1,0:T(8,128)} %param.10) | copy-start | bytes 147460
  39.0 25.8 %collective-permute-start.10 = (f32[3,8,32,8]{3,2,1,0:T(8,128)}, f32[3,8,32,8]{3,2,1,0:T(8,128)S(1)}, u32[]{:S(2)}, u32[]{:S(2)}) collective-permute-start(f32[3,8,32,8]{3,2,1,0:T(8,128)} %get-tuple-element.81), channel_id=1, source_target_pairs={{0,2},{2,4},{4,6},{1,3},{3,5},{5,7},{8,10},{10,12},{12,14},{9,11},... | collective-permute-start | bytes 73736 | tf_op jit(solution)/shard_map/ppermute | solution.py:19
  40.4 18.4 %collective-permute-start.6 = (f32[3,32,8]{2,1,0:T(8,128)S(1)}, f32[3,32,8]{2,1,0:T(8,128)S(1)}, u32[]{:S(2)}, u32[]{:S(2)}) collective-permute-start(f32[3,32,8]{2,1,0:T(8,128)S(1)} %get-tuple-element.106), channel_id=1, source_target_pairs={{0,2},{2,4},{4,6},{1,3},{3,5},{5,7},{8,10},{10,12},{12,14},{9,11},... | collective-permute-start | bytes 9224 | tf_op jit(solution)/shard_map/ppermute | solution.py:19
  44.5 15.6 %collective-permute-start.7 = (f32[3,32,8]{2,1,0:T(8,128)S(1)}, f32[3,32,8]{2,1,0:T(8,128)S(1)}, u32[]{:S(2)}, u32[]{:S(2)}) collective-permute-start(f32[3,32,8]{2,1,0:T(8,128)S(1)} %get-tuple-element.107), channel_id=1, source_target_pairs={{2,0},{4,2},{6,4},{3,1},{5,3},{7,5},{10,8},{12,10},{14,12},{11,9},... | collective-permute-start | bytes 9224 | tf_op jit(solution)/shard_map/ppermute | solution.py:22
  47.6 2.1 %copy-start.9 = (f32[1,16,4096]{2,0,1:T(1,128)}, f32[1,16,4096]{2,0,1:T(1,128)S(1)}, u32[]{:S(2)}) copy-start(f32[1,16,4096]{2,0,1:T(1,128)S(1)} %slice.1007) | copy-start | bytes 786436
  49.7 7.6 %copy-start.2 = (f32[3,16,4096]{2,0,1:T(4,128)S(1)}, f32[3,16,4096]{2,0,1:T(4,128)}, u32[]{:S(2)}) copy-start(f32[3,16,4096]{2,0,1:T(4,128)} %get-tuple-element.73) | copy-start | bytes 2359300
  57.3 1.5 copy-start.33
  57.3 15.0 %copy-start.10 = (f32[1,16,4096]{2,0,1:T(1,128)S(1)}, f32[1,16,4096]{2,0,1:T(1,128)}, u32[]{:S(2)}) copy-start(f32[1,16,4096]{2,0,1:T(1,128)} %copy-done.9) | copy-start | bytes 786436
  58.8 7.6 %copy-start.34 = (f32[3,32,8]{2,1,0:T(8,128)}, f32[3,32,8]{2,1,0:T(8,128)S(1)}, u32[]{:S(2)}) copy-start(f32[3,32,8]{2,1,0:T(8,128)S(1)} %collective-permute-done.6) | copy-start | bytes 9220
  58.8 7.3 %collective-permute-start.11 = (f32[3,8,32,8]{3,2,1,0:T(8,128)S(1)}, f32[3,8,32,8]{3,2,1,0:T(8,128)S(1)}, u32[]{:S(2)}, u32[]{:S(2)}) collective-permute-start(f32[3,8,32,8]{3,2,1,0:T(8,128)S(1)} %copy-done.33), channel_id=1, source_target_pairs={{2,0},{4,2},{6,4},{3,1},{5,3},{7,5},{10,8},{12,10},{14,12},{11,9},... | collective-permute-start | bytes 73736 | tf_op jit(solution)/shard_map/ppermute | solution.py:22
  60.1 6.3 %copy-start.36 = (f32[3,32,8]{2,1,0:T(8,128)}, f32[3,32,8]{2,1,0:T(8,128)S(1)}, u32[]{:S(2)}) copy-start(f32[3,32,8]{2,1,0:T(8,128)S(1)} %collective-permute-done.7) | copy-start | bytes 9220
  60.8 34.4 %collective-permute-start.8 = (f32[3,8,144]{2,1,0:T(8,128)}, f32[3,8,144]{2,1,0:T(8,128)}, u32[]{:S(2)}, u32[]{:S(2)}) collective-permute-start(f32[3,8,144]{2,1,0:T(8,128)} %get-tuple-element.94), channel_id=1, source_target_pairs={{0,1},{2,3},{4,5},{6,7},{8,9},{10,11},{12,13},{14,15},{16,17},{18,... | collective-permute-start | bytes 41480 | tf_op jit(solution)/shard_map/ppermute | solution.py:19
  64.8 30.4 %collective-permute-start.9 = (f32[3,8,144]{2,1,0:T(8,128)}, f32[3,8,144]{2,1,0:T(8,128)}, u32[]{:S(2)}, u32[]{:S(2)}) collective-permute-start(f32[3,8,144]{2,1,0:T(8,128)} %get-tuple-element.95), channel_id=1, source_target_pairs={{1,0},{3,2},{5,4},{7,6},{9,8},{11,10},{13,12},{15,14},{17,16},{19,... | collective-permute-start | bytes 41480 | tf_op jit(solution)/shard_map/ppermute | solution.py:22
  66.4 24.9 %collective-permute-start.12 = (f32[3,8,8,144]{3,2,1,0:T(8,128)S(1)}, f32[3,8,8,144]{3,2,1,0:T(8,128)S(1)}, u32[]{:S(2)}, u32[]{:S(2)}) collective-permute-start(f32[3,8,8,144]{3,2,1,0:T(8,128)S(1)} %get-tuple-element.75), channel_id=1, source_target_pairs={{0,1},{2,3},{4,5},{6,7},{8,9},{10,11},{12,13},{14,15},{16,17},{18,... | collective-permute-start | bytes 331784 | tf_op jit(solution)/shard_map/ppermute | solution.py:19
  74.0 4.2 %collective-permute-start.2 = (f32[20,32,2]{2,1,0:T(8,128)S(1)}, f32[20,32,2]{2,1,0:T(8,128)S(1)}, u32[]{:S(2)}, u32[]{:S(2)}) collective-permute-start(f32[20,32,2]{2,1,0:T(8,128)S(1)} %get-tuple-element.83), channel_id=1, source_target_pairs={{0,2},{2,4},{4,6},{1,3},{3,5},{5,7},{8,10},{10,12},{12,14},{9,11},... | collective-permute-start | bytes 15368 | tf_op jit(solution)/shard_map/ppermute | solution.py:19
  76.9 6.6 %collective-permute-start.3 = (f32[20,32,2]{2,1,0:T(8,128)S(1)}, f32[20,32,2]{2,1,0:T(8,128)S(1)}, u32[]{:S(2)}, u32[]{:S(2)}) collective-permute-start(f32[20,32,2]{2,1,0:T(8,128)S(1)} %get-tuple-element.84), channel_id=1, source_target_pairs={{2,0},{4,2},{6,4},{3,1},{5,3},{7,5},{10,8},{12,10},{14,12},{11,9},... | collective-permute-start | bytes 15368 | tf_op jit(solution)/shard_map/ppermute | solution.py:22
  78.3 6.7 %collective-permute-start.30 = (f32[1,2,128]{2,1,0:T(2,128)S(1)}, f32[1,2,128]{2,1,0:T(2,128)S(1)}, u32[]{:S(2)}, u32[]{:S(2)}) collective-permute-start(f32[1,2,128]{2,1,0:T(2,128)S(1)} %bitcast.291), channel_id=1, source_target_pairs={{0,2},{2,0},{4,6},{6,4},{1,3},{3,1},{5,7},{7,5},{8,10},{10,8},{12,... | collective-permute-start | bytes 3080 | tf_op jit(solution)/shard_map/ppermute | solution.py:40
  83.6 3.2 %collective-permute-start.4 = (f32[20,2,132]{2,1,0:T(2,128)S(1)}, f32[20,2,132]{2,1,0:T(2,128)S(1)}, u32[]{:S(2)}, u32[]{:S(2)}) collective-permute-start(f32[20,2,132]{2,1,0:T(2,128)S(1)} %get-tuple-element.77), channel_id=1, source_target_pairs={{0,1},{2,3},{4,5},{6,7},{8,9},{10,11},{12,13},{14,15},{16,17},{18,... | collective-permute-start | bytes 63368 | tf_op jit(solution)/shard_map/ppermute | solution.py:19
  84.9 5.9 %collective-permute-start.5 = (f32[20,2,132]{2,1,0:T(2,128)S(1)}, f32[20,2,132]{2,1,0:T(2,128)S(1)}, u32[]{:S(2)}, u32[]{:S(2)}) collective-permute-start(f32[20,2,132]{2,1,0:T(2,128)S(1)} %get-tuple-element.78), channel_id=1, source_target_pairs={{1,0},{3,2},{5,4},{7,6},{9,8},{11,10},{13,12},{15,14},{17,16},{19,... | collective-permute-start | bytes 63368 | tf_op jit(solution)/shard_map/ppermute | solution.py:22
  86.8 8.0 %collective-permute-start.13 = (f32[3,8,8,144]{3,2,1,0:T(8,128)S(1)}, f32[3,8,8,144]{3,2,1,0:T(8,128)S(1)}, u32[]{:S(2)}, u32[]{:S(2)}) collective-permute-start(f32[3,8,8,144]{3,2,1,0:T(8,128)S(1)} %get-tuple-element.76), channel_id=1, source_target_pairs={{1,0},{3,2},{5,4},{7,6},{9,8},{11,10},{13,12},{15,14},{17,16},{19,... | collective-permute-start | bytes 331784 | tf_op jit(solution)/shard_map/ppermute | solution.py:22
  91.2 4.0 %copy-start.8 = (f32[3,32,128]{2,1,0:T(8,128)S(1)}, f32[3,32,128]{2,1,0:T(8,128)}, u32[]{:S(2)}) copy-start(f32[3,32,128]{2,1,0:T(8,128)} %param.10) | copy-start | bytes 147460
  91.2 4.0 %copy-start.35 = (f32[3,32,8]{2,1,0:T(8,128)S(1)}, f32[3,32,8]{2,1,0:T(8,128)}, u32[]{:S(2)}) copy-start(f32[3,32,8]{2,1,0:T(8,128)} %copy-done.34) | copy-start | bytes 9220
  91.2 4.0 %copy-start.37 = (f32[3,32,8]{2,1,0:T(8,128)S(1)}, f32[3,32,8]{2,1,0:T(8,128)}, u32[]{:S(2)}) copy-start(f32[3,32,8]{2,1,0:T(8,128)} %copy-done.36) | copy-start | bytes 9220
  91.2 4.9 %copy-start.21 = (f32[46,142]{1,0:T(8,128)S(1)}, f32[46,142]{1,0:T(8,128)}, u32[]{:S(2)}) copy-start(f32[46,142]{1,0:T(8,128)} %slice.1037) | copy-start | bytes 78388
  91.3 5.1 %copy-start.19 = (f32[44,140]{1,0:T(8,128)S(1)}, f32[44,140]{1,0:T(8,128)}, u32[]{:S(2)}) copy-start(f32[44,140]{1,0:T(8,128)} %slice.1044) | copy-start | bytes 73924
  95.2 1.5 copy-start.17
  97.2 47.3 %copy-start.15 = (f32[3,40,136]{2,1,0:T(8,128)}, f32[3,40,136]{2,1,0:T(8,128)S(1)}, u32[]{:S(2)}) copy-start(f32[3,40,136]{2,1,0:T(8,128)S(1)} %get-tuple-element.72) | copy-start | bytes 195844
  97.7 47.0 %copy-start.13 = (f32[3,38,134]{2,1,0:T(8,128)}, f32[3,38,134]{2,1,0:T(8,128)S(1)}, u32[]{:S(2)}) copy-start(f32[3,38,134]{2,1,0:T(8,128)S(1)} %get-tuple-element.70) | copy-start | bytes 183316
  98.3 46.7 %copy-start.11 = (f32[3,36,132]{2,1,0:T(8,128)}, f32[3,36,132]{2,1,0:T(8,128)S(1)}, u32[]{:S(2)}) copy-start(f32[3,36,132]{2,1,0:T(8,128)S(1)} %get-tuple-element.68) | copy-start | bytes 171076
  99.0 6.0 %collective-permute-start.14 = (f32[3,32,128]{2,1,0:T(8,128)S(1)}, f32[3,32,128]{2,1,0:T(8,128)S(1)}, u32[]{:S(2)}, u32[]{:S(2)}) collective-permute-start(f32[3,32,128]{2,1,0:T(8,128)S(1)} %fusion.208), channel_id=1, source_target_pairs={{0,8},{8,16},{16,24},{1,9},{9,17},{17,25},{2,10},{10,18},{18,26},{... | collective-permute-start | bytes 147464 | tf_op jit(solution)/shard_map/ppermute | solution.py:30
  105.0 5.8 %collective-permute-start.15 = (f32[3,32,8]{2,1,0:T(8,128)S(1)}, f32[3,32,8]{2,1,0:T(8,128)S(1)}, u32[]{:S(2)}, u32[]{:S(2)}) collective-permute-start(f32[3,32,8]{2,1,0:T(8,128)S(1)} %get-tuple-element.104), channel_id=1, source_target_pairs={{0,2},{2,4},{4,6},{1,3},{3,5},{5,7},{8,10},{10,12},{12,14},{9,11},... | collective-permute-start | bytes 9224 | tf_op jit(solution)/shard_map/ppermute | solution.py:19
  108.7 5.0 %collective-permute-start.16 = (f32[3,32,8]{2,1,0:T(8,128)S(1)}, f32[3,32,8]{2,1,0:T(8,128)S(1)}, u32[]{:S(2)}, u32[]{:S(2)}) collective-permute-start(f32[3,32,8]{2,1,0:T(8,128)S(1)} %get-tuple-element.105), channel_id=1, source_target_pairs={{2,0},{4,2},{6,4},{3,1},{5,3},{7,5},{10,8},{12,10},{14,12},{11,9},... | collective-permute-start | bytes 9224 | tf_op jit(solution)/shard_map/ppermute | solution.py:22
  113.8 3.2 %collective-permute-start.17 = (f32[3,8,144]{2,1,0:T(8,128)S(1)}, f32[3,8,144]{2,1,0:T(8,128)S(1)}, u32[]{:S(2)}, u32[]{:S(2)}) collective-permute-start(f32[3,8,144]{2,1,0:T(8,128)S(1)} %get-tuple-element.92), channel_id=1, source_target_pairs={{0,1},{2,3},{4,5},{6,7},{8,9},{10,11},{12,13},{14,15},{16,17},{18,... | collective-permute-start | bytes 41480 | tf_op jit(solution)/shard_map/ppermute | solution.py:19
  115.2 5.7 %collective-permute-start.18 = (f32[3,8,144]{2,1,0:T(8,128)S(1)}, f32[3,8,144]{2,1,0:T(8,128)S(1)}, u32[]{:S(2)}, u32[]{:S(2)}) collective-permute-start(f32[3,8,144]{2,1,0:T(8,128)S(1)} %get-tuple-element.93), channel_id=1, source_target_pairs={{1,0},{3,2},{5,4},{7,6},{9,8},{11,10},{13,12},{15,14},{17,16},{19,... | collective-permute-start | bytes 41480 | tf_op jit(solution)/shard_map/ppermute | solution.py:22
  122.8 6.1 %collective-permute-start.19 = (f32[3,32,128]{2,1,0:T(8,128)S(1)}, f32[3,32,128]{2,1,0:T(8,128)S(1)}, u32[]{:S(2)}, u32[]{:S(2)}) collective-permute-start(f32[3,32,128]{2,1,0:T(8,128)S(1)} %fusion.204), channel_id=1, source_target_pairs={{0,8},{8,16},{16,24},{1,9},{9,17},{17,25},{2,10},{10,18},{18,26},{... | collective-permute-start | bytes 147464 | tf_op jit(solution)/shard_map/ppermute | solution.py:30
  129.0 4.3 %collective-permute-start.20 = (f32[3,32,8]{2,1,0:T(8,128)S(1)}, f32[3,32,8]{2,1,0:T(8,128)S(1)}, u32[]{:S(2)}, u32[]{:S(2)}) collective-permute-start(f32[3,32,8]{2,1,0:T(8,128)S(1)} %get-tuple-element.102), channel_id=1, source_target_pairs={{0,2},{2,4},{4,6},{1,3},{3,5},{5,7},{8,10},{10,12},{12,14},{9,11},... | collective-permute-start | bytes 9224 | tf_op jit(solution)/shard_map/ppermute | solution.py:19
  131.3 4.9 %collective-permute-start.21 = (f32[3,32,8]{2,1,0:T(8,128)S(1)}, f32[3,32,8]{2,1,0:T(8,128)S(1)}, u32[]{:S(2)}, u32[]{:S(2)}) collective-permute-start(f32[3,32,8]{2,1,0:T(8,128)S(1)} %get-tuple-element.103), channel_id=1, source_target_pairs={{2,0},{4,2},{6,4},{3,1},{5,3},{7,5},{10,8},{12,10},{14,12},{11,9},... | collective-permute-start | bytes 9224 | tf_op jit(solution)/shard_map/ppermute | solution.py:22
  136.3 4.0 %collective-permute-start.22 = (f32[3,8,144]{2,1,0:T(8,128)S(1)}, f32[3,8,144]{2,1,0:T(8,128)S(1)}, u32[]{:S(2)}, u32[]{:S(2)}) collective-permute-start(f32[3,8,144]{2,1,0:T(8,128)S(1)} %get-tuple-element.90), channel_id=1, source_target_pairs={{0,1},{2,3},{4,5},{6,7},{8,9},{10,11},{12,13},{14,15},{16,17},{18,... | collective-permute-start | bytes 41480 | tf_op jit(solution)/shard_map/ppermute | solution.py:19
  137.9 5.7 %collective-permute-start.23 = (f32[3,8,144]{2,1,0:T(8,128)S(1)}, f32[3,8,144]{2,1,0:T(8,128)S(1)}, u32[]{:S(2)}, u32[]{:S(2)}) collective-permute-start(f32[3,8,144]{2,1,0:T(8,128)S(1)} %get-tuple-element.91), channel_id=1, source_target_pairs={{1,0},{3,2},{5,4},{7,6},{9,8},{11,10},{13,12},{15,14},{17,16},{19,... | collective-permute-start | bytes 41480 | tf_op jit(solution)/shard_map/ppermute | solution.py:22
  144.8 4.8 %copy-start.6 = (f32[18,34,130]{2,1,0:T(8,128)S(1)}, f32[18,34,130]{2,1,0:T(8,128)}, u32[]{:S(2)}) copy-start(f32[18,34,130]{2,1,0:T(8,128)} %broadcast_multiply_fusion.1) | copy-start | bytes 954724
  145.5 6.5 %collective-permute-start.24 = (f32[3,32,128]{2,1,0:T(8,128)S(1)}, f32[3,32,128]{2,1,0:T(8,128)S(1)}, u32[]{:S(2)}, u32[]{:S(2)}) collective-permute-start(f32[3,32,128]{2,1,0:T(8,128)S(1)} %fusion.200), channel_id=1, source_target_pairs={{0,8},{8,16},{16,24},{1,9},{9,17},{17,25},{2,10},{10,18},{18,26},{... | collective-permute-start | bytes 147464 | tf_op jit(solution)/shard_map/ppermute | solution.py:30
  152.8 15.9 %collective-permute-start.25 = (f32[3,32,8]{2,1,0:T(8,128)S(1)}, f32[3,32,8]{2,1,0:T(8,128)S(1)}, u32[]{:S(2)}, u32[]{:S(2)}) collective-permute-start(f32[3,32,8]{2,1,0:T(8,128)S(1)} %get-tuple-element.100), channel_id=1, source_target_pairs={{0,2},{2,4},{4,6},{1,3},{3,5},{5,7},{8,10},{10,12},{12,14},{9,11},... | collective-permute-start | bytes 9224 | tf_op jit(solution)/shard_map/ppermute | solution.py:19
  155.7 12.9 %collective-permute-start.26 = (f32[3,32,8]{2,1,0:T(8,128)S(1)}, f32[3,32,8]{2,1,0:T(8,128)S(1)}, u32[]{:S(2)}, u32[]{:S(2)}) collective-permute-start(f32[3,32,8]{2,1,0:T(8,128)S(1)} %get-tuple-element.101), channel_id=1, source_target_pairs={{2,0},{4,2},{6,4},{3,1},{5,3},{7,5},{10,8},{12,10},{14,12},{11,9},... | collective-permute-start | bytes 9224 | tf_op jit(solution)/shard_map/ppermute | solution.py:22
  168.6 8.2 %copy-start.22 = (f32[46,142]{1,0:T(8,128)S(1)}, f32[46,142]{1,0:T(8,128)}, u32[]{:S(2)}) copy-start(f32[46,142]{1,0:T(8,128)} %slice.1037) | copy-start | bytes 78388
  168.7 3.9 %collective-permute-start.27 = (f32[3,8,144]{2,1,0:T(8,128)S(1)}, f32[3,8,144]{2,1,0:T(8,128)S(1)}, u32[]{:S(2)}, u32[]{:S(2)}) collective-permute-start(f32[3,8,144]{2,1,0:T(8,128)S(1)} %get-tuple-element.88), channel_id=1, source_target_pairs={{0,1},{2,3},{4,5},{6,7},{8,9},{10,11},{12,13},{14,15},{16,17},{18,... | collective-permute-start | bytes 41480 | tf_op jit(solution)/shard_map/ppermute | solution.py:19
  170.8 6.3 %copy-start.20 = (f32[44,140]{1,0:T(8,128)S(1)}, f32[44,140]{1,0:T(8,128)}, u32[]{:S(2)}) copy-start(f32[44,140]{1,0:T(8,128)} %slice.1044) | copy-start | bytes 73924
  170.8 5.9 %collective-permute-start.28 = (f32[3,8,144]{2,1,0:T(8,128)S(1)}, f32[3,8,144]{2,1,0:T(8,128)S(1)}, u32[]{:S(2)}, u32[]{:S(2)}) collective-permute-start(f32[3,8,144]{2,1,0:T(8,128)S(1)} %get-tuple-element.89), channel_id=1, source_target_pairs={{1,0},{3,2},{5,4},{7,6},{9,8},{11,10},{13,12},{15,14},{17,16},{19,... | collective-permute-start | bytes 41480 | tf_op jit(solution)/shard_map/ppermute | solution.py:22
  172.7 4.7 %copy-start.18 = (f32[42,138]{1,0:T(8,128)S(1)}, f32[42,138]{1,0:T(8,128)}, u32[]{:S(2)}) copy-start(f32[42,138]{1,0:T(8,128)} %slice.1051) | copy-start | bytes 69556
  177.4 0.9 copy-start.12
  178.0 1.0 copy-start.32
  178.5 1.3 copy-start.23
  178.5 1.3 copy-start.24
  178.7 1.1 copy-start.1
  178.7 1.3 copy-start.3
  178.8 1.5 copy-start.4
  178.8 1.7 copy-start.5
  180.5 1.1 copy-start.38
  180.5 4.2 %copy-start.39 = (f32[2,128]{1,0:T(2,128)S(1)}, f32[2,128]{1,0:T(2,128)}, u32[]{:S(2)}) copy-start(f32[2,128]{1,0:T(2,128)} %get-tuple-element.111) | copy-start | bytes 3076
  181.1 3.7 %collective-permute-start.29 = (f32[3,2,128]{2,1,0:T(2,128)S(1)}, f32[3,2,128]{2,1,0:T(2,128)S(1)}, u32[]{:S(2)}, u32[]{:S(2)}) collective-permute-start(f32[3,2,128]{2,1,0:T(2,128)S(1)} %bitcast.290), channel_id=1, source_target_pairs={{0,2},{2,0},{4,6},{6,4},{1,3},{3,1},{5,7},{7,5},{8,10},{10,8},{12,... | collective-permute-start | bytes 9224 | tf_op jit(solution)/shard_map/ppermute | solution.py:40
  181.6 4.7 %collective-permute-start.32 = (f32[1,1,128]{2,1,0:T(1,128)S(1)}, f32[1,1,128]{2,1,0:T(1,128)S(1)}, u32[]{:S(2)}, u32[]{:S(2)}) collective-permute-start(f32[1,1,128]{2,1,0:T(1,128)S(1)} %fusion.220), channel_id=1, source_target_pairs={{0,4},{4,0},{2,6},{6,2},{1,5},{5,1},{3,7},{7,3},{8,12},{12,8},{10,... | collective-permute-start | bytes 1544 | tf_op jit(solution)/shard_map/ppermute | solution.py:40
  184.8 3.6 %collective-permute-start.31 = (f32[3,1,128]{2,1,0:T(1,128)S(1)}, f32[3,1,128]{2,1,0:T(1,128)S(1)}, u32[]{:S(2)}, u32[]{:S(2)}) collective-permute-start(f32[3,1,128]{2,1,0:T(1,128)S(1)} %fusion.215), channel_id=1, source_target_pairs={{0,4},{4,0},{2,6},{6,2},{1,5},{5,1},{3,7},{7,3},{8,12},{12,8},{10,... | collective-permute-start | bytes 4616 | tf_op jit(solution)/shard_map/ppermute | solution.py:40
  (9 other events, 7.8 us)
where the time goes:
time: 193 us; the launch traced here: 189 us
  starting transfers between devices  76.8 us (40%)
  other arithmetic  35.3 us (18%)
  local copies, waits for them, and re-layouts  33.2 us (17%)
  waiting for transfers between devices  28 us (15%)
  matrix products  14.7 us (8%)
    ppermute x13, starting transfers between devices, padded_2(): lax.ppermute(lax.slice_in_dim(block, block.shape[dim] - width, None, axis...  36.3 us
    ppermute x13, waiting for transfers between devices, padded_2(): lax.ppermute(lax.slice_in_dim(block, 0, width, axis=dim), axis, backward)  23.3 us
    ppermute x13, starting transfers between devices, padded_2(): lax.ppermute(lax.slice_in_dim(block, 0, width, axis=dim), axis, backward)  18.4 us
    dot_general x16, matrix products, lookup_row(): return jnp.dot(table_all, indicator, precision=lax.Precision.HIGHEST)  13.7 us
    ppermute x3, starting transfers between devices, from_behind(): lax.ppermute(value, axis, [(source, source + steps) for source in range(l...  12.2 us
    mul x1, other arithmetic, shade_from(): (2.0 * centre + tensor[:, 2:, 1:-1, 1:-1] + tensor[:, :-2, 1:-1, 1:-1] +...  11.6 us
    eq x16, local copies, waits for them, and re-layouts, lookup_row(): row_labels.reshape(1, -1) == material_ids[:, None]  11.5 us
    ppermute x4, starting transfers between devices, from_partner(): return lax.ppermute(block, axis, route)  9.93 us
  transfers between devices with their start and end apart: 33, of which 11 were waited for; matrix products, arithmetic and copies ran while one was open for 36% of the time, Pallas kernels for 0%

commit v1 on v0

--- a/solution.py
+++ b/solution.py
@@ -137,14 +137,11 @@
     tensor_rim = structure(padded) * inside[None]
     shading = shade_from(tensor_rim)
     table_all = jnp.concatenate([opacity_table[None], extinction_table, albedo_table], axis=0)
-    material_ids = jnp.arange(table_all.shape[1], dtype=jnp.int32)
-
-    def lookup_row(row_labels):
-        indicator = (row_labels.reshape(1, -1) == material_ids[:, None]).astype(jnp.float32)
-        return jnp.dot(table_all, indicator, precision=lax.Precision.HIGHEST)
-
-    looked = lax.map(lookup_row, labels)
-    looked = looked.transpose(1, 0, 2).reshape(7, brick_l, brick_a, brick_v)
+    looked = jnp.broadcast_to(table_all[:, 0, None, None, None], (7,) + labels.shape)
+    for material in range(1, table_all.shape[1]):
+        looked = jnp.where(
+            (labels == material)[None], table_all[:, material, None, None, None], looked
+        )
     extinct = looked[1:4] * density[None]
     extinct_slabs = extinct.reshape(3, SLABS, layer_rows, brick_a, brick_v)
     running = jnp.cumsum(extinct_slabs, axis=2) - extinct_slabs

time: 193 us -> 172 us (0.89)
  local copies, waits for them, and re-layouts: 33.2 us -> 15.4 us
  other arithmetic: 35.3 us -> 51.2 us
  matrix products: 14.7 us -> 1.93 us
  waiting for transfers between devices: 28 us -> 24 us
    dot_general x16 -> x0, matrix products: 13.7 us -> none  [lookup_row(): return jnp.dot(table_all, indicator, precision=lax.Precision.HIGHEST)]
    eq x16 -> x0, local copies, waits for them, and re-layouts: 11.5 us -> none  [lookup_row(): row_labels.reshape(1, -1) == material_ids[:, None]]
    slice x5 -> x1, local copies, waits for them, and re-layouts: 9.11 us -> 0.43 us  [shards(): table_all[:, material, None, None, None]]
    ppermute x13, waiting for transfers between devices: 23.3 us -> 19.8 us  [padded_2(): lax.ppermute(lax.slice_in_dim(block, 0, width, axis=dim), axis, backward)]
    slice x6, other arithmetic: 1.37 us -> 4.66 us  [padded_2(): lax.slice_in_dim(block, block.shape[dim] - width, None, axis=dim)]
    ppermute x4, starting transfers between devices: 9.93 us -> 6.98 us  [from_partner(): return lax.ppermute(block, axis, route)]
    select_n x0 -> x1, other arithmetic: none -> 2.69 us  [shards(): jnp.where((labels == material)[None], table_all[:, material, None, None,...]
    unnamed x6, other arithmetic: 4.05 us -> 6.52 us
  transfers between devices with their start and end apart: 33 -> 33, of which waited for: 11 -> 11; matrix products, arithmetic and copies ran while one was open for 36% -> 31% of each run, Pallas kernels for 0% -> 0%
where the time goes in v1:
time: 172 us; the launch traced here: 169 us
  starting transfers between devices  75.1 us (44%)
  other arithmetic  51.2 us (30%)
  waiting for transfers between devices  24 us (14%)
  local copies, waits for them, and re-layouts  15.4 us (9%)
  matrix products  1.93 us (1%)
    ppermute x13, starting transfers between devices, padded_2(): lax.ppermute(lax.slice_in_dim(block, block.shape[dim] - width, None, axis...  38.3 us
    ppermute x13, waiting for transfers between devices, padded_2(): lax.ppermute(lax.slice_in_dim(block, 0, width, axis=dim), axis, backward)  19.8 us
    ppermute x13, starting transfers between devices, padded_2(): lax.ppermute(lax.slice_in_dim(block, 0, width, axis=dim), axis, backward)  18.2 us
    mul x1, other arithmetic, shade_from(): (2.0 * centre + tensor[:, 2:, 1:-1, 1:-1] + tensor[:, :-2, 1:-1, 1:-1] +...  11.7 us
    ppermute x3, starting transfers between devices, from_behind(): lax.ppermute(value, axis, [(source, source + steps) for source in range(l...  11.6 us
    mul x31, other arithmetic, propagate(): current = current * jnp.exp(-light_step * depth_here)  8.69 us
    ppermute x4, starting transfers between devices, from_partner(): return lax.ppermute(block, axis, route)  6.98 us
    unnamed x6, other arithmetic  6.52 us
  transfers between devices with their start and end apart: 33, of which 11 were waited for; matrix products, arithmetic and copies ran while one was open for 31% of the time, Pallas kernels for 0%

profile of v1, /device:TPU:16, one launch (start us, length us, event | category | flops | bytes accessed | tf_op | source)
XLA Modules:
  0.0 168.7 jit_solution(14870742901384553546)
XLA Ops:
  0.0 1.4 fusion.227
  1.4 3.5 %collective-permute-start = (f32[2,32,128]{2,1,0:T(8,128)}, f32[2,32,128]{2,1,0:T(8,128)}, u32[]{:S(2)}, u32[]{:S(2)}) collective-permute-start(f32[2,32,128]{2,1,0:T(8,128)} %get-tuple-element.55), channel_id=1, source_target_pairs={{0,8},{8,16},{16,24},{1,9},{9,17},{17,25},{2,10},{10,18},{18,26},{... | collective-permute-start | bytes 98312 | tf_op jit(solution)/shard_map/ppermute | solution.py:19
  4.9 2.4 %collective-permute-start.1 = (f32[2,32,128]{2,1,0:T(8,128)}, f32[2,32,128]{2,1,0:T(8,128)}, u32[]{:S(2)}, u32[]{:S(2)}) collective-permute-start(f32[2,32,128]{2,1,0:T(8,128)} %get-tuple-element.54), channel_id=1, source_target_pairs={{8,0},{16,8},{24,16},{9,1},{17,9},{25,17},{10,2},{18,10},{26,18},{... | collective-permute-start | bytes 98312 | tf_op jit(solution)/shard_map/ppermute | solution.py:22
  8.4 1.6 broadcast_compare_fusion.14
  10.0 2.7 %select_select_fusion = f32[7,16,32,128]{3,2,1,0:T(8,128)S(1)} fusion(f32[7]{0:T(128)S(1)} %get-tuple-element.6, f32[7]{0:T(128)S(1)} %get-tuple-element.7, f32[7]{0:T(128)S(1)} %get-tuple-element.8, f32[7]{0:T(128)S(1)} %get-tuple-element.9, f32[7]{0:T(128)S(1)} %get-tuple-element.10, f32[7]{0:T(128)S(1)} %get-tuple-element.11, f32[7]{0:T(128)S(1)} %get-tuple-element.12, ...), kind=kLoop, calls=%fused_computation.1 | loop fusion | flops 6881280 | bytes 2818496 | tf_op jit(solution)/shard_map/jit(_where)/select_n | solution.py:142
  12.9 1.0 fusion.225
  13.9 1.3 collective-permute-start.10
  15.9 4.1 %collective-permute-start.6 = (f32[3,32,8]{2,1,0:T(8,128)}, f32[3,32,8]{2,1,0:T(8,128)S(1)}, u32[]{:S(2)}, u32[]{:S(2)}) collective-permute-start(f32[3,32,8]{2,1,0:T(8,128)} %get-tuple-element.89), channel_id=1, source_target_pairs={{0,2},{2,4},{4,6},{1,3},{3,5},{5,7},{8,10},{10,12},{12,14},{9,11},... | collective-permute-start | bytes 9224 | tf_op jit(solution)/shard_map/ppermute | solution.py:19
  20.0 1.3 collective-permute-start.7
  21.3 1.0 fusion.235
  22.3 1.9 %fusion.1 = f32[16,32,128]{2,1,0:T(8,128)} fusion(f32[16,32,128]{2,1,0:T(8,128)} %param.6, f32[7,16,32,128]{3,2,1,0:T(8,128)S(1)} %select_select_fusion), kind=kOutput, calls=%fused_computation.12 | convolution fusion | flops 100876288 | bytes 786432 | tf_op jit(solution)/shard_map/dot_general | solution.py:168
  24.4 1.1 broadcast_multiply_fusion.1
  30.4 1.3 collective-permute-start.11
  31.7 1.4 pad_maximum_fusion.25
  33.2 4.0 %collective-permute-start.8 = (f32[3,8,144]{2,1,0:T(8,128)}, f32[3,8,144]{2,1,0:T(8,128)}, u32[]{:S(2)}, u32[]{:S(2)}) collective-permute-start(f32[3,8,144]{2,1,0:T(8,128)} %get-tuple-element.77), channel_id=1, source_target_pairs={{0,1},{2,3},{4,5},{6,7},{8,9},{10,11},{12,13},{14,15},{16,17},{18,... | collective-permute-start | bytes 41480 | tf_op jit(solution)/shard_map/ppermute | solution.py:19
  37.2 1.3 collective-permute-start.9
  38.5 1.0 pad_maximum_fusion.10
  39.5 5.1 %collective-permute-start.12 = (f32[3,8,8,144]{3,2,1,0:T(8,128)}, f32[3,8,8,144]{3,2,1,0:T(8,128)S(1)}, u32[]{:S(2)}, u32[]{:S(2)}) collective-permute-start(f32[3,8,8,144]{3,2,1,0:T(8,128)} %get-tuple-element.45), channel_id=1, source_target_pairs={{0,1},{2,3},{4,5},{6,7},{8,9},{10,11},{12,13},{14,15},{16,17},{18,... | collective-permute-start | bytes 331784 | tf_op jit(solution)/shard_map/ppermute | solution.py:19
  44.6 0.8 constant_dynamic-update-slice_fusion.2
  45.4 1.7 %exponential_subtract_fusion = (f32[16,32,128]{2,1,0:T(8,128)}, f32[16,32]{1,0:T(8,128)S(1)}, f32[20,32,128]{2,1,0:T(8,128)S(1)}) fusion(f32[16,32,128]{2,1,0:T(8,128)} %param.6, f32[7,16,32,128]{3,2,1,0:T(8,128)S(1)} %select_select_fusion, f32[20,32,128]{2,1,0:T(8,128)S(1)} %constant_dynamic-update-slice_fusion.2), kind=kLoop, calls=%fused_computation.50 | loop fusion | flops 327168 | bytes 1056768 | tf_op jit(solution)/shard_map/sub | solution.py:166
  47.8 0.9 fusion.226
  48.8 3.5 %collective-permute-start.2 = (f32[20,32,2]{2,1,0:T(8,128)}, f32[20,32,2]{2,1,0:T(8,128)}, u32[]{:S(2)}, u32[]{:S(2)}) collective-permute-start(f32[20,32,2]{2,1,0:T(8,128)} %get-tuple-element.51), channel_id=1, source_target_pairs={{0,2},{2,4},{4,6},{1,3},{3,5},{5,7},{8,10},{10,12},{12,14},{9,11},... | collective-permute-start | bytes 15368 | tf_op jit(solution)/shard_map/ppermute | solution.py:19
  52.3 1.3 collective-permute-start.3
  54.2 1.4 exp.114
  56.3 2.5 %collective-permute-start.30 = (f32[1,2,128]{2,1,0:T(2,128)S(1)}, f32[1,2,128]{2,1,0:T(2,128)S(1)}, u32[]{:S(2)}, u32[]{:S(2)}) collective-permute-start(f32[1,2,128]{2,1,0:T(2,128)S(1)} %bitcast.276), channel_id=1, source_target_pairs={{0,2},{2,0},{4,6},{6,4},{1,3},{3,1},{5,7},{7,5},{8,10},{10,8},{12,... | collective-permute-start | bytes 3080 | tf_op jit(solution)/shard_map/ppermute | solution.py:40
  58.8 1.2 pad_maximum_fusion.13
  60.1 1.3 collective-permute-start.4
  61.4 1.3 collective-permute-start.5
  63.2 1.3 collective-permute-start.13
  64.5 2.7 %collective-permute-done.5 = f32[20,2,132]{2,1,0:T(2,128)S(1)} collective-permute-done((f32[20,2,132]{2,1,0:T(2,128)S(1)}, f32[20,2,132]{2,1,0:T(2,128)S(1)}, u32[]{:S(2)}, u32[]{:S(2)}) %collective-permute-start.5) | collective-permute-done | bytes 21152 | tf_op jit(solution)/shard_map/ppermute | solution.py:22
  67.3 1.5 pad_maximum_fusion.1
  68.8 2.7 %collective-permute-done.13 = f32[3,8,8,144]{3,2,1,0:T(8,128)S(1)} collective-permute-done((f32[3,8,8,144]{3,2,1,0:T(8,128)}, f32[3,8,8,144]{3,2,1,0:T(8,128)S(1)}, u32[]{:S(2)}, u32[]{:S(2)}) %collective-permute-start.13) | collective-permute-done | bytes 110624 | tf_op jit(solution)/shard_map/ppermute | solution.py:22
  71.9 1.1 maximum_multiply_fusion
  75.8 4.1 %collective-permute-start.14 = (f32[3,32,128]{2,1,0:T(8,128)S(1)}, f32[3,32,128]{2,1,0:T(8,128)S(1)}, u32[]{:S(2)}, u32[]{:S(2)}) collective-permute-start(f32[3,32,128]{2,1,0:T(8,128)S(1)} %fusion.197), channel_id=1, source_target_pairs={{0,8},{8,16},{16,24},{1,9},{9,17},{17,25},{2,10},{10,18},{18,26},{... | collective-permute-start | bytes 147464 | tf_op jit(solution)/shard_map/ppermute | solution.py:30
  80.4 1.5 collective-permute-done.14
  81.9 3.3 %collective-permute-start.15 = (f32[3,32,8]{2,1,0:T(8,128)S(1)}, f32[3,32,8]{2,1,0:T(8,128)S(1)}, u32[]{:S(2)}, u32[]{:S(2)}) collective-permute-start(f32[3,32,8]{2,1,0:T(8,128)S(1)} %get-tuple-element.87), channel_id=1, source_target_pairs={{0,2},{2,4},{4,6},{1,3},{3,5},{5,7},{8,10},{10,12},{12,14},{9,11},... | collective-permute-start | bytes 9224 | tf_op jit(solution)/shard_map/ppermute | solution.py:19
  85.2 1.3 collective-permute-start.16
  86.5 2.1 %bitcast_dynamic-update-slice_fusion.4 = f32[6,18,34,130]{3,2,1,0:T(8,128)S(1)} fusion(f32[6,18,34,130]{3,2,1,0:T(8,128)S(1)} %bitcast_dynamic-update-slice_fusion.5, f32[20,32,2]{2,1,0:T(8,128)} %collective-permute-done.3, f32[20,32,128]{2,1,0:T(8,128)S(1)} %constant_dynamic-update-slice_fusion, f32[20,32,2]{2,1,0:T(8,128)} %collective-permute-done.2, ...), kind=kLoop, calls=%fused_computation.35 | loop fusion | flops 716040 | bytes 1157120
  88.6 1.6 collective-permute-done.16
  90.3 1.6 collective-permute-start.17
  91.9 1.5 collective-permute-start.18
  93.6 4.0 %collective-permute-done.18 = f32[3,8,144]{2,1,0:T(8,128)S(1)} collective-permute-done((f32[3,8,144]{2,1,0:T(8,128)S(1)}, f32[3,8,144]{2,1,0:T(8,128)S(1)}, u32[]{:S(2)}, u32[]{:S(2)}) %collective-permute-start.18) | collective-permute-done | bytes 13856 | tf_op jit(solution)/shard_map/ppermute | solution.py:22
  99.5 4.1 %collective-permute-start.19 = (f32[3,32,128]{2,1,0:T(8,128)S(1)}, f32[3,32,128]{2,1,0:T(8,128)S(1)}, u32[]{:S(2)}, u32[]{:S(2)}) collective-permute-start(f32[3,32,128]{2,1,0:T(8,128)S(1)} %fusion.193), channel_id=1, source_target_pairs={{0,8},{8,16},{16,24},{1,9},{9,17},{17,25},{2,10},{10,18},{18,26},{... | collective-permute-start | bytes 147464 | tf_op jit(solution)/shard_map/ppermute | solution.py:30
  103.5 2.5 %bitcast_dynamic-update-slice_fusion.2 = f32[6,18,34,130]{3,2,1,0:T(8,128)S(1)} fusion(f32[6,18,34,130]{3,2,1,0:T(8,128)S(1)} %bitcast_dynamic-update-slice_fusion.3, f32[20,36,132]{2,1,0:T(8,128)S(1)} %pad_maximum_fusion.1, f32[20,32,2]{2,1,0:T(8,128)} %collective-permute-done.3, f32[20,32,128]{2,1,0:T(8,128)S(1)} %constant_dynamic-update-slice_fusion, ...), kind=kLoop, calls=%fused_computation.33 | loop fusion | flops 875160 | bytes 2631680
  106.1 3.0 %collective-permute-start.20 = (f32[3,32,8]{2,1,0:T(8,128)S(1)}, f32[3,32,8]{2,1,0:T(8,128)S(1)}, u32[]{:S(2)}, u32[]{:S(2)}) collective-permute-start(f32[3,32,8]{2,1,0:T(8,128)S(1)} %get-tuple-element.85), channel_id=1, source_target_pairs={{0,2},{2,4},{4,6},{1,3},{3,5},{5,7},{8,10},{10,12},{12,14},{9,11},... | collective-permute-start | bytes 9224 | tf_op jit(solution)/shard_map/ppermute | solution.py:19
  109.1 1.3 collective-permute-start.21
  111.1 2.7 %collective-permute-done.21 = f32[3,32,8]{2,1,0:T(8,128)S(1)} collective-permute-done((f32[3,32,8]{2,1,0:T(8,128)S(1)}, f32[3,32,8]{2,1,0:T(8,128)S(1)}, u32[]{:S(2)}, u32[]{:S(2)}) %collective-permute-start.21) | collective-permute-done | bytes 3104 | tf_op jit(solution)/shard_map/ppermute | solution.py:22
  113.9 1.6 collective-permute-start.22
  115.5 1.3 collective-permute-start.23
  116.8 2.3 %bitcast_dynamic-update-slice_fusion = f32[6,18,34,130]{3,2,1,0:T(8,128)S(1)} fusion(f32[6,18,34,130]{3,2,1,0:T(8,128)S(1)} %bitcast_dynamic-update-slice_fusion.1, f32[20,36,132]{2,1,0:T(8,128)S(1)} %pad_maximum_fusion.1, f32[20,32,2]{2,1,0:T(8,128)} %collective-permute-done.3, f32[20,32,128]{2,1,0:T(8,128)S(1)} %constant_dynamic-update-slice_fusion, ...), kind=kLoop, calls=%fused_computation.31 | loop fusion | flops 875160 | bytes 2631680 | tf_op jit(solution)/shard_map/stack | solution.py:70
  119.1 2.1 %collective-permute-done.23 = f32[3,8,144]{2,1,0:T(8,128)S(1)} collective-permute-done((f32[3,8,144]{2,1,0:T(8,128)S(1)}, f32[3,8,144]{2,1,0:T(8,128)S(1)}, u32[]{:S(2)}, u32[]{:S(2)}) %collective-permute-start.23) | collective-permute-done | bytes 13856 | tf_op jit(solution)/shard_map/ppermute | solution.py:22
  123.1 3.5 %collective-permute-start.24 = (f32[3,32,128]{2,1,0:T(8,128)S(1)}, f32[3,32,128]{2,1,0:T(8,128)S(1)}, u32[]{:S(2)}, u32[]{:S(2)}) collective-permute-start(f32[3,32,128]{2,1,0:T(8,128)S(1)} %fusion.189), channel_id=1, source_target_pairs={{0,8},{8,16},{16,24},{1,9},{9,17},{17,25},{2,10},{10,18},{18,26},{... | collective-permute-start | bytes 147464 | tf_op jit(solution)/shard_map/ppermute | solution.py:30
  126.6 2.4 %broadcast_multiply_fusion = f32[6,18,34,130]{3,2,1,0:T(8,128)} fusion(f32[6,18,34,130]{3,2,1,0:T(8,128)S(1)} %bitcast_dynamic-update-slice_fusion, f32[18,34,130]{2,1,0:T(8,128)S(1)} %copy-done.5), kind=kLoop, calls=%fused_computation | loop fusion | flops 477360 | bytes 4137120 | tf_op jit(solution)/shard_map/mul | solution.py:137
  130.7 2.6 %collective-permute-start.25 = (f32[3,32,8]{2,1,0:T(8,128)}, f32[3,32,8]{2,1,0:T(8,128)S(1)}, u32[]{:S(2)}, u32[]{:S(2)}) collective-permute-start(f32[3,32,8]{2,1,0:T(8,128)} %get-tuple-element.83), channel_id=1, source_target_pairs={{0,2},{2,4},{4,6},{1,3},{3,5},{5,7},{8,10},{10,12},{12,14},{9,11},... | collective-permute-start | bytes 9224 | tf_op jit(solution)/shard_map/ppermute | solution.py:19
  133.3 1.3 collective-permute-start.26
  134.6 11.7 %fusion = f32[6,16,32,128]{3,2,1,0:T(8,128)S(1)} fusion(f32[6,18,34,130]{3,2,1,0:T(8,128)} %broadcast_multiply_fusion), kind=kLoop, calls=%fused_computation.3 | loop fusion | flops 3145728 | bytes 12582912 | tf_op jit(solution)/shard_map/mul | solution.py:45
  146.4 0.9 pad_maximum_fusion.16
  147.3 3.3 %collective-permute-start.27 = (f32[3,8,144]{2,1,0:T(8,128)S(1)}, f32[3,8,144]{2,1,0:T(8,128)S(1)}, u32[]{:S(2)}, u32[]{:S(2)}) collective-permute-start(f32[3,8,144]{2,1,0:T(8,128)S(1)} %get-tuple-element.71), channel_id=1, source_target_pairs={{0,1},{2,3},{4,5},{6,7},{8,9},{10,11},{12,13},{14,15},{16,17},{18,... | collective-permute-start | bytes 41480 | tf_op jit(solution)/shard_map/ppermute | solution.py:19
  150.6 1.5 collective-permute-start.28
  152.4 4.0 %collective-permute-done.28 = f32[3,8,144]{2,1,0:T(8,128)S(1)} collective-permute-done((f32[3,8,144]{2,1,0:T(8,128)S(1)}, f32[3,8,144]{2,1,0:T(8,128)S(1)}, u32[]{:S(2)}, u32[]{:S(2)}) %collective-permute-start.28) | collective-permute-done | bytes 13856 | tf_op jit(solution)/shard_map/ppermute | solution.py:22
  156.3 0.9 maximum_multiply_fusion.3
  161.2 3.1 %collective-permute-start.32 = (f32[1,1,128]{2,1,0:T(1,128)S(1)}, f32[1,1,128]{2,1,0:T(1,128)S(1)}, u32[]{:S(2)}, u32[]{:S(2)}) collective-permute-start(f32[1,1,128]{2,1,0:T(1,128)S(1)} %fusion.209), channel_id=1, source_target_pairs={{0,4},{4,0},{2,6},{6,2},{1,5},{5,1},{3,7},{7,3},{8,12},{12,8},{10,... | collective-permute-start | bytes 1544 | tf_op jit(solution)/shard_map/ppermute | solution.py:40
  164.3 1.1 collective-permute-start.31
  165.9 2.0 %collective-permute-done.31 = f32[3,1,128]{2,1,0:T(1,128)S(1)} collective-permute-done((f32[3,1,128]{2,1,0:T(1,128)S(1)}, f32[3,1,128]{2,1,0:T(1,128)S(1)}, u32[]{:S(2)}, u32[]{:S(2)}) %collective-permute-start.31) | collective-permute-done | bytes 1568 | tf_op jit(solution)/shard_map/ppermute | solution.py:40
  (183 shorter events, 25.1 us)
Async XLA Ops:
  1.4 43.2 %collective-permute-start = (f32[2,32,128]{2,1,0:T(8,128)}, f32[2,32,128]{2,1,0:T(8,128)}, u32[]{:S(2)}, u32[]{:S(2)}) collective-permute-start(f32[2,32,128]{2,1,0:T(8,128)} %get-tuple-element.55), channel_id=1, source_target_pairs={{0,8},{8,16},{16,24},{1,9},{9,17},{17,25},{2,10},{10,18},{18,26},{... | collective-permute-start | bytes 98312 | tf_op jit(solution)/shard_map/ppermute | solution.py:19
  4.9 42.2 %collective-permute-start.1 = (f32[2,32,128]{2,1,0:T(8,128)}, f32[2,32,128]{2,1,0:T(8,128)}, u32[]{:S(2)}, u32[]{:S(2)}) collective-permute-start(f32[2,32,128]{2,1,0:T(8,128)} %get-tuple-element.54), channel_id=1, source_target_pairs={{8,0},{16,8},{24,16},{9,1},{17,9},{25,17},{10,2},{18,10},{26,18},{... | collective-permute-start | bytes 98312 | tf_op jit(solution)/shard_map/ppermute | solution.py:22
  8.4 4.3 %copy-start.2 = (f32[16,32,128]{2,1,0:T(8,128)S(1)}, f32[16,32,128]{2,1,0:T(8,128)}, u32[]{:S(2)}) copy-start(f32[16,32,128]{2,1,0:T(8,128)} %param.6) | copy-start | bytes 786436
  12.8 2.4 %copy-start.6 = (f32[3,32,128]{2,1,0:T(8,128)S(1)}, f32[3,32,128]{2,1,0:T(8,128)}, u32[]{:S(2)}) copy-start(f32[3,32,128]{2,1,0:T(8,128)} %param.8) | copy-start | bytes 147460
  13.9 23.3 %collective-permute-start.10 = (f32[3,8,32,8]{3,2,1,0:T(8,128)}, f32[3,8,32,8]{3,2,1,0:T(8,128)S(1)}, u32[]{:S(2)}, u32[]{:S(2)}) collective-permute-start(f32[3,8,32,8]{3,2,1,0:T(8,128)} %get-tuple-element.49), channel_id=1, source_target_pairs={{0,2},{2,4},{4,6},{1,3},{3,5},{5,7},{8,10},{10,12},{12,14},{9,11},... | collective-permute-start | bytes 73736 | tf_op jit(solution)/shard_map/ppermute | solution.py:19
  15.9 14.5 %collective-permute-start.6 = (f32[3,32,8]{2,1,0:T(8,128)}, f32[3,32,8]{2,1,0:T(8,128)S(1)}, u32[]{:S(2)}, u32[]{:S(2)}) collective-permute-start(f32[3,32,8]{2,1,0:T(8,128)} %get-tuple-element.89), channel_id=1, source_target_pairs={{0,2},{2,4},{4,6},{1,3},{3,5},{5,7},{8,10},{10,12},{12,14},{9,11},... | collective-permute-start | bytes 9224 | tf_op jit(solution)/shard_map/ppermute | solution.py:19
  20.0 11.7 %collective-permute-start.7 = (f32[3,32,8]{2,1,0:T(8,128)}, f32[3,32,8]{2,1,0:T(8,128)}, u32[]{:S(2)}, u32[]{:S(2)}) collective-permute-start(f32[3,32,8]{2,1,0:T(8,128)} %get-tuple-element.90), channel_id=1, source_target_pairs={{2,0},{4,2},{6,4},{3,1},{5,3},{7,5},{10,8},{12,10},{14,12},{11,9},... | collective-permute-start | bytes 9224 | tf_op jit(solution)/shard_map/ppermute | solution.py:22
  30.4 9.0 %copy-start.30 = (f32[3,32,8]{2,1,0:T(8,128)}, f32[3,32,8]{2,1,0:T(8,128)S(1)}, u32[]{:S(2)}) copy-start(f32[3,32,8]{2,1,0:T(8,128)S(1)} %collective-permute-done.6) | copy-start | bytes 9220
  30.4 8.0 %collective-permute-start.11 = (f32[3,8,32,8]{3,2,1,0:T(8,128)}, f32[3,8,32,8]{3,2,1,0:T(8,128)S(1)}, u32[]{:S(2)}, u32[]{:S(2)}) collective-permute-start(f32[3,8,32,8]{3,2,1,0:T(8,128)} %get-tuple-element.50), channel_id=1, source_target_pairs={{2,0},{4,2},{6,4},{3,1},{5,3},{7,5},{10,8},{12,10},{14,12},{11,9},... | collective-permute-start | bytes 73736 | tf_op jit(solution)/shard_map/ppermute | solution.py:22
  33.2 38.7 %collective-permute-start.8 = (f32[3,8,144]{2,1,0:T(8,128)}, f32[3,8,144]{2,1,0:T(8,128)}, u32[]{:S(2)}, u32[]{:S(2)}) collective-permute-start(f32[3,8,144]{2,1,0:T(8,128)} %get-tuple-element.77), channel_id=1, source_target_pairs={{0,1},{2,3},{4,5},{6,7},{8,9},{10,11},{12,13},{14,15},{16,17},{18,... | collective-permute-start | bytes 41480 | tf_op jit(solution)/shard_map/ppermute | solution.py:19
  37.2 34.7 %collective-permute-start.9 = (f32[3,8,144]{2,1,0:T(8,128)}, f32[3,8,144]{2,1,0:T(8,128)}, u32[]{:S(2)}, u32[]{:S(2)}) collective-permute-start(f32[3,8,144]{2,1,0:T(8,128)} %get-tuple-element.78), channel_id=1, source_target_pairs={{1,0},{3,2},{5,4},{7,6},{9,8},{11,10},{13,12},{15,14},{17,16},{19,... | collective-permute-start | bytes 41480 | tf_op jit(solution)/shard_map/ppermute | solution.py:22
  39.5 29.3 %collective-permute-start.12 = (f32[3,8,8,144]{3,2,1,0:T(8,128)}, f32[3,8,8,144]{3,2,1,0:T(8,128)S(1)}, u32[]{:S(2)}, u32[]{:S(2)}) collective-permute-start(f32[3,8,8,144]{3,2,1,0:T(8,128)} %get-tuple-element.45), channel_id=1, source_target_pairs={{0,1},{2,3},{4,5},{6,7},{8,9},{10,11},{12,13},{14,15},{16,17},{18,... | collective-permute-start | bytes 331784 | tf_op jit(solution)/shard_map/ppermute | solution.py:19
  48.8 7.5 %collective-permute-start.2 = (f32[20,32,2]{2,1,0:T(8,128)}, f32[20,32,2]{2,1,0:T(8,128)}, u32[]{:S(2)}, u32[]{:S(2)}) collective-permute-start(f32[20,32,2]{2,1,0:T(8,128)} %get-tuple-element.51), channel_id=1, source_target_pairs={{0,2},{2,4},{4,6},{1,3},{3,5},{5,7},{8,10},{10,12},{12,14},{9,11},... | collective-permute-start | bytes 15368 | tf_op jit(solution)/shard_map/ppermute | solution.py:19
  52.3 6.5 %collective-permute-start.3 = (f32[20,32,2]{2,1,0:T(8,128)}, f32[20,32,2]{2,1,0:T(8,128)}, u32[]{:S(2)}, u32[]{:S(2)}) collective-permute-start(f32[20,32,2]{2,1,0:T(8,128)} %get-tuple-element.52), channel_id=1, source_target_pairs={{2,0},{4,2},{6,4},{3,1},{5,3},{7,5},{10,8},{12,10},{14,12},{11,9},... | collective-permute-start | bytes 15368 | tf_op jit(solution)/shard_map/ppermute | solution.py:22
  56.3 5.0 %collective-permute-start.30 = (f32[1,2,128]{2,1,0:T(2,128)S(1)}, f32[1,2,128]{2,1,0:T(2,128)S(1)}, u32[]{:S(2)}, u32[]{:S(2)}) collective-permute-start(f32[1,2,128]{2,1,0:T(2,128)S(1)} %bitcast.276), channel_id=1, source_target_pairs={{0,2},{2,0},{4,6},{6,4},{1,3},{3,1},{5,7},{7,5},{8,10},{10,8},{12,... | collective-permute-start | bytes 3080 | tf_op jit(solution)/shard_map/ppermute | solution.py:40
  60.1 3.2 %collective-permute-start.4 = (f32[20,2,132]{2,1,0:T(2,128)S(1)}, f32[20,2,132]{2,1,0:T(2,128)S(1)}, u32[]{:S(2)}, u32[]{:S(2)}) collective-permute-start(f32[20,2,132]{2,1,0:T(2,128)S(1)} %get-tuple-element.47), channel_id=1, source_target_pairs={{0,1},{2,3},{4,5},{6,7},{8,9},{10,11},{12,13},{14,15},{16,17},{18,... | collective-permute-start | bytes 63368 | tf_op jit(solution)/shard_map/ppermute | solution.py:19
  61.4 5.9 %collective-permute-start.5 = (f32[20,2,132]{2,1,0:T(2,128)S(1)}, f32[20,2,132]{2,1,0:T(2,128)S(1)}, u32[]{:S(2)}, u32[]{:S(2)}) collective-permute-start(f32[20,2,132]{2,1,0:T(2,128)S(1)} %get-tuple-element.48), channel_id=1, source_target_pairs={{1,0},{3,2},{5,4},{7,6},{9,8},{11,10},{13,12},{15,14},{17,16},{19,... | collective-permute-start | bytes 63368 | tf_op jit(solution)/shard_map/ppermute | solution.py:22
  63.2 8.2 %collective-permute-start.13 = (f32[3,8,8,144]{3,2,1,0:T(8,128)}, f32[3,8,8,144]{3,2,1,0:T(8,128)S(1)}, u32[]{:S(2)}, u32[]{:S(2)}) collective-permute-start(f32[3,8,8,144]{3,2,1,0:T(8,128)} %get-tuple-element.46), channel_id=1, source_target_pairs={{1,0},{3,2},{5,4},{7,6},{9,8},{11,10},{13,12},{15,14},{17,16},{19,... | collective-permute-start | bytes 331784 | tf_op jit(solution)/shard_map/ppermute | solution.py:22
  68.7 3.1 %copy-start.7 = (f32[3,32,128]{2,1,0:T(8,128)S(1)}, f32[3,32,128]{2,1,0:T(8,128)}, u32[]{:S(2)}) copy-start(f32[3,32,128]{2,1,0:T(8,128)} %param.8) | copy-start | bytes 147460
  68.7 3.1 %copy-start.31 = (f32[3,32,8]{2,1,0:T(8,128)S(1)}, f32[3,32,8]{2,1,0:T(8,128)}, u32[]{:S(2)}) copy-start(f32[3,32,8]{2,1,0:T(8,128)} %copy-done.30) | copy-start | bytes 9220
  68.7 4.2 %copy-start.18 = (f32[46,142]{1,0:T(8,128)S(1)}, f32[46,142]{1,0:T(8,128)}, u32[]{:S(2)}) copy-start(f32[46,142]{1,0:T(8,128)} %slice.1089) | copy-start | bytes 78388
  68.8 4.5 %copy-start.16 = (f32[44,140]{1,0:T(8,128)S(1)}, f32[44,140]{1,0:T(8,128)}, u32[]{:S(2)}) copy-start(f32[44,140]{1,0:T(8,128)} %slice.1096) | copy-start | bytes 73924
  71.8 50.0 %copy-start = (f32[3,8,48,144]{3,2,1,0:T(8,128)}, f32[3,8,48,144]{3,2,1,0:T(8,128)S(1)}, u32[]{:S(2)}) copy-start(f32[3,8,48,144]{3,2,1,0:T(8,128)S(1)} %pad_maximum_fusion) | copy-start | bytes 1990660
  71.8 1.7 %copy-start.14 = (f32[42,138]{1,0:T(8,128)S(1)}, f32[42,138]{1,0:T(8,128)}, u32[]{:S(2)}) copy-start(f32[42,138]{1,0:T(8,128)} %slice.1103) | copy-start | bytes 69556
  71.8 2.0 %copy-start.26 = (f32[40,136]{1,0:T(8,128)S(1)}, f32[40,136]{1,0:T(8,128)}, u32[]{:S(2)}) copy-start(f32[40,136]{1,0:T(8,128)} %slice.1110) | copy-start | bytes 65284
  74.1 48.0 %copy-start.12 = (f32[3,40,136]{2,1,0:T(8,128)}, f32[3,40,136]{2,1,0:T(8,128)S(1)}, u32[]{:S(2)}) copy-start(f32[3,40,136]{2,1,0:T(8,128)S(1)} %get-tuple-element.42) | copy-start | bytes 195844
  74.1 0.8 copy-start.22
  74.6 47.7 %copy-start.10 = (f32[3,38,134]{2,1,0:T(8,128)}, f32[3,38,134]{2,1,0:T(8,128)S(1)}, u32[]{:S(2)}) copy-start(f32[3,38,134]{2,1,0:T(8,128)S(1)} %get-tuple-element.40) | copy-start | bytes 183316
  75.2 47.3 %copy-start.8 = (f32[3,36,132]{2,1,0:T(8,128)}, f32[3,36,132]{2,1,0:T(8,128)S(1)}, u32[]{:S(2)}) copy-start(f32[3,36,132]{2,1,0:T(8,128)S(1)} %get-tuple-element.38) | copy-start | bytes 171076
  75.8 6.0 %collective-permute-start.14 = (f32[3,32,128]{2,1,0:T(8,128)S(1)}, f32[3,32,128]{2,1,0:T(8,128)S(1)}, u32[]{:S(2)}, u32[]{:S(2)}) collective-permute-start(f32[3,32,128]{2,1,0:T(8,128)S(1)} %fusion.197), channel_id=1, source_target_pairs={{0,8},{8,16},{16,24},{1,9},{9,17},{17,25},{2,10},{10,18},{18,26},{... | collective-permute-start | bytes 147464 | tf_op jit(solution)/shard_map/ppermute | solution.py:30
  81.9 6.7 %collective-permute-start.15 = (f32[3,32,8]{2,1,0:T(8,128)S(1)}, f32[3,32,8]{2,1,0:T(8,128)S(1)}, u32[]{:S(2)}, u32[]{:S(2)}) collective-permute-start(f32[3,32,8]{2,1,0:T(8,128)S(1)} %get-tuple-element.87), channel_id=1, source_target_pairs={{0,2},{2,4},{4,6},{1,3},{3,5},{5,7},{8,10},{10,12},{12,14},{9,11},... | collective-permute-start | bytes 9224 | tf_op jit(solution)/shard_map/ppermute | solution.py:19
  85.2 5.0 %collective-permute-start.16 = (f32[3,32,8]{2,1,0:T(8,128)S(1)}, f32[3,32,8]{2,1,0:T(8,128)S(1)}, u32[]{:S(2)}, u32[]{:S(2)}) collective-permute-start(f32[3,32,8]{2,1,0:T(8,128)S(1)} %get-tuple-element.88), channel_id=1, source_target_pairs={{2,0},{4,2},{6,4},{3,1},{5,3},{7,5},{10,8},{12,10},{14,12},{11,9},... | collective-permute-start | bytes 9224 | tf_op jit(solution)/shard_map/ppermute | solution.py:22
  90.3 3.3 %collective-permute-start.17 = (f32[3,8,144]{2,1,0:T(8,128)S(1)}, f32[3,8,144]{2,1,0:T(8,128)S(1)}, u32[]{:S(2)}, u32[]{:S(2)}) collective-permute-start(f32[3,8,144]{2,1,0:T(8,128)S(1)} %get-tuple-element.75), channel_id=1, source_target_pairs={{0,1},{2,3},{4,5},{6,7},{8,9},{10,11},{12,13},{14,15},{16,17},{18,... | collective-permute-start | bytes 41480 | tf_op jit(solution)/shard_map/ppermute | solution.py:19
  91.9 5.7 %collective-permute-start.18 = (f32[3,8,144]{2,1,0:T(8,128)S(1)}, f32[3,8,144]{2,1,0:T(8,128)S(1)}, u32[]{:S(2)}, u32[]{:S(2)}) collective-permute-start(f32[3,8,144]{2,1,0:T(8,128)S(1)} %get-tuple-element.76), channel_id=1, source_target_pairs={{1,0},{3,2},{5,4},{7,6},{9,8},{11,10},{13,12},{15,14},{17,16},{19,... | collective-permute-start | bytes 41480 | tf_op jit(solution)/shard_map/ppermute | solution.py:22
  99.5 6.5 %collective-permute-start.19 = (f32[3,32,128]{2,1,0:T(8,128)S(1)}, f32[3,32,128]{2,1,0:T(8,128)S(1)}, u32[]{:S(2)}, u32[]{:S(2)}) collective-permute-start(f32[3,32,128]{2,1,0:T(8,128)S(1)} %fusion.193), channel_id=1, source_target_pairs={{0,8},{8,16},{16,24},{1,9},{9,17},{17,25},{2,10},{10,18},{18,26},{... | collective-permute-start | bytes 147464 | tf_op jit(solution)/shard_map/ppermute | solution.py:30
  106.1 4.9 %collective-permute-start.20 = (f32[3,32,8]{2,1,0:T(8,128)S(1)}, f32[3,32,8]{2,1,0:T(8,128)S(1)}, u32[]{:S(2)}, u32[]{:S(2)}) collective-permute-start(f32[3,32,8]{2,1,0:T(8,128)S(1)} %get-tuple-element.85), channel_id=1, source_target_pairs={{0,2},{2,4},{4,6},{1,3},{3,5},{5,7},{8,10},{10,12},{12,14},{9,11},... | collective-permute-start | bytes 9224 | tf_op jit(solution)/shard_map/ppermute | solution.py:19
  109.1 4.7 %collective-permute-start.21 = (f32[3,32,8]{2,1,0:T(8,128)S(1)}, f32[3,32,8]{2,1,0:T(8,128)S(1)}, u32[]{:S(2)}, u32[]{:S(2)}) collective-permute-start(f32[3,32,8]{2,1,0:T(8,128)S(1)} %get-tuple-element.86), channel_id=1, source_target_pairs={{2,0},{4,2},{6,4},{3,1},{5,3},{7,5},{10,8},{12,10},{14,12},{11,9},... | collective-permute-start | bytes 9224 | tf_op jit(solution)/shard_map/ppermute | solution.py:22
  113.9 5.2 %collective-permute-start.22 = (f32[3,8,144]{2,1,0:T(8,128)S(1)}, f32[3,8,144]{2,1,0:T(8,128)S(1)}, u32[]{:S(2)}, u32[]{:S(2)}) collective-permute-start(f32[3,8,144]{2,1,0:T(8,128)S(1)} %get-tuple-element.73), channel_id=1, source_target_pairs={{0,1},{2,3},{4,5},{6,7},{8,9},{10,11},{12,13},{14,15},{16,17},{18,... | collective-permute-start | bytes 41480 | tf_op jit(solution)/shard_map/ppermute | solution.py:19
  115.5 5.7 %collective-permute-start.23 = (f32[3,8,144]{2,1,0:T(8,128)S(1)}, f32[3,8,144]{2,1,0:T(8,128)S(1)}, u32[]{:S(2)}, u32[]{:S(2)}) collective-permute-start(f32[3,8,144]{2,1,0:T(8,128)S(1)} %get-tuple-element.74), channel_id=1, source_target_pairs={{1,0},{3,2},{5,4},{7,6},{9,8},{11,10},{13,12},{15,14},{17,16},{19,... | collective-permute-start | bytes 41480 | tf_op jit(solution)/shard_map/ppermute | solution.py:22
  122.1 4.5 %copy-start.5 = (f32[18,34,130]{2,1,0:T(8,128)S(1)}, f32[18,34,130]{2,1,0:T(8,128)}, u32[]{:S(2)}) copy-start(f32[18,34,130]{2,1,0:T(8,128)} %broadcast_multiply_fusion.1) | copy-start | bytes 954724
  123.1 6.2 %collective-permute-start.24 = (f32[3,32,128]{2,1,0:T(8,128)S(1)}, f32[3,32,128]{2,1,0:T(8,128)S(1)}, u32[]{:S(2)}, u32[]{:S(2)}) collective-permute-start(f32[3,32,128]{2,1,0:T(8,128)S(1)} %fusion.189), channel_id=1, source_target_pairs={{0,8},{8,16},{16,24},{1,9},{9,17},{17,25},{2,10},{10,18},{18,26},{... | collective-permute-start | bytes 147464 | tf_op jit(solution)/shard_map/ppermute | solution.py:30
  130.7 15.7 %collective-permute-start.25 = (f32[3,32,8]{2,1,0:T(8,128)}, f32[3,32,8]{2,1,0:T(8,128)S(1)}, u32[]{:S(2)}, u32[]{:S(2)}) collective-permute-start(f32[3,32,8]{2,1,0:T(8,128)} %get-tuple-element.83), channel_id=1, source_target_pairs={{0,2},{2,4},{4,6},{1,3},{3,5},{5,7},{8,10},{10,12},{12,14},{9,11},... | collective-permute-start | bytes 9224 | tf_op jit(solution)/shard_map/ppermute | solution.py:19
  133.3 13.1 %collective-permute-start.26 = (f32[3,32,8]{2,1,0:T(8,128)}, f32[3,32,8]{2,1,0:T(8,128)}, u32[]{:S(2)}, u32[]{:S(2)}) collective-permute-start(f32[3,32,8]{2,1,0:T(8,128)} %get-tuple-element.84), channel_id=1, source_target_pairs={{2,0},{4,2},{6,4},{3,1},{5,3},{7,5},{10,8},{12,10},{14,12},{11,9},... | collective-permute-start | bytes 9224 | tf_op jit(solution)/shard_map/ppermute | solution.py:22
  146.3 10.0 %copy-start.1 = (f32[3,8,48,144]{3,2,1,0:T(8,128)S(1)}, f32[3,8,48,144]{3,2,1,0:T(8,128)}, u32[]{:S(2)}) copy-start(f32[3,8,48,144]{3,2,1,0:T(8,128)} %copy-done) | copy-start | bytes 1990660
  146.3 10.9 %copy-start.19 = (f32[46,142]{1,0:T(8,128)S(1)}, f32[46,142]{1,0:T(8,128)}, u32[]{:S(2)}) copy-start(f32[46,142]{1,0:T(8,128)} %slice.1089) | copy-start | bytes 78388
  146.4 11.2 %copy-start.17 = (f32[44,140]{1,0:T(8,128)S(1)}, f32[44,140]{1,0:T(8,128)}, u32[]{:S(2)}) copy-start(f32[44,140]{1,0:T(8,128)} %slice.1096) | copy-start | bytes 73924
  147.3 5.1 %collective-permute-start.27 = (f32[3,8,144]{2,1,0:T(8,128)S(1)}, f32[3,8,144]{2,1,0:T(8,128)S(1)}, u32[]{:S(2)}, u32[]{:S(2)}) collective-permute-start(f32[3,8,144]{2,1,0:T(8,128)S(1)} %get-tuple-element.71), channel_id=1, source_target_pairs={{0,1},{2,3},{4,5},{6,7},{8,9},{10,11},{12,13},{14,15},{16,17},{18,... | collective-permute-start | bytes 41480 | tf_op jit(solution)/shard_map/ppermute | solution.py:19
  150.6 5.7 %collective-permute-start.28 = (f32[3,8,144]{2,1,0:T(8,128)S(1)}, f32[3,8,144]{2,1,0:T(8,128)S(1)}, u32[]{:S(2)}, u32[]{:S(2)}) collective-permute-start(f32[3,8,144]{2,1,0:T(8,128)S(1)} %get-tuple-element.72), channel_id=1, source_target_pairs={{1,0},{3,2},{5,4},{7,6},{9,8},{11,10},{13,12},{15,14},{17,16},{19,... | collective-permute-start | bytes 41480 | tf_op jit(solution)/shard_map/ppermute | solution.py:22
  152.3 5.5 %copy-start.15 = (f32[42,138]{1,0:T(8,128)S(1)}, f32[42,138]{1,0:T(8,128)}, u32[]{:S(2)}) copy-start(f32[42,138]{1,0:T(8,128)} %slice.1103) | copy-start | bytes 69556
  157.3 0.9 copy-start.13
  157.3 0.9 copy-start.27
  157.5 0.9 copy-start.11
  157.6 0.9 copy-start.25
  157.8 0.9 copy-start.9
  157.9 0.9 copy-start.23
  158.4 1.0 copy-start.29
  159.0 1.2 copy-start.3
  159.0 1.2 copy-start.4
  159.0 1.3 copy-start.20
  159.0 1.3 copy-start.21
  160.4 3.9 %copy-start.33 = (f32[2,128]{1,0:T(2,128)S(1)}, f32[2,128]{1,0:T(2,128)}, u32[]{:S(2)}) copy-start(f32[2,128]{1,0:T(2,128)} %get-tuple-element.94) | copy-start | bytes 3076
  161.0 3.3 %collective-permute-start.29 = (f32[3,2,128]{2,1,0:T(2,128)S(1)}, f32[3,2,128]{2,1,0:T(2,128)S(1)}, u32[]{:S(2)}, u32[]{:S(2)}) collective-permute-start(f32[3,2,128]{2,1,0:T(2,128)S(1)} %bitcast.275), channel_id=1, source_target_pairs={{0,2},{2,0},{4,6},{6,4},{1,3},{3,1},{5,7},{7,5},{8,10},{10,8},{12,... | collective-permute-start | bytes 9224 | tf_op jit(solution)/shard_map/ppermute | solution.py:40
  161.2 4.7 %collective-permute-start.32 = (f32[1,1,128]{2,1,0:T(1,128)S(1)}, f32[1,1,128]{2,1,0:T(1,128)S(1)}, u32[]{:S(2)}, u32[]{:S(2)}) collective-permute-start(f32[1,1,128]{2,1,0:T(1,128)S(1)} %fusion.209), channel_id=1, source_target_pairs={{0,4},{4,0},{2,6},{6,2},{1,5},{5,1},{3,7},{7,3},{8,12},{12,8},{10,... | collective-permute-start | bytes 1544 | tf_op jit(solution)/shard_map/ppermute | solution.py:40
  164.3 3.6 %collective-permute-start.31 = (f32[3,1,128]{2,1,0:T(1,128)S(1)}, f32[3,1,128]{2,1,0:T(1,128)S(1)}, u32[]{:S(2)}, u32[]{:S(2)}) collective-permute-start(f32[3,1,128]{2,1,0:T(1,128)S(1)} %fusion.204), channel_id=1, source_target_pairs={{0,4},{4,0},{2,6},{6,2},{1,5},{5,1},{3,7},{7,3},{8,12},{12,8},{10,... | collective-permute-start | bytes 4616 | tf_op jit(solution)/shard_map/ppermute | solution.py:40
  (3 other events, 2.4 us)

commit v2 on v1

--- a/solution.py
+++ b/solution.py
@@ -84,16 +84,40 @@
     return ((places >= 0) & (places < devices * width)).astype(jnp.float32)
 
 
-def propagate(current, depth_rim, plane_inside, brick_a, brick_v, light_step):
+def halo(block, axis, dim, width):
+    count = lax.axis_size(axis)
+    size = block.shape[dim]
+    lows, highs = [], []
+    for hop in range(1, count):
+        need = min(size, width - (hop - 1) * size)
+        if need <= 0:
+            break
+        forward = [(i, i + hop) for i in range(count - hop)]
+        backward = [(target, source) for source, target in forward]
+        low = lax.slice_in_dim(block, size - need, None, axis=dim)
+        lows.insert(0, lax.ppermute(low, axis, forward))
+        highs.append(lax.ppermute(lax.slice_in_dim(block, 0, need, axis=dim), axis, backward))
+    block = jnp.concatenate(lows + [block] + highs, axis=dim)
+    missing = width - sum(part.shape[dim] for part in lows)
+    if missing > 0:
+        widths = [(0, 0)] * block.ndim
+        widths[dim] = (missing, missing)
+        block = jnp.pad(block, widths)
+    return block
+
+
+def propagate(current, border_in, depth_rim, plane_inside, brick_a, brick_v, light_step):
+    widest = (depth_rim.shape[2] - brick_a) // 2
     starts = []
     for slab_num in range(SLABS):
-        border = SLABS - slab_num
+        border = border_in - slab_num
         starts.append(current[:, border : border + brick_a, border : border + brick_v])
+        offset = widest - border
         depth_here = depth_rim[
             :,
             slab_num,
-            slab_num : slab_num + brick_a + 2 * border,
-            slab_num : slab_num + brick_v + 2 * border,
+            offset : offset + brick_a + 2 * border,
+            offset : offset + brick_v + 2 * border,
         ]
         current = current * jnp.exp(-light_step * depth_here)
         centre = current[:, 1:-1, 1:-1]
@@ -105,11 +129,12 @@
             - 4.0 * centre
         )
         inner = border - 1
+        offset = widest - inner
         current = (
             current
             * plane_inside[
-                slab_num + 1 : slab_num + 1 + brick_a + 2 * inner,
-                slab_num + 1 : slab_num + 1 + brick_v + 2 * inner,
+                offset : offset + brick_a + 2 * inner,
+                offset : offset + brick_v + 2 * inner,
             ][None]
         )
     return (current, jnp.stack(starts, axis=1))
@@ -146,19 +171,25 @@
     extinct_slabs = extinct.reshape(3, SLABS, layer_rows, brick_a, brick_v)
     running = jnp.cumsum(extinct_slabs, axis=2) - extinct_slabs
     slab_depth = jnp.sum(extinct_slabs, axis=2)
-    depth_rim = padded_2(slab_depth, (("view", 3), ("across", 2)), SLABS)
+    widest = SLABS * n_light
+    depth_rim = halo(halo(slab_depth, "across", 2, widest), "view", 3, widest)
+    sun_rim = halo(halo(sunlight, "across", 1, widest), "view", 2, widest)
     plane_inside = (
-        rim_mask(across_idx, n_across, brick_a, SLABS)[:, None]
-        * rim_mask(view_idx, n_view, brick_v, SLABS)[None, :]
+        rim_mask(across_idx, n_across, brick_a, widest)[:, None]
+        * rim_mask(view_idx, n_view, brick_v, widest)[None, :]
     )
     starts = None
-    incoming = sunlight
+    incoming = sun_rim
     for section_num in range(n_light):
-        current = padded_2(incoming, (("view", 2), ("across", 1)), SLABS)
-        outgoing, starts = propagate(current, depth_rim, plane_inside, brick_a, brick_v, light_step)
+        border = SLABS * (n_light - section_num)
+        outgoing, starts = propagate(
+            incoming, border, depth_rim, plane_inside, brick_a, brick_v, light_step
+        )
         if section_num + 1 < n_light:
             arrived = from_behind(outgoing, "light", 1)
-            incoming = jnp.where(light_idx == 0, sunlight, arrived)
+            cut = widest - border + SLABS
+            sun_here = sun_rim[:, cut : cut + brick_a + 2 * (border - SLABS), cut : cut + brick_v + 2 * (border - SLABS)]
+            incoming = jnp.where(light_idx == 0, sun_here, arrived)
     lighting = (starts[:, :, None] * jnp.exp(-light_step * running)).reshape(
         3, brick_l, brick_a, brick_v
     )

time: 172 us -> 158 us (0.919)
  local copies, waits for them, and re-layouts: 15.4 us -> 40.6 us
  starting transfers between devices: 75.1 us -> 53.7 us
  waiting for transfers between devices: 24 us -> 12.4 us
  other arithmetic: 51.2 us -> 47 us
    ppermute x13 -> x3, starting transfers between devices: 38.3 us -> 8.93 us  [padded_2(): lax.ppermute(lax.slice_in_dim(block, block.shape[dim] - width, None, axis...]
    ppermute x0 -> x8, starting transfers between devices: none -> 26.3 us  [the longest x4 21 us: halo(): lows.insert(0, lax.ppermute(low, axis, forward))]
    slice x8 -> x35, local copies, waits for them, and re-layouts: 4.94 us -> 27.4 us  [the longest x30 20.7 us: propagate(): plane_inside[offset:offset + brick_a + 2 * inner, offset:offset + brick_v...]
    ppermute x13 -> x3, waiting for transfers between devices: 19.8 us -> 1.52 us  [padded_2(): lax.ppermute(lax.slice_in_dim(block, 0, width, axis=dim), axis, backward)]
    ppermute x13 -> x3, starting transfers between devices: 18.2 us -> 4.93 us  [padded_2(): lax.ppermute(lax.slice_in_dim(block, 0, width, axis=dim), axis, backward)]
    ppermute x3, waiting for transfers between devices: 1.78 us -> 8.42 us  [from_behind(): lax.ppermute(value, axis, [(source, source + steps) for source in range(l...]
    ppermute x0 -> x2, local copies, waits for them, and re-layouts: none -> 4.9 us  [the longest x1 2.5 us: halo(): lax.ppermute(lax.slice_in_dim(block, 0, need, axis=dim), axis, backward)]
    slice x6 -> x1, other arithmetic: 4.66 us -> 0.19 us  [padded_2(): lax.slice_in_dim(block, block.shape[dim] - width, None, axis=dim)]
  transfers between devices with their start and end apart: 33 -> 21, of which waited for: 11 -> 5; matrix products, arithmetic and copies ran while one was open for 31% -> 41% of each run, Pallas kernels for 0% -> 0%
where the time goes in v2:
time: 158 us; the launch traced here: 156 us
  starting transfers between devices  53.7 us (34%)
  other arithmetic  47 us (30%)
  local copies, waits for them, and re-layouts  40.6 us (26%)
  waiting for transfers between devices  12.4 us (8%)
    ppermute x4, starting transfers between devices, halo(): lows.insert(0, lax.ppermute(low, axis, forward))  21 us
    slice x30, local copies, waits for them, and re-layouts, propagate(): plane_inside[offset:offset + brick_a + 2 * inner, offset:offset + brick_v...  20.7 us
    mul x1, other arithmetic, shade_from(): (2.0 * centre + tensor[:, 2:, 1:-1, 1:-1] + tensor[:, :-2, 1:-1, 1:-1] +...  12.2 us
    mul x31, other arithmetic, propagate(): current = current * jnp.exp(-light_step * depth_here)  11 us
    ppermute x3, starting transfers between devices, from_behind(): lax.ppermute(value, axis, [(source, source + steps) for source in range(l...  9.37 us
    ppermute x3, starting transfers between devices, padded_2(): lax.ppermute(lax.slice_in_dim(block, block.shape[dim] - width, None, axis...  8.93 us
    ppermute x3, waiting for transfers between devices, from_behind(): lax.ppermute(value, axis, [(source, source + steps) for source in range(l...  8.42 us
    unnamed x92, local copies, waits for them, and re-layouts  6.61 us
  transfers between devices with their start and end apart: 21, of which 5 were waited for; matrix products, arithmetic and copies ran while one was open for 41% of the time, Pallas kernels for 0%

profile of v2, /device:TPU:16, one launch (start us, length us, event | category | flops | bytes accessed | tf_op | source)
XLA Modules:
  0.0 155.8 jit_solution(4471625248700477999)
XLA Ops:
  1.2 1.6 %broadcast_compare_fusion.14 = (pred[16,32,128]{2,1,0:T(8,128)(4,1)S(1)}, pred[16,32,128]{2,1,0:T(8,128)(4,1)S(1)}, pred[16,32,128]{2,1,0:T(8,128)(4,1)S(1)}, pr...) fusion(s32[16,32,128]{2,1,0:T(8,128)} %param.7), kind=kLoop, calls=%fused_computation.399 | loop fusion | flops 983040 | bytes 1245184 | tf_op jit(solution)/shard_map/eq | solution.py:168
  2.8 2.7 %select_select_fusion = f32[7,16,32,128]{3,2,1,0:T(8,128)S(1)} fusion(f32[7]{0:T(128)S(1)} %get-tuple-element.6, f32[7]{0:T(128)S(1)} %get-tuple-element.7, f32[7]{0:T(128)S(1)} %get-tuple-element.8, f32[7]{0:T(128)S(1)} %get-tuple-element.9, f32[7]{0:T(128)S(1)} %get-tuple-element.10, f32[7]{0:T(128)S(1)} %get-tuple-element.11, f32[7]{0:T(128)S(1)} %get-tuple-element.12, ...), kind=kLoop, calls=%fused_computation.2 | loop fusion | flops 6881280 | bytes 2818496 | tf_op jit(solution)/shard_map/jit(_where)/select_n | solution.py:167
  5.7 4.2 %collective-permute-start.10 = (f32[3,8,32,128]{3,2,1,0:T(8,128)S(1)}, f32[3,8,32,128]{3,2,1,0:T(8,128)}, u32[]{:S(2)}, u32[]{:S(2)}) collective-permute-start(f32[3,8,32,128]{3,2,1,0:T(8,128)S(1)} %reduce_sum.27), channel_id=1, source_target_pairs={{0,1},{2,3},{4,5},{6,7},{8,9},{10,11},{12,13},{14,15},{16,17},{18,... | collective-permute-start | bytes 1179656 | tf_op jit(solution)/shard_map/ppermute | solution.py:98
  9.9 1.3 collective-permute-start.11
  11.8 3.5 %collective-permute-start = (f32[2,32,128]{2,1,0:T(8,128)}, f32[2,32,128]{2,1,0:T(8,128)S(1)}, u32[]{:S(2)}, u32[]{:S(2)}) collective-permute-start(f32[2,32,128]{2,1,0:T(8,128)} %get-tuple-element.47), channel_id=1, source_target_pairs={{0,8},{8,16},{16,24},{1,9},{9,17},{17,25},{2,10},{10,18},{18,26},{... | collective-permute-start | bytes 98312 | tf_op jit(solution)/shard_map/ppermute | solution.py:19
  15.3 2.4 %collective-permute-start.1 = (f32[2,32,128]{2,1,0:T(8,128)}, f32[2,32,128]{2,1,0:T(8,128)S(1)}, u32[]{:S(2)}, u32[]{:S(2)}) collective-permute-start(f32[2,32,128]{2,1,0:T(8,128)} %get-tuple-element.46), channel_id=1, source_target_pairs={{8,0},{16,8},{24,16},{9,1},{17,9},{25,17},{10,2},{18,10},{26,18},{... | collective-permute-start | bytes 98312 | tf_op jit(solution)/shard_map/ppermute | solution.py:22
  17.6 5.3 %collective-permute-start.6 = (f32[3,32,128]{2,1,0:T(8,128)}, f32[3,32,128]{2,1,0:T(8,128)S(1)}, u32[]{:S(2)}, u32[]{:S(2)}) collective-permute-start(f32[3,32,128]{2,1,0:T(8,128)} %param.8), channel_id=1, source_target_pairs={{0,1},{2,3},{4,5},{6,7},{8,9},{10,11},{12,13},{14,15},{16,17},{18,... | collective-permute-start | bytes 147464 | tf_op jit(solution)/shard_map/ppermute | solution.py:98
  23.0 1.0 fusion.302
  24.0 1.0 fusion.1
  25.1 1.1 broadcast_multiply_fusion.1
  26.2 0.7 slice.1184
  26.9 0.7 slice.1191
  27.8 0.7 slice.1205
  28.5 0.7 slice.1212
  29.2 0.7 slice.1219
  30.0 0.7 slice.1226
  30.7 0.7 slice.1233
  31.4 0.7 slice.1240
  32.1 0.7 slice.1247
  32.9 0.7 slice.1254
  33.6 0.7 slice.1261
  34.3 0.7 slice.1268
  35.0 0.7 slice.1275
  35.7 0.7 slice.1282
  37.9 0.7 slice.1303
  38.6 0.7 slice.1310
  41.4 0.7 slice.1338
  47.1 0.8 exponential_subtract_fusion
  48.2 2.4 %collective-permute-start.2 = (f32[20,32,2]{2,1,0:T(8,128)S(1)}, f32[20,32,2]{2,1,0:T(8,128)S(1)}, u32[]{:S(2)}, u32[]{:S(2)}) collective-permute-start(f32[20,32,2]{2,1,0:T(8,128)S(1)} %get-tuple-element.43), channel_id=1, source_target_pairs={{0,2},{2,4},{4,6},{1,3},{3,5},{5,7},{8,10},{10,12},{12,14},{9,11},... | collective-permute-start | bytes 15368 | tf_op jit(solution)/shard_map/ppermute | solution.py:19
  50.6 1.3 collective-permute-start.3
  51.9 1.3 collective-permute-start.7
  53.2 1.5 collective-permute-done.3
  54.9 3.0 %collective-permute-start.4 = (f32[20,2,132]{2,1,0:T(2,128)S(1)}, f32[20,2,132]{2,1,0:T(2,128)S(1)}, u32[]{:S(2)}, u32[]{:S(2)}) collective-permute-start(f32[20,2,132]{2,1,0:T(2,128)S(1)} %get-tuple-element.41), channel_id=1, source_target_pairs={{0,1},{2,3},{4,5},{6,7},{8,9},{10,11},{12,13},{14,15},{16,17},{18,... | collective-permute-start | bytes 63368 | tf_op jit(solution)/shard_map/ppermute | solution.py:19
  58.6 1.3 collective-permute-start.5
  59.9 0.8 constant_dynamic-update-slice_fusion.5
  60.7 0.8 constant_dynamic-update-slice_fusion.4
  61.5 0.8 fusion.298
  62.3 6.2 %collective-permute-start.8 = (f32[3,96,32]{2,1,0:T(8,128)}, f32[3,96,32]{2,1,0:T(8,128)}, u32[]{:S(2)}, u32[]{:S(2)}) collective-permute-start(f32[3,96,32]{2,1,0:T(8,128)} %get-tuple-element.63), channel_id=1, source_target_pairs={{0,2},{2,4},{4,6},{1,3},{3,5},{5,7},{8,10},{10,12},{12,14},{9,11},... | collective-permute-start | bytes 110600 | tf_op jit(solution)/shard_map/ppermute | solution.py:98
  68.4 1.3 collective-permute-start.9
  70.6 0.8 bitcast_dynamic-update-slice_fusion.4
  71.7 1.2 bitcast_dynamic-update-slice_fusion.2
  72.9 2.0 %copy-done.3 = f32[6,18,34,130]{3,2,1,0:T(8,128)} copy-done((f32[6,18,34,130]{3,2,1,0:T(8,128)}, f32[6,18,34,130]{3,2,1,0:T(8,128)S(1)}, u32[]{:S(2)}) %copy-start.3) | copy-done | bytes 1909464
  75.0 1.2 pad_maximum_fusion.1
  76.1 1.9 %fusion.295 = (f32[3,8,96,32]{3,2,1,0:T(8,128)}, f32[3,8,96,32]{3,2,1,0:T(8,128)}) fusion(f32[3,8,96,128]{3,2,1,0:T(8,128)S(1)} %pad_maximum_fusion.1), kind=kLoop, calls=%fused_computation.523 | loop fusion | bytes 1179648 | tf_op jit(solution)/shard_map/slice | solution.py:97
  78.0 1.6 %copy.21 = f32[3,8,96,32]{2,3,1,0:T(8,128)S(1)} copy(f32[3,8,96,32]{3,2,1,0:T(8,128)} %get-tuple-element.39) | data formatting | bytes 589824 | tf_op jit(solution)/shard_map/slice | solution.py:97
  79.6 5.3 %collective-permute-start.12 = (f32[3,8,96,32]{2,3,1,0:T(8,128)S(1)}, f32[3,8,96,32]{2,3,1,0:T(8,128)}, u32[]{:S(2)}, u32[]{:S(2)}) collective-permute-start(f32[3,8,96,32]{2,3,1,0:T(8,128)S(1)} %copy.21), channel_id=1, source_target_pairs={{0,2},{2,4},{4,6},{1,3},{3,5},{5,7},{8,10},{10,12},{12,14},{9,11},... | collective-permute-start | bytes 884744 | tf_op jit(solution)/shard_map/ppermute | solution.py:98
  85.0 2.4 %copy.22 = f32[3,8,96,32]{2,3,1,0:T(8,128)} copy(f32[3,8,96,32]{3,2,1,0:T(8,128)} %get-tuple-element.40) | data formatting | bytes 589824 | tf_op jit(solution)/shard_map/slice | solution.py:99
  87.3 1.5 collective-permute-start.13
  88.8 1.5 bitcast_dynamic-update-slice_fusion.1
  90.3 1.9 %bitcast_dynamic-update-slice_fusion = f32[6,18,34,130]{3,2,1,0:T(8,128)} fusion(f32[6,18,34,130]{3,2,1,0:T(8,128)} %bitcast_dynamic-update-slice_fusion.1, f32[20,36,132]{2,1,0:T(8,128)S(1)} %pad_maximum_fusion.2, f32[20,32,2]{2,1,0:T(8,128)S(1)} %collective-permute-done.3, f32[20,32,128]{2,1,0:T(8,128)S(1)} %constant_dynamic-update-slice_fusion, ...), kind=kLoop, calls=%fused_computation.32 | loop fusion | flops 875160 | bytes 1753920 | tf_op jit(solution)/shard_map/stack | solution.py:70
  92.2 2.4 %copy.23 = f32[3,8,96,32]{3,2,1,0:T(8,128)} copy(f32[3,8,96,32]{2,3,1,0:T(8,128)} %collective-permute-done.12) | data formatting | bytes 589824 | tf_op jit(solution)/shard_map/ppermute | solution.py:98
  94.6 2.5 %copy.24 = f32[3,8,96,32]{3,2,1,0:T(8,128)} copy(f32[3,8,96,32]{2,3,1,0:T(8,128)} %collective-permute-done.13) | data formatting | bytes 589824 | tf_op jit(solution)/shard_map/ppermute | solution.py:99
  97.1 2.9 %pad_maximum_fusion = f32[3,8,96,192]{3,2,1,0:T(8,128)S(1)} fusion(f32[3,8,96,32]{3,2,1,0:T(8,128)} %copy.24, f32[3,8,32,128]{3,2,1,0:T(8,128)} %collective-permute-done.11, f32[3,8,32,128]{3,2,1,0:T(8,128)S(1)} %reduce_sum.27, f32[3,8,32,128]{3,2,1,0:T(8,128)} %collective-permute-done.10, f32[3,8,96,32]{3,2,1,0:T(8,128)} %copy.23), kind=kLoop, calls=%fused_computation | loop fusion | flops 1769472 | bytes 3538944 | tf_op jit(solution)/shard_map/concatenate | solution.py:100
  100.0 1.2 fusion.36
  105.0 3.6 %collective-permute-start.14 = (f32[3,80,176]{2,1,0:T(8,128)S(1)}, f32[3,80,176]{2,1,0:T(8,128)S(1)}, u32[]{:S(2)}, u32[]{:S(2)}) collective-permute-start(f32[3,80,176]{2,1,0:T(8,128)S(1)} %fusion.108), channel_id=1, source_target_pairs={{0,8},{8,16},{16,24},{1,9},{9,17},{17,25},{2,10},{10,18},{18,26},{... | collective-permute-start | bytes 506888 | tf_op jit(solution)/shard_map/ppermute | solution.py:30
  108.6 2.4 %broadcast_multiply_fusion = f32[6,18,34,130]{3,2,1,0:T(8,128)} fusion(f32[6,18,34,130]{3,2,1,0:T(8,128)S(1)} %bitcast.549, f32[18,34,130]{2,1,0:T(8,128)S(1)} %copy-done.6), kind=kLoop, calls=%fused_computation.1 | loop fusion | flops 477360 | bytes 4137120 | tf_op jit(solution)/shard_map/mul | solution.py:162
  111.0 2.7 %collective-permute-done.14 = f32[3,80,176]{2,1,0:T(8,128)S(1)} collective-permute-done((f32[3,80,176]{2,1,0:T(8,128)S(1)}, f32[3,80,176]{2,1,0:T(8,128)S(1)}, u32[]{:S(2)}, u32[]{:S(2)}) %collective-permute-start.14) | collective-permute-done | bytes 168992 | tf_op jit(solution)/shard_map/ppermute | solution.py:30
  117.2 3.8 %collective-permute-start.15 = (f32[3,64,160]{2,1,0:T(8,128)S(1)}, f32[3,64,160]{2,1,0:T(8,128)S(1)}, u32[]{:S(2)}, u32[]{:S(2)}) collective-permute-start(f32[3,64,160]{2,1,0:T(8,128)S(1)} %fusion.172), channel_id=1, source_target_pairs={{0,8},{8,16},{16,24},{1,9},{9,17},{17,25},{2,10},{10,18},{18,26},{... | collective-permute-start | bytes 368648 | tf_op jit(solution)/shard_map/ppermute | solution.py:30
  121.0 12.2 %fusion = f32[6,16,32,128]{3,2,1,0:T(8,128)} fusion(f32[6,18,34,130]{3,2,1,0:T(8,128)} %broadcast_multiply_fusion), kind=kLoop, calls=%fused_computation.4 | loop fusion | flops 3145728 | bytes 12582912 | tf_op jit(solution)/shard_map/mul | solution.py:45
  136.3 1.9 %collective-permute-start.16 = (f32[3,48,144]{2,1,0:T(8,128)S(1)}, f32[3,48,144]{2,1,0:T(8,128)S(1)}, u32[]{:S(2)}, u32[]{:S(2)}) collective-permute-start(f32[3,48,144]{2,1,0:T(8,128)S(1)} %fusion.236), channel_id=1, source_target_pairs={{0,8},{8,16},{16,24},{1,9},{9,17},{17,25},{2,10},{10,18},{18,26},{... | collective-permute-start | bytes 248840 | tf_op jit(solution)/shard_map/ppermute | solution.py:30
  138.5 5.8 %collective-permute-done.16 = f32[3,48,144]{2,1,0:T(8,128)S(1)} collective-permute-done((f32[3,48,144]{2,1,0:T(8,128)S(1)}, f32[3,48,144]{2,1,0:T(8,128)S(1)}, u32[]{:S(2)}, u32[]{:S(2)}) %collective-permute-start.16) | collective-permute-done | bytes 82976 | tf_op jit(solution)/shard_map/ppermute | solution.py:30
  149.0 2.4 %collective-permute-start.20 = (f32[1,1,128]{2,1,0:T(1,128)S(1)}, f32[1,1,128]{2,1,0:T(1,128)S(1)}, u32[]{:S(2)}, u32[]{:S(2)}) collective-permute-start(f32[1,1,128]{2,1,0:T(1,128)S(1)} %fusion.286), channel_id=1, source_target_pairs={{0,4},{4,0},{2,6},{6,2},{1,5},{5,1},{3,7},{7,3},{8,12},{12,8},{10,... | collective-permute-start | bytes 1544 | tf_op jit(solution)/shard_map/ppermute | solution.py:40
  151.4 1.1 collective-permute-start.19
  153.0 2.0 %collective-permute-done.19 = f32[3,1,128]{2,1,0:T(1,128)S(1)} collective-permute-done((f32[3,1,128]{2,1,0:T(1,128)S(1)}, f32[3,1,128]{2,1,0:T(1,128)S(1)}, u32[]{:S(2)}, u32[]{:S(2)}) %collective-permute-start.19) | collective-permute-done | bytes 1568 | tf_op jit(solution)/shard_map/ppermute | solution.py:40
  (195 shorter events, 28.9 us)
Async XLA Ops:
  1.1 4.3 %copy-start.4 = (f32[16,32,128]{2,1,0:T(8,128)S(1)}, f32[16,32,128]{2,1,0:T(8,128)}, u32[]{:S(2)}) copy-start(f32[16,32,128]{2,1,0:T(8,128)} %param.6) | copy-start | bytes 786436
  5.5 41.6 %copy-start = (f32[7,16,32,128]{3,2,1,0:T(8,128)}, f32[7,16,32,128]{3,2,1,0:T(8,128)S(1)}, u32[]{:S(2)}) copy-start(f32[7,16,32,128]{3,2,1,0:T(8,128)S(1)} %select_select_fusion) | copy-start | bytes 5505028
  5.7 67.3 %collective-permute-start.10 = (f32[3,8,32,128]{3,2,1,0:T(8,128)S(1)}, f32[3,8,32,128]{3,2,1,0:T(8,128)}, u32[]{:S(2)}, u32[]{:S(2)}) collective-permute-start(f32[3,8,32,128]{3,2,1,0:T(8,128)S(1)} %reduce_sum.27), channel_id=1, source_target_pairs={{0,1},{2,3},{4,5},{6,7},{8,9},{10,11},{12,13},{14,15},{16,17},{18,... | collective-permute-start | bytes 1179656 | tf_op jit(solution)/shard_map/ppermute | solution.py:98
  9.9 65.1 %collective-permute-start.11 = (f32[3,8,32,128]{3,2,1,0:T(8,128)S(1)}, f32[3,8,32,128]{3,2,1,0:T(8,128)}, u32[]{:S(2)}, u32[]{:S(2)}) collective-permute-start(f32[3,8,32,128]{3,2,1,0:T(8,128)S(1)} %reduce_sum.27), channel_id=1, source_target_pairs={{1,0},{3,2},{5,4},{7,6},{9,8},{11,10},{13,12},{15,14},{17,16},{19,... | collective-permute-start | bytes 1179656 | tf_op jit(solution)/shard_map/ppermute | solution.py:99
  11.8 35.3 %collective-permute-start = (f32[2,32,128]{2,1,0:T(8,128)}, f32[2,32,128]{2,1,0:T(8,128)S(1)}, u32[]{:S(2)}, u32[]{:S(2)}) collective-permute-start(f32[2,32,128]{2,1,0:T(8,128)} %get-tuple-element.47), channel_id=1, source_target_pairs={{0,8},{8,16},{16,24},{1,9},{9,17},{17,25},{2,10},{10,18},{18,26},{... | collective-permute-start | bytes 98312 | tf_op jit(solution)/shard_map/ppermute | solution.py:19
  15.3 32.7 %collective-permute-start.1 = (f32[2,32,128]{2,1,0:T(8,128)}, f32[2,32,128]{2,1,0:T(8,128)S(1)}, u32[]{:S(2)}, u32[]{:S(2)}) collective-permute-start(f32[2,32,128]{2,1,0:T(8,128)} %get-tuple-element.46), channel_id=1, source_target_pairs={{8,0},{16,8},{24,16},{9,1},{17,9},{25,17},{10,2},{18,10},{26,18},{... | collective-permute-start | bytes 98312 | tf_op jit(solution)/shard_map/ppermute | solution.py:22
  17.6 40.4 %collective-permute-start.6 = (f32[3,32,128]{2,1,0:T(8,128)}, f32[3,32,128]{2,1,0:T(8,128)S(1)}, u32[]{:S(2)}, u32[]{:S(2)}) collective-permute-start(f32[3,32,128]{2,1,0:T(8,128)} %param.8), channel_id=1, source_target_pairs={{0,1},{2,3},{4,5},{6,7},{8,9},{10,11},{12,13},{14,15},{16,17},{18,... | collective-permute-start | bytes 147464 | tf_op jit(solution)/shard_map/ppermute | solution.py:98
  47.9 2.7 %collective-permute-start.18 = (f32[1,2,128]{2,1,0:T(2,128)S(1)}, f32[1,2,128]{2,1,0:T(2,128)S(1)}, u32[]{:S(2)}, u32[]{:S(2)}) collective-permute-start(f32[1,2,128]{2,1,0:T(2,128)S(1)} %bitcast.561), channel_id=1, source_target_pairs={{0,2},{2,0},{4,6},{6,4},{1,3},{3,1},{5,7},{7,5},{8,10},{10,8},{12,... | collective-permute-start | bytes 3080 | tf_op jit(solution)/shard_map/ppermute | solution.py:40
  48.2 3.7 %collective-permute-start.2 = (f32[20,32,2]{2,1,0:T(8,128)S(1)}, f32[20,32,2]{2,1,0:T(8,128)S(1)}, u32[]{:S(2)}, u32[]{:S(2)}) collective-permute-start(f32[20,32,2]{2,1,0:T(8,128)S(1)} %get-tuple-element.43), channel_id=1, source_target_pairs={{0,2},{2,4},{4,6},{1,3},{3,5},{5,7},{8,10},{10,12},{12,14},{9,11},... | collective-permute-start | bytes 15368 | tf_op jit(solution)/shard_map/ppermute | solution.py:19
  50.6 4.1 %collective-permute-start.3 = (f32[20,32,2]{2,1,0:T(8,128)S(1)}, f32[20,32,2]{2,1,0:T(8,128)S(1)}, u32[]{:S(2)}, u32[]{:S(2)}) collective-permute-start(f32[20,32,2]{2,1,0:T(8,128)S(1)} %get-tuple-element.44), channel_id=1, source_target_pairs={{2,0},{4,2},{6,4},{3,1},{5,3},{7,5},{10,8},{12,10},{14,12},{11,9},... | collective-permute-start | bytes 15368 | tf_op jit(solution)/shard_map/ppermute | solution.py:22
  51.9 9.6 %collective-permute-start.7 = (f32[3,32,128]{2,1,0:T(8,128)}, f32[3,32,128]{2,1,0:T(8,128)S(1)}, u32[]{:S(2)}, u32[]{:S(2)}) collective-permute-start(f32[3,32,128]{2,1,0:T(8,128)} %param.8), channel_id=1, source_target_pairs={{1,0},{3,2},{5,4},{7,6},{9,8},{11,10},{13,12},{15,14},{17,16},{19,... | collective-permute-start | bytes 147464 | tf_op jit(solution)/shard_map/ppermute | solution.py:99
  54.9 13.5 %collective-permute-start.4 = (f32[20,2,132]{2,1,0:T(2,128)S(1)}, f32[20,2,132]{2,1,0:T(2,128)S(1)}, u32[]{:S(2)}, u32[]{:S(2)}) collective-permute-start(f32[20,2,132]{2,1,0:T(2,128)S(1)} %get-tuple-element.41), channel_id=1, source_target_pairs={{0,1},{2,3},{4,5},{6,7},{8,9},{10,11},{12,13},{14,15},{16,17},{18,... | collective-permute-start | bytes 63368 | tf_op jit(solution)/shard_map/ppermute | solution.py:19
  58.0 0.6 copy-start.38
  58.6 11.1 %collective-permute-start.5 = (f32[20,2,132]{2,1,0:T(2,128)S(1)}, f32[20,2,132]{2,1,0:T(2,128)S(1)}, u32[]{:S(2)}, u32[]{:S(2)}) collective-permute-start(f32[20,2,132]{2,1,0:T(2,128)S(1)} %get-tuple-element.42), channel_id=1, source_target_pairs={{1,0},{3,2},{5,4},{7,6},{9,8},{11,10},{13,12},{15,14},{17,16},{19,... | collective-permute-start | bytes 63368 | tf_op jit(solution)/shard_map/ppermute | solution.py:22
  62.3 37.7 %collective-permute-start.8 = (f32[3,96,32]{2,1,0:T(8,128)}, f32[3,96,32]{2,1,0:T(8,128)}, u32[]{:S(2)}, u32[]{:S(2)}) collective-permute-start(f32[3,96,32]{2,1,0:T(8,128)} %get-tuple-element.63), channel_id=1, source_target_pairs={{0,2},{2,4},{4,6},{1,3},{3,5},{5,7},{8,10},{10,12},{12,14},{9,11},... | collective-permute-start | bytes 110600 | tf_op jit(solution)/shard_map/ppermute | solution.py:98
  68.4 31.6 %collective-permute-start.9 = (f32[3,96,32]{2,1,0:T(8,128)}, f32[3,96,32]{2,1,0:T(8,128)}, u32[]{:S(2)}, u32[]{:S(2)}) collective-permute-start(f32[3,96,32]{2,1,0:T(8,128)} %get-tuple-element.64), channel_id=1, source_target_pairs={{2,0},{4,2},{6,4},{3,1},{5,3},{7,5},{10,8},{12,10},{14,12},{11,9},... | collective-permute-start | bytes 110600 | tf_op jit(solution)/shard_map/ppermute | solution.py:99
  72.9 2.0 %copy-start.3 = (f32[6,18,34,130]{3,2,1,0:T(8,128)}, f32[6,18,34,130]{3,2,1,0:T(8,128)S(1)}, u32[]{:S(2)}) copy-start(f32[6,18,34,130]{3,2,1,0:T(8,128)S(1)} %bitcast_dynamic-update-slice_fusion.2) | copy-start | bytes 5728324
  79.6 12.6 %collective-permute-start.12 = (f32[3,8,96,32]{2,3,1,0:T(8,128)S(1)}, f32[3,8,96,32]{2,3,1,0:T(8,128)}, u32[]{:S(2)}, u32[]{:S(2)}) collective-permute-start(f32[3,8,96,32]{2,3,1,0:T(8,128)S(1)} %copy.21), channel_id=1, source_target_pairs={{0,2},{2,4},{4,6},{1,3},{3,5},{5,7},{8,10},{10,12},{12,14},{9,11},... | collective-permute-start | bytes 884744 | tf_op jit(solution)/shard_map/ppermute | solution.py:98
  87.3 7.3 %collective-permute-start.13 = (f32[3,8,96,32]{2,3,1,0:T(8,128)}, f32[3,8,96,32]{2,3,1,0:T(8,128)}, u32[]{:S(2)}, u32[]{:S(2)}) collective-permute-start(f32[3,8,96,32]{2,3,1,0:T(8,128)} %copy.22), channel_id=1, source_target_pairs={{2,0},{4,2},{6,4},{3,1},{5,3},{7,5},{10,8},{12,10},{14,12},{11,9},... | collective-permute-start | bytes 884744 | tf_op jit(solution)/shard_map/ppermute | solution.py:99
  97.1 4.1 %copy-start.10 = (f32[94,190]{1,0:T(8,128)S(1)}, f32[94,190]{1,0:T(8,128)}, u32[]{:S(2)}) copy-start(f32[94,190]{1,0:T(8,128)} %slice.1184) | copy-start | bytes 214324
  100.0 1.7 %copy-start.9 = (f32[92,188]{1,0:T(8,128)S(1)}, f32[92,188]{1,0:T(8,128)}, u32[]{:S(2)}) copy-start(f32[92,188]{1,0:T(8,128)} %slice.1191) | copy-start | bytes 207556
  101.2 7.4 %slice-start = ((s8[4423680]{0:T(1024)(128)(4,1)}), s8[4194304]{0:T(1024)(128)(4,1)S(1)}, s32[]{:S(2)}) async-start(s8[4423680]{0:T(1024)(128)(4,1)} %bitcast.548), calls=%async_computation | async-start | bytes 8388608
  101.7 1.1 copy-start.14
  102.2 1.1 copy-start.13
  102.8 0.9 copy-start.12
  102.8 5.8 %slice-start.1 = ((s8[4423680]{0:T(1024)(128)(4,1)}), s8[229376]{0:T(1024)(128)(4,1)S(1)}, s32[]{:S(2)}) async-start(s8[4423680]{0:T(1024)(128)(4,1)} %bitcast.548), calls=%async_computation.1 | async-start | bytes 458752
  103.3 0.9 copy-start.11
  103.7 0.9 copy-start.18
  104.2 4.4 %copy-start.6 = (f32[18,34,130]{2,1,0:T(8,128)S(1)}, f32[18,34,130]{2,1,0:T(8,128)}, u32[]{:S(2)}) copy-start(f32[18,34,130]{2,1,0:T(8,128)} %broadcast_multiply_fusion.1) | copy-start | bytes 954724
  105.0 8.9 %copy-start.17 = (f32[78,174]{1,0:T(8,128)S(1)}, f32[78,174]{1,0:T(8,128)}, u32[]{:S(2)}) copy-start(f32[78,174]{1,0:T(8,128)} %slice.1240) | copy-start | bytes 162868
  105.0 8.7 %collective-permute-start.14 = (f32[3,80,176]{2,1,0:T(8,128)S(1)}, f32[3,80,176]{2,1,0:T(8,128)S(1)}, u32[]{:S(2)}, u32[]{:S(2)}) collective-permute-start(f32[3,80,176]{2,1,0:T(8,128)S(1)} %fusion.108), channel_id=1, source_target_pairs={{0,8},{8,16},{16,24},{1,9},{9,17},{17,25},{2,10},{10,18},{18,26},{... | collective-permute-start | bytes 506888 | tf_op jit(solution)/shard_map/ppermute | solution.py:30
  111.0 3.3 %copy-start.16 = (f32[76,172]{1,0:T(8,128)S(1)}, f32[76,172]{1,0:T(8,128)}, u32[]{:S(2)}) copy-start(f32[76,172]{1,0:T(8,128)} %slice.1247) | copy-start | bytes 156868
  113.9 0.9 copy-start.15
  114.3 0.9 copy-start.22
  114.8 0.9 copy-start.21
  115.2 0.9 copy-start.20
  115.6 0.9 copy-start.19
  116.1 0.8 copy-start.26
  117.2 16.3 %copy-start.25 = (f32[62,158]{1,0:T(8,128)S(1)}, f32[62,158]{1,0:T(8,128)}, u32[]{:S(2)}) copy-start(f32[62,158]{1,0:T(8,128)} %slice.1296) | copy-start | bytes 117556
  117.2 16.1 %collective-permute-start.15 = (f32[3,64,160]{2,1,0:T(8,128)S(1)}, f32[3,64,160]{2,1,0:T(8,128)S(1)}, u32[]{:S(2)}, u32[]{:S(2)}) collective-permute-start(f32[3,64,160]{2,1,0:T(8,128)S(1)} %fusion.172), channel_id=1, source_target_pairs={{0,8},{8,16},{16,24},{1,9},{9,17},{17,25},{2,10},{10,18},{18,26},{... | collective-permute-start | bytes 368648 | tf_op jit(solution)/shard_map/ppermute | solution.py:30
  133.3 0.8 copy-start.24
  133.3 1.2 copy-start.23
  133.5 1.3 copy-start.30
  134.1 1.0 copy-start.29
  134.4 1.0 copy-start.28
  134.8 1.0 copy-start.27
  135.1 0.9 copy-start.34
  135.4 2.8 %copy-start.2 = (f32[6,16,32,128]{3,2,1,0:T(8,128)S(1)}, f32[6,16,32,128]{3,2,1,0:T(8,128)}, u32[]{:S(2)}) copy-start(f32[6,16,32,128]{3,2,1,0:T(8,128)} %fusion) | copy-start | bytes 4718596
  136.1 8.3 %copy-start.33 = (f32[46,142]{1,0:T(8,128)S(1)}, f32[46,142]{1,0:T(8,128)}, u32[]{:S(2)}) copy-start(f32[46,142]{1,0:T(8,128)} %slice.1353) | copy-start | bytes 78388
  136.3 8.4 %copy-start.32 = (f32[44,140]{1,0:T(8,128)S(1)}, f32[44,140]{1,0:T(8,128)}, u32[]{:S(2)}) copy-start(f32[44,140]{1,0:T(8,128)} %slice.1361) | copy-start | bytes 73924
  136.3 7.9 %collective-permute-start.16 = (f32[3,48,144]{2,1,0:T(8,128)S(1)}, f32[3,48,144]{2,1,0:T(8,128)S(1)}, u32[]{:S(2)}, u32[]{:S(2)}) collective-permute-start(f32[3,48,144]{2,1,0:T(8,128)S(1)} %fusion.236), channel_id=1, source_target_pairs={{0,8},{8,16},{16,24},{1,9},{9,17},{17,25},{2,10},{10,18},{18,26},{... | collective-permute-start | bytes 248840 | tf_op jit(solution)/shard_map/ppermute | solution.py:30
  138.5 6.5 %copy-start.31 = (f32[42,138]{1,0:T(8,128)S(1)}, f32[42,138]{1,0:T(8,128)}, u32[]{:S(2)}) copy-start(f32[42,138]{1,0:T(8,128)} %slice.1369) | copy-start | bytes 69556
  144.4 0.9 copy-start.37
  144.7 0.8 copy-start.36
  145.0 0.8 copy-start.35
  146.0 1.5 copy-start.1
  146.0 1.7 %copy-start.5 = (f32[3,8,2,32,128]{4,3,2,1,0:T(8,128)S(1)}, f32[3,8,2,32,128]{4,3,2,1,0:T(8,128)}, u32[]{:S(2)}) copy-start(f32[3,8,2,32,128]{4,3,2,1,0:T(8,128)} %fusion.302) | copy-start | bytes 2359300
  146.0 1.7 %copy-start.7 = (f32[16,32,128]{2,1,0:T(8,128)S(1)}, f32[16,32,128]{2,1,0:T(8,128)}, u32[]{:S(2)}) copy-start(f32[16,32,128]{2,1,0:T(8,128)} %fusion.1) | copy-start | bytes 786436
  146.0 1.8 %copy-start.8 = (f32[16,32,128]{2,1,0:T(8,128)S(1)}, f32[16,32,128]{2,1,0:T(8,128)}, u32[]{:S(2)}) copy-start(f32[16,32,128]{2,1,0:T(8,128)} %get-tuple-element.37) | copy-start | bytes 786436
  148.4 3.0 %collective-permute-start.17 = (f32[3,2,128]{2,1,0:T(2,128)S(1)}, f32[3,2,128]{2,1,0:T(2,128)S(1)}, u32[]{:S(2)}, u32[]{:S(2)}) collective-permute-start(f32[3,2,128]{2,1,0:T(2,128)S(1)} %bitcast.560), channel_id=1, source_target_pairs={{0,2},{2,0},{4,6},{6,4},{1,3},{3,1},{5,7},{7,5},{8,10},{10,8},{12,... | collective-permute-start | bytes 9224 | tf_op jit(solution)/shard_map/ppermute | solution.py:40
  149.0 3.9 %collective-permute-start.20 = (f32[1,1,128]{2,1,0:T(1,128)S(1)}, f32[1,1,128]{2,1,0:T(1,128)S(1)}, u32[]{:S(2)}, u32[]{:S(2)}) collective-permute-start(f32[1,1,128]{2,1,0:T(1,128)S(1)} %fusion.286), channel_id=1, source_target_pairs={{0,4},{4,0},{2,6},{6,2},{1,5},{5,1},{3,7},{7,3},{8,12},{12,8},{10,... | collective-permute-start | bytes 1544 | tf_op jit(solution)/shard_map/ppermute | solution.py:40
  151.4 3.6 %collective-permute-start.19 = (f32[3,1,128]{2,1,0:T(1,128)S(1)}, f32[3,1,128]{2,1,0:T(1,128)S(1)}, u32[]{:S(2)}, u32[]{:S(2)}) collective-permute-start(f32[3,1,128]{2,1,0:T(1,128)S(1)} %fusion.281), channel_id=1, source_target_pairs={{0,4},{4,0},{2,6},{6,2},{1,5},{5,1},{3,7},{7,3},{8,12},{12,8},{10,... | collective-permute-start | bytes 4616 | tf_op jit(solution)/shard_map/ppermute | solution.py:40

commit v3 on v2

--- a/solution.py
+++ b/solution.py
@@ -106,7 +106,14 @@
     return block
 
 
-def propagate(current, border_in, depth_rim, plane_inside, brick_a, brick_v, light_step):
+def plane_mask(border, brick_a, brick_v):
+    return (
+        rim_mask(lax.axis_index("across"), lax.axis_size("across"), brick_a, border)[:, None]
+        * rim_mask(lax.axis_index("view"), lax.axis_size("view"), brick_v, border)[None, :]
+    )
+
+
+def propagate(current, border_in, depth_rim, brick_a, brick_v, light_step):
     widest = (depth_rim.shape[2] - brick_a) // 2
     starts = []
     for slab_num in range(SLABS):
@@ -128,15 +135,7 @@
             + current[:, 1:-1, 2:]
             - 4.0 * centre
         )
-        inner = border - 1
-        offset = widest - inner
-        current = (
-            current
-            * plane_inside[
-                offset : offset + brick_a + 2 * inner,
-                offset : offset + brick_v + 2 * inner,
-            ][None]
-        )
+        current = current * plane_mask(border - 1, brick_a, brick_v)[None]
     return (current, jnp.stack(starts, axis=1))
 
 
@@ -172,18 +171,16 @@
     running = jnp.cumsum(extinct_slabs, axis=2) - extinct_slabs
     slab_depth = jnp.sum(extinct_slabs, axis=2)
     widest = SLABS * n_light
-    depth_rim = halo(halo(slab_depth, "across", 2, widest), "view", 3, widest)
-    sun_rim = halo(halo(sunlight, "across", 1, widest), "view", 2, widest)
-    plane_inside = (
-        rim_mask(across_idx, n_across, brick_a, widest)[:, None]
-        * rim_mask(view_idx, n_view, brick_v, widest)[None, :]
-    )
+    both = jnp.concatenate([slab_depth, sunlight[:, None]], axis=1)
+    both_rim = halo(halo(both, "across", 2, widest), "view", 3, widest)
+    depth_rim = both_rim[:, :SLABS]
+    sun_rim = both_rim[:, SLABS]
     starts = None
     incoming = sun_rim
     for section_num in range(n_light):
         border = SLABS * (n_light - section_num)
         outgoing, starts = propagate(
-            incoming, border, depth_rim, plane_inside, brick_a, brick_v, light_step
+            incoming, border, depth_rim, brick_a, brick_v, light_step
         )
         if section_num + 1 < n_light:
             arrived = from_behind(outgoing, "light", 1)

time: 158 us -> 149 us (0.943)
  local copies, waits for them, and re-layouts: 40.6 us -> 13.7 us
  other arithmetic: 47 us -> 69.7 us
  starting transfers between devices: 53.7 us -> 45.1 us
  waiting for transfers between devices: 12.4 us -> 16.8 us
    slice x30 -> x0, local copies, waits for them, and re-layouts: 20.7 us -> none  [propagate(): plane_inside[offset:offset + brick_a + 2 * inner, offset:offset + brick_v...]
    mul x4 -> x34, other arithmetic: 0.9 us -> 21.2 us  [the longest x31 19.7 us: plane_mask(): rim_mask(lax.axis_index('across'), lax.axis_size('across'), brick_a, border)]
    ppermute x4 -> x2, starting transfers between devices: 21 us -> 10.2 us  [halo(): lows.insert(0, lax.ppermute(low, axis, forward))]
    ppermute x4, starting transfers between devices: 4.19 us -> 7.76 us  [from_partner(): return lax.ppermute(block, axis, route)]
    ppermute x3, waiting for transfers between devices: 1.52 us -> 4.77 us  [padded_2(): lax.ppermute(lax.slice_in_dim(block, 0, width, axis=dim), axis, backward)]
    ppermute x4 -> x2, starting transfers between devices: 5.31 us -> 2.56 us  [halo(): lax.ppermute(lax.slice_in_dim(block, 0, need, axis=dim), axis, backward)]
    slice x3 -> x2, local copies, waits for them, and re-layouts: 4.26 us -> 1.68 us  [halo(): low = lax.slice_in_dim(block, size - need, None, axis=dim)]
    mul x1, other arithmetic: 2.36 us -> 4.67 us  [shards(): tensor_rim = structure(padded) * inside[None]]
  transfers between devices with their start and end apart: 21 -> 17, of which waited for: 5 -> 6; matrix products, arithmetic and copies ran while one was open for 41% -> 35% of each run, Pallas kernels for 0% -> 0%
where the time goes in v3:
time: 149 us; the launch traced here: 148 us
  other arithmetic  69.7 us (47%)
  starting transfers between devices  45.1 us (30%)
  waiting for transfers between devices  16.8 us (11%)
  local copies, waits for them, and re-layouts  13.7 us (9%)
    mul x31, other arithmetic, plane_mask(): rim_mask(lax.axis_index('across'), lax.axis_size('across'), brick_a, border)  19.7 us
    mul x1, other arithmetic, shade_from(): (2.0 * centre + tensor[:, 2:, 1:-1, 1:-1] + tensor[:, :-2, 1:-1, 1:-1] +...  12.2 us
    mul x31, other arithmetic, propagate(): current = current * jnp.exp(-light_step * depth_here)  10.8 us
    ppermute x2, starting transfers between devices, halo(): lows.insert(0, lax.ppermute(low, axis, forward))  10.2 us
    ppermute x3, starting transfers between devices, padded_2(): lax.ppermute(lax.slice_in_dim(block, block.shape[dim] - width, None, axis...  10.1 us
    ppermute x3, waiting for transfers between devices, from_behind(): lax.ppermute(value, axis, [(source, source + steps) for source in range(l...  9.58 us
    ppermute x3, starting transfers between devices, from_behind(): lax.ppermute(value, axis, [(source, source + steps) for source in range(l...  9.36 us
    ppermute x4, starting transfers between devices, from_partner(): return lax.ppermute(block, axis, route)  7.76 us
  transfers between devices with their start and end apart: 17, of which 6 were waited for; matrix products, arithmetic and copies ran while one was open for 35% of the time, Pallas kernels for 0%

profile of v3, /device:TPU:16, one launch (start us, length us, event | category | flops | bytes accessed | tf_op | source)
XLA Modules:
  0.0 147.6 jit_solution(4988666941793730282)
XLA Ops:
  0.0 0.7 pad_maximum_fusion.14
  1.2 1.6 %broadcast_compare_fusion.14 = (pred[16,32,128]{2,1,0:T(8,128)(4,1)S(1)}, pred[16,32,128]{2,1,0:T(8,128)(4,1)S(1)}, pred[16,32,128]{2,1,0:T(8,128)(4,1)S(1)}, pr...) fusion(s32[16,32,128]{2,1,0:T(8,128)} %param.7), kind=kLoop, calls=%fused_computation.400 | loop fusion | flops 983040 | bytes 1245184 | tf_op jit(solution)/shard_map/eq | solution.py:167
  2.8 2.6 %select_select_fusion = f32[7,16,32,128]{3,2,1,0:T(8,128)S(1)} fusion(f32[7]{0:T(128)S(1)} %get-tuple-element.6, f32[7]{0:T(128)S(1)} %get-tuple-element.7, f32[7]{0:T(128)S(1)} %get-tuple-element.8, f32[7]{0:T(128)S(1)} %get-tuple-element.9, f32[7]{0:T(128)S(1)} %get-tuple-element.10, f32[7]{0:T(128)S(1)} %get-tuple-element.11, f32[7]{0:T(128)S(1)} %get-tuple-element.12, ...), kind=kLoop, calls=%fused_computation.2 | loop fusion | flops 6881280 | bytes 2818496 | tf_op jit(solution)/shard_map/jit(_where)/select_n | solution.py:166
  6.2 0.8 pad_maximum_fusion.9
  7.0 4.2 %collective-permute-start.6 = (f32[3,9,32,128]{3,2,1,0:T(8,128)}, f32[3,9,32,128]{3,2,1,0:T(8,128)}, u32[]{:S(2)}, u32[]{:S(2)}) collective-permute-start(f32[3,9,32,128]{3,2,1,0:T(8,128)} %pad_maximum_fusion.9), channel_id=1, source_target_pairs={{0,1},{2,3},{4,5},{6,7},{8,9},{10,11},{12,13},{14,15},{16,17},{18,... | collective-permute-start | bytes 1327112 | tf_op jit(solution)/shard_map/ppermute | solution.py:98
  11.2 1.3 collective-permute-start.7
  13.2 3.5 %collective-permute-start = (f32[2,32,128]{2,1,0:T(8,128)}, f32[2,32,128]{2,1,0:T(8,128)}, u32[]{:S(2)}, u32[]{:S(2)}) collective-permute-start(f32[2,32,128]{2,1,0:T(8,128)} %get-tuple-element.45), channel_id=1, source_target_pairs={{0,8},{8,16},{16,24},{1,9},{9,17},{17,25},{2,10},{10,18},{18,26},{... | collective-permute-start | bytes 98312 | tf_op jit(solution)/shard_map/ppermute | solution.py:19
  16.6 2.4 %collective-permute-start.1 = (f32[2,32,128]{2,1,0:T(8,128)}, f32[2,32,128]{2,1,0:T(8,128)S(1)}, u32[]{:S(2)}, u32[]{:S(2)}) collective-permute-start(f32[2,32,128]{2,1,0:T(8,128)} %get-tuple-element.44), channel_id=1, source_target_pairs={{8,0},{16,8},{24,16},{9,1},{17,9},{25,17},{10,2},{18,10},{26,18},{... | collective-permute-start | bytes 98312 | tf_op jit(solution)/shard_map/ppermute | solution.py:22
  19.0 1.0 fusion.301
  20.0 1.0 fusion.1
  21.1 1.0 broadcast_multiply_fusion.1
  23.2 0.7 broadcast_multiply_fusion.2
  24.0 0.7 broadcast_multiply_fusion.8
  24.7 0.7 broadcast_multiply_fusion.7
  25.4 0.7 broadcast_multiply_fusion.6
  26.1 0.7 broadcast_multiply_fusion.5
  26.8 0.7 broadcast_multiply_fusion.12
  27.5 0.7 broadcast_multiply_fusion.11
  28.2 0.7 broadcast_multiply_fusion.10
  28.9 0.7 broadcast_multiply_fusion.9
  29.6 0.7 broadcast_multiply_fusion.16
  30.3 0.7 broadcast_multiply_fusion.15
  31.1 0.7 broadcast_multiply_fusion.14
  31.7 0.7 broadcast_multiply_fusion.13
  32.4 0.7 broadcast_multiply_fusion.20
  33.1 0.7 broadcast_multiply_fusion.19
  34.5 0.7 broadcast_multiply_fusion.17
  35.2 0.7 broadcast_multiply_fusion.24
  37.3 0.7 broadcast_multiply_fusion.21
  38.7 0.7 broadcast_multiply_fusion.27
  43.5 0.8 constant_dynamic-update-slice_fusion.2
  44.2 0.8 exponential_subtract_fusion
  45.1 1.3 collective-permute-start.2
  46.5 1.3 collective-permute-start.3
  47.9 2.9 %collective-permute-start.14 = (f32[1,2,128]{2,1,0:T(2,128)S(1)}, f32[1,2,128]{2,1,0:T(2,128)S(1)}, u32[]{:S(2)}, u32[]{:S(2)}) collective-permute-start(f32[1,2,128]{2,1,0:T(2,128)S(1)} %bitcast.569), channel_id=1, source_target_pairs={{0,2},{2,0},{4,6},{6,4},{1,3},{3,1},{5,7},{7,5},{8,10},{10,8},{12,... | collective-permute-start | bytes 3080 | tf_op jit(solution)/shard_map/ppermute | solution.py:40
  50.7 1.0 collective-permute-done.3
  51.9 5.3 %collective-permute-start.4 = (f32[20,2,132]{2,1,0:T(2,128)S(1)}, f32[20,2,132]{2,1,0:T(2,128)S(1)}, u32[]{:S(2)}, u32[]{:S(2)}) collective-permute-start(f32[20,2,132]{2,1,0:T(2,128)S(1)} %get-tuple-element.39), channel_id=1, source_target_pairs={{0,1},{2,3},{4,5},{6,7},{8,9},{10,11},{12,13},{14,15},{16,17},{18,... | collective-permute-start | bytes 63368 | tf_op jit(solution)/shard_map/ppermute | solution.py:19
  57.2 1.5 collective-permute-start.5
  59.3 3.8 %collective-permute-done.5 = f32[20,2,132]{2,1,0:T(2,128)S(1)} collective-permute-done((f32[20,2,132]{2,1,0:T(2,128)S(1)}, f32[20,2,132]{2,1,0:T(2,128)S(1)}, u32[]{:S(2)}, u32[]{:S(2)}) %collective-permute-start.5) | collective-permute-done | bytes 21152 | tf_op jit(solution)/shard_map/ppermute | solution.py:22
  63.9 0.8 bitcast_dynamic-update-slice_fusion.4
  65.1 1.2 bitcast_dynamic-update-slice_fusion.2
  66.9 1.0 bitcast_dynamic-update-slice_fusion
  68.0 2.1 %copy-done.3 = f32[6,18,34,130]{3,2,1,0:T(8,128)} copy-done((f32[6,18,34,130]{3,2,1,0:T(8,128)}, f32[6,18,34,130]{3,2,1,0:T(8,128)S(1)}, u32[]{:S(2)}) %copy-start.3) | copy-done | bytes 1909464
  70.1 1.2 pad_maximum_fusion.1
  71.8 1.2 copy.33
  73.0 6.0 %collective-permute-start.8 = (f32[3,9,96,32]{2,3,1,0:T(8,128)}, f32[3,9,96,32]{2,3,1,0:T(8,128)S(1)}, u32[]{:S(2)}, u32[]{:S(2)}) collective-permute-start(f32[3,9,96,32]{2,3,1,0:T(8,128)} %copy.33), channel_id=1, source_target_pairs={{0,2},{2,4},{4,6},{1,3},{3,5},{5,7},{8,10},{10,12},{12,14},{9,11},... | collective-permute-start | bytes 995336 | tf_op jit(solution)/shard_map/ppermute | solution.py:98
  79.0 1.2 copy.34
  80.2 1.3 collective-permute-start.9
  81.5 4.7 %broadcast_multiply_fusion = f32[6,18,34,130]{3,2,1,0:T(8,128)} fusion(f32[6,18,34,130]{3,2,1,0:T(8,128)} %copy-done.3, f32[18,34,130]{2,1,0:T(8,128)S(1)} %copy-done.6), kind=kLoop, calls=%fused_computation.1 | loop fusion | flops 477360 | bytes 4137120 | tf_op jit(solution)/shard_map/mul | solution.py:161
  86.1 1.5 %copy.35 = f32[3,9,96,32]{3,2,1,0:T(8,128)} copy(f32[3,9,96,32]{2,3,1,0:T(8,128)S(1)} %collective-permute-done.8) | data formatting | bytes 663552 | tf_op jit(solution)/shard_map/ppermute | solution.py:98
  87.7 1.5 %copy.36 = f32[3,9,96,32]{3,2,1,0:T(8,128)} copy(f32[3,9,96,32]{2,3,1,0:T(8,128)S(1)} %collective-permute-done.9) | data formatting | bytes 663552 | tf_op jit(solution)/shard_map/ppermute | solution.py:99
  89.2 3.1 %pad_maximum_fusion = f32[3,9,96,192]{3,2,1,0:T(8,128)S(1)} fusion(f32[3,9,96,32]{3,2,1,0:T(8,128)} %copy.36, f32[3,9,32,128]{3,2,1,0:T(8,128)} %collective-permute-done.7, f32[3,1,32,128]{3,2,1,0:T(8,128)S(1)} %bitcast.559, f32[3,8,32,128]{3,2,1,0:T(8,128)S(1)} %reduce_sum.27, f32[3,9,32,128]{3,2,1,0:T(8,128)} %collective-permute-done.6, f32[3,9,96,32]{3,2,1,0:T(8,128)} %copy.35), kind=kLoop, calls=%fused_computation | loop fusion | flops 2488320 | bytes 3981312 | tf_op jit(solution)/shard_map/concatenate | solution.py:100
  95.9 3.8 %collective-permute-start.10 = (f32[3,80,176]{2,1,0:T(8,128)S(1)}, f32[3,80,176]{2,1,0:T(8,128)S(1)}, u32[]{:S(2)}, u32[]{:S(2)}) collective-permute-start(f32[3,80,176]{2,1,0:T(8,128)S(1)} %fusion.108), channel_id=1, source_target_pairs={{0,8},{8,16},{16,24},{1,9},{9,17},{17,25},{2,10},{10,18},{18,26},{... | collective-permute-start | bytes 506888 | tf_op jit(solution)/shard_map/ppermute | solution.py:30
  99.8 4.3 %collective-permute-done.10 = f32[3,80,176]{2,1,0:T(8,128)S(1)} collective-permute-done((f32[3,80,176]{2,1,0:T(8,128)S(1)}, f32[3,80,176]{2,1,0:T(8,128)S(1)}, u32[]{:S(2)}, u32[]{:S(2)}) %collective-permute-start.10) | collective-permute-done | bytes 168992 | tf_op jit(solution)/shard_map/ppermute | solution.py:30
  107.4 1.0 fusion.172
  108.4 3.6 %collective-permute-start.11 = (f32[3,64,160]{2,1,0:T(8,128)}, f32[3,64,160]{2,1,0:T(8,128)S(1)}, u32[]{:S(2)}, u32[]{:S(2)}) collective-permute-start(f32[3,64,160]{2,1,0:T(8,128)} %fusion.172), channel_id=1, source_target_pairs={{0,8},{8,16},{16,24},{1,9},{9,17},{17,25},{2,10},{10,18},{18,26},{... | collective-permute-start | bytes 368648 | tf_op jit(solution)/shard_map/ppermute | solution.py:30
  112.0 12.2 %fusion = f32[6,16,32,128]{3,2,1,0:T(8,128)} fusion(f32[6,18,34,130]{3,2,1,0:T(8,128)} %broadcast_multiply_fusion), kind=kLoop, calls=%fused_computation.4 | loop fusion | flops 3145728 | bytes 12582912 | tf_op jit(solution)/shard_map/mul | solution.py:45
  124.2 1.1 fusion.168
  127.9 1.9 %collective-permute-start.12 = (f32[3,48,144]{2,1,0:T(8,128)S(1)}, f32[3,48,144]{2,1,0:T(8,128)S(1)}, u32[]{:S(2)}, u32[]{:S(2)}) collective-permute-start(f32[3,48,144]{2,1,0:T(8,128)S(1)} %fusion.236), channel_id=1, source_target_pairs={{0,8},{8,16},{16,24},{1,9},{9,17},{17,25},{2,10},{10,18},{18,26},{... | collective-permute-start | bytes 248840 | tf_op jit(solution)/shard_map/ppermute | solution.py:30
  130.1 5.2 %collective-permute-done.12 = f32[3,48,144]{2,1,0:T(8,128)S(1)} collective-permute-done((f32[3,48,144]{2,1,0:T(8,128)S(1)}, f32[3,48,144]{2,1,0:T(8,128)S(1)}, u32[]{:S(2)}, u32[]{:S(2)}) %collective-permute-start.12) | collective-permute-done | bytes 82976 | tf_op jit(solution)/shard_map/ppermute | solution.py:30
  139.5 1.1 collective-permute-start.13
  140.6 2.6 %collective-permute-start.16 = (f32[1,1,128]{2,1,0:T(1,128)S(1)}, f32[1,1,128]{2,1,0:T(1,128)S(1)}, u32[]{:S(2)}, u32[]{:S(2)}) collective-permute-start(f32[1,1,128]{2,1,0:T(1,128)S(1)} %fusion.286), channel_id=1, source_target_pairs={{0,4},{4,0},{2,6},{6,2},{1,5},{5,1},{3,7},{7,3},{8,12},{12,8},{10,... | collective-permute-start | bytes 1544 | tf_op jit(solution)/shard_map/ppermute | solution.py:40
  143.3 1.1 collective-permute-start.15
  144.9 2.0 %collective-permute-done.15 = f32[3,1,128]{2,1,0:T(1,128)S(1)} collective-permute-done((f32[3,1,128]{2,1,0:T(1,128)S(1)}, f32[3,1,128]{2,1,0:T(1,128)S(1)}, u32[]{:S(2)}, u32[]{:S(2)}) %collective-permute-start.15) | collective-permute-done | bytes 1568 | tf_op jit(solution)/shard_map/ppermute | solution.py:40
  (246 shorter events, 27.3 us)
Async XLA Ops:
  1.1 4.2 %copy-start.4 = (f32[16,32,128]{2,1,0:T(8,128)S(1)}, f32[16,32,128]{2,1,0:T(8,128)}, u32[]{:S(2)}) copy-start(f32[16,32,128]{2,1,0:T(8,128)} %param.6) | copy-start | bytes 786436
  5.4 38.8 %copy-start = (f32[7,16,32,128]{3,2,1,0:T(8,128)}, f32[7,16,32,128]{3,2,1,0:T(8,128)S(1)}, u32[]{:S(2)}) copy-start(f32[7,16,32,128]{3,2,1,0:T(8,128)S(1)} %select_select_fusion) | copy-start | bytes 5505028
  5.4 0.8 copy-start.11
  7.0 60.9 %collective-permute-start.6 = (f32[3,9,32,128]{3,2,1,0:T(8,128)}, f32[3,9,32,128]{3,2,1,0:T(8,128)}, u32[]{:S(2)}, u32[]{:S(2)}) collective-permute-start(f32[3,9,32,128]{3,2,1,0:T(8,128)} %pad_maximum_fusion.9), channel_id=1, source_target_pairs={{0,1},{2,3},{4,5},{6,7},{8,9},{10,11},{12,13},{14,15},{16,17},{18,... | collective-permute-start | bytes 1327112 | tf_op jit(solution)/shard_map/ppermute | solution.py:98
  11.2 58.8 %collective-permute-start.7 = (f32[3,9,32,128]{3,2,1,0:T(8,128)}, f32[3,9,32,128]{3,2,1,0:T(8,128)}, u32[]{:S(2)}, u32[]{:S(2)}) collective-permute-start(f32[3,9,32,128]{3,2,1,0:T(8,128)} %pad_maximum_fusion.9), channel_id=1, source_target_pairs={{1,0},{3,2},{5,4},{7,6},{9,8},{11,10},{13,12},{15,14},{17,16},{19,... | collective-permute-start | bytes 1327112 | tf_op jit(solution)/shard_map/ppermute | solution.py:99
  13.2 30.3 %collective-permute-start = (f32[2,32,128]{2,1,0:T(8,128)}, f32[2,32,128]{2,1,0:T(8,128)}, u32[]{:S(2)}, u32[]{:S(2)}) collective-permute-start(f32[2,32,128]{2,1,0:T(8,128)} %get-tuple-element.45), channel_id=1, source_target_pairs={{0,8},{8,16},{16,24},{1,9},{9,17},{17,25},{2,10},{10,18},{18,26},{... | collective-permute-start | bytes 98312 | tf_op jit(solution)/shard_map/ppermute | solution.py:19
  16.6 28.3 %collective-permute-start.1 = (f32[2,32,128]{2,1,0:T(8,128)}, f32[2,32,128]{2,1,0:T(8,128)S(1)}, u32[]{:S(2)}, u32[]{:S(2)}) collective-permute-start(f32[2,32,128]{2,1,0:T(8,128)} %get-tuple-element.44), channel_id=1, source_target_pairs={{8,0},{16,8},{24,16},{9,1},{17,9},{25,17},{10,2},{18,10},{26,18},{... | collective-permute-start | bytes 98312 | tf_op jit(solution)/shard_map/ppermute | solution.py:22
  45.1 5.6 %collective-permute-start.2 = (f32[20,32,2]{2,1,0:T(8,128)S(1)}, f32[20,32,2]{2,1,0:T(8,128)S(1)}, u32[]{:S(2)}, u32[]{:S(2)}) collective-permute-start(f32[20,32,2]{2,1,0:T(8,128)S(1)} %get-tuple-element.41), channel_id=1, source_target_pairs={{0,2},{2,4},{4,6},{1,3},{3,5},{5,7},{8,10},{10,12},{12,14},{9,11},... | collective-permute-start | bytes 15368 | tf_op jit(solution)/shard_map/ppermute | solution.py:19
  46.5 5.2 %collective-permute-start.3 = (f32[20,32,2]{2,1,0:T(8,128)S(1)}, f32[20,32,2]{2,1,0:T(8,128)S(1)}, u32[]{:S(2)}, u32[]{:S(2)}) collective-permute-start(f32[20,32,2]{2,1,0:T(8,128)S(1)} %get-tuple-element.42), channel_id=1, source_target_pairs={{2,0},{4,2},{6,4},{3,1},{5,3},{7,5},{10,8},{12,10},{14,12},{11,9},... | collective-permute-start | bytes 15368 | tf_op jit(solution)/shard_map/ppermute | solution.py:22
  47.9 10.8 %collective-permute-start.14 = (f32[1,2,128]{2,1,0:T(2,128)S(1)}, f32[1,2,128]{2,1,0:T(2,128)S(1)}, u32[]{:S(2)}, u32[]{:S(2)}) collective-permute-start(f32[1,2,128]{2,1,0:T(2,128)S(1)} %bitcast.569), channel_id=1, source_target_pairs={{0,2},{2,0},{4,6},{6,4},{1,3},{3,1},{5,7},{7,5},{8,10},{10,8},{12,... | collective-permute-start | bytes 3080 | tf_op jit(solution)/shard_map/ppermute | solution.py:40
  51.9 7.4 %collective-permute-start.4 = (f32[20,2,132]{2,1,0:T(2,128)S(1)}, f32[20,2,132]{2,1,0:T(2,128)S(1)}, u32[]{:S(2)}, u32[]{:S(2)}) collective-permute-start(f32[20,2,132]{2,1,0:T(2,128)S(1)} %get-tuple-element.39), channel_id=1, source_target_pairs={{0,1},{2,3},{4,5},{6,7},{8,9},{10,11},{12,13},{14,15},{16,17},{18,... | collective-permute-start | bytes 63368 | tf_op jit(solution)/shard_map/ppermute | solution.py:19
  57.2 5.9 %collective-permute-start.5 = (f32[20,2,132]{2,1,0:T(2,128)S(1)}, f32[20,2,132]{2,1,0:T(2,128)S(1)}, u32[]{:S(2)}, u32[]{:S(2)}) collective-permute-start(f32[20,2,132]{2,1,0:T(2,128)S(1)} %get-tuple-element.40), channel_id=1, source_target_pairs={{1,0},{3,2},{5,4},{7,6},{9,8},{11,10},{13,12},{15,14},{17,16},{19,... | collective-permute-start | bytes 63368 | tf_op jit(solution)/shard_map/ppermute | solution.py:22
  68.0 2.1 %copy-start.3 = (f32[6,18,34,130]{3,2,1,0:T(8,128)}, f32[6,18,34,130]{3,2,1,0:T(8,128)S(1)}, u32[]{:S(2)}) copy-start(f32[6,18,34,130]{3,2,1,0:T(8,128)S(1)} %bitcast_dynamic-update-slice_fusion) | copy-start | bytes 5728324
  73.0 8.5 %copy-start.6 = (f32[18,34,130]{2,1,0:T(8,128)S(1)}, f32[18,34,130]{2,1,0:T(8,128)}, u32[]{:S(2)}) copy-start(f32[18,34,130]{2,1,0:T(8,128)} %broadcast_multiply_fusion.1) | copy-start | bytes 954724
  73.0 13.1 %collective-permute-start.8 = (f32[3,9,96,32]{2,3,1,0:T(8,128)}, f32[3,9,96,32]{2,3,1,0:T(8,128)S(1)}, u32[]{:S(2)}, u32[]{:S(2)}) collective-permute-start(f32[3,9,96,32]{2,3,1,0:T(8,128)} %copy.33), channel_id=1, source_target_pairs={{0,2},{2,4},{4,6},{1,3},{3,5},{5,7},{8,10},{10,12},{12,14},{9,11},... | collective-permute-start | bytes 995336 | tf_op jit(solution)/shard_map/ppermute | solution.py:98
  80.2 7.5 %collective-permute-start.9 = (f32[3,9,96,32]{2,3,1,0:T(8,128)}, f32[3,9,96,32]{2,3,1,0:T(8,128)S(1)}, u32[]{:S(2)}, u32[]{:S(2)}) collective-permute-start(f32[3,9,96,32]{2,3,1,0:T(8,128)} %copy.34), channel_id=1, source_target_pairs={{2,0},{4,2},{6,4},{3,1},{5,3},{7,5},{10,8},{12,10},{14,12},{11,9},... | collective-permute-start | bytes 995336 | tf_op jit(solution)/shard_map/ppermute | solution.py:99
  92.4 0.9 copy-start.12
  92.8 0.9 copy-start.13
  93.3 0.9 copy-start.14
  93.8 0.9 copy-start.15
  94.2 0.9 copy-start.16
  94.7 0.9 copy-start.20
  95.6 8.8 %copy-start.17 = (f32[78,174]{1,0:T(8,128)S(1)}, f32[78,174]{1,0:T(8,128)}, u32[]{:S(2)}) copy-start(f32[78,174]{1,0:T(8,128)} %broadcast_multiply_fusion.11) | copy-start | bytes 162868
  95.9 8.9 %copy-start.18 = (f32[76,172]{1,0:T(8,128)S(1)}, f32[76,172]{1,0:T(8,128)}, u32[]{:S(2)}) copy-start(f32[76,172]{1,0:T(8,128)} %broadcast_multiply_fusion.10) | copy-start | bytes 156868
  95.9 8.2 %collective-permute-start.10 = (f32[3,80,176]{2,1,0:T(8,128)S(1)}, f32[3,80,176]{2,1,0:T(8,128)S(1)}, u32[]{:S(2)}, u32[]{:S(2)}) collective-permute-start(f32[3,80,176]{2,1,0:T(8,128)S(1)} %fusion.108), channel_id=1, source_target_pairs={{0,8},{8,16},{16,24},{1,9},{9,17},{17,25},{2,10},{10,18},{18,26},{... | collective-permute-start | bytes 506888 | tf_op jit(solution)/shard_map/ppermute | solution.py:30
  99.8 4.4 %copy-start.7 = (f32[3,96,192]{2,1,0:T(8,128)}, f32[3,96,192]{2,1,0:T(8,128)S(1)}, u32[]{:S(2)}) copy-start(f32[3,96,192]{2,1,0:T(8,128)S(1)} %slice_bitcast_fusion.4) | copy-start | bytes 663556
  104.4 0.9 copy-start.19
  104.8 0.9 copy-start.21
  105.2 0.9 copy-start.22
  105.7 0.9 copy-start.23
  106.1 0.9 copy-start.24
  106.6 0.8 copy-start.28
  108.4 17.0 %copy-start.25 = (f32[62,158]{1,0:T(8,128)S(1)}, f32[62,158]{1,0:T(8,128)}, u32[]{:S(2)}) copy-start(f32[62,158]{1,0:T(8,128)} %broadcast_multiply_fusion.19) | copy-start | bytes 117556
  108.4 15.8 %collective-permute-start.11 = (f32[3,64,160]{2,1,0:T(8,128)}, f32[3,64,160]{2,1,0:T(8,128)S(1)}, u32[]{:S(2)}, u32[]{:S(2)}) collective-permute-start(f32[3,64,160]{2,1,0:T(8,128)} %fusion.172), channel_id=1, source_target_pairs={{0,8},{8,16},{16,24},{1,9},{9,17},{17,25},{2,10},{10,18},{18,26},{... | collective-permute-start | bytes 368648 | tf_op jit(solution)/shard_map/ppermute | solution.py:30
  124.2 1.5 %copy-start.26 = (f32[60,156]{1,0:T(8,128)S(1)}, f32[60,156]{1,0:T(8,128)}, u32[]{:S(2)}) copy-start(f32[60,156]{1,0:T(8,128)} %broadcast_multiply_fusion.18) | copy-start | bytes 112324
  124.2 1.9 %copy-start.27 = (f32[58,154]{1,0:T(8,128)S(1)}, f32[58,154]{1,0:T(8,128)}, u32[]{:S(2)}) copy-start(f32[58,154]{1,0:T(8,128)} %broadcast_multiply_fusion.17) | copy-start | bytes 107188
  125.4 1.0 copy-start.29
  125.7 1.0 copy-start.30
  126.1 1.0 copy-start.31
  126.4 0.9 copy-start.32
  126.7 1.0 copy-start.36
  127.0 2.8 %copy-start.2 = (f32[6,16,32,128]{3,2,1,0:T(8,128)S(1)}, f32[6,16,32,128]{3,2,1,0:T(8,128)}, u32[]{:S(2)}) copy-start(f32[6,16,32,128]{3,2,1,0:T(8,128)} %fusion) | copy-start | bytes 4718596
  127.4 8.0 %copy-start.8 = (f32[3,96,192]{2,1,0:T(8,128)S(1)}, f32[3,96,192]{2,1,0:T(8,128)}, u32[]{:S(2)}) copy-start(f32[3,96,192]{2,1,0:T(8,128)} %copy-done.7) | copy-start | bytes 663556
  127.7 7.8 %copy-start.35 = (f32[46,142]{1,0:T(8,128)S(1)}, f32[46,142]{1,0:T(8,128)}, u32[]{:S(2)}) copy-start(f32[46,142]{1,0:T(8,128)} %broadcast_multiply_fusion.27) | copy-start | bytes 78388
  127.9 7.8 %copy-start.34 = (f32[44,140]{1,0:T(8,128)S(1)}, f32[44,140]{1,0:T(8,128)}, u32[]{:S(2)}) copy-start(f32[44,140]{1,0:T(8,128)} %broadcast_multiply_fusion.26) | copy-start | bytes 73924
  127.9 7.4 %collective-permute-start.12 = (f32[3,48,144]{2,1,0:T(8,128)S(1)}, f32[3,48,144]{2,1,0:T(8,128)S(1)}, u32[]{:S(2)}, u32[]{:S(2)}) collective-permute-start(f32[3,48,144]{2,1,0:T(8,128)S(1)} %fusion.236), channel_id=1, source_target_pairs={{0,8},{8,16},{16,24},{1,9},{9,17},{17,25},{2,10},{10,18},{18,26},{... | collective-permute-start | bytes 248840 | tf_op jit(solution)/shard_map/ppermute | solution.py:30
  130.1 6.0 %copy-start.33 = (f32[42,138]{1,0:T(8,128)S(1)}, f32[42,138]{1,0:T(8,128)}, u32[]{:S(2)}) copy-start(f32[42,138]{1,0:T(8,128)} %broadcast_multiply_fusion.25) | copy-start | bytes 69556
  135.5 0.9 copy-start.39
  135.8 0.8 copy-start.38
  136.0 0.8 copy-start.37
  136.6 1.3 copy-start.40
  137.1 1.5 %copy-start.1 = (f32[7,16,32,128]{3,2,1,0:T(8,128)S(1)}, f32[7,16,32,128]{3,2,1,0:T(8,128)}, u32[]{:S(2)}) copy-start(f32[7,16,32,128]{3,2,1,0:T(8,128)} %copy-done) | copy-start | bytes 5505028
  137.1 1.7 %copy-start.5 = (f32[3,8,2,32,128]{4,3,2,1,0:T(8,128)S(1)}, f32[3,8,2,32,128]{4,3,2,1,0:T(8,128)}, u32[]{:S(2)}) copy-start(f32[3,8,2,32,128]{4,3,2,1,0:T(8,128)} %fusion.301) | copy-start | bytes 2359300
  137.1 1.7 %copy-start.9 = (f32[16,32,128]{2,1,0:T(8,128)S(1)}, f32[16,32,128]{2,1,0:T(8,128)}, u32[]{:S(2)}) copy-start(f32[16,32,128]{2,1,0:T(8,128)} %fusion.1) | copy-start | bytes 786436
  137.1 1.8 %copy-start.10 = (f32[16,32,128]{2,1,0:T(8,128)S(1)}, f32[16,32,128]{2,1,0:T(8,128)}, u32[]{:S(2)}) copy-start(f32[16,32,128]{2,1,0:T(8,128)} %get-tuple-element.35) | copy-start | bytes 786436
  138.9 1.7 %copy-start.41 = (f32[1,1,2,128]{3,2,1,0:T(2,128)S(1)}, f32[1,1,2,128]{3,2,1,0:T(2,128)}, u32[]{:S(2)}) copy-start(f32[1,1,2,128]{3,2,1,0:T(2,128)} %get-tuple-element.69) | copy-start | bytes 3076
  138.9 4.4 %copy-start.42 = (f32[2,128]{1,0:T(2,128)S(1)}, f32[2,128]{1,0:T(2,128)}, u32[]{:S(2)}) copy-start(f32[2,128]{1,0:T(2,128)} %get-tuple-element.68) | copy-start | bytes 3076
  139.5 3.8 %collective-permute-start.13 = (f32[3,2,128]{2,1,0:T(2,128)S(1)}, f32[3,2,128]{2,1,0:T(2,128)S(1)}, u32[]{:S(2)}, u32[]{:S(2)}) collective-permute-start(f32[3,2,128]{2,1,0:T(2,128)S(1)} %bitcast.568), channel_id=1, source_target_pairs={{0,2},{2,0},{4,6},{6,4},{1,3},{3,1},{5,7},{7,5},{8,10},{10,8},{12,... | collective-permute-start | bytes 9224 | tf_op jit(solution)/shard_map/ppermute | solution.py:40
  140.6 4.2 %collective-permute-start.16 = (f32[1,1,128]{2,1,0:T(1,128)S(1)}, f32[1,1,128]{2,1,0:T(1,128)S(1)}, u32[]{:S(2)}, u32[]{:S(2)}) collective-permute-start(f32[1,1,128]{2,1,0:T(1,128)S(1)} %fusion.286), channel_id=1, source_target_pairs={{0,4},{4,0},{2,6},{6,2},{1,5},{5,1},{3,7},{7,3},{8,12},{12,8},{10,... | collective-permute-start | bytes 1544 | tf_op jit(solution)/shard_map/ppermute | solution.py:40
  143.3 3.6 %collective-permute-start.15 = (f32[3,1,128]{2,1,0:T(1,128)S(1)}, f32[3,1,128]{2,1,0:T(1,128)S(1)}, u32[]{:S(2)}, u32[]{:S(2)}) collective-permute-start(f32[3,1,128]{2,1,0:T(1,128)S(1)} %fusion.281), channel_id=1, source_target_pairs={{0,4},{4,0},{2,6},{6,2},{1,5},{5,1},{3,7},{7,3},{8,12},{12,8},{10,... | collective-permute-start | bytes 4616 | tf_op jit(solution)/shard_map/ppermute | solution.py:40

commit v4 on v3

--- a/solution.py
+++ b/solution.py
@@ -113,20 +113,20 @@
     )
 
 
-def propagate(current, border_in, depth_rim, brick_a, brick_v, light_step):
-    widest = (depth_rim.shape[2] - brick_a) // 2
+def propagate(current, border_in, fade_rim, brick_a, brick_v):
+    widest = (fade_rim.shape[2] - brick_a) // 2
     starts = []
     for slab_num in range(SLABS):
         border = border_in - slab_num
         starts.append(current[:, border : border + brick_a, border : border + brick_v])
         offset = widest - border
-        depth_here = depth_rim[
+        fade_here = fade_rim[
             :,
             slab_num,
             offset : offset + brick_a + 2 * border,
             offset : offset + brick_v + 2 * border,
         ]
-        current = current * jnp.exp(-light_step * depth_here)
+        current = current * fade_here
         centre = current[:, 1:-1, 1:-1]
         current = centre + BLUR * (
             current[:, :-2, 1:-1]
@@ -135,7 +135,6 @@
             + current[:, 1:-1, 2:]
             - 4.0 * centre
         )
-        current = current * plane_mask(border - 1, brick_a, brick_v)[None]
     return (current, jnp.stack(starts, axis=1))
 
 
@@ -173,14 +172,14 @@
     widest = SLABS * n_light
     both = jnp.concatenate([slab_depth, sunlight[:, None]], axis=1)
     both_rim = halo(halo(both, "across", 2, widest), "view", 3, widest)
-    depth_rim = both_rim[:, :SLABS]
     sun_rim = both_rim[:, SLABS]
+    fade_rim = jnp.exp(-light_step * both_rim[:, :SLABS]) * plane_mask(widest, brick_a, brick_v)
     starts = None
     incoming = sun_rim
     for section_num in range(n_light):
         border = SLABS * (n_light - section_num)
         outgoing, starts = propagate(
-            incoming, border, depth_rim, brick_a, brick_v, light_step
+            incoming, border, fade_rim, brick_a, brick_v
         )
         if section_num + 1 < n_light:
             arrived = from_behind(outgoing, "light", 1)

time: 149 us -> 131 us (0.88)
  other arithmetic: 69.7 us -> 48.3 us
  local copies, waits for them, and re-layouts: 13.7 us -> 19.5 us
    mul x31 -> x1, other arithmetic: 19.7 us -> 0.07 us  [plane_mask(): rim_mask(lax.axis_index('across'), lax.axis_size('across'), brick_a, border)]
    concatenate x2 -> x1, other arithmetic: 4.31 us -> 1.23 us  [halo(): block = jnp.concatenate(lows + [block] + highs, axis=dim)]
    slice x2, local copies, waits for them, and re-layouts: 1.68 us -> 4.52 us  [halo(): low = lax.slice_in_dim(block, size - need, None, axis=dim)]
    mul x1, other arithmetic: 4.67 us -> 2.35 us  [shards(): tensor_rim = structure(padded) * inside[None]]
    mul x34 -> x32, other arithmetic: 12.3 us -> 14.6 us  [the longest x31 11.6 us: propagate(): current = current * fade_here]
    ppermute x3, waiting for transfers between devices: 9.58 us -> 8.07 us  [from_behind(): lax.ppermute(value, axis, [(source, source + steps) for source in range(l...]
    unnamed x5 -> x6, other arithmetic: 3.4 us -> 4.27 us
    unnamed x94 -> x40, local copies, waits for them, and re-layouts: 5.43 us -> 4.72 us
  transfers between devices with their start and end apart: 17 -> 17, of which waited for: 6 -> 7; matrix products, arithmetic and copies ran while one was open for 35% -> 25% of each run, Pallas kernels for 0% -> 0%
where the time goes in v4:
time: 131 us; the launch traced here: 130 us
  other arithmetic  48.3 us (37%)
  starting transfers between devices  45.4 us (35%)
  local copies, waits for them, and re-layouts  19.5 us (15%)
  waiting for transfers between devices  16 us (12%)
    mul x1, other arithmetic, shade_from(): (2.0 * centre + tensor[:, 2:, 1:-1, 1:-1] + tensor[:, :-2, 1:-1, 1:-1] +...  12.2 us
    mul x31, other arithmetic, propagate(): current = current * fade_here  11.6 us
    ppermute x2, starting transfers between devices, halo(): lows.insert(0, lax.ppermute(low, axis, forward))  10.8 us
    ppermute x3, starting transfers between devices, from_behind(): lax.ppermute(value, axis, [(source, source + steps) for source in range(l...  10.4 us
    ppermute x3, starting transfers between devices, padded_2(): lax.ppermute(lax.slice_in_dim(block, block.shape[dim] - width, None, axis...  10.1 us
    ppermute x3, waiting for transfers between devices, from_behind(): lax.ppermute(value, axis, [(source, source + steps) for source in range(l...  8.07 us
    ppermute x4, starting transfers between devices, from_partner(): return lax.ppermute(block, axis, route)  6.34 us
    ppermute x3, waiting for transfers between devices, padded_2(): lax.ppermute(lax.slice_in_dim(block, 0, width, axis=dim), axis, backward)  5.2 us
  transfers between devices with their start and end apart: 17, of which 7 were waited for; matrix products, arithmetic and copies ran while one was open for 25% of the time, Pallas kernels for 0%

profile of v4, /device:TPU:16, one launch (start us, length us, event | category | flops | bytes accessed | tf_op | source)
XLA Modules:
  0.0 130.2 jit_solution(4763379276551325787)
XLA Ops:
  0.0 0.7 pad_maximum_fusion.18
  0.7 0.4 slice_reduce_fusion.15
  1.2 1.6 %broadcast_compare_fusion.14 = (pred[16,32,128]{2,1,0:T(8,128)(4,1)S(1)}, pred[16,32,128]{2,1,0:T(8,128)(4,1)S(1)}, pred[16,32,128]{2,1,0:T(8,128)(4,1)S(1)}, pr...) fusion(s32[16,32,128]{2,1,0:T(8,128)} %param.7), kind=kLoop, calls=%fused_computation.296 | loop fusion | flops 983040 | bytes 1245184 | tf_op jit(solution)/shard_map/eq | solution.py:166
  2.7 2.6 %select_select_fusion = f32[7,16,32,128]{3,2,1,0:T(8,128)S(1)} fusion(f32[7]{0:T(128)S(1)} %get-tuple-element.6, f32[7]{0:T(128)S(1)} %get-tuple-element.7, f32[7]{0:T(128)S(1)} %get-tuple-element.8, f32[7]{0:T(128)S(1)} %get-tuple-element.9, f32[7]{0:T(128)S(1)} %get-tuple-element.10, f32[7]{0:T(128)S(1)} %get-tuple-element.11, f32[7]{0:T(128)S(1)} %get-tuple-element.12, ...), kind=kLoop, calls=%fused_computation.9 | loop fusion | flops 6881280 | bytes 2818496 | tf_op jit(solution)/shard_map/jit(_where)/select_n | solution.py:165
  5.5 0.7 copy-done.12
  6.2 0.8 pad_maximum_fusion.13
  7.0 4.2 %collective-permute-start.6 = (f32[3,9,32,128]{3,2,1,0:T(8,128)}, f32[3,9,32,128]{3,2,1,0:T(8,128)}, u32[]{:S(2)}, u32[]{:S(2)}) collective-permute-start(f32[3,9,32,128]{3,2,1,0:T(8,128)} %pad_maximum_fusion.13), channel_id=1, source_target_pairs={{0,1},{2,3},{4,5},{6,7},{8,9},{10,11},{12,13},{14,15},{16,17},{18,... | collective-permute-start | bytes 1327112 | tf_op jit(solution)/shard_map/ppermute | solution.py:98
  11.2 1.3 collective-permute-start.7
  12.5 0.6 fusion.177
  13.2 3.5 %collective-permute-start = (f32[2,32,128]{2,1,0:T(8,128)}, f32[2,32,128]{2,1,0:T(8,128)}, u32[]{:S(2)}, u32[]{:S(2)}) collective-permute-start(f32[2,32,128]{2,1,0:T(8,128)} %get-tuple-element.47), channel_id=1, source_target_pairs={{0,8},{8,16},{16,24},{1,9},{9,17},{17,25},{2,10},{10,18},{18,26},{... | collective-permute-start | bytes 98312 | tf_op jit(solution)/shard_map/ppermute | solution.py:19
  16.6 2.4 %collective-permute-start.1 = (f32[2,32,128]{2,1,0:T(8,128)}, f32[2,32,128]{2,1,0:T(8,128)}, u32[]{:S(2)}, u32[]{:S(2)}) collective-permute-start(f32[2,32,128]{2,1,0:T(8,128)} %get-tuple-element.46), channel_id=1, source_target_pairs={{8,0},{16,8},{24,16},{9,1},{17,9},{25,17},{10,2},{18,10},{26,18},{... | collective-permute-start | bytes 98312 | tf_op jit(solution)/shard_map/ppermute | solution.py:22
  19.0 1.0 fusion.181
  20.5 1.0 broadcast_multiply_fusion.1
  21.6 0.8 constant_dynamic-update-slice_fusion.2
  22.4 0.8 exponential_subtract_fusion
  23.1 0.8 constant_dynamic-update-slice_fusion
  24.1 1.3 %collective-permute-start.2 = (f32[20,32,2]{2,1,0:T(8,128)S(1)}, f32[20,32,2]{2,1,0:T(8,128)S(1)}, u32[]{:S(2)}, u32[]{:S(2)}) collective-permute-start(f32[20,32,2]{2,1,0:T(8,128)S(1)} %get-tuple-element.43), channel_id=1, source_target_pairs={{0,2},{2,4},{4,6},{1,3},{3,5},{5,7},{8,10},{10,12},{12,14},{9,11},... | collective-permute-start | bytes 15368 | tf_op jit(solution)/shard_map/ppermute | solution.py:19
  25.4 1.3 collective-permute-start.3
  26.8 2.9 %collective-permute-start.14 = (f32[1,2,128]{2,1,0:T(2,128)S(1)}, f32[1,2,128]{2,1,0:T(2,128)S(1)}, u32[]{:S(2)}, u32[]{:S(2)}) collective-permute-start(f32[1,2,128]{2,1,0:T(2,128)S(1)} %bitcast.331), channel_id=1, source_target_pairs={{0,2},{2,0},{4,6},{6,4},{1,3},{3,1},{5,7},{7,5},{8,10},{10,8},{12,... | collective-permute-start | bytes 3080 | tf_op jit(solution)/shard_map/ppermute | solution.py:40
  29.7 1.0 collective-permute-done.3
  30.8 5.3 %collective-permute-start.4 = (f32[20,2,132]{2,1,0:T(2,128)S(1)}, f32[20,2,132]{2,1,0:T(2,128)S(1)}, u32[]{:S(2)}, u32[]{:S(2)}) collective-permute-start(f32[20,2,132]{2,1,0:T(2,128)S(1)} %get-tuple-element.41), channel_id=1, source_target_pairs={{0,1},{2,3},{4,5},{6,7},{8,9},{10,11},{12,13},{14,15},{16,17},{18,... | collective-permute-start | bytes 63368 | tf_op jit(solution)/shard_map/ppermute | solution.py:19
  36.2 1.3 collective-permute-start.5
  37.8 4.2 %collective-permute-done.5 = f32[20,2,132]{2,1,0:T(2,128)S(1)} collective-permute-done((f32[20,2,132]{2,1,0:T(2,128)S(1)}, f32[20,2,132]{2,1,0:T(2,128)S(1)}, u32[]{:S(2)}, u32[]{:S(2)}) %collective-permute-start.5) | collective-permute-done | bytes 21152 | tf_op jit(solution)/shard_map/ppermute | solution.py:22
  42.1 0.4 pad_maximum_fusion.6
  42.5 0.5 bitcast_dynamic-update-slice_fusion.5
  42.9 0.8 bitcast_dynamic-update-slice_fusion.4
  44.0 1.2 bitcast_dynamic-update-slice_fusion.2
  45.3 2.0 %copy-done.5 = f32[6,18,34,130]{3,2,1,0:T(8,128)} copy-done((f32[6,18,34,130]{3,2,1,0:T(8,128)}, f32[6,18,34,130]{3,2,1,0:T(8,128)S(1)}, u32[]{:S(2)}) %copy-start.5) | copy-done | bytes 1909464
  47.3 1.2 pad_maximum_fusion.5
  48.5 2.0 %fusion.175 = (f32[3,9,96,32]{3,2,1,0:T(8,128)}, f32[3,9,96,32]{3,2,1,0:T(8,128)}) fusion(f32[3,9,96,128]{3,2,1,0:T(8,128)S(1)} %pad_maximum_fusion.5), kind=kLoop, calls=%fused_computation.405 | loop fusion | bytes 1327104 | tf_op jit(solution)/shard_map/slice | solution.py:97
  50.5 2.5 %copy.33 = f32[3,9,96,32]{2,3,1,0:T(8,128)} copy(f32[3,9,96,32]{3,2,1,0:T(8,128)} %get-tuple-element.39) | data formatting | bytes 663552 | tf_op jit(solution)/shard_map/slice | solution.py:97
  53.0 6.6 %collective-permute-start.8 = (f32[3,9,96,32]{2,3,1,0:T(8,128)}, f32[3,9,96,32]{2,3,1,0:T(8,128)}, u32[]{:S(2)}, u32[]{:S(2)}) collective-permute-start(f32[3,9,96,32]{2,3,1,0:T(8,128)} %copy.33), channel_id=1, source_target_pairs={{0,2},{2,4},{4,6},{1,3},{3,5},{5,7},{8,10},{10,12},{12,14},{9,11},... | collective-permute-start | bytes 995336 | tf_op jit(solution)/shard_map/ppermute | solution.py:98
  59.7 2.5 %copy.34 = f32[3,9,96,32]{2,3,1,0:T(8,128)} copy(f32[3,9,96,32]{3,2,1,0:T(8,128)} %get-tuple-element.40) | data formatting | bytes 663552 | tf_op jit(solution)/shard_map/slice | solution.py:99
  62.2 1.5 %collective-permute-start.9 = (f32[3,9,96,32]{2,3,1,0:T(8,128)}, f32[3,9,96,32]{2,3,1,0:T(8,128)}, u32[]{:S(2)}, u32[]{:S(2)}) collective-permute-start(f32[3,9,96,32]{2,3,1,0:T(8,128)} %copy.34), channel_id=1, source_target_pairs={{2,0},{4,2},{6,4},{3,1},{5,3},{7,5},{10,8},{12,10},{14,12},{11,9},... | collective-permute-start | bytes 995336 | tf_op jit(solution)/shard_map/ppermute | solution.py:99
  63.6 1.5 %bitcast_dynamic-update-slice_fusion.1 = f32[6,18,34,130]{3,2,1,0:T(8,128)} fusion(f32[6,18,34,130]{3,2,1,0:T(8,128)} %copy-done.5, f32[20,36,132]{2,1,0:T(8,128)S(1)} %pad_maximum_fusion.6), kind=kLoop, calls=%fused_computation.40 | loop fusion | flops 397800 | bytes 2010240
  65.1 1.9 %bitcast_dynamic-update-slice_fusion = f32[6,18,34,130]{3,2,1,0:T(8,128)} fusion(f32[6,18,34,130]{3,2,1,0:T(8,128)} %bitcast_dynamic-update-slice_fusion.1, f32[20,36,132]{2,1,0:T(8,128)S(1)} %pad_maximum_fusion.6, f32[20,32,2]{2,1,0:T(8,128)S(1)} %collective-permute-done.3, f32[20,32,128]{2,1,0:T(8,128)S(1)} %constant_dynamic-update-slice_fusion, ...), kind=kLoop, calls=%fused_computation.39 | loop fusion | flops 875160 | bytes 1753920 | tf_op jit(solution)/shard_map/stack | solution.py:70
  67.0 2.5 %copy.35 = f32[3,9,96,32]{3,2,1,0:T(8,128)} copy(f32[3,9,96,32]{2,3,1,0:T(8,128)} %collective-permute-done.8) | data formatting | bytes 663552 | tf_op jit(solution)/shard_map/ppermute | solution.py:98
  69.6 2.6 %copy.36 = f32[3,9,96,32]{3,2,1,0:T(8,128)} copy(f32[3,9,96,32]{2,3,1,0:T(8,128)} %collective-permute-done.9) | data formatting | bytes 663552 | tf_op jit(solution)/shard_map/ppermute | solution.py:99
  72.2 3.0 %fusion.2 = f32[3,8,96,192]{3,2,1,0:T(8,128)S(1)} fusion(f32[3,9,96,32]{3,2,1,0:T(8,128)} %copy.36, f32[3,9,96,32]{3,2,1,0:T(8,128)} %copy.35, f32[3,9,32,128]{3,2,1,0:T(8,128)} %collective-permute-done.7, f32[3,9,32,128]{3,2,1,0:T(8,128)} %collective-permute-done.6, f32[3,1,32,128]{3,2,1,0:T(8,128)S(1)} %bitcast.320, f32[3,8,32,128]{3,2,1,0:T(8,128)S(1)} %reduce_sum.27, ...), kind=kLoop, calls=%fused_computation.3 | loop fusion | flops 3096576 | bytes 3833856 | tf_op jit(solution)/shard_map/mul | solution.py:176
  75.2 1.0 fusion.24
  76.2 0.4 fusion.20
  76.7 0.4 fusion.16
  77.1 0.4 fusion.12
  77.6 0.4 fusion.37
  78.0 0.4 fusion.33
  78.4 0.4 fusion.29
  78.9 0.4 fusion.25
  79.6 4.1 %collective-permute-start.10 = (f32[3,80,176]{2,1,0:T(8,128)S(1)}, f32[3,80,176]{2,1,0:T(8,128)S(1)}, u32[]{:S(2)}, u32[]{:S(2)}) collective-permute-start(f32[3,80,176]{2,1,0:T(8,128)S(1)} %fusion.64), channel_id=1, source_target_pairs={{0,8},{8,16},{16,24},{1,9},{9,17},{17,25},{2,10},{10,18},{18,26},{... | collective-permute-start | bytes 506888 | tf_op jit(solution)/shard_map/ppermute | solution.py:30
  83.7 2.4 %broadcast_multiply_fusion = f32[6,18,34,130]{3,2,1,0:T(8,128)} fusion(f32[6,18,34,130]{3,2,1,0:T(8,128)S(1)} %bitcast.315, f32[18,34,130]{2,1,0:T(8,128)S(1)} %copy-done.8), kind=kLoop, calls=%fused_computation.8 | loop fusion | flops 477360 | bytes 4137120 | tf_op jit(solution)/shard_map/mul | solution.py:160
  86.1 2.2 %collective-permute-done.10 = f32[3,80,176]{2,1,0:T(8,128)S(1)} collective-permute-done((f32[3,80,176]{2,1,0:T(8,128)S(1)}, f32[3,80,176]{2,1,0:T(8,128)S(1)}, u32[]{:S(2)}, u32[]{:S(2)}) %collective-permute-start.10) | collective-permute-done | bytes 168992 | tf_op jit(solution)/shard_map/ppermute | solution.py:30
  88.5 0.4 fusion.57
  91.3 4.4 %collective-permute-start.11 = (f32[3,64,160]{2,1,0:T(8,128)S(1)}, f32[3,64,160]{2,1,0:T(8,128)}, u32[]{:S(2)}, u32[]{:S(2)}) collective-permute-start(f32[3,64,160]{2,1,0:T(8,128)S(1)} %fusion.96), channel_id=1, source_target_pairs={{0,8},{8,16},{16,24},{1,9},{9,17},{17,25},{2,10},{10,18},{18,26},{... | collective-permute-start | bytes 368648 | tf_op jit(solution)/shard_map/ppermute | solution.py:30
  95.8 12.2 %fusion.3 = f32[6,16,32,128]{3,2,1,0:T(8,128)} fusion(f32[6,18,34,130]{3,2,1,0:T(8,128)} %broadcast_multiply_fusion), kind=kLoop, calls=%fused_computation.11 | loop fusion | flops 3145728 | bytes 12582912 | tf_op jit(solution)/shard_map/mul | solution.py:45
  108.0 1.1 fusion.93
  111.5 1.9 %collective-permute-start.12 = (f32[3,48,144]{2,1,0:T(8,128)S(1)}, f32[3,48,144]{2,1,0:T(8,128)S(1)}, u32[]{:S(2)}, u32[]{:S(2)}) collective-permute-start(f32[3,48,144]{2,1,0:T(8,128)S(1)} %fusion.128), channel_id=1, source_target_pairs={{0,8},{8,16},{16,24},{1,9},{9,17},{17,25},{2,10},{10,18},{18,26},{... | collective-permute-start | bytes 248840 | tf_op jit(solution)/shard_map/ppermute | solution.py:30
  113.6 5.9 %collective-permute-done.12 = f32[3,48,144]{2,1,0:T(8,128)S(1)} collective-permute-done((f32[3,48,144]{2,1,0:T(8,128)S(1)}, f32[3,48,144]{2,1,0:T(8,128)S(1)}, u32[]{:S(2)}, u32[]{:S(2)}) %collective-permute-start.12) | collective-permute-done | bytes 82976 | tf_op jit(solution)/shard_map/ppermute | solution.py:30
  122.2 0.4 copy-done.1
  122.9 0.5 fusion.7
  123.5 0.5 collective-permute-start.13
  124.0 1.9 %collective-permute-start.16 = (f32[1,1,128]{2,1,0:T(1,128)S(1)}, f32[1,1,128]{2,1,0:T(1,128)S(1)}, u32[]{:S(2)}, u32[]{:S(2)}) collective-permute-start(f32[1,1,128]{2,1,0:T(1,128)S(1)} %fusion.166), channel_id=1, source_target_pairs={{0,4},{4,0},{2,6},{6,2},{1,5},{5,1},{3,7},{7,3},{8,12},{12,8},{10,... | collective-permute-start | bytes 1544 | tf_op jit(solution)/shard_map/ppermute | solution.py:40
  125.8 1.1 collective-permute-start.15
  127.0 0.5 collective-permute-done.16
  127.6 1.9 %collective-permute-done.15 = f32[3,1,128]{2,1,0:T(1,128)S(1)} collective-permute-done((f32[3,1,128]{2,1,0:T(1,128)S(1)}, f32[3,1,128]{2,1,0:T(1,128)S(1)}, u32[]{:S(2)}, u32[]{:S(2)}) %collective-permute-start.15) | collective-permute-done | bytes 1568 | tf_op jit(solution)/shard_map/ppermute | solution.py:40
  129.6 0.6 pad_maximum_fusion.17
  (103 shorter events, 10.5 us)
Async XLA Ops:
  1.1 4.2 %copy-start.6 = (f32[16,32,128]{2,1,0:T(8,128)S(1)}, f32[16,32,128]{2,1,0:T(8,128)}, u32[]{:S(2)}) copy-start(f32[16,32,128]{2,1,0:T(8,128)} %param.6) | copy-start | bytes 786436
  5.4 17.0 %copy-start = (f32[7,16,32,128]{3,2,1,0:T(8,128)}, f32[7,16,32,128]{3,2,1,0:T(8,128)S(1)}, u32[]{:S(2)}) copy-start(f32[7,16,32,128]{3,2,1,0:T(8,128)S(1)} %select_select_fusion) | copy-start | bytes 5505028
  5.4 0.8 copy-start.12
  7.0 38.2 %collective-permute-start.6 = (f32[3,9,32,128]{3,2,1,0:T(8,128)}, f32[3,9,32,128]{3,2,1,0:T(8,128)}, u32[]{:S(2)}, u32[]{:S(2)}) collective-permute-start(f32[3,9,32,128]{3,2,1,0:T(8,128)} %pad_maximum_fusion.13), channel_id=1, source_target_pairs={{0,1},{2,3},{4,5},{6,7},{8,9},{10,11},{12,13},{14,15},{16,17},{18,... | collective-permute-start | bytes 1327112 | tf_op jit(solution)/shard_map/ppermute | solution.py:98
  11.2 36.0 %collective-permute-start.7 = (f32[3,9,32,128]{3,2,1,0:T(8,128)}, f32[3,9,32,128]{3,2,1,0:T(8,128)}, u32[]{:S(2)}, u32[]{:S(2)}) collective-permute-start(f32[3,9,32,128]{3,2,1,0:T(8,128)} %pad_maximum_fusion.13), channel_id=1, source_target_pairs={{1,0},{3,2},{5,4},{7,6},{9,8},{11,10},{13,12},{15,14},{17,16},{19,... | collective-permute-start | bytes 1327112 | tf_op jit(solution)/shard_map/ppermute | solution.py:99
  13.2 8.5 %collective-permute-start = (f32[2,32,128]{2,1,0:T(8,128)}, f32[2,32,128]{2,1,0:T(8,128)}, u32[]{:S(2)}, u32[]{:S(2)}) collective-permute-start(f32[2,32,128]{2,1,0:T(8,128)} %get-tuple-element.47), channel_id=1, source_target_pairs={{0,8},{8,16},{16,24},{1,9},{9,17},{17,25},{2,10},{10,18},{18,26},{... | collective-permute-start | bytes 98312 | tf_op jit(solution)/shard_map/ppermute | solution.py:19
  16.6 6.5 %collective-permute-start.1 = (f32[2,32,128]{2,1,0:T(8,128)}, f32[2,32,128]{2,1,0:T(8,128)}, u32[]{:S(2)}, u32[]{:S(2)}) collective-permute-start(f32[2,32,128]{2,1,0:T(8,128)} %get-tuple-element.46), channel_id=1, source_target_pairs={{8,0},{16,8},{24,16},{9,1},{17,9},{25,17},{10,2},{18,10},{26,18},{... | collective-permute-start | bytes 98312 | tf_op jit(solution)/shard_map/ppermute | solution.py:22
  24.1 5.6 %collective-permute-start.2 = (f32[20,32,2]{2,1,0:T(8,128)S(1)}, f32[20,32,2]{2,1,0:T(8,128)S(1)}, u32[]{:S(2)}, u32[]{:S(2)}) collective-permute-start(f32[20,32,2]{2,1,0:T(8,128)S(1)} %get-tuple-element.43), channel_id=1, source_target_pairs={{0,2},{2,4},{4,6},{1,3},{3,5},{5,7},{8,10},{10,12},{12,14},{9,11},... | collective-permute-start | bytes 15368 | tf_op jit(solution)/shard_map/ppermute | solution.py:19
  25.4 5.2 %collective-permute-start.3 = (f32[20,32,2]{2,1,0:T(8,128)S(1)}, f32[20,32,2]{2,1,0:T(8,128)S(1)}, u32[]{:S(2)}, u32[]{:S(2)}) collective-permute-start(f32[20,32,2]{2,1,0:T(8,128)S(1)} %get-tuple-element.44), channel_id=1, source_target_pairs={{2,0},{4,2},{6,4},{3,1},{5,3},{7,5},{10,8},{12,10},{14,12},{11,9},... | collective-permute-start | bytes 15368 | tf_op jit(solution)/shard_map/ppermute | solution.py:22
  26.8 10.7 %collective-permute-start.14 = (f32[1,2,128]{2,1,0:T(2,128)S(1)}, f32[1,2,128]{2,1,0:T(2,128)S(1)}, u32[]{:S(2)}, u32[]{:S(2)}) collective-permute-start(f32[1,2,128]{2,1,0:T(2,128)S(1)} %bitcast.331), channel_id=1, source_target_pairs={{0,2},{2,0},{4,6},{6,4},{1,3},{3,1},{5,7},{7,5},{8,10},{10,8},{12,... | collective-permute-start | bytes 3080 | tf_op jit(solution)/shard_map/ppermute | solution.py:40
  30.8 7.0 %collective-permute-start.4 = (f32[20,2,132]{2,1,0:T(2,128)S(1)}, f32[20,2,132]{2,1,0:T(2,128)S(1)}, u32[]{:S(2)}, u32[]{:S(2)}) collective-permute-start(f32[20,2,132]{2,1,0:T(2,128)S(1)} %get-tuple-element.41), channel_id=1, source_target_pairs={{0,1},{2,3},{4,5},{6,7},{8,9},{10,11},{12,13},{14,15},{16,17},{18,... | collective-permute-start | bytes 63368 | tf_op jit(solution)/shard_map/ppermute | solution.py:19
  36.2 5.9 %collective-permute-start.5 = (f32[20,2,132]{2,1,0:T(2,128)S(1)}, f32[20,2,132]{2,1,0:T(2,128)S(1)}, u32[]{:S(2)}, u32[]{:S(2)}) collective-permute-start(f32[20,2,132]{2,1,0:T(2,128)S(1)} %get-tuple-element.42), channel_id=1, source_target_pairs={{1,0},{3,2},{5,4},{7,6},{9,8},{11,10},{13,12},{15,14},{17,16},{19,... | collective-permute-start | bytes 63368 | tf_op jit(solution)/shard_map/ppermute | solution.py:22
  44.0 3.3 %copy-start.13 = (f32[3,32,128]{2,1,0:T(8,128)S(1)}, f32[3,32,128]{2,1,0:T(8,128)}, u32[]{:S(2)}) copy-start(f32[3,32,128]{2,1,0:T(8,128)} %param.8) | copy-start | bytes 147460
  45.2 2.0 %copy-start.5 = (f32[6,18,34,130]{3,2,1,0:T(8,128)}, f32[6,18,34,130]{3,2,1,0:T(8,128)S(1)}, u32[]{:S(2)}) copy-start(f32[6,18,34,130]{3,2,1,0:T(8,128)S(1)} %bitcast_dynamic-update-slice_fusion.2) | copy-start | bytes 5728324
  53.0 14.0 %collective-permute-start.8 = (f32[3,9,96,32]{2,3,1,0:T(8,128)}, f32[3,9,96,32]{2,3,1,0:T(8,128)}, u32[]{:S(2)}, u32[]{:S(2)}) collective-permute-start(f32[3,9,96,32]{2,3,1,0:T(8,128)} %copy.33), channel_id=1, source_target_pairs={{0,2},{2,4},{4,6},{1,3},{3,5},{5,7},{8,10},{10,12},{12,14},{9,11},... | collective-permute-start | bytes 995336 | tf_op jit(solution)/shard_map/ppermute | solution.py:98
  62.2 7.4 %collective-permute-start.9 = (f32[3,9,96,32]{2,3,1,0:T(8,128)}, f32[3,9,96,32]{2,3,1,0:T(8,128)}, u32[]{:S(2)}, u32[]{:S(2)}) collective-permute-start(f32[3,9,96,32]{2,3,1,0:T(8,128)} %copy.34), channel_id=1, source_target_pairs={{2,0},{4,2},{6,4},{3,1},{5,3},{7,5},{10,8},{12,10},{14,12},{11,9},... | collective-permute-start | bytes 995336 | tf_op jit(solution)/shard_map/ppermute | solution.py:99
  72.2 3.0 %copy-start.2 = (f32[3,9,96,32]{3,2,1,0:T(8,128)S(1)}, f32[3,9,96,32]{3,2,1,0:T(8,128)}, u32[]{:S(2)}) copy-start(f32[3,9,96,32]{3,2,1,0:T(8,128)} %copy.35) | copy-start | bytes 995332
  72.2 3.0 %copy-start.3 = (f32[3,9,96,32]{3,2,1,0:T(8,128)S(1)}, f32[3,9,96,32]{3,2,1,0:T(8,128)}, u32[]{:S(2)}) copy-start(f32[3,9,96,32]{3,2,1,0:T(8,128)} %copy.36) | copy-start | bytes 995332
  76.2 12.1 %copy-start.9 = (f32[3,96,192]{2,1,0:T(8,128)}, f32[3,96,192]{2,1,0:T(8,128)S(1)}, u32[]{:S(2)}) copy-start(f32[3,96,192]{2,1,0:T(8,128)S(1)} %get-tuple-element.36) | copy-start | bytes 663556
  76.2 7.5 %slice-start = ((s8[4423680]{0:T(1024)(128)(4,1)}), s8[4194304]{0:T(1024)(128)(4,1)S(1)}, s32[]{:S(2)}) async-start(s8[4423680]{0:T(1024)(128)(4,1)} %bitcast.314), calls=%async_computation | async-start | bytes 8388608
  77.6 6.1 %slice-start.1 = ((s8[4423680]{0:T(1024)(128)(4,1)}), s8[229376]{0:T(1024)(128)(4,1)S(1)}, s32[]{:S(2)}) async-start(s8[4423680]{0:T(1024)(128)(4,1)} %bitcast.314), calls=%async_computation.1 | async-start | bytes 458752
  78.8 4.9 %copy-start.8 = (f32[18,34,130]{2,1,0:T(8,128)S(1)}, f32[18,34,130]{2,1,0:T(8,128)}, u32[]{:S(2)}) copy-start(f32[18,34,130]{2,1,0:T(8,128)} %broadcast_multiply_fusion.1) | copy-start | bytes 954724
  79.6 8.7 %collective-permute-start.10 = (f32[3,80,176]{2,1,0:T(8,128)S(1)}, f32[3,80,176]{2,1,0:T(8,128)S(1)}, u32[]{:S(2)}, u32[]{:S(2)}) collective-permute-start(f32[3,80,176]{2,1,0:T(8,128)S(1)} %fusion.64), channel_id=1, source_target_pairs={{0,8},{8,16},{16,24},{1,9},{9,17},{17,25},{2,10},{10,18},{18,26},{... | collective-permute-start | bytes 506888 | tf_op jit(solution)/shard_map/ppermute | solution.py:30
  91.3 16.6 %copy-start.10 = (f32[3,96,192]{2,1,0:T(8,128)S(1)}, f32[3,96,192]{2,1,0:T(8,128)}, u32[]{:S(2)}) copy-start(f32[3,96,192]{2,1,0:T(8,128)} %copy-done.9) | copy-start | bytes 663556
  91.3 16.6 %collective-permute-start.11 = (f32[3,64,160]{2,1,0:T(8,128)S(1)}, f32[3,64,160]{2,1,0:T(8,128)}, u32[]{:S(2)}, u32[]{:S(2)}) collective-permute-start(f32[3,64,160]{2,1,0:T(8,128)S(1)} %fusion.96), channel_id=1, source_target_pairs={{0,8},{8,16},{16,24},{1,9},{9,17},{17,25},{2,10},{10,18},{18,26},{... | collective-permute-start | bytes 368648 | tf_op jit(solution)/shard_map/ppermute | solution.py:30
  110.6 2.8 %copy-start.4 = (f32[6,16,32,128]{3,2,1,0:T(8,128)S(1)}, f32[6,16,32,128]{3,2,1,0:T(8,128)}, u32[]{:S(2)}) copy-start(f32[6,16,32,128]{3,2,1,0:T(8,128)} %fusion.3) | copy-start | bytes 4718596
  111.5 8.0 %collective-permute-start.12 = (f32[3,48,144]{2,1,0:T(8,128)S(1)}, f32[3,48,144]{2,1,0:T(8,128)S(1)}, u32[]{:S(2)}, u32[]{:S(2)}) collective-permute-start(f32[3,48,144]{2,1,0:T(8,128)S(1)} %fusion.128), channel_id=1, source_target_pairs={{0,8},{8,16},{16,24},{1,9},{9,17},{17,25},{2,10},{10,18},{18,26},{... | collective-permute-start | bytes 248840 | tf_op jit(solution)/shard_map/ppermute | solution.py:30
  121.1 1.5 %copy-start.1 = (f32[7,16,32,128]{3,2,1,0:T(8,128)S(1)}, f32[7,16,32,128]{3,2,1,0:T(8,128)}, u32[]{:S(2)}) copy-start(f32[7,16,32,128]{3,2,1,0:T(8,128)} %copy-done) | copy-start | bytes 5505028
  121.1 1.7 %copy-start.7 = (f32[3,8,2,32,128]{4,3,2,1,0:T(8,128)S(1)}, f32[3,8,2,32,128]{4,3,2,1,0:T(8,128)}, u32[]{:S(2)}) copy-start(f32[3,8,2,32,128]{4,3,2,1,0:T(8,128)} %fusion.181) | copy-start | bytes 2359300
  121.1 1.7 %copy-start.11 = (f32[16,32,128]{2,1,0:T(8,128)S(1)}, f32[16,32,128]{2,1,0:T(8,128)}, u32[]{:S(2)}) copy-start(f32[16,32,128]{2,1,0:T(8,128)} %get-tuple-element.37) | copy-start | bytes 786436
  123.5 2.3 %collective-permute-start.13 = (f32[3,2,128]{2,1,0:T(2,128)S(1)}, f32[3,2,128]{2,1,0:T(2,128)S(1)}, u32[]{:S(2)}, u32[]{:S(2)}) collective-permute-start(f32[3,2,128]{2,1,0:T(2,128)S(1)} %bitcast.330), channel_id=1, source_target_pairs={{0,2},{2,0},{4,6},{6,4},{1,3},{3,1},{5,7},{7,5},{8,10},{10,8},{12,... | collective-permute-start | bytes 9224 | tf_op jit(solution)/shard_map/ppermute | solution.py:40
  124.0 3.5 %collective-permute-start.16 = (f32[1,1,128]{2,1,0:T(1,128)S(1)}, f32[1,1,128]{2,1,0:T(1,128)S(1)}, u32[]{:S(2)}, u32[]{:S(2)}) collective-permute-start(f32[1,1,128]{2,1,0:T(1,128)S(1)} %fusion.166), channel_id=1, source_target_pairs={{0,4},{4,0},{2,6},{6,2},{1,5},{5,1},{3,7},{7,3},{8,12},{12,8},{10,... | collective-permute-start | bytes 1544 | tf_op jit(solution)/shard_map/ppermute | solution.py:40
  125.8 3.6 %collective-permute-start.15 = (f32[3,1,128]{2,1,0:T(1,128)S(1)}, f32[3,1,128]{2,1,0:T(1,128)S(1)}, u32[]{:S(2)}, u32[]{:S(2)}) collective-permute-start(f32[3,1,128]{2,1,0:T(1,128)S(1)} %fusion.161), channel_id=1, source_target_pairs={{0,4},{4,0},{2,6},{6,2},{1,5},{5,1},{3,7},{7,3},{8,12},{12,8},{10,... | collective-permute-start | bytes 4616 | tf_op jit(solution)/shard_map/ppermute | solution.py:40

commit v5 on v4

--- a/solution.py
+++ b/solution.py
@@ -40,43 +40,27 @@
     return lax.ppermute(block, axis, route)
 
 
-def shade_from(tensor):
-    centre = tensor[:, 1:-1, 1:-1, 1:-1]
-    smooth = (
+def smooth(field):
+    centre = field[1:-1, 1:-1, 1:-1]
+    return (
         2.0 * centre
-        + tensor[:, 2:, 1:-1, 1:-1]
-        + tensor[:, :-2, 1:-1, 1:-1]
-        + tensor[:, 1:-1, 2:, 1:-1]
-        + tensor[:, 1:-1, :-2, 1:-1]
-        + tensor[:, 1:-1, 1:-1, 2:]
-        + tensor[:, 1:-1, 1:-1, :-2]
+        + field[2:, 1:-1, 1:-1]
+        + field[:-2, 1:-1, 1:-1]
+        + field[1:-1, 2:, 1:-1]
+        + field[1:-1, :-2, 1:-1]
+        + field[1:-1, 1:-1, 2:]
+        + field[1:-1, 1:-1, :-2]
     ) * 0.125
-    aligned = (
-        0.64 * smooth[0]
-        + 0.1296 * smooth[1]
-        + 0.2304 * smooth[2]
-        + 0.576 * smooth[3]
-        + 0.768 * smooth[4]
-        + 0.3456 * smooth[5]
-    )
-    trace_sum = smooth[0] + smooth[1] + smooth[2]
-    return 0.25 + aligned / (trace_sum + SOFTEN)
-
-
-def structure(window):
+
+
+def shade_from(window, inside):
     slope_light = (window[2:, 1:-1, 1:-1] - window[:-2, 1:-1, 1:-1]) * 0.5
     slope_across = (window[1:-1, 2:, 1:-1] - window[1:-1, :-2, 1:-1]) * 0.5
     slope_view = (window[1:-1, 1:-1, 2:] - window[1:-1, 1:-1, :-2]) * 0.5
-    return jnp.stack(
-        [
-            slope_light * slope_light,
-            slope_across * slope_across,
-            slope_view * slope_view,
-            slope_light * slope_across,
-            slope_light * slope_view,
-            slope_across * slope_view,
-        ]
-    )
+    along = 0.8 * slope_light + 0.36 * slope_across + 0.48 * slope_view
+    aligned = along * along * inside
+    trace = (slope_light * slope_light + slope_across * slope_across + slope_view * slope_view) * inside
+    return 0.25 + smooth(aligned) / (smooth(trace) + SOFTEN)
 
 
 def rim_mask(position, devices, width, border):
@@ -157,8 +141,7 @@
         * rim_mask(across_idx, n_across, brick_a, 1)[None, :, None]
         * rim_mask(view_idx, n_view, brick_v, 1)[None, None, :]
     )
-    tensor_rim = structure(padded) * inside[None]
-    shading = shade_from(tensor_rim)
+    shading = shade_from(padded, inside)
     table_all = jnp.concatenate([opacity_table[None], extinction_table, albedo_table], axis=0)
     looked = jnp.broadcast_to(table_all[:, 0, None, None, None], (7,) + labels.shape)
     for material in range(1, table_all.shape[1]):

time: 131 us -> 111 us (0.85)
  other arithmetic: 48.3 us -> 31.8 us
  local copies, waits for them, and re-layouts: 19.5 us -> 16.8 us
  starting transfers between devices: 45.4 us -> 42.7 us
    mul x3 -> x2, other arithmetic: 14.7 us -> 4.54 us  [the longest x1 2.27 us: shade_from(): aligned = along * along * inside]
    unnamed x6 -> x0, other arithmetic: 4.27 us -> none
    ppermute x3, waiting for transfers between devices: 5.2 us -> 1.86 us  [padded_2(): lax.ppermute(lax.slice_in_dim(block, 0, width, axis=dim), axis, backward)]
    ppermute x3, waiting for transfers between devices: 8.07 us -> 11.3 us  [from_behind(): lax.ppermute(value, axis, [(source, source + steps) for source in range(l...]
    unnamed x40 -> x36, local copies, waits for them, and re-layouts: 4.72 us -> 2.12 us
    ppermute x4, starting transfers between devices: 6.34 us -> 4.35 us  [from_partner(): return lax.ppermute(block, axis, route)]
    another operation x1 -> x0, other arithmetic: 1.89 us -> none  [structure(): jnp.stack([slope_light * slope_light, slope_across * slope_across, slope_...]
    ppermute x3, starting transfers between devices: 10.4 us -> 8.58 us  [from_behind(): lax.ppermute(value, axis, [(source, source + steps) for source in range(l...]
  transfers between devices with their start and end apart: 17 -> 17, of which waited for: 7 -> 8; matrix products, arithmetic and copies ran while one was open for 25% -> 21% of each run, Pallas kernels for 0% -> 0%
where the time goes in v5:
time: 111 us; the launch traced here: 109 us
  starting transfers between devices  42.7 us (38%)
  other arithmetic  31.8 us (29%)
  local copies, waits for them, and re-layouts  16.8 us (15%)
  waiting for transfers between devices  16.5 us (15%)
    ppermute x2, starting transfers between devices, halo(): lows.insert(0, lax.ppermute(low, axis, forward))  11.9 us
    ppermute x3, waiting for transfers between devices, from_behind(): lax.ppermute(value, axis, [(source, source + steps) for source in range(l...  11.3 us
    mul x31, other arithmetic, propagate(): current = current * fade_here  10.7 us
    ppermute x3, starting transfers between devices, padded_2(): lax.ppermute(lax.slice_in_dim(block, block.shape[dim] - width, None, axis...  10.1 us
    ppermute x3, starting transfers between devices, from_behind(): lax.ppermute(value, axis, [(source, source + steps) for source in range(l...  8.58 us
    ppermute x3, starting transfers between devices, padded_2(): lax.ppermute(lax.slice_in_dim(block, 0, width, axis=dim), axis, backward)  4.94 us
    slice x2, local copies, waits for them, and re-layouts, halo(): low = lax.slice_in_dim(block, size - need, None, axis=dim)  4.5 us
    ppermute x4, starting transfers between devices, from_partner(): return lax.ppermute(block, axis, route)  4.35 us
  transfers between devices with their start and end apart: 17, of which 8 were waited for; matrix products, arithmetic and copies ran while one was open for 21% of the time, Pallas kernels for 0%

profile of v5, /device:TPU:16, one launch (start us, length us, event | category | flops | bytes accessed | tf_op | source)
XLA Modules:
  0.0 109.5 jit_solution(15747571689892307313)
XLA Ops:
  0.0 0.7 pad_maximum_fusion.18
  0.7 0.4 slice_reduce_fusion.15
  1.2 1.6 %broadcast_compare_fusion.14 = (pred[16,32,128]{2,1,0:T(8,128)(4,1)S(1)}, pred[16,32,128]{2,1,0:T(8,128)(4,1)S(1)}, pred[16,32,128]{2,1,0:T(8,128)(4,1)S(1)}, pr...) fusion(s32[16,32,128]{2,1,0:T(8,128)} %param.7), kind=kLoop, calls=%fused_computation.289 | loop fusion | flops 983040 | bytes 1245184 | tf_op jit(solution)/shard_map/eq | solution.py:149
  2.8 2.6 %select_select_fusion = f32[7,16,32,128]{3,2,1,0:T(8,128)S(1)} fusion(f32[7]{0:T(128)S(1)} %get-tuple-element.6, f32[7]{0:T(128)S(1)} %get-tuple-element.7, f32[7]{0:T(128)S(1)} %get-tuple-element.8, f32[7]{0:T(128)S(1)} %get-tuple-element.9, f32[7]{0:T(128)S(1)} %get-tuple-element.10, f32[7]{0:T(128)S(1)} %get-tuple-element.11, f32[7]{0:T(128)S(1)} %get-tuple-element.12, ...), kind=kLoop, calls=%fused_computation.8 | loop fusion | flops 6881280 | bytes 2818496 | tf_op jit(solution)/shard_map/jit(_where)/select_n | solution.py:148
  5.6 0.6 copy-done.11
  6.2 0.8 pad_maximum_fusion.13
  7.0 4.2 %collective-permute-start.6 = (f32[3,9,32,128]{3,2,1,0:T(8,128)}, f32[3,9,32,128]{3,2,1,0:T(8,128)}, u32[]{:S(2)}, u32[]{:S(2)}) collective-permute-start(f32[3,9,32,128]{3,2,1,0:T(8,128)} %pad_maximum_fusion.13), channel_id=1, source_target_pairs={{0,1},{2,3},{4,5},{6,7},{8,9},{10,11},{12,13},{14,15},{16,17},{18,... | collective-permute-start | bytes 1327112 | tf_op jit(solution)/shard_map/ppermute | solution.py:82
  11.2 1.3 %collective-permute-start.7 = (f32[3,9,32,128]{3,2,1,0:T(8,128)}, f32[3,9,32,128]{3,2,1,0:T(8,128)}, u32[]{:S(2)}, u32[]{:S(2)}) collective-permute-start(f32[3,9,32,128]{3,2,1,0:T(8,128)} %pad_maximum_fusion.13), channel_id=1, source_target_pairs={{1,0},{3,2},{5,4},{7,6},{9,8},{11,10},{13,12},{15,14},{17,16},{19,... | collective-permute-start | bytes 1327112 | tf_op jit(solution)/shard_map/ppermute | solution.py:83
  12.5 0.6 fusion.172
  13.1 3.5 %collective-permute-start = (f32[2,32,128]{2,1,0:T(8,128)}, f32[2,32,128]{2,1,0:T(8,128)S(1)}, u32[]{:S(2)}, u32[]{:S(2)}) collective-permute-start(f32[2,32,128]{2,1,0:T(8,128)} %get-tuple-element.47), channel_id=1, source_target_pairs={{0,8},{8,16},{16,24},{1,9},{9,17},{17,25},{2,10},{10,18},{18,26},{... | collective-permute-start | bytes 98312 | tf_op jit(solution)/shard_map/ppermute | solution.py:19
  16.6 2.4 %collective-permute-start.1 = (f32[2,32,128]{2,1,0:T(8,128)}, f32[2,32,128]{2,1,0:T(8,128)S(1)}, u32[]{:S(2)}, u32[]{:S(2)}) collective-permute-start(f32[2,32,128]{2,1,0:T(8,128)} %get-tuple-element.46), channel_id=1, source_target_pairs={{8,0},{16,8},{24,16},{9,1},{17,9},{25,17},{10,2},{18,10},{26,18},{... | collective-permute-start | bytes 98312 | tf_op jit(solution)/shard_map/ppermute | solution.py:22
  18.9 0.9 fusion.176
  19.9 1.0 fusion.3
  21.1 0.8 exponential_subtract_fusion
  21.9 0.7 collective-permute-done.1
  22.6 0.9 fusion.171
  23.5 1.3 %collective-permute-start.2 = (f32[20,32,2]{2,1,0:T(8,128)}, f32[20,32,2]{2,1,0:T(8,128)S(1)}, u32[]{:S(2)}, u32[]{:S(2)}) collective-permute-start(f32[20,32,2]{2,1,0:T(8,128)} %get-tuple-element.43), channel_id=1, source_target_pairs={{0,2},{2,4},{4,6},{1,3},{3,5},{5,7},{8,10},{10,12},{12,14},{9,11},... | collective-permute-start | bytes 15368 | tf_op jit(solution)/shard_map/ppermute | solution.py:19
  24.8 1.3 %collective-permute-start.3 = (f32[20,32,2]{2,1,0:T(8,128)}, f32[20,32,2]{2,1,0:T(8,128)S(1)}, u32[]{:S(2)}, u32[]{:S(2)}) collective-permute-start(f32[20,32,2]{2,1,0:T(8,128)} %get-tuple-element.44), channel_id=1, source_target_pairs={{2,0},{4,2},{6,4},{3,1},{5,3},{7,5},{10,8},{12,10},{14,12},{11,9},... | collective-permute-start | bytes 15368 | tf_op jit(solution)/shard_map/ppermute | solution.py:22
  26.2 2.9 %collective-permute-start.14 = (f32[1,2,128]{2,1,0:T(2,128)S(1)}, f32[1,2,128]{2,1,0:T(2,128)S(1)}, u32[]{:S(2)}, u32[]{:S(2)}) collective-permute-start(f32[1,2,128]{2,1,0:T(2,128)S(1)} %bitcast.315), channel_id=1, source_target_pairs={{0,2},{2,0},{4,6},{6,4},{1,3},{3,1},{5,7},{7,5},{8,10},{10,8},{12,... | collective-permute-start | bytes 3080 | tf_op jit(solution)/shard_map/ppermute | solution.py:40
  29.1 1.2 %collective-permute-done.3 = f32[20,32,2]{2,1,0:T(8,128)S(1)} collective-permute-done((f32[20,32,2]{2,1,0:T(8,128)}, f32[20,32,2]{2,1,0:T(8,128)S(1)}, u32[]{:S(2)}, u32[]{:S(2)}) %collective-permute-start.3) | collective-permute-done | bytes 5152 | tf_op jit(solution)/shard_map/ppermute | solution.py:22
  30.5 5.3 %collective-permute-start.4 = (f32[20,2,132]{2,1,0:T(2,128)S(1)}, f32[20,2,132]{2,1,0:T(2,128)S(1)}, u32[]{:S(2)}, u32[]{:S(2)}) collective-permute-start(f32[20,2,132]{2,1,0:T(2,128)S(1)} %get-tuple-element.41), channel_id=1, source_target_pairs={{0,1},{2,3},{4,5},{6,7},{8,9},{10,11},{12,13},{14,15},{16,17},{18,... | collective-permute-start | bytes 63368 | tf_op jit(solution)/shard_map/ppermute | solution.py:19
  35.8 1.3 %collective-permute-start.5 = (f32[20,2,132]{2,1,0:T(2,128)S(1)}, f32[20,2,132]{2,1,0:T(2,128)}, u32[]{:S(2)}, u32[]{:S(2)}) collective-permute-start(f32[20,2,132]{2,1,0:T(2,128)S(1)} %get-tuple-element.42), channel_id=1, source_target_pairs={{1,0},{3,2},{5,4},{7,6},{9,8},{11,10},{13,12},{15,14},{17,16},{19,... | collective-permute-start | bytes 63368 | tf_op jit(solution)/shard_map/ppermute | solution.py:22
  37.1 1.2 %pad_maximum_fusion.5 = f32[3,9,96,128]{3,2,1,0:T(8,128)S(1)} fusion(f32[3,9,32,128]{3,2,1,0:T(8,128)} %collective-permute-done.7, f32[3,1,32,128]{3,2,1,0:T(8,128)S(1)} %bitcast.303, f32[3,8,32,128]{3,2,1,0:T(8,128)S(1)} %reduce_sum.27, f32[3,9,32,128]{3,2,1,0:T(8,128)} %collective-permute-done.6), kind=kLoop, calls=%fused_computation.9 | loop fusion | flops 995328 | bytes 2654208 | tf_op jit(solution)/shard_map/concatenate | solution.py:84
  38.4 2.0 %fusion.170 = (f32[3,9,96,32]{3,2,1,0:T(8,128)}, f32[3,9,96,32]{3,2,1,0:T(8,128)}) fusion(f32[3,9,96,128]{3,2,1,0:T(8,128)S(1)} %pad_maximum_fusion.5), kind=kLoop, calls=%fused_computation.398 | loop fusion | bytes 1327104 | tf_op jit(solution)/shard_map/slice | solution.py:81
  40.4 2.5 %copy.33 = f32[3,9,96,32]{2,3,1,0:T(8,128)} copy(f32[3,9,96,32]{3,2,1,0:T(8,128)} %get-tuple-element.39) | data formatting | bytes 663552 | tf_op jit(solution)/shard_map/slice | solution.py:81
  42.9 7.8 %collective-permute-start.8 = (f32[3,9,96,32]{2,3,1,0:T(8,128)}, f32[3,9,96,32]{2,3,1,0:T(8,128)}, u32[]{:S(2)}, u32[]{:S(2)}) collective-permute-start(f32[3,9,96,32]{2,3,1,0:T(8,128)} %copy.33), channel_id=1, source_target_pairs={{0,2},{2,4},{4,6},{1,3},{3,5},{5,7},{8,10},{10,12},{12,14},{9,11},... | collective-permute-start | bytes 995336 | tf_op jit(solution)/shard_map/ppermute | solution.py:82
  50.7 2.5 %copy.34 = f32[3,9,96,32]{2,3,1,0:T(8,128)} copy(f32[3,9,96,32]{3,2,1,0:T(8,128)} %get-tuple-element.40) | data formatting | bytes 663552 | tf_op jit(solution)/shard_map/slice | solution.py:83
  53.2 1.5 %collective-permute-start.9 = (f32[3,9,96,32]{2,3,1,0:T(8,128)}, f32[3,9,96,32]{2,3,1,0:T(8,128)}, u32[]{:S(2)}, u32[]{:S(2)}) collective-permute-start(f32[3,9,96,32]{2,3,1,0:T(8,128)} %copy.34), channel_id=1, source_target_pairs={{2,0},{4,2},{6,4},{3,1},{5,3},{7,5},{10,8},{12,10},{14,12},{11,9},... | collective-permute-start | bytes 995336 | tf_op jit(solution)/shard_map/ppermute | solution.py:83
  54.7 0.6 copy-done.12
  55.3 1.5 %pad_maximum_fusion.6 = f32[20,36,132]{2,1,0:T(8,128)S(1)} fusion(f32[20,2,132]{2,1,0:T(2,128)} %collective-permute-done.5, f32[20,32,2]{2,1,0:T(8,128)} %copy-done.4, f32[20,32,128]{2,1,0:T(8,128)S(1)} %constant_dynamic-update-slice_fusion, f32[20,32,2]{2,1,0:T(8,128)} %copy-done.2, f32[20,2,132]{2,1,0:T(2,128)} %copy-done.12), kind=kLoop, calls=%fused_computation.14 | loop fusion | flops 380160 | bytes 760320 | tf_op jit(solution)/shard_map/concatenate | solution.py:23
  56.8 2.5 %copy.35 = f32[3,9,96,32]{3,2,1,0:T(8,128)} copy(f32[3,9,96,32]{2,3,1,0:T(8,128)} %collective-permute-done.8) | data formatting | bytes 663552 | tf_op jit(solution)/shard_map/ppermute | solution.py:82
  59.3 2.5 %copy.36 = f32[3,9,96,32]{3,2,1,0:T(8,128)} copy(f32[3,9,96,32]{2,3,1,0:T(8,128)} %collective-permute-done.9) | data formatting | bytes 663552 | tf_op jit(solution)/shard_map/ppermute | solution.py:83
  61.9 3.0 %fusion.2 = f32[3,8,96,192]{3,2,1,0:T(8,128)S(1)} fusion(f32[3,9,96,32]{3,2,1,0:T(8,128)} %copy.36, f32[3,9,96,32]{3,2,1,0:T(8,128)} %copy.35, f32[3,9,32,128]{3,2,1,0:T(8,128)} %collective-permute-done.7, f32[3,9,32,128]{3,2,1,0:T(8,128)} %collective-permute-done.6, f32[3,1,32,128]{3,2,1,0:T(8,128)S(1)} %bitcast.304, f32[3,8,32,128]{3,2,1,0:T(8,128)S(1)} %reduce_sum.27, ...), kind=kLoop, calls=%fused_computation.3 | loop fusion | flops 3096576 | bytes 3833856 | tf_op jit(solution)/shard_map/mul | solution.py:159
  64.8 1.0 fusion.20
  65.9 0.4 fusion.16
  66.3 0.4 fusion.12
  66.8 0.4 fusion.8
  67.2 0.4 fusion.33
  67.6 0.4 fusion.29
  68.1 0.4 fusion.25
  68.5 0.4 fusion.21
  68.9 0.3 fusion.59
  69.3 2.8 %collective-permute-start.10 = (f32[3,80,176]{2,1,0:T(8,128)S(1)}, f32[3,80,176]{2,1,0:T(8,128)S(1)}, u32[]{:S(2)}, u32[]{:S(2)}) collective-permute-start(f32[3,80,176]{2,1,0:T(8,128)S(1)} %fusion.59), channel_id=1, source_target_pairs={{0,8},{8,16},{16,24},{1,9},{9,17},{17,25},{2,10},{10,18},{18,26},{... | collective-permute-start | bytes 506888 | tf_op jit(solution)/shard_map/ppermute | solution.py:30
  72.1 2.3 %multiply_multiply_fusion = f32[18,34,130]{2,1,0:T(8,128)S(1)} fusion(f32[130]{0:T(256)S(1)} %and_convert_fusion.2, f32[18,34]{1,0:T(8,128)S(1)} %broadcast_multiply_fusion.1, f32[20,36,132]{2,1,0:T(8,128)S(1)} %pad_maximum_fusion.6, f32[20,32,2]{2,1,0:T(8,128)S(1)} %copy-done.5, f32[20,32,128]{2,1,0:T(8,128)S(1)} %constant_dynamic-update-slice_fusion, ...), kind=kLoop, calls=%fused_computation.12 | loop fusion | flops 1511640 | bytes 1974328 | tf_op jit(solution)/shard_map/mul | solution.py:62
  74.4 3.3 %collective-permute-done.10 = f32[3,80,176]{2,1,0:T(8,128)S(1)} collective-permute-done((f32[3,80,176]{2,1,0:T(8,128)S(1)}, f32[3,80,176]{2,1,0:T(8,128)S(1)}, u32[]{:S(2)}, u32[]{:S(2)}) %collective-permute-start.10) | collective-permute-done | bytes 168992 | tf_op jit(solution)/shard_map/ppermute | solution.py:30
  77.8 0.4 fusion.52
  78.2 0.4 fusion.48
  78.6 0.4 fusion.44
  79.0 0.4 fusion.72
  79.4 0.4 fusion.68
  79.7 0.4 fusion.64
  80.1 0.4 fusion.60
  80.7 3.0 %collective-permute-start.11 = (f32[3,64,160]{2,1,0:T(8,128)S(1)}, f32[3,64,160]{2,1,0:T(8,128)S(1)}, u32[]{:S(2)}, u32[]{:S(2)}) collective-permute-start(f32[3,64,160]{2,1,0:T(8,128)S(1)} %fusion.91), channel_id=1, source_target_pairs={{0,8},{8,16},{16,24},{1,9},{9,17},{17,25},{2,10},{10,18},{18,26},{... | collective-permute-start | bytes 368648 | tf_op jit(solution)/shard_map/ppermute | solution.py:30
  83.7 2.3 %multiply_multiply_fusion.1 = f32[18,34,130]{2,1,0:T(8,128)S(1)} fusion(f32[130]{0:T(256)S(1)} %and_convert_fusion.2, f32[18,34]{1,0:T(8,128)S(1)} %broadcast_multiply_fusion.1, f32[20,36,132]{2,1,0:T(8,128)S(1)} %pad_maximum_fusion.6, f32[20,32,2]{2,1,0:T(8,128)S(1)} %copy-done.5, f32[20,32,128]{2,1,0:T(8,128)S(1)} %constant_dynamic-update-slice_fusion, ...), kind=kLoop, calls=%fused_computation.13 | loop fusion | flops 1352520 | bytes 1974328 | tf_op jit(solution)/shard_map/mul | solution.py:61
  86.0 3.2 %collective-permute-done.11 = f32[3,64,160]{2,1,0:T(8,128)S(1)} collective-permute-done((f32[3,64,160]{2,1,0:T(8,128)S(1)}, f32[3,64,160]{2,1,0:T(8,128)S(1)}, u32[]{:S(2)}, u32[]{:S(2)}) %collective-permute-start.11) | collective-permute-done | bytes 122912 | tf_op jit(solution)/shard_map/ppermute | solution.py:30
  91.8 2.8 %collective-permute-start.12 = (f32[3,48,144]{2,1,0:T(8,128)S(1)}, f32[3,48,144]{2,1,0:T(8,128)S(1)}, u32[]{:S(2)}, u32[]{:S(2)}) collective-permute-start(f32[3,48,144]{2,1,0:T(8,128)S(1)} %fusion.123), channel_id=1, source_target_pairs={{0,8},{8,16},{16,24},{1,9},{9,17},{17,25},{2,10},{10,18},{18,26},{... | collective-permute-start | bytes 248840 | tf_op jit(solution)/shard_map/ppermute | solution.py:30
  94.6 0.9 fusion.40
  95.4 4.9 %collective-permute-done.12 = f32[3,48,144]{2,1,0:T(8,128)S(1)} collective-permute-done((f32[3,48,144]{2,1,0:T(8,128)S(1)}, f32[3,48,144]{2,1,0:T(8,128)S(1)}, u32[]{:S(2)}, u32[]{:S(2)}) %collective-permute-start.12) | collective-permute-done | bytes 82976 | tf_op jit(solution)/shard_map/ppermute | solution.py:30
  103.3 0.5 fusion.6
  104.3 0.8 collective-permute-done.13
  105.1 1.1 collective-permute-start.15
  106.2 1.4 %collective-permute-done.16 = f32[1,1,128]{2,1,0:T(1,128)S(1)} collective-permute-done((f32[1,1,128]{2,1,0:T(1,128)S(1)}, f32[1,1,128]{2,1,0:T(1,128)S(1)}, u32[]{:S(2)}, u32[]{:S(2)}) %collective-permute-start.16) | collective-permute-done | bytes 544 | tf_op jit(solution)/shard_map/ppermute | solution.py:40
  107.7 1.0 collective-permute-done.15
  108.9 0.6 pad_maximum_fusion.17
  (91 shorter events, 7.3 us)
Async XLA Ops:
  1.1 4.2 %copy-start.6 = (f32[16,32,128]{2,1,0:T(8,128)S(1)}, f32[16,32,128]{2,1,0:T(8,128)}, u32[]{:S(2)}) copy-start(f32[16,32,128]{2,1,0:T(8,128)} %param.6) | copy-start | bytes 786436
  5.4 0.8 copy-start.11
  7.0 30.1 %collective-permute-start.6 = (f32[3,9,32,128]{3,2,1,0:T(8,128)}, f32[3,9,32,128]{3,2,1,0:T(8,128)}, u32[]{:S(2)}, u32[]{:S(2)}) collective-permute-start(f32[3,9,32,128]{3,2,1,0:T(8,128)} %pad_maximum_fusion.13), channel_id=1, source_target_pairs={{0,1},{2,3},{4,5},{6,7},{8,9},{10,11},{12,13},{14,15},{16,17},{18,... | collective-permute-start | bytes 1327112 | tf_op jit(solution)/shard_map/ppermute | solution.py:82
  11.2 25.9 %collective-permute-start.7 = (f32[3,9,32,128]{3,2,1,0:T(8,128)}, f32[3,9,32,128]{3,2,1,0:T(8,128)}, u32[]{:S(2)}, u32[]{:S(2)}) collective-permute-start(f32[3,9,32,128]{3,2,1,0:T(8,128)} %pad_maximum_fusion.13), channel_id=1, source_target_pairs={{1,0},{3,2},{5,4},{7,6},{9,8},{11,10},{13,12},{15,14},{17,16},{19,... | collective-permute-start | bytes 1327112 | tf_op jit(solution)/shard_map/ppermute | solution.py:83
  13.1 8.0 %collective-permute-start = (f32[2,32,128]{2,1,0:T(8,128)}, f32[2,32,128]{2,1,0:T(8,128)S(1)}, u32[]{:S(2)}, u32[]{:S(2)}) collective-permute-start(f32[2,32,128]{2,1,0:T(8,128)} %get-tuple-element.47), channel_id=1, source_target_pairs={{0,8},{8,16},{16,24},{1,9},{9,17},{17,25},{2,10},{10,18},{18,26},{... | collective-permute-start | bytes 98312 | tf_op jit(solution)/shard_map/ppermute | solution.py:19
  16.6 6.0 %collective-permute-start.1 = (f32[2,32,128]{2,1,0:T(8,128)}, f32[2,32,128]{2,1,0:T(8,128)S(1)}, u32[]{:S(2)}, u32[]{:S(2)}) collective-permute-start(f32[2,32,128]{2,1,0:T(8,128)} %get-tuple-element.46), channel_id=1, source_target_pairs={{8,0},{16,8},{24,16},{9,1},{17,9},{25,17},{10,2},{18,10},{26,18},{... | collective-permute-start | bytes 98312 | tf_op jit(solution)/shard_map/ppermute | solution.py:22
  23.5 5.6 %collective-permute-start.2 = (f32[20,32,2]{2,1,0:T(8,128)}, f32[20,32,2]{2,1,0:T(8,128)S(1)}, u32[]{:S(2)}, u32[]{:S(2)}) collective-permute-start(f32[20,32,2]{2,1,0:T(8,128)} %get-tuple-element.43), channel_id=1, source_target_pairs={{0,2},{2,4},{4,6},{1,3},{3,5},{5,7},{8,10},{10,12},{12,14},{9,11},... | collective-permute-start | bytes 15368 | tf_op jit(solution)/shard_map/ppermute | solution.py:19
  24.8 5.4 %collective-permute-start.3 = (f32[20,32,2]{2,1,0:T(8,128)}, f32[20,32,2]{2,1,0:T(8,128)S(1)}, u32[]{:S(2)}, u32[]{:S(2)}) collective-permute-start(f32[20,32,2]{2,1,0:T(8,128)} %get-tuple-element.44), channel_id=1, source_target_pairs={{2,0},{4,2},{6,4},{3,1},{5,3},{7,5},{10,8},{12,10},{14,12},{11,9},... | collective-permute-start | bytes 15368 | tf_op jit(solution)/shard_map/ppermute | solution.py:22
  26.2 28.4 %collective-permute-start.14 = (f32[1,2,128]{2,1,0:T(2,128)S(1)}, f32[1,2,128]{2,1,0:T(2,128)S(1)}, u32[]{:S(2)}, u32[]{:S(2)}) collective-permute-start(f32[1,2,128]{2,1,0:T(2,128)S(1)} %bitcast.315), channel_id=1, source_target_pairs={{0,2},{2,0},{4,6},{6,4},{1,3},{3,1},{5,7},{7,5},{8,10},{10,8},{12,... | collective-permute-start | bytes 3080 | tf_op jit(solution)/shard_map/ppermute | solution.py:40
  29.1 9.3 %copy-start.2 = (f32[20,32,2]{2,1,0:T(8,128)}, f32[20,32,2]{2,1,0:T(8,128)S(1)}, u32[]{:S(2)}) copy-start(f32[20,32,2]{2,1,0:T(8,128)S(1)} %collective-permute-done.2) | copy-start | bytes 15364
  30.3 8.1 %copy-start.4 = (f32[20,32,2]{2,1,0:T(8,128)}, f32[20,32,2]{2,1,0:T(8,128)S(1)}, u32[]{:S(2)}) copy-start(f32[20,32,2]{2,1,0:T(8,128)S(1)} %collective-permute-done.3) | copy-start | bytes 15364
  30.5 24.2 %collective-permute-start.4 = (f32[20,2,132]{2,1,0:T(2,128)S(1)}, f32[20,2,132]{2,1,0:T(2,128)S(1)}, u32[]{:S(2)}, u32[]{:S(2)}) collective-permute-start(f32[20,2,132]{2,1,0:T(2,128)S(1)} %get-tuple-element.41), channel_id=1, source_target_pairs={{0,1},{2,3},{4,5},{6,7},{8,9},{10,11},{12,13},{14,15},{16,17},{18,... | collective-permute-start | bytes 63368 | tf_op jit(solution)/shard_map/ppermute | solution.py:19
  35.8 19.5 %collective-permute-start.5 = (f32[20,2,132]{2,1,0:T(2,128)S(1)}, f32[20,2,132]{2,1,0:T(2,128)}, u32[]{:S(2)}, u32[]{:S(2)}) collective-permute-start(f32[20,2,132]{2,1,0:T(2,128)S(1)} %get-tuple-element.42), channel_id=1, source_target_pairs={{1,0},{3,2},{5,4},{7,6},{9,8},{11,10},{13,12},{15,14},{17,16},{19,... | collective-permute-start | bytes 63368 | tf_op jit(solution)/shard_map/ppermute | solution.py:22
  42.9 13.9 %collective-permute-start.8 = (f32[3,9,96,32]{2,3,1,0:T(8,128)}, f32[3,9,96,32]{2,3,1,0:T(8,128)}, u32[]{:S(2)}, u32[]{:S(2)}) collective-permute-start(f32[3,9,96,32]{2,3,1,0:T(8,128)} %copy.33), channel_id=1, source_target_pairs={{0,2},{2,4},{4,6},{1,3},{3,5},{5,7},{8,10},{10,12},{12,14},{9,11},... | collective-permute-start | bytes 995336 | tf_op jit(solution)/shard_map/ppermute | solution.py:82
  53.2 6.2 %collective-permute-start.9 = (f32[3,9,96,32]{2,3,1,0:T(8,128)}, f32[3,9,96,32]{2,3,1,0:T(8,128)}, u32[]{:S(2)}, u32[]{:S(2)}) collective-permute-start(f32[3,9,96,32]{2,3,1,0:T(8,128)} %copy.34), channel_id=1, source_target_pairs={{2,0},{4,2},{6,4},{3,1},{5,3},{7,5},{10,8},{12,10},{14,12},{11,9},... | collective-permute-start | bytes 995336 | tf_op jit(solution)/shard_map/ppermute | solution.py:83
  54.7 0.6 copy-start.12
  61.9 3.0 %copy-start = (f32[3,9,96,32]{3,2,1,0:T(8,128)S(1)}, f32[3,9,96,32]{3,2,1,0:T(8,128)}, u32[]{:S(2)}) copy-start(f32[3,9,96,32]{3,2,1,0:T(8,128)} %copy.35) | copy-start | bytes 995332
  61.9 3.0 %copy-start.1 = (f32[3,9,96,32]{3,2,1,0:T(8,128)S(1)}, f32[3,9,96,32]{3,2,1,0:T(8,128)}, u32[]{:S(2)}) copy-start(f32[3,9,96,32]{3,2,1,0:T(8,128)} %copy.36) | copy-start | bytes 995332
  68.5 3.6 %copy-start.3 = (f32[20,32,2]{2,1,0:T(8,128)S(1)}, f32[20,32,2]{2,1,0:T(8,128)}, u32[]{:S(2)}) copy-start(f32[20,32,2]{2,1,0:T(8,128)} %copy-done.2) | copy-start | bytes 15364
  68.5 3.6 %copy-start.5 = (f32[20,32,2]{2,1,0:T(8,128)S(1)}, f32[20,32,2]{2,1,0:T(8,128)}, u32[]{:S(2)}) copy-start(f32[20,32,2]{2,1,0:T(8,128)} %copy-done.4) | copy-start | bytes 15364
  68.5 3.6 %copy-start.13 = (f32[20,2,132]{2,1,0:T(2,128)S(1)}, f32[20,2,132]{2,1,0:T(2,128)}, u32[]{:S(2)}) copy-start(f32[20,2,132]{2,1,0:T(2,128)} %copy-done.12) | copy-start | bytes 63364
  69.3 8.4 %collective-permute-start.10 = (f32[3,80,176]{2,1,0:T(8,128)S(1)}, f32[3,80,176]{2,1,0:T(8,128)S(1)}, u32[]{:S(2)}, u32[]{:S(2)}) collective-permute-start(f32[3,80,176]{2,1,0:T(8,128)S(1)} %fusion.59), channel_id=1, source_target_pairs={{0,8},{8,16},{16,24},{1,9},{9,17},{17,25},{2,10},{10,18},{18,26},{... | collective-permute-start | bytes 506888 | tf_op jit(solution)/shard_map/ppermute | solution.py:30
  80.7 8.5 %collective-permute-start.11 = (f32[3,64,160]{2,1,0:T(8,128)S(1)}, f32[3,64,160]{2,1,0:T(8,128)S(1)}, u32[]{:S(2)}, u32[]{:S(2)}) collective-permute-start(f32[3,64,160]{2,1,0:T(8,128)S(1)} %fusion.91), channel_id=1, source_target_pairs={{0,8},{8,16},{16,24},{1,9},{9,17},{17,25},{2,10},{10,18},{18,26},{... | collective-permute-start | bytes 368648 | tf_op jit(solution)/shard_map/ppermute | solution.py:30
  91.8 8.6 %collective-permute-start.12 = (f32[3,48,144]{2,1,0:T(8,128)S(1)}, f32[3,48,144]{2,1,0:T(8,128)S(1)}, u32[]{:S(2)}, u32[]{:S(2)}) collective-permute-start(f32[3,48,144]{2,1,0:T(8,128)S(1)} %fusion.123), channel_id=1, source_target_pairs={{0,8},{8,16},{16,24},{1,9},{9,17},{17,25},{2,10},{10,18},{18,26},{... | collective-permute-start | bytes 248840 | tf_op jit(solution)/shard_map/ppermute | solution.py:30
  101.9 1.1 copy-start.7
  102.0 1.2 %copy-start.8 = (f32[3,8,2,32,128]{4,3,2,1,0:T(8,128)S(1)}, f32[3,8,2,32,128]{4,3,2,1,0:T(8,128)}, u32[]{:S(2)}) copy-start(f32[3,8,2,32,128]{4,3,2,1,0:T(8,128)} %fusion.176) | copy-start | bytes 2359300
  102.0 1.3 %copy-start.9 = (f32[16,32,128]{2,1,0:T(8,128)S(1)}, f32[16,32,128]{2,1,0:T(8,128)}, u32[]{:S(2)}) copy-start(f32[16,32,128]{2,1,0:T(8,128)} %fusion.3) | copy-start | bytes 786436
  102.0 1.3 %copy-start.10 = (f32[16,32,128]{2,1,0:T(8,128)S(1)}, f32[16,32,128]{2,1,0:T(8,128)}, u32[]{:S(2)}) copy-start(f32[16,32,128]{2,1,0:T(8,128)} %get-tuple-element.37) | copy-start | bytes 786436
  103.9 1.2 %collective-permute-start.13 = (f32[3,2,128]{2,1,0:T(2,128)S(1)}, f32[3,2,128]{2,1,0:T(2,128)S(1)}, u32[]{:S(2)}, u32[]{:S(2)}) collective-permute-start(f32[3,2,128]{2,1,0:T(2,128)S(1)} %bitcast.314), channel_id=1, source_target_pairs={{0,2},{2,0},{4,6},{6,4},{1,3},{3,1},{5,7},{7,5},{8,10},{10,8},{12,... | collective-permute-start | bytes 9224 | tf_op jit(solution)/shard_map/ppermute | solution.py:40
  104.1 3.6 %collective-permute-start.16 = (f32[1,1,128]{2,1,0:T(1,128)S(1)}, f32[1,1,128]{2,1,0:T(1,128)S(1)}, u32[]{:S(2)}, u32[]{:S(2)}) collective-permute-start(f32[1,1,128]{2,1,0:T(1,128)S(1)} %fusion.161), channel_id=1, source_target_pairs={{0,4},{4,0},{2,6},{6,2},{1,5},{5,1},{3,7},{7,3},{8,12},{12,8},{10,... | collective-permute-start | bytes 1544 | tf_op jit(solution)/shard_map/ppermute | solution.py:40
  105.1 3.6 %collective-permute-start.15 = (f32[3,1,128]{2,1,0:T(1,128)S(1)}, f32[3,1,128]{2,1,0:T(1,128)S(1)}, u32[]{:S(2)}, u32[]{:S(2)}) collective-permute-start(f32[3,1,128]{2,1,0:T(1,128)S(1)} %fusion.156), channel_id=1, source_target_pairs={{0,4},{4,0},{2,6},{6,2},{1,5},{5,1},{3,7},{7,3},{8,12},{12,8},{10,... | collective-permute-start | bytes 4616 | tf_op jit(solution)/shard_map/ppermute | solution.py:40

commit v6 on v5

--- a/solution.py
+++ b/solution.py
@@ -135,13 +135,6 @@
     light_idx = lax.axis_index("light")
     view_idx = lax.axis_index("view")
     across_idx = lax.axis_index("across")
-    padded = padded_2(density, (("light", 0), ("view", 2), ("across", 1)), 2)
-    inside = (
-        rim_mask(light_idx, n_light, brick_l, 1)[:, None, None]
-        * rim_mask(across_idx, n_across, brick_a, 1)[None, :, None]
-        * rim_mask(view_idx, n_view, brick_v, 1)[None, None, :]
-    )
-    shading = shade_from(padded, inside)
     table_all = jnp.concatenate([opacity_table[None], extinction_table, albedo_table], axis=0)
     looked = jnp.broadcast_to(table_all[:, 0, None, None, None], (7,) + labels.shape)
     for material in range(1, table_all.shape[1]):
@@ -153,10 +146,25 @@
     running = jnp.cumsum(extinct_slabs, axis=2) - extinct_slabs
     slab_depth = jnp.sum(extinct_slabs, axis=2)
     widest = SLABS * n_light
-    both = jnp.concatenate([slab_depth, sunlight[:, None]], axis=1)
-    both_rim = halo(halo(both, "across", 2, widest), "view", 3, widest)
-    sun_rim = both_rim[:, SLABS]
-    fade_rim = jnp.exp(-light_step * both_rim[:, :SLABS]) * plane_mask(widest, brick_a, brick_v)
+    stack = jnp.concatenate(
+        [density, slab_depth.reshape(3 * SLABS, brick_a, brick_v), sunlight], axis=0
+    )
+    stack_rim = halo(halo(stack, "view", 2, widest), "across", 1, widest)
+    rim_a = brick_a + 2 * widest
+    rim_v = brick_v + 2 * widest
+    depth_rim = stack_rim[brick_l : brick_l + 3 * SLABS].reshape(3, SLABS, rim_a, rim_v)
+    sun_rim = stack_rim[brick_l + 3 * SLABS :]
+    fade_rim = jnp.exp(-light_step * depth_rim) * plane_mask(widest, brick_a, brick_v)
+    density_side = stack_rim[
+        :brick_l, widest - 2 : widest + brick_a + 2, widest - 2 : widest + brick_v + 2
+    ]
+    padded = padded_2(density_side, (("light", 0),), 2)
+    inside = (
+        rim_mask(light_idx, n_light, brick_l, 1)[:, None, None]
+        * rim_mask(across_idx, n_across, brick_a, 1)[None, :, None]
+        * rim_mask(view_idx, n_view, brick_v, 1)[None, None, :]
+    )
+    shading = shade_from(padded, inside)
     starts = None
     incoming = sun_rim
     for section_num in range(n_light):
@@ -182,27 +190,25 @@
     transmit = jnp.exp(-jnp.sum(optical, axis=-1))
     pixels = brick_l * brick_a
     piece_len = pixels // n_view
-    colour_now = colour_sum.reshape(3, n_view, piece_len)
-    transmit_now = transmit.reshape(1, n_view, piece_len)
+    image_now = jnp.concatenate(
+        [colour_sum.reshape(3, n_view, piece_len), transmit.reshape(1, n_view, piece_len)], axis=0
+    )
     bit_count = n_view.bit_length() - 1
     for bit_num in range(bit_count):
-        kept = colour_now.shape[1]
-        colour_pairs = colour_now.reshape(3, kept // 2, 2, piece_len)
-        transmit_pairs = transmit_now.reshape(1, kept // 2, 2, piece_len)
+        kept = image_now.shape[1]
+        pairs = image_now.reshape(4, kept // 2, 2, piece_len)
         my_bit = view_idx // 2**bit_num % 2
         first_half = my_bit == 0
-        keep_colour = jnp.where(first_half, colour_pairs[:, :, 0], colour_pairs[:, :, 1])
-        send_colour = jnp.where(first_half, colour_pairs[:, :, 1], colour_pairs[:, :, 0])
-        keep_transmit = jnp.where(first_half, transmit_pairs[:, :, 0], transmit_pairs[:, :, 1])
-        send_transmit = jnp.where(first_half, transmit_pairs[:, :, 1], transmit_pairs[:, :, 0])
-        got_colour, got_transmit = from_partner((send_colour, send_transmit), "view", bit_num)
-        front_colour = jnp.where(first_half, keep_colour, got_colour)
-        back_colour = jnp.where(first_half, got_colour, keep_colour)
-        front_transmit = jnp.where(first_half, keep_transmit, got_transmit)
-        colour_now = front_colour + front_transmit * back_colour
-        transmit_now = keep_transmit * got_transmit
-    final_colour = colour_now[:, 0]
-    final_transmit = transmit_now[:, 0]
+        keep = jnp.where(first_half, pairs[:, :, 0], pairs[:, :, 1])
+        send = jnp.where(first_half, pairs[:, :, 1], pairs[:, :, 0])
+        got = from_partner(send, "view", bit_num)
+        front = jnp.where(first_half, keep, got)
+        back = jnp.where(first_half, got, keep)
+        image_now = jnp.concatenate(
+            [front[:3] + front[3:] * back[:3], keep[3:] * got[3:]], axis=0
+        )
+    final_colour = image_now[:3, 0]
+    final_transmit = image_now[3:, 0]
     rows_out = brick_l // n_view
     opacity = 1.0 - final_transmit.reshape(1, rows_out, brick_a)
     return jnp.concatenate([final_colour.reshape(3, rows_out, brick_a), opacity], axis=0)

time: 111 us -> 121 us (1.090)
  waiting for transfers between devices: 16.5 us -> 40.1 us
  starting transfers between devices: 42.7 us -> 30.2 us
  local copies, waits for them, and re-layouts: 16.8 us -> 14.7 us
    ppermute x2, waiting for transfers between devices: 0.01 us -> 20.6 us  [halo(): lows.insert(0, lax.ppermute(low, axis, forward))]
    ppermute x3 -> x1, starting transfers between devices: 10.1 us -> 4.28 us  [padded_2(): lax.ppermute(lax.slice_in_dim(block, block.shape[dim] - width, None, axis...]
    ppermute x2, starting transfers between devices: 11.9 us -> 6.19 us  [halo(): lows.insert(0, lax.ppermute(low, axis, forward))]
    ppermute x2, waiting for transfers between devices: 0.01 us -> 5.48 us  [halo(): lax.ppermute(lax.slice_in_dim(block, 0, need, axis=dim), axis, backward)]
    mul x4 -> x2, other arithmetic: 5.26 us -> 0.24 us  [the longest x1 0.24 us: shards(): jnp.exp(-light_step * depth_rim) * plane_mask(widest, brick_a, brick_v)]
    ppermute x4 -> x2, starting transfers between devices: 4.35 us -> 8.86 us  [from_partner(): return lax.ppermute(block, axis, route)]
    ppermute x3, starting transfers between devices: 8.58 us -> 5.97 us  [from_behind(): lax.ppermute(value, axis, [(source, source + steps) for source in range(l...]
    ppermute x3 -> x1, starting transfers between devices: 4.94 us -> 2.35 us  [padded_2(): lax.ppermute(lax.slice_in_dim(block, 0, width, axis=dim), axis, backward)]
  transfers between devices with their start and end apart: 17 -> 11, of which waited for: 8 -> 8; matrix products, arithmetic and copies ran while one was open for 21% -> 17% of each run, Pallas kernels for 0% -> 0%
where the time goes in v6:
time: 121 us; the launch traced here: 119 us
  waiting for transfers between devices  40.1 us (33%)
  other arithmetic  31.9 us (26%)
  starting transfers between devices  30.2 us (25%)
  local copies, waits for them, and re-layouts  14.7 us (12%)
  matrix products  1.93 us (2%)
    ppermute x2, waiting for transfers between devices, halo(): lows.insert(0, lax.ppermute(low, axis, forward))  20.6 us
    ppermute x3, waiting for transfers between devices, from_behind(): lax.ppermute(value, axis, [(source, source + steps) for source in range(l...  11.6 us
    mul x31, other arithmetic, propagate(): current = current * fade_here  11 us
    ppermute x2, starting transfers between devices, from_partner(): return lax.ppermute(block, axis, route)  8.86 us
    ppermute x2, starting transfers between devices, halo(): lows.insert(0, lax.ppermute(low, axis, forward))  6.19 us
    ppermute x3, starting transfers between devices, from_behind(): lax.ppermute(value, axis, [(source, source + steps) for source in range(l...  5.97 us
    ppermute x2, waiting for transfers between devices, halo(): lax.ppermute(lax.slice_in_dim(block, 0, need, axis=dim), axis, backward)  5.48 us
    ppermute x1, starting transfers between devices, padded_2(): lax.ppermute(lax.slice_in_dim(block, block.shape[dim] - width, None, axis...  4.28 us
  transfers between devices with their start and end apart: 11, of which 8 were waited for; matrix products, arithmetic and copies ran while one was open for 17% of the time, Pallas kernels for 0%

profile of v6, /device:TPU:16, one launch (start us, length us, event | category | flops | bytes accessed | tf_op | source)
XLA Modules:
  0.0 119.4 jit_solution(15150377651334086069)
XLA Ops:
  0.0 0.7 pad_maximum_fusion.9
  0.7 0.4 slice_reduce_fusion.15
  1.2 1.5 %broadcast_compare_fusion.14 = (pred[16,32,128]{2,1,0:T(8,128)(4,1)S(1)}, pred[16,32,128]{2,1,0:T(8,128)(4,1)S(1)}, pred[16,32,128]{2,1,0:T(8,128)(4,1)S(1)}, pr...) fusion(s32[16,32,128]{2,1,0:T(8,128)} %param.7), kind=kLoop, calls=%fused_computation.280 | loop fusion | flops 983040 | bytes 1245184 | tf_op jit(solution)/shard_map/eq | solution.py:142
  2.7 2.6 %select_select_fusion = f32[7,16,32,128]{3,2,1,0:T(8,128)S(1)} fusion(f32[7]{0:T(128)S(1)} %get-tuple-element.6, f32[7]{0:T(128)S(1)} %get-tuple-element.7, f32[7]{0:T(128)S(1)} %get-tuple-element.8, f32[7]{0:T(128)S(1)} %get-tuple-element.9, f32[7]{0:T(128)S(1)} %get-tuple-element.10, f32[7]{0:T(128)S(1)} %get-tuple-element.11, f32[7]{0:T(128)S(1)} %get-tuple-element.12, ...), kind=kLoop, calls=%fused_computation.4 | loop fusion | flops 6881280 | bytes 2818496 | tf_op jit(solution)/shard_map/jit(_where)/select_n | solution.py:141
  5.4 1.1 slice_multiply_fusion.1
  6.4 1.2 %reduce_sum.27 = f32[3,8,32,128]{3,2,1,0:T(8,128)S(1)} reduce(f32[3,8,2,32,128]{4,3,2,1,0:T(8,128)} %bitcast.221, f32[]{:T(128)} %constant.63.clone.1), dimensions={2}, to_apply=%region_0.1 | reduce | flops 98304 | bytes 1179652 | tf_op jit(solution)/shard_map/reduce_sum | solution.py:147
  7.7 1.1 fusion.160
  8.9 2.4 %copy.47 = f32[43,32,32]{0,2,1:T(8,128)} copy(f32[43,32,32]{2,1,0:T(8,128)} %get-tuple-element.45) | data formatting | bytes 352256 | tf_op jit(solution)/shard_map/slice | solution.py:81
  11.2 2.5 %collective-permute-start = (f32[43,32,32]{0,2,1:T(8,128)}, f32[43,32,32]{0,2,1:T(8,128)}, u32[]{:S(2)}, u32[]{:S(2)}) collective-permute-start(f32[43,32,32]{0,2,1:T(8,128)} %copy.47), channel_id=1, source_target_pairs={{0,2},{2,4},{4,6},{1,3},{3,5},{5,7},{8,10},{10,12},{12,14},{9,11},... | collective-permute-start | bytes 528392 | tf_op jit(solution)/shard_map/ppermute | solution.py:82
  13.8 1.3 %copy.48 = f32[43,32,32]{0,2,1:T(8,128)} copy(f32[43,32,32]{2,1,0:T(8,128)S(1)} %get-tuple-element.46) | data formatting | bytes 352256 | tf_op jit(solution)/shard_map/slice | solution.py:83
  15.1 1.3 %collective-permute-start.1 = (f32[43,32,32]{0,2,1:T(8,128)}, f32[43,32,32]{0,2,1:T(8,128)}, u32[]{:S(2)}, u32[]{:S(2)}) collective-permute-start(f32[43,32,32]{0,2,1:T(8,128)} %copy.48), channel_id=1, source_target_pairs={{2,0},{4,2},{6,4},{3,1},{5,3},{7,5},{10,8},{12,10},{14,12},{11,9},... | collective-permute-start | bytes 528392 | tf_op jit(solution)/shard_map/ppermute | solution.py:83
  16.4 0.8 fusion.152
  17.3 1.7 %copy.49 = f32[43,32,32]{2,1,0:T(8,128)S(1)} copy(f32[43,32,32]{0,2,1:T(8,128)} %collective-permute-done) | data formatting | bytes 352256 | tf_op jit(solution)/shard_map/ppermute | solution.py:82
  19.0 0.7 collective-permute-done.1
  19.7 1.7 %copy.50 = f32[43,32,32]{2,1,0:T(8,128)S(1)} copy(f32[43,32,32]{0,2,1:T(8,128)} %collective-permute-done.1) | data formatting | bytes 352256 | tf_op jit(solution)/shard_map/ppermute | solution.py:83
  21.4 0.9 copy-done
  22.3 0.6 pad_maximum_fusion.1
  23.0 3.6 %collective-permute-start.2 = (f32[43,32,192]{2,1,0:T(8,128)S(1)}, f32[43,32,192]{2,1,0:T(8,128)S(1)}, u32[]{:S(2)}, u32[]{:S(2)}) collective-permute-start(f32[43,32,192]{2,1,0:T(8,128)S(1)} %pad_maximum_fusion.1), channel_id=1, source_target_pairs={{0,1},{2,3},{4,5},{6,7},{8,9},{10,11},{12,13},{14,15},{16,17},{18,... | collective-permute-start | bytes 3170312 | tf_op jit(solution)/shard_map/ppermute | solution.py:82
  26.6 1.3 %collective-permute-start.3 = (f32[43,32,192]{2,1,0:T(8,128)S(1)}, f32[43,32,192]{2,1,0:T(8,128)S(1)}, u32[]{:S(2)}, u32[]{:S(2)}) collective-permute-start(f32[43,32,192]{2,1,0:T(8,128)S(1)} %pad_maximum_fusion.1), channel_id=1, source_target_pairs={{1,0},{3,2},{5,4},{7,6},{9,8},{11,10},{13,12},{15,14},{17,16},{19,... | collective-permute-start | bytes 3170312 | tf_op jit(solution)/shard_map/ppermute | solution.py:83
  28.0 1.9 %fusion.1 = f32[16,32,128]{2,1,0:T(8,128)} fusion(f32[16,32,128]{2,1,0:T(8,128)S(1)} %copy-done.4, f32[7,16,32,128]{3,2,1,0:T(8,128)} %copy-done.12), kind=kOutput, calls=%fused_computation.7 | convolution fusion | flops 100876288 | bytes 786432 | tf_op jit(solution)/shard_map/dot_general | solution.py:186
  30.0 1.0 fusion.164
  31.0 20.6 %collective-permute-done.2 = f32[43,32,192]{2,1,0:T(8,128)S(1)} collective-permute-done((f32[43,32,192]{2,1,0:T(8,128)S(1)}, f32[43,32,192]{2,1,0:T(8,128)S(1)}, u32[]{:S(2)}, u32[]{:S(2)}) %collective-permute-start.2) | collective-permute-done | bytes 1056800 | tf_op jit(solution)/shard_map/ppermute | solution.py:82
  51.5 4.8 %collective-permute-done.3 = f32[43,32,192]{2,1,0:T(8,128)S(1)} collective-permute-done((f32[43,32,192]{2,1,0:T(8,128)S(1)}, f32[43,32,192]{2,1,0:T(8,128)S(1)}, u32[]{:S(2)}, u32[]{:S(2)}) %collective-permute-start.3) | collective-permute-done | bytes 1056800 | tf_op jit(solution)/shard_map/ppermute | solution.py:83
  56.3 0.8 pad_maximum_fusion.7
  57.1 2.3 %collective-permute-start.4 = (f32[2,36,132]{2,1,0:T(8,128)}, f32[2,36,132]{2,1,0:T(8,128)}, u32[]{:S(2)}, u32[]{:S(2)}) collective-permute-start(f32[2,36,132]{2,1,0:T(8,128)} %get-tuple-element.39), channel_id=1, source_target_pairs={{8,0},{16,8},{24,16},{9,1},{17,9},{25,17},{10,2},{18,10},{26,18},{... | collective-permute-start | bytes 114056 | tf_op jit(solution)/shard_map/ppermute | solution.py:22
  59.5 4.3 %collective-permute-start.5 = (f32[2,36,132]{2,1,0:T(8,128)}, f32[2,36,132]{2,1,0:T(8,128)}, u32[]{:S(2)}, u32[]{:S(2)}) collective-permute-start(f32[2,36,132]{2,1,0:T(8,128)} %get-tuple-element.40), channel_id=1, source_target_pairs={{0,8},{8,16},{16,24},{1,9},{9,17},{17,25},{2,10},{10,18},{18,26},{... | collective-permute-start | bytes 114056 | tf_op jit(solution)/shard_map/ppermute | solution.py:19
  63.8 3.0 %pad_maximum_fusion = f32[43,96,192]{2,1,0:T(8,128)S(1)} fusion(f32[43,32,192]{2,1,0:T(8,128)S(1)} %collective-permute-done.3, f32[43,32,32]{2,1,0:T(8,128)S(1)} %copy-done.1, f32[3,32,128]{2,1,0:T(8,128)S(1)} %copy-done.16, f32[24,32,128]{2,1,0:T(8,128)S(1)} %bitcast.215, f32[16,32,128]{2,1,0:T(8,128)S(1)} %copy-done.4, f32[43,32,32]{2,1,0:T(8,128)S(1)} %copy.49, ...), kind=kLoop, calls=%fused_computation | loop fusion | flops 4755456 | bytes 6340608 | tf_op jit(solution)/shard_map/concatenate | solution.py:84
  67.1 1.6 %copy-done.11 = f32[43,96,192]{2,1,0:T(8,128)} copy-done((f32[43,96,192]{2,1,0:T(8,128)}, f32[43,96,192]{2,1,0:T(8,128)S(1)}, u32[]{:S(2)}) %copy-start.11) | copy-done | bytes 3170328
  69.1 0.4 fusion.14
  69.5 0.4 fusion.10
  70.0 0.4 fusion.6
  70.4 0.4 fusion.31
  70.8 0.4 fusion.27
  71.3 0.4 fusion.23
  71.7 0.4 fusion.19
  72.1 1.0 fusion.57
  73.2 1.9 %collective-permute-start.6 = (f32[3,80,176]{2,1,0:T(8,128)}, f32[3,80,176]{2,1,0:T(8,128)}, u32[]{:S(2)}, u32[]{:S(2)}) collective-permute-start(f32[3,80,176]{2,1,0:T(8,128)} %fusion.57), channel_id=1, source_target_pairs={{0,8},{8,16},{16,24},{1,9},{9,17},{17,25},{2,10},{10,18},{18,26},{... | collective-permute-start | bytes 506888 | tf_op jit(solution)/shard_map/ppermute | solution.py:30
  75.2 1.5 %slice.1052 = f32[16,36,132]{2,1,0:T(8,128)S(1)} slice(f32[43,96,192]{2,1,0:T(8,128)} %copy-done.11), slice={[0:16], [30:66], [30:162]} | slice | bytes 608256 | tf_op jit(solution)/shard_map/slice | solution.py:158
  76.7 1.0 pad_maximum_fusion.2
  77.7 3.9 %collective-permute-done.6 = f32[3,80,176]{2,1,0:T(8,128)} collective-permute-done((f32[3,80,176]{2,1,0:T(8,128)}, f32[3,80,176]{2,1,0:T(8,128)}, u32[]{:S(2)}, u32[]{:S(2)}) %collective-permute-start.6) | collective-permute-done | bytes 168992 | tf_op jit(solution)/shard_map/ppermute | solution.py:30
  81.6 1.3 %fusion.54 = f32[3,80,176]{2,1,0:T(8,128)S(1)} fusion(f32[3,8,96,192]{3,2,0,1:T(8,128)} %copy-done.6, f32[3,80,176]{2,1,0:T(8,128)} %collective-permute-done.6, f32[43,32,192]{2,1,0:T(8,128)S(1)} %collective-permute-done.3, f32[43,32,192]{2,1,0:T(8,128)S(1)} %collective-permute-done.2, f32[43,32,32]{2,1,0:T(8,128)S(1)} %copy-done.2, ...), kind=kLoop, calls=%fused_computation.128 | loop fusion | flops 337920 | bytes 3677185 | tf_op jit(solution)/shard_map/mul | solution.py:113
  82.9 0.4 fusion.50
  83.3 0.4 fusion.46
  83.7 0.4 fusion.42
  84.1 0.4 fusion.70
  84.4 0.4 fusion.66
  84.8 0.4 fusion.62
  85.1 0.4 fusion.58
  85.8 1.9 %collective-permute-start.7 = (f32[3,64,160]{2,1,0:T(8,128)S(1)}, f32[3,64,160]{2,1,0:T(8,128)S(1)}, u32[]{:S(2)}, u32[]{:S(2)}) collective-permute-start(f32[3,64,160]{2,1,0:T(8,128)S(1)} %fusion.89), channel_id=1, source_target_pairs={{0,8},{8,16},{16,24},{1,9},{9,17},{17,25},{2,10},{10,18},{18,26},{... | collective-permute-start | bytes 368648 | tf_op jit(solution)/shard_map/ppermute | solution.py:30
  87.7 2.1 %multiply_multiply_fusion.1 = (f32[18,34,130]{2,1,0:T(8,128)S(1)}, f32[18,34,130]{2,1,0:T(8,128)S(1)}) fusion(f32[16,36,132]{2,1,0:T(8,128)S(1)} %slice.1052, f32[2,36,132]{2,1,0:T(8,128)} %collective-permute-done.5, f32[2,36,132]{2,1,0:T(8,128)} %collective-permute-done.4, f32[130]{0:T(256)S(1)} %and_convert_fusion.2, ...), kind=kLoop, calls=%fused_computation.9 | loop fusion | flops 1750320 | bytes 2292568 | tf_op jit(solution)/shard_map/mul | solution.py:61
  89.8 3.6 %collective-permute-done.7 = f32[3,64,160]{2,1,0:T(8,128)S(1)} collective-permute-done((f32[3,64,160]{2,1,0:T(8,128)S(1)}, f32[3,64,160]{2,1,0:T(8,128)S(1)}, u32[]{:S(2)}, u32[]{:S(2)}) %collective-permute-start.7) | collective-permute-done | bytes 122912 | tf_op jit(solution)/shard_map/ppermute | solution.py:30
  93.5 0.3 fusion.82
  93.9 0.3 fusion.78
  94.2 0.3 fusion.74
  95.9 2.1 %collective-permute-start.8 = (f32[3,48,144]{2,1,0:T(8,128)S(1)}, f32[3,48,144]{2,1,0:T(8,128)S(1)}, u32[]{:S(2)}, u32[]{:S(2)}) collective-permute-start(f32[3,48,144]{2,1,0:T(8,128)S(1)} %fusion.121), channel_id=1, source_target_pairs={{0,8},{8,16},{16,24},{1,9},{9,17},{17,25},{2,10},{10,18},{18,26},{... | collective-permute-start | bytes 248840 | tf_op jit(solution)/shard_map/ppermute | solution.py:30
  98.1 0.9 fusion.38
  99.0 4.2 %collective-permute-done.8 = f32[3,48,144]{2,1,0:T(8,128)S(1)} collective-permute-done((f32[3,48,144]{2,1,0:T(8,128)S(1)}, f32[3,48,144]{2,1,0:T(8,128)S(1)}, u32[]{:S(2)}, u32[]{:S(2)}) %collective-permute-start.8) | collective-permute-done | bytes 82976 | tf_op jit(solution)/shard_map/ppermute | solution.py:30
  105.9 0.4 copy-done.13
  106.7 0.5 fusion.4
  107.3 1.9 %collective-permute-start.9 = (f32[4,2,128]{2,1,0:T(2,128)S(1)}, f32[4,2,128]{2,1,0:T(2,128)S(1)}, u32[]{:S(2)}, u32[]{:S(2)}) collective-permute-start(f32[4,2,128]{2,1,0:T(2,128)S(1)} %bitcast.230), channel_id=1, source_target_pairs={{0,2},{2,0},{4,6},{6,4},{1,3},{3,1},{5,7},{7,5},{8,10},{10,8},{12,... | collective-permute-start | bytes 12296 | tf_op jit(solution)/shard_map/ppermute | solution.py:40
  109.2 0.8 collective-permute-done.9
  110.0 7.0 %collective-permute-start.10 = (f32[4,1,128]{2,0,1:T(4,128)S(1)}, f32[4,1,128]{2,0,1:T(4,128)S(1)}, u32[]{:S(2)}, u32[]{:S(2)}) collective-permute-start(f32[4,1,128]{2,0,1:T(4,128)S(1)} %bitcast.231), channel_id=1, source_target_pairs={{0,4},{4,0},{2,6},{6,2},{1,5},{5,1},{3,7},{7,3},{8,12},{12,8},{10,... | collective-permute-start | bytes 6152 | tf_op jit(solution)/shard_map/ppermute | solution.py:40
  117.0 1.6 %collective-permute-done.10 = f32[4,1,128]{2,0,1:T(4,128)S(1)} collective-permute-done((f32[4,1,128]{2,0,1:T(4,128)S(1)}, f32[4,1,128]{2,0,1:T(4,128)S(1)}, u32[]{:S(2)}, u32[]{:S(2)}) %collective-permute-start.10) | collective-permute-done | bytes 2080 | tf_op jit(solution)/shard_map/ppermute | solution.py:40
  118.8 0.6 pad_maximum_fusion.8
  (97 shorter events, 6.2 us)
Async XLA Ops:
  1.1 4.2 %copy-start.3 = (f32[16,32,128]{2,1,0:T(8,128)S(1)}, f32[16,32,128]{2,1,0:T(8,128)}, u32[]{:S(2)}) copy-start(f32[16,32,128]{2,1,0:T(8,128)} %param.6) | copy-start | bytes 786436
  5.3 11.1 %copy-start.12 = (f32[7,16,32,128]{3,2,1,0:T(8,128)}, f32[7,16,32,128]{3,2,1,0:T(8,128)S(1)}, u32[]{:S(2)}) copy-start(f32[7,16,32,128]{3,2,1,0:T(8,128)S(1)} %select_select_fusion) | copy-start | bytes 5505028
  5.4 2.3 %copy-start.15 = (f32[3,32,128]{2,1,0:T(8,128)S(1)}, f32[3,32,128]{2,1,0:T(8,128)}, u32[]{:S(2)}) copy-start(f32[3,32,128]{2,1,0:T(8,128)} %param.8) | copy-start | bytes 147460
  7.7 13.8 %copy-start.8 = (f32[3,8,32,128]{3,2,1,0:T(8,128)}, f32[3,8,32,128]{3,2,1,0:T(8,128)S(1)}, u32[]{:S(2)}) copy-start(f32[3,8,32,128]{3,2,1,0:T(8,128)S(1)} %reduce_sum.27) | copy-start | bytes 1179652
  11.2 6.0 %collective-permute-start = (f32[43,32,32]{0,2,1:T(8,128)}, f32[43,32,32]{0,2,1:T(8,128)}, u32[]{:S(2)}, u32[]{:S(2)}) collective-permute-start(f32[43,32,32]{0,2,1:T(8,128)} %copy.47), channel_id=1, source_target_pairs={{0,2},{2,4},{4,6},{1,3},{3,5},{5,7},{8,10},{10,12},{12,14},{9,11},... | collective-permute-start | bytes 528392 | tf_op jit(solution)/shard_map/ppermute | solution.py:82
  15.1 4.6 %collective-permute-start.1 = (f32[43,32,32]{0,2,1:T(8,128)}, f32[43,32,32]{0,2,1:T(8,128)}, u32[]{:S(2)}, u32[]{:S(2)}) collective-permute-start(f32[43,32,32]{0,2,1:T(8,128)} %copy.48), channel_id=1, source_target_pairs={{2,0},{4,2},{6,4},{3,1},{5,3},{7,5},{10,8},{12,10},{14,12},{11,9},... | collective-permute-start | bytes 528392 | tf_op jit(solution)/shard_map/ppermute | solution.py:83
  21.4 0.9 copy-start
  22.3 5.7 %copy-start.4 = (f32[16,32,128]{2,1,0:T(8,128)S(1)}, f32[16,32,128]{2,1,0:T(8,128)}, u32[]{:S(2)}) copy-start(f32[16,32,128]{2,1,0:T(8,128)} %param.6) | copy-start | bytes 786436
  22.3 7.7 %copy-start.14 = (f32[3,16,32,128]{3,2,1,0:T(8,128)S(1)}, f32[3,16,32,128]{3,2,1,0:T(8,128)}, u32[]{:S(2)}) copy-start(f32[3,16,32,128]{3,2,1,0:T(8,128)} %slice_multiply_fusion.1) | copy-start | bytes 2359300
  22.9 33.4 %copy-start.1 = (f32[43,32,32]{2,1,0:T(8,128)S(1)}, f32[43,32,32]{2,1,0:T(8,128)}, u32[]{:S(2)}) copy-start(f32[43,32,32]{2,1,0:T(8,128)} %copy-done) | copy-start | bytes 528388
  22.9 33.3 %copy-start.9 = (f32[3,8,32,128]{3,2,1,0:T(8,128)S(1)}, f32[3,8,32,128]{3,2,1,0:T(8,128)}, u32[]{:S(2)}) copy-start(f32[3,8,32,128]{3,2,1,0:T(8,128)} %copy-done.8) | copy-start | bytes 1179652
  22.9 33.3 %copy-start.16 = (f32[3,32,128]{2,1,0:T(8,128)S(1)}, f32[3,32,128]{2,1,0:T(8,128)}, u32[]{:S(2)}) copy-start(f32[3,32,128]{2,1,0:T(8,128)} %param.8) | copy-start | bytes 147460
  23.0 28.6 %collective-permute-start.2 = (f32[43,32,192]{2,1,0:T(8,128)S(1)}, f32[43,32,192]{2,1,0:T(8,128)S(1)}, u32[]{:S(2)}, u32[]{:S(2)}) collective-permute-start(f32[43,32,192]{2,1,0:T(8,128)S(1)} %pad_maximum_fusion.1), channel_id=1, source_target_pairs={{0,1},{2,3},{4,5},{6,7},{8,9},{10,11},{12,13},{14,15},{16,17},{18,... | collective-permute-start | bytes 3170312 | tf_op jit(solution)/shard_map/ppermute | solution.py:82
  26.6 29.7 %collective-permute-start.3 = (f32[43,32,192]{2,1,0:T(8,128)S(1)}, f32[43,32,192]{2,1,0:T(8,128)S(1)}, u32[]{:S(2)}, u32[]{:S(2)}) collective-permute-start(f32[43,32,192]{2,1,0:T(8,128)S(1)} %pad_maximum_fusion.1), channel_id=1, source_target_pairs={{1,0},{3,2},{5,4},{7,6},{9,8},{11,10},{13,12},{15,14},{17,16},{19,... | collective-permute-start | bytes 3170312 | tf_op jit(solution)/shard_map/ppermute | solution.py:83
  57.1 19.6 %collective-permute-start.4 = (f32[2,36,132]{2,1,0:T(8,128)}, f32[2,36,132]{2,1,0:T(8,128)}, u32[]{:S(2)}, u32[]{:S(2)}) collective-permute-start(f32[2,36,132]{2,1,0:T(8,128)} %get-tuple-element.39), channel_id=1, source_target_pairs={{8,0},{16,8},{24,16},{9,1},{17,9},{25,17},{10,2},{18,10},{26,18},{... | collective-permute-start | bytes 114056 | tf_op jit(solution)/shard_map/ppermute | solution.py:22
  59.5 17.2 %collective-permute-start.5 = (f32[2,36,132]{2,1,0:T(8,128)}, f32[2,36,132]{2,1,0:T(8,128)}, u32[]{:S(2)}, u32[]{:S(2)}) collective-permute-start(f32[2,36,132]{2,1,0:T(8,128)} %get-tuple-element.40), channel_id=1, source_target_pairs={{0,8},{8,16},{16,24},{1,9},{9,17},{17,25},{2,10},{10,18},{18,26},{... | collective-permute-start | bytes 114056 | tf_op jit(solution)/shard_map/ppermute | solution.py:19
  66.7 1.9 %copy-start.11 = (f32[43,96,192]{2,1,0:T(8,128)}, f32[43,96,192]{2,1,0:T(8,128)S(1)}, u32[]{:S(2)}) copy-start(f32[43,96,192]{2,1,0:T(8,128)S(1)} %pad_maximum_fusion) | copy-start | bytes 9510916
  68.9 2.8 %copy-start.6 = (f32[3,8,96,192]{3,2,0,1:T(8,128)}, f32[3,8,96,192]{3,2,0,1:T(8,128)S(1)}, u32[]{:S(2)}) copy-start(f32[3,8,96,192]{3,2,0,1:T(8,128)S(1)} %copy_multiply_fusion) | copy-start | bytes 5308420
  73.2 8.4 %collective-permute-start.6 = (f32[3,80,176]{2,1,0:T(8,128)}, f32[3,80,176]{2,1,0:T(8,128)}, u32[]{:S(2)}, u32[]{:S(2)}) collective-permute-start(f32[3,80,176]{2,1,0:T(8,128)} %fusion.57), channel_id=1, source_target_pairs={{0,8},{8,16},{16,24},{1,9},{9,17},{17,25},{2,10},{10,18},{18,26},{... | collective-permute-start | bytes 506888 | tf_op jit(solution)/shard_map/ppermute | solution.py:30
  75.2 6.4 %copy-start.2 = (f32[43,32,32]{2,1,0:T(8,128)S(1)}, f32[43,32,32]{2,1,0:T(8,128)}, u32[]{:S(2)}) copy-start(f32[43,32,32]{2,1,0:T(8,128)} %copy-done) | copy-start | bytes 528388
  75.2 6.4 %copy-start.5 = (f32[16,32,128]{2,1,0:T(8,128)S(1)}, f32[16,32,128]{2,1,0:T(8,128)}, u32[]{:S(2)}) copy-start(f32[16,32,128]{2,1,0:T(8,128)} %param.6) | copy-start | bytes 786436
  75.2 6.4 %copy-start.10 = (f32[3,8,32,128]{3,2,1,0:T(8,128)S(1)}, f32[3,8,32,128]{3,2,1,0:T(8,128)}, u32[]{:S(2)}) copy-start(f32[3,8,32,128]{3,2,1,0:T(8,128)} %copy-done.8) | copy-start | bytes 1179652
  75.2 6.4 %copy-start.17 = (f32[3,32,128]{2,1,0:T(8,128)S(1)}, f32[3,32,128]{2,1,0:T(8,128)}, u32[]{:S(2)}) copy-start(f32[3,32,128]{2,1,0:T(8,128)} %param.8) | copy-start | bytes 147460
  77.7 5.2 %copy-start.7 = (f32[3,8,96,192]{3,2,0,1:T(8,128)S(1)}, f32[3,8,96,192]{3,2,0,1:T(8,128)}, u32[]{:S(2)}) copy-start(f32[3,8,96,192]{3,2,0,1:T(8,128)} %copy-done.6) | copy-start | bytes 5308420
  85.8 7.6 %collective-permute-start.7 = (f32[3,64,160]{2,1,0:T(8,128)S(1)}, f32[3,64,160]{2,1,0:T(8,128)S(1)}, u32[]{:S(2)}, u32[]{:S(2)}) collective-permute-start(f32[3,64,160]{2,1,0:T(8,128)S(1)} %fusion.89), channel_id=1, source_target_pairs={{0,8},{8,16},{16,24},{1,9},{9,17},{17,25},{2,10},{10,18},{18,26},{... | collective-permute-start | bytes 368648 | tf_op jit(solution)/shard_map/ppermute | solution.py:30
  95.9 7.3 %collective-permute-start.8 = (f32[3,48,144]{2,1,0:T(8,128)S(1)}, f32[3,48,144]{2,1,0:T(8,128)S(1)}, u32[]{:S(2)}, u32[]{:S(2)}) collective-permute-start(f32[3,48,144]{2,1,0:T(8,128)S(1)} %fusion.121), channel_id=1, source_target_pairs={{0,8},{8,16},{16,24},{1,9},{9,17},{17,25},{2,10},{10,18},{18,26},{... | collective-permute-start | bytes 248840 | tf_op jit(solution)/shard_map/ppermute | solution.py:30
  104.8 1.5 %copy-start.13 = (f32[7,16,32,128]{3,2,1,0:T(8,128)S(1)}, f32[7,16,32,128]{3,2,1,0:T(8,128)}, u32[]{:S(2)}) copy-start(f32[7,16,32,128]{3,2,1,0:T(8,128)} %copy-done.12) | copy-start | bytes 5505028
  104.9 1.7 %copy-start.18 = (f32[3,8,2,32,128]{4,3,2,1,0:T(8,128)S(1)}, f32[3,8,2,32,128]{4,3,2,1,0:T(8,128)}, u32[]{:S(2)}) copy-start(f32[3,8,2,32,128]{4,3,2,1,0:T(8,128)} %fusion.164) | copy-start | bytes 2359300
  104.9 1.7 %copy-start.19 = (f32[16,32,128]{2,1,0:T(8,128)S(1)}, f32[16,32,128]{2,1,0:T(8,128)}, u32[]{:S(2)}) copy-start(f32[16,32,128]{2,1,0:T(8,128)} %get-tuple-element.42) | copy-start | bytes 786436
  104.9 1.8 %copy-start.20 = (f32[16,32,128]{2,1,0:T(8,128)S(1)}, f32[16,32,128]{2,1,0:T(8,128)}, u32[]{:S(2)}) copy-start(f32[16,32,128]{2,1,0:T(8,128)} %fusion.1) | copy-start | bytes 786436
  107.3 2.7 %collective-permute-start.9 = (f32[4,2,128]{2,1,0:T(2,128)S(1)}, f32[4,2,128]{2,1,0:T(2,128)S(1)}, u32[]{:S(2)}, u32[]{:S(2)}) collective-permute-start(f32[4,2,128]{2,1,0:T(2,128)S(1)} %bitcast.230), channel_id=1, source_target_pairs={{0,2},{2,0},{4,6},{6,4},{1,3},{3,1},{5,7},{7,5},{8,10},{10,8},{12,... | collective-permute-start | bytes 12296 | tf_op jit(solution)/shard_map/ppermute | solution.py:40
  110.0 8.6 %collective-permute-start.10 = (f32[4,1,128]{2,0,1:T(4,128)S(1)}, f32[4,1,128]{2,0,1:T(4,128)S(1)}, u32[]{:S(2)}, u32[]{:S(2)}) collective-permute-start(f32[4,1,128]{2,0,1:T(4,128)S(1)} %bitcast.231), channel_id=1, source_target_pairs={{0,4},{4,0},{2,6},{6,2},{1,5},{5,1},{3,7},{7,3},{8,12},{12,8},{10,... | collective-permute-start | bytes 6152 | tf_op jit(solution)/shard_map/ppermute | solution.py:40

commit v7 on v6

--- a/solution.py
+++ b/solution.py
@@ -135,6 +135,13 @@
     light_idx = lax.axis_index("light")
     view_idx = lax.axis_index("view")
     across_idx = lax.axis_index("across")
+    padded = padded_2(density, (("light", 0), ("view", 2), ("across", 1)), 2)
+    inside = (
+        rim_mask(light_idx, n_light, brick_l, 1)[:, None, None]
+        * rim_mask(across_idx, n_across, brick_a, 1)[None, :, None]
+        * rim_mask(view_idx, n_view, brick_v, 1)[None, None, :]
+    )
+    shading = shade_from(padded, inside)
     table_all = jnp.concatenate([opacity_table[None], extinction_table, albedo_table], axis=0)
     looked = jnp.broadcast_to(table_all[:, 0, None, None, None], (7,) + labels.shape)
     for material in range(1, table_all.shape[1]):
@@ -146,25 +153,10 @@
     running = jnp.cumsum(extinct_slabs, axis=2) - extinct_slabs
     slab_depth = jnp.sum(extinct_slabs, axis=2)
     widest = SLABS * n_light
-    stack = jnp.concatenate(
-        [density, slab_depth.reshape(3 * SLABS, brick_a, brick_v), sunlight], axis=0
-    )
-    stack_rim = halo(halo(stack, "view", 2, widest), "across", 1, widest)
-    rim_a = brick_a + 2 * widest
-    rim_v = brick_v + 2 * widest
-    depth_rim = stack_rim[brick_l : brick_l + 3 * SLABS].reshape(3, SLABS, rim_a, rim_v)
-    sun_rim = stack_rim[brick_l + 3 * SLABS :]
-    fade_rim = jnp.exp(-light_step * depth_rim) * plane_mask(widest, brick_a, brick_v)
-    density_side = stack_rim[
-        :brick_l, widest - 2 : widest + brick_a + 2, widest - 2 : widest + brick_v + 2
-    ]
-    padded = padded_2(density_side, (("light", 0),), 2)
-    inside = (
-        rim_mask(light_idx, n_light, brick_l, 1)[:, None, None]
-        * rim_mask(across_idx, n_across, brick_a, 1)[None, :, None]
-        * rim_mask(view_idx, n_view, brick_v, 1)[None, None, :]
-    )
-    shading = shade_from(padded, inside)
+    both = jnp.concatenate([slab_depth, sunlight[:, None]], axis=1)
+    both_rim = halo(halo(both, "across", 2, widest), "view", 3, widest)
+    sun_rim = both_rim[:, SLABS]
+    fade_rim = jnp.exp(-light_step * both_rim[:, :SLABS]) * plane_mask(widest, brick_a, brick_v)
     starts = None
     incoming = sun_rim
     for section_num in range(n_light):

time: 121 us -> 111 us (0.917)
  waiting for transfers between devices: 40.1 us -> 17 us
  starting transfers between devices: 30.2 us -> 42.5 us
  local copies, waits for them, and re-layouts: 14.7 us -> 16.8 us
    ppermute x2, waiting for transfers between devices: 20.6 us -> 0.01 us  [halo(): lows.insert(0, lax.ppermute(low, axis, forward))]
    ppermute x1 -> x3, starting transfers between devices: 4.28 us -> 11.7 us  [padded_2(): lax.ppermute(lax.slice_in_dim(block, block.shape[dim] - width, None, axis...]
    ppermute x2, starting transfers between devices: 6.19 us -> 12.8 us  [halo(): lows.insert(0, lax.ppermute(low, axis, forward))]
    ppermute x2, starting transfers between devices: 8.86 us -> 2.34 us  [from_partner(): return lax.ppermute(block, axis, route)]
    ppermute x2, waiting for transfers between devices: 5.48 us -> 0.01 us  [halo(): lax.ppermute(lax.slice_in_dim(block, 0, need, axis=dim), axis, backward)]
    mul x1 -> x2, other arithmetic: 0.24 us -> 5.23 us  [the longest x1 2.96 us: shards(): jnp.exp(-light_step * both_rim[:, :SLABS])]
    ppermute x1 -> x3, starting transfers between devices: 2.35 us -> 4.93 us  [padded_2(): lax.ppermute(lax.slice_in_dim(block, 0, width, axis=dim), axis, backward)]
    concatenate x2 -> x1, other arithmetic: 3.58 us -> 1.23 us  [halo(): block = jnp.concatenate(lows + [block] + highs, axis=dim)]
  transfers between devices with their start and end apart: 11 -> 15, of which waited for: 8 -> 7; matrix products, arithmetic and copies ran while one was open for 17% -> 20% of each run, Pallas kernels for 0% -> 0%
where the time goes in v7:
time: 111 us; the launch traced here: 110 us
  starting transfers between devices  42.5 us (38%)
  other arithmetic  32 us (29%)
  waiting for transfers between devices  17 us (15%)
  local copies, waits for them, and re-layouts  16.8 us (15%)
    ppermute x2, starting transfers between devices, halo(): lows.insert(0, lax.ppermute(low, axis, forward))  12.8 us
    ppermute x3, waiting for transfers between devices, from_behind(): lax.ppermute(value, axis, [(source, source + steps) for source in range(l...  12.1 us
    ppermute x3, starting transfers between devices, padded_2(): lax.ppermute(lax.slice_in_dim(block, block.shape[dim] - width, None, axis...  11.7 us
    mul x31, other arithmetic, propagate(): current = current * fade_here  10.7 us
    ppermute x3, starting transfers between devices, from_behind(): lax.ppermute(value, axis, [(source, source + steps) for source in range(l...  8.17 us
    ppermute x3, starting transfers between devices, padded_2(): lax.ppermute(lax.slice_in_dim(block, 0, width, axis=dim), axis, backward)  4.93 us
    slice x2, local copies, waits for them, and re-layouts, halo(): low = lax.slice_in_dim(block, size - need, None, axis=dim)  4.47 us
    mul x1, other arithmetic, shards(): jnp.exp(-light_step * both_rim[:, :SLABS])  2.96 us
  transfers between devices with their start and end apart: 15, of which 7 were waited for; matrix products, arithmetic and copies ran while one was open for 20% of the time, Pallas kernels for 0%

profile of v7, /device:TPU:16, one launch (start us, length us, event | category | flops | bytes accessed | tf_op | source)
XLA Modules:
  0.0 110.0 jit_solution(3644386006426635150)
XLA Ops:
  0.0 0.7 pad_maximum_fusion.18
  0.7 0.4 slice_reduce_fusion.15
  1.2 1.6 %broadcast_compare_fusion.14 = (pred[16,32,128]{2,1,0:T(8,128)(4,1)S(1)}, pred[16,32,128]{2,1,0:T(8,128)(4,1)S(1)}, pred[16,32,128]{2,1,0:T(8,128)(4,1)S(1)}, pr...) fusion(s32[16,32,128]{2,1,0:T(8,128)} %param.7), kind=kLoop, calls=%fused_computation.289 | loop fusion | flops 983040 | bytes 1245184 | tf_op jit(solution)/shard_map/eq | solution.py:149
  2.8 2.7 %select_select_fusion = f32[7,16,32,128]{3,2,1,0:T(8,128)S(1)} fusion(f32[7]{0:T(128)S(1)} %get-tuple-element.6, f32[7]{0:T(128)S(1)} %get-tuple-element.7, f32[7]{0:T(128)S(1)} %get-tuple-element.8, f32[7]{0:T(128)S(1)} %get-tuple-element.9, f32[7]{0:T(128)S(1)} %get-tuple-element.10, f32[7]{0:T(128)S(1)} %get-tuple-element.11, f32[7]{0:T(128)S(1)} %get-tuple-element.12, ...), kind=kLoop, calls=%fused_computation.8 | loop fusion | flops 6881280 | bytes 2818496 | tf_op jit(solution)/shard_map/jit(_where)/select_n | solution.py:148
  5.7 0.6 copy-done.11
  6.3 0.8 pad_maximum_fusion.13
  7.1 1.3 %collective-permute-start.7 = (f32[3,9,32,128]{3,2,1,0:T(8,128)}, f32[3,9,32,128]{3,2,1,0:T(8,128)}, u32[]{:S(2)}, u32[]{:S(2)}) collective-permute-start(f32[3,9,32,128]{3,2,1,0:T(8,128)} %pad_maximum_fusion.13), channel_id=1, source_target_pairs={{1,0},{3,2},{5,4},{7,6},{9,8},{11,10},{13,12},{15,14},{17,16},{19,... | collective-permute-start | bytes 1327112 | tf_op jit(solution)/shard_map/ppermute | solution.py:83
  8.4 6.1 %collective-permute-start.6 = (f32[3,9,32,128]{3,2,1,0:T(8,128)}, f32[3,9,32,128]{3,2,1,0:T(8,128)}, u32[]{:S(2)}, u32[]{:S(2)}) collective-permute-start(f32[3,9,32,128]{3,2,1,0:T(8,128)} %pad_maximum_fusion.13), channel_id=1, source_target_pairs={{0,1},{2,3},{4,5},{6,7},{8,9},{10,11},{12,13},{14,15},{16,17},{18,... | collective-permute-start | bytes 1327112 | tf_op jit(solution)/shard_map/ppermute | solution.py:82
  14.5 0.6 fusion.164
  15.1 3.5 %collective-permute-start = (f32[2,32,128]{2,1,0:T(8,128)S(1)}, f32[2,32,128]{2,1,0:T(8,128)S(1)}, u32[]{:S(2)}, u32[]{:S(2)}) collective-permute-start(f32[2,32,128]{2,1,0:T(8,128)S(1)} %get-tuple-element.51), channel_id=1, source_target_pairs={{0,8},{8,16},{16,24},{1,9},{9,17},{17,25},{2,10},{10,18},{18,26},{... | collective-permute-start | bytes 98312 | tf_op jit(solution)/shard_map/ppermute | solution.py:19
  18.6 2.4 %collective-permute-start.1 = (f32[2,32,128]{2,1,0:T(8,128)}, f32[2,32,128]{2,1,0:T(8,128)S(1)}, u32[]{:S(2)}, u32[]{:S(2)}) collective-permute-start(f32[2,32,128]{2,1,0:T(8,128)} %get-tuple-element.50), channel_id=1, source_target_pairs={{8,0},{16,8},{24,16},{9,1},{17,9},{25,17},{10,2},{18,10},{26,18},{... | collective-permute-start | bytes 98312 | tf_op jit(solution)/shard_map/ppermute | solution.py:22
  20.9 0.9 fusion.168
  21.9 1.0 fusion.3
  23.1 0.8 fusion.154
  23.8 0.8 collective-permute-done.1
  24.6 0.9 fusion.163
  25.5 1.3 %collective-permute-start.3 = (f32[20,32,2]{2,1,0:T(8,128)}, f32[20,32,2]{2,1,0:T(8,128)S(1)}, u32[]{:S(2)}, u32[]{:S(2)}) collective-permute-start(f32[20,32,2]{2,1,0:T(8,128)} %get-tuple-element.48), channel_id=1, source_target_pairs={{2,0},{4,2},{6,4},{3,1},{5,3},{7,5},{10,8},{12,10},{14,12},{11,9},... | collective-permute-start | bytes 15368 | tf_op jit(solution)/shard_map/ppermute | solution.py:22
  26.8 3.0 %collective-permute-start.2 = (f32[20,32,2]{2,1,0:T(8,128)}, f32[20,32,2]{2,1,0:T(8,128)S(1)}, u32[]{:S(2)}, u32[]{:S(2)}) collective-permute-start(f32[20,32,2]{2,1,0:T(8,128)} %get-tuple-element.47), channel_id=1, source_target_pairs={{0,2},{2,4},{4,6},{1,3},{3,5},{5,7},{8,10},{10,12},{12,14},{9,11},... | collective-permute-start | bytes 15368 | tf_op jit(solution)/shard_map/ppermute | solution.py:19
  29.9 1.4 %collective-permute-done.2 = f32[20,32,2]{2,1,0:T(8,128)S(1)} collective-permute-done((f32[20,32,2]{2,1,0:T(8,128)}, f32[20,32,2]{2,1,0:T(8,128)S(1)}, u32[]{:S(2)}, u32[]{:S(2)}) %collective-permute-start.2) | collective-permute-done | bytes 5152 | tf_op jit(solution)/shard_map/ppermute | solution.py:19
  31.5 1.3 %collective-permute-start.5 = (f32[20,2,132]{2,1,0:T(2,128)S(1)}, f32[20,2,132]{2,1,0:T(2,128)S(1)}, u32[]{:S(2)}, u32[]{:S(2)}) collective-permute-start(f32[20,2,132]{2,1,0:T(2,128)S(1)} %get-tuple-element.46), channel_id=1, source_target_pairs={{1,0},{3,2},{5,4},{7,6},{9,8},{11,10},{13,12},{15,14},{17,16},{19,... | collective-permute-start | bytes 63368 | tf_op jit(solution)/shard_map/ppermute | solution.py:22
  32.8 5.2 %collective-permute-start.4 = (f32[20,2,132]{2,1,0:T(2,128)S(1)}, f32[20,2,132]{2,1,0:T(2,128)}, u32[]{:S(2)}, u32[]{:S(2)}) collective-permute-start(f32[20,2,132]{2,1,0:T(2,128)S(1)} %get-tuple-element.45), channel_id=1, source_target_pairs={{0,1},{2,3},{4,5},{6,7},{8,9},{10,11},{12,13},{14,15},{16,17},{18,... | collective-permute-start | bytes 63368 | tf_op jit(solution)/shard_map/ppermute | solution.py:19
  38.0 1.2 %pad_maximum_fusion.5 = f32[3,9,96,128]{3,2,1,0:T(8,128)S(1)} fusion(f32[3,9,32,128]{3,2,1,0:T(8,128)} %collective-permute-done.7, f32[3,1,32,128]{3,2,1,0:T(8,128)S(1)} %bitcast.281, f32[3,8,32,128]{3,2,1,0:T(8,128)S(1)} %reduce_sum.27, f32[3,9,32,128]{3,2,1,0:T(8,128)} %collective-permute-done.6), kind=kLoop, calls=%fused_computation.9 | loop fusion | flops 995328 | bytes 2654208 | tf_op jit(solution)/shard_map/concatenate | solution.py:84
  39.2 2.0 %fusion.162 = (f32[3,9,96,32]{3,2,1,0:T(8,128)}, f32[3,9,96,32]{3,2,1,0:T(8,128)}) fusion(f32[3,9,96,128]{3,2,1,0:T(8,128)S(1)} %pad_maximum_fusion.5), kind=kLoop, calls=%fused_computation.392 | loop fusion | bytes 1327104 | tf_op jit(solution)/shard_map/slice | solution.py:81
  41.2 2.5 %copy.49 = f32[3,9,96,32]{2,3,1,0:T(8,128)} copy(f32[3,9,96,32]{3,2,1,0:T(8,128)} %get-tuple-element.44) | data formatting | bytes 663552 | tf_op jit(solution)/shard_map/slice | solution.py:83
  43.7 1.3 %collective-permute-start.9 = (f32[3,9,96,32]{2,3,1,0:T(8,128)}, f32[3,9,96,32]{2,3,1,0:T(8,128)}, u32[]{:S(2)}, u32[]{:S(2)}) collective-permute-start(f32[3,9,96,32]{2,3,1,0:T(8,128)} %copy.49), channel_id=1, source_target_pairs={{2,0},{4,2},{6,4},{3,1},{5,3},{7,5},{10,8},{12,10},{14,12},{11,9},... | collective-permute-start | bytes 995336 | tf_op jit(solution)/shard_map/ppermute | solution.py:83
  45.0 2.5 %copy.48 = f32[3,9,96,32]{2,3,1,0:T(8,128)} copy(f32[3,9,96,32]{3,2,1,0:T(8,128)} %get-tuple-element.43) | data formatting | bytes 663552 | tf_op jit(solution)/shard_map/slice | solution.py:81
  47.5 6.7 %collective-permute-start.8 = (f32[3,9,96,32]{2,3,1,0:T(8,128)}, f32[3,9,96,32]{2,3,1,0:T(8,128)}, u32[]{:S(2)}, u32[]{:S(2)}) collective-permute-start(f32[3,9,96,32]{2,3,1,0:T(8,128)} %copy.48), channel_id=1, source_target_pairs={{0,2},{2,4},{4,6},{1,3},{3,5},{5,7},{8,10},{10,12},{12,14},{9,11},... | collective-permute-start | bytes 995336 | tf_op jit(solution)/shard_map/ppermute | solution.py:82
  54.3 0.6 copy-done.12
  54.9 1.5 %pad_maximum_fusion.6 = f32[20,36,132]{2,1,0:T(8,128)S(1)} fusion(f32[20,2,132]{2,1,0:T(2,128)} %copy-done.12, f32[20,32,2]{2,1,0:T(8,128)} %copy-done.2, f32[20,32,128]{2,1,0:T(8,128)S(1)} %constant_dynamic-update-slice_fusion, f32[20,32,2]{2,1,0:T(8,128)} %copy-done.4, f32[20,2,132]{2,1,0:T(2,128)} %collective-permute-done.4), kind=kLoop, calls=%fused_computation.14 | loop fusion | flops 380160 | bytes 760320 | tf_op jit(solution)/shard_map/concatenate | solution.py:23
  56.4 2.5 %copy.51 = f32[3,9,96,32]{3,2,1,0:T(8,128)} copy(f32[3,9,96,32]{2,3,1,0:T(8,128)} %collective-permute-done.9) | data formatting | bytes 663552 | tf_op jit(solution)/shard_map/ppermute | solution.py:83
  58.9 2.5 %copy.50 = f32[3,9,96,32]{3,2,1,0:T(8,128)} copy(f32[3,9,96,32]{2,3,1,0:T(8,128)} %collective-permute-done.8) | data formatting | bytes 663552 | tf_op jit(solution)/shard_map/ppermute | solution.py:82
  61.5 3.0 %fusion.2 = f32[3,8,96,192]{3,2,1,0:T(8,128)S(1)} fusion(f32[3,9,96,32]{3,2,1,0:T(8,128)} %copy.51, f32[3,9,96,32]{3,2,1,0:T(8,128)} %copy.50, f32[3,9,32,128]{3,2,1,0:T(8,128)} %collective-permute-done.7, f32[3,9,32,128]{3,2,1,0:T(8,128)} %collective-permute-done.6, f32[3,1,32,128]{3,2,1,0:T(8,128)S(1)} %bitcast.282, f32[3,8,32,128]{3,2,1,0:T(8,128)S(1)} %reduce_sum.27, ...), kind=kLoop, calls=%fused_computation.3 | loop fusion | flops 3096576 | bytes 3833856 | tf_op jit(solution)/shard_map/mul | solution.py:159
  64.5 1.0 fusion.20
  65.5 0.4 fusion.16
  65.9 0.4 fusion.12
  66.4 0.4 fusion.8
  66.8 0.4 fusion.33
  67.3 0.4 fusion.29
  67.7 0.4 fusion.25
  68.1 0.4 fusion.21
  68.6 0.3 fusion.59
  68.9 2.7 %collective-permute-start.10 = (f32[3,80,176]{2,1,0:T(8,128)S(1)}, f32[3,80,176]{2,1,0:T(8,128)S(1)}, u32[]{:S(2)}, u32[]{:S(2)}) collective-permute-start(f32[3,80,176]{2,1,0:T(8,128)S(1)} %fusion.59), channel_id=1, source_target_pairs={{0,8},{8,16},{16,24},{1,9},{9,17},{17,25},{2,10},{10,18},{18,26},{... | collective-permute-start | bytes 506888 | tf_op jit(solution)/shard_map/ppermute | solution.py:30
  71.6 2.3 %multiply_multiply_fusion = f32[18,34,130]{2,1,0:T(8,128)S(1)} fusion(f32[130]{0:T(256)S(1)} %and_convert_fusion.2, f32[18,34]{1,0:T(8,128)S(1)} %broadcast_multiply_fusion.1, f32[20,36,132]{2,1,0:T(8,128)S(1)} %pad_maximum_fusion.6, f32[20,32,2]{2,1,0:T(8,128)S(1)} %copy-done.3, f32[20,32,128]{2,1,0:T(8,128)S(1)} %constant_dynamic-update-slice_fusion, ...), kind=kLoop, calls=%fused_computation.12 | loop fusion | flops 1511640 | bytes 1974328 | tf_op jit(solution)/shard_map/mul | solution.py:62
  73.9 3.6 %collective-permute-done.10 = f32[3,80,176]{2,1,0:T(8,128)S(1)} collective-permute-done((f32[3,80,176]{2,1,0:T(8,128)S(1)}, f32[3,80,176]{2,1,0:T(8,128)S(1)}, u32[]{:S(2)}, u32[]{:S(2)}) %collective-permute-start.10) | collective-permute-done | bytes 168992 | tf_op jit(solution)/shard_map/ppermute | solution.py:30
  77.8 0.4 fusion.52
  78.1 0.4 fusion.48
  78.5 0.4 fusion.44
  78.9 0.4 fusion.72
  79.3 0.4 fusion.68
  79.6 0.4 fusion.64
  80.0 0.4 fusion.60
  80.6 2.7 %collective-permute-start.11 = (f32[3,64,160]{2,1,0:T(8,128)S(1)}, f32[3,64,160]{2,1,0:T(8,128)S(1)}, u32[]{:S(2)}, u32[]{:S(2)}) collective-permute-start(f32[3,64,160]{2,1,0:T(8,128)S(1)} %fusion.91), channel_id=1, source_target_pairs={{0,8},{8,16},{16,24},{1,9},{9,17},{17,25},{2,10},{10,18},{18,26},{... | collective-permute-start | bytes 368648 | tf_op jit(solution)/shard_map/ppermute | solution.py:30
  83.4 2.3 %multiply_multiply_fusion.1 = f32[18,34,130]{2,1,0:T(8,128)S(1)} fusion(f32[130]{0:T(256)S(1)} %and_convert_fusion.2, f32[18,34]{1,0:T(8,128)S(1)} %broadcast_multiply_fusion.1, f32[20,36,132]{2,1,0:T(8,128)S(1)} %pad_maximum_fusion.6, f32[20,32,2]{2,1,0:T(8,128)S(1)} %copy-done.3, f32[20,32,128]{2,1,0:T(8,128)S(1)} %constant_dynamic-update-slice_fusion, ...), kind=kLoop, calls=%fused_computation.13 | loop fusion | flops 1352520 | bytes 1974328 | tf_op jit(solution)/shard_map/mul | solution.py:61
  85.6 3.8 %collective-permute-done.11 = f32[3,64,160]{2,1,0:T(8,128)S(1)} collective-permute-done((f32[3,64,160]{2,1,0:T(8,128)S(1)}, f32[3,64,160]{2,1,0:T(8,128)S(1)}, u32[]{:S(2)}, u32[]{:S(2)}) %collective-permute-start.11) | collective-permute-done | bytes 122912 | tf_op jit(solution)/shard_map/ppermute | solution.py:30
  89.9 0.3 fusion.80
  90.2 0.3 fusion.76
  92.0 2.7 %collective-permute-start.12 = (f32[3,48,144]{2,1,0:T(8,128)S(1)}, f32[3,48,144]{2,1,0:T(8,128)S(1)}, u32[]{:S(2)}, u32[]{:S(2)}) collective-permute-start(f32[3,48,144]{2,1,0:T(8,128)S(1)} %fusion.123), channel_id=1, source_target_pairs={{0,8},{8,16},{16,24},{1,9},{9,17},{17,25},{2,10},{10,18},{18,26},{... | collective-permute-start | bytes 248840 | tf_op jit(solution)/shard_map/ppermute | solution.py:30
  94.7 0.9 fusion.40
  95.6 4.7 %collective-permute-done.12 = f32[3,48,144]{2,1,0:T(8,128)S(1)} collective-permute-done((f32[3,48,144]{2,1,0:T(8,128)S(1)}, f32[3,48,144]{2,1,0:T(8,128)S(1)}, u32[]{:S(2)}, u32[]{:S(2)}) %collective-permute-start.12) | collective-permute-done | bytes 82976 | tf_op jit(solution)/shard_map/ppermute | solution.py:30
  103.4 0.5 fusion.6
  104.1 1.1 %collective-permute-done.13 = f32[4,2,128]{2,1,0:T(2,128)S(1)} collective-permute-done((f32[4,2,128]{2,1,0:T(2,128)S(1)}, f32[4,2,128]{2,1,0:T(2,128)S(1)}, u32[]{:S(2)}, u32[]{:S(2)}) %collective-permute-start.13) | collective-permute-done | bytes 4128 | tf_op jit(solution)/shard_map/ppermute | solution.py:40
  105.3 2.3 %collective-permute-start.14 = (f32[4,1,128]{2,0,1:T(4,128)S(1)}, f32[4,1,128]{2,0,1:T(4,128)S(1)}, u32[]{:S(2)}, u32[]{:S(2)}) collective-permute-start(f32[4,1,128]{2,0,1:T(4,128)S(1)} %bitcast.290), channel_id=1, source_target_pairs={{0,4},{4,0},{2,6},{6,2},{1,5},{5,1},{3,7},{7,3},{8,12},{12,8},{10,... | collective-permute-start | bytes 6152 | tf_op jit(solution)/shard_map/ppermute | solution.py:40
  107.6 1.6 %collective-permute-done.14 = f32[4,1,128]{2,0,1:T(4,128)S(1)} collective-permute-done((f32[4,1,128]{2,0,1:T(4,128)S(1)}, f32[4,1,128]{2,0,1:T(4,128)S(1)}, u32[]{:S(2)}, u32[]{:S(2)}) %collective-permute-start.14) | collective-permute-done | bytes 2080 | tf_op jit(solution)/shard_map/ppermute | solution.py:40
  109.3 0.6 pad_maximum_fusion.17
  (93 shorter events, 6.4 us)
Async XLA Ops:
  1.1 4.3 %copy-start.6 = (f32[16,32,128]{2,1,0:T(8,128)S(1)}, f32[16,32,128]{2,1,0:T(8,128)}, u32[]{:S(2)}) copy-start(f32[16,32,128]{2,1,0:T(8,128)} %param.6) | copy-start | bytes 786436
  5.5 0.8 copy-start.11
  7.1 30.8 %collective-permute-start.7 = (f32[3,9,32,128]{3,2,1,0:T(8,128)}, f32[3,9,32,128]{3,2,1,0:T(8,128)}, u32[]{:S(2)}, u32[]{:S(2)}) collective-permute-start(f32[3,9,32,128]{3,2,1,0:T(8,128)} %pad_maximum_fusion.13), channel_id=1, source_target_pairs={{1,0},{3,2},{5,4},{7,6},{9,8},{11,10},{13,12},{15,14},{17,16},{19,... | collective-permute-start | bytes 1327112 | tf_op jit(solution)/shard_map/ppermute | solution.py:83
  8.4 29.6 %collective-permute-start.6 = (f32[3,9,32,128]{3,2,1,0:T(8,128)}, f32[3,9,32,128]{3,2,1,0:T(8,128)}, u32[]{:S(2)}, u32[]{:S(2)}) collective-permute-start(f32[3,9,32,128]{3,2,1,0:T(8,128)} %pad_maximum_fusion.13), channel_id=1, source_target_pairs={{0,1},{2,3},{4,5},{6,7},{8,9},{10,11},{12,13},{14,15},{16,17},{18,... | collective-permute-start | bytes 1327112 | tf_op jit(solution)/shard_map/ppermute | solution.py:82
  15.1 8.0 %collective-permute-start = (f32[2,32,128]{2,1,0:T(8,128)S(1)}, f32[2,32,128]{2,1,0:T(8,128)S(1)}, u32[]{:S(2)}, u32[]{:S(2)}) collective-permute-start(f32[2,32,128]{2,1,0:T(8,128)S(1)} %get-tuple-element.51), channel_id=1, source_target_pairs={{0,8},{8,16},{16,24},{1,9},{9,17},{17,25},{2,10},{10,18},{18,26},{... | collective-permute-start | bytes 98312 | tf_op jit(solution)/shard_map/ppermute | solution.py:19
  18.6 6.0 %collective-permute-start.1 = (f32[2,32,128]{2,1,0:T(8,128)}, f32[2,32,128]{2,1,0:T(8,128)S(1)}, u32[]{:S(2)}, u32[]{:S(2)}) collective-permute-start(f32[2,32,128]{2,1,0:T(8,128)} %get-tuple-element.50), channel_id=1, source_target_pairs={{8,0},{16,8},{24,16},{9,1},{17,9},{25,17},{10,2},{18,10},{26,18},{... | collective-permute-start | bytes 98312 | tf_op jit(solution)/shard_map/ppermute | solution.py:22
  25.5 4.4 %collective-permute-start.3 = (f32[20,32,2]{2,1,0:T(8,128)}, f32[20,32,2]{2,1,0:T(8,128)S(1)}, u32[]{:S(2)}, u32[]{:S(2)}) collective-permute-start(f32[20,32,2]{2,1,0:T(8,128)} %get-tuple-element.48), channel_id=1, source_target_pairs={{2,0},{4,2},{6,4},{3,1},{5,3},{7,5},{10,8},{12,10},{14,12},{11,9},... | collective-permute-start | bytes 15368 | tf_op jit(solution)/shard_map/ppermute | solution.py:22
  26.8 4.5 %collective-permute-start.2 = (f32[20,32,2]{2,1,0:T(8,128)}, f32[20,32,2]{2,1,0:T(8,128)S(1)}, u32[]{:S(2)}, u32[]{:S(2)}) collective-permute-start(f32[20,32,2]{2,1,0:T(8,128)} %get-tuple-element.47), channel_id=1, source_target_pairs={{0,2},{2,4},{4,6},{1,3},{3,5},{5,7},{8,10},{10,12},{12,14},{9,11},... | collective-permute-start | bytes 15368 | tf_op jit(solution)/shard_map/ppermute | solution.py:19
  29.9 9.3 %copy-start.2 = (f32[20,32,2]{2,1,0:T(8,128)}, f32[20,32,2]{2,1,0:T(8,128)S(1)}, u32[]{:S(2)}) copy-start(f32[20,32,2]{2,1,0:T(8,128)S(1)} %collective-permute-done.3) | copy-start | bytes 15364
  31.3 7.9 %copy-start.4 = (f32[20,32,2]{2,1,0:T(8,128)}, f32[20,32,2]{2,1,0:T(8,128)S(1)}, u32[]{:S(2)}) copy-start(f32[20,32,2]{2,1,0:T(8,128)S(1)} %collective-permute-done.2) | copy-start | bytes 15364
  31.5 22.8 %collective-permute-start.5 = (f32[20,2,132]{2,1,0:T(2,128)S(1)}, f32[20,2,132]{2,1,0:T(2,128)S(1)}, u32[]{:S(2)}, u32[]{:S(2)}) collective-permute-start(f32[20,2,132]{2,1,0:T(2,128)S(1)} %get-tuple-element.46), channel_id=1, source_target_pairs={{1,0},{3,2},{5,4},{7,6},{9,8},{11,10},{13,12},{15,14},{17,16},{19,... | collective-permute-start | bytes 63368 | tf_op jit(solution)/shard_map/ppermute | solution.py:22
  32.8 22.1 %collective-permute-start.4 = (f32[20,2,132]{2,1,0:T(2,128)S(1)}, f32[20,2,132]{2,1,0:T(2,128)}, u32[]{:S(2)}, u32[]{:S(2)}) collective-permute-start(f32[20,2,132]{2,1,0:T(2,128)S(1)} %get-tuple-element.45), channel_id=1, source_target_pairs={{0,1},{2,3},{4,5},{6,7},{8,9},{10,11},{12,13},{14,15},{16,17},{18,... | collective-permute-start | bytes 63368 | tf_op jit(solution)/shard_map/ppermute | solution.py:19
  43.7 12.7 %collective-permute-start.9 = (f32[3,9,96,32]{2,3,1,0:T(8,128)}, f32[3,9,96,32]{2,3,1,0:T(8,128)}, u32[]{:S(2)}, u32[]{:S(2)}) collective-permute-start(f32[3,9,96,32]{2,3,1,0:T(8,128)} %copy.49), channel_id=1, source_target_pairs={{2,0},{4,2},{6,4},{3,1},{5,3},{7,5},{10,8},{12,10},{14,12},{11,9},... | collective-permute-start | bytes 995336 | tf_op jit(solution)/shard_map/ppermute | solution.py:83
  47.5 11.5 %collective-permute-start.8 = (f32[3,9,96,32]{2,3,1,0:T(8,128)}, f32[3,9,96,32]{2,3,1,0:T(8,128)}, u32[]{:S(2)}, u32[]{:S(2)}) collective-permute-start(f32[3,9,96,32]{2,3,1,0:T(8,128)} %copy.48), channel_id=1, source_target_pairs={{0,2},{2,4},{4,6},{1,3},{3,5},{5,7},{8,10},{10,12},{12,14},{9,11},... | collective-permute-start | bytes 995336 | tf_op jit(solution)/shard_map/ppermute | solution.py:82
  54.3 0.6 copy-start.12
  61.5 3.0 %copy-start = (f32[3,9,96,32]{3,2,1,0:T(8,128)S(1)}, f32[3,9,96,32]{3,2,1,0:T(8,128)}, u32[]{:S(2)}) copy-start(f32[3,9,96,32]{3,2,1,0:T(8,128)} %copy.51) | copy-start | bytes 995332
  61.5 3.0 %copy-start.1 = (f32[3,9,96,32]{3,2,1,0:T(8,128)S(1)}, f32[3,9,96,32]{3,2,1,0:T(8,128)}, u32[]{:S(2)}) copy-start(f32[3,9,96,32]{3,2,1,0:T(8,128)} %copy.50) | copy-start | bytes 995332
  68.1 3.5 %copy-start.3 = (f32[20,32,2]{2,1,0:T(8,128)S(1)}, f32[20,32,2]{2,1,0:T(8,128)}, u32[]{:S(2)}) copy-start(f32[20,32,2]{2,1,0:T(8,128)} %copy-done.2) | copy-start | bytes 15364
  68.1 3.5 %copy-start.5 = (f32[20,32,2]{2,1,0:T(8,128)S(1)}, f32[20,32,2]{2,1,0:T(8,128)}, u32[]{:S(2)}) copy-start(f32[20,32,2]{2,1,0:T(8,128)} %copy-done.4) | copy-start | bytes 15364
  68.1 3.5 %copy-start.13 = (f32[20,2,132]{2,1,0:T(2,128)S(1)}, f32[20,2,132]{2,1,0:T(2,128)}, u32[]{:S(2)}) copy-start(f32[20,2,132]{2,1,0:T(2,128)} %copy-done.12) | copy-start | bytes 63364
  68.9 8.7 %collective-permute-start.10 = (f32[3,80,176]{2,1,0:T(8,128)S(1)}, f32[3,80,176]{2,1,0:T(8,128)S(1)}, u32[]{:S(2)}, u32[]{:S(2)}) collective-permute-start(f32[3,80,176]{2,1,0:T(8,128)S(1)} %fusion.59), channel_id=1, source_target_pairs={{0,8},{8,16},{16,24},{1,9},{9,17},{17,25},{2,10},{10,18},{18,26},{... | collective-permute-start | bytes 506888 | tf_op jit(solution)/shard_map/ppermute | solution.py:30
  80.6 8.8 %collective-permute-start.11 = (f32[3,64,160]{2,1,0:T(8,128)S(1)}, f32[3,64,160]{2,1,0:T(8,128)S(1)}, u32[]{:S(2)}, u32[]{:S(2)}) collective-permute-start(f32[3,64,160]{2,1,0:T(8,128)S(1)} %fusion.91), channel_id=1, source_target_pairs={{0,8},{8,16},{16,24},{1,9},{9,17},{17,25},{2,10},{10,18},{18,26},{... | collective-permute-start | bytes 368648 | tf_op jit(solution)/shard_map/ppermute | solution.py:30
  92.0 8.4 %collective-permute-start.12 = (f32[3,48,144]{2,1,0:T(8,128)S(1)}, f32[3,48,144]{2,1,0:T(8,128)S(1)}, u32[]{:S(2)}, u32[]{:S(2)}) collective-permute-start(f32[3,48,144]{2,1,0:T(8,128)S(1)} %fusion.123), channel_id=1, source_target_pairs={{0,8},{8,16},{16,24},{1,9},{9,17},{17,25},{2,10},{10,18},{18,26},{... | collective-permute-start | bytes 248840 | tf_op jit(solution)/shard_map/ppermute | solution.py:30
  102.1 1.0 copy-start.7
  102.1 1.2 %copy-start.8 = (f32[3,8,2,32,128]{4,3,2,1,0:T(8,128)S(1)}, f32[3,8,2,32,128]{4,3,2,1,0:T(8,128)}, u32[]{:S(2)}) copy-start(f32[3,8,2,32,128]{4,3,2,1,0:T(8,128)} %fusion.168) | copy-start | bytes 2359300
  102.1 1.3 %copy-start.9 = (f32[16,32,128]{2,1,0:T(8,128)S(1)}, f32[16,32,128]{2,1,0:T(8,128)}, u32[]{:S(2)}) copy-start(f32[16,32,128]{2,1,0:T(8,128)} %fusion.3) | copy-start | bytes 786436
  102.1 1.3 %copy-start.10 = (f32[16,32,128]{2,1,0:T(8,128)S(1)}, f32[16,32,128]{2,1,0:T(8,128)}, u32[]{:S(2)}) copy-start(f32[16,32,128]{2,1,0:T(8,128)} %get-tuple-element.42) | copy-start | bytes 786436
  104.0 1.2 %collective-permute-start.13 = (f32[4,2,128]{2,1,0:T(2,128)S(1)}, f32[4,2,128]{2,1,0:T(2,128)S(1)}, u32[]{:S(2)}, u32[]{:S(2)}) collective-permute-start(f32[4,2,128]{2,1,0:T(2,128)S(1)} %bitcast.289), channel_id=1, source_target_pairs={{0,2},{2,0},{4,6},{6,4},{1,3},{3,1},{5,7},{7,5},{8,10},{10,8},{12,... | collective-permute-start | bytes 12296 | tf_op jit(solution)/shard_map/ppermute | solution.py:40
  105.3 3.8 %collective-permute-start.14 = (f32[4,1,128]{2,0,1:T(4,128)S(1)}, f32[4,1,128]{2,0,1:T(4,128)S(1)}, u32[]{:S(2)}, u32[]{:S(2)}) collective-permute-start(f32[4,1,128]{2,0,1:T(4,128)S(1)} %bitcast.290), channel_id=1, source_target_pairs={{0,4},{4,0},{2,6},{6,2},{1,5},{5,1},{3,7},{7,3},{8,12},{12,8},{10,... | collective-permute-start | bytes 6152 | tf_op jit(solution)/shard_map/ppermute | solution.py:40

commit v8 on v7

--- a/solution.py
+++ b/solution.py
@@ -135,28 +135,41 @@
     light_idx = lax.axis_index("light")
     view_idx = lax.axis_index("view")
     across_idx = lax.axis_index("across")
-    padded = padded_2(density, (("light", 0), ("view", 2), ("across", 1)), 2)
+    widest = SLABS * n_light
+    stack = jnp.concatenate([density, labels.astype(jnp.float32), sunlight], axis=0)
+    stack_rim = halo(halo(stack, "across", 1, widest), "view", 2, widest)
+    density_rim = stack_rim[:brick_l]
+    labels_rim = stack_rim[brick_l : 2 * brick_l]
+    sun_rim = stack_rim[2 * brick_l :]
+    density_side = density_rim[
+        :, widest - 2 : widest + brick_a + 2, widest - 2 : widest + brick_v + 2
+    ]
+    padded = padded_2(density_side, (("light", 0),), 2)
     inside = (
         rim_mask(light_idx, n_light, brick_l, 1)[:, None, None]
         * rim_mask(across_idx, n_across, brick_a, 1)[None, :, None]
         * rim_mask(view_idx, n_view, brick_v, 1)[None, None, :]
     )
     shading = shade_from(padded, inside)
-    table_all = jnp.concatenate([opacity_table[None], extinction_table, albedo_table], axis=0)
-    looked = jnp.broadcast_to(table_all[:, 0, None, None, None], (7,) + labels.shape)
+    table_all = jnp.concatenate([opacity_table[None], albedo_table], axis=0)
+    looked = jnp.broadcast_to(table_all[:, 0, None, None, None], (4,) + labels.shape)
     for material in range(1, table_all.shape[1]):
         looked = jnp.where(
             (labels == material)[None], table_all[:, material, None, None, None], looked
         )
-    extinct = looked[1:4] * density[None]
+    extinct_rim = jnp.broadcast_to(extinction_table[:, 0, None, None, None], (3,) + labels_rim.shape)
+    for material in range(1, extinction_table.shape[1]):
+        extinct_rim = jnp.where(
+            (labels_rim == material)[None], extinction_table[:, material, None, None, None], extinct_rim
+        )
+    extinct_rim = extinct_rim * density_rim[None]
+    rim_a = brick_a + 2 * widest
+    rim_v = brick_v + 2 * widest
+    slab_depth = jnp.sum(extinct_rim.reshape(3, SLABS, layer_rows, rim_a, rim_v), axis=2)
+    extinct = extinct_rim[:, :, widest : widest + brick_a, widest : widest + brick_v]
     extinct_slabs = extinct.reshape(3, SLABS, layer_rows, brick_a, brick_v)
     running = jnp.cumsum(extinct_slabs, axis=2) - extinct_slabs
-    slab_depth = jnp.sum(extinct_slabs, axis=2)
-    widest = SLABS * n_light
-    both = jnp.concatenate([slab_depth, sunlight[:, None]], axis=1)
-    both_rim = halo(halo(both, "across", 2, widest), "view", 3, widest)
-    sun_rim = both_rim[:, SLABS]
-    fade_rim = jnp.exp(-light_step * both_rim[:, :SLABS]) * plane_mask(widest, brick_a, brick_v)
+    fade_rim = jnp.exp(-light_step * slab_depth) * plane_mask(widest, brick_a, brick_v)
     starts = None
     incoming = sun_rim
     for section_num in range(n_light):
@@ -173,7 +186,7 @@
         3, brick_l, brick_a, brick_v
     )
     optical = looked[0] * density * view_step
-    colour = (1.0 - jnp.exp(-optical))[None] * looked[4:7] * (shading[None] * lighting + AMBIENT)
+    colour = (1.0 - jnp.exp(-optical))[None] * looked[1:4] * (shading[None] * lighting + AMBIENT)
     upper = (jnp.arange(brick_v)[:, None] < jnp.arange(brick_v)[None, :]).astype(jnp.float32)
     before = jnp.dot(optical.reshape(-1, brick_v), upper, precision=lax.Precision.HIGHEST).reshape(
         brick_l, brick_a, brick_v

time: 111 us -> 120 us (1.081); the launches traced: 110 us -> 118 us
  other arithmetic: 32 us -> 51.8 us
  starting transfers between devices: 42.5 us -> 32.4 us
  local copies, waits for them, and re-layouts: 16.8 us -> 14.2 us
    reduce_sum x1, other arithmetic: 0.06 us -> 9.07 us  [shards(): jnp.sum(extinct_rim.reshape(3, SLABS, layer_rows, rim_a, rim_v), axis=2)]
    ppermute x3 -> x1, starting transfers between devices: 11.7 us -> 4.28 us  [padded_2(): lax.ppermute(lax.slice_in_dim(block, block.shape[dim] - width, None, axis...]
    ppermute x2, starting transfers between devices: 2.34 us -> 9.25 us  [from_partner(): return lax.ppermute(block, axis, route)]
    ppermute x2, starting transfers between devices: 12.8 us -> 7.68 us  [halo(): lows.insert(0, lax.ppermute(low, axis, forward))]
    select_n x0 -> x1, other arithmetic: none -> 4.19 us  [shards(): jnp.where((labels_rim == material)[None], extinction_table[:, material, N...]
    eq x0 -> x1, other arithmetic: none -> 3.69 us  [shards(): labels_rim == material]
    ppermute x2, waiting for transfers between devices: 0.01 us -> 2.66 us  [halo(): lax.ppermute(lax.slice_in_dim(block, 0, need, axis=dim), axis, backward)]
    ppermute x3, waiting for transfers between devices: 12.1 us -> 9.52 us  [from_behind(): lax.ppermute(value, axis, [(source, source + steps) for source in range(l...]
  transfers between devices with their start and end apart: 15 -> 11, of which waited for: 7 -> 7; matrix products, arithmetic and copies ran while one was open for 20% -> 32% of each run, Pallas kernels for 0% -> 0%
where the time goes in v8:
time: 120 us; the launch traced here: 118 us
  other arithmetic  51.8 us (43%)
  starting transfers between devices  32.4 us (27%)
  waiting for transfers between devices  15.8 us (13%)
  local copies, waits for them, and re-layouts  14.2 us (12%)
  matrix products  1.94 us (2%)
  between operations  1.37 us (1%)
    mul x31, other arithmetic, propagate(): current = current * fade_here  10 us
    ppermute x3, waiting for transfers between devices, from_behind(): lax.ppermute(value, axis, [(source, source + steps) for source in range(l...  9.52 us
    ppermute x2, starting transfers between devices, from_partner(): return lax.ppermute(block, axis, route)  9.25 us
    reduce_sum x1, other arithmetic, shards(): jnp.sum(extinct_rim.reshape(3, SLABS, layer_rows, rim_a, rim_v), axis=2)  9.07 us
    ppermute x2, starting transfers between devices, halo(): lows.insert(0, lax.ppermute(low, axis, forward))  7.68 us
    ppermute x3, starting transfers between devices, from_behind(): lax.ppermute(value, axis, [(source, source + steps) for source in range(l...  6.11 us
    ppermute x1, starting transfers between devices, padded_2(): lax.ppermute(lax.slice_in_dim(block, block.shape[dim] - width, None, axis...  4.28 us
    select_n x1, other arithmetic, shards(): jnp.where((labels_rim == material)[None], extinction_table[:, material, N...  4.19 us
  transfers between devices with their start and end apart: 11, of which 7 were waited for; matrix products, arithmetic and copies ran while one was open for 32% of the time, Pallas kernels for 0%

profile of v8, /device:TPU:16, one launch (start us, length us, event | category | flops | bytes accessed | tf_op | source)
XLA Modules:
  0.0 117.5 jit_solution(10352848308737480330)
XLA Ops:
  0.0 1.0 convert_element_type.39
  1.0 1.1 pad_maximum_fusion.5
  2.2 1.4 %collective-permute-start.1 = (f32[35,32,128]{2,1,0:T(8,128)S(1)}, f32[35,32,128]{2,1,0:T(8,128)S(1)}, u32[]{:S(2)}, u32[]{:S(2)}) collective-permute-start(f32[35,32,128]{2,1,0:T(8,128)S(1)} %pad_maximum_fusion.5), channel_id=1, source_target_pairs={{1,0},{3,2},{5,4},{7,6},{9,8},{11,10},{13,12},{15,14},{17,16},{19,... | collective-permute-start | bytes 1720328 | tf_op jit(solution)/shard_map/ppermute | solution.py:83
  3.6 4.6 %collective-permute-start = (f32[35,32,128]{2,1,0:T(8,128)S(1)}, f32[35,32,128]{2,1,0:T(8,128)S(1)}, u32[]{:S(2)}, u32[]{:S(2)}) collective-permute-start(f32[35,32,128]{2,1,0:T(8,128)S(1)} %pad_maximum_fusion.5), channel_id=1, source_target_pairs={{0,1},{2,3},{4,5},{6,7},{8,9},{10,11},{12,13},{14,15},{16,17},{18,... | collective-permute-start | bytes 1720328 | tf_op jit(solution)/shard_map/ppermute | solution.py:82
  8.2 1.6 %broadcast_compare_fusion.29 = (pred[16,32,128]{2,1,0:T(8,128)(4,1)S(1)}, pred[16,32,128]{2,1,0:T(8,128)(4,1)S(1)}, pred[16,32,128]{2,1,0:T(8,128)(4,1)S(1)}, pr...) fusion(s32[16,32,128]{2,1,0:T(8,128)} %param.7), kind=kLoop, calls=%fused_computation.300 | loop fusion | flops 983040 | bytes 1245184 | tf_op jit(solution)/shard_map/eq | solution.py:158
  9.9 0.4 slice_reduce_fusion.31
  10.3 1.2 %select_select_fusion.1 = f32[4,16,32,128]{3,2,1,0:T(8,128)S(1)} fusion(f32[4]{0:T(128)S(1)} %get-tuple-element.22, f32[4]{0:T(128)S(1)} %get-tuple-element.23, f32[4]{0:T(128)S(1)} %get-tuple-element.24, f32[4]{0:T(128)S(1)} %get-tuple-element.25, f32[4]{0:T(128)S(1)} %get-tuple-element.26, f32[4]{0:T(128)S(1)} %get-tuple-element.27, ...), kind=kLoop, calls=%fused_computation.9 | loop fusion | flops 3932160 | bytes 2031872 | tf_op jit(solution)/shard_map/jit(_where)/select_n | solution.py:157
  11.6 1.0 copy-done.13
  12.5 0.8 fusion.156
  13.3 0.7 exp.32
  14.0 0.6 and_convert_fusion.2
  14.6 0.9 slice_reduce_fusion.15
  15.5 0.7 broadcast_multiply_fusion
  16.2 2.7 %collective-permute-done.1 = f32[35,32,128]{2,1,0:T(8,128)S(1)} collective-permute-done((f32[35,32,128]{2,1,0:T(8,128)S(1)}, f32[35,32,128]{2,1,0:T(8,128)S(1)}, u32[]{:S(2)}, u32[]{:S(2)}) %collective-permute-start.1) | collective-permute-done | bytes 573472 | tf_op jit(solution)/shard_map/ppermute | solution.py:83
  18.9 1.2 %collective-permute-done = f32[35,32,128]{2,1,0:T(8,128)S(1)} collective-permute-done((f32[35,32,128]{2,1,0:T(8,128)S(1)}, f32[35,32,128]{2,1,0:T(8,128)S(1)}, u32[]{:S(2)}, u32[]{:S(2)}) %collective-permute-start) | collective-permute-done | bytes 573472 | tf_op jit(solution)/shard_map/ppermute | solution.py:82
  20.2 1.8 %fusion.164 = (f32[35,96,32]{2,1,0:T(8,128)}, f32[35,96,32]{2,1,0:T(8,128)S(1)}) fusion(f32[35,96,128]{2,1,0:T(8,128)S(1)} %pad_maximum_fusion.1), kind=kLoop, calls=%fused_computation.415 | loop fusion | bytes 1720320 | tf_op jit(solution)/shard_map/slice | solution.py:81
  22.1 1.9 %copy.97 = f32[35,96,32]{1,2,0:T(8,128)S(1)} copy(f32[35,96,32]{2,1,0:T(8,128)} %get-tuple-element.72) | data formatting | bytes 860160 | tf_op jit(solution)/shard_map/slice | solution.py:81
  24.0 1.4 %copy.98 = f32[35,96,32]{1,2,0:T(8,128)} copy(f32[35,96,32]{2,1,0:T(8,128)S(1)} %get-tuple-element.73) | data formatting | bytes 860160 | tf_op jit(solution)/shard_map/slice | solution.py:83
  25.4 1.3 %collective-permute-start.3 = (f32[35,96,32]{1,2,0:T(8,128)}, f32[35,96,32]{1,2,0:T(8,128)}, u32[]{:S(2)}, u32[]{:S(2)}) collective-permute-start(f32[35,96,32]{1,2,0:T(8,128)} %copy.98), channel_id=1, source_target_pairs={{2,0},{4,2},{6,4},{3,1},{5,3},{7,5},{10,8},{12,10},{14,12},{11,9},... | collective-permute-start | bytes 1290248 | tf_op jit(solution)/shard_map/ppermute | solution.py:83
  26.7 3.1 %collective-permute-start.2 = (f32[35,96,32]{1,2,0:T(8,128)S(1)}, f32[35,96,32]{1,2,0:T(8,128)S(1)}, u32[]{:S(2)}, u32[]{:S(2)}) collective-permute-start(f32[35,96,32]{1,2,0:T(8,128)S(1)} %copy.97), channel_id=1, source_target_pairs={{0,2},{2,4},{4,6},{1,3},{3,5},{5,7},{8,10},{10,12},{12,14},{9,11},... | collective-permute-start | bytes 1290248 | tf_op jit(solution)/shard_map/ppermute | solution.py:82
  29.8 0.7 broadcast_multiply_fusion.1
  30.4 1.9 %fusion = f32[16,32,128]{2,1,0:T(8,128)} fusion(f32[16,32,128]{2,1,0:T(8,128)S(1)} %copy-done.5, f32[4,16,32,128]{3,2,1,0:T(8,128)} %copy-done.13), kind=kOutput, calls=%fused_computation.6 | convolution fusion | flops 100876288 | bytes 786432 | tf_op jit(solution)/shard_map/dot_general | solution.py:191
  32.4 0.5 copy.99
  32.9 1.6 %copy.100 = f32[35,96,32]{2,1,0:T(8,128)S(1)} copy(f32[35,96,32]{1,2,0:T(8,128)} %collective-permute-done.3) | data formatting | bytes 860160 | tf_op jit(solution)/shard_map/ppermute | solution.py:83
  34.5 2.8 %pad_maximum_fusion = f32[35,96,192]{2,1,0:T(8,128)S(1)} fusion(f32[35,96,32]{2,1,0:T(8,128)S(1)} %copy.100, f32[35,32,128]{2,1,0:T(8,128)} %copy-done, f32[3,32,128]{2,1,0:T(8,128)S(1)} %copy-done.23, f32[16,32,128]{2,1,0:T(8,128)} %copy-done.8, f32[16,32,128]{2,1,0:T(8,128)} %param.6, f32[35,32,128]{2,1,0:T(8,128)} %copy-done.2, f32[35,96,32]{2,1,0:T(8,128)S(1)} %copy.99), kind=kLoop, calls=%fused_computation.2 | loop fusion | flops 3870720 | bytes 5160960 | tf_op jit(solution)/shard_map/concatenate | solution.py:84
  37.3 1.0 slice.1345
  38.3 3.7 %broadcast_compare_fusion.14 = (pred[16,96,192]{2,1,0:T(8,128)(4,1)S(1)}, pred[16,96,192]{2,1,0:T(8,128)(4,1)S(1)}, pred[16,96,192]{2,1,0:T(8,128)(4,1)S(1)}, pr...) fusion(f32[35,96,192]{2,1,0:T(8,128)S(1)} %pad_maximum_fusion), kind=kLoop, calls=%fused_computation.35 | loop fusion | flops 4423680 | bytes 5603328 | tf_op jit(solution)/shard_map/eq | solution.py:163
  42.3 1.2 pad_maximum_fusion.7
  43.5 2.3 %collective-permute-start.4 = (f32[2,36,132]{2,1,0:T(8,128)}, f32[2,36,132]{2,1,0:T(8,128)}, u32[]{:S(2)}, u32[]{:S(2)}) collective-permute-start(f32[2,36,132]{2,1,0:T(8,128)} %get-tuple-element.55), channel_id=1, source_target_pairs={{8,0},{16,8},{24,16},{9,1},{17,9},{25,17},{10,2},{18,10},{26,18},{... | collective-permute-start | bytes 114056 | tf_op jit(solution)/shard_map/ppermute | solution.py:22
  45.8 4.3 %collective-permute-start.5 = (f32[2,36,132]{2,1,0:T(8,128)}, f32[2,36,132]{2,1,0:T(8,128)}, u32[]{:S(2)}, u32[]{:S(2)}) collective-permute-start(f32[2,36,132]{2,1,0:T(8,128)} %get-tuple-element.56), channel_id=1, source_target_pairs={{0,8},{8,16},{16,24},{1,9},{9,17},{17,25},{2,10},{10,18},{18,26},{... | collective-permute-start | bytes 114056 | tf_op jit(solution)/shard_map/ppermute | solution.py:19
  50.7 0.8 slice.1339
  51.7 4.2 %select_select_fusion = f32[3,16,96,192]{3,2,1,0:T(8,128)} fusion(f32[3]{0:T(128)S(1)} %copy-done.60, f32[3]{0:T(128)S(1)} %copy-done.61, f32[3]{0:T(128)S(1)} %copy-done.51, f32[3]{0:T(128)S(1)} %copy-done.52, f32[3]{0:T(128)S(1)} %copy-done.53, f32[3]{0:T(128)S(1)} %copy-done.54, f32[3]{0:T(128)S(1)} %copy-done.55, f32[3]{0:T(128)S(1)} %copy-done.56, ...), kind=kLoop, calls=%fused_computation | loop fusion | flops 8847360 | bytes 6488196 | tf_op jit(solution)/shard_map/jit(_where)/select_n | solution.py:162
  56.0 9.1 %multiply_reduce_fusion = f32[3,8,96,192]{3,2,1,0:T(8,128)} fusion(f32[8,2,96,192]{3,2,1,0:T(8,128)S(1)} %bitcast.302, f32[3]{0:T(128)} %get-tuple-element.19, f32[3]{0:T(128)} %get-tuple-element.20, f32[3]{0:T(128)S(1)} %copy-done.51, f32[3]{0:T(128)S(1)} %copy-done.52, f32[3]{0:T(128)S(1)} %copy-done.53, f32[3]{0:T(128)S(1)} %copy-done.54, ...), kind=kLoop, calls=%fused_computation.1 | loop fusion | flops 14598144 | bytes 7372992 | tf_op jit(solution)/shard_map/reduce_sum | solution.py:168
  65.0 2.1 %exponential_multiply_fusion = f32[3,8,96,192]{3,2,1,0:T(8,128)S(1)} fusion(f32[3,8,96,192]{3,2,1,0:T(8,128)} %multiply_reduce_fusion, f32[96,192]{1,0:T(8,128)} %broadcast_multiply_fusion), kind=kLoop, calls=%fused_computation.3 | loop fusion | flops 884736 | bytes 3612672 | tf_op jit(solution)/shard_map/mul | solution.py:172
  67.4 0.4 fusion.18
  67.9 0.4 fusion.14
  68.3 0.4 fusion.10
  68.8 0.4 fusion.35
  69.2 0.4 fusion.31
  69.6 0.4 fusion.27
  70.1 0.4 fusion.23
  70.8 2.3 %collective-permute-start.6 = (f32[3,80,176]{2,1,0:T(8,128)S(1)}, f32[3,80,176]{2,1,0:T(8,128)S(1)}, u32[]{:S(2)}, u32[]{:S(2)}) collective-permute-start(f32[3,80,176]{2,1,0:T(8,128)S(1)} %fusion.61), channel_id=1, source_target_pairs={{0,8},{8,16},{16,24},{1,9},{9,17},{17,25},{2,10},{10,18},{18,26},{... | collective-permute-start | bytes 506888 | tf_op jit(solution)/shard_map/ppermute | solution.py:30
  73.1 1.8 %fusion.5 = f32[3,16,32,128]{3,2,1,0:T(8,128)S(1)} fusion(f32[3,16,96,192]{3,2,1,0:T(8,128)} %select_select_fusion, f32[16,32,128]{2,1,0:T(8,128)S(1)} %copy-done.24, f32[3]{0:T(128)S(1)} %copy-done.42, f32[3]{0:T(128)S(1)} %copy-done.49, f32[3]{0:T(128)S(1)} %copy-done.47, f32[3]{0:T(128)S(1)} %copy-done.45, f32[3]{0:T(128)S(1)} %copy-done.43, ...), kind=kLoop, calls=%fused_computation.16 | loop fusion | flops 1179648 | bytes 2162748 | tf_op jit(solution)/shard_map/mul | solution.py:165
  74.9 1.4 %fusion.168 = f32[3,8,2,32,128]{4,3,2,1,0:T(8,128)S(1)} fusion(f32[3,8,2,32,128]{4,3,2,1,0:T(8,128)S(1)} %bitcast.313), kind=kOutput, calls=%fused_computation.419 | output fusion | flops 196608 | bytes 1572864 | tf_op jit(solution)/shard_map/jit(cumsum)/reduce_window_sum | solution.py:171
  76.6 1.0 pad_maximum_fusion.2
  77.6 1.5 %collective-permute-done.6 = f32[3,80,176]{2,1,0:T(8,128)S(1)} collective-permute-done((f32[3,80,176]{2,1,0:T(8,128)S(1)}, f32[3,80,176]{2,1,0:T(8,128)S(1)}, u32[]{:S(2)}, u32[]{:S(2)}) %collective-permute-start.6) | collective-permute-done | bytes 168992 | tf_op jit(solution)/shard_map/ppermute | solution.py:30
  79.3 0.4 fusion.54
  79.7 0.4 fusion.50
  80.1 0.4 fusion.46
  80.5 0.4 fusion.74
  80.8 0.4 fusion.70
  81.2 0.4 fusion.66
  82.2 1.9 %collective-permute-start.7 = (f32[3,64,160]{2,1,0:T(8,128)S(1)}, f32[3,64,160]{2,1,0:T(8,128)S(1)}, u32[]{:S(2)}, u32[]{:S(2)}) collective-permute-start(f32[3,64,160]{2,1,0:T(8,128)S(1)} %fusion.93), channel_id=1, source_target_pairs={{0,8},{8,16},{16,24},{1,9},{9,17},{17,25},{2,10},{10,18},{18,26},{... | collective-permute-start | bytes 368648 | tf_op jit(solution)/shard_map/ppermute | solution.py:30
  84.2 2.1 %multiply_multiply_fusion.1 = (f32[18,34,130]{2,1,0:T(8,128)S(1)}, f32[18,34,130]{2,1,0:T(8,128)S(1)}) fusion(f32[16,36,132]{2,1,0:T(8,128)S(1)} %slice.1120, f32[2,36,132]{2,1,0:T(8,128)} %collective-permute-done.5, f32[2,36,132]{2,1,0:T(8,128)} %collective-permute-done.4, f32[130]{0:T(256)S(1)} %copy-done.63, f32[18,34]{1,0:T(8,128)S(1)} %copy-done.40, ...), kind=kLoop, calls=%fused_computation.8 | loop fusion | flops 1750320 | bytes 2292568 | tf_op jit(solution)/shard_map/mul | solution.py:61
  86.2 3.5 %collective-permute-done.7 = f32[3,64,160]{2,1,0:T(8,128)S(1)} collective-permute-done((f32[3,64,160]{2,1,0:T(8,128)S(1)}, f32[3,64,160]{2,1,0:T(8,128)S(1)}, u32[]{:S(2)}, u32[]{:S(2)}) %collective-permute-start.7) | collective-permute-done | bytes 122912 | tf_op jit(solution)/shard_map/ppermute | solution.py:30
  92.4 1.9 %collective-permute-start.8 = (f32[3,48,144]{2,1,0:T(8,128)S(1)}, f32[3,48,144]{2,1,0:T(8,128)S(1)}, u32[]{:S(2)}, u32[]{:S(2)}) collective-permute-start(f32[3,48,144]{2,1,0:T(8,128)S(1)} %fusion.125), channel_id=1, source_target_pairs={{0,8},{8,16},{16,24},{1,9},{9,17},{17,25},{2,10},{10,18},{18,26},{... | collective-permute-start | bytes 248840 | tf_op jit(solution)/shard_map/ppermute | solution.py:30
  94.3 0.9 fusion.42
  95.2 4.5 %collective-permute-done.8 = f32[3,48,144]{2,1,0:T(8,128)S(1)} collective-permute-done((f32[3,48,144]{2,1,0:T(8,128)S(1)}, f32[3,48,144]{2,1,0:T(8,128)S(1)}, u32[]{:S(2)}, u32[]{:S(2)}) %collective-permute-start.8) | collective-permute-done | bytes 82976 | tf_op jit(solution)/shard_map/ppermute | solution.py:30
  102.6 2.2 %fusion.8 = f32[3,16,32]{2,1,0:T(8,128)S(1)} fusion(f32[4,16,32,128]{3,2,1,0:T(8,128)S(1)} %copy-done.14, f32[3,16,32,128]{3,2,1,0:T(8,128)S(1)} %bitcast.315, f32[3,16,32,128]{3,2,1,0:T(8,128)S(1)} %bitcast.314, f32[16,32,128]{2,1,0:T(8,128)S(1)} %copy-done.31, f32[16,32,128]{2,1,0:T(8,128)S(1)} %fusion.42, f32[16,32,128]{2,1,0:T(8,128)S(1)} %copy-done.30, ...), kind=kLoop, calls=%fused_computation.20 | loop fusion | flops 2947584 | bytes 4528188 | tf_op jit(solution)/shard_map/reduce_sum | solution.py:194
  105.0 1.2 %collective-permute-start.9 = (f32[4,2,128]{2,1,0:T(2,128)S(1)}, f32[4,2,128]{2,1,0:T(2,128)S(1)}, u32[]{:S(2)}, u32[]{:S(2)}) collective-permute-start(f32[4,2,128]{2,1,0:T(2,128)S(1)} %bitcast.326), channel_id=1, source_target_pairs={{0,2},{2,0},{4,6},{6,4},{1,3},{3,1},{5,7},{7,5},{8,10},{10,8},{12,... | collective-permute-start | bytes 12296 | tf_op jit(solution)/shard_map/ppermute | solution.py:40
  106.2 0.8 collective-permute-done.9
  107.1 8.1 %collective-permute-start.10 = (f32[4,1,128]{2,0,1:T(4,128)S(1)}, f32[4,1,128]{2,0,1:T(4,128)S(1)}, u32[]{:S(2)}, u32[]{:S(2)}) collective-permute-start(f32[4,1,128]{2,0,1:T(4,128)S(1)} %bitcast.327), channel_id=1, source_target_pairs={{0,4},{4,0},{2,6},{6,2},{1,5},{5,1},{3,7},{7,3},{8,12},{12,8},{10,... | collective-permute-start | bytes 6152 | tf_op jit(solution)/shard_map/ppermute | solution.py:40
  115.1 1.6 %collective-permute-done.10 = f32[4,1,128]{2,0,1:T(4,128)S(1)} collective-permute-done((f32[4,1,128]{2,0,1:T(4,128)S(1)}, f32[4,1,128]{2,0,1:T(4,128)S(1)}, u32[]{:S(2)}, u32[]{:S(2)}) %collective-permute-start.10) | collective-permute-done | bytes 2080 | tf_op jit(solution)/shard_map/ppermute | solution.py:40
  116.9 0.6 pad_maximum_fusion.8
  (195 shorter events, 8.2 us)
Async XLA Ops:
  0.0 9.9 %copy-start.62 = (f32[3,16]{1,0:T(4,128)S(1)}, f32[3,16]{1,0:T(4,128)}, u32[]{:S(2)}) copy-start(f32[3,16]{1,0:T(4,128)} %param.11) | copy-start | bytes 580
  0.0 9.9 %copy-start.64 = (f32[16]{0:T(128)S(1)}, f32[16]{0:T(128)}, u32[]{:S(2)}) copy-start(f32[16]{0:T(128)} %param.9) | copy-start | bytes 196
  1.0 19.1 %copy-start.8 = (f32[16,32,128]{2,1,0:T(8,128)}, f32[16,32,128]{2,1,0:T(8,128)S(1)}, u32[]{:S(2)}) copy-start(f32[16,32,128]{2,1,0:T(8,128)S(1)} %convert_element_type.39) | copy-start | bytes 786436
  1.0 11.5 %copy-start.5 = (f32[16,32,128]{2,1,0:T(8,128)S(1)}, f32[16,32,128]{2,1,0:T(8,128)}, u32[]{:S(2)}) copy-start(f32[16,32,128]{2,1,0:T(8,128)} %param.6) | copy-start | bytes 786436
  2.1 12.4 %copy-start.39 = (f32[3,16]{1,0:T(4,128)S(1)}, f32[3,16]{1,0:T(4,128)}, u32[]{:S(2)}) copy-start(f32[3,16]{1,0:T(4,128)} %param.10) | copy-start | bytes 580
  2.2 18.0 %copy-start.23 = (f32[3,32,128]{2,1,0:T(8,128)S(1)}, f32[3,32,128]{2,1,0:T(8,128)}, u32[]{:S(2)}) copy-start(f32[3,32,128]{2,1,0:T(8,128)} %param.8) | copy-start | bytes 147460
  2.2 16.7 %collective-permute-start.1 = (f32[35,32,128]{2,1,0:T(8,128)S(1)}, f32[35,32,128]{2,1,0:T(8,128)S(1)}, u32[]{:S(2)}, u32[]{:S(2)}) collective-permute-start(f32[35,32,128]{2,1,0:T(8,128)S(1)} %pad_maximum_fusion.5), channel_id=1, source_target_pairs={{1,0},{3,2},{5,4},{7,6},{9,8},{11,10},{13,12},{15,14},{17,16},{19,... | collective-permute-start | bytes 1720328 | tf_op jit(solution)/shard_map/ppermute | solution.py:83
  3.6 16.5 %collective-permute-start = (f32[35,32,128]{2,1,0:T(8,128)S(1)}, f32[35,32,128]{2,1,0:T(8,128)S(1)}, u32[]{:S(2)}, u32[]{:S(2)}) collective-permute-start(f32[35,32,128]{2,1,0:T(8,128)S(1)} %pad_maximum_fusion.5), channel_id=1, source_target_pairs={{0,1},{2,3},{4,5},{6,7},{8,9},{10,11},{12,13},{14,15},{16,17},{18,... | collective-permute-start | bytes 1720328 | tf_op jit(solution)/shard_map/ppermute | solution.py:82
  18.9 3.1 %copy-start = (f32[35,32,128]{2,1,0:T(8,128)}, f32[35,32,128]{2,1,0:T(8,128)S(1)}, u32[]{:S(2)}) copy-start(f32[35,32,128]{2,1,0:T(8,128)S(1)} %collective-permute-done.1) | copy-start | bytes 1720324
  25.4 7.5 %collective-permute-start.3 = (f32[35,96,32]{1,2,0:T(8,128)}, f32[35,96,32]{1,2,0:T(8,128)}, u32[]{:S(2)}, u32[]{:S(2)}) collective-permute-start(f32[35,96,32]{1,2,0:T(8,128)} %copy.98), channel_id=1, source_target_pairs={{2,0},{4,2},{6,4},{3,1},{5,3},{7,5},{10,8},{12,10},{14,12},{11,9},... | collective-permute-start | bytes 1290248 | tf_op jit(solution)/shard_map/ppermute | solution.py:83
  26.7 5.7 %collective-permute-start.2 = (f32[35,96,32]{1,2,0:T(8,128)S(1)}, f32[35,96,32]{1,2,0:T(8,128)S(1)}, u32[]{:S(2)}, u32[]{:S(2)}) collective-permute-start(f32[35,96,32]{1,2,0:T(8,128)S(1)} %copy.97), channel_id=1, source_target_pairs={{0,2},{2,4},{4,6},{1,3},{3,5},{5,7},{8,10},{10,12},{12,14},{9,11},... | collective-permute-start | bytes 1290248 | tf_op jit(solution)/shard_map/ppermute | solution.py:82
  37.3 4.7 %copy-start.11 = (f32[35,96,192]{2,1,0:T(8,128)}, f32[35,96,192]{2,1,0:T(8,128)S(1)}, u32[]{:S(2)}) copy-start(f32[35,96,192]{2,1,0:T(8,128)S(1)} %pad_maximum_fusion) | copy-start | bytes 7741444
  38.3 3.7 %copy-start.1 = (f32[35,32,128]{2,1,0:T(8,128)S(1)}, f32[35,32,128]{2,1,0:T(8,128)}, u32[]{:S(2)}) copy-start(f32[35,32,128]{2,1,0:T(8,128)} %copy-done) | copy-start | bytes 1720324
  38.3 3.7 %copy-start.3 = (f32[35,32,128]{2,1,0:T(8,128)S(1)}, f32[35,32,128]{2,1,0:T(8,128)}, u32[]{:S(2)}) copy-start(f32[35,32,128]{2,1,0:T(8,128)} %copy-done.2) | copy-start | bytes 1720324
  38.3 3.7 %copy-start.6 = (f32[16,32,128]{2,1,0:T(8,128)S(1)}, f32[16,32,128]{2,1,0:T(8,128)}, u32[]{:S(2)}) copy-start(f32[16,32,128]{2,1,0:T(8,128)} %param.6) | copy-start | bytes 786436
  38.3 3.7 %copy-start.9 = (f32[16,32,128]{2,1,0:T(8,128)S(1)}, f32[16,32,128]{2,1,0:T(8,128)}, u32[]{:S(2)}) copy-start(f32[16,32,128]{2,1,0:T(8,128)} %copy-done.8) | copy-start | bytes 786436
  42.1 8.1 %copy-start.25 = (pred[16,96,192]{2,1,0:T(8,128)(4,1)}, pred[16,96,192]{2,1,0:T(8,128)(4,1)S(1)}, u32[]{:S(2)}) copy-start(pred[16,96,192]{2,1,0:T(8,128)(4,1)S(1)} %get-tuple-element.57) | copy-start | bytes 884740
  42.1 8.2 %copy-start.26 = (pred[16,96,192]{2,1,0:T(8,128)(4,1)}, pred[16,96,192]{2,1,0:T(8,128)(4,1)S(1)}, u32[]{:S(2)}) copy-start(pred[16,96,192]{2,1,0:T(8,128)(4,1)S(1)} %get-tuple-element.58) | copy-start | bytes 884740
  42.1 8.3 %copy-start.27 = (pred[16,96,192]{2,1,0:T(8,128)(4,1)}, pred[16,96,192]{2,1,0:T(8,128)(4,1)S(1)}, u32[]{:S(2)}) copy-start(pred[16,96,192]{2,1,0:T(8,128)(4,1)S(1)} %get-tuple-element.59) | copy-start | bytes 884740
  42.1 8.5 %copy-start.28 = (pred[16,96,192]{2,1,0:T(8,128)(4,1)}, pred[16,96,192]{2,1,0:T(8,128)(4,1)S(1)}, u32[]{:S(2)}) copy-start(pred[16,96,192]{2,1,0:T(8,128)(4,1)S(1)} %get-tuple-element.60) | copy-start | bytes 884740
  42.1 8.6 %copy-start.29 = (pred[16,96,192]{2,1,0:T(8,128)(4,1)}, pred[16,96,192]{2,1,0:T(8,128)(4,1)S(1)}, u32[]{:S(2)}) copy-start(pred[16,96,192]{2,1,0:T(8,128)(4,1)S(1)} %get-tuple-element.61) | copy-start | bytes 884740
  42.1 9.4 %copy-start.15 = (pred[16,96,192]{2,1,0:T(8,128)(4,1)}, pred[16,96,192]{2,1,0:T(8,128)(4,1)S(1)}, u32[]{:S(2)}) copy-start(pred[16,96,192]{2,1,0:T(8,128)(4,1)S(1)} %get-tuple-element.64) | copy-start | bytes 884740
  42.1 9.4 %copy-start.16 = (pred[16,96,192]{2,1,0:T(8,128)(4,1)}, pred[16,96,192]{2,1,0:T(8,128)(4,1)S(1)}, u32[]{:S(2)}) copy-start(pred[16,96,192]{2,1,0:T(8,128)(4,1)S(1)} %get-tuple-element.65) | copy-start | bytes 884740
  42.1 9.4 %copy-start.17 = (pred[16,96,192]{2,1,0:T(8,128)(4,1)}, pred[16,96,192]{2,1,0:T(8,128)(4,1)S(1)}, u32[]{:S(2)}) copy-start(pred[16,96,192]{2,1,0:T(8,128)(4,1)S(1)} %get-tuple-element.66) | copy-start | bytes 884740
  42.1 9.4 %copy-start.18 = (pred[16,96,192]{2,1,0:T(8,128)(4,1)}, pred[16,96,192]{2,1,0:T(8,128)(4,1)S(1)}, u32[]{:S(2)}) copy-start(pred[16,96,192]{2,1,0:T(8,128)(4,1)S(1)} %get-tuple-element.67) | copy-start | bytes 884740
  42.1 9.4 %copy-start.19 = (pred[16,96,192]{2,1,0:T(8,128)(4,1)}, pred[16,96,192]{2,1,0:T(8,128)(4,1)S(1)}, u32[]{:S(2)}) copy-start(pred[16,96,192]{2,1,0:T(8,128)(4,1)S(1)} %get-tuple-element.68) | copy-start | bytes 884740
  42.2 9.4 %copy-start.20 = (pred[16,96,192]{2,1,0:T(8,128)(4,1)}, pred[16,96,192]{2,1,0:T(8,128)(4,1)S(1)}, u32[]{:S(2)}) copy-start(pred[16,96,192]{2,1,0:T(8,128)(4,1)S(1)} %get-tuple-element.69) | copy-start | bytes 884740
  42.2 9.4 %copy-start.21 = (pred[16,96,192]{2,1,0:T(8,128)(4,1)}, pred[16,96,192]{2,1,0:T(8,128)(4,1)S(1)}, u32[]{:S(2)}) copy-start(pred[16,96,192]{2,1,0:T(8,128)(4,1)S(1)} %get-tuple-element.70) | copy-start | bytes 884740
  42.2 9.4 %copy-start.22 = (pred[16,96,192]{2,1,0:T(8,128)(4,1)}, pred[16,96,192]{2,1,0:T(8,128)(4,1)S(1)}, u32[]{:S(2)}) copy-start(pred[16,96,192]{2,1,0:T(8,128)(4,1)S(1)} %get-tuple-element.71) | copy-start | bytes 884740
  42.2 9.4 %copy-start.51 = (f32[3]{0:T(128)S(1)}, f32[3]{0:T(128)}, u32[]{:S(2)}) copy-start(f32[3]{0:T(128)} %get-tuple-element.6) | copy-start | bytes 40
  42.2 9.4 %copy-start.52 = (f32[3]{0:T(128)S(1)}, f32[3]{0:T(128)}, u32[]{:S(2)}) copy-start(f32[3]{0:T(128)} %get-tuple-element.7) | copy-start | bytes 40
  42.2 9.4 %copy-start.53 = (f32[3]{0:T(128)S(1)}, f32[3]{0:T(128)}, u32[]{:S(2)}) copy-start(f32[3]{0:T(128)} %get-tuple-element.8) | copy-start | bytes 40
  42.2 9.4 %copy-start.54 = (f32[3]{0:T(128)S(1)}, f32[3]{0:T(128)}, u32[]{:S(2)}) copy-start(f32[3]{0:T(128)} %get-tuple-element.9) | copy-start | bytes 40
  42.2 9.4 %copy-start.55 = (f32[3]{0:T(128)S(1)}, f32[3]{0:T(128)}, u32[]{:S(2)}) copy-start(f32[3]{0:T(128)} %get-tuple-element.10) | copy-start | bytes 40
  42.2 9.4 %copy-start.56 = (f32[3]{0:T(128)S(1)}, f32[3]{0:T(128)}, u32[]{:S(2)}) copy-start(f32[3]{0:T(128)} %get-tuple-element.11) | copy-start | bytes 40
  42.2 9.4 %copy-start.57 = (f32[3]{0:T(128)S(1)}, f32[3]{0:T(128)}, u32[]{:S(2)}) copy-start(f32[3]{0:T(128)} %get-tuple-element.12) | copy-start | bytes 40
  42.3 9.4 %copy-start.58 = (f32[3]{0:T(128)S(1)}, f32[3]{0:T(128)}, u32[]{:S(2)}) copy-start(f32[3]{0:T(128)} %get-tuple-element.13) | copy-start | bytes 40
  42.3 9.4 %copy-start.59 = (f32[3]{0:T(128)S(1)}, f32[3]{0:T(128)}, u32[]{:S(2)}) copy-start(f32[3]{0:T(128)} %get-tuple-element.14) | copy-start | bytes 40
  42.3 9.4 %copy-start.60 = (f32[3]{0:T(128)S(1)}, f32[3]{0:T(128)}, u32[]{:S(2)}) copy-start(f32[3]{0:T(128)} %get-tuple-element.19) | copy-start | bytes 40
  42.3 9.4 %copy-start.61 = (f32[3]{0:T(128)S(1)}, f32[3]{0:T(128)}, u32[]{:S(2)}) copy-start(f32[3]{0:T(128)} %get-tuple-element.20) | copy-start | bytes 40
  43.5 33.1 %collective-permute-start.4 = (f32[2,36,132]{2,1,0:T(8,128)}, f32[2,36,132]{2,1,0:T(8,128)}, u32[]{:S(2)}, u32[]{:S(2)}) collective-permute-start(f32[2,36,132]{2,1,0:T(8,128)} %get-tuple-element.55), channel_id=1, source_target_pairs={{8,0},{16,8},{24,16},{9,1},{17,9},{25,17},{10,2},{18,10},{26,18},{... | collective-permute-start | bytes 114056 | tf_op jit(solution)/shard_map/ppermute | solution.py:22
  45.8 30.7 %collective-permute-start.5 = (f32[2,36,132]{2,1,0:T(8,128)}, f32[2,36,132]{2,1,0:T(8,128)}, u32[]{:S(2)}, u32[]{:S(2)}) collective-permute-start(f32[2,36,132]{2,1,0:T(8,128)} %get-tuple-element.56), channel_id=1, source_target_pairs={{0,8},{8,16},{16,24},{1,9},{9,17},{17,25},{2,10},{10,18},{18,26},{... | collective-permute-start | bytes 114056 | tf_op jit(solution)/shard_map/ppermute | solution.py:19
  50.4 22.7 %copy-start.32 = (pred[16,32,128]{2,1,0:T(8,128)(4,1)}, pred[16,32,128]{2,1,0:T(8,128)(4,1)S(1)}, u32[]{:S(2)}) copy-start(pred[16,32,128]{2,1,0:T(8,128)(4,1)S(1)} %slice.1343) | copy-start | bytes 196612
  50.6 22.5 %copy-start.34 = (pred[16,32,128]{2,1,0:T(8,128)(4,1)}, pred[16,32,128]{2,1,0:T(8,128)(4,1)S(1)}, u32[]{:S(2)}) copy-start(pred[16,32,128]{2,1,0:T(8,128)(4,1)S(1)} %slice.1342) | copy-start | bytes 196612
  50.7 22.4 %copy-start.36 = (pred[16,32,128]{2,1,0:T(8,128)(4,1)}, pred[16,32,128]{2,1,0:T(8,128)(4,1)S(1)}, u32[]{:S(2)}) copy-start(pred[16,32,128]{2,1,0:T(8,128)(4,1)S(1)} %slice.1341) | copy-start | bytes 196612
  51.7 4.3 %slice-start = ((f32[35,96,192]{2,1,0:T(8,128)}), f32[16,96,192]{2,1,0:T(8,128)S(1)}, s32[]{:S(2)}) async-start(f32[35,96,192]{2,1,0:T(8,128)} %copy-done.11), calls=%async_computation | async-start | bytes 3145728 | tf_op jit(solution)/shard_map/slice | solution.py:141
  51.7 4.2 %copy-start.42 = (f32[3]{0:T(128)S(1)}, f32[3]{0:T(128)}, u32[]{:S(2)}) copy-start(f32[3]{0:T(128)} %get-tuple-element.5) | copy-start | bytes 40
  51.7 4.2 %copy-start.43 = (f32[3]{0:T(128)S(1)}, f32[3]{0:T(128)}, u32[]{:S(2)}) copy-start(f32[3]{0:T(128)} %get-tuple-element.15) | copy-start | bytes 40
  51.7 4.2 %copy-start.45 = (f32[3]{0:T(128)S(1)}, f32[3]{0:T(128)}, u32[]{:S(2)}) copy-start(f32[3]{0:T(128)} %get-tuple-element.16) | copy-start | bytes 40
  51.7 4.2 %copy-start.47 = (f32[3]{0:T(128)S(1)}, f32[3]{0:T(128)}, u32[]{:S(2)}) copy-start(f32[3]{0:T(128)} %get-tuple-element.17) | copy-start | bytes 40
  51.7 4.2 %copy-start.49 = (f32[3]{0:T(128)S(1)}, f32[3]{0:T(128)}, u32[]{:S(2)}) copy-start(f32[3]{0:T(128)} %get-tuple-element.18) | copy-start | bytes 40
  65.0 2.2 %copy-start.7 = (f32[16,32,128]{2,1,0:T(8,128)S(1)}, f32[16,32,128]{2,1,0:T(8,128)}, u32[]{:S(2)}) copy-start(f32[16,32,128]{2,1,0:T(8,128)} %param.6) | copy-start | bytes 786436
  65.0 2.2 %copy-start.10 = (f32[16,32,128]{2,1,0:T(8,128)S(1)}, f32[16,32,128]{2,1,0:T(8,128)}, u32[]{:S(2)}) copy-start(f32[16,32,128]{2,1,0:T(8,128)} %copy-done.8) | copy-start | bytes 786436
  69.6 3.5 %copy-start.24 = (f32[16,32,128]{2,1,0:T(8,128)S(1)}, f32[16,32,128]{2,1,0:T(8,128)}, u32[]{:S(2)}) copy-start(f32[16,32,128]{2,1,0:T(8,128)} %slice.1345) | copy-start | bytes 786436
  69.6 3.5 %copy-start.38 = (pred[16,32,128]{2,1,0:T(8,128)(4,1)S(1)}, pred[16,32,128]{2,1,0:T(8,128)(4,1)}, u32[]{:S(2)}) copy-start(pred[16,32,128]{2,1,0:T(8,128)(4,1)} %slice.1339) | copy-start | bytes 196612
  70.5 5.8 %copy-start.12 = (f32[35,96,192]{2,1,0:T(8,128)S(1)}, f32[35,96,192]{2,1,0:T(8,128)}, u32[]{:S(2)}) copy-start(f32[35,96,192]{2,1,0:T(8,128)} %copy-done.11) | copy-start | bytes 7741444
  70.8 8.2 %collective-permute-start.6 = (f32[3,80,176]{2,1,0:T(8,128)S(1)}, f32[3,80,176]{2,1,0:T(8,128)S(1)}, u32[]{:S(2)}, u32[]{:S(2)}) collective-permute-start(f32[3,80,176]{2,1,0:T(8,128)S(1)} %fusion.61), channel_id=1, source_target_pairs={{0,8},{8,16},{16,24},{1,9},{9,17},{17,25},{2,10},{10,18},{18,26},{... | collective-permute-start | bytes 506888 | tf_op jit(solution)/shard_map/ppermute | solution.py:30
  81.2 2.9 %copy-start.40 = (f32[18,34]{1,0:T(8,128)S(1)}, f32[18,34]{1,0:T(8,128)}, u32[]{:S(2)}) copy-start(f32[18,34]{1,0:T(8,128)} %broadcast_multiply_fusion.1) | copy-start | bytes 7348
  81.2 2.9 %copy-start.63 = (f32[130]{0:T(256)S(1)}, f32[130]{0:T(256)}, u32[]{:S(2)}) copy-start(f32[130]{0:T(256)} %and_convert_fusion.2) | copy-start | bytes 1564
  82.2 7.6 %collective-permute-start.7 = (f32[3,64,160]{2,1,0:T(8,128)S(1)}, f32[3,64,160]{2,1,0:T(8,128)S(1)}, u32[]{:S(2)}, u32[]{:S(2)}) collective-permute-start(f32[3,64,160]{2,1,0:T(8,128)S(1)} %fusion.93), channel_id=1, source_target_pairs={{0,8},{8,16},{16,24},{1,9},{9,17},{17,25},{2,10},{10,18},{18,26},{... | collective-permute-start | bytes 368648 | tf_op jit(solution)/shard_map/ppermute | solution.py:30
  92.4 7.3 %collective-permute-start.8 = (f32[3,48,144]{2,1,0:T(8,128)S(1)}, f32[3,48,144]{2,1,0:T(8,128)S(1)}, u32[]{:S(2)}, u32[]{:S(2)}) collective-permute-start(f32[3,48,144]{2,1,0:T(8,128)S(1)} %fusion.125), channel_id=1, source_target_pairs={{0,8},{8,16},{16,24},{1,9},{9,17},{17,25},{2,10},{10,18},{18,26},{... | collective-permute-start | bytes 248840 | tf_op jit(solution)/shard_map/ppermute | solution.py:30
  102.5 2.4 %copy-start.41 = (f32[1,2,2,128]{3,2,1,0:T(2,128)S(1)}, f32[1,2,2,128]{3,2,1,0:T(2,128)}, u32[]{:S(2)}) copy-start(f32[1,2,2,128]{3,2,1,0:T(2,128)} %exp.32) | copy-start | bytes 6148
  105.0 2.0 %collective-permute-start.9 = (f32[4,2,128]{2,1,0:T(2,128)S(1)}, f32[4,2,128]{2,1,0:T(2,128)S(1)}, u32[]{:S(2)}, u32[]{:S(2)}) collective-permute-start(f32[4,2,128]{2,1,0:T(2,128)S(1)} %bitcast.326), channel_id=1, source_target_pairs={{0,2},{2,0},{4,6},{6,4},{1,3},{3,1},{5,7},{7,5},{8,10},{10,8},{12,... | collective-permute-start | bytes 12296 | tf_op jit(solution)/shard_map/ppermute | solution.py:40
  107.1 9.6 %collective-permute-start.10 = (f32[4,1,128]{2,0,1:T(4,128)S(1)}, f32[4,1,128]{2,0,1:T(4,128)S(1)}, u32[]{:S(2)}, u32[]{:S(2)}) collective-permute-start(f32[4,1,128]{2,0,1:T(4,128)S(1)} %bitcast.327), channel_id=1, source_target_pairs={{0,4},{4,0},{2,6},{6,2},{1,5},{5,1},{3,7},{7,3},{8,12},{12,8},{10,... | collective-permute-start | bytes 6152 | tf_op jit(solution)/shard_map/ppermute | solution.py:40
  (13 other events, 18.7 us)

commit v9 on v7

--- a/solution.py
+++ b/solution.py
@@ -1,6 +1,8 @@
 import jax
 import jax.numpy as jnp
 from jax import lax
+from jax.experimental import pallas as pl
+from jax.experimental.pallas import tpu as pltpu
 from jax.sharding import PartitionSpec as P
 
 SLABS = 8
@@ -122,6 +124,51 @@
     return (current, jnp.stack(starts, axis=1))
 
 
+def fade_rim_of(extinction_table, density_rim, labels_rim, mask, light_step):
+    rows, rim_a, rim_v = density_rim.shape
+    layer_rows = rows // SLABS
+    colours, materials = extinction_table.shape
+    chunk = 8 if rim_a % 8 == 0 else rim_a
+
+    def kernel(table_ref, density_ref, labels_ref, mask_ref, out_ref):
+        def one_slab(slab_num, carry):
+            for first in range(0, rim_a, chunk):
+                part = slice(first, first + chunk)
+                depth = [None] * colours
+                for row in range(layer_rows):
+                    row_num = slab_num * layer_rows + row
+                    here = labels_ref[row_num, part, :]
+                    cells = density_ref[row_num, part, :]
+                    looked = [jnp.full(here.shape, table_ref[c, 0]) for c in range(colours)]
+                    for material in range(1, materials):
+                        match = here == float(material)
+                        looked = [
+                            jnp.where(match, table_ref[c, material], looked[c]) for c in range(colours)
+                        ]
+                    for c in range(colours):
+                        term = looked[c] * cells
+                        depth[c] = term if depth[c] is None else depth[c] + term
+                for c in range(colours):
+                    out_ref[c, slab_num, part, :] = (
+                        jnp.exp(-light_step * depth[c]) * mask_ref[part, :]
+                    )
+            return carry
+
+        lax.fori_loop(0, SLABS, one_slab, 0)
+
+    return pl.pallas_call(
+        kernel,
+        out_shape=jax.ShapeDtypeStruct((colours, SLABS, rim_a, rim_v), jnp.float32),
+        in_specs=[
+            pl.BlockSpec(memory_space=pltpu.SMEM),
+            pl.BlockSpec(memory_space=pltpu.VMEM),
+            pl.BlockSpec(memory_space=pltpu.VMEM),
+            pl.BlockSpec(memory_space=pltpu.VMEM),
+        ],
+        out_specs=pl.BlockSpec(memory_space=pltpu.VMEM),
+    )(extinction_table, density_rim, labels_rim, mask)
+
+
 def shards(density, labels, sunlight, opacity_table, extinction_table, albedo_table):
     brick_l, brick_a, brick_v = density.shape
     n_light = lax.axis_size("light")
@@ -135,7 +182,16 @@
     light_idx = lax.axis_index("light")
     view_idx = lax.axis_index("view")
     across_idx = lax.axis_index("across")
-    padded = padded_2(density, (("light", 0), ("view", 2), ("across", 1)), 2)
+    widest = SLABS * n_light
+    stack = jnp.concatenate([density, labels.astype(jnp.float32), sunlight], axis=0)
+    stack_rim = halo(halo(stack, "across", 1, widest), "view", 2, widest)
+    density_rim = stack_rim[:brick_l]
+    labels_rim = stack_rim[brick_l : 2 * brick_l]
+    sun_rim = stack_rim[2 * brick_l :]
+    density_side = density_rim[
+        :, widest - 2 : widest + brick_a + 2, widest - 2 : widest + brick_v + 2
+    ]
+    padded = padded_2(density_side, (("light", 0),), 2)
     inside = (
         rim_mask(light_idx, n_light, brick_l, 1)[:, None, None]
         * rim_mask(across_idx, n_across, brick_a, 1)[None, :, None]
@@ -151,12 +207,9 @@
     extinct = looked[1:4] * density[None]
     extinct_slabs = extinct.reshape(3, SLABS, layer_rows, brick_a, brick_v)
     running = jnp.cumsum(extinct_slabs, axis=2) - extinct_slabs
-    slab_depth = jnp.sum(extinct_slabs, axis=2)
-    widest = SLABS * n_light
-    both = jnp.concatenate([slab_depth, sunlight[:, None]], axis=1)
-    both_rim = halo(halo(both, "across", 2, widest), "view", 3, widest)
-    sun_rim = both_rim[:, SLABS]
-    fade_rim = jnp.exp(-light_step * both_rim[:, :SLABS]) * plane_mask(widest, brick_a, brick_v)
+    fade_rim = fade_rim_of(
+        extinction_table, density_rim, labels_rim, plane_mask(widest, brick_a, brick_v), light_step
+    )
     starts = None
     incoming = sun_rim
     for section_num in range(n_light):

time: 111 us -> 111 us (level)
  starting transfers between devices: 42.5 us -> 29.8 us
  Pallas kernels: 0 us -> 8.6 us
  waiting for transfers between devices: 17 us -> 22.6 us
  local copies, waits for them, and re-layouts: 16.8 us -> 15.6 us
    pallas_call x0 -> x1, Pallas kernels: none -> 8.6 us  [fade_rim_of(): pl.pallas_call(kernel, out_shape=jax.ShapeDtypeStruct((colours, SLABS, ri...]
    ppermute x3 -> x1, starting transfers between devices: 11.7 us -> 4.28 us  [padded_2(): lax.ppermute(lax.slice_in_dim(block, block.shape[dim] - width, None, axis...]
    ppermute x2, starting transfers between devices: 12.8 us -> 5.59 us  [halo(): lows.insert(0, lax.ppermute(low, axis, forward))]
    ppermute x2, starting transfers between devices: 2.34 us -> 8.88 us  [from_partner(): return lax.ppermute(block, axis, route)]
    ppermute x2, waiting for transfers between devices: 0.01 us -> 5.36 us  [halo(): lax.ppermute(lax.slice_in_dim(block, 0, need, axis=dim), axis, backward)]
    mul x2 -> x0, other arithmetic: 5.23 us -> none  [the longest x1 2.96 us: shards(): jnp.exp(-light_step * both_rim[:, :SLABS])]
    ppermute x2, waiting for transfers between devices: 0.01 us -> 3.49 us  [halo(): lows.insert(0, lax.ppermute(low, axis, forward))]
    ppermute x3 -> x1, starting transfers between devices: 4.93 us -> 2.35 us  [padded_2(): lax.ppermute(lax.slice_in_dim(block, 0, width, axis=dim), axis, backward)]
  transfers between devices with their start and end apart: 15 -> 11, of which waited for: 7 -> 8; matrix products, arithmetic and copies ran while one was open for 20% -> 24% of each run, Pallas kernels for 0% -> 8%
where the time goes in v9:
time: 111 us; the launch traced here: 110 us
  other arithmetic  31.3 us (28%)
  starting transfers between devices  29.8 us (27%)
  waiting for transfers between devices  22.6 us (20%)
  local copies, waits for them, and re-layouts  15.6 us (14%)
  Pallas kernels  8.6 us (8%)
    mul x31, other arithmetic, propagate(): current = current * fade_here  12.1 us
    ppermute x3, waiting for transfers between devices, from_behind(): lax.ppermute(value, axis, [(source, source + steps) for source in range(l...  11.4 us
    ppermute x2, starting transfers between devices, from_partner(): return lax.ppermute(block, axis, route)  8.88 us
    pallas_call x1, Pallas kernels, fade_rim_of(): pl.pallas_call(kernel, out_shape=jax.ShapeDtypeStruct((colours, SLABS, ri...  8.6 us
    ppermute x3, starting transfers between devices, from_behind(): lax.ppermute(value, axis, [(source, source + steps) for source in range(l...  6.1 us
    ppermute x2, starting transfers between devices, halo(): lows.insert(0, lax.ppermute(low, axis, forward))  5.59 us
    ppermute x2, waiting for transfers between devices, halo(): lax.ppermute(lax.slice_in_dim(block, 0, need, axis=dim), axis, backward)  5.36 us
    ppermute x1, starting transfers between devices, padded_2(): lax.ppermute(lax.slice_in_dim(block, block.shape[dim] - width, None, axis...  4.28 us
  transfers between devices with their start and end apart: 11, of which 8 were waited for; matrix products, arithmetic and copies ran while one was open for 24% of the time, Pallas kernels for 8%

profile of v9, /device:TPU:16, one launch (start us, length us, event | category | flops | bytes accessed | tf_op | source)
XLA Modules:
  0.0 109.5 jit_solution(18271086070655281421)
XLA Ops:
  0.0 1.0 convert_element_type.39
  1.1 1.1 %pad_maximum_fusion.5 = f32[35,32,128]{2,1,0:T(8,128)S(1)} fusion(f32[3,32,128]{2,1,0:T(8,128)} %param.8, f32[16,32,128]{2,1,0:T(8,128)S(1)} %convert_element_type.39, f32[16,32,128]{2,1,0:T(8,128)} %param.6), kind=kLoop, calls=%fused_computation.18 | loop fusion | flops 286720 | bytes 1146880 | tf_op jit(solution)/shard_map/concatenate | solution.py:186
  2.2 3.5 %collective-permute-start = (f32[35,32,128]{2,1,0:T(8,128)S(1)}, f32[35,32,128]{2,1,0:T(8,128)S(1)}, u32[]{:S(2)}, u32[]{:S(2)}) collective-permute-start(f32[35,32,128]{2,1,0:T(8,128)S(1)} %pad_maximum_fusion.5), channel_id=1, source_target_pairs={{0,1},{2,3},{4,5},{6,7},{8,9},{10,11},{12,13},{14,15},{16,17},{18,... | collective-permute-start | bytes 1720328 | tf_op jit(solution)/shard_map/ppermute | solution.py:84
  5.6 1.3 %collective-permute-start.1 = (f32[35,32,128]{2,1,0:T(8,128)S(1)}, f32[35,32,128]{2,1,0:T(8,128)S(1)}, u32[]{:S(2)}, u32[]{:S(2)}) collective-permute-start(f32[35,32,128]{2,1,0:T(8,128)S(1)} %pad_maximum_fusion.5), channel_id=1, source_target_pairs={{1,0},{3,2},{5,4},{7,6},{9,8},{11,10},{13,12},{15,14},{17,16},{19,... | collective-permute-start | bytes 1720328 | tf_op jit(solution)/shard_map/ppermute | solution.py:85
  7.0 0.6 broadcast_compare_fusion.14
  7.7 0.4 slice_reduce_fusion.15
  8.1 2.6 %select_select_fusion = f32[7,16,32,128]{3,2,1,0:T(8,128)S(1)} fusion(f32[7]{0:T(128)S(1)} %get-tuple-element.6, f32[7]{0:T(128)S(1)} %get-tuple-element.7, f32[7]{0:T(128)S(1)} %get-tuple-element.8, f32[7]{0:T(128)S(1)} %get-tuple-element.9, f32[7]{0:T(128)S(1)} %get-tuple-element.10, f32[7]{0:T(128)S(1)} %get-tuple-element.11, f32[7]{0:T(128)S(1)} %get-tuple-element.12, ...), kind=kLoop, calls=%fused_computation.1 | loop fusion | flops 6881280 | bytes 2818496 | tf_op jit(solution)/shard_map/jit(_where)/select_n | solution.py:204
  10.8 0.9 fusion.151
  11.6 0.7 broadcast_multiply_fusion.mask_ref
  12.4 1.0 fusion
  13.4 1.0 slice_multiply_fusion
  14.3 3.5 %collective-permute-done = f32[35,32,128]{2,1,0:T(8,128)S(1)} collective-permute-done((f32[35,32,128]{2,1,0:T(8,128)S(1)}, f32[35,32,128]{2,1,0:T(8,128)S(1)}, u32[]{:S(2)}, u32[]{:S(2)}) %collective-permute-start) | collective-permute-done | bytes 573472 | tf_op jit(solution)/shard_map/ppermute | solution.py:84
  17.8 4.1 %collective-permute-done.1 = f32[35,32,128]{2,1,0:T(8,128)S(1)} collective-permute-done((f32[35,32,128]{2,1,0:T(8,128)S(1)}, f32[35,32,128]{2,1,0:T(8,128)S(1)}, u32[]{:S(2)}, u32[]{:S(2)}) %collective-permute-start.1) | collective-permute-done | bytes 573472 | tf_op jit(solution)/shard_map/ppermute | solution.py:85
  22.1 1.8 %fusion.160 = (f32[35,96,32]{2,1,0:T(8,128)}, f32[35,96,32]{2,1,0:T(8,128)S(1)}) fusion(f32[35,96,128]{2,1,0:T(8,128)S(1)} %pad_maximum_fusion.1), kind=kLoop, calls=%fused_computation.377 | loop fusion | bytes 1720320 | tf_op jit(solution)/shard_map/slice | solution.py:83
  23.9 2.0 %copy.123 = f32[35,96,32]{1,2,0:T(8,128)S(1)} copy(f32[35,96,32]{2,1,0:T(8,128)} %get-tuple-element.45) | data formatting | bytes 860160 | tf_op jit(solution)/shard_map/slice | solution.py:83
  25.9 2.1 %collective-permute-start.2 = (f32[35,96,32]{1,2,0:T(8,128)S(1)}, f32[35,96,32]{1,2,0:T(8,128)}, u32[]{:S(2)}, u32[]{:S(2)}) collective-permute-start(f32[35,96,32]{1,2,0:T(8,128)S(1)} %copy.123), channel_id=1, source_target_pairs={{0,2},{2,4},{4,6},{1,3},{3,5},{5,7},{8,10},{10,12},{12,14},{9,11},... | collective-permute-start | bytes 1290248 | tf_op jit(solution)/shard_map/ppermute | solution.py:84
  28.1 1.3 %copy.124 = f32[35,96,32]{1,2,0:T(8,128)} copy(f32[35,96,32]{2,1,0:T(8,128)S(1)} %get-tuple-element.46) | data formatting | bytes 860160 | tf_op jit(solution)/shard_map/slice | solution.py:85
  29.4 1.3 %collective-permute-start.3 = (f32[35,96,32]{1,2,0:T(8,128)}, f32[35,96,32]{1,2,0:T(8,128)}, u32[]{:S(2)}, u32[]{:S(2)}) collective-permute-start(f32[35,96,32]{1,2,0:T(8,128)} %copy.124), channel_id=1, source_target_pairs={{2,0},{4,2},{6,4},{3,1},{5,3},{7,5},{10,8},{12,10},{14,12},{11,9},... | collective-permute-start | bytes 1290248 | tf_op jit(solution)/shard_map/ppermute | solution.py:85
  30.7 0.9 fusion.164
  31.7 1.6 %copy.125 = f32[35,96,32]{2,1,0:T(8,128)S(1)} copy(f32[35,96,32]{1,2,0:T(8,128)} %collective-permute-done.2) | data formatting | bytes 860160 | tf_op jit(solution)/shard_map/ppermute | solution.py:84
  33.3 1.2 %collective-permute-done.3 = f32[35,96,32]{1,2,0:T(8,128)} collective-permute-done((f32[35,96,32]{1,2,0:T(8,128)}, f32[35,96,32]{1,2,0:T(8,128)}, u32[]{:S(2)}, u32[]{:S(2)}) %collective-permute-start.3) | collective-permute-done | bytes 430112 | tf_op jit(solution)/shard_map/ppermute | solution.py:85
  34.5 1.6 %copy.126 = f32[35,96,32]{2,1,0:T(8,128)S(1)} copy(f32[35,96,32]{1,2,0:T(8,128)} %collective-permute-done.3) | data formatting | bytes 860160 | tf_op jit(solution)/shard_map/ppermute | solution.py:85
  36.1 1.8 %pad_maximum_fusion.7 = (f32[2,36,132]{2,1,0:T(8,128)}, f32[2,36,132]{2,1,0:T(8,128)}) fusion(f32[35,96,32]{2,1,0:T(8,128)S(1)} %copy.126, f32[35,96,32]{2,1,0:T(8,128)S(1)} %copy.125, f32[35,32,128]{2,1,0:T(8,128)} %copy-done.8, f32[35,32,128]{2,1,0:T(8,128)} %copy-done.5, f32[3,32,128]{2,1,0:T(8,128)S(1)} %copy-done.17, f32[16,32,128]{2,1,0:T(8,128)} %copy-done.11, ...), kind=kLoop, calls=%fused_computation.303 | loop fusion | flops 114048 | bytes 2656512 | tf_op jit(solution)/shard_map/slice | solution.py:24
  37.9 2.3 %collective-permute-start.4 = (f32[2,36,132]{2,1,0:T(8,128)}, f32[2,36,132]{2,1,0:T(8,128)}, u32[]{:S(2)}, u32[]{:S(2)}) collective-permute-start(f32[2,36,132]{2,1,0:T(8,128)} %get-tuple-element.39), channel_id=1, source_target_pairs={{8,0},{16,8},{24,16},{9,1},{17,9},{25,17},{10,2},{18,10},{26,18},{... | collective-permute-start | bytes 114056 | tf_op jit(solution)/shard_map/ppermute | solution.py:24
  40.3 4.3 %collective-permute-start.5 = (f32[2,36,132]{2,1,0:T(8,128)}, f32[2,36,132]{2,1,0:T(8,128)}, u32[]{:S(2)}, u32[]{:S(2)}) collective-permute-start(f32[2,36,132]{2,1,0:T(8,128)} %get-tuple-element.40), channel_id=1, source_target_pairs={{0,8},{8,16},{16,24},{1,9},{9,17},{17,25},{2,10},{10,18},{18,26},{... | collective-permute-start | bytes 114056 | tf_op jit(solution)/shard_map/ppermute | solution.py:21
  44.6 1.6 %pad_maximum_fusion = f32[35,96,192]{2,1,0:T(8,128)S(1)} fusion(f32[35,96,32]{2,1,0:T(8,128)S(1)} %copy.126, f32[35,32,128]{2,1,0:T(8,128)S(1)} %copy-done.9, f32[3,32,128]{2,1,0:T(8,128)S(1)} %copy-done.17, f32[16,32,128]{2,1,0:T(8,128)S(1)} %copy-done.12, f32[16,32,128]{2,1,0:T(8,128)S(1)} %copy-done.1, f32[35,32,128]{2,1,0:T(8,128)S(1)} %copy-done.6, ...), kind=kLoop, calls=%fused_computation | loop fusion | flops 3870720 | bytes 5160960 | tf_op jit(solution)/shard_map/concatenate | solution.py:86
  46.2 2.3 %fusion.159 = (f32[16,96,192]{2,1,0:T(8,128)}, f32[16,96,192]{2,1,0:T(8,128)}) fusion(f32[35,96,192]{2,1,0:T(8,128)S(1)} %pad_maximum_fusion), kind=kLoop, calls=%fused_computation.376 | loop fusion | bytes 4718592 | tf_op jit(solution)/shard_map/slice | solution.py:189
  48.5 0.5 copy-done.14
  48.9 8.6 %shard_map.64 = f32[3,8,96,192]{3,2,1,0:T(8,128)} custom-call(f32[3,16]{1,0:T(4,128)} %table_ref.1, f32[16,96,192]{2,1,0:T(8,128)} %get-tuple-element.42.density_ref, f32[16,96,192]{2,1,0:T(8,128)} %get-tuple-element.41.labels_ref, f32[96,192]{1,0:T(8,128)} %broadcast_multiply_fusion.mask_ref), custom_call_target="tpu_custom_call" | custom-call | tf_op jit(solution)/shard_map/pallas_call | solution.py:159
  57.5 1.3 %fusion.17 = f32[3,96,192]{2,1,0:T(8,128)S(1)} fusion(f32[3,8,96,192]{3,2,1,0:T(8,128)} %shard_map.64, f32[35,96,32]{2,1,0:T(8,128)S(1)} %copy.126, f32[35,96,32]{2,1,0:T(8,128)S(1)} %copy.125, f32[35,32,128]{2,1,0:T(8,128)} %copy-done.8, f32[35,32,128]{2,1,0:T(8,128)} %copy-done.5, f32[3,32,128]{2,1,0:T(8,128)S(1)} %copy-done.17, ...), kind=kLoop, calls=%fused_computation.44 | loop fusion | flops 387072 | bytes 3022848 | tf_op jit(solution)/shard_map/mul | solution.py:115
  58.8 0.5 copy-done.3
  59.3 0.4 fusion.13
  59.8 0.4 fusion.9
  60.2 0.4 fusion.5
  60.7 0.4 fusion.30
  61.1 0.4 fusion.26
  61.5 0.4 fusion.22
  61.9 0.4 fusion.18
  62.4 1.0 fusion.56
  63.4 1.9 %collective-permute-start.6 = (f32[3,80,176]{2,1,0:T(8,128)}, f32[3,80,176]{2,1,0:T(8,128)}, u32[]{:S(2)}, u32[]{:S(2)}) collective-permute-start(f32[3,80,176]{2,1,0:T(8,128)} %fusion.56), channel_id=1, source_target_pairs={{0,8},{8,16},{16,24},{1,9},{9,17},{17,25},{2,10},{10,18},{18,26},{... | collective-permute-start | bytes 506888 | tf_op jit(solution)/shard_map/ppermute | solution.py:32
  65.4 1.5 %slice.1056 = f32[16,36,132]{2,1,0:T(8,128)S(1)} slice(f32[35,96,192]{2,1,0:T(8,128)} %copy-done.14), slice={[0:16], [30:66], [30:162]} | slice | bytes 608256 | tf_op jit(solution)/shard_map/slice | solution.py:191
  67.0 1.0 pad_maximum_fusion.2
  68.0 3.8 %collective-permute-done.6 = f32[3,80,176]{2,1,0:T(8,128)} collective-permute-done((f32[3,80,176]{2,1,0:T(8,128)}, f32[3,80,176]{2,1,0:T(8,128)}, u32[]{:S(2)}, u32[]{:S(2)}) %collective-permute-start.6) | collective-permute-done | bytes 168992 | tf_op jit(solution)/shard_map/ppermute | solution.py:32
  71.8 1.2 %fusion.53 = f32[3,80,176]{2,1,0:T(8,128)S(1)} fusion(f32[3,8,96,192]{3,2,1,0:T(8,128)S(1)} %copy-done.4, f32[3,80,176]{2,1,0:T(8,128)} %collective-permute-done.6, f32[35,96,32]{2,1,0:T(8,128)S(1)} %copy.126, f32[35,96,32]{2,1,0:T(8,128)S(1)} %copy.125, f32[35,32,128]{2,1,0:T(8,128)} %copy-done.8, f32[35,32,128]{2,1,0:T(8,128)} %copy-done.5, ...), kind=kLoop, calls=%fused_computation.125 | loop fusion | flops 337920 | bytes 3087361 | tf_op jit(solution)/shard_map/mul | solution.py:115
  73.0 0.4 fusion.49
  73.4 0.4 fusion.45
  73.8 0.4 fusion.41
  74.2 0.4 fusion.69
  74.5 0.4 fusion.65
  74.9 0.4 fusion.61
  75.3 0.4 fusion.57
  75.9 2.3 %collective-permute-start.7 = (f32[3,64,160]{2,1,0:T(8,128)S(1)}, f32[3,64,160]{2,1,0:T(8,128)S(1)}, u32[]{:S(2)}, u32[]{:S(2)}) collective-permute-start(f32[3,64,160]{2,1,0:T(8,128)S(1)} %fusion.88), channel_id=1, source_target_pairs={{0,8},{8,16},{16,24},{1,9},{9,17},{17,25},{2,10},{10,18},{18,26},{... | collective-permute-start | bytes 368648 | tf_op jit(solution)/shard_map/ppermute | solution.py:32
  78.2 2.1 %multiply_multiply_fusion.1 = (f32[18,34,130]{2,1,0:T(8,128)S(1)}, f32[18,34,130]{2,1,0:T(8,128)S(1)}) fusion(f32[16,36,132]{2,1,0:T(8,128)S(1)} %slice.1056, f32[2,36,132]{2,1,0:T(8,128)} %collective-permute-done.5, f32[2,36,132]{2,1,0:T(8,128)} %collective-permute-done.4, f32[130]{0:T(256)S(1)} %and_convert_fusion.2, ...), kind=kLoop, calls=%fused_computation.6 | loop fusion | flops 1750320 | bytes 2292568 | tf_op jit(solution)/shard_map/mul | solution.py:63
  80.3 3.3 %collective-permute-done.7 = f32[3,64,160]{2,1,0:T(8,128)S(1)} collective-permute-done((f32[3,64,160]{2,1,0:T(8,128)S(1)}, f32[3,64,160]{2,1,0:T(8,128)S(1)}, u32[]{:S(2)}, u32[]{:S(2)}) %collective-permute-start.7) | collective-permute-done | bytes 122912 | tf_op jit(solution)/shard_map/ppermute | solution.py:32
  86.2 1.9 %collective-permute-start.8 = (f32[3,48,144]{2,1,0:T(8,128)S(1)}, f32[3,48,144]{2,1,0:T(8,128)S(1)}, u32[]{:S(2)}, u32[]{:S(2)}) collective-permute-start(f32[3,48,144]{2,1,0:T(8,128)S(1)} %fusion.120), channel_id=1, source_target_pairs={{0,8},{8,16},{16,24},{1,9},{9,17},{17,25},{2,10},{10,18},{18,26},{... | collective-permute-start | bytes 248840 | tf_op jit(solution)/shard_map/ppermute | solution.py:32
  88.2 0.9 fusion.37
  89.0 4.2 %collective-permute-done.8 = f32[3,48,144]{2,1,0:T(8,128)S(1)} collective-permute-done((f32[3,48,144]{2,1,0:T(8,128)S(1)}, f32[3,48,144]{2,1,0:T(8,128)S(1)}, u32[]{:S(2)}, u32[]{:S(2)}) %collective-permute-start.8) | collective-permute-done | bytes 82976 | tf_op jit(solution)/shard_map/ppermute | solution.py:32
  96.0 0.4 copy-done.16
  96.8 0.5 fusion.3
  97.4 3.7 %collective-permute-start.9 = (f32[4,2,128]{2,1,0:T(2,128)S(1)}, f32[4,2,128]{2,1,0:T(2,128)S(1)}, u32[]{:S(2)}, u32[]{:S(2)}) collective-permute-start(f32[4,2,128]{2,1,0:T(2,128)S(1)} %bitcast.280), channel_id=1, source_target_pairs={{0,2},{2,0},{4,6},{6,4},{1,3},{3,1},{5,7},{7,5},{8,10},{10,8},{12,... | collective-permute-start | bytes 12296 | tf_op jit(solution)/shard_map/ppermute | solution.py:42
  101.1 0.8 collective-permute-done.9
  101.9 5.2 %collective-permute-start.10 = (f32[4,1,128]{2,0,1:T(4,128)S(1)}, f32[4,1,128]{2,0,1:T(4,128)S(1)}, u32[]{:S(2)}, u32[]{:S(2)}) collective-permute-start(f32[4,1,128]{2,0,1:T(4,128)S(1)} %bitcast.281), channel_id=1, source_target_pairs={{0,4},{4,0},{2,6},{6,2},{1,5},{5,1},{3,7},{7,3},{8,12},{12,8},{10,... | collective-permute-start | bytes 6152 | tf_op jit(solution)/shard_map/ppermute | solution.py:42
  107.1 1.6 %collective-permute-done.10 = f32[4,1,128]{2,0,1:T(4,128)S(1)} collective-permute-done((f32[4,1,128]{2,0,1:T(4,128)S(1)}, f32[4,1,128]{2,0,1:T(4,128)S(1)}, u32[]{:S(2)}, u32[]{:S(2)}) %collective-permute-start.10) | collective-permute-done | bytes 2080 | tf_op jit(solution)/shard_map/ppermute | solution.py:42
  108.9 0.6 pad_maximum_fusion.8
  (107 shorter events, 6.6 us)
Async XLA Ops:
  0.0 7.0 %copy-start.22 = (s32[16,32,128]{2,1,0:T(8,128)S(1)}, s32[16,32,128]{2,1,0:T(8,128)}, u32[]{:S(2)}) copy-start(s32[16,32,128]{2,1,0:T(8,128)} %param.7) | copy-start | bytes 786436
  0.0 7.7 %copy-start.23 = (f32[3,16]{1,0:T(4,128)S(1)}, f32[3,16]{1,0:T(4,128)}, u32[]{:S(2)}) copy-start(f32[3,16]{1,0:T(4,128)} %table_ref.1) | copy-start | bytes 580
  0.0 7.7 %copy-start.25 = (f32[16]{0:T(128)S(1)}, f32[16]{0:T(128)}, u32[]{:S(2)}) copy-start(f32[16]{0:T(128)} %param.9) | copy-start | bytes 196
  0.0 7.7 %copy-start.24 = (f32[3,16]{1,0:T(4,128)S(1)}, f32[3,16]{1,0:T(4,128)}, u32[]{:S(2)}) copy-start(f32[3,16]{1,0:T(4,128)} %param.11) | copy-start | bytes 580
  1.0 20.9 %copy-start.11 = (f32[16,32,128]{2,1,0:T(8,128)}, f32[16,32,128]{2,1,0:T(8,128)S(1)}, u32[]{:S(2)}) copy-start(f32[16,32,128]{2,1,0:T(8,128)S(1)} %convert_element_type.39) | copy-start | bytes 786436
  2.2 15.6 %collective-permute-start = (f32[35,32,128]{2,1,0:T(8,128)S(1)}, f32[35,32,128]{2,1,0:T(8,128)S(1)}, u32[]{:S(2)}, u32[]{:S(2)}) collective-permute-start(f32[35,32,128]{2,1,0:T(8,128)S(1)} %pad_maximum_fusion.5), channel_id=1, source_target_pairs={{0,1},{2,3},{4,5},{6,7},{8,9},{10,11},{12,13},{14,15},{16,17},{18,... | collective-permute-start | bytes 1720328 | tf_op jit(solution)/shard_map/ppermute | solution.py:84
  5.6 16.3 %collective-permute-start.1 = (f32[35,32,128]{2,1,0:T(8,128)S(1)}, f32[35,32,128]{2,1,0:T(8,128)S(1)}, u32[]{:S(2)}, u32[]{:S(2)}) collective-permute-start(f32[35,32,128]{2,1,0:T(8,128)S(1)} %pad_maximum_fusion.5), channel_id=1, source_target_pairs={{1,0},{3,2},{5,4},{7,6},{9,8},{11,10},{13,12},{15,14},{17,16},{19,... | collective-permute-start | bytes 1720328 | tf_op jit(solution)/shard_map/ppermute | solution.py:85
  7.0 3.8 %copy-start = (f32[16,32,128]{2,1,0:T(8,128)S(1)}, f32[16,32,128]{2,1,0:T(8,128)}, u32[]{:S(2)}) copy-start(f32[16,32,128]{2,1,0:T(8,128)} %param.6) | copy-start | bytes 786436
  10.7 7.1 %copy-start.15 = (f32[7,16,32,128]{3,2,1,0:T(8,128)}, f32[7,16,32,128]{3,2,1,0:T(8,128)S(1)}, u32[]{:S(2)}) copy-start(f32[7,16,32,128]{3,2,1,0:T(8,128)S(1)} %select_select_fusion) | copy-start | bytes 5505028
  10.8 11.2 %copy-start.17 = (f32[3,32,128]{2,1,0:T(8,128)S(1)}, f32[3,32,128]{2,1,0:T(8,128)}, u32[]{:S(2)}) copy-start(f32[3,32,128]{2,1,0:T(8,128)} %param.8) | copy-start | bytes 147460
  17.8 6.1 %copy-start.5 = (f32[35,32,128]{2,1,0:T(8,128)}, f32[35,32,128]{2,1,0:T(8,128)S(1)}, u32[]{:S(2)}) copy-start(f32[35,32,128]{2,1,0:T(8,128)S(1)} %collective-permute-done) | copy-start | bytes 1720324
  22.0 1.9 %copy-start.8 = (f32[35,32,128]{2,1,0:T(8,128)}, f32[35,32,128]{2,1,0:T(8,128)S(1)}, u32[]{:S(2)}) copy-start(f32[35,32,128]{2,1,0:T(8,128)S(1)} %collective-permute-done.1) | copy-start | bytes 1720324
  23.9 6.8 %copy-start.19 = (f32[3,16,32,128]{3,2,1,0:T(8,128)S(1)}, f32[3,16,32,128]{3,2,1,0:T(8,128)}, u32[]{:S(2)}) copy-start(f32[3,16,32,128]{3,2,1,0:T(8,128)} %slice_multiply_fusion) | copy-start | bytes 2359300
  25.9 5.7 %collective-permute-start.2 = (f32[35,96,32]{1,2,0:T(8,128)S(1)}, f32[35,96,32]{1,2,0:T(8,128)}, u32[]{:S(2)}, u32[]{:S(2)}) collective-permute-start(f32[35,96,32]{1,2,0:T(8,128)S(1)} %copy.123), channel_id=1, source_target_pairs={{0,2},{2,4},{4,6},{1,3},{3,5},{5,7},{8,10},{10,12},{12,14},{9,11},... | collective-permute-start | bytes 1290248 | tf_op jit(solution)/shard_map/ppermute | solution.py:84
  29.4 5.1 %collective-permute-start.3 = (f32[35,96,32]{1,2,0:T(8,128)}, f32[35,96,32]{1,2,0:T(8,128)}, u32[]{:S(2)}, u32[]{:S(2)}) collective-permute-start(f32[35,96,32]{1,2,0:T(8,128)} %copy.124), channel_id=1, source_target_pairs={{2,0},{4,2},{6,4},{3,1},{5,3},{7,5},{10,8},{12,10},{14,12},{11,9},... | collective-permute-start | bytes 1290248 | tf_op jit(solution)/shard_map/ppermute | solution.py:85
  36.1 8.5 %copy-start.1 = (f32[16,32,128]{2,1,0:T(8,128)S(1)}, f32[16,32,128]{2,1,0:T(8,128)}, u32[]{:S(2)}) copy-start(f32[16,32,128]{2,1,0:T(8,128)} %param.6) | copy-start | bytes 786436
  36.1 8.5 %copy-start.6 = (f32[35,32,128]{2,1,0:T(8,128)S(1)}, f32[35,32,128]{2,1,0:T(8,128)}, u32[]{:S(2)}) copy-start(f32[35,32,128]{2,1,0:T(8,128)} %copy-done.5) | copy-start | bytes 1720324
  36.1 8.5 %copy-start.9 = (f32[35,32,128]{2,1,0:T(8,128)S(1)}, f32[35,32,128]{2,1,0:T(8,128)}, u32[]{:S(2)}) copy-start(f32[35,32,128]{2,1,0:T(8,128)} %copy-done.8) | copy-start | bytes 1720324
  36.1 8.5 %copy-start.12 = (f32[16,32,128]{2,1,0:T(8,128)S(1)}, f32[16,32,128]{2,1,0:T(8,128)}, u32[]{:S(2)}) copy-start(f32[16,32,128]{2,1,0:T(8,128)} %copy-done.11) | copy-start | bytes 786436
  37.9 29.0 %collective-permute-start.4 = (f32[2,36,132]{2,1,0:T(8,128)}, f32[2,36,132]{2,1,0:T(8,128)}, u32[]{:S(2)}, u32[]{:S(2)}) collective-permute-start(f32[2,36,132]{2,1,0:T(8,128)} %get-tuple-element.39), channel_id=1, source_target_pairs={{8,0},{16,8},{24,16},{9,1},{17,9},{25,17},{10,2},{18,10},{26,18},{... | collective-permute-start | bytes 114056 | tf_op jit(solution)/shard_map/ppermute | solution.py:24
  40.3 26.7 %collective-permute-start.5 = (f32[2,36,132]{2,1,0:T(8,128)}, f32[2,36,132]{2,1,0:T(8,128)}, u32[]{:S(2)}, u32[]{:S(2)}) collective-permute-start(f32[2,36,132]{2,1,0:T(8,128)} %get-tuple-element.40), channel_id=1, source_target_pairs={{0,8},{8,16},{16,24},{1,9},{9,17},{17,25},{2,10},{10,18},{18,26},{... | collective-permute-start | bytes 114056 | tf_op jit(solution)/shard_map/ppermute | solution.py:21
  46.2 2.8 %copy-start.14 = (f32[35,96,192]{2,1,0:T(8,128)}, f32[35,96,192]{2,1,0:T(8,128)S(1)}, u32[]{:S(2)}) copy-start(f32[35,96,192]{2,1,0:T(8,128)S(1)} %pad_maximum_fusion) | copy-start | bytes 7741444
  57.5 1.8 %copy-start.3 = (f32[3,8,96,192]{3,2,1,0:T(8,128)S(1)}, f32[3,8,96,192]{3,2,1,0:T(8,128)}, u32[]{:S(2)}) copy-start(f32[3,8,96,192]{3,2,1,0:T(8,128)} %shard_map.64) | copy-start | bytes 5308420
  63.4 8.4 %collective-permute-start.6 = (f32[3,80,176]{2,1,0:T(8,128)}, f32[3,80,176]{2,1,0:T(8,128)}, u32[]{:S(2)}, u32[]{:S(2)}) collective-permute-start(f32[3,80,176]{2,1,0:T(8,128)} %fusion.56), channel_id=1, source_target_pairs={{0,8},{8,16},{16,24},{1,9},{9,17},{17,25},{2,10},{10,18},{18,26},{... | collective-permute-start | bytes 506888 | tf_op jit(solution)/shard_map/ppermute | solution.py:32
  65.4 6.4 %copy-start.2 = (f32[16,32,128]{2,1,0:T(8,128)S(1)}, f32[16,32,128]{2,1,0:T(8,128)}, u32[]{:S(2)}) copy-start(f32[16,32,128]{2,1,0:T(8,128)} %param.6) | copy-start | bytes 786436
  65.4 6.4 %copy-start.4 = (f32[3,8,96,192]{3,2,1,0:T(8,128)S(1)}, f32[3,8,96,192]{3,2,1,0:T(8,128)}, u32[]{:S(2)}) copy-start(f32[3,8,96,192]{3,2,1,0:T(8,128)} %shard_map.64) | copy-start | bytes 5308420
  65.4 6.4 %copy-start.13 = (f32[16,32,128]{2,1,0:T(8,128)S(1)}, f32[16,32,128]{2,1,0:T(8,128)}, u32[]{:S(2)}) copy-start(f32[16,32,128]{2,1,0:T(8,128)} %copy-done.11) | copy-start | bytes 786436
  75.9 7.7 %copy-start.7 = (f32[35,32,128]{2,1,0:T(8,128)S(1)}, f32[35,32,128]{2,1,0:T(8,128)}, u32[]{:S(2)}) copy-start(f32[35,32,128]{2,1,0:T(8,128)} %copy-done.5) | copy-start | bytes 1720324
  75.9 7.7 %copy-start.10 = (f32[35,32,128]{2,1,0:T(8,128)S(1)}, f32[35,32,128]{2,1,0:T(8,128)}, u32[]{:S(2)}) copy-start(f32[35,32,128]{2,1,0:T(8,128)} %copy-done.8) | copy-start | bytes 1720324
  75.9 7.7 %collective-permute-start.7 = (f32[3,64,160]{2,1,0:T(8,128)S(1)}, f32[3,64,160]{2,1,0:T(8,128)S(1)}, u32[]{:S(2)}, u32[]{:S(2)}) collective-permute-start(f32[3,64,160]{2,1,0:T(8,128)S(1)} %fusion.88), channel_id=1, source_target_pairs={{0,8},{8,16},{16,24},{1,9},{9,17},{17,25},{2,10},{10,18},{18,26},{... | collective-permute-start | bytes 368648 | tf_op jit(solution)/shard_map/ppermute | solution.py:32
  86.2 7.0 %collective-permute-start.8 = (f32[3,48,144]{2,1,0:T(8,128)S(1)}, f32[3,48,144]{2,1,0:T(8,128)S(1)}, u32[]{:S(2)}, u32[]{:S(2)}) collective-permute-start(f32[3,48,144]{2,1,0:T(8,128)S(1)} %fusion.120), channel_id=1, source_target_pairs={{0,8},{8,16},{16,24},{1,9},{9,17},{17,25},{2,10},{10,18},{18,26},{... | collective-permute-start | bytes 248840 | tf_op jit(solution)/shard_map/ppermute | solution.py:32
  94.9 1.5 %copy-start.16 = (f32[7,16,32,128]{3,2,1,0:T(8,128)S(1)}, f32[7,16,32,128]{3,2,1,0:T(8,128)}, u32[]{:S(2)}) copy-start(f32[7,16,32,128]{3,2,1,0:T(8,128)} %copy-done.15) | copy-start | bytes 5505028
  94.9 1.7 %copy-start.18 = (f32[3,8,2,32,128]{4,3,2,1,0:T(8,128)S(1)}, f32[3,8,2,32,128]{4,3,2,1,0:T(8,128)}, u32[]{:S(2)}) copy-start(f32[3,8,2,32,128]{4,3,2,1,0:T(8,128)} %fusion.164) | copy-start | bytes 2359300
  95.0 1.7 %copy-start.20 = (f32[16,32,128]{2,1,0:T(8,128)S(1)}, f32[16,32,128]{2,1,0:T(8,128)}, u32[]{:S(2)}) copy-start(f32[16,32,128]{2,1,0:T(8,128)} %get-tuple-element.44) | copy-start | bytes 786436
  95.0 1.8 %copy-start.21 = (f32[16,32,128]{2,1,0:T(8,128)S(1)}, f32[16,32,128]{2,1,0:T(8,128)}, u32[]{:S(2)}) copy-start(f32[16,32,128]{2,1,0:T(8,128)} %fusion) | copy-start | bytes 786436
  97.4 4.5 %collective-permute-start.9 = (f32[4,2,128]{2,1,0:T(2,128)S(1)}, f32[4,2,128]{2,1,0:T(2,128)S(1)}, u32[]{:S(2)}, u32[]{:S(2)}) collective-permute-start(f32[4,2,128]{2,1,0:T(2,128)S(1)} %bitcast.280), channel_id=1, source_target_pairs={{0,2},{2,0},{4,6},{6,4},{1,3},{3,1},{5,7},{7,5},{8,10},{10,8},{12,... | collective-permute-start | bytes 12296 | tf_op jit(solution)/shard_map/ppermute | solution.py:42
  101.9 6.8 %collective-permute-start.10 = (f32[4,1,128]{2,0,1:T(4,128)S(1)}, f32[4,1,128]{2,0,1:T(4,128)S(1)}, u32[]{:S(2)}, u32[]{:S(2)}) collective-permute-start(f32[4,1,128]{2,0,1:T(4,128)S(1)} %bitcast.281), channel_id=1, source_target_pairs={{0,4},{4,0},{2,6},{6,2},{1,5},{5,1},{3,7},{7,3},{8,12},{12,8},{10,... | collective-permute-start | bytes 6152 | tf_op jit(solution)/shard_map/ppermute | solution.py:42

commit v10 on v9

--- a/solution.py
+++ b/solution.py
@@ -191,13 +191,6 @@
     density_side = density_rim[
         :, widest - 2 : widest + brick_a + 2, widest - 2 : widest + brick_v + 2
     ]
-    padded = padded_2(density_side, (("light", 0),), 2)
-    inside = (
-        rim_mask(light_idx, n_light, brick_l, 1)[:, None, None]
-        * rim_mask(across_idx, n_across, brick_a, 1)[None, :, None]
-        * rim_mask(view_idx, n_view, brick_v, 1)[None, None, :]
-    )
-    shading = shade_from(padded, inside)
     table_all = jnp.concatenate([opacity_table[None], extinction_table, albedo_table], axis=0)
     looked = jnp.broadcast_to(table_all[:, 0, None, None, None], (7,) + labels.shape)
     for material in range(1, table_all.shape[1]):
@@ -217,11 +210,20 @@
         outgoing, starts = propagate(
             incoming, border, fade_rim, brick_a, brick_v
         )
+        if section_num == 0:
+            outgoing, density_side = lax.optimization_barrier((outgoing, density_side))
         if section_num + 1 < n_light:
             arrived = from_behind(outgoing, "light", 1)
             cut = widest - border + SLABS
             sun_here = sun_rim[:, cut : cut + brick_a + 2 * (border - SLABS), cut : cut + brick_v + 2 * (border - SLABS)]
             incoming = jnp.where(light_idx == 0, sun_here, arrived)
+    padded = padded_2(density_side, (("light", 0),), 2)
+    inside = (
+        rim_mask(light_idx, n_light, brick_l, 1)[:, None, None]
+        * rim_mask(across_idx, n_across, brick_a, 1)[None, :, None]
+        * rim_mask(view_idx, n_view, brick_v, 1)[None, None, :]
+    )
+    shading = shade_from(padded, inside)
     lighting = (starts[:, :, None] * jnp.exp(-light_step * running)).reshape(
         3, brick_l, brick_a, brick_v
     )

time: 111 us -> 111 us (level)
  waiting for transfers between devices: 22.6 us -> 19.2 us
  local copies, waits for them, and re-layouts: 15.6 us -> 18.1 us
  starting transfers between devices: 29.8 us -> 32.2 us
  other arithmetic: 31.3 us -> 29.7 us
    ppermute x3, starting transfers between devices: 6.1 us -> 10.8 us  [from_behind(): lax.ppermute(value, axis, [(source, source + steps) for source in range(l...]
    ppermute x3, waiting for transfers between devices: 11.4 us -> 8.07 us  [from_behind(): lax.ppermute(value, axis, [(source, source + steps) for source in range(l...]
    slice x1 -> x0, other arithmetic: 1.81 us -> none  [padded_2(): lax.slice_in_dim(block, 0, width, axis=dim)]
    ppermute x2, starting transfers between devices: 8.88 us -> 7.08 us  [from_partner(): return lax.ppermute(block, axis, route)]
    slice x0 -> x1, local copies, waits for them, and re-layouts: none -> 1.59 us  [padded_2(): lax.slice_in_dim(block, 0, width, axis=dim)]
    unnamed x60 -> x54, local copies, waits for them, and re-layouts: 2.38 us -> 3.91 us
    concatenate x2, other arithmetic: 1.66 us -> 2.9 us  [halo(): block = jnp.concatenate(lows + [block] + highs, axis=dim)]
  transfers between devices with their start and end apart: 11 -> 11, of which waited for: 8 -> 8; matrix products, arithmetic and copies ran while one was open for 24% -> 15% of each run, Pallas kernels for 8% -> 0%
where the time goes in v10:
time: 111 us; the launch traced here: 109 us
  starting transfers between devices  32.2 us (29%)
  other arithmetic  29.7 us (27%)
  waiting for transfers between devices  19.2 us (17%)
  local copies, waits for them, and re-layouts  18.1 us (16%)
  Pallas kernels  8.54 us (8%)
    mul x31, other arithmetic, propagate(): current = current * fade_here  12.1 us
    ppermute x3, starting transfers between devices, from_behind(): lax.ppermute(value, axis, [(source, source + steps) for source in range(l...  10.8 us
    pallas_call x1, Pallas kernels, fade_rim_of(): pl.pallas_call(kernel, out_shape=jax.ShapeDtypeStruct((colours, SLABS, ri...  8.54 us
    ppermute x3, waiting for transfers between devices, from_behind(): lax.ppermute(value, axis, [(source, source + steps) for source in range(l...  8.07 us
    ppermute x2, starting transfers between devices, from_partner(): return lax.ppermute(block, axis, route)  7.08 us
    ppermute x2, starting transfers between devices, halo(): lows.insert(0, lax.ppermute(low, axis, forward))  5.58 us
    ppermute x2, waiting for transfers between devices, halo(): lax.ppermute(lax.slice_in_dim(block, 0, need, axis=dim), axis, backward)  5.19 us
    unnamed x54, local copies, waits for them, and re-layouts  3.91 us
  transfers between devices with their start and end apart: 11, of which 8 were waited for; matrix products, arithmetic and copies ran while one was open for 15% of the time, Pallas kernels for 0%

profile of v10, /device:TPU:16, one launch (start us, length us, event | category | flops | bytes accessed | tf_op | source)
XLA Modules:
  0.0 109.3 jit_solution(5687941615073451314)
XLA Ops:
  0.0 1.0 convert_element_type.39
  1.1 1.1 %pad_maximum_fusion.4 = f32[35,32,128]{2,1,0:T(8,128)S(1)} fusion(f32[3,32,128]{2,1,0:T(8,128)} %param.8, f32[16,32,128]{2,1,0:T(8,128)S(1)} %convert_element_type.39, f32[16,32,128]{2,1,0:T(8,128)} %param.6), kind=kLoop, calls=%fused_computation.17 | loop fusion | flops 286720 | bytes 1146880 | tf_op jit(solution)/shard_map/concatenate | solution.py:186
  2.2 3.5 %collective-permute-start = (f32[35,32,128]{2,1,0:T(8,128)S(1)}, f32[35,32,128]{2,1,0:T(8,128)S(1)}, u32[]{:S(2)}, u32[]{:S(2)}) collective-permute-start(f32[35,32,128]{2,1,0:T(8,128)S(1)} %pad_maximum_fusion.4), channel_id=1, source_target_pairs={{0,1},{2,3},{4,5},{6,7},{8,9},{10,11},{12,13},{14,15},{16,17},{18,... | collective-permute-start | bytes 1720328 | tf_op jit(solution)/shard_map/ppermute | solution.py:84
  5.6 1.3 %collective-permute-start.1 = (f32[35,32,128]{2,1,0:T(8,128)S(1)}, f32[35,32,128]{2,1,0:T(8,128)S(1)}, u32[]{:S(2)}, u32[]{:S(2)}) collective-permute-start(f32[35,32,128]{2,1,0:T(8,128)S(1)} %pad_maximum_fusion.4), channel_id=1, source_target_pairs={{1,0},{3,2},{5,4},{7,6},{9,8},{11,10},{13,12},{15,14},{17,16},{19,... | collective-permute-start | bytes 1720328 | tf_op jit(solution)/shard_map/ppermute | solution.py:85
  7.0 0.6 broadcast_compare_fusion.14
  7.7 0.4 slice_reduce_fusion.15
  8.1 2.6 %select_select_fusion = f32[7,16,32,128]{3,2,1,0:T(8,128)S(1)} fusion(f32[7]{0:T(128)S(1)} %get-tuple-element.10, f32[7]{0:T(128)S(1)} %get-tuple-element.11, f32[7]{0:T(128)S(1)} %get-tuple-element.12, f32[7]{0:T(128)S(1)} %get-tuple-element.13, f32[7]{0:T(128)S(1)} %get-tuple-element.14, f32[7]{0:T(128)S(1)} %get-tuple-element.15, ...), kind=kLoop, calls=%fused_computation.1 | loop fusion | flops 6881280 | bytes 2818496 | tf_op jit(solution)/shard_map/jit(_where)/select_n | solution.py:197
  10.8 0.9 fusion.151
  11.6 0.7 broadcast_multiply_fusion.mask_ref
  12.4 1.0 fusion
  13.3 1.0 slice_multiply_fusion
  14.3 3.5 %collective-permute-done = f32[35,32,128]{2,1,0:T(8,128)S(1)} collective-permute-done((f32[35,32,128]{2,1,0:T(8,128)S(1)}, f32[35,32,128]{2,1,0:T(8,128)S(1)}, u32[]{:S(2)}, u32[]{:S(2)}) %collective-permute-start) | collective-permute-done | bytes 573472 | tf_op jit(solution)/shard_map/ppermute | solution.py:84
  17.8 4.1 %collective-permute-done.1 = f32[35,32,128]{2,1,0:T(8,128)S(1)} collective-permute-done((f32[35,32,128]{2,1,0:T(8,128)S(1)}, f32[35,32,128]{2,1,0:T(8,128)S(1)}, u32[]{:S(2)}, u32[]{:S(2)}) %collective-permute-start.1) | collective-permute-done | bytes 573472 | tf_op jit(solution)/shard_map/ppermute | solution.py:85
  22.1 1.8 %fusion.160 = (f32[35,96,32]{2,1,0:T(8,128)}, f32[35,96,32]{2,1,0:T(8,128)S(1)}) fusion(f32[35,96,128]{2,1,0:T(8,128)S(1)} %pad_maximum_fusion.1), kind=kLoop, calls=%fused_computation.377 | loop fusion | bytes 1720320 | tf_op jit(solution)/shard_map/slice | solution.py:83
  23.9 2.0 %copy.123 = f32[35,96,32]{1,2,0:T(8,128)S(1)} copy(f32[35,96,32]{2,1,0:T(8,128)} %get-tuple-element.47) | data formatting | bytes 860160 | tf_op jit(solution)/shard_map/slice | solution.py:83
  25.9 2.1 %collective-permute-start.2 = (f32[35,96,32]{1,2,0:T(8,128)S(1)}, f32[35,96,32]{1,2,0:T(8,128)}, u32[]{:S(2)}, u32[]{:S(2)}) collective-permute-start(f32[35,96,32]{1,2,0:T(8,128)S(1)} %copy.123), channel_id=1, source_target_pairs={{0,2},{2,4},{4,6},{1,3},{3,5},{5,7},{8,10},{10,12},{12,14},{9,11},... | collective-permute-start | bytes 1290248 | tf_op jit(solution)/shard_map/ppermute | solution.py:84
  28.1 1.4 %copy.124 = f32[35,96,32]{1,2,0:T(8,128)} copy(f32[35,96,32]{2,1,0:T(8,128)S(1)} %get-tuple-element.48) | data formatting | bytes 860160 | tf_op jit(solution)/shard_map/slice | solution.py:85
  29.4 1.5 %collective-permute-start.3 = (f32[35,96,32]{1,2,0:T(8,128)}, f32[35,96,32]{1,2,0:T(8,128)}, u32[]{:S(2)}, u32[]{:S(2)}) collective-permute-start(f32[35,96,32]{1,2,0:T(8,128)} %copy.124), channel_id=1, source_target_pairs={{2,0},{4,2},{6,4},{3,1},{5,3},{7,5},{10,8},{12,10},{14,12},{11,9},... | collective-permute-start | bytes 1290248 | tf_op jit(solution)/shard_map/ppermute | solution.py:85
  31.0 0.9 fusion.165
  31.9 1.6 %copy.125 = f32[35,96,32]{2,1,0:T(8,128)S(1)} copy(f32[35,96,32]{1,2,0:T(8,128)} %collective-permute-done.2) | data formatting | bytes 860160 | tf_op jit(solution)/shard_map/ppermute | solution.py:84
  33.5 1.1 collective-permute-done.3
  34.5 1.6 %copy.126 = f32[35,96,32]{2,1,0:T(8,128)S(1)} copy(f32[35,96,32]{1,2,0:T(8,128)} %collective-permute-done.3) | data formatting | bytes 860160 | tf_op jit(solution)/shard_map/ppermute | solution.py:85
  36.1 2.8 %pad_maximum_fusion = f32[35,96,192]{2,1,0:T(8,128)S(1)} fusion(f32[35,96,32]{2,1,0:T(8,128)S(1)} %copy.126, f32[35,32,128]{2,1,0:T(8,128)} %copy-done.6, f32[3,32,128]{2,1,0:T(8,128)S(1)} %copy-done.15, f32[16,32,128]{2,1,0:T(8,128)} %copy-done.8, f32[16,32,128]{2,1,0:T(8,128)} %param.6, f32[35,32,128]{2,1,0:T(8,128)} %copy-done.4, f32[35,96,32]{2,1,0:T(8,128)S(1)} %copy.125), kind=kLoop, calls=%fused_computation | loop fusion | flops 3870720 | bytes 5160960 | tf_op jit(solution)/shard_map/concatenate | solution.py:86
  38.9 2.0 %fusion.159 = (f32[16,96,192]{2,1,0:T(8,128)}, f32[16,96,192]{2,1,0:T(8,128)}) fusion(f32[35,96,192]{2,1,0:T(8,128)S(1)} %pad_maximum_fusion), kind=kLoop, calls=%fused_computation.376 | loop fusion | bytes 4718592 | tf_op jit(solution)/shard_map/slice | solution.py:189
  40.9 1.1 %slice.1104 = f32[16,36,132]{2,1,0:T(8,128)} slice(f32[35,96,192]{2,1,0:T(8,128)S(1)} %pad_maximum_fusion), slice={[0:16], [30:66], [30:162]} | slice | bytes 608256 | tf_op jit(solution)/shard_map/slice | solution.py:191
  42.1 8.5 %shard_map.64 = f32[3,8,96,192]{3,2,1,0:T(8,128)} custom-call(f32[3,16]{1,0:T(4,128)} %table_ref.1, f32[16,96,192]{2,1,0:T(8,128)} %get-tuple-element.44.density_ref, f32[16,96,192]{2,1,0:T(8,128)} %get-tuple-element.43.labels_ref, f32[96,192]{1,0:T(8,128)} %broadcast_multiply_fusion.mask_ref), custom_call_target="tpu_custom_call" | custom-call | tf_op jit(solution)/shard_map/pallas_call | solution.py:159
  50.6 1.3 %fusion.17 = f32[3,96,192]{2,1,0:T(8,128)S(1)} fusion(f32[3,8,96,192]{3,2,1,0:T(8,128)} %shard_map.64, f32[35,96,32]{2,1,0:T(8,128)S(1)} %copy.126, f32[35,96,32]{2,1,0:T(8,128)S(1)} %copy.125, f32[35,32,128]{2,1,0:T(8,128)} %copy-done.6, f32[35,32,128]{2,1,0:T(8,128)} %copy-done.4, f32[3,32,128]{2,1,0:T(8,128)S(1)} %copy-done.15, ...), kind=kLoop, calls=%fused_computation.43 | loop fusion | flops 387072 | bytes 3022848 | tf_op jit(solution)/shard_map/mul | solution.py:115
  51.9 0.5 copy-done
  52.4 0.4 fusion.13
  52.9 0.4 fusion.9
  53.3 0.4 fusion.5
  53.8 0.4 fusion.30
  54.2 0.4 fusion.26
  54.6 0.4 fusion.22
  55.1 0.4 fusion.18
  55.5 1.0 fusion.56
  56.5 1.6 %fusion.161 = (f32[2,36,132]{2,1,0:T(8,128)}, f32[2,36,132]{2,1,0:T(8,128)}) fusion(f32[16,36,132]{2,1,0:T(8,128)} %slice.1104), kind=kLoop, calls=%fused_computation.378 | loop fusion | bytes 152064 | tf_op jit(solution)/shard_map/slice | solution.py:24
  58.1 3.5 %collective-permute-start.5 = (f32[2,36,132]{2,1,0:T(8,128)}, f32[2,36,132]{2,1,0:T(8,128)}, u32[]{:S(2)}, u32[]{:S(2)}) collective-permute-start(f32[2,36,132]{2,1,0:T(8,128)} %get-tuple-element.52), channel_id=1, source_target_pairs={{0,8},{8,16},{16,24},{1,9},{9,17},{17,25},{2,10},{10,18},{18,26},{... | collective-permute-start | bytes 114056 | tf_op jit(solution)/shard_map/ppermute | solution.py:21
  61.7 2.5 %collective-permute-start.4 = (f32[2,36,132]{2,1,0:T(8,128)}, f32[2,36,132]{2,1,0:T(8,128)S(1)}, u32[]{:S(2)}, u32[]{:S(2)}) collective-permute-start(f32[2,36,132]{2,1,0:T(8,128)} %get-tuple-element.51), channel_id=1, source_target_pairs={{8,0},{16,8},{24,16},{9,1},{17,9},{25,17},{10,2},{18,10},{26,18},{... | collective-permute-start | bytes 114056 | tf_op jit(solution)/shard_map/ppermute | solution.py:24
  64.1 3.5 %collective-permute-start.6 = (f32[3,80,176]{2,1,0:T(8,128)}, f32[3,80,176]{2,1,0:T(8,128)S(1)}, u32[]{:S(2)}, u32[]{:S(2)}) collective-permute-start(f32[3,80,176]{2,1,0:T(8,128)} %fusion.56), channel_id=1, source_target_pairs={{0,8},{8,16},{16,24},{1,9},{9,17},{17,25},{2,10},{10,18},{18,26},{... | collective-permute-start | bytes 506888 | tf_op jit(solution)/shard_map/ppermute | solution.py:32
  67.6 0.9 constant_dynamic-update-slice_fusion.2
  68.5 1.1 %constant_dynamic-update-slice_fusion.1 = f32[20,36,132]{2,1,0:T(8,128)S(1)} fusion(f32[20,36,132]{2,1,0:T(8,128)S(1)} %constant_dynamic-update-slice_fusion.2, f32[16,36,132]{2,1,0:T(8,128)} %slice.1104), kind=kLoop, calls=%fused_computation.327 | loop fusion | bytes 959488
  69.7 3.6 %collective-permute-done.6 = f32[3,80,176]{2,1,0:T(8,128)S(1)} collective-permute-done((f32[3,80,176]{2,1,0:T(8,128)}, f32[3,80,176]{2,1,0:T(8,128)S(1)}, u32[]{:S(2)}, u32[]{:S(2)}) %collective-permute-start.6) | collective-permute-done | bytes 168992 | tf_op jit(solution)/shard_map/ppermute | solution.py:32
  73.3 1.2 %fusion.53 = f32[3,80,176]{2,1,0:T(8,128)S(1)} fusion(f32[3,8,96,192]{3,2,1,0:T(8,128)} %shard_map.64, f32[3,80,176]{2,1,0:T(8,128)S(1)} %collective-permute-done.6, f32[35,96,32]{2,1,0:T(8,128)S(1)} %copy.126, f32[35,96,32]{2,1,0:T(8,128)S(1)} %copy.125, f32[35,32,128]{2,1,0:T(8,128)S(1)} %copy-done.7, f32[35,32,128]{2,1,0:T(8,128)S(1)} %copy-done.5, ...), kind=kLoop, calls=%fused_computation.124 | loop fusion | flops 337920 | bytes 3087361 | tf_op jit(solution)/shard_map/mul | solution.py:115
  74.6 0.4 fusion.49
  74.9 0.4 fusion.45
  75.3 0.4 fusion.41
  75.7 0.4 fusion.69
  76.1 0.4 fusion.65
  76.5 0.4 fusion.61
  76.8 0.4 fusion.57
  77.5 3.8 %collective-permute-start.7 = (f32[3,64,160]{2,1,0:T(8,128)S(1)}, f32[3,64,160]{2,1,0:T(8,128)S(1)}, u32[]{:S(2)}, u32[]{:S(2)}) collective-permute-start(f32[3,64,160]{2,1,0:T(8,128)S(1)} %fusion.88), channel_id=1, source_target_pairs={{0,8},{8,16},{16,24},{1,9},{9,17},{17,25},{2,10},{10,18},{18,26},{... | collective-permute-start | bytes 368648 | tf_op jit(solution)/shard_map/ppermute | solution.py:32
  81.3 2.0 %multiply_multiply_fusion.1 = (f32[18,34,130]{2,1,0:T(8,128)S(1)}, f32[18,34,130]{2,1,0:T(8,128)S(1)}) fusion(f32[16,36,132]{2,1,0:T(8,128)S(1)} %copy-done.12, f32[2,36,132]{2,1,0:T(8,128)} %collective-permute-done.5, f32[2,36,132]{2,1,0:T(8,128)S(1)} %collective-permute-done.4, f32[130]{0:T(256)S(1)} %and_convert_fusion, ...), kind=kLoop, calls=%fused_computation.6 | loop fusion | flops 1750320 | bytes 2292568 | tf_op jit(solution)/shard_map/mul | solution.py:63
  83.4 1.8 %collective-permute-done.7 = f32[3,64,160]{2,1,0:T(8,128)S(1)} collective-permute-done((f32[3,64,160]{2,1,0:T(8,128)S(1)}, f32[3,64,160]{2,1,0:T(8,128)S(1)}, u32[]{:S(2)}, u32[]{:S(2)}) %collective-permute-start.7) | collective-permute-done | bytes 122912 | tf_op jit(solution)/shard_map/ppermute | solution.py:32
  87.8 3.5 %collective-permute-start.8 = (f32[3,48,144]{2,1,0:T(8,128)S(1)}, f32[3,48,144]{2,1,0:T(8,128)S(1)}, u32[]{:S(2)}, u32[]{:S(2)}) collective-permute-start(f32[3,48,144]{2,1,0:T(8,128)S(1)} %fusion.120), channel_id=1, source_target_pairs={{0,8},{8,16},{16,24},{1,9},{9,17},{17,25},{2,10},{10,18},{18,26},{... | collective-permute-start | bytes 248840 | tf_op jit(solution)/shard_map/ppermute | solution.py:32
  91.3 0.9 fusion.37
  92.2 2.7 %collective-permute-done.8 = f32[3,48,144]{2,1,0:T(8,128)S(1)} collective-permute-done((f32[3,48,144]{2,1,0:T(8,128)S(1)}, f32[3,48,144]{2,1,0:T(8,128)S(1)}, u32[]{:S(2)}, u32[]{:S(2)}) %collective-permute-start.8) | collective-permute-done | bytes 82976 | tf_op jit(solution)/shard_map/ppermute | solution.py:32
  97.6 0.4 copy-done.11
  98.3 0.5 fusion.3
  98.9 2.8 %collective-permute-start.9 = (f32[4,2,128]{2,1,0:T(2,128)S(1)}, f32[4,2,128]{2,1,0:T(2,128)S(1)}, u32[]{:S(2)}, u32[]{:S(2)}) collective-permute-start(f32[4,2,128]{2,1,0:T(2,128)S(1)} %bitcast.280), channel_id=1, source_target_pairs={{0,2},{2,0},{4,6},{6,4},{1,3},{3,1},{5,7},{7,5},{8,10},{10,8},{12,... | collective-permute-start | bytes 12296 | tf_op jit(solution)/shard_map/ppermute | solution.py:42
  101.8 0.8 collective-permute-done.9
  102.6 4.3 %collective-permute-start.10 = (f32[4,1,128]{2,0,1:T(4,128)S(1)}, f32[4,1,128]{2,0,1:T(4,128)S(1)}, u32[]{:S(2)}, u32[]{:S(2)}) collective-permute-start(f32[4,1,128]{2,0,1:T(4,128)S(1)} %bitcast.281), channel_id=1, source_target_pairs={{0,4},{4,0},{2,6},{6,2},{1,5},{5,1},{3,7},{7,3},{8,12},{12,8},{10,... | collective-permute-start | bytes 6152 | tf_op jit(solution)/shard_map/ppermute | solution.py:42
  106.9 1.6 %collective-permute-done.10 = f32[4,1,128]{2,0,1:T(4,128)S(1)} collective-permute-done((f32[4,1,128]{2,0,1:T(4,128)S(1)}, f32[4,1,128]{2,0,1:T(4,128)S(1)}, u32[]{:S(2)}, u32[]{:S(2)}) %collective-permute-start.10) | collective-permute-done | bytes 2080 | tf_op jit(solution)/shard_map/ppermute | solution.py:42
  108.7 0.6 pad_maximum_fusion.5
  (101 shorter events, 6.6 us)
Async XLA Ops:
  0.0 7.0 %copy-start.18 = (s32[16,32,128]{2,1,0:T(8,128)S(1)}, s32[16,32,128]{2,1,0:T(8,128)}, u32[]{:S(2)}) copy-start(s32[16,32,128]{2,1,0:T(8,128)} %param.7) | copy-start | bytes 786436
  0.0 7.7 %copy-start.19 = (f32[3,16]{1,0:T(4,128)S(1)}, f32[3,16]{1,0:T(4,128)}, u32[]{:S(2)}) copy-start(f32[3,16]{1,0:T(4,128)} %table_ref.1) | copy-start | bytes 580
  0.0 7.7 %copy-start.21 = (f32[16]{0:T(128)S(1)}, f32[16]{0:T(128)}, u32[]{:S(2)}) copy-start(f32[16]{0:T(128)} %param.9) | copy-start | bytes 196
  0.0 7.7 %copy-start.20 = (f32[3,16]{1,0:T(4,128)S(1)}, f32[3,16]{1,0:T(4,128)}, u32[]{:S(2)}) copy-start(f32[3,16]{1,0:T(4,128)} %param.11) | copy-start | bytes 580
  1.0 20.9 %copy-start.8 = (f32[16,32,128]{2,1,0:T(8,128)}, f32[16,32,128]{2,1,0:T(8,128)S(1)}, u32[]{:S(2)}) copy-start(f32[16,32,128]{2,1,0:T(8,128)S(1)} %convert_element_type.39) | copy-start | bytes 786436
  2.2 15.6 %collective-permute-start = (f32[35,32,128]{2,1,0:T(8,128)S(1)}, f32[35,32,128]{2,1,0:T(8,128)S(1)}, u32[]{:S(2)}, u32[]{:S(2)}) collective-permute-start(f32[35,32,128]{2,1,0:T(8,128)S(1)} %pad_maximum_fusion.4), channel_id=1, source_target_pairs={{0,1},{2,3},{4,5},{6,7},{8,9},{10,11},{12,13},{14,15},{16,17},{18,... | collective-permute-start | bytes 1720328 | tf_op jit(solution)/shard_map/ppermute | solution.py:84
  5.6 16.3 %collective-permute-start.1 = (f32[35,32,128]{2,1,0:T(8,128)S(1)}, f32[35,32,128]{2,1,0:T(8,128)S(1)}, u32[]{:S(2)}, u32[]{:S(2)}) collective-permute-start(f32[35,32,128]{2,1,0:T(8,128)S(1)} %pad_maximum_fusion.4), channel_id=1, source_target_pairs={{1,0},{3,2},{5,4},{7,6},{9,8},{11,10},{13,12},{15,14},{17,16},{19,... | collective-permute-start | bytes 1720328 | tf_op jit(solution)/shard_map/ppermute | solution.py:85
  7.0 3.8 %copy-start.2 = (f32[16,32,128]{2,1,0:T(8,128)S(1)}, f32[16,32,128]{2,1,0:T(8,128)}, u32[]{:S(2)}) copy-start(f32[16,32,128]{2,1,0:T(8,128)} %param.6) | copy-start | bytes 786436
  10.7 7.1 %copy-start.10 = (f32[7,16,32,128]{3,2,1,0:T(8,128)}, f32[7,16,32,128]{3,2,1,0:T(8,128)S(1)}, u32[]{:S(2)}) copy-start(f32[7,16,32,128]{3,2,1,0:T(8,128)S(1)} %select_select_fusion) | copy-start | bytes 5505028
  10.8 11.2 %copy-start.15 = (f32[3,32,128]{2,1,0:T(8,128)S(1)}, f32[3,32,128]{2,1,0:T(8,128)}, u32[]{:S(2)}) copy-start(f32[3,32,128]{2,1,0:T(8,128)} %param.8) | copy-start | bytes 147460
  17.8 6.1 %copy-start.4 = (f32[35,32,128]{2,1,0:T(8,128)}, f32[35,32,128]{2,1,0:T(8,128)S(1)}, u32[]{:S(2)}) copy-start(f32[35,32,128]{2,1,0:T(8,128)S(1)} %collective-permute-done) | copy-start | bytes 1720324
  22.0 1.9 %copy-start.6 = (f32[35,32,128]{2,1,0:T(8,128)}, f32[35,32,128]{2,1,0:T(8,128)S(1)}, u32[]{:S(2)}) copy-start(f32[35,32,128]{2,1,0:T(8,128)S(1)} %collective-permute-done.1) | copy-start | bytes 1720324
  23.9 7.0 %copy-start.14 = (f32[3,16,32,128]{3,2,1,0:T(8,128)S(1)}, f32[3,16,32,128]{3,2,1,0:T(8,128)}, u32[]{:S(2)}) copy-start(f32[3,16,32,128]{3,2,1,0:T(8,128)} %slice_multiply_fusion) | copy-start | bytes 2359300
  25.9 6.0 %collective-permute-start.2 = (f32[35,96,32]{1,2,0:T(8,128)S(1)}, f32[35,96,32]{1,2,0:T(8,128)}, u32[]{:S(2)}, u32[]{:S(2)}) collective-permute-start(f32[35,96,32]{1,2,0:T(8,128)S(1)} %copy.123), channel_id=1, source_target_pairs={{0,2},{2,4},{4,6},{1,3},{3,5},{5,7},{8,10},{10,12},{12,14},{9,11},... | collective-permute-start | bytes 1290248 | tf_op jit(solution)/shard_map/ppermute | solution.py:84
  29.4 5.1 %collective-permute-start.3 = (f32[35,96,32]{1,2,0:T(8,128)}, f32[35,96,32]{1,2,0:T(8,128)}, u32[]{:S(2)}, u32[]{:S(2)}) collective-permute-start(f32[35,96,32]{1,2,0:T(8,128)} %copy.124), channel_id=1, source_target_pairs={{2,0},{4,2},{6,4},{3,1},{5,3},{7,5},{10,8},{12,10},{14,12},{11,9},... | collective-permute-start | bytes 1290248 | tf_op jit(solution)/shard_map/ppermute | solution.py:85
  50.6 1.8 %copy-start = (f32[3,8,96,192]{3,2,1,0:T(8,128)S(1)}, f32[3,8,96,192]{3,2,1,0:T(8,128)}, u32[]{:S(2)}) copy-start(f32[3,8,96,192]{3,2,1,0:T(8,128)} %shard_map.64) | copy-start | bytes 5308420
  58.1 9.6 %collective-permute-start.5 = (f32[2,36,132]{2,1,0:T(8,128)}, f32[2,36,132]{2,1,0:T(8,128)}, u32[]{:S(2)}, u32[]{:S(2)}) collective-permute-start(f32[2,36,132]{2,1,0:T(8,128)} %get-tuple-element.52), channel_id=1, source_target_pairs={{0,8},{8,16},{16,24},{1,9},{9,17},{17,25},{2,10},{10,18},{18,26},{... | collective-permute-start | bytes 114056 | tf_op jit(solution)/shard_map/ppermute | solution.py:21
  61.7 11.7 %copy-start.5 = (f32[35,32,128]{2,1,0:T(8,128)S(1)}, f32[35,32,128]{2,1,0:T(8,128)}, u32[]{:S(2)}) copy-start(f32[35,32,128]{2,1,0:T(8,128)} %copy-done.4) | copy-start | bytes 1720324
  61.7 11.7 %copy-start.7 = (f32[35,32,128]{2,1,0:T(8,128)S(1)}, f32[35,32,128]{2,1,0:T(8,128)}, u32[]{:S(2)}) copy-start(f32[35,32,128]{2,1,0:T(8,128)} %copy-done.6) | copy-start | bytes 1720324
  61.7 8.0 %collective-permute-start.4 = (f32[2,36,132]{2,1,0:T(8,128)}, f32[2,36,132]{2,1,0:T(8,128)S(1)}, u32[]{:S(2)}, u32[]{:S(2)}) collective-permute-start(f32[2,36,132]{2,1,0:T(8,128)} %get-tuple-element.51), channel_id=1, source_target_pairs={{8,0},{16,8},{24,16},{9,1},{17,9},{25,17},{10,2},{18,10},{26,18},{... | collective-permute-start | bytes 114056 | tf_op jit(solution)/shard_map/ppermute | solution.py:24
  64.1 9.2 %collective-permute-start.6 = (f32[3,80,176]{2,1,0:T(8,128)}, f32[3,80,176]{2,1,0:T(8,128)S(1)}, u32[]{:S(2)}, u32[]{:S(2)}) collective-permute-start(f32[3,80,176]{2,1,0:T(8,128)} %fusion.56), channel_id=1, source_target_pairs={{0,8},{8,16},{16,24},{1,9},{9,17},{17,25},{2,10},{10,18},{18,26},{... | collective-permute-start | bytes 506888 | tf_op jit(solution)/shard_map/ppermute | solution.py:32
  69.7 4.8 %copy-start.1 = (f32[3,8,96,192]{3,2,1,0:T(8,128)S(1)}, f32[3,8,96,192]{3,2,1,0:T(8,128)}, u32[]{:S(2)}) copy-start(f32[3,8,96,192]{3,2,1,0:T(8,128)} %shard_map.64) | copy-start | bytes 5308420
  76.4 4.9 %copy-start.12 = (f32[16,36,132]{2,1,0:T(8,128)S(1)}, f32[16,36,132]{2,1,0:T(8,128)}, u32[]{:S(2)}) copy-start(f32[16,36,132]{2,1,0:T(8,128)} %slice.1104) | copy-start | bytes 912388
  77.5 7.7 %copy-start.3 = (f32[16,32,128]{2,1,0:T(8,128)S(1)}, f32[16,32,128]{2,1,0:T(8,128)}, u32[]{:S(2)}) copy-start(f32[16,32,128]{2,1,0:T(8,128)} %param.6) | copy-start | bytes 786436
  77.5 7.7 %copy-start.9 = (f32[16,32,128]{2,1,0:T(8,128)S(1)}, f32[16,32,128]{2,1,0:T(8,128)}, u32[]{:S(2)}) copy-start(f32[16,32,128]{2,1,0:T(8,128)} %copy-done.8) | copy-start | bytes 786436
  77.5 7.7 %collective-permute-start.7 = (f32[3,64,160]{2,1,0:T(8,128)S(1)}, f32[3,64,160]{2,1,0:T(8,128)S(1)}, u32[]{:S(2)}, u32[]{:S(2)}) collective-permute-start(f32[3,64,160]{2,1,0:T(8,128)S(1)} %fusion.88), channel_id=1, source_target_pairs={{0,8},{8,16},{16,24},{1,9},{9,17},{17,25},{2,10},{10,18},{18,26},{... | collective-permute-start | bytes 368648 | tf_op jit(solution)/shard_map/ppermute | solution.py:32
  87.8 7.0 %collective-permute-start.8 = (f32[3,48,144]{2,1,0:T(8,128)S(1)}, f32[3,48,144]{2,1,0:T(8,128)S(1)}, u32[]{:S(2)}, u32[]{:S(2)}) collective-permute-start(f32[3,48,144]{2,1,0:T(8,128)S(1)} %fusion.120), channel_id=1, source_target_pairs={{0,8},{8,16},{16,24},{1,9},{9,17},{17,25},{2,10},{10,18},{18,26},{... | collective-permute-start | bytes 248840 | tf_op jit(solution)/shard_map/ppermute | solution.py:32
  96.5 1.5 %copy-start.11 = (f32[7,16,32,128]{3,2,1,0:T(8,128)S(1)}, f32[7,16,32,128]{3,2,1,0:T(8,128)}, u32[]{:S(2)}) copy-start(f32[7,16,32,128]{3,2,1,0:T(8,128)} %copy-done.10) | copy-start | bytes 5505028
  96.5 1.7 %copy-start.13 = (f32[3,8,2,32,128]{4,3,2,1,0:T(8,128)S(1)}, f32[3,8,2,32,128]{4,3,2,1,0:T(8,128)}, u32[]{:S(2)}) copy-start(f32[3,8,2,32,128]{4,3,2,1,0:T(8,128)} %fusion.165) | copy-start | bytes 2359300
  96.5 1.7 %copy-start.16 = (f32[16,32,128]{2,1,0:T(8,128)S(1)}, f32[16,32,128]{2,1,0:T(8,128)}, u32[]{:S(2)}) copy-start(f32[16,32,128]{2,1,0:T(8,128)} %get-tuple-element.46) | copy-start | bytes 786436
  96.5 1.8 %copy-start.17 = (f32[16,32,128]{2,1,0:T(8,128)S(1)}, f32[16,32,128]{2,1,0:T(8,128)}, u32[]{:S(2)}) copy-start(f32[16,32,128]{2,1,0:T(8,128)} %fusion) | copy-start | bytes 786436
  98.9 3.6 %collective-permute-start.9 = (f32[4,2,128]{2,1,0:T(2,128)S(1)}, f32[4,2,128]{2,1,0:T(2,128)S(1)}, u32[]{:S(2)}, u32[]{:S(2)}) collective-permute-start(f32[4,2,128]{2,1,0:T(2,128)S(1)} %bitcast.280), channel_id=1, source_target_pairs={{0,2},{2,0},{4,6},{6,4},{1,3},{3,1},{5,7},{7,5},{8,10},{10,8},{12,... | collective-permute-start | bytes 12296 | tf_op jit(solution)/shard_map/ppermute | solution.py:42
  102.6 5.8 %collective-permute-start.10 = (f32[4,1,128]{2,0,1:T(4,128)S(1)}, f32[4,1,128]{2,0,1:T(4,128)S(1)}, u32[]{:S(2)}, u32[]{:S(2)}) collective-permute-start(f32[4,1,128]{2,0,1:T(4,128)S(1)} %bitcast.281), channel_id=1, source_target_pairs={{0,4},{4,0},{2,6},{6,2},{1,5},{5,1},{3,7},{7,3},{8,12},{12,8},{10,... | collective-permute-start | bytes 6152 | tf_op jit(solution)/shard_map/ppermute | solution.py:42

commit v11 on v10

--- a/solution.py
+++ b/solution.py
@@ -74,6 +74,20 @@
     count = lax.axis_size(axis)
     size = block.shape[dim]
     lows, highs = [], []
+    if count == 2:
+        need = min(size, width)
+        first = lax.axis_index(axis) == 0
+        send = block
+        if need < size:
+            send = jnp.where(
+                first,
+                lax.slice_in_dim(block, size - need, None, axis=dim),
+                lax.slice_in_dim(block, 0, need, axis=dim),
+            )
+        got = lax.ppermute(send, axis, [(0, 1), (1, 0)])
+        lows = [jnp.where(first, jnp.zeros_like(got), got)]
+        highs = [jnp.where(first, got, jnp.zeros_like(got))]
+        count = 0
     for hop in range(1, count):
         need = min(size, width - (hop - 1) * size)
         if need <= 0:
@@ -240,22 +254,12 @@
     image_now = jnp.concatenate(
         [colour_sum.reshape(3, n_view, piece_len), transmit.reshape(1, n_view, piece_len)], axis=0
     )
-    bit_count = n_view.bit_length() - 1
-    for bit_num in range(bit_count):
-        kept = image_now.shape[1]
-        pairs = image_now.reshape(4, kept // 2, 2, piece_len)
-        my_bit = view_idx // 2**bit_num % 2
-        first_half = my_bit == 0
-        keep = jnp.where(first_half, pairs[:, :, 0], pairs[:, :, 1])
-        send = jnp.where(first_half, pairs[:, :, 1], pairs[:, :, 0])
-        got = from_partner(send, "view", bit_num)
-        front = jnp.where(first_half, keep, got)
-        back = jnp.where(first_half, got, keep)
-        image_now = jnp.concatenate(
-            [front[:3] + front[3:] * back[:3], keep[3:] * got[3:]], axis=0
-        )
-    final_colour = image_now[:3, 0]
-    final_transmit = image_now[3:, 0]
+    segments = lax.all_to_all(image_now, "view", 1, 1, tiled=True)
+    final_colour = segments[:3, n_view - 1]
+    final_transmit = segments[3:, n_view - 1]
+    for segment in range(n_view - 2, -1, -1):
+        final_colour = segments[:3, segment] + segments[3:, segment] * final_colour
+        final_transmit = segments[3:, segment] * final_transmit
     rows_out = brick_l // n_view
     opacity = 1.0 - final_transmit.reshape(1, rows_out, brick_a)
     return jnp.concatenate([final_colour.reshape(3, rows_out, brick_a), opacity], axis=0)

time: 111 us -> 108 us (0.973)
  blocking collectives: 0 us -> 12.3 us
  starting transfers between devices: 32.2 us -> 21.2 us
  waiting for transfers between devices: 19.2 us -> 16.8 us
  local copies, waits for them, and re-layouts: 18.1 us -> 16 us
    all_to_all x0 -> x1, blocking collectives: none -> 12.3 us  [shards(): segments = lax.all_to_all(image_now, 'view', 1, 1, tiled=True)]
    ppermute x2 -> x1, starting transfers between devices: 7.08 us -> 1.58 us  [halo(): got = lax.ppermute(send, axis, [(0, 1), (1, 0)])]
    ppermute x2 -> x1, starting transfers between devices: 5.58 us -> 1.44 us  [halo(): lows.insert(0, lax.ppermute(low, axis, forward))]
    ppermute x2 -> x1, waiting for transfers between devices: 3.52 us -> 0.01 us  [halo(): lows.insert(0, lax.ppermute(low, axis, forward))]
    ppermute x2 -> x1, waiting for transfers between devices: 2.39 us -> 5.87 us  [halo(): got = lax.ppermute(send, axis, [(0, 1), (1, 0)])]
    ppermute x2 -> x1, waiting for transfers between devices: 5.19 us -> 2.89 us  [halo(): lax.ppermute(lax.slice_in_dim(block, 0, need, axis=dim), axis, backward)]
    slice x2, local copies, waits for them, and re-layouts: 3.83 us -> 1.94 us  [halo(): low = lax.slice_in_dim(block, size - need, None, axis=dim)]
    ppermute x2 -> x1, starting transfers between devices: 2.75 us -> 1.46 us  [halo(): lax.ppermute(lax.slice_in_dim(block, 0, need, axis=dim), axis, backward)]
  transfers between devices with their start and end apart: 11 -> 8, of which waited for: 8 -> 5; matrix products, arithmetic and copies ran while one was open for 15% -> 14% of each run, Pallas kernels for 0% -> 0%
where the time goes in v11:
time: 108 us; the launch traced here: 106 us
  other arithmetic  29.8 us (28%)
  starting transfers between devices  21.2 us (20%)
  waiting for transfers between devices  16.8 us (16%)
  local copies, waits for them, and re-layouts  16 us (15%)
  blocking collectives  12.3 us (11%)
  Pallas kernels  8.54 us (8%)
    all_to_all x1, blocking collectives, shards(): segments = lax.all_to_all(image_now, 'view', 1, 1, tiled=True)  12.3 us
    mul x31, other arithmetic, propagate(): current = current * fade_here  12.1 us
    ppermute x3, starting transfers between devices, from_behind(): lax.ppermute(value, axis, [(source, source + steps) for source in range(l...  10.8 us
    pallas_call x1, Pallas kernels, fade_rim_of(): pl.pallas_call(kernel, out_shape=jax.ShapeDtypeStruct((colours, SLABS, ri...  8.54 us
    ppermute x3, waiting for transfers between devices, from_behind(): lax.ppermute(value, axis, [(source, source + steps) for source in range(l...  8.07 us
    ppermute x1, waiting for transfers between devices, halo(): got = lax.ppermute(send, axis, [(0, 1), (1, 0)])  5.87 us
    unnamed x53, local copies, waits for them, and re-layouts  4.22 us
    ppermute x1, starting transfers between devices, padded_2(): lax.ppermute(lax.slice_in_dim(block, block.shape[dim] - width, None, axis...  3.47 us
  transfers between devices with their start and end apart: 8, of which 5 were waited for; matrix products, arithmetic and copies ran while one was open for 14% of the time, Pallas kernels for 0%

profile of v11, /device:TPU:16, one launch (start us, length us, event | category | flops | bytes accessed | tf_op | source)
XLA Modules:
  0.0 106.3 jit_solution(16166012239739582796)
XLA Ops:
  0.0 1.0 convert_element_type.39
  1.1 1.1 %pad_maximum_fusion.4 = f32[35,32,128]{2,1,0:T(8,128)S(1)} fusion(f32[3,32,128]{2,1,0:T(8,128)} %param.8, f32[16,32,128]{2,1,0:T(8,128)S(1)} %convert_element_type.39, f32[16,32,128]{2,1,0:T(8,128)} %param.6), kind=kLoop, calls=%fused_computation.17 | loop fusion | flops 286720 | bytes 1146880 | tf_op jit(solution)/shard_map/concatenate | solution.py:200
  2.2 1.6 %collective-permute-start = (f32[35,32,128]{2,1,0:T(8,128)S(1)}, f32[35,32,128]{2,1,0:T(8,128)S(1)}, u32[]{:S(2)}, u32[]{:S(2)}) collective-permute-start(f32[35,32,128]{2,1,0:T(8,128)S(1)} %pad_maximum_fusion.4), channel_id=1, source_target_pairs={{0,1},{1,0},{2,3},{3,2},{4,5},{5,4},{6,7},{7,6},{8,9},{9,8},{10,11... | collective-permute-start | bytes 1720328 | tf_op jit(solution)/shard_map/ppermute | solution.py:87
  3.8 0.6 broadcast_compare_fusion.14
  4.5 0.4 slice_reduce_fusion.15
  4.9 2.6 %select_select_fusion = f32[7,16,32,128]{3,2,1,0:T(8,128)S(1)} fusion(f32[7]{0:T(128)S(1)} %get-tuple-element.14, f32[7]{0:T(128)S(1)} %get-tuple-element.15, f32[7]{0:T(128)S(1)} %get-tuple-element.16, f32[7]{0:T(128)S(1)} %get-tuple-element.17, f32[7]{0:T(128)S(1)} %get-tuple-element.18, f32[7]{0:T(128)S(1)} %get-tuple-element.19, ...), kind=kLoop, calls=%fused_computation.1 | loop fusion | flops 6881280 | bytes 2818496 | tf_op jit(solution)/shard_map/jit(_where)/select_n | solution.py:211
  7.5 0.9 exponential_subtract_fusion
  8.4 0.7 broadcast_multiply_fusion.mask_ref
  9.1 1.0 fusion
  10.1 1.0 slice_multiply_fusion
  11.1 5.9 %collective-permute-done = f32[35,32,128]{2,1,0:T(8,128)S(1)} collective-permute-done((f32[35,32,128]{2,1,0:T(8,128)S(1)}, f32[35,32,128]{2,1,0:T(8,128)S(1)}, u32[]{:S(2)}, u32[]{:S(2)}) %collective-permute-start) | collective-permute-done | bytes 573472 | tf_op jit(solution)/shard_map/ppermute | solution.py:87
  17.3 0.6 fusion.158
  18.2 1.3 %copy.107 = f32[35,96,32]{1,2,0:T(8,128)} copy(f32[35,96,32]{2,1,0:T(8,128)S(1)} %get-tuple-element.47) | data formatting | bytes 860160 | tf_op jit(solution)/shard_map/slice | solution.py:97
  19.5 1.4 %collective-permute-start.1 = (f32[35,96,32]{1,2,0:T(8,128)}, f32[35,96,32]{1,2,0:T(8,128)S(1)}, u32[]{:S(2)}, u32[]{:S(2)}) collective-permute-start(f32[35,96,32]{1,2,0:T(8,128)} %copy.107), channel_id=1, source_target_pairs={{0,2},{2,4},{4,6},{1,3},{3,5},{5,7},{8,10},{10,12},{12,14},{9,11},... | collective-permute-start | bytes 1290248 | tf_op jit(solution)/shard_map/ppermute | solution.py:98
  21.0 1.4 %copy.108 = f32[35,96,32]{1,2,0:T(8,128)} copy(f32[35,96,32]{2,1,0:T(8,128)S(1)} %get-tuple-element.48) | data formatting | bytes 860160 | tf_op jit(solution)/shard_map/slice | solution.py:99
  22.4 1.5 %collective-permute-start.2 = (f32[35,96,32]{1,2,0:T(8,128)}, f32[35,96,32]{1,2,0:T(8,128)}, u32[]{:S(2)}, u32[]{:S(2)}) collective-permute-start(f32[35,96,32]{1,2,0:T(8,128)} %copy.108), channel_id=1, source_target_pairs={{2,0},{4,2},{6,4},{3,1},{5,3},{7,5},{10,8},{12,10},{14,12},{11,9},... | collective-permute-start | bytes 1290248 | tf_op jit(solution)/shard_map/ppermute | solution.py:99
  23.9 0.9 fusion.162
  24.8 0.5 copy.109
  25.4 2.9 %collective-permute-done.2 = f32[35,96,32]{1,2,0:T(8,128)} collective-permute-done((f32[35,96,32]{1,2,0:T(8,128)}, f32[35,96,32]{1,2,0:T(8,128)}, u32[]{:S(2)}, u32[]{:S(2)}) %collective-permute-start.2) | collective-permute-done | bytes 430112 | tf_op jit(solution)/shard_map/ppermute | solution.py:99
  28.3 1.6 %copy.110 = f32[35,96,32]{2,1,0:T(8,128)S(1)} copy(f32[35,96,32]{1,2,0:T(8,128)} %collective-permute-done.2) | data formatting | bytes 860160 | tf_op jit(solution)/shard_map/ppermute | solution.py:99
  29.8 2.8 %pad_maximum_fusion = f32[35,96,192]{2,1,0:T(8,128)S(1)} fusion(f32[35,96,32]{2,1,0:T(8,128)S(1)} %copy.110, f32[35,32,128]{2,1,0:T(8,128)} %copy-done.6, f32[3,32,128]{2,1,0:T(8,128)S(1)} %copy-done.15, f32[16,32,128]{2,1,0:T(8,128)} %copy-done.8, f32[16,32,128]{2,1,0:T(8,128)} %param.6, f32[35,32,128]{2,1,0:T(8,128)} %copy-done.4, f32[35,96,32]{2,1,0:T(8,128)S(1)} %copy.109), kind=kLoop, calls=%fused_computation | loop fusion | flops 3870720 | bytes 5160960 | tf_op jit(solution)/shard_map/concatenate | solution.py:100
  32.6 2.0 %fusion.157 = (f32[16,96,192]{2,1,0:T(8,128)}, f32[16,96,192]{2,1,0:T(8,128)}) fusion(f32[35,96,192]{2,1,0:T(8,128)S(1)} %pad_maximum_fusion), kind=kLoop, calls=%fused_computation.366 | loop fusion | bytes 4718592 | tf_op jit(solution)/shard_map/slice | solution.py:203
  34.7 1.1 %slice.1071 = f32[16,36,132]{2,1,0:T(8,128)} slice(f32[35,96,192]{2,1,0:T(8,128)S(1)} %pad_maximum_fusion), slice={[0:16], [30:66], [30:162]} | slice | bytes 608256 | tf_op jit(solution)/shard_map/slice | solution.py:205
  35.8 8.5 %shard_map.64 = f32[3,8,96,192]{3,2,1,0:T(8,128)} custom-call(f32[3,16]{1,0:T(4,128)} %table_ref.1, f32[16,96,192]{2,1,0:T(8,128)} %get-tuple-element.44.density_ref, f32[16,96,192]{2,1,0:T(8,128)} %get-tuple-element.43.labels_ref, f32[96,192]{1,0:T(8,128)} %broadcast_multiply_fusion.mask_ref), custom_call_target="tpu_custom_call" | custom-call | tf_op jit(solution)/shard_map/pallas_call | solution.py:173
  44.4 1.3 %fusion.17 = f32[3,96,192]{2,1,0:T(8,128)S(1)} fusion(f32[3,8,96,192]{3,2,1,0:T(8,128)} %shard_map.64, f32[35,96,32]{2,1,0:T(8,128)S(1)} %copy.110, f32[35,96,32]{2,1,0:T(8,128)S(1)} %copy.109, f32[35,32,128]{2,1,0:T(8,128)} %copy-done.6, f32[35,32,128]{2,1,0:T(8,128)} %copy-done.4, f32[3,32,128]{2,1,0:T(8,128)S(1)} %copy-done.15, ...), kind=kLoop, calls=%fused_computation.43 | loop fusion | flops 387072 | bytes 3022848 | tf_op jit(solution)/shard_map/mul | solution.py:129
  45.7 0.5 copy-done
  46.2 0.4 fusion.13
  46.6 0.4 fusion.9
  47.1 0.4 fusion.5
  47.5 0.4 fusion.30
  47.9 0.4 fusion.26
  48.3 0.4 fusion.22
  48.8 0.4 fusion.18
  49.2 1.0 fusion.56
  50.2 1.6 %fusion.159 = (f32[2,36,132]{2,1,0:T(8,128)}, f32[2,36,132]{2,1,0:T(8,128)}) fusion(f32[16,36,132]{2,1,0:T(8,128)} %slice.1071), kind=kLoop, calls=%fused_computation.368 | loop fusion | bytes 152064 | tf_op jit(solution)/shard_map/slice | solution.py:24
  51.8 3.5 %collective-permute-start.4 = (f32[2,36,132]{2,1,0:T(8,128)}, f32[2,36,132]{2,1,0:T(8,128)}, u32[]{:S(2)}, u32[]{:S(2)}) collective-permute-start(f32[2,36,132]{2,1,0:T(8,128)} %get-tuple-element.52), channel_id=1, source_target_pairs={{0,8},{8,16},{16,24},{1,9},{9,17},{17,25},{2,10},{10,18},{18,26},{... | collective-permute-start | bytes 114056 | tf_op jit(solution)/shard_map/ppermute | solution.py:21
  55.4 2.5 %collective-permute-start.3 = (f32[2,36,132]{2,1,0:T(8,128)}, f32[2,36,132]{2,1,0:T(8,128)S(1)}, u32[]{:S(2)}, u32[]{:S(2)}) collective-permute-start(f32[2,36,132]{2,1,0:T(8,128)} %get-tuple-element.51), channel_id=1, source_target_pairs={{8,0},{16,8},{24,16},{9,1},{17,9},{25,17},{10,2},{18,10},{26,18},{... | collective-permute-start | bytes 114056 | tf_op jit(solution)/shard_map/ppermute | solution.py:24
  57.9 3.5 %collective-permute-start.5 = (f32[3,80,176]{2,1,0:T(8,128)}, f32[3,80,176]{2,1,0:T(8,128)S(1)}, u32[]{:S(2)}, u32[]{:S(2)}) collective-permute-start(f32[3,80,176]{2,1,0:T(8,128)} %fusion.56), channel_id=1, source_target_pairs={{0,8},{8,16},{16,24},{1,9},{9,17},{17,25},{2,10},{10,18},{18,26},{... | collective-permute-start | bytes 506888 | tf_op jit(solution)/shard_map/ppermute | solution.py:32
  61.4 0.9 constant_dynamic-update-slice_fusion.2
  62.3 1.1 %constant_dynamic-update-slice_fusion.1 = f32[20,36,132]{2,1,0:T(8,128)S(1)} fusion(f32[20,36,132]{2,1,0:T(8,128)S(1)} %constant_dynamic-update-slice_fusion.2, f32[16,36,132]{2,1,0:T(8,128)} %slice.1071), kind=kLoop, calls=%fused_computation.329 | loop fusion | bytes 959488
  63.4 3.6 %collective-permute-done.5 = f32[3,80,176]{2,1,0:T(8,128)S(1)} collective-permute-done((f32[3,80,176]{2,1,0:T(8,128)}, f32[3,80,176]{2,1,0:T(8,128)S(1)}, u32[]{:S(2)}, u32[]{:S(2)}) %collective-permute-start.5) | collective-permute-done | bytes 168992 | tf_op jit(solution)/shard_map/ppermute | solution.py:32
  67.0 1.2 %fusion.53 = f32[3,80,176]{2,1,0:T(8,128)S(1)} fusion(f32[3,8,96,192]{3,2,1,0:T(8,128)} %shard_map.64, f32[3,80,176]{2,1,0:T(8,128)S(1)} %collective-permute-done.5, f32[35,96,32]{2,1,0:T(8,128)S(1)} %copy.110, f32[35,96,32]{2,1,0:T(8,128)S(1)} %copy.109, f32[35,32,128]{2,1,0:T(8,128)S(1)} %copy-done.7, f32[35,32,128]{2,1,0:T(8,128)S(1)} %copy-done.5, ...), kind=kLoop, calls=%fused_computation.126 | loop fusion | flops 337920 | bytes 3087361 | tf_op jit(solution)/shard_map/mul | solution.py:129
  68.3 0.4 fusion.49
  68.7 0.4 fusion.45
  69.0 0.4 fusion.41
  69.4 0.4 fusion.69
  69.8 0.4 fusion.65
  70.2 0.4 fusion.61
  70.5 0.4 fusion.57
  71.2 3.8 %collective-permute-start.6 = (f32[3,64,160]{2,1,0:T(8,128)S(1)}, f32[3,64,160]{2,1,0:T(8,128)S(1)}, u32[]{:S(2)}, u32[]{:S(2)}) collective-permute-start(f32[3,64,160]{2,1,0:T(8,128)S(1)} %fusion.88), channel_id=1, source_target_pairs={{0,8},{8,16},{16,24},{1,9},{9,17},{17,25},{2,10},{10,18},{18,26},{... | collective-permute-start | bytes 368648 | tf_op jit(solution)/shard_map/ppermute | solution.py:32
  75.0 2.0 %multiply_multiply_fusion.1 = (f32[18,34,130]{2,1,0:T(8,128)S(1)}, f32[18,34,130]{2,1,0:T(8,128)S(1)}) fusion(f32[16,36,132]{2,1,0:T(8,128)S(1)} %copy-done.12, f32[2,36,132]{2,1,0:T(8,128)} %collective-permute-done.4, f32[2,36,132]{2,1,0:T(8,128)S(1)} %collective-permute-done.3, f32[130]{0:T(256)S(1)} %and_convert_fusion, ...), kind=kLoop, calls=%fused_computation.6 | loop fusion | flops 1750320 | bytes 2292568 | tf_op jit(solution)/shard_map/mul | solution.py:63
  77.1 1.8 %collective-permute-done.6 = f32[3,64,160]{2,1,0:T(8,128)S(1)} collective-permute-done((f32[3,64,160]{2,1,0:T(8,128)S(1)}, f32[3,64,160]{2,1,0:T(8,128)S(1)}, u32[]{:S(2)}, u32[]{:S(2)}) %collective-permute-start.6) | collective-permute-done | bytes 122912 | tf_op jit(solution)/shard_map/ppermute | solution.py:32
  79.1 0.3 fusion.81
  79.4 0.3 fusion.77
  79.8 0.3 fusion.73
  80.4 0.3 fusion.97
  80.7 0.3 fusion.93
  81.5 3.5 %collective-permute-start.7 = (f32[3,48,144]{2,1,0:T(8,128)S(1)}, f32[3,48,144]{2,1,0:T(8,128)S(1)}, u32[]{:S(2)}, u32[]{:S(2)}) collective-permute-start(f32[3,48,144]{2,1,0:T(8,128)S(1)} %fusion.120), channel_id=1, source_target_pairs={{0,8},{8,16},{16,24},{1,9},{9,17},{17,25},{2,10},{10,18},{18,26},{... | collective-permute-start | bytes 248840 | tf_op jit(solution)/shard_map/ppermute | solution.py:32
  85.0 0.9 fusion.37
  85.9 2.7 %collective-permute-done.7 = f32[3,48,144]{2,1,0:T(8,128)S(1)} collective-permute-done((f32[3,48,144]{2,1,0:T(8,128)S(1)}, f32[3,48,144]{2,1,0:T(8,128)S(1)}, u32[]{:S(2)}, u32[]{:S(2)}) %collective-permute-start.7) | collective-permute-done | bytes 82976 | tf_op jit(solution)/shard_map/ppermute | solution.py:32
  91.3 0.4 copy-done.11
  92.0 0.5 fusion.3
  92.6 12.3 %all_to_all.5 = f32[4,4,128]{2,0,1:T(4,128)S(1)} all-to-all(f32[4,4,128]{2,0,1:T(4,128)S(1)} %copy.143), channel_id=1, replica_groups=mesh['light'=4,'view'=4,'across'=2] {'view'}, dimensions={1} | all-to-all | bytes 16384 | tf_op jit(solution)/shard_map/all_to_all | solution.py:257
  105.7 0.6 pad_maximum_fusion.6
  (94 shorter events, 5.9 us)
Async XLA Ops:
  0.0 3.8 %copy-start.18 = (s32[16,32,128]{2,1,0:T(8,128)S(1)}, s32[16,32,128]{2,1,0:T(8,128)}, u32[]{:S(2)}) copy-start(s32[16,32,128]{2,1,0:T(8,128)} %param.7) | copy-start | bytes 786436
  0.0 4.5 %copy-start.19 = (f32[3,16]{1,0:T(4,128)S(1)}, f32[3,16]{1,0:T(4,128)}, u32[]{:S(2)}) copy-start(f32[3,16]{1,0:T(4,128)} %table_ref.1) | copy-start | bytes 580
  0.0 4.5 %copy-start.21 = (f32[16]{0:T(128)S(1)}, f32[16]{0:T(128)}, u32[]{:S(2)}) copy-start(f32[16]{0:T(128)} %param.9) | copy-start | bytes 196
  0.0 4.5 %copy-start.20 = (f32[3,16]{1,0:T(4,128)S(1)}, f32[3,16]{1,0:T(4,128)}, u32[]{:S(2)}) copy-start(f32[3,16]{1,0:T(4,128)} %param.11) | copy-start | bytes 580
  1.0 16.1 %copy-start.8 = (f32[16,32,128]{2,1,0:T(8,128)}, f32[16,32,128]{2,1,0:T(8,128)S(1)}, u32[]{:S(2)}) copy-start(f32[16,32,128]{2,1,0:T(8,128)S(1)} %convert_element_type.39) | copy-start | bytes 786436
  2.2 14.8 %collective-permute-start = (f32[35,32,128]{2,1,0:T(8,128)S(1)}, f32[35,32,128]{2,1,0:T(8,128)S(1)}, u32[]{:S(2)}, u32[]{:S(2)}) collective-permute-start(f32[35,32,128]{2,1,0:T(8,128)S(1)} %pad_maximum_fusion.4), channel_id=1, source_target_pairs={{0,1},{1,0},{2,3},{3,2},{4,5},{5,4},{6,7},{7,6},{8,9},{9,8},{10,11... | collective-permute-start | bytes 1720328 | tf_op jit(solution)/shard_map/ppermute | solution.py:87
  3.8 3.8 %copy-start.2 = (f32[16,32,128]{2,1,0:T(8,128)S(1)}, f32[16,32,128]{2,1,0:T(8,128)}, u32[]{:S(2)}) copy-start(f32[16,32,128]{2,1,0:T(8,128)} %param.6) | copy-start | bytes 786436
  7.5 9.6 %copy-start.10 = (f32[7,16,32,128]{3,2,1,0:T(8,128)}, f32[7,16,32,128]{3,2,1,0:T(8,128)S(1)}, u32[]{:S(2)}) copy-start(f32[7,16,32,128]{3,2,1,0:T(8,128)S(1)} %select_select_fusion) | copy-start | bytes 5505028
  10.1 7.0 %copy-start.15 = (f32[3,32,128]{2,1,0:T(8,128)S(1)}, f32[3,32,128]{2,1,0:T(8,128)}, u32[]{:S(2)}) copy-start(f32[3,32,128]{2,1,0:T(8,128)} %param.8) | copy-start | bytes 147460
  17.1 0.8 copy-start.4
  17.1 1.1 %copy-start.6 = (f32[35,32,128]{2,1,0:T(8,128)}, f32[35,32,128]{2,1,0:T(8,128)S(1)}, u32[]{:S(2)}) copy-start(f32[35,32,128]{2,1,0:T(8,128)S(1)} %get-tuple-element.54) | copy-start | bytes 1720324
  19.5 4.4 %copy-start.14 = (f32[3,16,32,128]{3,2,1,0:T(8,128)S(1)}, f32[3,16,32,128]{3,2,1,0:T(8,128)}, u32[]{:S(2)}) copy-start(f32[3,16,32,128]{3,2,1,0:T(8,128)} %slice_multiply_fusion) | copy-start | bytes 2359300
  19.5 5.3 %collective-permute-start.1 = (f32[35,96,32]{1,2,0:T(8,128)}, f32[35,96,32]{1,2,0:T(8,128)S(1)}, u32[]{:S(2)}, u32[]{:S(2)}) collective-permute-start(f32[35,96,32]{1,2,0:T(8,128)} %copy.107), channel_id=1, source_target_pairs={{0,2},{2,4},{4,6},{1,3},{3,5},{5,7},{8,10},{10,12},{12,14},{9,11},... | collective-permute-start | bytes 1290248 | tf_op jit(solution)/shard_map/ppermute | solution.py:98
  22.4 5.9 %collective-permute-start.2 = (f32[35,96,32]{1,2,0:T(8,128)}, f32[35,96,32]{1,2,0:T(8,128)}, u32[]{:S(2)}, u32[]{:S(2)}) collective-permute-start(f32[35,96,32]{1,2,0:T(8,128)} %copy.108), channel_id=1, source_target_pairs={{2,0},{4,2},{6,4},{3,1},{5,3},{7,5},{10,8},{12,10},{14,12},{11,9},... | collective-permute-start | bytes 1290248 | tf_op jit(solution)/shard_map/ppermute | solution.py:99
  44.4 1.8 %copy-start = (f32[3,8,96,192]{3,2,1,0:T(8,128)S(1)}, f32[3,8,96,192]{3,2,1,0:T(8,128)}, u32[]{:S(2)}) copy-start(f32[3,8,96,192]{3,2,1,0:T(8,128)} %shard_map.64) | copy-start | bytes 5308420
  51.8 9.6 %collective-permute-start.4 = (f32[2,36,132]{2,1,0:T(8,128)}, f32[2,36,132]{2,1,0:T(8,128)}, u32[]{:S(2)}, u32[]{:S(2)}) collective-permute-start(f32[2,36,132]{2,1,0:T(8,128)} %get-tuple-element.52), channel_id=1, source_target_pairs={{0,8},{8,16},{16,24},{1,9},{9,17},{17,25},{2,10},{10,18},{18,26},{... | collective-permute-start | bytes 114056 | tf_op jit(solution)/shard_map/ppermute | solution.py:21
  55.4 11.7 %copy-start.5 = (f32[35,32,128]{2,1,0:T(8,128)S(1)}, f32[35,32,128]{2,1,0:T(8,128)}, u32[]{:S(2)}) copy-start(f32[35,32,128]{2,1,0:T(8,128)} %copy-done.4) | copy-start | bytes 1720324
  55.4 11.7 %copy-start.7 = (f32[35,32,128]{2,1,0:T(8,128)S(1)}, f32[35,32,128]{2,1,0:T(8,128)}, u32[]{:S(2)}) copy-start(f32[35,32,128]{2,1,0:T(8,128)} %copy-done.6) | copy-start | bytes 1720324
  55.4 8.0 %collective-permute-start.3 = (f32[2,36,132]{2,1,0:T(8,128)}, f32[2,36,132]{2,1,0:T(8,128)S(1)}, u32[]{:S(2)}, u32[]{:S(2)}) collective-permute-start(f32[2,36,132]{2,1,0:T(8,128)} %get-tuple-element.51), channel_id=1, source_target_pairs={{8,0},{16,8},{24,16},{9,1},{17,9},{25,17},{10,2},{18,10},{26,18},{... | collective-permute-start | bytes 114056 | tf_op jit(solution)/shard_map/ppermute | solution.py:24
  57.9 9.2 %collective-permute-start.5 = (f32[3,80,176]{2,1,0:T(8,128)}, f32[3,80,176]{2,1,0:T(8,128)S(1)}, u32[]{:S(2)}, u32[]{:S(2)}) collective-permute-start(f32[3,80,176]{2,1,0:T(8,128)} %fusion.56), channel_id=1, source_target_pairs={{0,8},{8,16},{16,24},{1,9},{9,17},{17,25},{2,10},{10,18},{18,26},{... | collective-permute-start | bytes 506888 | tf_op jit(solution)/shard_map/ppermute | solution.py:32
  63.4 4.8 %copy-start.1 = (f32[3,8,96,192]{3,2,1,0:T(8,128)S(1)}, f32[3,8,96,192]{3,2,1,0:T(8,128)}, u32[]{:S(2)}) copy-start(f32[3,8,96,192]{3,2,1,0:T(8,128)} %shard_map.64) | copy-start | bytes 5308420
  70.2 4.9 %copy-start.12 = (f32[16,36,132]{2,1,0:T(8,128)S(1)}, f32[16,36,132]{2,1,0:T(8,128)}, u32[]{:S(2)}) copy-start(f32[16,36,132]{2,1,0:T(8,128)} %slice.1071) | copy-start | bytes 912388
  71.2 7.7 %copy-start.3 = (f32[16,32,128]{2,1,0:T(8,128)S(1)}, f32[16,32,128]{2,1,0:T(8,128)}, u32[]{:S(2)}) copy-start(f32[16,32,128]{2,1,0:T(8,128)} %param.6) | copy-start | bytes 786436
  71.2 7.7 %copy-start.9 = (f32[16,32,128]{2,1,0:T(8,128)S(1)}, f32[16,32,128]{2,1,0:T(8,128)}, u32[]{:S(2)}) copy-start(f32[16,32,128]{2,1,0:T(8,128)} %copy-done.8) | copy-start | bytes 786436
  71.2 7.7 %collective-permute-start.6 = (f32[3,64,160]{2,1,0:T(8,128)S(1)}, f32[3,64,160]{2,1,0:T(8,128)S(1)}, u32[]{:S(2)}, u32[]{:S(2)}) collective-permute-start(f32[3,64,160]{2,1,0:T(8,128)S(1)} %fusion.88), channel_id=1, source_target_pairs={{0,8},{8,16},{16,24},{1,9},{9,17},{17,25},{2,10},{10,18},{18,26},{... | collective-permute-start | bytes 368648 | tf_op jit(solution)/shard_map/ppermute | solution.py:32
  81.5 7.0 %collective-permute-start.7 = (f32[3,48,144]{2,1,0:T(8,128)S(1)}, f32[3,48,144]{2,1,0:T(8,128)S(1)}, u32[]{:S(2)}, u32[]{:S(2)}) collective-permute-start(f32[3,48,144]{2,1,0:T(8,128)S(1)} %fusion.120), channel_id=1, source_target_pairs={{0,8},{8,16},{16,24},{1,9},{9,17},{17,25},{2,10},{10,18},{18,26},{... | collective-permute-start | bytes 248840 | tf_op jit(solution)/shard_map/ppermute | solution.py:32
  90.2 1.5 %copy-start.11 = (f32[7,16,32,128]{3,2,1,0:T(8,128)S(1)}, f32[7,16,32,128]{3,2,1,0:T(8,128)}, u32[]{:S(2)}) copy-start(f32[7,16,32,128]{3,2,1,0:T(8,128)} %copy-done.10) | copy-start | bytes 5505028
  90.2 1.7 %copy-start.13 = (f32[3,8,2,32,128]{4,3,2,1,0:T(8,128)S(1)}, f32[3,8,2,32,128]{4,3,2,1,0:T(8,128)}, u32[]{:S(2)}) copy-start(f32[3,8,2,32,128]{4,3,2,1,0:T(8,128)} %fusion.162) | copy-start | bytes 2359300
  90.2 1.7 %copy-start.16 = (f32[16,32,128]{2,1,0:T(8,128)S(1)}, f32[16,32,128]{2,1,0:T(8,128)}, u32[]{:S(2)}) copy-start(f32[16,32,128]{2,1,0:T(8,128)} %get-tuple-element.45) | copy-start | bytes 786436
  90.3 1.8 %copy-start.17 = (f32[16,32,128]{2,1,0:T(8,128)S(1)}, f32[16,32,128]{2,1,0:T(8,128)}, u32[]{:S(2)}) copy-start(f32[16,32,128]{2,1,0:T(8,128)} %fusion) | copy-start | bytes 786436

commit v12 on v10

--- a/solution.py
+++ b/solution.py
@@ -74,6 +74,20 @@
     count = lax.axis_size(axis)
     size = block.shape[dim]
     lows, highs = [], []
+    if count == 2:
+        need = min(size, width)
+        first = lax.axis_index(axis) == 0
+        send = block
+        if need < size:
+            send = jnp.where(
+                first,
+                lax.slice_in_dim(block, size - need, None, axis=dim),
+                lax.slice_in_dim(block, 0, need, axis=dim),
+            )
+        got = lax.ppermute(send, axis, [(0, 1), (1, 0)])
+        lows = [jnp.where(first, jnp.zeros_like(got), got)]
+        highs = [jnp.where(first, got, jnp.zeros_like(got))]
+        count = 0
     for hop in range(1, count):
         need = min(size, width - (hop - 1) * size)
         if need <= 0:

time: 111 us -> 106 us (0.955)
  starting transfers between devices: 32.2 us -> 29.2 us
  local copies, waits for them, and re-layouts: 18.1 us -> 15.5 us
    ppermute x0 -> x1, waiting for transfers between devices: none -> 5.87 us  [halo(): got = lax.ppermute(send, axis, [(0, 1), (1, 0)])]
    ppermute x2 -> x1, starting transfers between devices: 5.58 us -> 1.44 us  [halo(): lows.insert(0, lax.ppermute(low, axis, forward))]
    ppermute x2 -> x1, waiting for transfers between devices: 3.52 us -> 0.01 us  [halo(): lows.insert(0, lax.ppermute(low, axis, forward))]
    ppermute x2 -> x1, waiting for transfers between devices: 5.19 us -> 2.89 us  [halo(): lax.ppermute(lax.slice_in_dim(block, 0, need, axis=dim), axis, backward)]
    slice x2, local copies, waits for them, and re-layouts: 3.83 us -> 1.94 us  [halo(): low = lax.slice_in_dim(block, size - need, None, axis=dim)]
    ppermute x0 -> x1, starting transfers between devices: none -> 1.58 us  [halo(): got = lax.ppermute(send, axis, [(0, 1), (1, 0)])]
    ppermute x2 -> x1, starting transfers between devices: 2.75 us -> 1.46 us  [halo(): lax.ppermute(lax.slice_in_dim(block, 0, need, axis=dim), axis, backward)]
  transfers between devices with their start and end apart: 11 -> 10, of which waited for: 8 -> 7; matrix products, arithmetic and copies ran while one was open for 15% -> 15% of each run, Pallas kernels for 0% -> 0%
where the time goes in v12:
time: 106 us; the launch traced here: 104 us
  other arithmetic  29.8 us (28%)
  starting transfers between devices  29.2 us (28%)
  waiting for transfers between devices  19.2 us (18%)
  local copies, waits for them, and re-layouts  15.5 us (15%)
  Pallas kernels  8.54 us (8%)
    mul x31, other arithmetic, propagate(): current = current * fade_here  12.1 us
    ppermute x3, starting transfers between devices, from_behind(): lax.ppermute(value, axis, [(source, source + steps) for source in range(l...  10.8 us
    pallas_call x1, Pallas kernels, fade_rim_of(): pl.pallas_call(kernel, out_shape=jax.ShapeDtypeStruct((colours, SLABS, ri...  8.54 us
    ppermute x3, waiting for transfers between devices, from_behind(): lax.ppermute(value, axis, [(source, source + steps) for source in range(l...  8.07 us
    ppermute x2, starting transfers between devices, from_partner(): return lax.ppermute(block, axis, route)  7.92 us
    ppermute x1, waiting for transfers between devices, halo(): got = lax.ppermute(send, axis, [(0, 1), (1, 0)])  5.87 us
    unnamed x54, local copies, waits for them, and re-layouts  4.22 us
    ppermute x1, starting transfers between devices, padded_2(): lax.ppermute(lax.slice_in_dim(block, block.shape[dim] - width, None, axis...  3.47 us
  transfers between devices with their start and end apart: 10, of which 7 were waited for; matrix products, arithmetic and copies ran while one was open for 15% of the time, Pallas kernels for 0%

profile of v12, /device:TPU:16, one launch (start us, length us, event | category | flops | bytes accessed | tf_op | source)
XLA Modules:
  0.0 103.9 jit_solution(16560571399573038006)
XLA Ops:
  0.0 1.0 convert_element_type.39
  1.1 1.1 %pad_maximum_fusion.4 = f32[35,32,128]{2,1,0:T(8,128)S(1)} fusion(f32[3,32,128]{2,1,0:T(8,128)} %param.8, f32[16,32,128]{2,1,0:T(8,128)S(1)} %convert_element_type.39, f32[16,32,128]{2,1,0:T(8,128)} %param.6), kind=kLoop, calls=%fused_computation.17 | loop fusion | flops 286720 | bytes 1146880 | tf_op jit(solution)/shard_map/concatenate | solution.py:200
  2.2 1.6 %collective-permute-start = (f32[35,32,128]{2,1,0:T(8,128)S(1)}, f32[35,32,128]{2,1,0:T(8,128)S(1)}, u32[]{:S(2)}, u32[]{:S(2)}) collective-permute-start(f32[35,32,128]{2,1,0:T(8,128)S(1)} %pad_maximum_fusion.4), channel_id=1, source_target_pairs={{0,1},{1,0},{2,3},{3,2},{4,5},{5,4},{6,7},{7,6},{8,9},{9,8},{10,11... | collective-permute-start | bytes 1720328 | tf_op jit(solution)/shard_map/ppermute | solution.py:87
  3.8 0.6 broadcast_compare_fusion.14
  4.5 0.4 slice_reduce_fusion.15
  4.9 2.6 %select_select_fusion = f32[7,16,32,128]{3,2,1,0:T(8,128)S(1)} fusion(f32[7]{0:T(128)S(1)} %get-tuple-element.10, f32[7]{0:T(128)S(1)} %get-tuple-element.11, f32[7]{0:T(128)S(1)} %get-tuple-element.12, f32[7]{0:T(128)S(1)} %get-tuple-element.13, f32[7]{0:T(128)S(1)} %get-tuple-element.14, f32[7]{0:T(128)S(1)} %get-tuple-element.15, ...), kind=kLoop, calls=%fused_computation.1 | loop fusion | flops 6881280 | bytes 2818496 | tf_op jit(solution)/shard_map/jit(_where)/select_n | solution.py:211
  7.5 0.9 fusion.151
  8.4 0.7 broadcast_multiply_fusion.mask_ref
  9.1 1.0 fusion
  10.1 1.0 slice_multiply_fusion
  11.1 5.9 %collective-permute-done = f32[35,32,128]{2,1,0:T(8,128)S(1)} collective-permute-done((f32[35,32,128]{2,1,0:T(8,128)S(1)}, f32[35,32,128]{2,1,0:T(8,128)S(1)}, u32[]{:S(2)}, u32[]{:S(2)}) %collective-permute-start) | collective-permute-done | bytes 573472 | tf_op jit(solution)/shard_map/ppermute | solution.py:87
  17.3 0.6 fusion.160
  18.2 1.3 %copy.123 = f32[35,96,32]{1,2,0:T(8,128)} copy(f32[35,96,32]{2,1,0:T(8,128)S(1)} %get-tuple-element.47) | data formatting | bytes 860160 | tf_op jit(solution)/shard_map/slice | solution.py:97
  19.5 1.4 %collective-permute-start.1 = (f32[35,96,32]{1,2,0:T(8,128)}, f32[35,96,32]{1,2,0:T(8,128)S(1)}, u32[]{:S(2)}, u32[]{:S(2)}) collective-permute-start(f32[35,96,32]{1,2,0:T(8,128)} %copy.123), channel_id=1, source_target_pairs={{0,2},{2,4},{4,6},{1,3},{3,5},{5,7},{8,10},{10,12},{12,14},{9,11},... | collective-permute-start | bytes 1290248 | tf_op jit(solution)/shard_map/ppermute | solution.py:98
  21.0 1.4 %copy.124 = f32[35,96,32]{1,2,0:T(8,128)} copy(f32[35,96,32]{2,1,0:T(8,128)S(1)} %get-tuple-element.48) | data formatting | bytes 860160 | tf_op jit(solution)/shard_map/slice | solution.py:99
  22.4 1.5 %collective-permute-start.2 = (f32[35,96,32]{1,2,0:T(8,128)}, f32[35,96,32]{1,2,0:T(8,128)}, u32[]{:S(2)}, u32[]{:S(2)}) collective-permute-start(f32[35,96,32]{1,2,0:T(8,128)} %copy.124), channel_id=1, source_target_pairs={{2,0},{4,2},{6,4},{3,1},{5,3},{7,5},{10,8},{12,10},{14,12},{11,9},... | collective-permute-start | bytes 1290248 | tf_op jit(solution)/shard_map/ppermute | solution.py:99
  23.9 0.9 fusion.165
  24.8 0.5 copy.125
  25.4 2.9 %collective-permute-done.2 = f32[35,96,32]{1,2,0:T(8,128)} collective-permute-done((f32[35,96,32]{1,2,0:T(8,128)}, f32[35,96,32]{1,2,0:T(8,128)}, u32[]{:S(2)}, u32[]{:S(2)}) %collective-permute-start.2) | collective-permute-done | bytes 430112 | tf_op jit(solution)/shard_map/ppermute | solution.py:99
  28.3 1.6 %copy.126 = f32[35,96,32]{2,1,0:T(8,128)S(1)} copy(f32[35,96,32]{1,2,0:T(8,128)} %collective-permute-done.2) | data formatting | bytes 860160 | tf_op jit(solution)/shard_map/ppermute | solution.py:99
  29.8 2.8 %pad_maximum_fusion = f32[35,96,192]{2,1,0:T(8,128)S(1)} fusion(f32[35,96,32]{2,1,0:T(8,128)S(1)} %copy.126, f32[35,32,128]{2,1,0:T(8,128)} %copy-done.6, f32[3,32,128]{2,1,0:T(8,128)S(1)} %copy-done.15, f32[16,32,128]{2,1,0:T(8,128)} %copy-done.8, f32[16,32,128]{2,1,0:T(8,128)} %param.6, f32[35,32,128]{2,1,0:T(8,128)} %copy-done.4, f32[35,96,32]{2,1,0:T(8,128)S(1)} %copy.125), kind=kLoop, calls=%fused_computation | loop fusion | flops 3870720 | bytes 5160960 | tf_op jit(solution)/shard_map/concatenate | solution.py:100
  32.6 2.0 %fusion.159 = (f32[16,96,192]{2,1,0:T(8,128)}, f32[16,96,192]{2,1,0:T(8,128)}) fusion(f32[35,96,192]{2,1,0:T(8,128)S(1)} %pad_maximum_fusion), kind=kLoop, calls=%fused_computation.378 | loop fusion | bytes 4718592 | tf_op jit(solution)/shard_map/slice | solution.py:203
  34.7 1.1 %slice.1104 = f32[16,36,132]{2,1,0:T(8,128)} slice(f32[35,96,192]{2,1,0:T(8,128)S(1)} %pad_maximum_fusion), slice={[0:16], [30:66], [30:162]} | slice | bytes 608256 | tf_op jit(solution)/shard_map/slice | solution.py:205
  35.8 8.5 %shard_map.64 = f32[3,8,96,192]{3,2,1,0:T(8,128)} custom-call(f32[3,16]{1,0:T(4,128)} %table_ref.1, f32[16,96,192]{2,1,0:T(8,128)} %get-tuple-element.44.density_ref, f32[16,96,192]{2,1,0:T(8,128)} %get-tuple-element.43.labels_ref, f32[96,192]{1,0:T(8,128)} %broadcast_multiply_fusion.mask_ref), custom_call_target="tpu_custom_call" | custom-call | tf_op jit(solution)/shard_map/pallas_call | solution.py:173
  44.4 1.3 %fusion.17 = f32[3,96,192]{2,1,0:T(8,128)S(1)} fusion(f32[3,8,96,192]{3,2,1,0:T(8,128)} %shard_map.64, f32[35,96,32]{2,1,0:T(8,128)S(1)} %copy.126, f32[35,96,32]{2,1,0:T(8,128)S(1)} %copy.125, f32[35,32,128]{2,1,0:T(8,128)} %copy-done.6, f32[35,32,128]{2,1,0:T(8,128)} %copy-done.4, f32[3,32,128]{2,1,0:T(8,128)S(1)} %copy-done.15, ...), kind=kLoop, calls=%fused_computation.43 | loop fusion | flops 387072 | bytes 3022848 | tf_op jit(solution)/shard_map/mul | solution.py:129
  45.7 0.5 copy-done
  46.2 0.4 fusion.13
  46.6 0.4 fusion.9
  47.1 0.4 fusion.5
  47.5 0.4 fusion.30
  47.9 0.4 fusion.26
  48.3 0.4 fusion.22
  48.8 0.4 fusion.18
  49.2 1.0 fusion.56
  50.2 1.6 %fusion.161 = (f32[2,36,132]{2,1,0:T(8,128)}, f32[2,36,132]{2,1,0:T(8,128)}) fusion(f32[16,36,132]{2,1,0:T(8,128)} %slice.1104), kind=kLoop, calls=%fused_computation.380 | loop fusion | bytes 152064 | tf_op jit(solution)/shard_map/slice | solution.py:24
  51.8 3.5 %collective-permute-start.4 = (f32[2,36,132]{2,1,0:T(8,128)}, f32[2,36,132]{2,1,0:T(8,128)}, u32[]{:S(2)}, u32[]{:S(2)}) collective-permute-start(f32[2,36,132]{2,1,0:T(8,128)} %get-tuple-element.52), channel_id=1, source_target_pairs={{0,8},{8,16},{16,24},{1,9},{9,17},{17,25},{2,10},{10,18},{18,26},{... | collective-permute-start | bytes 114056 | tf_op jit(solution)/shard_map/ppermute | solution.py:21
  55.4 2.5 %collective-permute-start.3 = (f32[2,36,132]{2,1,0:T(8,128)}, f32[2,36,132]{2,1,0:T(8,128)S(1)}, u32[]{:S(2)}, u32[]{:S(2)}) collective-permute-start(f32[2,36,132]{2,1,0:T(8,128)} %get-tuple-element.51), channel_id=1, source_target_pairs={{8,0},{16,8},{24,16},{9,1},{17,9},{25,17},{10,2},{18,10},{26,18},{... | collective-permute-start | bytes 114056 | tf_op jit(solution)/shard_map/ppermute | solution.py:24
  57.9 3.5 %collective-permute-start.5 = (f32[3,80,176]{2,1,0:T(8,128)}, f32[3,80,176]{2,1,0:T(8,128)S(1)}, u32[]{:S(2)}, u32[]{:S(2)}) collective-permute-start(f32[3,80,176]{2,1,0:T(8,128)} %fusion.56), channel_id=1, source_target_pairs={{0,8},{8,16},{16,24},{1,9},{9,17},{17,25},{2,10},{10,18},{18,26},{... | collective-permute-start | bytes 506888 | tf_op jit(solution)/shard_map/ppermute | solution.py:32
  61.4 0.9 constant_dynamic-update-slice_fusion.2
  62.3 1.1 %constant_dynamic-update-slice_fusion.1 = f32[20,36,132]{2,1,0:T(8,128)S(1)} fusion(f32[20,36,132]{2,1,0:T(8,128)S(1)} %constant_dynamic-update-slice_fusion.2, f32[16,36,132]{2,1,0:T(8,128)} %slice.1104), kind=kLoop, calls=%fused_computation.329 | loop fusion | bytes 959488
  63.4 3.6 %collective-permute-done.5 = f32[3,80,176]{2,1,0:T(8,128)S(1)} collective-permute-done((f32[3,80,176]{2,1,0:T(8,128)}, f32[3,80,176]{2,1,0:T(8,128)S(1)}, u32[]{:S(2)}, u32[]{:S(2)}) %collective-permute-start.5) | collective-permute-done | bytes 168992 | tf_op jit(solution)/shard_map/ppermute | solution.py:32
  67.0 1.2 %fusion.53 = f32[3,80,176]{2,1,0:T(8,128)S(1)} fusion(f32[3,8,96,192]{3,2,1,0:T(8,128)} %shard_map.64, f32[3,80,176]{2,1,0:T(8,128)S(1)} %collective-permute-done.5, f32[35,96,32]{2,1,0:T(8,128)S(1)} %copy.126, f32[35,96,32]{2,1,0:T(8,128)S(1)} %copy.125, f32[35,32,128]{2,1,0:T(8,128)S(1)} %copy-done.7, f32[35,32,128]{2,1,0:T(8,128)S(1)} %copy-done.5, ...), kind=kLoop, calls=%fused_computation.126 | loop fusion | flops 337920 | bytes 3087361 | tf_op jit(solution)/shard_map/mul | solution.py:129
  68.3 0.4 fusion.49
  68.7 0.4 fusion.45
  69.1 0.4 fusion.41
  69.4 0.4 fusion.69
  69.8 0.4 fusion.65
  70.2 0.4 fusion.61
  70.5 0.4 fusion.57
  71.2 3.8 %collective-permute-start.6 = (f32[3,64,160]{2,1,0:T(8,128)S(1)}, f32[3,64,160]{2,1,0:T(8,128)S(1)}, u32[]{:S(2)}, u32[]{:S(2)}) collective-permute-start(f32[3,64,160]{2,1,0:T(8,128)S(1)} %fusion.88), channel_id=1, source_target_pairs={{0,8},{8,16},{16,24},{1,9},{9,17},{17,25},{2,10},{10,18},{18,26},{... | collective-permute-start | bytes 368648 | tf_op jit(solution)/shard_map/ppermute | solution.py:32
  75.1 2.0 %multiply_multiply_fusion.1 = (f32[18,34,130]{2,1,0:T(8,128)S(1)}, f32[18,34,130]{2,1,0:T(8,128)S(1)}) fusion(f32[16,36,132]{2,1,0:T(8,128)S(1)} %copy-done.12, f32[2,36,132]{2,1,0:T(8,128)} %collective-permute-done.4, f32[2,36,132]{2,1,0:T(8,128)S(1)} %collective-permute-done.3, f32[130]{0:T(256)S(1)} %and_convert_fusion, ...), kind=kLoop, calls=%fused_computation.6 | loop fusion | flops 1750320 | bytes 2292568 | tf_op jit(solution)/shard_map/mul | solution.py:63
  77.1 1.8 %collective-permute-done.6 = f32[3,64,160]{2,1,0:T(8,128)S(1)} collective-permute-done((f32[3,64,160]{2,1,0:T(8,128)S(1)}, f32[3,64,160]{2,1,0:T(8,128)S(1)}, u32[]{:S(2)}, u32[]{:S(2)}) %collective-permute-start.6) | collective-permute-done | bytes 122912 | tf_op jit(solution)/shard_map/ppermute | solution.py:32
  79.1 0.3 fusion.81
  79.5 0.3 fusion.77
  81.5 3.5 %collective-permute-start.7 = (f32[3,48,144]{2,1,0:T(8,128)S(1)}, f32[3,48,144]{2,1,0:T(8,128)S(1)}, u32[]{:S(2)}, u32[]{:S(2)}) collective-permute-start(f32[3,48,144]{2,1,0:T(8,128)S(1)} %fusion.120), channel_id=1, source_target_pairs={{0,8},{8,16},{16,24},{1,9},{9,17},{17,25},{2,10},{10,18},{18,26},{... | collective-permute-start | bytes 248840 | tf_op jit(solution)/shard_map/ppermute | solution.py:32
  85.0 0.9 fusion.37
  85.9 2.7 %collective-permute-done.7 = f32[3,48,144]{2,1,0:T(8,128)S(1)} collective-permute-done((f32[3,48,144]{2,1,0:T(8,128)S(1)}, f32[3,48,144]{2,1,0:T(8,128)S(1)}, u32[]{:S(2)}, u32[]{:S(2)}) %collective-permute-start.7) | collective-permute-done | bytes 82976 | tf_op jit(solution)/shard_map/ppermute | solution.py:32
  91.3 0.4 copy-done.11
  92.0 0.5 fusion.3
  92.7 2.8 %collective-permute-start.8 = (f32[4,2,128]{2,1,0:T(2,128)S(1)}, f32[4,2,128]{2,1,0:T(2,128)S(1)}, u32[]{:S(2)}, u32[]{:S(2)}) collective-permute-start(f32[4,2,128]{2,1,0:T(2,128)S(1)} %bitcast.280), channel_id=1, source_target_pairs={{0,2},{2,0},{4,6},{6,4},{1,3},{3,1},{5,7},{7,5},{8,10},{10,8},{12,... | collective-permute-start | bytes 12296 | tf_op jit(solution)/shard_map/ppermute | solution.py:42
  95.5 0.8 collective-permute-done.8
  96.3 5.1 %collective-permute-start.9 = (f32[4,1,128]{2,0,1:T(4,128)S(1)}, f32[4,1,128]{2,0,1:T(4,128)S(1)}, u32[]{:S(2)}, u32[]{:S(2)}) collective-permute-start(f32[4,1,128]{2,0,1:T(4,128)S(1)} %bitcast.281), channel_id=1, source_target_pairs={{0,4},{4,0},{2,6},{6,2},{1,5},{5,1},{3,7},{7,3},{8,12},{12,8},{10,... | collective-permute-start | bytes 6152 | tf_op jit(solution)/shard_map/ppermute | solution.py:42
  101.5 1.6 %collective-permute-done.9 = f32[4,1,128]{2,0,1:T(4,128)S(1)} collective-permute-done((f32[4,1,128]{2,0,1:T(4,128)S(1)}, f32[4,1,128]{2,0,1:T(4,128)S(1)}, u32[]{:S(2)}, u32[]{:S(2)}) %collective-permute-start.9) | collective-permute-done | bytes 2080 | tf_op jit(solution)/shard_map/ppermute | solution.py:42
  103.3 0.6 pad_maximum_fusion.5
  (100 shorter events, 6.4 us)
Async XLA Ops:
  0.0 3.8 %copy-start.18 = (s32[16,32,128]{2,1,0:T(8,128)S(1)}, s32[16,32,128]{2,1,0:T(8,128)}, u32[]{:S(2)}) copy-start(s32[16,32,128]{2,1,0:T(8,128)} %param.7) | copy-start | bytes 786436
  0.0 4.5 %copy-start.19 = (f32[3,16]{1,0:T(4,128)S(1)}, f32[3,16]{1,0:T(4,128)}, u32[]{:S(2)}) copy-start(f32[3,16]{1,0:T(4,128)} %table_ref.1) | copy-start | bytes 580
  0.0 4.5 %copy-start.21 = (f32[16]{0:T(128)S(1)}, f32[16]{0:T(128)}, u32[]{:S(2)}) copy-start(f32[16]{0:T(128)} %param.9) | copy-start | bytes 196
  0.0 4.5 %copy-start.20 = (f32[3,16]{1,0:T(4,128)S(1)}, f32[3,16]{1,0:T(4,128)}, u32[]{:S(2)}) copy-start(f32[3,16]{1,0:T(4,128)} %param.11) | copy-start | bytes 580
  1.0 16.1 %copy-start.8 = (f32[16,32,128]{2,1,0:T(8,128)}, f32[16,32,128]{2,1,0:T(8,128)S(1)}, u32[]{:S(2)}) copy-start(f32[16,32,128]{2,1,0:T(8,128)S(1)} %convert_element_type.39) | copy-start | bytes 786436
  2.2 14.8 %collective-permute-start = (f32[35,32,128]{2,1,0:T(8,128)S(1)}, f32[35,32,128]{2,1,0:T(8,128)S(1)}, u32[]{:S(2)}, u32[]{:S(2)}) collective-permute-start(f32[35,32,128]{2,1,0:T(8,128)S(1)} %pad_maximum_fusion.4), channel_id=1, source_target_pairs={{0,1},{1,0},{2,3},{3,2},{4,5},{5,4},{6,7},{7,6},{8,9},{9,8},{10,11... | collective-permute-start | bytes 1720328 | tf_op jit(solution)/shard_map/ppermute | solution.py:87
  3.8 3.8 %copy-start.2 = (f32[16,32,128]{2,1,0:T(8,128)S(1)}, f32[16,32,128]{2,1,0:T(8,128)}, u32[]{:S(2)}) copy-start(f32[16,32,128]{2,1,0:T(8,128)} %param.6) | copy-start | bytes 786436
  7.5 9.6 %copy-start.10 = (f32[7,16,32,128]{3,2,1,0:T(8,128)}, f32[7,16,32,128]{3,2,1,0:T(8,128)S(1)}, u32[]{:S(2)}) copy-start(f32[7,16,32,128]{3,2,1,0:T(8,128)S(1)} %select_select_fusion) | copy-start | bytes 5505028
  10.1 7.0 %copy-start.15 = (f32[3,32,128]{2,1,0:T(8,128)S(1)}, f32[3,32,128]{2,1,0:T(8,128)}, u32[]{:S(2)}) copy-start(f32[3,32,128]{2,1,0:T(8,128)} %param.8) | copy-start | bytes 147460
  17.1 0.8 copy-start.4
  17.1 1.1 %copy-start.6 = (f32[35,32,128]{2,1,0:T(8,128)}, f32[35,32,128]{2,1,0:T(8,128)S(1)}, u32[]{:S(2)}) copy-start(f32[35,32,128]{2,1,0:T(8,128)S(1)} %get-tuple-element.54) | copy-start | bytes 1720324
  19.5 4.4 %copy-start.14 = (f32[3,16,32,128]{3,2,1,0:T(8,128)S(1)}, f32[3,16,32,128]{3,2,1,0:T(8,128)}, u32[]{:S(2)}) copy-start(f32[3,16,32,128]{3,2,1,0:T(8,128)} %slice_multiply_fusion) | copy-start | bytes 2359300
  19.5 5.3 %collective-permute-start.1 = (f32[35,96,32]{1,2,0:T(8,128)}, f32[35,96,32]{1,2,0:T(8,128)S(1)}, u32[]{:S(2)}, u32[]{:S(2)}) collective-permute-start(f32[35,96,32]{1,2,0:T(8,128)} %copy.123), channel_id=1, source_target_pairs={{0,2},{2,4},{4,6},{1,3},{3,5},{5,7},{8,10},{10,12},{12,14},{9,11},... | collective-permute-start | bytes 1290248 | tf_op jit(solution)/shard_map/ppermute | solution.py:98
  22.4 5.9 %collective-permute-start.2 = (f32[35,96,32]{1,2,0:T(8,128)}, f32[35,96,32]{1,2,0:T(8,128)}, u32[]{:S(2)}, u32[]{:S(2)}) collective-permute-start(f32[35,96,32]{1,2,0:T(8,128)} %copy.124), channel_id=1, source_target_pairs={{2,0},{4,2},{6,4},{3,1},{5,3},{7,5},{10,8},{12,10},{14,12},{11,9},... | collective-permute-start | bytes 1290248 | tf_op jit(solution)/shard_map/ppermute | solution.py:99
  44.4 1.8 %copy-start = (f32[3,8,96,192]{3,2,1,0:T(8,128)S(1)}, f32[3,8,96,192]{3,2,1,0:T(8,128)}, u32[]{:S(2)}) copy-start(f32[3,8,96,192]{3,2,1,0:T(8,128)} %shard_map.64) | copy-start | bytes 5308420
  51.8 9.6 %collective-permute-start.4 = (f32[2,36,132]{2,1,0:T(8,128)}, f32[2,36,132]{2,1,0:T(8,128)}, u32[]{:S(2)}, u32[]{:S(2)}) collective-permute-start(f32[2,36,132]{2,1,0:T(8,128)} %get-tuple-element.52), channel_id=1, source_target_pairs={{0,8},{8,16},{16,24},{1,9},{9,17},{17,25},{2,10},{10,18},{18,26},{... | collective-permute-start | bytes 114056 | tf_op jit(solution)/shard_map/ppermute | solution.py:21
  55.4 11.7 %copy-start.5 = (f32[35,32,128]{2,1,0:T(8,128)S(1)}, f32[35,32,128]{2,1,0:T(8,128)}, u32[]{:S(2)}) copy-start(f32[35,32,128]{2,1,0:T(8,128)} %copy-done.4) | copy-start | bytes 1720324
  55.4 11.7 %copy-start.7 = (f32[35,32,128]{2,1,0:T(8,128)S(1)}, f32[35,32,128]{2,1,0:T(8,128)}, u32[]{:S(2)}) copy-start(f32[35,32,128]{2,1,0:T(8,128)} %copy-done.6) | copy-start | bytes 1720324
  55.4 8.0 %collective-permute-start.3 = (f32[2,36,132]{2,1,0:T(8,128)}, f32[2,36,132]{2,1,0:T(8,128)S(1)}, u32[]{:S(2)}, u32[]{:S(2)}) collective-permute-start(f32[2,36,132]{2,1,0:T(8,128)} %get-tuple-element.51), channel_id=1, source_target_pairs={{8,0},{16,8},{24,16},{9,1},{17,9},{25,17},{10,2},{18,10},{26,18},{... | collective-permute-start | bytes 114056 | tf_op jit(solution)/shard_map/ppermute | solution.py:24
  57.9 9.2 %collective-permute-start.5 = (f32[3,80,176]{2,1,0:T(8,128)}, f32[3,80,176]{2,1,0:T(8,128)S(1)}, u32[]{:S(2)}, u32[]{:S(2)}) collective-permute-start(f32[3,80,176]{2,1,0:T(8,128)} %fusion.56), channel_id=1, source_target_pairs={{0,8},{8,16},{16,24},{1,9},{9,17},{17,25},{2,10},{10,18},{18,26},{... | collective-permute-start | bytes 506888 | tf_op jit(solution)/shard_map/ppermute | solution.py:32
  63.4 4.8 %copy-start.1 = (f32[3,8,96,192]{3,2,1,0:T(8,128)S(1)}, f32[3,8,96,192]{3,2,1,0:T(8,128)}, u32[]{:S(2)}) copy-start(f32[3,8,96,192]{3,2,1,0:T(8,128)} %shard_map.64) | copy-start | bytes 5308420
  70.2 4.9 %copy-start.12 = (f32[16,36,132]{2,1,0:T(8,128)S(1)}, f32[16,36,132]{2,1,0:T(8,128)}, u32[]{:S(2)}) copy-start(f32[16,36,132]{2,1,0:T(8,128)} %slice.1104) | copy-start | bytes 912388
  71.2 7.7 %copy-start.3 = (f32[16,32,128]{2,1,0:T(8,128)S(1)}, f32[16,32,128]{2,1,0:T(8,128)}, u32[]{:S(2)}) copy-start(f32[16,32,128]{2,1,0:T(8,128)} %param.6) | copy-start | bytes 786436
  71.2 7.7 %copy-start.9 = (f32[16,32,128]{2,1,0:T(8,128)S(1)}, f32[16,32,128]{2,1,0:T(8,128)}, u32[]{:S(2)}) copy-start(f32[16,32,128]{2,1,0:T(8,128)} %copy-done.8) | copy-start | bytes 786436
  71.2 7.7 %collective-permute-start.6 = (f32[3,64,160]{2,1,0:T(8,128)S(1)}, f32[3,64,160]{2,1,0:T(8,128)S(1)}, u32[]{:S(2)}, u32[]{:S(2)}) collective-permute-start(f32[3,64,160]{2,1,0:T(8,128)S(1)} %fusion.88), channel_id=1, source_target_pairs={{0,8},{8,16},{16,24},{1,9},{9,17},{17,25},{2,10},{10,18},{18,26},{... | collective-permute-start | bytes 368648 | tf_op jit(solution)/shard_map/ppermute | solution.py:32
  81.5 7.0 %collective-permute-start.7 = (f32[3,48,144]{2,1,0:T(8,128)S(1)}, f32[3,48,144]{2,1,0:T(8,128)S(1)}, u32[]{:S(2)}, u32[]{:S(2)}) collective-permute-start(f32[3,48,144]{2,1,0:T(8,128)S(1)} %fusion.120), channel_id=1, source_target_pairs={{0,8},{8,16},{16,24},{1,9},{9,17},{17,25},{2,10},{10,18},{18,26},{... | collective-permute-start | bytes 248840 | tf_op jit(solution)/shard_map/ppermute | solution.py:32
  90.2 1.5 %copy-start.11 = (f32[7,16,32,128]{3,2,1,0:T(8,128)S(1)}, f32[7,16,32,128]{3,2,1,0:T(8,128)}, u32[]{:S(2)}) copy-start(f32[7,16,32,128]{3,2,1,0:T(8,128)} %copy-done.10) | copy-start | bytes 5505028
  90.2 1.7 %copy-start.13 = (f32[3,8,2,32,128]{4,3,2,1,0:T(8,128)S(1)}, f32[3,8,2,32,128]{4,3,2,1,0:T(8,128)}, u32[]{:S(2)}) copy-start(f32[3,8,2,32,128]{4,3,2,1,0:T(8,128)} %fusion.165) | copy-start | bytes 2359300
  90.2 1.7 %copy-start.16 = (f32[16,32,128]{2,1,0:T(8,128)S(1)}, f32[16,32,128]{2,1,0:T(8,128)}, u32[]{:S(2)}) copy-start(f32[16,32,128]{2,1,0:T(8,128)} %get-tuple-element.46) | copy-start | bytes 786436
  90.3 1.8 %copy-start.17 = (f32[16,32,128]{2,1,0:T(8,128)S(1)}, f32[16,32,128]{2,1,0:T(8,128)}, u32[]{:S(2)}) copy-start(f32[16,32,128]{2,1,0:T(8,128)} %fusion) | copy-start | bytes 786436
  92.7 3.6 %collective-permute-start.8 = (f32[4,2,128]{2,1,0:T(2,128)S(1)}, f32[4,2,128]{2,1,0:T(2,128)S(1)}, u32[]{:S(2)}, u32[]{:S(2)}) collective-permute-start(f32[4,2,128]{2,1,0:T(2,128)S(1)} %bitcast.280), channel_id=1, source_target_pairs={{0,2},{2,0},{4,6},{6,4},{1,3},{3,1},{5,7},{7,5},{8,10},{10,8},{12,... | collective-permute-start | bytes 12296 | tf_op jit(solution)/shard_map/ppermute | solution.py:42
  96.3 6.7 %collective-permute-start.9 = (f32[4,1,128]{2,0,1:T(4,128)S(1)}, f32[4,1,128]{2,0,1:T(4,128)S(1)}, u32[]{:S(2)}, u32[]{:S(2)}) collective-permute-start(f32[4,1,128]{2,0,1:T(4,128)S(1)} %bitcast.281), channel_id=1, source_target_pairs={{0,4},{4,0},{2,6},{6,2},{1,5},{5,1},{3,7},{7,3},{8,12},{12,8},{10,... | collective-permute-start | bytes 6152 | tf_op jit(solution)/shard_map/ppermute | solution.py:42

commit v13 on v12

--- a/solution.py
+++ b/solution.py
@@ -138,21 +138,21 @@
     return (current, jnp.stack(starts, axis=1))
 
 
-def fade_rim_of(extinction_table, density_rim, labels_rim, mask, light_step):
-    rows, rim_a, rim_v = density_rim.shape
+def fade_rim_of(extinction_table, stack_rim, rows, mask, light_step):
+    _, rim_a, rim_v = stack_rim.shape
     layer_rows = rows // SLABS
     colours, materials = extinction_table.shape
     chunk = 8 if rim_a % 8 == 0 else rim_a
 
-    def kernel(table_ref, density_ref, labels_ref, mask_ref, out_ref):
+    def kernel(table_ref, stack_ref, mask_ref, out_ref):
         def one_slab(slab_num, carry):
             for first in range(0, rim_a, chunk):
                 part = slice(first, first + chunk)
                 depth = [None] * colours
                 for row in range(layer_rows):
                     row_num = slab_num * layer_rows + row
-                    here = labels_ref[row_num, part, :]
-                    cells = density_ref[row_num, part, :]
+                    here = stack_ref[rows + row_num, part, :]
+                    cells = stack_ref[row_num, part, :]
                     looked = [jnp.full(here.shape, table_ref[c, 0]) for c in range(colours)]
                     for material in range(1, materials):
                         match = here == float(material)
@@ -177,10 +177,9 @@
             pl.BlockSpec(memory_space=pltpu.SMEM),
             pl.BlockSpec(memory_space=pltpu.VMEM),
             pl.BlockSpec(memory_space=pltpu.VMEM),
-            pl.BlockSpec(memory_space=pltpu.VMEM),
         ],
         out_specs=pl.BlockSpec(memory_space=pltpu.VMEM),
-    )(extinction_table, density_rim, labels_rim, mask)
+    )(extinction_table, stack_rim, mask)
 
 
 def shards(density, labels, sunlight, opacity_table, extinction_table, albedo_table):
@@ -200,7 +199,6 @@
     stack = jnp.concatenate([density, labels.astype(jnp.float32), sunlight], axis=0)
     stack_rim = halo(halo(stack, "across", 1, widest), "view", 2, widest)
     density_rim = stack_rim[:brick_l]
-    labels_rim = stack_rim[brick_l : 2 * brick_l]
     sun_rim = stack_rim[2 * brick_l :]
     density_side = density_rim[
         :, widest - 2 : widest + brick_a + 2, widest - 2 : widest + brick_v + 2
@@ -215,7 +213,7 @@
     extinct_slabs = extinct.reshape(3, SLABS, layer_rows, brick_a, brick_v)
     running = jnp.cumsum(extinct_slabs, axis=2) - extinct_slabs
     fade_rim = fade_rim_of(
-        extinction_table, density_rim, labels_rim, plane_mask(widest, brick_a, brick_v), light_step
+        extinction_table, stack_rim, brick_l, plane_mask(widest, brick_a, brick_v), light_step
     )
     starts = None
     incoming = sun_rim

time: 106 us -> 104 us (0.981)
  local copies, waits for them, and re-layouts: 15.5 us -> 11.9 us
  other arithmetic: 29.8 us -> 31.9 us
  waiting for transfers between devices: 19.2 us -> 20.5 us
  starting transfers between devices: 29.2 us -> 28.1 us
    mul x31, other arithmetic: 12.1 us -> 14.7 us  [propagate(): current = current * fade_here]
    ppermute x3, waiting for transfers between devices: 8.07 us -> 10.3 us  [from_behind(): lax.ppermute(value, axis, [(source, source + steps) for source in range(l...]
    slice x1 -> x0, local copies, waits for them, and re-layouts: 2.03 us -> none  [shards(): labels_rim = stack_rim[brick_l:2 * brick_l]]
    slice x1, local copies, waits for them, and re-layouts: 1.59 us -> 0.01 us  [padded_2(): lax.slice_in_dim(block, 0, width, axis=dim)]
    unnamed x54 -> x48, local copies, waits for them, and re-layouts: 4.22 us -> 2.76 us
    ppermute x1, waiting for transfers between devices: 2.89 us -> 1.53 us  [halo(): lax.ppermute(lax.slice_in_dim(block, 0, need, axis=dim), axis, backward)]
    ppermute x1, local copies, waits for them, and re-layouts: 0.53 us -> 1.73 us  [halo(): lows.insert(0, lax.ppermute(low, axis, forward))]
    concatenate x2, other arithmetic: 2.91 us -> 3.99 us  [halo(): block = jnp.concatenate(lows + [block] + highs, axis=dim)]
  transfers between devices with their start and end apart: 10 -> 10, of which waited for: 7 -> 8; matrix products, arithmetic and copies ran while one was open for 15% -> 13% of each run, Pallas kernels for 0% -> 0%
where the time goes in v13:
time: 104 us; the launch traced here: 103 us
  other arithmetic  31.9 us (31%)
  starting transfers between devices  28.1 us (27%)
  waiting for transfers between devices  20.5 us (20%)
  local copies, waits for them, and re-layouts  11.9 us (11%)
  Pallas kernels  8.69 us (8%)
    mul x31, other arithmetic, propagate(): current = current * fade_here  14.7 us
    ppermute x3, starting transfers between devices, from_behind(): lax.ppermute(value, axis, [(source, source + steps) for source in range(l...  10.7 us
    ppermute x3, waiting for transfers between devices, from_behind(): lax.ppermute(value, axis, [(source, source + steps) for source in range(l...  10.3 us
    pallas_call x1, Pallas kernels, fade_rim_of(): pl.pallas_call(kernel, out_shape=jax.ShapeDtypeStruct((colours, SLABS, ri...  8.69 us
    ppermute x2, starting transfers between devices, from_partner(): return lax.ppermute(block, axis, route)  7.08 us
    ppermute x1, waiting for transfers between devices, halo(): got = lax.ppermute(send, axis, [(0, 1), (1, 0)])  5.88 us
    concatenate x2, other arithmetic, halo(): block = jnp.concatenate(lows + [block] + highs, axis=dim)  3.99 us
    ppermute x1, starting transfers between devices, padded_2(): lax.ppermute(lax.slice_in_dim(block, block.shape[dim] - width, None, axis...  3.48 us
  transfers between devices with their start and end apart: 10, of which 8 were waited for; matrix products, arithmetic and copies ran while one was open for 13% of the time, Pallas kernels for 0%

profile of v13, /device:TPU:16, one launch (start us, length us, event | category | flops | bytes accessed | tf_op | source)
XLA Modules:
  0.0 102.7 jit_solution(17191119315021453410)
XLA Ops:
  0.0 1.0 convert_element_type.39
  1.1 1.1 %pad_maximum_fusion.4 = f32[35,32,128]{2,1,0:T(8,128)S(1)} fusion(f32[3,32,128]{2,1,0:T(8,128)} %param.8, f32[16,32,128]{2,1,0:T(8,128)S(1)} %convert_element_type.39, f32[16,32,128]{2,1,0:T(8,128)} %param.6), kind=kLoop, calls=%fused_computation.17 | loop fusion | flops 286720 | bytes 1146880 | tf_op jit(solution)/shard_map/concatenate | solution.py:199
  2.2 1.6 %collective-permute-start = (f32[35,32,128]{2,1,0:T(8,128)S(1)}, f32[35,32,128]{2,1,0:T(8,128)S(1)}, u32[]{:S(2)}, u32[]{:S(2)}) collective-permute-start(f32[35,32,128]{2,1,0:T(8,128)S(1)} %pad_maximum_fusion.4), channel_id=1, source_target_pairs={{0,1},{1,0},{2,3},{3,2},{4,5},{5,4},{6,7},{7,6},{8,9},{9,8},{10,11... | collective-permute-start | bytes 1720328 | tf_op jit(solution)/shard_map/ppermute | solution.py:87
  3.8 0.6 broadcast_compare_fusion.14
  4.5 0.4 slice_reduce_fusion.15
  4.9 2.6 %select_select_fusion = f32[7,16,32,128]{3,2,1,0:T(8,128)S(1)} fusion(f32[7]{0:T(128)S(1)} %get-tuple-element.10, f32[7]{0:T(128)S(1)} %get-tuple-element.11, f32[7]{0:T(128)S(1)} %get-tuple-element.12, f32[7]{0:T(128)S(1)} %get-tuple-element.13, f32[7]{0:T(128)S(1)} %get-tuple-element.14, f32[7]{0:T(128)S(1)} %get-tuple-element.15, ...), kind=kLoop, calls=%fused_computation.1 | loop fusion | flops 6881280 | bytes 2818496 | tf_op jit(solution)/shard_map/jit(_where)/select_n | solution.py:209
  7.5 0.9 fusion.151
  8.4 0.7 broadcast_multiply_fusion.mask_ref
  9.1 1.0 fusion
  10.1 1.0 slice_multiply_fusion
  11.1 5.9 %collective-permute-done = f32[35,32,128]{2,1,0:T(8,128)S(1)} collective-permute-done((f32[35,32,128]{2,1,0:T(8,128)S(1)}, f32[35,32,128]{2,1,0:T(8,128)S(1)}, u32[]{:S(2)}, u32[]{:S(2)}) %collective-permute-start) | collective-permute-done | bytes 573472 | tf_op jit(solution)/shard_map/ppermute | solution.py:87
  17.3 0.6 fusion.159
  18.1 1.3 %copy.123 = f32[35,96,32]{1,2,0:T(8,128)} copy(f32[35,96,32]{2,1,0:T(8,128)S(1)} %get-tuple-element.45) | data formatting | bytes 860160 | tf_op jit(solution)/shard_map/slice | solution.py:97
  19.4 1.4 %collective-permute-start.1 = (f32[35,96,32]{1,2,0:T(8,128)}, f32[35,96,32]{1,2,0:T(8,128)S(1)}, u32[]{:S(2)}, u32[]{:S(2)}) collective-permute-start(f32[35,96,32]{1,2,0:T(8,128)} %copy.123), channel_id=1, source_target_pairs={{0,2},{2,4},{4,6},{1,3},{3,5},{5,7},{8,10},{10,12},{12,14},{9,11},... | collective-permute-start | bytes 1290248 | tf_op jit(solution)/shard_map/ppermute | solution.py:98
  20.9 1.3 %copy.124 = f32[35,96,32]{1,2,0:T(8,128)} copy(f32[35,96,32]{2,1,0:T(8,128)S(1)} %get-tuple-element.46) | data formatting | bytes 860160 | tf_op jit(solution)/shard_map/slice | solution.py:99
  22.2 1.5 %collective-permute-start.2 = (f32[35,96,32]{1,2,0:T(8,128)}, f32[35,96,32]{1,2,0:T(8,128)S(1)}, u32[]{:S(2)}, u32[]{:S(2)}) collective-permute-start(f32[35,96,32]{1,2,0:T(8,128)} %copy.124), channel_id=1, source_target_pairs={{2,0},{4,2},{6,4},{3,1},{5,3},{7,5},{10,8},{12,10},{14,12},{11,9},... | collective-permute-start | bytes 1290248 | tf_op jit(solution)/shard_map/ppermute | solution.py:99
  23.8 1.0 fusion.164
  24.7 1.7 %copy.125 = f32[35,96,32]{2,1,0:T(8,128)} copy(f32[35,96,32]{1,2,0:T(8,128)S(1)} %collective-permute-done.1) | data formatting | bytes 860160 | tf_op jit(solution)/shard_map/ppermute | solution.py:98
  26.5 1.5 %collective-permute-done.2 = f32[35,96,32]{1,2,0:T(8,128)S(1)} collective-permute-done((f32[35,96,32]{1,2,0:T(8,128)}, f32[35,96,32]{1,2,0:T(8,128)S(1)}, u32[]{:S(2)}, u32[]{:S(2)}) %collective-permute-start.2) | collective-permute-done | bytes 430112 | tf_op jit(solution)/shard_map/ppermute | solution.py:99
  28.0 1.7 %copy.126 = f32[35,96,32]{2,1,0:T(8,128)} copy(f32[35,96,32]{1,2,0:T(8,128)S(1)} %collective-permute-done.2) | data formatting | bytes 860160 | tf_op jit(solution)/shard_map/ppermute | solution.py:99
  29.7 3.9 %pad_maximum_fusion.stack_ref = f32[35,96,192]{2,1,0:T(8,128)S(1)} fusion(f32[35,96,32]{2,1,0:T(8,128)} %copy.126, f32[35,32,128]{2,1,0:T(8,128)} %copy-done.8, f32[3,32,128]{2,1,0:T(8,128)S(1)} %copy-done.15, f32[16,32,128]{2,1,0:T(8,128)} %copy-done.9, f32[16,32,128]{2,1,0:T(8,128)} %param.6, f32[35,32,128]{2,1,0:T(8,128)} %copy-done.7, f32[35,96,32]{2,1,0:T(8,128)} %copy.125), kind=kLoop, calls=%fused_computation | loop fusion | flops 3870720 | bytes 5160960 | tf_op jit(solution)/shard_map/concatenate | solution.py:100
  33.6 1.3 %slice.1096 = f32[16,36,132]{2,1,0:T(8,128)} slice(f32[35,96,192]{2,1,0:T(8,128)S(1)} %pad_maximum_fusion.stack_ref), slice={[0:16], [30:66], [30:162]} | slice | bytes 608256 | tf_op jit(solution)/shard_map/slice | solution.py:203
  34.9 0.7 copy-done.1
  35.6 8.7 %shard_map.64 = f32[3,8,96,192]{3,2,1,0:T(8,128)} custom-call(f32[3,16]{1,0:T(4,128)} %table_ref.1, f32[35,96,192]{2,1,0:T(8,128)} %copy-done.1, f32[96,192]{1,0:T(8,128)} %broadcast_multiply_fusion.mask_ref), custom_call_target="tpu_custom_call" | custom-call | tf_op jit(solution)/shard_map/pallas_call | solution.py:173
  44.3 1.2 %fusion.17 = f32[3,96,192]{2,1,0:T(8,128)S(1)} fusion(f32[3,8,96,192]{3,2,1,0:T(8,128)} %shard_map.64, f32[35,96,192]{2,1,0:T(8,128)} %copy-done.1), kind=kLoop, calls=%fused_computation.43 | loop fusion | flops 55296 | bytes 663552 | tf_op jit(solution)/shard_map/mul | solution.py:129
  45.6 1.4 %fusion.13 = f32[3,94,190]{2,1,0:T(8,128)S(1)} fusion(f32[3,8,96,192]{3,2,1,0:T(8,128)} %shard_map.64, f32[3,96,192]{2,1,0:T(8,128)S(1)} %fusion.17), kind=kLoop, calls=%fused_computation.35 | loop fusion | flops 428640 | bytes 1500240 | tf_op jit(solution)/shard_map/mul | solution.py:129
  47.0 0.4 fusion.9
  47.4 0.4 fusion.5
  47.9 0.4 fusion.30
  48.3 0.4 fusion.26
  48.7 0.4 fusion.22
  49.2 0.4 fusion.18
  49.6 0.3 fusion.56
  49.9 0.3 copy-done.6
  50.3 3.5 %collective-permute-start.4 = (f32[2,36,132]{2,1,0:T(8,128)S(1)}, f32[2,36,132]{2,1,0:T(8,128)S(1)}, u32[]{:S(2)}, u32[]{:S(2)}) collective-permute-start(f32[2,36,132]{2,1,0:T(8,128)S(1)} %get-tuple-element.50), channel_id=1, source_target_pairs={{0,8},{8,16},{16,24},{1,9},{9,17},{17,25},{2,10},{10,18},{18,26},{... | collective-permute-start | bytes 114056 | tf_op jit(solution)/shard_map/ppermute | solution.py:21
  53.8 2.3 %collective-permute-start.3 = (f32[2,36,132]{2,1,0:T(8,128)S(1)}, f32[2,36,132]{2,1,0:T(8,128)S(1)}, u32[]{:S(2)}, u32[]{:S(2)}) collective-permute-start(f32[2,36,132]{2,1,0:T(8,128)S(1)} %get-tuple-element.49), channel_id=1, source_target_pairs={{8,0},{16,8},{24,16},{9,1},{17,9},{25,17},{10,2},{18,10},{26,18},{... | collective-permute-start | bytes 114056 | tf_op jit(solution)/shard_map/ppermute | solution.py:24
  56.2 3.5 %collective-permute-start.5 = (f32[3,80,176]{2,1,0:T(8,128)S(1)}, f32[3,80,176]{2,1,0:T(8,128)S(1)}, u32[]{:S(2)}, u32[]{:S(2)}) collective-permute-start(f32[3,80,176]{2,1,0:T(8,128)S(1)} %fusion.56), channel_id=1, source_target_pairs={{0,8},{8,16},{16,24},{1,9},{9,17},{17,25},{2,10},{10,18},{18,26},{... | collective-permute-start | bytes 506888 | tf_op jit(solution)/shard_map/ppermute | solution.py:32
  59.8 0.4 collective-permute-done.3
  60.2 5.0 %collective-permute-done.5 = f32[3,80,176]{2,1,0:T(8,128)S(1)} collective-permute-done((f32[3,80,176]{2,1,0:T(8,128)S(1)}, f32[3,80,176]{2,1,0:T(8,128)S(1)}, u32[]{:S(2)}, u32[]{:S(2)}) %collective-permute-start.5) | collective-permute-done | bytes 168992 | tf_op jit(solution)/shard_map/ppermute | solution.py:32
  65.2 1.1 %fusion.53 = f32[3,80,176]{2,1,0:T(8,128)S(1)} fusion(f32[3,8,96,192]{3,2,1,0:T(8,128)S(1)} %copy-done, f32[3,80,176]{2,1,0:T(8,128)S(1)} %collective-permute-done.5, f32[35,96,192]{2,1,0:T(8,128)} %copy-done.1, pred[]{:T(512)S(6)} %eq.140), kind=kLoop, calls=%fused_computation.126 | loop fusion | flops 84480 | bytes 675841 | tf_op jit(solution)/shard_map/mul | solution.py:129
  66.3 0.4 fusion.49
  66.7 0.4 fusion.45
  67.1 0.4 fusion.41
  67.5 0.4 fusion.69
  67.8 0.4 fusion.65
  68.2 0.4 fusion.61
  68.6 0.4 fusion.57
  69.2 3.7 %collective-permute-start.6 = (f32[3,64,160]{2,1,0:T(8,128)S(1)}, f32[3,64,160]{2,1,0:T(8,128)S(1)}, u32[]{:S(2)}, u32[]{:S(2)}) collective-permute-start(f32[3,64,160]{2,1,0:T(8,128)S(1)} %fusion.88), channel_id=1, source_target_pairs={{0,8},{8,16},{16,24},{1,9},{9,17},{17,25},{2,10},{10,18},{18,26},{... | collective-permute-start | bytes 368648 | tf_op jit(solution)/shard_map/ppermute | solution.py:32
  72.9 1.2 %multiply_multiply_fusion.1 = (f32[18,34,130]{2,1,0:T(8,128)S(1)}, f32[18,34,130]{2,1,0:T(8,128)S(1)}) fusion(f32[16,36,132]{2,1,0:T(8,128)S(1)} %copy-done.6, f32[2,36,132]{2,1,0:T(8,128)S(1)} %collective-permute-done.4, f32[2,36,132]{2,1,0:T(8,128)S(1)} %collective-permute-done.3, f32[130]{0:T(256)S(1)} %and_convert_fusion, ...), kind=kLoop, calls=%fused_computation.6 | loop fusion | flops 1750320 | bytes 2292568 | tf_op jit(solution)/shard_map/mul | solution.py:63
  74.1 2.7 %collective-permute-done.6 = f32[3,64,160]{2,1,0:T(8,128)S(1)} collective-permute-done((f32[3,64,160]{2,1,0:T(8,128)S(1)}, f32[3,64,160]{2,1,0:T(8,128)S(1)}, u32[]{:S(2)}, u32[]{:S(2)}) %collective-permute-start.6) | collective-permute-done | bytes 122912 | tf_op jit(solution)/shard_map/ppermute | solution.py:32
  76.8 1.1 %fusion.85 = f32[3,64,160]{2,1,0:T(8,128)S(1)} fusion(f32[3,8,96,192]{3,2,1,0:T(8,128)S(1)} %copy-done, f32[3,64,160]{2,1,0:T(8,128)S(1)} %collective-permute-done.6, f32[35,96,192]{2,1,0:T(8,128)} %copy-done.1, pred[]{:T(512)S(6)} %eq.140), kind=kLoop, calls=%fused_computation.191 | loop fusion | flops 61440 | bytes 491521 | tf_op jit(solution)/shard_map/mul | solution.py:129
  78.2 0.3 fusion.77
  78.5 0.3 fusion.73
  80.3 3.5 %collective-permute-start.7 = (f32[3,48,144]{2,1,0:T(8,128)S(1)}, f32[3,48,144]{2,1,0:T(8,128)S(1)}, u32[]{:S(2)}, u32[]{:S(2)}) collective-permute-start(f32[3,48,144]{2,1,0:T(8,128)S(1)} %fusion.120), channel_id=1, source_target_pairs={{0,8},{8,16},{16,24},{1,9},{9,17},{17,25},{2,10},{10,18},{18,26},{... | collective-permute-start | bytes 248840 | tf_op jit(solution)/shard_map/ppermute | solution.py:32
  83.7 0.9 fusion.37
  84.6 2.7 %collective-permute-done.7 = f32[3,48,144]{2,1,0:T(8,128)S(1)} collective-permute-done((f32[3,48,144]{2,1,0:T(8,128)S(1)}, f32[3,48,144]{2,1,0:T(8,128)S(1)}, u32[]{:S(2)}, u32[]{:S(2)}) %collective-permute-start.7) | collective-permute-done | bytes 82976 | tf_op jit(solution)/shard_map/ppermute | solution.py:32
  87.3 1.1 %fusion.117 = (f32[3,48,144]{2,1,0:T(8,128)S(1)}, f32[3,48,144]{2,1,0:T(8,128)S(1)}) fusion(f32[3,8,96,192]{3,2,1,0:T(8,128)S(1)} %copy-done, f32[3,48,144]{2,1,0:T(8,128)S(1)} %collective-permute-done.7, f32[35,96,192]{2,1,0:T(8,128)} %copy-done.1, pred[]{:T(512)S(6)} %eq.140), kind=kLoop, calls=%fused_computation.256 | loop fusion | flops 41472 | bytes 414721 | tf_op jit(solution)/shard_map/mul | solution.py:129
  91.0 0.5 copy-done.5
  91.7 0.5 fusion.3
  92.3 2.8 %collective-permute-start.8 = (f32[4,2,128]{2,1,0:T(2,128)S(1)}, f32[4,2,128]{2,1,0:T(2,128)S(1)}, u32[]{:S(2)}, u32[]{:S(2)}) collective-permute-start(f32[4,2,128]{2,1,0:T(2,128)S(1)} %bitcast.280), channel_id=1, source_target_pairs={{0,2},{2,0},{4,6},{6,4},{1,3},{3,1},{5,7},{7,5},{8,10},{10,8},{12,... | collective-permute-start | bytes 12296 | tf_op jit(solution)/shard_map/ppermute | solution.py:42
  95.2 0.8 collective-permute-done.8
  96.1 4.3 %collective-permute-start.9 = (f32[4,1,128]{2,0,1:T(4,128)S(1)}, f32[4,1,128]{2,0,1:T(4,128)S(1)}, u32[]{:S(2)}, u32[]{:S(2)}) collective-permute-start(f32[4,1,128]{2,0,1:T(4,128)S(1)} %bitcast.281), channel_id=1, source_target_pairs={{0,4},{4,0},{2,6},{6,2},{1,5},{5,1},{3,7},{7,3},{8,12},{12,8},{10,... | collective-permute-start | bytes 6152 | tf_op jit(solution)/shard_map/ppermute | solution.py:42
  100.3 1.6 %collective-permute-done.9 = f32[4,1,128]{2,0,1:T(4,128)S(1)} collective-permute-done((f32[4,1,128]{2,0,1:T(4,128)S(1)}, f32[4,1,128]{2,0,1:T(4,128)S(1)}, u32[]{:S(2)}, u32[]{:S(2)}) %collective-permute-start.9) | collective-permute-done | bytes 2080 | tf_op jit(solution)/shard_map/ppermute | solution.py:42
  102.1 0.6 pad_maximum_fusion.5
  (93 shorter events, 6.0 us)
Async XLA Ops:
  0.0 3.8 %copy-start.14 = (s32[16,32,128]{2,1,0:T(8,128)S(1)}, s32[16,32,128]{2,1,0:T(8,128)}, u32[]{:S(2)}) copy-start(s32[16,32,128]{2,1,0:T(8,128)} %param.7) | copy-start | bytes 786436
  0.0 4.5 %copy-start.16 = (f32[3,16]{1,0:T(4,128)S(1)}, f32[3,16]{1,0:T(4,128)}, u32[]{:S(2)}) copy-start(f32[3,16]{1,0:T(4,128)} %table_ref.1) | copy-start | bytes 580
  0.0 4.5 %copy-start.18 = (f32[16]{0:T(128)S(1)}, f32[16]{0:T(128)}, u32[]{:S(2)}) copy-start(f32[16]{0:T(128)} %param.9) | copy-start | bytes 196
  0.0 4.5 %copy-start.17 = (f32[3,16]{1,0:T(4,128)S(1)}, f32[3,16]{1,0:T(4,128)}, u32[]{:S(2)}) copy-start(f32[3,16]{1,0:T(4,128)} %param.11) | copy-start | bytes 580
  1.0 16.1 %copy-start.9 = (f32[16,32,128]{2,1,0:T(8,128)}, f32[16,32,128]{2,1,0:T(8,128)S(1)}, u32[]{:S(2)}) copy-start(f32[16,32,128]{2,1,0:T(8,128)S(1)} %convert_element_type.39) | copy-start | bytes 786436
  2.2 14.8 %collective-permute-start = (f32[35,32,128]{2,1,0:T(8,128)S(1)}, f32[35,32,128]{2,1,0:T(8,128)S(1)}, u32[]{:S(2)}, u32[]{:S(2)}) collective-permute-start(f32[35,32,128]{2,1,0:T(8,128)S(1)} %pad_maximum_fusion.4), channel_id=1, source_target_pairs={{0,1},{1,0},{2,3},{3,2},{4,5},{5,4},{6,7},{7,6},{8,9},{9,8},{10,11... | collective-permute-start | bytes 1720328 | tf_op jit(solution)/shard_map/ppermute | solution.py:87
  3.8 3.8 %copy-start.2 = (f32[16,32,128]{2,1,0:T(8,128)S(1)}, f32[16,32,128]{2,1,0:T(8,128)}, u32[]{:S(2)}) copy-start(f32[16,32,128]{2,1,0:T(8,128)} %param.6) | copy-start | bytes 786436
  7.5 9.6 %copy-start.4 = (f32[7,16,32,128]{3,2,1,0:T(8,128)}, f32[7,16,32,128]{3,2,1,0:T(8,128)S(1)}, u32[]{:S(2)}) copy-start(f32[7,16,32,128]{3,2,1,0:T(8,128)S(1)} %select_select_fusion) | copy-start | bytes 5505028
  10.1 7.0 %copy-start.15 = (f32[3,32,128]{2,1,0:T(8,128)S(1)}, f32[3,32,128]{2,1,0:T(8,128)}, u32[]{:S(2)}) copy-start(f32[3,32,128]{2,1,0:T(8,128)} %param.8) | copy-start | bytes 147460
  17.1 0.8 copy-start.7
  17.1 1.0 copy-start.8
  19.4 4.3 %copy-start.11 = (f32[3,16,32,128]{3,2,1,0:T(8,128)S(1)}, f32[3,16,32,128]{3,2,1,0:T(8,128)}, u32[]{:S(2)}) copy-start(f32[3,16,32,128]{3,2,1,0:T(8,128)} %slice_multiply_fusion) | copy-start | bytes 2359300
  19.4 5.3 %collective-permute-start.1 = (f32[35,96,32]{1,2,0:T(8,128)}, f32[35,96,32]{1,2,0:T(8,128)S(1)}, u32[]{:S(2)}, u32[]{:S(2)}) collective-permute-start(f32[35,96,32]{1,2,0:T(8,128)} %copy.123), channel_id=1, source_target_pairs={{0,2},{2,4},{4,6},{1,3},{3,5},{5,7},{8,10},{10,12},{12,14},{9,11},... | collective-permute-start | bytes 1290248 | tf_op jit(solution)/shard_map/ppermute | solution.py:98
  22.2 5.8 %collective-permute-start.2 = (f32[35,96,32]{1,2,0:T(8,128)}, f32[35,96,32]{1,2,0:T(8,128)S(1)}, u32[]{:S(2)}, u32[]{:S(2)}) collective-permute-start(f32[35,96,32]{1,2,0:T(8,128)} %copy.124), channel_id=1, source_target_pairs={{2,0},{4,2},{6,4},{3,1},{5,3},{7,5},{10,8},{12,10},{14,12},{11,9},... | collective-permute-start | bytes 1290248 | tf_op jit(solution)/shard_map/ppermute | solution.py:99
  33.6 2.0 %copy-start.1 = (f32[35,96,192]{2,1,0:T(8,128)}, f32[35,96,192]{2,1,0:T(8,128)S(1)}, u32[]{:S(2)}) copy-start(f32[35,96,192]{2,1,0:T(8,128)S(1)} %pad_maximum_fusion.stack_ref) | copy-start | bytes 7741444
  44.3 2.7 %copy-start = (f32[3,8,96,192]{3,2,1,0:T(8,128)S(1)}, f32[3,8,96,192]{3,2,1,0:T(8,128)}, u32[]{:S(2)}) copy-start(f32[3,8,96,192]{3,2,1,0:T(8,128)} %shard_map.64) | copy-start | bytes 5308420
  49.1 1.1 %copy-start.6 = (f32[16,36,132]{2,1,0:T(8,128)S(1)}, f32[16,36,132]{2,1,0:T(8,128)}, u32[]{:S(2)}) copy-start(f32[16,36,132]{2,1,0:T(8,128)} %slice.1096) | copy-start | bytes 912388
  50.3 9.4 %collective-permute-start.4 = (f32[2,36,132]{2,1,0:T(8,128)S(1)}, f32[2,36,132]{2,1,0:T(8,128)S(1)}, u32[]{:S(2)}, u32[]{:S(2)}) collective-permute-start(f32[2,36,132]{2,1,0:T(8,128)S(1)} %get-tuple-element.50), channel_id=1, source_target_pairs={{0,8},{8,16},{16,24},{1,9},{9,17},{17,25},{2,10},{10,18},{18,26},{... | collective-permute-start | bytes 114056 | tf_op jit(solution)/shard_map/ppermute | solution.py:21
  53.8 6.3 %collective-permute-start.3 = (f32[2,36,132]{2,1,0:T(8,128)S(1)}, f32[2,36,132]{2,1,0:T(8,128)S(1)}, u32[]{:S(2)}, u32[]{:S(2)}) collective-permute-start(f32[2,36,132]{2,1,0:T(8,128)S(1)} %get-tuple-element.49), channel_id=1, source_target_pairs={{8,0},{16,8},{24,16},{9,1},{17,9},{25,17},{10,2},{18,10},{26,18},{... | collective-permute-start | bytes 114056 | tf_op jit(solution)/shard_map/ppermute | solution.py:24
  56.2 9.0 %collective-permute-start.5 = (f32[3,80,176]{2,1,0:T(8,128)S(1)}, f32[3,80,176]{2,1,0:T(8,128)S(1)}, u32[]{:S(2)}, u32[]{:S(2)}) collective-permute-start(f32[3,80,176]{2,1,0:T(8,128)S(1)} %fusion.56), channel_id=1, source_target_pairs={{0,8},{8,16},{16,24},{1,9},{9,17},{17,25},{2,10},{10,18},{18,26},{... | collective-permute-start | bytes 506888 | tf_op jit(solution)/shard_map/ppermute | solution.py:32
  69.2 7.6 %collective-permute-start.6 = (f32[3,64,160]{2,1,0:T(8,128)S(1)}, f32[3,64,160]{2,1,0:T(8,128)S(1)}, u32[]{:S(2)}, u32[]{:S(2)}) collective-permute-start(f32[3,64,160]{2,1,0:T(8,128)S(1)} %fusion.88), channel_id=1, source_target_pairs={{0,8},{8,16},{16,24},{1,9},{9,17},{17,25},{2,10},{10,18},{18,26},{... | collective-permute-start | bytes 368648 | tf_op jit(solution)/shard_map/ppermute | solution.py:32
  80.3 7.0 %collective-permute-start.7 = (f32[3,48,144]{2,1,0:T(8,128)S(1)}, f32[3,48,144]{2,1,0:T(8,128)S(1)}, u32[]{:S(2)}, u32[]{:S(2)}) collective-permute-start(f32[3,48,144]{2,1,0:T(8,128)S(1)} %fusion.120), channel_id=1, source_target_pairs={{0,8},{8,16},{16,24},{1,9},{9,17},{17,25},{2,10},{10,18},{18,26},{... | collective-permute-start | bytes 248840 | tf_op jit(solution)/shard_map/ppermute | solution.py:32
  89.8 1.1 %copy-start.3 = (f32[16,32,128]{2,1,0:T(8,128)S(1)}, f32[16,32,128]{2,1,0:T(8,128)}, u32[]{:S(2)}) copy-start(f32[16,32,128]{2,1,0:T(8,128)} %param.6) | copy-start | bytes 786436
  89.8 1.6 %copy-start.5 = (f32[7,16,32,128]{3,2,1,0:T(8,128)S(1)}, f32[7,16,32,128]{3,2,1,0:T(8,128)}, u32[]{:S(2)}) copy-start(f32[7,16,32,128]{3,2,1,0:T(8,128)} %copy-done.4) | copy-start | bytes 5505028
  89.9 1.8 %copy-start.10 = (f32[3,8,2,32,128]{4,3,2,1,0:T(8,128)S(1)}, f32[3,8,2,32,128]{4,3,2,1,0:T(8,128)}, u32[]{:S(2)}) copy-start(f32[3,8,2,32,128]{4,3,2,1,0:T(8,128)} %fusion.164) | copy-start | bytes 2359300
  89.9 1.8 %copy-start.12 = (f32[16,32,128]{2,1,0:T(8,128)S(1)}, f32[16,32,128]{2,1,0:T(8,128)}, u32[]{:S(2)}) copy-start(f32[16,32,128]{2,1,0:T(8,128)} %get-tuple-element.44) | copy-start | bytes 786436
  89.9 1.9 %copy-start.13 = (f32[16,32,128]{2,1,0:T(8,128)S(1)}, f32[16,32,128]{2,1,0:T(8,128)}, u32[]{:S(2)}) copy-start(f32[16,32,128]{2,1,0:T(8,128)} %fusion) | copy-start | bytes 786436
  92.3 3.7 %collective-permute-start.8 = (f32[4,2,128]{2,1,0:T(2,128)S(1)}, f32[4,2,128]{2,1,0:T(2,128)S(1)}, u32[]{:S(2)}, u32[]{:S(2)}) collective-permute-start(f32[4,2,128]{2,1,0:T(2,128)S(1)} %bitcast.280), channel_id=1, source_target_pairs={{0,2},{2,0},{4,6},{6,4},{1,3},{3,1},{5,7},{7,5},{8,10},{10,8},{12,... | collective-permute-start | bytes 12296 | tf_op jit(solution)/shard_map/ppermute | solution.py:42
  96.1 5.8 %collective-permute-start.9 = (f32[4,1,128]{2,0,1:T(4,128)S(1)}, f32[4,1,128]{2,0,1:T(4,128)S(1)}, u32[]{:S(2)}, u32[]{:S(2)}) collective-permute-start(f32[4,1,128]{2,0,1:T(4,128)S(1)} %bitcast.281), channel_id=1, source_target_pairs={{0,4},{4,0},{2,6},{6,2},{1,5},{5,1},{3,7},{7,3},{8,12},{12,8},{10,... | collective-permute-start | bytes 6152 | tf_op jit(solution)/shard_map/ppermute | solution.py:42

commit v14 on v13

--- a/solution.py
+++ b/solution.py
@@ -143,29 +143,36 @@
     layer_rows = rows // SLABS
     colours, materials = extinction_table.shape
     chunk = 8 if rim_a % 8 == 0 else rim_a
+    lanes = 128
+    windows = sorted(set(list(range(0, rim_v - lanes + 1, lanes)) + [rim_v - lanes]))
+    table_lanes = jnp.pad(
+        jnp.broadcast_to(extinction_table[:, None, :], (colours, chunk, materials)),
+        ((0, 0), (0, 0), (0, lanes - materials)),
+    )
 
     def kernel(table_ref, stack_ref, mask_ref, out_ref):
+        tables = [table_ref[c] for c in range(colours)]
+
         def one_slab(slab_num, carry):
             for first in range(0, rim_a, chunk):
                 part = slice(first, first + chunk)
-                depth = [None] * colours
-                for row in range(layer_rows):
-                    row_num = slab_num * layer_rows + row
-                    here = stack_ref[rows + row_num, part, :]
-                    cells = stack_ref[row_num, part, :]
-                    looked = [jnp.full(here.shape, table_ref[c, 0]) for c in range(colours)]
-                    for material in range(1, materials):
-                        match = here == float(material)
-                        looked = [
-                            jnp.where(match, table_ref[c, material], looked[c]) for c in range(colours)
-                        ]
+                for low in windows:
+                    window = slice(low, low + lanes)
+                    depth = [None] * colours
+                    for row in range(layer_rows):
+                        row_num = slab_num * layer_rows + row
+                        here = stack_ref[rows + row_num, part, window].astype(jnp.int32)
+                        cells = stack_ref[row_num, part, window]
+                        for c in range(colours):
+                            looked = jnp.take_along_axis(
+                                tables[c], here, axis=1, mode="promise_in_bounds"
+                            )
+                            term = looked * cells
+                            depth[c] = term if depth[c] is None else depth[c] + term
                     for c in range(colours):
-                        term = looked[c] * cells
-                        depth[c] = term if depth[c] is None else depth[c] + term
-                for c in range(colours):
-                    out_ref[c, slab_num, part, :] = (
-                        jnp.exp(-light_step * depth[c]) * mask_ref[part, :]
-                    )
+                        out_ref[c, slab_num, part, window] = (
+                            jnp.exp(-light_step * depth[c]) * mask_ref[part, window]
+                        )
             return carry
 
         lax.fori_loop(0, SLABS, one_slab, 0)
@@ -174,12 +181,12 @@
         kernel,
         out_shape=jax.ShapeDtypeStruct((colours, SLABS, rim_a, rim_v), jnp.float32),
         in_specs=[
-            pl.BlockSpec(memory_space=pltpu.SMEM),
+            pl.BlockSpec(memory_space=pltpu.VMEM),
             pl.BlockSpec(memory_space=pltpu.VMEM),
             pl.BlockSpec(memory_space=pltpu.VMEM),
         ],
         out_specs=pl.BlockSpec(memory_space=pltpu.VMEM),
-    )(extinction_table, stack_rim, mask)
+    )(table_lanes, stack_rim, mask)
 
 
 def shards(density, labels, sunlight, opacity_table, extinction_table, albedo_table):

time: 104 us -> 120 us (1.15)
  Pallas kernels: 8.69 us -> 25.4 us
    pallas_call x1, Pallas kernels: 8.69 us -> 25.4 us  [fade_rim_of(): pl.pallas_call(kernel, out_shape=jax.ShapeDtypeStruct((colours, SLABS, ri...]
  transfers between devices with their start and end apart: 10 -> 10, of which waited for: 8 -> 8; matrix products, arithmetic and copies ran while one was open for 13% -> 12% of each run, Pallas kernels for 0% -> 0%
where the time goes in v14:
time: 120 us; the launch traced here: 119 us
  other arithmetic  31.9 us (27%)
  starting transfers between devices  28.1 us (23%)
  Pallas kernels  25.4 us (21%)
  waiting for transfers between devices  19.9 us (17%)
  local copies, waits for them, and re-layouts  12.5 us (10%)
    pallas_call x1, Pallas kernels, fade_rim_of(): pl.pallas_call(kernel, out_shape=jax.ShapeDtypeStruct((colours, SLABS, ri...  25.4 us
    mul x31, other arithmetic, propagate(): current = current * fade_here  14.7 us
    ppermute x3, starting transfers between devices, from_behind(): lax.ppermute(value, axis, [(source, source + steps) for source in range(l...  10.7 us
    ppermute x3, waiting for transfers between devices, from_behind(): lax.ppermute(value, axis, [(source, source + steps) for source in range(l...  10.3 us
    ppermute x2, starting transfers between devices, from_partner(): return lax.ppermute(block, axis, route)  7.08 us
    ppermute x1, waiting for transfers between devices, halo(): got = lax.ppermute(send, axis, [(0, 1), (1, 0)])  5.28 us
    concatenate x2, other arithmetic, halo(): block = jnp.concatenate(lows + [block] + highs, axis=dim)  3.99 us
    ppermute x1, starting transfers between devices, padded_2(): lax.ppermute(lax.slice_in_dim(block, block.shape[dim] - width, None, axis...  3.48 us
  transfers between devices with their start and end apart: 10, of which 8 were waited for; matrix products, arithmetic and copies ran while one was open for 12% of the time, Pallas kernels for 0%

profile of v14, /device:TPU:16, one launch (start us, length us, event | category | flops | bytes accessed | tf_op | source)
XLA Modules:
  0.0 119.4 jit_solution(12070946697678804297)
XLA Ops:
  0.0 1.0 convert_element_type.41
  1.1 1.1 pad_maximum_fusion.4
  2.2 1.6 %collective-permute-start = (f32[35,32,128]{2,1,0:T(8,128)S(1)}, f32[35,32,128]{2,1,0:T(8,128)S(1)}, u32[]{:S(2)}, u32[]{:S(2)}) collective-permute-start(f32[35,32,128]{2,1,0:T(8,128)S(1)} %pad_maximum_fusion.4), channel_id=1, source_target_pairs={{0,1},{1,0},{2,3},{3,2},{4,5},{5,4},{6,7},{7,6},{8,9},{9,8},{10,11... | collective-permute-start | bytes 1720328 | tf_op jit(solution)/shard_map/ppermute | solution.py:87
  3.8 0.6 broadcast_compare_fusion.14
  4.5 0.4 slice_reduce_fusion.15
  4.9 2.6 %select_select_fusion = f32[7,16,32,128]{3,2,1,0:T(8,128)S(1)} fusion(f32[7]{0:T(128)S(1)} %get-tuple-element.10, f32[7]{0:T(128)S(1)} %get-tuple-element.11, f32[7]{0:T(128)S(1)} %get-tuple-element.12, f32[7]{0:T(128)S(1)} %get-tuple-element.13, f32[7]{0:T(128)S(1)} %get-tuple-element.14, f32[7]{0:T(128)S(1)} %get-tuple-element.15, ...), kind=kLoop, calls=%fused_computation.1 | loop fusion | flops 6881280 | bytes 2818496 | tf_op jit(solution)/shard_map/jit(_where)/select_n | solution.py:216
  7.5 0.9 fusion.151
  8.4 0.7 broadcast_multiply_fusion.mask_ref
  9.1 0.6 pad.4.table_ref
  9.7 1.0 fusion
  10.7 1.0 slice_multiply_fusion
  11.7 5.3 %collective-permute-done = f32[35,32,128]{2,1,0:T(8,128)S(1)} collective-permute-done((f32[35,32,128]{2,1,0:T(8,128)S(1)}, f32[35,32,128]{2,1,0:T(8,128)S(1)}, u32[]{:S(2)}, u32[]{:S(2)}) %collective-permute-start) | collective-permute-done | bytes 573472 | tf_op jit(solution)/shard_map/ppermute | solution.py:87
  17.3 0.6 fusion.159
  18.1 1.3 %copy.123 = f32[35,96,32]{1,2,0:T(8,128)} copy(f32[35,96,32]{2,1,0:T(8,128)S(1)} %get-tuple-element.45) | data formatting | bytes 860160 | tf_op jit(solution)/shard_map/slice | solution.py:97
  19.4 1.4 %collective-permute-start.1 = (f32[35,96,32]{1,2,0:T(8,128)}, f32[35,96,32]{1,2,0:T(8,128)S(1)}, u32[]{:S(2)}, u32[]{:S(2)}) collective-permute-start(f32[35,96,32]{1,2,0:T(8,128)} %copy.123), channel_id=1, source_target_pairs={{0,2},{2,4},{4,6},{1,3},{3,5},{5,7},{8,10},{10,12},{12,14},{9,11},... | collective-permute-start | bytes 1290248 | tf_op jit(solution)/shard_map/ppermute | solution.py:98
  20.9 1.3 %copy.124 = f32[35,96,32]{1,2,0:T(8,128)} copy(f32[35,96,32]{2,1,0:T(8,128)S(1)} %get-tuple-element.46) | data formatting | bytes 860160 | tf_op jit(solution)/shard_map/slice | solution.py:99
  22.2 1.5 %collective-permute-start.2 = (f32[35,96,32]{1,2,0:T(8,128)}, f32[35,96,32]{1,2,0:T(8,128)S(1)}, u32[]{:S(2)}, u32[]{:S(2)}) collective-permute-start(f32[35,96,32]{1,2,0:T(8,128)} %copy.124), channel_id=1, source_target_pairs={{2,0},{4,2},{6,4},{3,1},{5,3},{7,5},{10,8},{12,10},{14,12},{11,9},... | collective-permute-start | bytes 1290248 | tf_op jit(solution)/shard_map/ppermute | solution.py:99
  23.8 1.0 fusion.164
  24.7 1.7 %copy.125 = f32[35,96,32]{2,1,0:T(8,128)} copy(f32[35,96,32]{1,2,0:T(8,128)S(1)} %collective-permute-done.1) | data formatting | bytes 860160 | tf_op jit(solution)/shard_map/ppermute | solution.py:98
  26.5 1.5 %collective-permute-done.2 = f32[35,96,32]{1,2,0:T(8,128)S(1)} collective-permute-done((f32[35,96,32]{1,2,0:T(8,128)}, f32[35,96,32]{1,2,0:T(8,128)S(1)}, u32[]{:S(2)}, u32[]{:S(2)}) %collective-permute-start.2) | collective-permute-done | bytes 430112 | tf_op jit(solution)/shard_map/ppermute | solution.py:99
  28.0 1.7 %copy.126 = f32[35,96,32]{2,1,0:T(8,128)} copy(f32[35,96,32]{1,2,0:T(8,128)S(1)} %collective-permute-done.2) | data formatting | bytes 860160 | tf_op jit(solution)/shard_map/ppermute | solution.py:99
  29.7 3.9 %pad_maximum_fusion.stack_ref = f32[35,96,192]{2,1,0:T(8,128)S(1)} fusion(f32[35,96,32]{2,1,0:T(8,128)} %copy.126, f32[35,32,128]{2,1,0:T(8,128)} %copy-done.8, f32[3,32,128]{2,1,0:T(8,128)S(1)} %copy-done.15, f32[16,32,128]{2,1,0:T(8,128)} %copy-done.9, f32[16,32,128]{2,1,0:T(8,128)} %param.6, f32[35,32,128]{2,1,0:T(8,128)} %copy-done.7, f32[35,96,32]{2,1,0:T(8,128)} %copy.125), kind=kLoop, calls=%fused_computation | loop fusion | flops 3870720 | bytes 5160960 | tf_op jit(solution)/shard_map/concatenate | solution.py:100
  33.6 1.3 %slice.1096 = f32[16,36,132]{2,1,0:T(8,128)} slice(f32[35,96,192]{2,1,0:T(8,128)S(1)} %pad_maximum_fusion.stack_ref), slice={[0:16], [30:66], [30:162]} | slice | bytes 608256 | tf_op jit(solution)/shard_map/slice | solution.py:210
  34.9 0.7 copy-done.1
  35.6 25.4 %shard_map.64 = f32[3,8,96,192]{3,2,1,0:T(8,128)} custom-call(f32[3,8,128]{2,1,0:T(8,128)} %pad.4.table_ref, f32[35,96,192]{2,1,0:T(8,128)} %copy-done.1, f32[96,192]{1,0:T(8,128)} %broadcast_multiply_fusion.mask_ref), custom_call_target="tpu_custom_call" | custom-call | tf_op jit(solution)/shard_map/pallas_call | solution.py:180
  61.0 1.2 %fusion.17 = f32[3,96,192]{2,1,0:T(8,128)S(1)} fusion(f32[3,8,96,192]{3,2,1,0:T(8,128)} %shard_map.64, f32[35,96,192]{2,1,0:T(8,128)} %copy-done.1), kind=kLoop, calls=%fused_computation.43 | loop fusion | flops 55296 | bytes 663552 | tf_op jit(solution)/shard_map/mul | solution.py:129
  62.2 1.4 %fusion.13 = f32[3,94,190]{2,1,0:T(8,128)S(1)} fusion(f32[3,8,96,192]{3,2,1,0:T(8,128)} %shard_map.64, f32[3,96,192]{2,1,0:T(8,128)S(1)} %fusion.17), kind=kLoop, calls=%fused_computation.35 | loop fusion | flops 428640 | bytes 1500240 | tf_op jit(solution)/shard_map/mul | solution.py:129
  63.7 0.4 fusion.9
  64.1 0.4 fusion.5
  64.6 0.4 fusion.30
  65.0 0.4 fusion.26
  65.4 0.4 fusion.22
  65.8 0.4 fusion.18
  66.3 0.3 fusion.56
  66.6 0.3 copy-done.6
  66.9 3.5 %collective-permute-start.4 = (f32[2,36,132]{2,1,0:T(8,128)S(1)}, f32[2,36,132]{2,1,0:T(8,128)S(1)}, u32[]{:S(2)}, u32[]{:S(2)}) collective-permute-start(f32[2,36,132]{2,1,0:T(8,128)S(1)} %get-tuple-element.50), channel_id=1, source_target_pairs={{0,8},{8,16},{16,24},{1,9},{9,17},{17,25},{2,10},{10,18},{18,26},{... | collective-permute-start | bytes 114056 | tf_op jit(solution)/shard_map/ppermute | solution.py:21
  70.5 2.3 %collective-permute-start.3 = (f32[2,36,132]{2,1,0:T(8,128)S(1)}, f32[2,36,132]{2,1,0:T(8,128)S(1)}, u32[]{:S(2)}, u32[]{:S(2)}) collective-permute-start(f32[2,36,132]{2,1,0:T(8,128)S(1)} %get-tuple-element.49), channel_id=1, source_target_pairs={{8,0},{16,8},{24,16},{9,1},{17,9},{25,17},{10,2},{18,10},{26,18},{... | collective-permute-start | bytes 114056 | tf_op jit(solution)/shard_map/ppermute | solution.py:24
  72.9 3.5 %collective-permute-start.5 = (f32[3,80,176]{2,1,0:T(8,128)S(1)}, f32[3,80,176]{2,1,0:T(8,128)S(1)}, u32[]{:S(2)}, u32[]{:S(2)}) collective-permute-start(f32[3,80,176]{2,1,0:T(8,128)S(1)} %fusion.56), channel_id=1, source_target_pairs={{0,8},{8,16},{16,24},{1,9},{9,17},{17,25},{2,10},{10,18},{18,26},{... | collective-permute-start | bytes 506888 | tf_op jit(solution)/shard_map/ppermute | solution.py:32
  76.4 0.4 collective-permute-done.3
  76.9 5.0 %collective-permute-done.5 = f32[3,80,176]{2,1,0:T(8,128)S(1)} collective-permute-done((f32[3,80,176]{2,1,0:T(8,128)S(1)}, f32[3,80,176]{2,1,0:T(8,128)S(1)}, u32[]{:S(2)}, u32[]{:S(2)}) %collective-permute-start.5) | collective-permute-done | bytes 168992 | tf_op jit(solution)/shard_map/ppermute | solution.py:32
  81.8 1.1 fusion.53
  83.0 0.4 fusion.49
  83.4 0.4 fusion.45
  83.8 0.4 fusion.41
  84.2 0.4 fusion.69
  84.5 0.4 fusion.65
  84.9 0.4 fusion.61
  85.2 0.4 fusion.57
  85.9 3.7 %collective-permute-start.6 = (f32[3,64,160]{2,1,0:T(8,128)S(1)}, f32[3,64,160]{2,1,0:T(8,128)S(1)}, u32[]{:S(2)}, u32[]{:S(2)}) collective-permute-start(f32[3,64,160]{2,1,0:T(8,128)S(1)} %fusion.88), channel_id=1, source_target_pairs={{0,8},{8,16},{16,24},{1,9},{9,17},{17,25},{2,10},{10,18},{18,26},{... | collective-permute-start | bytes 368648 | tf_op jit(solution)/shard_map/ppermute | solution.py:32
  89.6 1.2 multiply_multiply_fusion.1
  90.8 2.7 %collective-permute-done.6 = f32[3,64,160]{2,1,0:T(8,128)S(1)} collective-permute-done((f32[3,64,160]{2,1,0:T(8,128)S(1)}, f32[3,64,160]{2,1,0:T(8,128)S(1)}, u32[]{:S(2)}, u32[]{:S(2)}) %collective-permute-start.6) | collective-permute-done | bytes 122912 | tf_op jit(solution)/shard_map/ppermute | solution.py:32
  93.4 1.1 fusion.85
  94.5 0.3 fusion.81
  96.9 3.5 %collective-permute-start.7 = (f32[3,48,144]{2,1,0:T(8,128)S(1)}, f32[3,48,144]{2,1,0:T(8,128)S(1)}, u32[]{:S(2)}, u32[]{:S(2)}) collective-permute-start(f32[3,48,144]{2,1,0:T(8,128)S(1)} %fusion.120), channel_id=1, source_target_pairs={{0,8},{8,16},{16,24},{1,9},{9,17},{17,25},{2,10},{10,18},{18,26},{... | collective-permute-start | bytes 248840 | tf_op jit(solution)/shard_map/ppermute | solution.py:32
  100.4 0.9 fusion.37
  101.3 2.7 %collective-permute-done.7 = f32[3,48,144]{2,1,0:T(8,128)S(1)} collective-permute-done((f32[3,48,144]{2,1,0:T(8,128)S(1)}, f32[3,48,144]{2,1,0:T(8,128)S(1)}, u32[]{:S(2)}, u32[]{:S(2)}) %collective-permute-start.7) | collective-permute-done | bytes 82976 | tf_op jit(solution)/shard_map/ppermute | solution.py:32
  104.0 1.1 fusion.117
  107.6 0.5 copy-done.5
  108.4 0.5 fusion.3
  109.0 2.8 %collective-permute-start.8 = (f32[4,2,128]{2,1,0:T(2,128)S(1)}, f32[4,2,128]{2,1,0:T(2,128)S(1)}, u32[]{:S(2)}, u32[]{:S(2)}) collective-permute-start(f32[4,2,128]{2,1,0:T(2,128)S(1)} %bitcast.280), channel_id=1, source_target_pairs={{0,2},{2,0},{4,6},{6,4},{1,3},{3,1},{5,7},{7,5},{8,10},{10,8},{12,... | collective-permute-start | bytes 12296 | tf_op jit(solution)/shard_map/ppermute | solution.py:42
  111.8 0.8 collective-permute-done.8
  112.7 4.3 %collective-permute-start.9 = (f32[4,1,128]{2,0,1:T(4,128)S(1)}, f32[4,1,128]{2,0,1:T(4,128)S(1)}, u32[]{:S(2)}, u32[]{:S(2)}) collective-permute-start(f32[4,1,128]{2,0,1:T(4,128)S(1)} %bitcast.281), channel_id=1, source_target_pairs={{0,4},{4,0},{2,6},{6,2},{1,5},{5,1},{3,7},{7,3},{8,12},{12,8},{10,... | collective-permute-start | bytes 6152 | tf_op jit(solution)/shard_map/ppermute | solution.py:42
  117.0 1.6 %collective-permute-done.9 = f32[4,1,128]{2,0,1:T(4,128)S(1)} collective-permute-done((f32[4,1,128]{2,0,1:T(4,128)S(1)}, f32[4,1,128]{2,0,1:T(4,128)S(1)}, u32[]{:S(2)}, u32[]{:S(2)}) %collective-permute-start.9) | collective-permute-done | bytes 2080 | tf_op jit(solution)/shard_map/ppermute | solution.py:42
  118.8 0.6 pad_maximum_fusion.5
  (95 shorter events, 6.3 us)
Async XLA Ops:
  0.0 3.8 %copy-start.14 = (s32[16,32,128]{2,1,0:T(8,128)S(1)}, s32[16,32,128]{2,1,0:T(8,128)}, u32[]{:S(2)}) copy-start(s32[16,32,128]{2,1,0:T(8,128)} %param.7) | copy-start | bytes 786436
  0.0 4.5 %copy-start.16 = (f32[3,16]{1,0:T(4,128)S(1)}, f32[3,16]{1,0:T(4,128)}, u32[]{:S(2)}) copy-start(f32[3,16]{1,0:T(4,128)} %param.10) | copy-start | bytes 580
  0.0 4.5 %copy-start.18 = (f32[16]{0:T(128)S(1)}, f32[16]{0:T(128)}, u32[]{:S(2)}) copy-start(f32[16]{0:T(128)} %param.9) | copy-start | bytes 196
  0.0 4.5 %copy-start.17 = (f32[3,16]{1,0:T(4,128)S(1)}, f32[3,16]{1,0:T(4,128)}, u32[]{:S(2)}) copy-start(f32[3,16]{1,0:T(4,128)} %param.11) | copy-start | bytes 580
  1.0 16.1 %copy-start.9 = (f32[16,32,128]{2,1,0:T(8,128)}, f32[16,32,128]{2,1,0:T(8,128)S(1)}, u32[]{:S(2)}) copy-start(f32[16,32,128]{2,1,0:T(8,128)S(1)} %convert_element_type.41) | copy-start | bytes 786436
  2.2 14.8 %collective-permute-start = (f32[35,32,128]{2,1,0:T(8,128)S(1)}, f32[35,32,128]{2,1,0:T(8,128)S(1)}, u32[]{:S(2)}, u32[]{:S(2)}) collective-permute-start(f32[35,32,128]{2,1,0:T(8,128)S(1)} %pad_maximum_fusion.4), channel_id=1, source_target_pairs={{0,1},{1,0},{2,3},{3,2},{4,5},{5,4},{6,7},{7,6},{8,9},{9,8},{10,11... | collective-permute-start | bytes 1720328 | tf_op jit(solution)/shard_map/ppermute | solution.py:87
  3.8 3.8 %copy-start.2 = (f32[16,32,128]{2,1,0:T(8,128)S(1)}, f32[16,32,128]{2,1,0:T(8,128)}, u32[]{:S(2)}) copy-start(f32[16,32,128]{2,1,0:T(8,128)} %param.6) | copy-start | bytes 786436
  7.5 9.6 %copy-start.4 = (f32[7,16,32,128]{3,2,1,0:T(8,128)}, f32[7,16,32,128]{3,2,1,0:T(8,128)S(1)}, u32[]{:S(2)}) copy-start(f32[7,16,32,128]{3,2,1,0:T(8,128)S(1)} %select_select_fusion) | copy-start | bytes 5505028
  10.7 6.4 %copy-start.15 = (f32[3,32,128]{2,1,0:T(8,128)S(1)}, f32[3,32,128]{2,1,0:T(8,128)}, u32[]{:S(2)}) copy-start(f32[3,32,128]{2,1,0:T(8,128)} %param.8) | copy-start | bytes 147460
  17.1 0.8 copy-start.7
  17.1 1.0 copy-start.8
  19.4 4.3 %copy-start.11 = (f32[3,16,32,128]{3,2,1,0:T(8,128)S(1)}, f32[3,16,32,128]{3,2,1,0:T(8,128)}, u32[]{:S(2)}) copy-start(f32[3,16,32,128]{3,2,1,0:T(8,128)} %slice_multiply_fusion) | copy-start | bytes 2359300
  19.4 5.3 %collective-permute-start.1 = (f32[35,96,32]{1,2,0:T(8,128)}, f32[35,96,32]{1,2,0:T(8,128)S(1)}, u32[]{:S(2)}, u32[]{:S(2)}) collective-permute-start(f32[35,96,32]{1,2,0:T(8,128)} %copy.123), channel_id=1, source_target_pairs={{0,2},{2,4},{4,6},{1,3},{3,5},{5,7},{8,10},{10,12},{12,14},{9,11},... | collective-permute-start | bytes 1290248 | tf_op jit(solution)/shard_map/ppermute | solution.py:98
  22.2 5.8 %collective-permute-start.2 = (f32[35,96,32]{1,2,0:T(8,128)}, f32[35,96,32]{1,2,0:T(8,128)S(1)}, u32[]{:S(2)}, u32[]{:S(2)}) collective-permute-start(f32[35,96,32]{1,2,0:T(8,128)} %copy.124), channel_id=1, source_target_pairs={{2,0},{4,2},{6,4},{3,1},{5,3},{7,5},{10,8},{12,10},{14,12},{11,9},... | collective-permute-start | bytes 1290248 | tf_op jit(solution)/shard_map/ppermute | solution.py:99
  33.6 2.0 %copy-start.1 = (f32[35,96,192]{2,1,0:T(8,128)}, f32[35,96,192]{2,1,0:T(8,128)S(1)}, u32[]{:S(2)}) copy-start(f32[35,96,192]{2,1,0:T(8,128)S(1)} %pad_maximum_fusion.stack_ref) | copy-start | bytes 7741444
  61.0 2.7 %copy-start = (f32[3,8,96,192]{3,2,1,0:T(8,128)S(1)}, f32[3,8,96,192]{3,2,1,0:T(8,128)}, u32[]{:S(2)}) copy-start(f32[3,8,96,192]{3,2,1,0:T(8,128)} %shard_map.64) | copy-start | bytes 5308420
  65.8 1.1 copy-start.6
  66.9 9.4 %collective-permute-start.4 = (f32[2,36,132]{2,1,0:T(8,128)S(1)}, f32[2,36,132]{2,1,0:T(8,128)S(1)}, u32[]{:S(2)}, u32[]{:S(2)}) collective-permute-start(f32[2,36,132]{2,1,0:T(8,128)S(1)} %get-tuple-element.50), channel_id=1, source_target_pairs={{0,8},{8,16},{16,24},{1,9},{9,17},{17,25},{2,10},{10,18},{18,26},{... | collective-permute-start | bytes 114056 | tf_op jit(solution)/shard_map/ppermute | solution.py:21
  70.5 6.3 %collective-permute-start.3 = (f32[2,36,132]{2,1,0:T(8,128)S(1)}, f32[2,36,132]{2,1,0:T(8,128)S(1)}, u32[]{:S(2)}, u32[]{:S(2)}) collective-permute-start(f32[2,36,132]{2,1,0:T(8,128)S(1)} %get-tuple-element.49), channel_id=1, source_target_pairs={{8,0},{16,8},{24,16},{9,1},{17,9},{25,17},{10,2},{18,10},{26,18},{... | collective-permute-start | bytes 114056 | tf_op jit(solution)/shard_map/ppermute | solution.py:24
  72.9 9.0 %collective-permute-start.5 = (f32[3,80,176]{2,1,0:T(8,128)S(1)}, f32[3,80,176]{2,1,0:T(8,128)S(1)}, u32[]{:S(2)}, u32[]{:S(2)}) collective-permute-start(f32[3,80,176]{2,1,0:T(8,128)S(1)} %fusion.56), channel_id=1, source_target_pairs={{0,8},{8,16},{16,24},{1,9},{9,17},{17,25},{2,10},{10,18},{18,26},{... | collective-permute-start | bytes 506888 | tf_op jit(solution)/shard_map/ppermute | solution.py:32
  85.9 7.6 %collective-permute-start.6 = (f32[3,64,160]{2,1,0:T(8,128)S(1)}, f32[3,64,160]{2,1,0:T(8,128)S(1)}, u32[]{:S(2)}, u32[]{:S(2)}) collective-permute-start(f32[3,64,160]{2,1,0:T(8,128)S(1)} %fusion.88), channel_id=1, source_target_pairs={{0,8},{8,16},{16,24},{1,9},{9,17},{17,25},{2,10},{10,18},{18,26},{... | collective-permute-start | bytes 368648 | tf_op jit(solution)/shard_map/ppermute | solution.py:32
  96.9 7.0 %collective-permute-start.7 = (f32[3,48,144]{2,1,0:T(8,128)S(1)}, f32[3,48,144]{2,1,0:T(8,128)S(1)}, u32[]{:S(2)}, u32[]{:S(2)}) collective-permute-start(f32[3,48,144]{2,1,0:T(8,128)S(1)} %fusion.120), channel_id=1, source_target_pairs={{0,8},{8,16},{16,24},{1,9},{9,17},{17,25},{2,10},{10,18},{18,26},{... | collective-permute-start | bytes 248840 | tf_op jit(solution)/shard_map/ppermute | solution.py:32
  106.5 1.1 copy-start.3
  106.5 1.6 %copy-start.5 = (f32[7,16,32,128]{3,2,1,0:T(8,128)S(1)}, f32[7,16,32,128]{3,2,1,0:T(8,128)}, u32[]{:S(2)}) copy-start(f32[7,16,32,128]{3,2,1,0:T(8,128)} %copy-done.4) | copy-start | bytes 5505028
  106.5 1.8 %copy-start.10 = (f32[3,8,2,32,128]{4,3,2,1,0:T(8,128)S(1)}, f32[3,8,2,32,128]{4,3,2,1,0:T(8,128)}, u32[]{:S(2)}) copy-start(f32[3,8,2,32,128]{4,3,2,1,0:T(8,128)} %fusion.164) | copy-start | bytes 2359300
  106.5 1.8 %copy-start.12 = (f32[16,32,128]{2,1,0:T(8,128)S(1)}, f32[16,32,128]{2,1,0:T(8,128)}, u32[]{:S(2)}) copy-start(f32[16,32,128]{2,1,0:T(8,128)} %get-tuple-element.44) | copy-start | bytes 786436
  106.6 1.9 %copy-start.13 = (f32[16,32,128]{2,1,0:T(8,128)S(1)}, f32[16,32,128]{2,1,0:T(8,128)}, u32[]{:S(2)}) copy-start(f32[16,32,128]{2,1,0:T(8,128)} %fusion) | copy-start | bytes 786436
  109.0 3.7 %collective-permute-start.8 = (f32[4,2,128]{2,1,0:T(2,128)S(1)}, f32[4,2,128]{2,1,0:T(2,128)S(1)}, u32[]{:S(2)}, u32[]{:S(2)}) collective-permute-start(f32[4,2,128]{2,1,0:T(2,128)S(1)} %bitcast.280), channel_id=1, source_target_pairs={{0,2},{2,0},{4,6},{6,4},{1,3},{3,1},{5,7},{7,5},{8,10},{10,8},{12,... | collective-permute-start | bytes 12296 | tf_op jit(solution)/shard_map/ppermute | solution.py:42
  112.7 5.8 %collective-permute-start.9 = (f32[4,1,128]{2,0,1:T(4,128)S(1)}, f32[4,1,128]{2,0,1:T(4,128)S(1)}, u32[]{:S(2)}, u32[]{:S(2)}) collective-permute-start(f32[4,1,128]{2,0,1:T(4,128)S(1)} %bitcast.281), channel_id=1, source_target_pairs={{0,4},{4,0},{2,6},{6,2},{1,5},{5,1},{3,7},{7,3},{8,12},{12,8},{10,... | collective-permute-start | bytes 6152 | tf_op jit(solution)/shard_map/ppermute | solution.py:42

commit v15 on v13

--- a/solution.py
+++ b/solution.py
@@ -142,7 +142,7 @@
     _, rim_a, rim_v = stack_rim.shape
     layer_rows = rows // SLABS
     colours, materials = extinction_table.shape
-    chunk = 8 if rim_a % 8 == 0 else rim_a
+    chunk = 16 if rim_a % 16 == 0 else (8 if rim_a % 8 == 0 else rim_a)
 
     def kernel(table_ref, stack_ref, mask_ref, out_ref):
         def one_slab(slab_num, carry):

time: 104 us -> 104 us (level)
  no operation moved by 1% of the time
where the time goes in v15:
time: 104 us; the launch traced here: 103 us
  other arithmetic  31.9 us (31%)
  starting transfers between devices  28.1 us (27%)
  waiting for transfers between devices  20.5 us (20%)
  local copies, waits for them, and re-layouts  11.9 us (11%)
  Pallas kernels  8.82 us (8%)
    mul x31, other arithmetic, propagate(): current = current * fade_here  14.7 us
    ppermute x3, starting transfers between devices, from_behind(): lax.ppermute(value, axis, [(source, source + steps) for source in range(l...  10.7 us
    ppermute x3, waiting for transfers between devices, from_behind(): lax.ppermute(value, axis, [(source, source + steps) for source in range(l...  10.3 us
    pallas_call x1, Pallas kernels, fade_rim_of(): pl.pallas_call(kernel, out_shape=jax.ShapeDtypeStruct((colours, SLABS, ri...  8.82 us
    ppermute x2, starting transfers between devices, from_partner(): return lax.ppermute(block, axis, route)  7.08 us
    ppermute x1, waiting for transfers between devices, halo(): got = lax.ppermute(send, axis, [(0, 1), (1, 0)])  5.88 us
    concatenate x2, other arithmetic, halo(): block = jnp.concatenate(lows + [block] + highs, axis=dim)  3.99 us
    ppermute x1, starting transfers between devices, padded_2(): lax.ppermute(lax.slice_in_dim(block, block.shape[dim] - width, None, axis...  3.48 us
  transfers between devices with their start and end apart: 10, of which 8 were waited for; matrix products, arithmetic and copies ran while one was open for 13% of the time, Pallas kernels for 0%

profile of v15, /device:TPU:16, one launch (start us, length us, event | category | flops | bytes accessed | tf_op | source)
XLA Modules:
  0.0 102.8 jit_solution(10135845545261386478)
XLA Ops:
  0.0 1.0 convert_element_type.39
  1.1 1.1 %pad_maximum_fusion.4 = f32[35,32,128]{2,1,0:T(8,128)S(1)} fusion(f32[3,32,128]{2,1,0:T(8,128)} %param.8, f32[16,32,128]{2,1,0:T(8,128)S(1)} %convert_element_type.39, f32[16,32,128]{2,1,0:T(8,128)} %param.6), kind=kLoop, calls=%fused_computation.17 | loop fusion | flops 286720 | bytes 1146880 | tf_op jit(solution)/shard_map/concatenate | solution.py:199
  2.2 1.6 %collective-permute-start = (f32[35,32,128]{2,1,0:T(8,128)S(1)}, f32[35,32,128]{2,1,0:T(8,128)S(1)}, u32[]{:S(2)}, u32[]{:S(2)}) collective-permute-start(f32[35,32,128]{2,1,0:T(8,128)S(1)} %pad_maximum_fusion.4), channel_id=1, source_target_pairs={{0,1},{1,0},{2,3},{3,2},{4,5},{5,4},{6,7},{7,6},{8,9},{9,8},{10,11... | collective-permute-start | bytes 1720328 | tf_op jit(solution)/shard_map/ppermute | solution.py:87
  3.8 0.6 broadcast_compare_fusion.14
  4.5 0.4 slice_reduce_fusion.15
  4.9 2.6 %select_select_fusion = f32[7,16,32,128]{3,2,1,0:T(8,128)S(1)} fusion(f32[7]{0:T(128)S(1)} %get-tuple-element.10, f32[7]{0:T(128)S(1)} %get-tuple-element.11, f32[7]{0:T(128)S(1)} %get-tuple-element.12, f32[7]{0:T(128)S(1)} %get-tuple-element.13, f32[7]{0:T(128)S(1)} %get-tuple-element.14, f32[7]{0:T(128)S(1)} %get-tuple-element.15, ...), kind=kLoop, calls=%fused_computation.1 | loop fusion | flops 6881280 | bytes 2818496 | tf_op jit(solution)/shard_map/jit(_where)/select_n | solution.py:209
  7.5 0.9 fusion.151
  8.4 0.7 broadcast_multiply_fusion.mask_ref
  9.1 1.0 fusion
  10.1 1.0 slice_multiply_fusion
  11.1 5.9 %collective-permute-done = f32[35,32,128]{2,1,0:T(8,128)S(1)} collective-permute-done((f32[35,32,128]{2,1,0:T(8,128)S(1)}, f32[35,32,128]{2,1,0:T(8,128)S(1)}, u32[]{:S(2)}, u32[]{:S(2)}) %collective-permute-start) | collective-permute-done | bytes 573472 | tf_op jit(solution)/shard_map/ppermute | solution.py:87
  17.3 0.6 fusion.159
  18.1 1.3 %copy.123 = f32[35,96,32]{1,2,0:T(8,128)} copy(f32[35,96,32]{2,1,0:T(8,128)S(1)} %get-tuple-element.45) | data formatting | bytes 860160 | tf_op jit(solution)/shard_map/slice | solution.py:97
  19.4 1.4 %collective-permute-start.1 = (f32[35,96,32]{1,2,0:T(8,128)}, f32[35,96,32]{1,2,0:T(8,128)S(1)}, u32[]{:S(2)}, u32[]{:S(2)}) collective-permute-start(f32[35,96,32]{1,2,0:T(8,128)} %copy.123), channel_id=1, source_target_pairs={{0,2},{2,4},{4,6},{1,3},{3,5},{5,7},{8,10},{10,12},{12,14},{9,11},... | collective-permute-start | bytes 1290248 | tf_op jit(solution)/shard_map/ppermute | solution.py:98
  20.9 1.3 %copy.124 = f32[35,96,32]{1,2,0:T(8,128)} copy(f32[35,96,32]{2,1,0:T(8,128)S(1)} %get-tuple-element.46) | data formatting | bytes 860160 | tf_op jit(solution)/shard_map/slice | solution.py:99
  22.2 1.5 %collective-permute-start.2 = (f32[35,96,32]{1,2,0:T(8,128)}, f32[35,96,32]{1,2,0:T(8,128)S(1)}, u32[]{:S(2)}, u32[]{:S(2)}) collective-permute-start(f32[35,96,32]{1,2,0:T(8,128)} %copy.124), channel_id=1, source_target_pairs={{2,0},{4,2},{6,4},{3,1},{5,3},{7,5},{10,8},{12,10},{14,12},{11,9},... | collective-permute-start | bytes 1290248 | tf_op jit(solution)/shard_map/ppermute | solution.py:99
  23.8 1.0 fusion.164
  24.7 1.7 %copy.125 = f32[35,96,32]{2,1,0:T(8,128)} copy(f32[35,96,32]{1,2,0:T(8,128)S(1)} %collective-permute-done.1) | data formatting | bytes 860160 | tf_op jit(solution)/shard_map/ppermute | solution.py:98
  26.5 1.5 %collective-permute-done.2 = f32[35,96,32]{1,2,0:T(8,128)S(1)} collective-permute-done((f32[35,96,32]{1,2,0:T(8,128)}, f32[35,96,32]{1,2,0:T(8,128)S(1)}, u32[]{:S(2)}, u32[]{:S(2)}) %collective-permute-start.2) | collective-permute-done | bytes 430112 | tf_op jit(solution)/shard_map/ppermute | solution.py:99
  28.0 1.7 %copy.126 = f32[35,96,32]{2,1,0:T(8,128)} copy(f32[35,96,32]{1,2,0:T(8,128)S(1)} %collective-permute-done.2) | data formatting | bytes 860160 | tf_op jit(solution)/shard_map/ppermute | solution.py:99
  29.7 3.9 %pad_maximum_fusion.stack_ref = f32[35,96,192]{2,1,0:T(8,128)S(1)} fusion(f32[35,96,32]{2,1,0:T(8,128)} %copy.126, f32[35,32,128]{2,1,0:T(8,128)} %copy-done.8, f32[3,32,128]{2,1,0:T(8,128)S(1)} %copy-done.15, f32[16,32,128]{2,1,0:T(8,128)} %copy-done.9, f32[16,32,128]{2,1,0:T(8,128)} %param.6, f32[35,32,128]{2,1,0:T(8,128)} %copy-done.7, f32[35,96,32]{2,1,0:T(8,128)} %copy.125), kind=kLoop, calls=%fused_computation | loop fusion | flops 3870720 | bytes 5160960 | tf_op jit(solution)/shard_map/concatenate | solution.py:100
  33.6 1.3 %slice.1096 = f32[16,36,132]{2,1,0:T(8,128)} slice(f32[35,96,192]{2,1,0:T(8,128)S(1)} %pad_maximum_fusion.stack_ref), slice={[0:16], [30:66], [30:162]} | slice | bytes 608256 | tf_op jit(solution)/shard_map/slice | solution.py:203
  34.9 0.7 copy-done.1
  35.6 8.8 %shard_map.64 = f32[3,8,96,192]{3,2,1,0:T(8,128)} custom-call(f32[3,16]{1,0:T(4,128)} %table_ref.1, f32[35,96,192]{2,1,0:T(8,128)} %copy-done.1, f32[96,192]{1,0:T(8,128)} %broadcast_multiply_fusion.mask_ref), custom_call_target="tpu_custom_call" | custom-call | tf_op jit(solution)/shard_map/pallas_call | solution.py:173
  44.4 1.2 %fusion.17 = f32[3,96,192]{2,1,0:T(8,128)S(1)} fusion(f32[3,8,96,192]{3,2,1,0:T(8,128)} %shard_map.64, f32[35,96,192]{2,1,0:T(8,128)} %copy-done.1), kind=kLoop, calls=%fused_computation.43 | loop fusion | flops 55296 | bytes 663552 | tf_op jit(solution)/shard_map/mul | solution.py:129
  45.7 1.4 %fusion.13 = f32[3,94,190]{2,1,0:T(8,128)S(1)} fusion(f32[3,8,96,192]{3,2,1,0:T(8,128)} %shard_map.64, f32[3,96,192]{2,1,0:T(8,128)S(1)} %fusion.17), kind=kLoop, calls=%fused_computation.35 | loop fusion | flops 428640 | bytes 1500240 | tf_op jit(solution)/shard_map/mul | solution.py:129
  47.1 0.4 fusion.9
  47.6 0.4 fusion.5
  48.0 0.4 fusion.30
  48.4 0.4 fusion.26
  48.9 0.4 fusion.22
  49.3 0.4 fusion.18
  49.7 0.3 fusion.56
  50.0 0.3 copy-done.6
  50.4 3.5 %collective-permute-start.4 = (f32[2,36,132]{2,1,0:T(8,128)S(1)}, f32[2,36,132]{2,1,0:T(8,128)S(1)}, u32[]{:S(2)}, u32[]{:S(2)}) collective-permute-start(f32[2,36,132]{2,1,0:T(8,128)S(1)} %get-tuple-element.50), channel_id=1, source_target_pairs={{0,8},{8,16},{16,24},{1,9},{9,17},{17,25},{2,10},{10,18},{18,26},{... | collective-permute-start | bytes 114056 | tf_op jit(solution)/shard_map/ppermute | solution.py:21
  54.0 2.3 %collective-permute-start.3 = (f32[2,36,132]{2,1,0:T(8,128)S(1)}, f32[2,36,132]{2,1,0:T(8,128)S(1)}, u32[]{:S(2)}, u32[]{:S(2)}) collective-permute-start(f32[2,36,132]{2,1,0:T(8,128)S(1)} %get-tuple-element.49), channel_id=1, source_target_pairs={{8,0},{16,8},{24,16},{9,1},{17,9},{25,17},{10,2},{18,10},{26,18},{... | collective-permute-start | bytes 114056 | tf_op jit(solution)/shard_map/ppermute | solution.py:24
  56.3 3.5 %collective-permute-start.5 = (f32[3,80,176]{2,1,0:T(8,128)S(1)}, f32[3,80,176]{2,1,0:T(8,128)S(1)}, u32[]{:S(2)}, u32[]{:S(2)}) collective-permute-start(f32[3,80,176]{2,1,0:T(8,128)S(1)} %fusion.56), channel_id=1, source_target_pairs={{0,8},{8,16},{16,24},{1,9},{9,17},{17,25},{2,10},{10,18},{18,26},{... | collective-permute-start | bytes 506888 | tf_op jit(solution)/shard_map/ppermute | solution.py:32
  59.9 0.4 collective-permute-done.3
  60.3 5.0 %collective-permute-done.5 = f32[3,80,176]{2,1,0:T(8,128)S(1)} collective-permute-done((f32[3,80,176]{2,1,0:T(8,128)S(1)}, f32[3,80,176]{2,1,0:T(8,128)S(1)}, u32[]{:S(2)}, u32[]{:S(2)}) %collective-permute-start.5) | collective-permute-done | bytes 168992 | tf_op jit(solution)/shard_map/ppermute | solution.py:32
  65.3 1.1 %fusion.53 = f32[3,80,176]{2,1,0:T(8,128)S(1)} fusion(f32[3,8,96,192]{3,2,1,0:T(8,128)S(1)} %copy-done, f32[3,80,176]{2,1,0:T(8,128)S(1)} %collective-permute-done.5, f32[35,96,192]{2,1,0:T(8,128)} %copy-done.1, pred[]{:T(512)S(6)} %eq.140), kind=kLoop, calls=%fused_computation.126 | loop fusion | flops 84480 | bytes 675841 | tf_op jit(solution)/shard_map/mul | solution.py:129
  66.4 0.4 fusion.49
  66.8 0.4 fusion.45
  67.2 0.4 fusion.41
  67.6 0.4 fusion.69
  68.0 0.4 fusion.65
  68.3 0.4 fusion.61
  68.7 0.4 fusion.57
  69.3 3.7 %collective-permute-start.6 = (f32[3,64,160]{2,1,0:T(8,128)S(1)}, f32[3,64,160]{2,1,0:T(8,128)S(1)}, u32[]{:S(2)}, u32[]{:S(2)}) collective-permute-start(f32[3,64,160]{2,1,0:T(8,128)S(1)} %fusion.88), channel_id=1, source_target_pairs={{0,8},{8,16},{16,24},{1,9},{9,17},{17,25},{2,10},{10,18},{18,26},{... | collective-permute-start | bytes 368648 | tf_op jit(solution)/shard_map/ppermute | solution.py:32
  73.0 1.2 %multiply_multiply_fusion.1 = (f32[18,34,130]{2,1,0:T(8,128)S(1)}, f32[18,34,130]{2,1,0:T(8,128)S(1)}) fusion(f32[16,36,132]{2,1,0:T(8,128)S(1)} %copy-done.6, f32[2,36,132]{2,1,0:T(8,128)S(1)} %collective-permute-done.4, f32[2,36,132]{2,1,0:T(8,128)S(1)} %collective-permute-done.3, f32[130]{0:T(256)S(1)} %and_convert_fusion, ...), kind=kLoop, calls=%fused_computation.6 | loop fusion | flops 1750320 | bytes 2292568 | tf_op jit(solution)/shard_map/mul | solution.py:63
  74.2 2.7 %collective-permute-done.6 = f32[3,64,160]{2,1,0:T(8,128)S(1)} collective-permute-done((f32[3,64,160]{2,1,0:T(8,128)S(1)}, f32[3,64,160]{2,1,0:T(8,128)S(1)}, u32[]{:S(2)}, u32[]{:S(2)}) %collective-permute-start.6) | collective-permute-done | bytes 122912 | tf_op jit(solution)/shard_map/ppermute | solution.py:32
  76.9 1.1 %fusion.85 = f32[3,64,160]{2,1,0:T(8,128)S(1)} fusion(f32[3,8,96,192]{3,2,1,0:T(8,128)S(1)} %copy-done, f32[3,64,160]{2,1,0:T(8,128)S(1)} %collective-permute-done.6, f32[35,96,192]{2,1,0:T(8,128)} %copy-done.1, pred[]{:T(512)S(6)} %eq.140), kind=kLoop, calls=%fused_computation.191 | loop fusion | flops 61440 | bytes 491521 | tf_op jit(solution)/shard_map/mul | solution.py:129
  78.0 0.3 fusion.81
  78.3 0.3 fusion.77
  80.4 3.5 %collective-permute-start.7 = (f32[3,48,144]{2,1,0:T(8,128)S(1)}, f32[3,48,144]{2,1,0:T(8,128)S(1)}, u32[]{:S(2)}, u32[]{:S(2)}) collective-permute-start(f32[3,48,144]{2,1,0:T(8,128)S(1)} %fusion.120), channel_id=1, source_target_pairs={{0,8},{8,16},{16,24},{1,9},{9,17},{17,25},{2,10},{10,18},{18,26},{... | collective-permute-start | bytes 248840 | tf_op jit(solution)/shard_map/ppermute | solution.py:32
  83.9 0.9 fusion.37
  84.8 2.7 %collective-permute-done.7 = f32[3,48,144]{2,1,0:T(8,128)S(1)} collective-permute-done((f32[3,48,144]{2,1,0:T(8,128)S(1)}, f32[3,48,144]{2,1,0:T(8,128)S(1)}, u32[]{:S(2)}, u32[]{:S(2)}) %collective-permute-start.7) | collective-permute-done | bytes 82976 | tf_op jit(solution)/shard_map/ppermute | solution.py:32
  87.4 1.1 %fusion.117 = (f32[3,48,144]{2,1,0:T(8,128)S(1)}, f32[3,48,144]{2,1,0:T(8,128)S(1)}) fusion(f32[3,8,96,192]{3,2,1,0:T(8,128)S(1)} %copy-done, f32[3,48,144]{2,1,0:T(8,128)S(1)} %collective-permute-done.7, f32[35,96,192]{2,1,0:T(8,128)} %copy-done.1, pred[]{:T(512)S(6)} %eq.140), kind=kLoop, calls=%fused_computation.256 | loop fusion | flops 41472 | bytes 414721 | tf_op jit(solution)/shard_map/mul | solution.py:129
  91.1 0.5 copy-done.5
  91.9 0.5 fusion.3
  92.5 2.8 %collective-permute-start.8 = (f32[4,2,128]{2,1,0:T(2,128)S(1)}, f32[4,2,128]{2,1,0:T(2,128)S(1)}, u32[]{:S(2)}, u32[]{:S(2)}) collective-permute-start(f32[4,2,128]{2,1,0:T(2,128)S(1)} %bitcast.280), channel_id=1, source_target_pairs={{0,2},{2,0},{4,6},{6,4},{1,3},{3,1},{5,7},{7,5},{8,10},{10,8},{12,... | collective-permute-start | bytes 12296 | tf_op jit(solution)/shard_map/ppermute | solution.py:42
  95.3 0.8 collective-permute-done.8
  96.2 4.3 %collective-permute-start.9 = (f32[4,1,128]{2,0,1:T(4,128)S(1)}, f32[4,1,128]{2,0,1:T(4,128)S(1)}, u32[]{:S(2)}, u32[]{:S(2)}) collective-permute-start(f32[4,1,128]{2,0,1:T(4,128)S(1)} %bitcast.281), channel_id=1, source_target_pairs={{0,4},{4,0},{2,6},{6,2},{1,5},{5,1},{3,7},{7,3},{8,12},{12,8},{10,... | collective-permute-start | bytes 6152 | tf_op jit(solution)/shard_map/ppermute | solution.py:42
  100.4 1.6 %collective-permute-done.9 = f32[4,1,128]{2,0,1:T(4,128)S(1)} collective-permute-done((f32[4,1,128]{2,0,1:T(4,128)S(1)}, f32[4,1,128]{2,0,1:T(4,128)S(1)}, u32[]{:S(2)}, u32[]{:S(2)}) %collective-permute-start.9) | collective-permute-done | bytes 2080 | tf_op jit(solution)/shard_map/ppermute | solution.py:42
  102.2 0.6 pad_maximum_fusion.5
  (93 shorter events, 6.0 us)
Async XLA Ops:
  0.0 3.8 %copy-start.14 = (s32[16,32,128]{2,1,0:T(8,128)S(1)}, s32[16,32,128]{2,1,0:T(8,128)}, u32[]{:S(2)}) copy-start(s32[16,32,128]{2,1,0:T(8,128)} %param.7) | copy-start | bytes 786436
  0.0 4.5 %copy-start.16 = (f32[3,16]{1,0:T(4,128)S(1)}, f32[3,16]{1,0:T(4,128)}, u32[]{:S(2)}) copy-start(f32[3,16]{1,0:T(4,128)} %table_ref.1) | copy-start | bytes 580
  0.0 4.5 %copy-start.18 = (f32[16]{0:T(128)S(1)}, f32[16]{0:T(128)}, u32[]{:S(2)}) copy-start(f32[16]{0:T(128)} %param.9) | copy-start | bytes 196
  0.0 4.5 %copy-start.17 = (f32[3,16]{1,0:T(4,128)S(1)}, f32[3,16]{1,0:T(4,128)}, u32[]{:S(2)}) copy-start(f32[3,16]{1,0:T(4,128)} %param.11) | copy-start | bytes 580
  1.0 16.1 %copy-start.9 = (f32[16,32,128]{2,1,0:T(8,128)}, f32[16,32,128]{2,1,0:T(8,128)S(1)}, u32[]{:S(2)}) copy-start(f32[16,32,128]{2,1,0:T(8,128)S(1)} %convert_element_type.39) | copy-start | bytes 786436
  2.2 14.8 %collective-permute-start = (f32[35,32,128]{2,1,0:T(8,128)S(1)}, f32[35,32,128]{2,1,0:T(8,128)S(1)}, u32[]{:S(2)}, u32[]{:S(2)}) collective-permute-start(f32[35,32,128]{2,1,0:T(8,128)S(1)} %pad_maximum_fusion.4), channel_id=1, source_target_pairs={{0,1},{1,0},{2,3},{3,2},{4,5},{5,4},{6,7},{7,6},{8,9},{9,8},{10,11... | collective-permute-start | bytes 1720328 | tf_op jit(solution)/shard_map/ppermute | solution.py:87
  3.8 3.8 %copy-start.2 = (f32[16,32,128]{2,1,0:T(8,128)S(1)}, f32[16,32,128]{2,1,0:T(8,128)}, u32[]{:S(2)}) copy-start(f32[16,32,128]{2,1,0:T(8,128)} %param.6) | copy-start | bytes 786436
  7.5 9.6 %copy-start.4 = (f32[7,16,32,128]{3,2,1,0:T(8,128)}, f32[7,16,32,128]{3,2,1,0:T(8,128)S(1)}, u32[]{:S(2)}) copy-start(f32[7,16,32,128]{3,2,1,0:T(8,128)S(1)} %select_select_fusion) | copy-start | bytes 5505028
  10.1 7.0 %copy-start.15 = (f32[3,32,128]{2,1,0:T(8,128)S(1)}, f32[3,32,128]{2,1,0:T(8,128)}, u32[]{:S(2)}) copy-start(f32[3,32,128]{2,1,0:T(8,128)} %param.8) | copy-start | bytes 147460
  17.1 0.8 copy-start.7
  17.1 1.0 copy-start.8
  19.4 4.3 %copy-start.11 = (f32[3,16,32,128]{3,2,1,0:T(8,128)S(1)}, f32[3,16,32,128]{3,2,1,0:T(8,128)}, u32[]{:S(2)}) copy-start(f32[3,16,32,128]{3,2,1,0:T(8,128)} %slice_multiply_fusion) | copy-start | bytes 2359300
  19.4 5.3 %collective-permute-start.1 = (f32[35,96,32]{1,2,0:T(8,128)}, f32[35,96,32]{1,2,0:T(8,128)S(1)}, u32[]{:S(2)}, u32[]{:S(2)}) collective-permute-start(f32[35,96,32]{1,2,0:T(8,128)} %copy.123), channel_id=1, source_target_pairs={{0,2},{2,4},{4,6},{1,3},{3,5},{5,7},{8,10},{10,12},{12,14},{9,11},... | collective-permute-start | bytes 1290248 | tf_op jit(solution)/shard_map/ppermute | solution.py:98
  22.2 5.8 %collective-permute-start.2 = (f32[35,96,32]{1,2,0:T(8,128)}, f32[35,96,32]{1,2,0:T(8,128)S(1)}, u32[]{:S(2)}, u32[]{:S(2)}) collective-permute-start(f32[35,96,32]{1,2,0:T(8,128)} %copy.124), channel_id=1, source_target_pairs={{2,0},{4,2},{6,4},{3,1},{5,3},{7,5},{10,8},{12,10},{14,12},{11,9},... | collective-permute-start | bytes 1290248 | tf_op jit(solution)/shard_map/ppermute | solution.py:99
  33.6 2.0 %copy-start.1 = (f32[35,96,192]{2,1,0:T(8,128)}, f32[35,96,192]{2,1,0:T(8,128)S(1)}, u32[]{:S(2)}) copy-start(f32[35,96,192]{2,1,0:T(8,128)S(1)} %pad_maximum_fusion.stack_ref) | copy-start | bytes 7741444
  44.4 2.7 %copy-start = (f32[3,8,96,192]{3,2,1,0:T(8,128)S(1)}, f32[3,8,96,192]{3,2,1,0:T(8,128)}, u32[]{:S(2)}) copy-start(f32[3,8,96,192]{3,2,1,0:T(8,128)} %shard_map.64) | copy-start | bytes 5308420
  49.3 1.1 %copy-start.6 = (f32[16,36,132]{2,1,0:T(8,128)S(1)}, f32[16,36,132]{2,1,0:T(8,128)}, u32[]{:S(2)}) copy-start(f32[16,36,132]{2,1,0:T(8,128)} %slice.1096) | copy-start | bytes 912388
  50.4 9.4 %collective-permute-start.4 = (f32[2,36,132]{2,1,0:T(8,128)S(1)}, f32[2,36,132]{2,1,0:T(8,128)S(1)}, u32[]{:S(2)}, u32[]{:S(2)}) collective-permute-start(f32[2,36,132]{2,1,0:T(8,128)S(1)} %get-tuple-element.50), channel_id=1, source_target_pairs={{0,8},{8,16},{16,24},{1,9},{9,17},{17,25},{2,10},{10,18},{18,26},{... | collective-permute-start | bytes 114056 | tf_op jit(solution)/shard_map/ppermute | solution.py:21
  54.0 6.3 %collective-permute-start.3 = (f32[2,36,132]{2,1,0:T(8,128)S(1)}, f32[2,36,132]{2,1,0:T(8,128)S(1)}, u32[]{:S(2)}, u32[]{:S(2)}) collective-permute-start(f32[2,36,132]{2,1,0:T(8,128)S(1)} %get-tuple-element.49), channel_id=1, source_target_pairs={{8,0},{16,8},{24,16},{9,1},{17,9},{25,17},{10,2},{18,10},{26,18},{... | collective-permute-start | bytes 114056 | tf_op jit(solution)/shard_map/ppermute | solution.py:24
  56.3 9.0 %collective-permute-start.5 = (f32[3,80,176]{2,1,0:T(8,128)S(1)}, f32[3,80,176]{2,1,0:T(8,128)S(1)}, u32[]{:S(2)}, u32[]{:S(2)}) collective-permute-start(f32[3,80,176]{2,1,0:T(8,128)S(1)} %fusion.56), channel_id=1, source_target_pairs={{0,8},{8,16},{16,24},{1,9},{9,17},{17,25},{2,10},{10,18},{18,26},{... | collective-permute-start | bytes 506888 | tf_op jit(solution)/shard_map/ppermute | solution.py:32
  69.3 7.6 %collective-permute-start.6 = (f32[3,64,160]{2,1,0:T(8,128)S(1)}, f32[3,64,160]{2,1,0:T(8,128)S(1)}, u32[]{:S(2)}, u32[]{:S(2)}) collective-permute-start(f32[3,64,160]{2,1,0:T(8,128)S(1)} %fusion.88), channel_id=1, source_target_pairs={{0,8},{8,16},{16,24},{1,9},{9,17},{17,25},{2,10},{10,18},{18,26},{... | collective-permute-start | bytes 368648 | tf_op jit(solution)/shard_map/ppermute | solution.py:32
  80.4 7.0 %collective-permute-start.7 = (f32[3,48,144]{2,1,0:T(8,128)S(1)}, f32[3,48,144]{2,1,0:T(8,128)S(1)}, u32[]{:S(2)}, u32[]{:S(2)}) collective-permute-start(f32[3,48,144]{2,1,0:T(8,128)S(1)} %fusion.120), channel_id=1, source_target_pairs={{0,8},{8,16},{16,24},{1,9},{9,17},{17,25},{2,10},{10,18},{18,26},{... | collective-permute-start | bytes 248840 | tf_op jit(solution)/shard_map/ppermute | solution.py:32
  90.0 1.1 %copy-start.3 = (f32[16,32,128]{2,1,0:T(8,128)S(1)}, f32[16,32,128]{2,1,0:T(8,128)}, u32[]{:S(2)}) copy-start(f32[16,32,128]{2,1,0:T(8,128)} %param.6) | copy-start | bytes 786436
  90.0 1.6 %copy-start.5 = (f32[7,16,32,128]{3,2,1,0:T(8,128)S(1)}, f32[7,16,32,128]{3,2,1,0:T(8,128)}, u32[]{:S(2)}) copy-start(f32[7,16,32,128]{3,2,1,0:T(8,128)} %copy-done.4) | copy-start | bytes 5505028
  90.0 1.8 %copy-start.10 = (f32[3,8,2,32,128]{4,3,2,1,0:T(8,128)S(1)}, f32[3,8,2,32,128]{4,3,2,1,0:T(8,128)}, u32[]{:S(2)}) copy-start(f32[3,8,2,32,128]{4,3,2,1,0:T(8,128)} %fusion.164) | copy-start | bytes 2359300
  90.0 1.8 %copy-start.12 = (f32[16,32,128]{2,1,0:T(8,128)S(1)}, f32[16,32,128]{2,1,0:T(8,128)}, u32[]{:S(2)}) copy-start(f32[16,32,128]{2,1,0:T(8,128)} %get-tuple-element.44) | copy-start | bytes 786436
  90.0 1.9 %copy-start.13 = (f32[16,32,128]{2,1,0:T(8,128)S(1)}, f32[16,32,128]{2,1,0:T(8,128)}, u32[]{:S(2)}) copy-start(f32[16,32,128]{2,1,0:T(8,128)} %fusion) | copy-start | bytes 786436
  92.5 3.7 %collective-permute-start.8 = (f32[4,2,128]{2,1,0:T(2,128)S(1)}, f32[4,2,128]{2,1,0:T(2,128)S(1)}, u32[]{:S(2)}, u32[]{:S(2)}) collective-permute-start(f32[4,2,128]{2,1,0:T(2,128)S(1)} %bitcast.280), channel_id=1, source_target_pairs={{0,2},{2,0},{4,6},{6,4},{1,3},{3,1},{5,7},{7,5},{8,10},{10,8},{12,... | collective-permute-start | bytes 12296 | tf_op jit(solution)/shard_map/ppermute | solution.py:42
  96.2 5.8 %collective-permute-start.9 = (f32[4,1,128]{2,0,1:T(4,128)S(1)}, f32[4,1,128]{2,0,1:T(4,128)S(1)}, u32[]{:S(2)}, u32[]{:S(2)}) collective-permute-start(f32[4,1,128]{2,0,1:T(4,128)S(1)} %bitcast.281), channel_id=1, source_target_pairs={{0,4},{4,0},{2,6},{6,2},{1,5},{5,1},{3,7},{7,3},{8,12},{12,8},{10,... | collective-permute-start | bytes 6152 | tf_op jit(solution)/shard_map/ppermute | solution.py:42

commit v16 on v15

--- a/solution.py
+++ b/solution.py
@@ -114,28 +114,44 @@
 
 
 def propagate(current, border_in, fade_rim, brick_a, brick_v):
-    widest = (fade_rim.shape[2] - brick_a) // 2
-    starts = []
-    for slab_num in range(SLABS):
-        border = border_in - slab_num
-        starts.append(current[:, border : border + brick_a, border : border + brick_v])
-        offset = widest - border
-        fade_here = fade_rim[
-            :,
-            slab_num,
-            offset : offset + brick_a + 2 * border,
-            offset : offset + brick_v + 2 * border,
-        ]
-        current = current * fade_here
-        centre = current[:, 1:-1, 1:-1]
-        current = centre + BLUR * (
-            current[:, :-2, 1:-1]
-            + current[:, 2:, 1:-1]
-            + current[:, 1:-1, :-2]
-            + current[:, 1:-1, 2:]
-            - 4.0 * centre
-        )
-    return (current, jnp.stack(starts, axis=1))
+    colours, _, rim_a, _ = fade_rim.shape
+    widest = (rim_a - brick_a) // 2
+    border_out = border_in - SLABS
+
+    def kernel(current_ref, fade_ref, out_ref, starts_ref):
+        for c in range(colours):
+            plane = current_ref[c]
+            for slab_num in range(SLABS):
+                border = border_in - slab_num
+                starts_ref[c, slab_num] = plane[border : border + brick_a, border : border + brick_v]
+                offset = widest - border
+                fade_here = fade_ref[c, slab_num][
+                    offset : offset + brick_a + 2 * border, offset : offset + brick_v + 2 * border
+                ]
+                plane = plane * fade_here
+                centre = plane[1:-1, 1:-1]
+                plane = centre + BLUR * (
+                    plane[:-2, 1:-1] + plane[2:, 1:-1] + plane[1:-1, :-2] + plane[1:-1, 2:] - 4.0 * centre
+                )
+            out_ref[c] = plane
+
+    return pl.pallas_call(
+        kernel,
+        out_shape=(
+            jax.ShapeDtypeStruct(
+                (colours, brick_a + 2 * border_out, brick_v + 2 * border_out), jnp.float32
+            ),
+            jax.ShapeDtypeStruct((colours, SLABS, brick_a, brick_v), jnp.float32),
+        ),
+        in_specs=[
+            pl.BlockSpec(memory_space=pltpu.VMEM),
+            pl.BlockSpec(memory_space=pltpu.VMEM),
+        ],
+        out_specs=(
+            pl.BlockSpec(memory_space=pltpu.VMEM),
+            pl.BlockSpec(memory_space=pltpu.VMEM),
+        ),
+    )(current, fade_rim)
 
 
 def fade_rim_of(extinction_table, stack_rim, rows, mask, light_step):

time: 104 us -> 117 us (1.12)
  Pallas kernels: 8.82 us -> 31.4 us
  other arithmetic: 31.9 us -> 23.1 us
    pallas_call x0 -> x4, Pallas kernels: none -> 22.6 us  [propagate(): pl.pallas_call(kernel, out_shape=(jax.ShapeDtypeStruct((colours, brick_a...]
    mul x31 -> x0, other arithmetic: 14.7 us -> none  [propagate(): current = current * fade_here]
    select_n x0 -> x3, other arithmetic: none -> 5.18 us  [shards(): incoming = jnp.where(light_idx == 0, sun_here, arrived)]
    unnamed x48 -> x39, local copies, waits for them, and re-layouts: 2.76 us -> 0.37 us
  transfers between devices with their start and end apart: 10 -> 10, of which waited for: 8 -> 8; matrix products, arithmetic and copies ran while one was open for 13% -> 12% of each run, Pallas kernels for 0% -> 0%
where the time goes in v16:
time: 117 us; the launch traced here: 116 us
  Pallas kernels  31.4 us (27%)
  starting transfers between devices  27.8 us (24%)
  other arithmetic  23.1 us (20%)
  waiting for transfers between devices  20.7 us (18%)
  local copies, waits for them, and re-layouts  11.1 us (9%)
    pallas_call x4, Pallas kernels, propagate(): pl.pallas_call(kernel, out_shape=(jax.ShapeDtypeStruct((colours, brick_a...  22.6 us
    ppermute x3, starting transfers between devices, from_behind(): lax.ppermute(value, axis, [(source, source + steps) for source in range(l...  10.6 us
    ppermute x3, waiting for transfers between devices, from_behind(): lax.ppermute(value, axis, [(source, source + steps) for source in range(l...  10.5 us
    pallas_call x1, Pallas kernels, fade_rim_of(): pl.pallas_call(kernel, out_shape=jax.ShapeDtypeStruct((colours, SLABS, ri...  8.82 us
    ppermute x2, starting transfers between devices, from_partner(): return lax.ppermute(block, axis, route)  7.08 us
    ppermute x1, waiting for transfers between devices, halo(): got = lax.ppermute(send, axis, [(0, 1), (1, 0)])  5.88 us
    select_n x3, other arithmetic, shards(): incoming = jnp.where(light_idx == 0, sun_here, arrived)  5.18 us
    concatenate x2, other arithmetic, halo(): block = jnp.concatenate(lows + [block] + highs, axis=dim)  3.99 us
  transfers between devices with their start and end apart: 10, of which 8 were waited for; matrix products, arithmetic and copies ran while one was open for 12% of the time, Pallas kernels for 0%

profile of v16, /device:TPU:16, one launch (start us, length us, event | category | flops | bytes accessed | tf_op | source)
XLA Modules:
  0.0 115.6 jit_solution(9789712393326312630)
XLA Ops:
  0.0 1.0 convert_element_type.39
  1.1 1.1 pad_maximum_fusion.4
  2.2 1.6 %collective-permute-start = (f32[35,32,128]{2,1,0:T(8,128)S(1)}, f32[35,32,128]{2,1,0:T(8,128)S(1)}, u32[]{:S(2)}, u32[]{:S(2)}) collective-permute-start(f32[35,32,128]{2,1,0:T(8,128)S(1)} %pad_maximum_fusion.4), channel_id=1, source_target_pairs={{0,1},{1,0},{2,3},{3,2},{4,5},{5,4},{6,7},{7,6},{8,9},{9,8},{10,11... | collective-permute-start | bytes 1720328 | tf_op jit(solution)/shard_map/ppermute | solution.py:87
  3.8 0.6 broadcast_compare_fusion.14
  4.5 0.4 slice_reduce_fusion.15
  4.9 2.6 %select_select_fusion = f32[7,16,32,128]{3,2,1,0:T(8,128)S(1)} fusion(f32[7]{0:T(128)S(1)} %get-tuple-element.18, f32[7]{0:T(128)S(1)} %get-tuple-element.19, f32[7]{0:T(128)S(1)} %get-tuple-element.20, f32[7]{0:T(128)S(1)} %get-tuple-element.21, f32[7]{0:T(128)S(1)} %get-tuple-element.22, f32[7]{0:T(128)S(1)} %get-tuple-element.23, ...), kind=kLoop, calls=%fused_computation.1 | loop fusion | flops 6881280 | bytes 2818496 | tf_op jit(solution)/shard_map/jit(_where)/select_n | solution.py:225
  7.5 0.9 fusion.18
  8.4 0.7 broadcast_multiply_fusion.mask_ref
  9.1 1.0 fusion
  10.1 1.0 slice_multiply_fusion
  11.1 5.9 %collective-permute-done = f32[35,32,128]{2,1,0:T(8,128)S(1)} collective-permute-done((f32[35,32,128]{2,1,0:T(8,128)S(1)}, f32[35,32,128]{2,1,0:T(8,128)S(1)}, u32[]{:S(2)}, u32[]{:S(2)}) %collective-permute-start) | collective-permute-done | bytes 573472 | tf_op jit(solution)/shard_map/ppermute | solution.py:87
  17.0 0.1 broadcast_select_fusion.1
  17.1 0.0 copy-done.3
  17.1 0.0 copy-start.6
  17.1 0.0 copy-start.7
  17.1 0.0 copy-done.8
  17.1 0.1 pad_maximum_fusion.1
  17.3 0.6 fusion.20
  17.9 0.0 copy-done.6
  17.9 0.2 copy-done.7
  18.1 1.3 %copy.27 = f32[35,96,32]{1,2,0:T(8,128)} copy(f32[35,96,32]{2,1,0:T(8,128)S(1)} %get-tuple-element.39) | data formatting | bytes 860160 | tf_op jit(solution)/shard_map/slice | solution.py:97
  19.4 1.4 %collective-permute-start.1 = (f32[35,96,32]{1,2,0:T(8,128)}, f32[35,96,32]{1,2,0:T(8,128)S(1)}, u32[]{:S(2)}, u32[]{:S(2)}) collective-permute-start(f32[35,96,32]{1,2,0:T(8,128)} %copy.27), channel_id=1, source_target_pairs={{0,2},{2,4},{4,6},{1,3},{3,5},{5,7},{8,10},{10,12},{12,14},{9,11},... | collective-permute-start | bytes 1290248 | tf_op jit(solution)/shard_map/ppermute | solution.py:98
  20.9 1.3 %copy.28 = f32[35,96,32]{1,2,0:T(8,128)} copy(f32[35,96,32]{2,1,0:T(8,128)S(1)} %get-tuple-element.40) | data formatting | bytes 860160 | tf_op jit(solution)/shard_map/slice | solution.py:99
  22.2 1.3 %collective-permute-start.2 = (f32[35,96,32]{1,2,0:T(8,128)}, f32[35,96,32]{1,2,0:T(8,128)S(1)}, u32[]{:S(2)}, u32[]{:S(2)}) collective-permute-start(f32[35,96,32]{1,2,0:T(8,128)} %copy.28), channel_id=1, source_target_pairs={{2,0},{4,2},{6,4},{3,1},{5,3},{7,5},{10,8},{12,10},{14,12},{11,9},... | collective-permute-start | bytes 1290248 | tf_op jit(solution)/shard_map/ppermute | solution.py:99
  23.5 0.1 broadcast_multiply_fusion.1
  23.6 1.0 fusion.24
  24.5 0.0 collective-permute-done.1
  24.5 1.7 %copy.29 = f32[35,96,32]{2,1,0:T(8,128)} copy(f32[35,96,32]{1,2,0:T(8,128)S(1)} %collective-permute-done.1) | data formatting | bytes 860160 | tf_op jit(solution)/shard_map/ppermute | solution.py:98
  26.3 1.7 %collective-permute-done.2 = f32[35,96,32]{1,2,0:T(8,128)S(1)} collective-permute-done((f32[35,96,32]{1,2,0:T(8,128)}, f32[35,96,32]{1,2,0:T(8,128)S(1)}, u32[]{:S(2)}, u32[]{:S(2)}) %collective-permute-start.2) | collective-permute-done | bytes 430112 | tf_op jit(solution)/shard_map/ppermute | solution.py:99
  28.0 1.7 %copy.30 = f32[35,96,32]{2,1,0:T(8,128)} copy(f32[35,96,32]{1,2,0:T(8,128)S(1)} %collective-permute-done.2) | data formatting | bytes 860160 | tf_op jit(solution)/shard_map/ppermute | solution.py:99
  29.7 3.9 %pad_maximum_fusion.stack_ref = f32[35,96,192]{2,1,0:T(8,128)S(1)} fusion(f32[35,96,32]{2,1,0:T(8,128)} %copy.30, f32[35,32,128]{2,1,0:T(8,128)} %copy-done.7, f32[3,32,128]{2,1,0:T(8,128)S(1)} %copy-done.14, f32[16,32,128]{2,1,0:T(8,128)} %copy-done.8, f32[16,32,128]{2,1,0:T(8,128)} %param.6, f32[35,32,128]{2,1,0:T(8,128)} %copy-done.6, f32[35,96,32]{2,1,0:T(8,128)} %copy.29), kind=kLoop, calls=%fused_computation | loop fusion | flops 3870720 | bytes 5160960 | tf_op jit(solution)/shard_map/concatenate | solution.py:100
  33.6 0.8 slice.271.current_ref
  34.4 1.3 %slice.272 = f32[16,36,132]{2,1,0:T(8,128)} slice(f32[35,96,192]{2,1,0:T(8,128)S(1)} %pad_maximum_fusion.stack_ref), slice={[0:16], [30:66], [30:162]} | slice | bytes 608256 | tf_op jit(solution)/shard_map/slice | solution.py:219
  35.7 8.8 %shard_map.64.fade_ref = f32[3,8,96,192]{3,2,1,0:T(8,128)} custom-call(f32[3,16]{1,0:T(4,128)} %table_ref.1, f32[35,96,192]{2,1,0:T(8,128)} %copy-done, f32[96,192]{1,0:T(8,128)} %broadcast_multiply_fusion.mask_ref), custom_call_target="tpu_custom_call" | custom-call | tf_op jit(solution)/shard_map/pallas_call | solution.py:189
  44.5 5.3 %shard_map.65 = (f32[3,80,176]{2,1,0:T(8,128)}, f32[3,8,32,128]{3,2,1,0:T(8,128)}) custom-call(f32[3,96,192]{2,1,0:T(8,128)} %slice.271.current_ref, f32[3,8,96,192]{3,2,1,0:T(8,128)} %shard_map.64.fade_ref), custom_call_target="tpu_custom_call" | custom-call | tf_op jit(solution)/shard_map/pallas_call | solution.py:138
  49.9 3.5 %collective-permute-start.4 = (f32[2,36,132]{2,1,0:T(8,128)S(1)}, f32[2,36,132]{2,1,0:T(8,128)S(1)}, u32[]{:S(2)}, u32[]{:S(2)}) collective-permute-start(f32[2,36,132]{2,1,0:T(8,128)S(1)} %get-tuple-element.44), channel_id=1, source_target_pairs={{0,8},{8,16},{16,24},{1,9},{9,17},{17,25},{2,10},{10,18},{18,26},{... | collective-permute-start | bytes 114056 | tf_op jit(solution)/shard_map/ppermute | solution.py:21
  53.4 0.1 exp.28
  53.5 2.3 %collective-permute-start.3 = (f32[2,36,132]{2,1,0:T(8,128)S(1)}, f32[2,36,132]{2,1,0:T(8,128)S(1)}, u32[]{:S(2)}, u32[]{:S(2)}) collective-permute-start(f32[2,36,132]{2,1,0:T(8,128)S(1)} %get-tuple-element.43), channel_id=1, source_target_pairs={{8,0},{16,8},{24,16},{9,1},{17,9},{25,17},{10,2},{18,10},{26,18},{... | collective-permute-start | bytes 114056 | tf_op jit(solution)/shard_map/ppermute | solution.py:24
  55.8 3.7 %collective-permute-start.5 = (f32[3,80,176]{2,1,0:T(8,128)}, f32[3,80,176]{2,1,0:T(8,128)S(1)}, u32[]{:S(2)}, u32[]{:S(2)}) collective-permute-start(f32[3,80,176]{2,1,0:T(8,128)} %get-tuple-element.13), channel_id=1, source_target_pairs={{0,8},{8,16},{16,24},{1,9},{9,17},{17,25},{2,10},{10,18},{18,26},{... | collective-permute-start | bytes 506888 | tf_op jit(solution)/shard_map/ppermute | solution.py:32
  59.5 0.0 collective-permute-done.4
  59.6 0.2 collective-permute-done.3
  59.8 5.2 %collective-permute-done.5 = f32[3,80,176]{2,1,0:T(8,128)S(1)} collective-permute-done((f32[3,80,176]{2,1,0:T(8,128)}, f32[3,80,176]{2,1,0:T(8,128)S(1)}, u32[]{:S(2)}, u32[]{:S(2)}) %collective-permute-start.5) | collective-permute-done | bytes 168992 | tf_op jit(solution)/shard_map/ppermute | solution.py:32
  65.0 1.8 %slice_select_fusion.current_ref = f32[3,80,176]{2,1,0:T(8,128)} fusion(f32[3,80,176]{2,1,0:T(8,128)S(1)} %collective-permute-done.5, f32[35,96,192]{2,1,0:T(8,128)} %copy-done, pred[]{:T(512)S(6)} %eq.140), kind=kLoop, calls=%fused_computation.43 | loop fusion | flops 42240 | bytes 506881 | tf_op jit(solution)/shard_map/jit(_where)/select_n | solution.py:247
  66.8 6.3 %shard_map.66 = (f32[3,64,160]{2,1,0:T(8,128)}, f32[3,8,32,128]{3,2,1,0:T(8,128)}) custom-call(f32[3,80,176]{2,1,0:T(8,128)} %slice_select_fusion.current_ref, f32[3,8,96,192]{3,2,1,0:T(8,128)} %shard_map.64.fade_ref), custom_call_target="tpu_custom_call" | custom-call | tf_op jit(solution)/shard_map/pallas_call | solution.py:138
  73.1 3.5 %collective-permute-start.6 = (f32[3,64,160]{2,1,0:T(8,128)}, f32[3,64,160]{2,1,0:T(8,128)S(1)}, u32[]{:S(2)}, u32[]{:S(2)}) collective-permute-start(f32[3,64,160]{2,1,0:T(8,128)} %get-tuple-element.14), channel_id=1, source_target_pairs={{0,8},{8,16},{16,24},{1,9},{9,17},{17,25},{2,10},{10,18},{18,26},{... | collective-permute-start | bytes 368648 | tf_op jit(solution)/shard_map/ppermute | solution.py:32
  76.6 1.1 multiply_multiply_fusion.1
  77.8 3.1 %collective-permute-done.6 = f32[3,64,160]{2,1,0:T(8,128)S(1)} collective-permute-done((f32[3,64,160]{2,1,0:T(8,128)}, f32[3,64,160]{2,1,0:T(8,128)S(1)}, u32[]{:S(2)}, u32[]{:S(2)}) %collective-permute-start.6) | collective-permute-done | bytes 122912 | tf_op jit(solution)/shard_map/ppermute | solution.py:32
  80.9 1.7 %slice_select_fusion.1.current_ref = f32[3,64,160]{2,1,0:T(8,128)} fusion(f32[3,64,160]{2,1,0:T(8,128)S(1)} %collective-permute-done.6, f32[35,96,192]{2,1,0:T(8,128)} %copy-done, pred[]{:T(512)S(6)} %eq.140), kind=kLoop, calls=%fused_computation.44 | loop fusion | flops 30720 | bytes 368641 | tf_op jit(solution)/shard_map/jit(_where)/select_n | solution.py:247
  82.6 5.8 %shard_map.67 = (f32[3,48,144]{2,1,0:T(8,128)}, f32[3,8,32,128]{3,2,1,0:T(8,128)}) custom-call(f32[3,64,160]{2,1,0:T(8,128)} %slice_select_fusion.1.current_ref, f32[3,8,96,192]{3,2,1,0:T(8,128)} %shard_map.64.fade_ref), custom_call_target="tpu_custom_call" | custom-call | tf_op jit(solution)/shard_map/pallas_call | solution.py:138
  88.4 3.5 %collective-permute-start.7 = (f32[3,48,144]{2,1,0:T(8,128)}, f32[3,48,144]{2,1,0:T(8,128)S(1)}, u32[]{:S(2)}, u32[]{:S(2)}) collective-permute-start(f32[3,48,144]{2,1,0:T(8,128)} %get-tuple-element.15), channel_id=1, source_target_pairs={{0,8},{8,16},{16,24},{1,9},{9,17},{17,25},{2,10},{10,18},{18,26},{... | collective-permute-start | bytes 248840 | tf_op jit(solution)/shard_map/ppermute | solution.py:32
  91.9 1.6 %fusion.8 = f32[16,32,128]{2,1,0:T(8,128)} fusion(f32[18,34,130]{2,1,0:T(8,128)S(1)} %get-tuple-element.42, f32[18,34,130]{2,1,0:T(8,128)S(1)} %get-tuple-element.41), kind=kLoop, calls=%fused_computation.24 | loop fusion | flops 1245184 | bytes 3932160 | tf_op jit(solution)/shard_map/add | solution.py:65
  93.5 2.1 %collective-permute-done.7 = f32[3,48,144]{2,1,0:T(8,128)S(1)} collective-permute-done((f32[3,48,144]{2,1,0:T(8,128)}, f32[3,48,144]{2,1,0:T(8,128)S(1)}, u32[]{:S(2)}, u32[]{:S(2)}) %collective-permute-start.7) | collective-permute-done | bytes 82976 | tf_op jit(solution)/shard_map/ppermute | solution.py:32
  95.6 1.7 %slice_select_fusion.2.current_ref = f32[3,48,144]{2,1,0:T(8,128)} fusion(f32[3,48,144]{2,1,0:T(8,128)S(1)} %collective-permute-done.7, f32[35,96,192]{2,1,0:T(8,128)} %copy-done, pred[]{:T(512)S(6)} %eq.140), kind=kLoop, calls=%fused_computation.45 | loop fusion | flops 20736 | bytes 248833 | tf_op jit(solution)/shard_map/jit(_where)/select_n | solution.py:247
  97.3 5.2 %shard_map.68 = (f32[3,32,128]{2,1,0:T(8,128)}, f32[3,8,32,128]{3,2,1,0:T(8,128)}) custom-call(f32[3,48,144]{2,1,0:T(8,128)} %slice_select_fusion.2.current_ref, f32[3,8,96,192]{3,2,1,0:T(8,128)} %shard_map.64.fade_ref), custom_call_target="tpu_custom_call" | custom-call | tf_op jit(solution)/shard_map/pallas_call | solution.py:138
  102.5 1.1 mul.237
  103.6 1.5 %fusion.3 = f32[3,16,32]{2,1,0:T(8,128)S(1)} fusion(f32[7,16,32,128]{3,2,1,0:T(8,128)S(1)} %copy-done.4, f32[3,16,32,128]{3,2,1,0:T(8,128)S(1)} %bitcast.56, f32[3,16,32,128]{3,2,1,0:T(8,128)S(1)} %bitcast.54, f32[16,32,128]{2,1,0:T(8,128)S(1)} %copy-done.12, f32[16,32,128]{2,1,0:T(8,128)} %fusion.8, f32[16,32,128]{2,1,0:T(8,128)S(1)} %copy-done.11, ...), kind=kLoop, calls=%fused_computation.11 | loop fusion | flops 1964544 | bytes 4200448 | tf_op jit(solution)/shard_map/reduce_sum | solution.py:264
  105.1 0.1 concatenate.40
  105.2 2.8 %collective-permute-start.8 = (f32[4,2,128]{2,1,0:T(2,128)S(1)}, f32[4,2,128]{2,1,0:T(2,128)S(1)}, u32[]{:S(2)}, u32[]{:S(2)}) collective-permute-start(f32[4,2,128]{2,1,0:T(2,128)S(1)} %bitcast.62), channel_id=1, source_target_pairs={{0,2},{2,0},{4,6},{6,4},{1,3},{3,1},{5,7},{7,5},{8,10},{10,8},{12,... | collective-permute-start | bytes 12296 | tf_op jit(solution)/shard_map/ppermute | solution.py:42
  108.0 0.8 collective-permute-done.8
  108.9 4.3 %collective-permute-start.9 = (f32[4,1,128]{2,0,1:T(4,128)S(1)}, f32[4,1,128]{2,0,1:T(4,128)S(1)}, u32[]{:S(2)}, u32[]{:S(2)}) collective-permute-start(f32[4,1,128]{2,0,1:T(4,128)S(1)} %bitcast.63), channel_id=1, source_target_pairs={{0,4},{4,0},{2,6},{6,2},{1,5},{5,1},{3,7},{7,3},{8,12},{12,8},{10,... | collective-permute-start | bytes 6152 | tf_op jit(solution)/shard_map/ppermute | solution.py:42
  113.2 1.6 %collective-permute-done.9 = f32[4,1,128]{2,0,1:T(4,128)S(1)} collective-permute-done((f32[4,1,128]{2,0,1:T(4,128)S(1)}, f32[4,1,128]{2,0,1:T(4,128)S(1)}, u32[]{:S(2)}, u32[]{:S(2)}) %collective-permute-start.9) | collective-permute-done | bytes 2080 | tf_op jit(solution)/shard_map/ppermute | solution.py:42
  114.8 0.1 reshape_squeeze.4
  114.9 0.1 sub.70
  114.9 0.6 pad_maximum_fusion.5
  (55 shorter events, 0.3 us)
Async XLA Ops:
  0.0 3.8 %copy-start.13 = (s32[16,32,128]{2,1,0:T(8,128)S(1)}, s32[16,32,128]{2,1,0:T(8,128)}, u32[]{:S(2)}) copy-start(s32[16,32,128]{2,1,0:T(8,128)} %param.7) | copy-start | bytes 786436
  0.0 4.5 %copy-start.15 = (f32[3,16]{1,0:T(4,128)S(1)}, f32[3,16]{1,0:T(4,128)}, u32[]{:S(2)}) copy-start(f32[3,16]{1,0:T(4,128)} %table_ref.1) | copy-start | bytes 580
  0.0 4.5 %copy-start.17 = (f32[16]{0:T(128)S(1)}, f32[16]{0:T(128)}, u32[]{:S(2)}) copy-start(f32[16]{0:T(128)} %param.9) | copy-start | bytes 196
  0.0 4.5 %copy-start.16 = (f32[3,16]{1,0:T(4,128)S(1)}, f32[3,16]{1,0:T(4,128)}, u32[]{:S(2)}) copy-start(f32[3,16]{1,0:T(4,128)} %param.11) | copy-start | bytes 580
  1.0 16.1 %copy-start.8 = (f32[16,32,128]{2,1,0:T(8,128)}, f32[16,32,128]{2,1,0:T(8,128)S(1)}, u32[]{:S(2)}) copy-start(f32[16,32,128]{2,1,0:T(8,128)S(1)} %convert_element_type.39) | copy-start | bytes 786436
  2.2 14.8 %collective-permute-start = (f32[35,32,128]{2,1,0:T(8,128)S(1)}, f32[35,32,128]{2,1,0:T(8,128)S(1)}, u32[]{:S(2)}, u32[]{:S(2)}) collective-permute-start(f32[35,32,128]{2,1,0:T(8,128)S(1)} %pad_maximum_fusion.4), channel_id=1, source_target_pairs={{0,1},{1,0},{2,3},{3,2},{4,5},{5,4},{6,7},{7,6},{8,9},{9,8},{10,11... | collective-permute-start | bytes 1720328 | tf_op jit(solution)/shard_map/ppermute | solution.py:87
  3.8 3.8 %copy-start.1 = (f32[16,32,128]{2,1,0:T(8,128)S(1)}, f32[16,32,128]{2,1,0:T(8,128)}, u32[]{:S(2)}) copy-start(f32[16,32,128]{2,1,0:T(8,128)} %param.6) | copy-start | bytes 786436
  7.5 9.6 %copy-start.3 = (f32[7,16,32,128]{3,2,1,0:T(8,128)}, f32[7,16,32,128]{3,2,1,0:T(8,128)S(1)}, u32[]{:S(2)}) copy-start(f32[7,16,32,128]{3,2,1,0:T(8,128)S(1)} %select_select_fusion) | copy-start | bytes 5505028
  10.1 7.0 %copy-start.14 = (f32[3,32,128]{2,1,0:T(8,128)S(1)}, f32[3,32,128]{2,1,0:T(8,128)}, u32[]{:S(2)}) copy-start(f32[3,32,128]{2,1,0:T(8,128)} %param.8) | copy-start | bytes 147460
  17.1 0.8 copy-start.6
  17.1 1.0 copy-start.7
  19.4 4.1 %copy-start.10 = (f32[3,16,32,128]{3,2,1,0:T(8,128)S(1)}, f32[3,16,32,128]{3,2,1,0:T(8,128)}, u32[]{:S(2)}) copy-start(f32[3,16,32,128]{3,2,1,0:T(8,128)} %slice_multiply_fusion) | copy-start | bytes 2359300
  19.4 5.1 %collective-permute-start.1 = (f32[35,96,32]{1,2,0:T(8,128)}, f32[35,96,32]{1,2,0:T(8,128)S(1)}, u32[]{:S(2)}, u32[]{:S(2)}) collective-permute-start(f32[35,96,32]{1,2,0:T(8,128)} %copy.27), channel_id=1, source_target_pairs={{0,2},{2,4},{4,6},{1,3},{3,5},{5,7},{8,10},{10,12},{12,14},{9,11},... | collective-permute-start | bytes 1290248 | tf_op jit(solution)/shard_map/ppermute | solution.py:98
  22.2 5.8 %collective-permute-start.2 = (f32[35,96,32]{1,2,0:T(8,128)}, f32[35,96,32]{1,2,0:T(8,128)S(1)}, u32[]{:S(2)}, u32[]{:S(2)}) collective-permute-start(f32[35,96,32]{1,2,0:T(8,128)} %copy.28), channel_id=1, source_target_pairs={{2,0},{4,2},{6,4},{3,1},{5,3},{7,5},{10,8},{12,10},{14,12},{11,9},... | collective-permute-start | bytes 1290248 | tf_op jit(solution)/shard_map/ppermute | solution.py:99
  33.6 2.1 %copy-start = (f32[35,96,192]{2,1,0:T(8,128)}, f32[35,96,192]{2,1,0:T(8,128)S(1)}, u32[]{:S(2)}) copy-start(f32[35,96,192]{2,1,0:T(8,128)S(1)} %pad_maximum_fusion.stack_ref) | copy-start | bytes 7741444
  44.5 5.3 %copy-start.5 = (f32[16,36,132]{2,1,0:T(8,128)S(1)}, f32[16,36,132]{2,1,0:T(8,128)}, u32[]{:S(2)}) copy-start(f32[16,36,132]{2,1,0:T(8,128)} %slice.272) | copy-start | bytes 912388
  49.9 9.6 %collective-permute-start.4 = (f32[2,36,132]{2,1,0:T(8,128)S(1)}, f32[2,36,132]{2,1,0:T(8,128)S(1)}, u32[]{:S(2)}, u32[]{:S(2)}) collective-permute-start(f32[2,36,132]{2,1,0:T(8,128)S(1)} %get-tuple-element.44), channel_id=1, source_target_pairs={{0,8},{8,16},{16,24},{1,9},{9,17},{17,25},{2,10},{10,18},{18,26},{... | collective-permute-start | bytes 114056 | tf_op jit(solution)/shard_map/ppermute | solution.py:21
  53.5 6.3 %collective-permute-start.3 = (f32[2,36,132]{2,1,0:T(8,128)S(1)}, f32[2,36,132]{2,1,0:T(8,128)S(1)}, u32[]{:S(2)}, u32[]{:S(2)}) collective-permute-start(f32[2,36,132]{2,1,0:T(8,128)S(1)} %get-tuple-element.43), channel_id=1, source_target_pairs={{8,0},{16,8},{24,16},{9,1},{17,9},{25,17},{10,2},{18,10},{26,18},{... | collective-permute-start | bytes 114056 | tf_op jit(solution)/shard_map/ppermute | solution.py:24
  55.8 9.2 %collective-permute-start.5 = (f32[3,80,176]{2,1,0:T(8,128)}, f32[3,80,176]{2,1,0:T(8,128)S(1)}, u32[]{:S(2)}, u32[]{:S(2)}) collective-permute-start(f32[3,80,176]{2,1,0:T(8,128)} %get-tuple-element.13), channel_id=1, source_target_pairs={{0,8},{8,16},{16,24},{1,9},{9,17},{17,25},{2,10},{10,18},{18,26},{... | collective-permute-start | bytes 506888 | tf_op jit(solution)/shard_map/ppermute | solution.py:32
  73.1 7.8 %collective-permute-start.6 = (f32[3,64,160]{2,1,0:T(8,128)}, f32[3,64,160]{2,1,0:T(8,128)S(1)}, u32[]{:S(2)}, u32[]{:S(2)}) collective-permute-start(f32[3,64,160]{2,1,0:T(8,128)} %get-tuple-element.14), channel_id=1, source_target_pairs={{0,8},{8,16},{16,24},{1,9},{9,17},{17,25},{2,10},{10,18},{18,26},{... | collective-permute-start | bytes 368648 | tf_op jit(solution)/shard_map/ppermute | solution.py:32
  88.4 7.2 %collective-permute-start.7 = (f32[3,48,144]{2,1,0:T(8,128)}, f32[3,48,144]{2,1,0:T(8,128)S(1)}, u32[]{:S(2)}, u32[]{:S(2)}) collective-permute-start(f32[3,48,144]{2,1,0:T(8,128)} %get-tuple-element.15), channel_id=1, source_target_pairs={{0,8},{8,16},{16,24},{1,9},{9,17},{17,25},{2,10},{10,18},{18,26},{... | collective-permute-start | bytes 248840 | tf_op jit(solution)/shard_map/ppermute | solution.py:32
  97.3 6.3 %copy-start.2 = (f32[16,32,128]{2,1,0:T(8,128)S(1)}, f32[16,32,128]{2,1,0:T(8,128)}, u32[]{:S(2)}) copy-start(f32[16,32,128]{2,1,0:T(8,128)} %param.6) | copy-start | bytes 786436
  97.3 6.3 %copy-start.4 = (f32[7,16,32,128]{3,2,1,0:T(8,128)S(1)}, f32[7,16,32,128]{3,2,1,0:T(8,128)}, u32[]{:S(2)}) copy-start(f32[7,16,32,128]{3,2,1,0:T(8,128)} %copy-done.3) | copy-start | bytes 5505028
  97.3 6.3 %copy-start.9 = (f32[3,8,2,32,128]{4,3,2,1,0:T(8,128)S(1)}, f32[3,8,2,32,128]{4,3,2,1,0:T(8,128)}, u32[]{:S(2)}) copy-start(f32[3,8,2,32,128]{4,3,2,1,0:T(8,128)} %fusion.24) | copy-start | bytes 2359300
  97.3 6.3 %copy-start.11 = (f32[16,32,128]{2,1,0:T(8,128)S(1)}, f32[16,32,128]{2,1,0:T(8,128)}, u32[]{:S(2)}) copy-start(f32[16,32,128]{2,1,0:T(8,128)} %get-tuple-element.38) | copy-start | bytes 786436
  97.3 6.3 %copy-start.12 = (f32[16,32,128]{2,1,0:T(8,128)S(1)}, f32[16,32,128]{2,1,0:T(8,128)}, u32[]{:S(2)}) copy-start(f32[16,32,128]{2,1,0:T(8,128)} %fusion) | copy-start | bytes 786436
  105.2 3.7 %collective-permute-start.8 = (f32[4,2,128]{2,1,0:T(2,128)S(1)}, f32[4,2,128]{2,1,0:T(2,128)S(1)}, u32[]{:S(2)}, u32[]{:S(2)}) collective-permute-start(f32[4,2,128]{2,1,0:T(2,128)S(1)} %bitcast.62), channel_id=1, source_target_pairs={{0,2},{2,0},{4,6},{6,4},{1,3},{3,1},{5,7},{7,5},{8,10},{10,8},{12,... | collective-permute-start | bytes 12296 | tf_op jit(solution)/shard_map/ppermute | solution.py:42
  108.9 5.8 %collective-permute-start.9 = (f32[4,1,128]{2,0,1:T(4,128)S(1)}, f32[4,1,128]{2,0,1:T(4,128)S(1)}, u32[]{:S(2)}, u32[]{:S(2)}) collective-permute-start(f32[4,1,128]{2,0,1:T(4,128)S(1)} %bitcast.63), channel_id=1, source_target_pairs={{0,4},{4,0},{2,6},{6,2},{1,5},{5,1},{3,7},{7,3},{8,12},{12,8},{10,... | collective-permute-start | bytes 6152 | tf_op jit(solution)/shard_map/ppermute | solution.py:42

commit v17 on v15

--- a/solution.py
+++ b/solution.py
@@ -113,6 +113,41 @@
     )
 
 
+def halo_plane(stack, width):
+    planes, size_a, size_v = stack.shape
+    n_view = lax.axis_size("view")
+    first = lax.axis_index("across") == 0
+
+    def for_partner(block):
+        if width >= size_a:
+            return block
+        return jnp.where(first, block[:, size_a - width :], block[:, :width])
+
+    swap = [(0, 1), (1, 0)]
+    forward = [(v, v + 1) for v in range(n_view - 1)]
+    backward = [(target, source) for source, target in forward]
+    diagonal_forward = [(v * 2 + a, (v + 1) * 2 + 1 - a) for a in range(2) for v in range(n_view - 1)]
+    diagonal_backward = [(target, source) for source, target in diagonal_forward]
+    left = stack[:, :, size_v - width :]
+    right = stack[:, :, :width]
+    centre_other = lax.ppermute(for_partner(stack), "across", swap)
+    left_own = lax.ppermute(left, "view", forward)
+    right_own = lax.ppermute(right, "view", backward)
+    left_other = lax.ppermute(for_partner(left), ("view", "across"), diagonal_forward)
+    right_other = lax.ppermute(for_partner(right), ("view", "across"), diagonal_backward)
+
+    def column(own, other):
+        empty = jnp.zeros_like(other)
+        return jnp.concatenate(
+            [jnp.where(first, empty, other), own, jnp.where(first, other, empty)], axis=1
+        )
+
+    return jnp.concatenate(
+        [column(left_own, left_other), column(stack, centre_other), column(right_own, right_other)],
+        axis=2,
+    )
+
+
 def propagate(current, border_in, fade_rim, brick_a, brick_v):
     widest = (fade_rim.shape[2] - brick_a) // 2
     starts = []
@@ -197,7 +232,10 @@
     across_idx = lax.axis_index("across")
     widest = SLABS * n_light
     stack = jnp.concatenate([density, labels.astype(jnp.float32), sunlight], axis=0)
-    stack_rim = halo(halo(stack, "across", 1, widest), "view", 2, widest)
+    if n_across == 2 and widest <= brick_a and widest <= brick_v:
+        stack_rim = halo_plane(stack, widest)
+    else:
+        stack_rim = halo(halo(stack, "across", 1, widest), "view", 2, widest)
     density_rim = stack_rim[:brick_l]
     sun_rim = stack_rim[2 * brick_l :]
     density_side = density_rim[

time: 104 us -> 114 us (1.096)
  waiting for transfers between devices: 20.5 us -> 27.1 us
  local copies, waits for them, and re-layouts: 11.9 us -> 15.5 us
    ppermute x3 -> x5, starting transfers between devices: 4.49 us -> 10.4 us  [the longest x1 3.8 us: halo_plane(): left_own = lax.ppermute(left, 'view', forward)]
    ppermute x2, starting transfers between devices: 7.08 us -> 1.13 us  [from_partner(): return lax.ppermute(block, axis, route)]
    ppermute x2 -> x4, local copies, waits for them, and re-layouts: 3.45 us -> 7.93 us  [the longest x1 2.35 us: halo_plane(): left_own = lax.ppermute(left, 'view', forward)]
    ppermute x3 -> x5, waiting for transfers between devices: 7.41 us -> 10.3 us  [the longest x1 10.3 us: halo_plane(): lax.ppermute(for_partner(left), ('view', 'across'), diagonal_forward)]
    ppermute x3, waiting for transfers between devices: 10.3 us -> 11.9 us  [from_behind(): lax.ppermute(value, axis, [(source, source + steps) for source in range(l...]
    slice x3, local copies, waits for them, and re-layouts: 3.24 us -> 1.88 us  [the longest x1 1.23 us: halo_plane(): right = stack[:, :, :width]]
    ppermute x2, waiting for transfers between devices: 2.39 us -> 3.71 us  [from_partner(): return lax.ppermute(block, axis, route)]
    unnamed x48 -> x50, local copies, waits for them, and re-layouts: 2.76 us -> 3.23 us
  transfers between devices with their start and end apart: 10 -> 12, of which waited for: 8 -> 7; matrix products, arithmetic and copies ran while one was open for 13% -> 18% of each run, Pallas kernels for 0% -> 0%
where the time goes in v17:
time: 114 us; the launch traced here: 113 us
  other arithmetic  31.3 us (27%)
  starting transfers between devices  28.1 us (25%)
  waiting for transfers between devices  27.1 us (24%)
  local copies, waits for them, and re-layouts  15.5 us (14%)
  Pallas kernels  8.82 us (8%)
    mul x31, other arithmetic, propagate(): current = current * fade_here  14.7 us
    ppermute x3, waiting for transfers between devices, from_behind(): lax.ppermute(value, axis, [(source, source + steps) for source in range(l...  11.9 us
    ppermute x3, starting transfers between devices, from_behind(): lax.ppermute(value, axis, [(source, source + steps) for source in range(l...  10.7 us
    ppermute x1, waiting for transfers between devices, halo_plane(): lax.ppermute(for_partner(left), ('view', 'across'), diagonal_forward)  10.3 us
    pallas_call x1, Pallas kernels, fade_rim_of(): pl.pallas_call(kernel, out_shape=jax.ShapeDtypeStruct((colours, SLABS, ri...  8.82 us
    concatenate x1, other arithmetic, halo_plane(): jnp.concatenate([column(left_own, left_other), column(stack, centre_other...  3.94 us
    ppermute x1, starting transfers between devices, halo_plane(): left_own = lax.ppermute(left, 'view', forward)  3.8 us
    ppermute x2, waiting for transfers between devices, from_partner(): return lax.ppermute(block, axis, route)  3.71 us
  transfers between devices with their start and end apart: 12, of which 7 were waited for; matrix products, arithmetic and copies ran while one was open for 18% of the time, Pallas kernels for 0%

profile of v17, /device:TPU:16, one launch (start us, length us, event | category | flops | bytes accessed | tf_op | source)
XLA Modules:
  0.0 112.5 jit_solution(8350234779743568401)
XLA Ops:
  0.0 1.0 convert_element_type.39
  1.0 1.1 pad_maximum_fusion.2
  2.1 1.6 %collective-permute-start.2 = (f32[35,32,128]{2,1,0:T(8,128)S(1)}, f32[35,32,128]{2,1,0:T(8,128)S(1)}, u32[]{:S(2)}, u32[]{:S(2)}) collective-permute-start(f32[35,32,128]{2,1,0:T(8,128)S(1)} %pad_maximum_fusion.2), channel_id=1, source_target_pairs={{0,1},{1,0},{2,3},{3,2},{4,5},{5,4},{6,7},{7,6},{8,9},{9,8},{10,11... | collective-permute-start | bytes 1720328 | tf_op jit(solution)/shard_map/ppermute | solution.py:133
  4.0 0.4 copy.176
  4.4 2.4 %collective-permute-start = (f32[35,32,32]{0,2,1:T(8,128)S(1)}, f32[35,32,32]{0,2,1:T(8,128)}, u32[]{:S(2)}, u32[]{:S(2)}) collective-permute-start(f32[35,32,32]{0,2,1:T(8,128)S(1)} %copy.176), channel_id=1, source_target_pairs={{0,3},{2,5},{4,7},{1,2},{3,4},{5,6},{8,11},{10,13},{12,15},{9,10},... | collective-permute-start | bytes 430088 | tf_op jit(solution)/shard_map/ppermute | solution.py:136
  6.8 3.8 %collective-permute-start.1 = (f32[35,32,32]{0,2,1:T(8,128)S(1)}, f32[35,32,32]{0,2,1:T(8,128)}, u32[]{:S(2)}, u32[]{:S(2)}) collective-permute-start(f32[35,32,32]{0,2,1:T(8,128)S(1)} %copy.176), channel_id=1, source_target_pairs={{0,2},{2,4},{4,6},{1,3},{3,5},{5,7},{8,10},{10,12},{12,14},{9,11},... | collective-permute-start | bytes 430088 | tf_op jit(solution)/shard_map/ppermute | solution.py:134
  10.5 1.2 %copy.181 = f32[35,32,32]{0,2,1:T(8,128)} copy(f32[35,32,32]{2,1,0:T(8,128)S(1)} %get-tuple-element.52) | data formatting | bytes 286720 | tf_op jit(solution)/shard_map/slice | solution.py:132
  11.8 1.4 %collective-permute-start.3 = (f32[35,32,32]{0,2,1:T(8,128)}, f32[35,32,32]{0,2,1:T(8,128)}, u32[]{:S(2)}, u32[]{:S(2)}) collective-permute-start(f32[35,32,32]{0,2,1:T(8,128)} %copy.181), channel_id=1, source_target_pairs={{3,0},{5,2},{7,4},{2,1},{4,3},{6,5},{11,8},{13,10},{15,12},{10,9},... | collective-permute-start | bytes 430088 | tf_op jit(solution)/shard_map/ppermute | solution.py:137
  13.2 1.3 %collective-permute-start.4 = (f32[35,32,32]{0,2,1:T(8,128)}, f32[35,32,32]{0,2,1:T(8,128)}, u32[]{:S(2)}, u32[]{:S(2)}) collective-permute-start(f32[35,32,32]{0,2,1:T(8,128)} %copy.181), channel_id=1, source_target_pairs={{2,0},{4,2},{6,4},{3,1},{5,3},{7,5},{10,8},{12,10},{14,12},{11,9},... | collective-permute-start | bytes 430088 | tf_op jit(solution)/shard_map/ppermute | solution.py:135
  14.5 0.6 broadcast_compare_fusion.14
  15.2 0.4 slice_reduce_fusion.15
  15.6 2.6 %select_select_fusion = f32[7,16,32,128]{3,2,1,0:T(8,128)S(1)} fusion(f32[7]{0:T(128)S(1)} %get-tuple-element.10, f32[7]{0:T(128)S(1)} %get-tuple-element.11, f32[7]{0:T(128)S(1)} %get-tuple-element.12, f32[7]{0:T(128)S(1)} %get-tuple-element.13, f32[7]{0:T(128)S(1)} %get-tuple-element.14, f32[7]{0:T(128)S(1)} %get-tuple-element.15, ...), kind=kLoop, calls=%fused_computation.1 | loop fusion | flops 6881280 | bytes 2818496 | tf_op jit(solution)/shard_map/jit(_where)/select_n | solution.py:247
  18.3 0.9 fusion.151
  19.3 0.3 copy-done.2
  19.6 1.0 fusion
  20.7 1.0 fusion.164
  21.6 0.7 broadcast_multiply_fusion.mask_ref
  22.4 10.3 %collective-permute-done = f32[35,32,32]{0,2,1:T(8,128)} collective-permute-done((f32[35,32,32]{0,2,1:T(8,128)S(1)}, f32[35,32,32]{0,2,1:T(8,128)}, u32[]{:S(2)}, u32[]{:S(2)}) %collective-permute-start) | collective-permute-done | bytes 143392 | tf_op jit(solution)/shard_map/ppermute | solution.py:136
  32.7 1.6 %copy.177 = f32[35,32,32]{2,1,0:T(8,128)S(1)} copy(f32[35,32,32]{0,2,1:T(8,128)} %collective-permute-done) | data formatting | bytes 286720 | tf_op jit(solution)/shard_map/ppermute | solution.py:136
  34.3 1.6 %copy.182 = f32[35,32,32]{2,1,0:T(8,128)S(1)} copy(f32[35,32,32]{0,2,1:T(8,128)} %collective-permute-done.3) | data formatting | bytes 286720 | tf_op jit(solution)/shard_map/ppermute | solution.py:137
  35.9 2.4 %copy.180 = f32[35,32,32]{2,1,0:T(8,128)} copy(f32[35,32,32]{0,2,1:T(8,128)} %collective-permute-done.1) | data formatting | bytes 286720 | tf_op jit(solution)/shard_map/ppermute | solution.py:134
  38.3 2.4 %copy.185 = f32[35,32,32]{2,1,0:T(8,128)} copy(f32[35,32,32]{0,2,1:T(8,128)} %collective-permute-done.4) | data formatting | bytes 286720 | tf_op jit(solution)/shard_map/ppermute | solution.py:135
  41.1 0.5 copy-done.5
  42.0 3.9 %maximum_maximum_fusion.stack_ref = f32[35,96,192]{2,1,0:T(8,128)S(1)} fusion(f32[35,32,32]{2,1,0:T(8,128)S(1)} %get-tuple-element.56, f32[35,32,32]{2,1,0:T(8,128)S(1)} %copy-done.12, f32[35,32,32]{2,1,0:T(8,128)S(1)} %get-tuple-element.55, f32[35,32,128]{2,1,0:T(8,128)S(1)} %get-tuple-element.54, f32[3,32,128]{2,1,0:T(8,128)S(1)} %copy-done.16, ...), kind=kLoop, calls=%fused_computation | loop fusion | flops 6451200 | bytes 5160960 | tf_op jit(solution)/shard_map/concatenate | solution.py:145
  46.0 1.3 %slice.1096 = f32[16,36,132]{2,1,0:T(8,128)} slice(f32[35,96,192]{2,1,0:T(8,128)S(1)} %maximum_maximum_fusion.stack_ref), slice={[0:16], [30:66], [30:162]} | slice | bytes 608256 | tf_op jit(solution)/shard_map/slice | solution.py:241
  47.3 0.7 copy-done.1
  48.0 8.8 %shard_map.64 = f32[3,8,96,192]{3,2,1,0:T(8,128)} custom-call(f32[3,16]{1,0:T(4,128)} %table_ref.1, f32[35,96,192]{2,1,0:T(8,128)} %copy-done.1, f32[96,192]{1,0:T(8,128)} %broadcast_multiply_fusion.mask_ref), custom_call_target="tpu_custom_call" | custom-call | tf_op jit(solution)/shard_map/pallas_call | solution.py:208
  56.8 1.2 %fusion.17 = f32[3,96,192]{2,1,0:T(8,128)S(1)} fusion(f32[3,8,96,192]{3,2,1,0:T(8,128)} %shard_map.64, f32[35,96,192]{2,1,0:T(8,128)} %copy-done.1), kind=kLoop, calls=%fused_computation.42 | loop fusion | flops 55296 | bytes 663552 | tf_op jit(solution)/shard_map/mul | solution.py:164
  58.1 1.4 %fusion.13 = f32[3,94,190]{2,1,0:T(8,128)S(1)} fusion(f32[3,8,96,192]{3,2,1,0:T(8,128)} %shard_map.64, f32[3,96,192]{2,1,0:T(8,128)S(1)} %fusion.17), kind=kLoop, calls=%fused_computation.34 | loop fusion | flops 428640 | bytes 1500240 | tf_op jit(solution)/shard_map/mul | solution.py:164
  59.5 0.4 fusion.9
  60.0 0.4 fusion.5
  60.4 0.4 fusion.30
  60.8 0.4 fusion.26
  61.3 0.4 fusion.22
  61.7 0.4 fusion.18
  62.1 0.3 fusion.56
  62.5 3.5 %collective-permute-start.6 = (f32[2,36,132]{2,1,0:T(8,128)S(1)}, f32[2,36,132]{2,1,0:T(8,128)S(1)}, u32[]{:S(2)}, u32[]{:S(2)}) collective-permute-start(f32[2,36,132]{2,1,0:T(8,128)S(1)} %get-tuple-element.48), channel_id=1, source_target_pairs={{0,8},{8,16},{16,24},{1,9},{9,17},{17,25},{2,10},{10,18},{18,26},{... | collective-permute-start | bytes 114056 | tf_op jit(solution)/shard_map/ppermute | solution.py:21
  66.1 2.3 %collective-permute-start.5 = (f32[2,36,132]{2,1,0:T(8,128)S(1)}, f32[2,36,132]{2,1,0:T(8,128)S(1)}, u32[]{:S(2)}, u32[]{:S(2)}) collective-permute-start(f32[2,36,132]{2,1,0:T(8,128)S(1)} %get-tuple-element.47), channel_id=1, source_target_pairs={{8,0},{16,8},{24,16},{9,1},{17,9},{25,17},{10,2},{18,10},{26,18},{... | collective-permute-start | bytes 114056 | tf_op jit(solution)/shard_map/ppermute | solution.py:24
  68.4 3.5 %collective-permute-start.7 = (f32[3,80,176]{2,1,0:T(8,128)S(1)}, f32[3,80,176]{2,1,0:T(8,128)S(1)}, u32[]{:S(2)}, u32[]{:S(2)}) collective-permute-start(f32[3,80,176]{2,1,0:T(8,128)S(1)} %fusion.56), channel_id=1, source_target_pairs={{0,8},{8,16},{16,24},{1,9},{9,17},{17,25},{2,10},{10,18},{18,26},{... | collective-permute-start | bytes 506888 | tf_op jit(solution)/shard_map/ppermute | solution.py:32
  72.0 1.2 %collective-permute-done.5 = f32[2,36,132]{2,1,0:T(8,128)S(1)} collective-permute-done((f32[2,36,132]{2,1,0:T(8,128)S(1)}, f32[2,36,132]{2,1,0:T(8,128)S(1)}, u32[]{:S(2)}, u32[]{:S(2)}) %collective-permute-start.5) | collective-permute-done | bytes 38048 | tf_op jit(solution)/shard_map/ppermute | solution.py:24
  73.2 5.6 %collective-permute-done.7 = f32[3,80,176]{2,1,0:T(8,128)S(1)} collective-permute-done((f32[3,80,176]{2,1,0:T(8,128)S(1)}, f32[3,80,176]{2,1,0:T(8,128)S(1)}, u32[]{:S(2)}, u32[]{:S(2)}) %collective-permute-start.7) | collective-permute-done | bytes 168992 | tf_op jit(solution)/shard_map/ppermute | solution.py:32
  78.8 1.1 %fusion.53 = f32[3,80,176]{2,1,0:T(8,128)S(1)} fusion(f32[3,8,96,192]{3,2,1,0:T(8,128)S(1)} %copy-done, f32[3,80,176]{2,1,0:T(8,128)S(1)} %collective-permute-done.7, f32[35,96,192]{2,1,0:T(8,128)} %copy-done.1, pred[]{:T(512)S(6)} %eq.140), kind=kLoop, calls=%fused_computation.129 | loop fusion | flops 84480 | bytes 675841 | tf_op jit(solution)/shard_map/mul | solution.py:164
  79.9 0.4 fusion.49
  80.3 0.4 fusion.45
  80.7 0.4 fusion.41
  81.1 0.4 fusion.69
  81.5 0.4 fusion.65
  81.8 0.4 fusion.61
  82.2 0.4 fusion.57
  82.8 3.7 %collective-permute-start.8 = (f32[3,64,160]{2,1,0:T(8,128)S(1)}, f32[3,64,160]{2,1,0:T(8,128)S(1)}, u32[]{:S(2)}, u32[]{:S(2)}) collective-permute-start(f32[3,64,160]{2,1,0:T(8,128)S(1)} %fusion.88), channel_id=1, source_target_pairs={{0,8},{8,16},{16,24},{1,9},{9,17},{17,25},{2,10},{10,18},{18,26},{... | collective-permute-start | bytes 368648 | tf_op jit(solution)/shard_map/ppermute | solution.py:32
  86.5 1.2 %multiply_multiply_fusion.1 = (f32[18,34,130]{2,1,0:T(8,128)S(1)}, f32[18,34,130]{2,1,0:T(8,128)S(1)}) fusion(f32[16,36,132]{2,1,0:T(8,128)S(1)} %copy-done.7, f32[2,36,132]{2,1,0:T(8,128)S(1)} %collective-permute-done.6, f32[2,36,132]{2,1,0:T(8,128)S(1)} %collective-permute-done.5, f32[130]{0:T(256)S(1)} %and_convert_fusion, ...), kind=kLoop, calls=%fused_computation.5 | loop fusion | flops 1750320 | bytes 2292568 | tf_op jit(solution)/shard_map/mul | solution.py:63
  87.7 3.7 %collective-permute-done.8 = f32[3,64,160]{2,1,0:T(8,128)S(1)} collective-permute-done((f32[3,64,160]{2,1,0:T(8,128)S(1)}, f32[3,64,160]{2,1,0:T(8,128)S(1)}, u32[]{:S(2)}, u32[]{:S(2)}) %collective-permute-start.8) | collective-permute-done | bytes 122912 | tf_op jit(solution)/shard_map/ppermute | solution.py:32
  91.4 1.1 fusion.85
  92.5 0.3 fusion.81
  92.8 0.3 fusion.77
  94.9 3.5 %collective-permute-start.9 = (f32[3,48,144]{2,1,0:T(8,128)S(1)}, f32[3,48,144]{2,1,0:T(8,128)S(1)}, u32[]{:S(2)}, u32[]{:S(2)}) collective-permute-start(f32[3,48,144]{2,1,0:T(8,128)S(1)} %fusion.120), channel_id=1, source_target_pairs={{0,8},{8,16},{16,24},{1,9},{9,17},{17,25},{2,10},{10,18},{18,26},{... | collective-permute-start | bytes 248840 | tf_op jit(solution)/shard_map/ppermute | solution.py:32
  98.4 0.9 fusion.37
  99.2 2.7 %collective-permute-done.9 = f32[3,48,144]{2,1,0:T(8,128)S(1)} collective-permute-done((f32[3,48,144]{2,1,0:T(8,128)S(1)}, f32[3,48,144]{2,1,0:T(8,128)S(1)}, u32[]{:S(2)}, u32[]{:S(2)}) %collective-permute-start.9) | collective-permute-done | bytes 82976 | tf_op jit(solution)/shard_map/ppermute | solution.py:32
  101.9 1.1 fusion.117
  106.1 0.5 fusion.3
  106.8 1.1 collective-permute-done.10
  108.0 1.1 collective-permute-start.11
  109.1 2.6 %collective-permute-done.11 = f32[4,1,128]{2,0,1:T(4,128)S(1)} collective-permute-done((f32[4,1,128]{2,0,1:T(4,128)S(1)}, f32[4,1,128]{2,0,1:T(4,128)S(1)}, u32[]{:S(2)}, u32[]{:S(2)}) %collective-permute-start.11) | collective-permute-done | bytes 2080 | tf_op jit(solution)/shard_map/ppermute | solution.py:42
  111.9 0.6 pad_maximum_fusion.3
  (102 shorter events, 6.9 us)
Async XLA Ops:
  1.0 3.0 %copy-start.9 = (f32[16,32,128]{2,1,0:T(8,128)}, f32[16,32,128]{2,1,0:T(8,128)S(1)}, u32[]{:S(2)}) copy-start(f32[16,32,128]{2,1,0:T(8,128)S(1)} %convert_element_type.39) | copy-start | bytes 786436
  2.1 12.4 %copy-start.15 = (s32[16,32,128]{2,1,0:T(8,128)S(1)}, s32[16,32,128]{2,1,0:T(8,128)}, u32[]{:S(2)}) copy-start(s32[16,32,128]{2,1,0:T(8,128)} %param.7) | copy-start | bytes 786436
  2.1 13.1 %copy-start.17 = (f32[3,16]{1,0:T(4,128)S(1)}, f32[3,16]{1,0:T(4,128)}, u32[]{:S(2)}) copy-start(f32[3,16]{1,0:T(4,128)} %table_ref.1) | copy-start | bytes 580
  2.1 13.1 %copy-start.18 = (f32[3,16]{1,0:T(4,128)S(1)}, f32[3,16]{1,0:T(4,128)}, u32[]{:S(2)}) copy-start(f32[3,16]{1,0:T(4,128)} %param.11) | copy-start | bytes 580
  2.1 13.0 %copy-start.19 = (f32[16]{0:T(128)S(1)}, f32[16]{0:T(128)}, u32[]{:S(2)}) copy-start(f32[16]{0:T(128)} %param.9) | copy-start | bytes 196
  2.1 38.8 %collective-permute-start.2 = (f32[35,32,128]{2,1,0:T(8,128)S(1)}, f32[35,32,128]{2,1,0:T(8,128)S(1)}, u32[]{:S(2)}, u32[]{:S(2)}) collective-permute-start(f32[35,32,128]{2,1,0:T(8,128)S(1)} %pad_maximum_fusion.2), channel_id=1, source_target_pairs={{0,1},{1,0},{2,3},{3,2},{4,5},{5,4},{6,7},{7,6},{8,9},{9,8},{10,11... | collective-permute-start | bytes 1720328 | tf_op jit(solution)/shard_map/ppermute | solution.py:133
  4.4 28.3 %collective-permute-start = (f32[35,32,32]{0,2,1:T(8,128)S(1)}, f32[35,32,32]{0,2,1:T(8,128)}, u32[]{:S(2)}, u32[]{:S(2)}) collective-permute-start(f32[35,32,32]{0,2,1:T(8,128)S(1)} %copy.176), channel_id=1, source_target_pairs={{0,3},{2,5},{4,7},{1,2},{3,4},{5,6},{8,11},{10,13},{12,15},{9,10},... | collective-permute-start | bytes 430088 | tf_op jit(solution)/shard_map/ppermute | solution.py:136
  6.8 29.2 %collective-permute-start.1 = (f32[35,32,32]{0,2,1:T(8,128)S(1)}, f32[35,32,32]{0,2,1:T(8,128)}, u32[]{:S(2)}, u32[]{:S(2)}) collective-permute-start(f32[35,32,32]{0,2,1:T(8,128)S(1)} %copy.176), channel_id=1, source_target_pairs={{0,2},{2,4},{4,6},{1,3},{3,5},{5,7},{8,10},{10,12},{12,14},{9,11},... | collective-permute-start | bytes 430088 | tf_op jit(solution)/shard_map/ppermute | solution.py:134
  11.8 6.4 %copy-start.4 = (f32[16,32,128]{2,1,0:T(8,128)S(1)}, f32[16,32,128]{2,1,0:T(8,128)}, u32[]{:S(2)}) copy-start(f32[16,32,128]{2,1,0:T(8,128)} %param.6) | copy-start | bytes 786436
  11.8 22.5 %collective-permute-start.3 = (f32[35,32,32]{0,2,1:T(8,128)}, f32[35,32,32]{0,2,1:T(8,128)}, u32[]{:S(2)}, u32[]{:S(2)}) collective-permute-start(f32[35,32,32]{0,2,1:T(8,128)} %copy.181), channel_id=1, source_target_pairs={{3,0},{5,2},{7,4},{2,1},{4,3},{6,5},{11,8},{13,10},{15,12},{10,9},... | collective-permute-start | bytes 430088 | tf_op jit(solution)/shard_map/ppermute | solution.py:137
  13.2 25.1 %collective-permute-start.4 = (f32[35,32,32]{0,2,1:T(8,128)}, f32[35,32,32]{0,2,1:T(8,128)}, u32[]{:S(2)}, u32[]{:S(2)}) collective-permute-start(f32[35,32,32]{0,2,1:T(8,128)} %copy.181), channel_id=1, source_target_pairs={{2,0},{4,2},{6,4},{3,1},{5,3},{7,5},{10,8},{12,10},{14,12},{11,9},... | collective-permute-start | bytes 430088 | tf_op jit(solution)/shard_map/ppermute | solution.py:135
  18.2 1.4 %copy-start.2 = (f32[7,16,32,128]{3,2,1,0:T(8,128)}, f32[7,16,32,128]{3,2,1,0:T(8,128)S(1)}, u32[]{:S(2)}) copy-start(f32[7,16,32,128]{3,2,1,0:T(8,128)S(1)} %select_select_fusion) | copy-start | bytes 5505028
  40.6 0.9 copy-start.5
  40.6 1.0 copy-start.10
  40.7 1.2 %copy-start.11 = (f32[35,32,32]{2,1,0:T(8,128)S(1)}, f32[35,32,32]{2,1,0:T(8,128)}, u32[]{:S(2)}) copy-start(f32[35,32,32]{2,1,0:T(8,128)} %copy.180) | copy-start | bytes 430084
  40.7 1.4 %copy-start.12 = (f32[35,32,32]{2,1,0:T(8,128)S(1)}, f32[35,32,32]{2,1,0:T(8,128)}, u32[]{:S(2)}) copy-start(f32[35,32,32]{2,1,0:T(8,128)} %copy.185) | copy-start | bytes 430084
  40.7 1.4 %copy-start.16 = (f32[3,32,128]{2,1,0:T(8,128)S(1)}, f32[3,32,128]{2,1,0:T(8,128)}, u32[]{:S(2)}) copy-start(f32[3,32,128]{2,1,0:T(8,128)} %param.8) | copy-start | bytes 147460
  46.0 2.0 %copy-start.1 = (f32[35,96,192]{2,1,0:T(8,128)}, f32[35,96,192]{2,1,0:T(8,128)S(1)}, u32[]{:S(2)}) copy-start(f32[35,96,192]{2,1,0:T(8,128)S(1)} %maximum_maximum_fusion.stack_ref) | copy-start | bytes 7741444
  56.8 2.7 %copy-start = (f32[3,8,96,192]{3,2,1,0:T(8,128)S(1)}, f32[3,8,96,192]{3,2,1,0:T(8,128)}, u32[]{:S(2)}) copy-start(f32[3,8,96,192]{3,2,1,0:T(8,128)} %shard_map.64) | copy-start | bytes 5308420
  61.3 1.2 %copy-start.7 = (f32[16,36,132]{2,1,0:T(8,128)S(1)}, f32[16,36,132]{2,1,0:T(8,128)}, u32[]{:S(2)}) copy-start(f32[16,36,132]{2,1,0:T(8,128)} %slice.1096) | copy-start | bytes 912388
  62.5 9.4 %collective-permute-start.6 = (f32[2,36,132]{2,1,0:T(8,128)S(1)}, f32[2,36,132]{2,1,0:T(8,128)S(1)}, u32[]{:S(2)}, u32[]{:S(2)}) collective-permute-start(f32[2,36,132]{2,1,0:T(8,128)S(1)} %get-tuple-element.48), channel_id=1, source_target_pairs={{0,8},{8,16},{16,24},{1,9},{9,17},{17,25},{2,10},{10,18},{18,26},{... | collective-permute-start | bytes 114056 | tf_op jit(solution)/shard_map/ppermute | solution.py:21
  66.1 7.1 %collective-permute-start.5 = (f32[2,36,132]{2,1,0:T(8,128)S(1)}, f32[2,36,132]{2,1,0:T(8,128)S(1)}, u32[]{:S(2)}, u32[]{:S(2)}) collective-permute-start(f32[2,36,132]{2,1,0:T(8,128)S(1)} %get-tuple-element.47), channel_id=1, source_target_pairs={{8,0},{16,8},{24,16},{9,1},{17,9},{25,17},{10,2},{18,10},{26,18},{... | collective-permute-start | bytes 114056 | tf_op jit(solution)/shard_map/ppermute | solution.py:24
  68.4 10.4 %collective-permute-start.7 = (f32[3,80,176]{2,1,0:T(8,128)S(1)}, f32[3,80,176]{2,1,0:T(8,128)S(1)}, u32[]{:S(2)}, u32[]{:S(2)}) collective-permute-start(f32[3,80,176]{2,1,0:T(8,128)S(1)} %fusion.56), channel_id=1, source_target_pairs={{0,8},{8,16},{16,24},{1,9},{9,17},{17,25},{2,10},{10,18},{18,26},{... | collective-permute-start | bytes 506888 | tf_op jit(solution)/shard_map/ppermute | solution.py:32
  82.8 8.6 %collective-permute-start.8 = (f32[3,64,160]{2,1,0:T(8,128)S(1)}, f32[3,64,160]{2,1,0:T(8,128)S(1)}, u32[]{:S(2)}, u32[]{:S(2)}) collective-permute-start(f32[3,64,160]{2,1,0:T(8,128)S(1)} %fusion.88), channel_id=1, source_target_pairs={{0,8},{8,16},{16,24},{1,9},{9,17},{17,25},{2,10},{10,18},{18,26},{... | collective-permute-start | bytes 368648 | tf_op jit(solution)/shard_map/ppermute | solution.py:32
  94.9 7.0 %collective-permute-start.9 = (f32[3,48,144]{2,1,0:T(8,128)S(1)}, f32[3,48,144]{2,1,0:T(8,128)S(1)}, u32[]{:S(2)}, u32[]{:S(2)}) collective-permute-start(f32[3,48,144]{2,1,0:T(8,128)S(1)} %fusion.120), channel_id=1, source_target_pairs={{0,8},{8,16},{16,24},{1,9},{9,17},{17,25},{2,10},{10,18},{18,26},{... | collective-permute-start | bytes 248840 | tf_op jit(solution)/shard_map/ppermute | solution.py:32
  104.2 1.5 %copy-start.3 = (f32[7,16,32,128]{3,2,1,0:T(8,128)S(1)}, f32[7,16,32,128]{3,2,1,0:T(8,128)}, u32[]{:S(2)}) copy-start(f32[7,16,32,128]{3,2,1,0:T(8,128)} %copy-done.2) | copy-start | bytes 5505028
  104.2 1.5 %copy-start.6 = (f32[16,32,128]{2,1,0:T(8,128)S(1)}, f32[16,32,128]{2,1,0:T(8,128)}, u32[]{:S(2)}) copy-start(f32[16,32,128]{2,1,0:T(8,128)} %param.6) | copy-start | bytes 786436
  104.2 1.7 %copy-start.8 = (f32[3,8,2,32,128]{4,3,2,1,0:T(8,128)S(1)}, f32[3,8,2,32,128]{4,3,2,1,0:T(8,128)}, u32[]{:S(2)}) copy-start(f32[3,8,2,32,128]{4,3,2,1,0:T(8,128)} %fusion.164) | copy-start | bytes 2359300
  104.3 1.8 %copy-start.13 = (f32[16,32,128]{2,1,0:T(8,128)S(1)}, f32[16,32,128]{2,1,0:T(8,128)}, u32[]{:S(2)}) copy-start(f32[16,32,128]{2,1,0:T(8,128)} %get-tuple-element.44) | copy-start | bytes 786436
  104.3 1.9 %copy-start.14 = (f32[16,32,128]{2,1,0:T(8,128)S(1)}, f32[16,32,128]{2,1,0:T(8,128)}, u32[]{:S(2)}) copy-start(f32[16,32,128]{2,1,0:T(8,128)} %fusion) | copy-start | bytes 786436
  106.7 1.2 %collective-permute-start.10 = (f32[4,2,128]{2,1,0:T(2,128)S(1)}, f32[4,2,128]{2,1,0:T(2,128)S(1)}, u32[]{:S(2)}, u32[]{:S(2)}) collective-permute-start(f32[4,2,128]{2,1,0:T(2,128)S(1)} %bitcast.280), channel_id=1, source_target_pairs={{0,2},{2,0},{4,6},{6,4},{1,3},{3,1},{5,7},{7,5},{8,10},{10,8},{12,... | collective-permute-start | bytes 12296 | tf_op jit(solution)/shard_map/ppermute | solution.py:42
  108.0 3.7 %collective-permute-start.11 = (f32[4,1,128]{2,0,1:T(4,128)S(1)}, f32[4,1,128]{2,0,1:T(4,128)S(1)}, u32[]{:S(2)}, u32[]{:S(2)}) collective-permute-start(f32[4,1,128]{2,0,1:T(4,128)S(1)} %bitcast.281), channel_id=1, source_target_pairs={{0,4},{4,0},{2,6},{6,2},{1,5},{5,1},{3,7},{7,3},{8,12},{12,8},{10,... | collective-permute-start | bytes 6152 | tf_op jit(solution)/shard_map/ppermute | solution.py:42

commit v18 on v15

--- a/solution.py
+++ b/solution.py
@@ -219,16 +219,17 @@
     incoming = sun_rim
     for section_num in range(n_light):
         border = SLABS * (n_light - section_num)
-        outgoing, starts = propagate(
+        outgoing, section_starts = propagate(
             incoming, border, fade_rim, brick_a, brick_v
         )
+        if starts is None:
+            starts = section_starts
+        else:
+            starts = jnp.where(light_idx == section_num, section_starts, starts)
         if section_num == 0:
             outgoing, density_side = lax.optimization_barrier((outgoing, density_side))
         if section_num + 1 < n_light:
-            arrived = from_behind(outgoing, "light", 1)
-            cut = widest - border + SLABS
-            sun_here = sun_rim[:, cut : cut + brick_a + 2 * (border - SLABS), cut : cut + brick_v + 2 * (border - SLABS)]
-            incoming = jnp.where(light_idx == 0, sun_here, arrived)
+            incoming = lax.ppermute(outgoing, "light", [(section_num, section_num + 1)])
     padded = padded_2(density_side, (("light", 0),), 2)
     inside = (
         rim_mask(light_idx, n_light, brick_l, 1)[:, None, None]

time: 104 us -> 97.4 us (0.937)
  starting transfers between devices: 28.1 us -> 21 us
  local copies, waits for them, and re-layouts: 11.9 us -> 15.9 us
  other arithmetic: 31.9 us -> 29.1 us
  waiting for transfers between devices: 20.5 us -> 19 us
    ppermute x3, starting transfers between devices: 10.7 us -> 3.49 us  [shards(): incoming = lax.ppermute(outgoing, 'light', [(section_num, section_num + 1)])]
    unnamed x48 -> x71, local copies, waits for them, and re-layouts: 2.76 us -> 6.55 us
    mul x31, other arithmetic: 14.7 us -> 11.7 us  [propagate(): current = current * fade_here]
    ppermute x1, waiting for transfers between devices: 0.4 us -> 2.7 us  [padded_2(): lax.ppermute(lax.slice_in_dim(block, 0, width, axis=dim), axis, backward)]
    ppermute x3, waiting for transfers between devices: 10.3 us -> 8.12 us  [shards(): incoming = lax.ppermute(outgoing, 'light', [(section_num, section_num + 1)])]
    ppermute x1, waiting for transfers between devices: 5.88 us -> 4.45 us  [halo(): got = lax.ppermute(send, axis, [(0, 1), (1, 0)])]
  transfers between devices with their start and end apart: 10 -> 10, of which waited for: 8 -> 7; matrix products, arithmetic and copies ran while one was open for 13% -> 18% of each run, Pallas kernels for 0% -> 0%
where the time goes in v18:
time: 97.4 us; the launch traced here: 95.5 us
  other arithmetic  29.1 us (30%)
  starting transfers between devices  21 us (22%)
  waiting for transfers between devices  19 us (20%)
  local copies, waits for them, and re-layouts  15.9 us (16%)
  Pallas kernels  8.76 us (9%)
  matrix products  0.99 us (1%)
    mul x31, other arithmetic, propagate(): current = current * fade_here  11.7 us
    pallas_call x1, Pallas kernels, fade_rim_of(): pl.pallas_call(kernel, out_shape=jax.ShapeDtypeStruct((colours, SLABS, ri...  8.76 us
    ppermute x3, waiting for transfers between devices, shards(): incoming = lax.ppermute(outgoing, 'light', [(section_num, section_num + 1)])  8.12 us
    ppermute x2, starting transfers between devices, from_partner(): return lax.ppermute(block, axis, route)  7.21 us
    unnamed x71, local copies, waits for them, and re-layouts  6.55 us
    ppermute x1, waiting for transfers between devices, halo(): got = lax.ppermute(send, axis, [(0, 1), (1, 0)])  4.45 us
    concatenate x2, other arithmetic, halo(): block = jnp.concatenate(lows + [block] + highs, axis=dim)  3.99 us
    ppermute x3, starting transfers between devices, shards(): incoming = lax.ppermute(outgoing, 'light', [(section_num, section_num + 1)])  3.49 us
  transfers between devices with their start and end apart: 10, of which 7 were waited for; matrix products, arithmetic and copies ran while one was open for 18% of the time, Pallas kernels for 0%

profile of v18, /device:TPU:16, one launch (start us, length us, event | category | flops | bytes accessed | tf_op | source)
XLA Modules:
  0.0 95.5 jit_solution(10209711814218282917)
XLA Ops:
  0.0 1.0 %convert_element_type.39 = f32[16,32,128]{2,1,0:T(8,128)S(1)} convert(s32[16,32,128]{2,1,0:T(8,128)} %param.7) | non-fusion elementwise | flops 65536 | bytes 524288 | tf_op jit(solution)/shard_map/convert_element_type | solution.py:199
  1.1 1.1 %pad_maximum_fusion.4 = f32[35,32,128]{2,1,0:T(8,128)S(1)} fusion(f32[3,32,128]{2,1,0:T(8,128)} %param.8, f32[16,32,128]{2,1,0:T(8,128)S(1)} %convert_element_type.39, f32[16,32,128]{2,1,0:T(8,128)} %param.6), kind=kLoop, calls=%fused_computation.17 | loop fusion | flops 286720 | bytes 1146880 | tf_op jit(solution)/shard_map/concatenate | solution.py:199
  2.2 1.6 %collective-permute-start = (f32[35,32,128]{2,1,0:T(8,128)S(1)}, f32[35,32,128]{2,1,0:T(8,128)S(1)}, u32[]{:S(2)}, u32[]{:S(2)}) collective-permute-start(f32[35,32,128]{2,1,0:T(8,128)S(1)} %pad_maximum_fusion.4), channel_id=1, source_target_pairs={{0,1},{1,0},{2,3},{3,2},{4,5},{5,4},{6,7},{7,6},{8,9},{9,8},{10,11... | collective-permute-start | bytes 1720328 | tf_op jit(solution)/shard_map/ppermute | solution.py:87
  3.8 1.4 %constant_dynamic-update-slice_fusion.34 = f32[3,8,32,128]{3,2,0,1:T(8,128)} fusion(f32[3,32,128]{2,1,0:T(8,128)} %param.8), kind=kLoop, calls=%fused_computation.335 | loop fusion | bytes 98304
  5.2 0.6 broadcast_compare_fusion.14
  5.9 0.4 slice_reduce_fusion.15
  6.4 2.6 %select_select_fusion = f32[7,16,32,128]{3,2,1,0:T(8,128)S(1)} fusion(f32[7]{0:T(128)S(1)} %get-tuple-element.10, f32[7]{0:T(128)S(1)} %get-tuple-element.11, f32[7]{0:T(128)S(1)} %get-tuple-element.12, f32[7]{0:T(128)S(1)} %get-tuple-element.13, f32[7]{0:T(128)S(1)} %get-tuple-element.14, f32[7]{0:T(128)S(1)} %get-tuple-element.15, ...), kind=kLoop, calls=%fused_computation.1 | loop fusion | flops 6881280 | bytes 2818496 | tf_op jit(solution)/shard_map/jit(_where)/select_n | solution.py:209
  9.0 0.8 fusion.143
  9.8 0.7 broadcast_multiply_fusion.mask_ref
  10.5 1.0 %fusion = f32[16,32,128]{2,1,0:T(8,128)} fusion(f32[16,32,128]{2,1,0:T(8,128)S(1)} %copy-done.2, f32[7,16,32,128]{3,2,1,0:T(8,128)S(1)} %select_select_fusion), kind=kOutput, calls=%fused_computation.4 | convolution fusion | flops 100876288 | bytes 786432 | tf_op jit(solution)/shard_map/dot_general | solution.py:246
  11.5 1.0 %slice_multiply_fusion = f32[3,16,32,128]{3,2,1,0:T(8,128)} fusion(f32[7,16,32,128]{3,2,1,0:T(8,128)S(1)} %select_select_fusion, f32[16,32,128]{2,1,0:T(8,128)S(1)} %copy-done.2), kind=kLoop, calls=%fused_computation.7 | loop fusion | flops 196608 | bytes 1835008 | tf_op jit(solution)/shard_map/mul | solution.py:212
  12.5 4.5 %collective-permute-done = f32[35,32,128]{2,1,0:T(8,128)S(1)} collective-permute-done((f32[35,32,128]{2,1,0:T(8,128)S(1)}, f32[35,32,128]{2,1,0:T(8,128)S(1)}, u32[]{:S(2)}, u32[]{:S(2)}) %collective-permute-start) | collective-permute-done | bytes 573472 | tf_op jit(solution)/shard_map/ppermute | solution.py:87
  17.3 0.6 fusion.172
  18.1 1.3 %copy.123 = f32[35,96,32]{1,2,0:T(8,128)} copy(f32[35,96,32]{2,1,0:T(8,128)S(1)} %get-tuple-element.85) | data formatting | bytes 860160 | tf_op jit(solution)/shard_map/slice | solution.py:97
  19.5 1.4 %collective-permute-start.1 = (f32[35,96,32]{1,2,0:T(8,128)}, f32[35,96,32]{1,2,0:T(8,128)S(1)}, u32[]{:S(2)}, u32[]{:S(2)}) collective-permute-start(f32[35,96,32]{1,2,0:T(8,128)} %copy.123), channel_id=1, source_target_pairs={{0,2},{2,4},{4,6},{1,3},{3,5},{5,7},{8,10},{10,12},{12,14},{9,11},... | collective-permute-start | bytes 1290248 | tf_op jit(solution)/shard_map/ppermute | solution.py:98
  20.9 1.3 %copy.124 = f32[35,96,32]{1,2,0:T(8,128)} copy(f32[35,96,32]{2,1,0:T(8,128)S(1)} %get-tuple-element.86) | data formatting | bytes 860160 | tf_op jit(solution)/shard_map/slice | solution.py:99
  22.2 1.5 %collective-permute-start.2 = (f32[35,96,32]{1,2,0:T(8,128)}, f32[35,96,32]{1,2,0:T(8,128)S(1)}, u32[]{:S(2)}, u32[]{:S(2)}) collective-permute-start(f32[35,96,32]{1,2,0:T(8,128)} %copy.124), channel_id=1, source_target_pairs={{2,0},{4,2},{6,4},{3,1},{5,3},{7,5},{10,8},{12,10},{14,12},{11,9},... | collective-permute-start | bytes 1290248 | tf_op jit(solution)/shard_map/ppermute | solution.py:99
  23.9 1.0 %fusion.177 = f32[3,8,2,32,128]{4,3,2,1,0:T(8,128)} fusion(f32[3,8,2,32,128]{4,3,2,1,0:T(8,128)S(1)} %bitcast.367), kind=kOutput, calls=%fused_computation.428 | output fusion | flops 196608 | bytes 1572864 | tf_op jit(solution)/shard_map/jit(cumsum)/reduce_window_sum | solution.py:214
  24.9 1.8 %copy.125 = f32[35,96,32]{2,1,0:T(8,128)} copy(f32[35,96,32]{1,2,0:T(8,128)S(1)} %collective-permute-done.1) | data formatting | bytes 860160 | tf_op jit(solution)/shard_map/ppermute | solution.py:98
  26.6 1.4 %collective-permute-done.2 = f32[35,96,32]{1,2,0:T(8,128)S(1)} collective-permute-done((f32[35,96,32]{1,2,0:T(8,128)}, f32[35,96,32]{1,2,0:T(8,128)S(1)}, u32[]{:S(2)}, u32[]{:S(2)}) %collective-permute-start.2) | collective-permute-done | bytes 430112 | tf_op jit(solution)/shard_map/ppermute | solution.py:99
  28.0 1.7 %copy.126 = f32[35,96,32]{2,1,0:T(8,128)} copy(f32[35,96,32]{1,2,0:T(8,128)S(1)} %collective-permute-done.2) | data formatting | bytes 860160 | tf_op jit(solution)/shard_map/ppermute | solution.py:99
  29.7 3.9 %pad_maximum_fusion.stack_ref = f32[35,96,192]{2,1,0:T(8,128)S(1)} fusion(f32[35,96,32]{2,1,0:T(8,128)} %copy.126, f32[35,32,128]{2,1,0:T(8,128)} %copy-done.8, f32[3,32,128]{2,1,0:T(8,128)S(1)} %copy-done.15, f32[16,32,128]{2,1,0:T(8,128)} %copy-done.9, f32[16,32,128]{2,1,0:T(8,128)} %param.6, f32[35,32,128]{2,1,0:T(8,128)} %copy-done.7, f32[35,96,32]{2,1,0:T(8,128)} %copy.125), kind=kLoop, calls=%fused_computation | loop fusion | flops 3870720 | bytes 5160960 | tf_op jit(solution)/shard_map/concatenate | solution.py:100
  33.6 1.3 %slice.1177 = f32[16,36,132]{2,1,0:T(8,128)} slice(f32[35,96,192]{2,1,0:T(8,128)S(1)} %pad_maximum_fusion.stack_ref), slice={[0:16], [30:66], [30:162]} | slice | bytes 608256 | tf_op jit(solution)/shard_map/slice | solution.py:203
  35.0 0.7 copy-done.1
  35.6 8.8 %shard_map.64 = f32[3,8,96,192]{3,2,1,0:T(8,128)} custom-call(f32[3,16]{1,0:T(4,128)} %table_ref.1, f32[35,96,192]{2,1,0:T(8,128)} %copy-done.1, f32[96,192]{1,0:T(8,128)} %broadcast_multiply_fusion.mask_ref), custom_call_target="tpu_custom_call" | custom-call | tf_op jit(solution)/shard_map/pallas_call | solution.py:173
  44.4 1.2 %fusion.17 = f32[3,96,192]{2,1,0:T(8,128)S(1)} fusion(f32[3,8,96,192]{3,2,1,0:T(8,128)} %shard_map.64, f32[35,96,192]{2,1,0:T(8,128)} %copy-done.1), kind=kLoop, calls=%fused_computation.44 | loop fusion | flops 55296 | bytes 663552 | tf_op jit(solution)/shard_map/mul | solution.py:129
  45.6 1.4 %fusion.13 = (f32[3,94,190]{2,1,0:T(8,128)S(1)}, f32[3,94,190]{2,1,0:T(8,128)S(1)}) fusion(f32[3,8,96,192]{3,2,1,0:T(8,128)} %shard_map.64, f32[3,96,192]{2,1,0:T(8,128)S(1)} %fusion.17), kind=kLoop, calls=%fused_computation.36 | loop fusion | flops 428640 | bytes 1714560 | tf_op jit(solution)/shard_map/mul | solution.py:129
  47.1 0.4 fusion.9
  47.5 0.4 fusion.5
  48.0 0.4 fusion.30
  48.4 0.4 fusion.26
  48.8 0.4 fusion.22
  49.2 0.4 fusion.18
  49.7 0.3 fusion.56
  50.0 0.3 copy-done.6
  50.3 3.5 %collective-permute-start.4 = (f32[2,36,132]{2,1,0:T(8,128)S(1)}, f32[2,36,132]{2,1,0:T(8,128)S(1)}, u32[]{:S(2)}, u32[]{:S(2)}) collective-permute-start(f32[2,36,132]{2,1,0:T(8,128)S(1)} %get-tuple-element.90), channel_id=1, source_target_pairs={{0,8},{8,16},{16,24},{1,9},{9,17},{17,25},{2,10},{10,18},{18,26},{... | collective-permute-start | bytes 114056 | tf_op jit(solution)/shard_map/ppermute | solution.py:21
  53.8 2.4 %collective-permute-start.3 = (f32[2,36,132]{2,1,0:T(8,128)S(1)}, f32[2,36,132]{2,1,0:T(8,128)S(1)}, u32[]{:S(2)}, u32[]{:S(2)}) collective-permute-start(f32[2,36,132]{2,1,0:T(8,128)S(1)} %get-tuple-element.89), channel_id=1, source_target_pairs={{8,0},{16,8},{24,16},{9,1},{17,9},{25,17},{10,2},{18,10},{26,18},{... | collective-permute-start | bytes 114056 | tf_op jit(solution)/shard_map/ppermute | solution.py:24
  56.2 0.7 collective-permute-start.5
  57.5 2.7 %collective-permute-done.3 = f32[2,36,132]{2,1,0:T(8,128)S(1)} collective-permute-done((f32[2,36,132]{2,1,0:T(8,128)S(1)}, f32[2,36,132]{2,1,0:T(8,128)S(1)}, u32[]{:S(2)}, u32[]{:S(2)}) %collective-permute-start.3) | collective-permute-done | bytes 38048 | tf_op jit(solution)/shard_map/ppermute | solution.py:24
  60.2 1.1 %multiply_multiply_fusion.1 = (f32[18,34,130]{2,1,0:T(8,128)S(1)}, f32[18,34,130]{2,1,0:T(8,128)S(1)}) fusion(f32[16,36,132]{2,1,0:T(8,128)S(1)} %copy-done.6, f32[2,36,132]{2,1,0:T(8,128)S(1)} %collective-permute-done.4, f32[2,36,132]{2,1,0:T(8,128)S(1)} %collective-permute-done.3, f32[130]{0:T(256)S(1)} %and_convert_fusion, ...), kind=kLoop, calls=%fused_computation.6 | loop fusion | flops 1750320 | bytes 2292568 | tf_op jit(solution)/shard_map/mul | solution.py:63
  61.3 0.9 fusion.37
  62.3 0.4 fusion.49
  62.7 0.4 fusion.45
  63.1 0.4 fusion.41
  63.5 0.4 fusion.69
  63.9 0.4 fusion.65
  64.2 0.4 fusion.61
  64.6 0.4 fusion.57
  65.2 1.5 %collective-permute-start.6 = (f32[3,64,160]{2,1,0:T(8,128)S(1)}, f32[3,64,160]{2,1,0:T(8,128)S(1)}, u32[]{:S(2)}, u32[]{:S(2)}) collective-permute-start(f32[3,64,160]{2,1,0:T(8,128)S(1)} %fusion.88), channel_id=1, source_target_pairs={{8,16},{9,17},{10,18},{11,19},{12,20},{13,21},{14,22},{15,23}} | collective-permute-start | bytes 368648 | tf_op jit(solution)/shard_map/ppermute | solution.py:232
  67.4 6.1 %collective-permute-done.6 = f32[3,64,160]{2,1,0:T(8,128)S(1)} collective-permute-done((f32[3,64,160]{2,1,0:T(8,128)S(1)}, f32[3,64,160]{2,1,0:T(8,128)S(1)}, u32[]{:S(2)}, u32[]{:S(2)}) %collective-permute-start.6) | collective-permute-done | bytes 122912 | tf_op jit(solution)/shard_map/ppermute | solution.py:232
  73.7 0.3 fusion.81
  74.0 0.3 fusion.77
  74.3 0.3 fusion.73
  75.5 0.3 fusion.89
  76.0 1.3 %collective-permute-start.7 = (f32[3,48,144]{2,1,0:T(8,128)S(1)}, f32[3,48,144]{2,1,0:T(8,128)S(1)}, u32[]{:S(2)}, u32[]{:S(2)}) collective-permute-start(f32[3,48,144]{2,1,0:T(8,128)S(1)} %fusion.120), channel_id=1, source_target_pairs={{16,24},{17,25},{18,26},{19,27},{20,28},{21,29},{22,30},{23,31}} | collective-permute-start | bytes 248840 | tf_op jit(solution)/shard_map/ppermute | solution.py:232
  78.0 2.0 %collective-permute-done.7 = f32[3,48,144]{2,1,0:T(8,128)S(1)} collective-permute-done((f32[3,48,144]{2,1,0:T(8,128)S(1)}, f32[3,48,144]{2,1,0:T(8,128)S(1)}, u32[]{:S(2)}, u32[]{:S(2)}) %collective-permute-start.7) | collective-permute-done | bytes 82976 | tf_op jit(solution)/shard_map/ppermute | solution.py:232
  82.9 0.6 copy-done.3
  83.5 0.6 copy-done.5
  84.4 0.5 fusion.3
  85.0 3.8 %collective-permute-start.8 = (f32[4,2,128]{2,1,0:T(2,128)S(1)}, f32[4,2,128]{2,1,0:T(2,128)S(1)}, u32[]{:S(2)}, u32[]{:S(2)}) collective-permute-start(f32[4,2,128]{2,1,0:T(2,128)S(1)} %bitcast.374), channel_id=1, source_target_pairs={{0,2},{2,0},{4,6},{6,4},{1,3},{3,1},{5,7},{7,5},{8,10},{10,8},{12,... | collective-permute-start | bytes 12296 | tf_op jit(solution)/shard_map/ppermute | solution.py:42
  88.8 0.8 collective-permute-done.8
  89.7 3.4 %collective-permute-start.9 = (f32[4,1,128]{2,0,1:T(4,128)S(1)}, f32[4,1,128]{2,0,1:T(4,128)S(1)}, u32[]{:S(2)}, u32[]{:S(2)}) collective-permute-start(f32[4,1,128]{2,0,1:T(4,128)S(1)} %bitcast.375), channel_id=1, source_target_pairs={{0,4},{4,0},{2,6},{6,2},{1,5},{5,1},{3,7},{7,3},{8,12},{12,8},{10,... | collective-permute-start | bytes 6152 | tf_op jit(solution)/shard_map/ppermute | solution.py:42
  93.1 1.6 %collective-permute-done.9 = f32[4,1,128]{2,0,1:T(4,128)S(1)} collective-permute-done((f32[4,1,128]{2,0,1:T(4,128)S(1)}, f32[4,1,128]{2,0,1:T(4,128)S(1)}, u32[]{:S(2)}, u32[]{:S(2)}) %collective-permute-start.9) | collective-permute-done | bytes 2080 | tf_op jit(solution)/shard_map/ppermute | solution.py:42
  94.9 0.6 pad_maximum_fusion.5
  (119 shorter events, 7.6 us)
Async XLA Ops:
  0.0 5.2 %copy-start.14 = (s32[16,32,128]{2,1,0:T(8,128)S(1)}, s32[16,32,128]{2,1,0:T(8,128)}, u32[]{:S(2)}) copy-start(s32[16,32,128]{2,1,0:T(8,128)} %param.7) | copy-start | bytes 786436
  0.0 5.9 %copy-start.17 = (f32[3,16]{1,0:T(4,128)S(1)}, f32[3,16]{1,0:T(4,128)}, u32[]{:S(2)}) copy-start(f32[3,16]{1,0:T(4,128)} %table_ref.1) | copy-start | bytes 580
  0.0 5.9 %copy-start.19 = (f32[16]{0:T(128)S(1)}, f32[16]{0:T(128)}, u32[]{:S(2)}) copy-start(f32[16]{0:T(128)} %param.9) | copy-start | bytes 196
  0.0 5.9 %copy-start.18 = (f32[3,16]{1,0:T(4,128)S(1)}, f32[3,16]{1,0:T(4,128)}, u32[]{:S(2)}) copy-start(f32[3,16]{1,0:T(4,128)} %param.11) | copy-start | bytes 580
  1.0 16.1 %copy-start.9 = (f32[16,32,128]{2,1,0:T(8,128)}, f32[16,32,128]{2,1,0:T(8,128)S(1)}, u32[]{:S(2)}) copy-start(f32[16,32,128]{2,1,0:T(8,128)S(1)} %convert_element_type.39) | copy-start | bytes 786436
  2.2 14.8 %collective-permute-start = (f32[35,32,128]{2,1,0:T(8,128)S(1)}, f32[35,32,128]{2,1,0:T(8,128)S(1)}, u32[]{:S(2)}, u32[]{:S(2)}) collective-permute-start(f32[35,32,128]{2,1,0:T(8,128)S(1)} %pad_maximum_fusion.4), channel_id=1, source_target_pairs={{0,1},{1,0},{2,3},{3,2},{4,5},{5,4},{6,7},{7,6},{8,9},{9,8},{10,11... | collective-permute-start | bytes 1720328 | tf_op jit(solution)/shard_map/ppermute | solution.py:87
  5.2 3.8 %copy-start.2 = (f32[16,32,128]{2,1,0:T(8,128)S(1)}, f32[16,32,128]{2,1,0:T(8,128)}, u32[]{:S(2)}) copy-start(f32[16,32,128]{2,1,0:T(8,128)} %param.6) | copy-start | bytes 786436
  9.0 8.1 %copy-start.4 = (f32[7,16,32,128]{3,2,1,0:T(8,128)}, f32[7,16,32,128]{3,2,1,0:T(8,128)S(1)}, u32[]{:S(2)}) copy-start(f32[7,16,32,128]{3,2,1,0:T(8,128)S(1)} %select_select_fusion) | copy-start | bytes 5505028
  11.5 5.6 %copy-start.15 = (f32[3,32,128]{2,1,0:T(8,128)S(1)}, f32[3,32,128]{2,1,0:T(8,128)}, u32[]{:S(2)}) copy-start(f32[3,32,128]{2,1,0:T(8,128)} %param.8) | copy-start | bytes 147460
  17.1 0.8 copy-start.7
  17.1 1.0 %copy-start.8 = (f32[35,32,128]{2,1,0:T(8,128)}, f32[35,32,128]{2,1,0:T(8,128)S(1)}, u32[]{:S(2)}) copy-start(f32[35,32,128]{2,1,0:T(8,128)S(1)} %get-tuple-element.92) | copy-start | bytes 1720324
  19.5 4.4 %copy-start.11 = (f32[3,16,32,128]{3,2,1,0:T(8,128)S(1)}, f32[3,16,32,128]{3,2,1,0:T(8,128)}, u32[]{:S(2)}) copy-start(f32[3,16,32,128]{3,2,1,0:T(8,128)} %slice_multiply_fusion) | copy-start | bytes 2359300
  19.5 5.4 %collective-permute-start.1 = (f32[35,96,32]{1,2,0:T(8,128)}, f32[35,96,32]{1,2,0:T(8,128)S(1)}, u32[]{:S(2)}, u32[]{:S(2)}) collective-permute-start(f32[35,96,32]{1,2,0:T(8,128)} %copy.123), channel_id=1, source_target_pairs={{0,2},{2,4},{4,6},{1,3},{3,5},{5,7},{8,10},{10,12},{12,14},{9,11},... | collective-permute-start | bytes 1290248 | tf_op jit(solution)/shard_map/ppermute | solution.py:98
  22.2 5.8 %collective-permute-start.2 = (f32[35,96,32]{1,2,0:T(8,128)}, f32[35,96,32]{1,2,0:T(8,128)S(1)}, u32[]{:S(2)}, u32[]{:S(2)}) collective-permute-start(f32[35,96,32]{1,2,0:T(8,128)} %copy.124), channel_id=1, source_target_pairs={{2,0},{4,2},{6,4},{3,1},{5,3},{7,5},{10,8},{12,10},{14,12},{11,9},... | collective-permute-start | bytes 1290248 | tf_op jit(solution)/shard_map/ppermute | solution.py:99
  33.6 2.0 %copy-start.1 = (f32[35,96,192]{2,1,0:T(8,128)}, f32[35,96,192]{2,1,0:T(8,128)S(1)}, u32[]{:S(2)}) copy-start(f32[35,96,192]{2,1,0:T(8,128)S(1)} %pad_maximum_fusion.stack_ref) | copy-start | bytes 7741444
  44.4 2.7 %copy-start = (f32[3,8,96,192]{3,2,1,0:T(8,128)S(1)}, f32[3,8,96,192]{3,2,1,0:T(8,128)}, u32[]{:S(2)}) copy-start(f32[3,8,96,192]{3,2,1,0:T(8,128)} %shard_map.64) | copy-start | bytes 5308420
  49.2 1.1 %copy-start.6 = (f32[16,36,132]{2,1,0:T(8,128)S(1)}, f32[16,36,132]{2,1,0:T(8,128)}, u32[]{:S(2)}) copy-start(f32[16,36,132]{2,1,0:T(8,128)} %slice.1177) | copy-start | bytes 912388
  49.2 7.6 %copy-start.16 = (f32[3,8,32,128]{3,2,0,1:T(8,128)S(1)}, f32[3,8,32,128]{3,2,0,1:T(8,128)}, u32[]{:S(2)}) copy-start(f32[3,8,32,128]{3,2,0,1:T(8,128)} %constant_dynamic-update-slice_fusion.34) | copy-start | bytes 1179652
  50.3 7.1 %collective-permute-start.4 = (f32[2,36,132]{2,1,0:T(8,128)S(1)}, f32[2,36,132]{2,1,0:T(8,128)S(1)}, u32[]{:S(2)}, u32[]{:S(2)}) collective-permute-start(f32[2,36,132]{2,1,0:T(8,128)S(1)} %get-tuple-element.90), channel_id=1, source_target_pairs={{0,8},{8,16},{16,24},{1,9},{9,17},{17,25},{2,10},{10,18},{18,26},{... | collective-permute-start | bytes 114056 | tf_op jit(solution)/shard_map/ppermute | solution.py:21
  53.8 6.3 %collective-permute-start.3 = (f32[2,36,132]{2,1,0:T(8,128)S(1)}, f32[2,36,132]{2,1,0:T(8,128)S(1)}, u32[]{:S(2)}, u32[]{:S(2)}) collective-permute-start(f32[2,36,132]{2,1,0:T(8,128)S(1)} %get-tuple-element.89), channel_id=1, source_target_pairs={{8,0},{16,8},{24,16},{9,1},{17,9},{25,17},{10,2},{18,10},{26,18},{... | collective-permute-start | bytes 114056 | tf_op jit(solution)/shard_map/ppermute | solution.py:24
  56.2 6.0 %collective-permute-start.5 = (f32[3,80,176]{2,1,0:T(8,128)S(1)}, f32[3,80,176]{2,1,0:T(8,128)S(1)}, u32[]{:S(2)}, u32[]{:S(2)}) collective-permute-start(f32[3,80,176]{2,1,0:T(8,128)S(1)} %fusion.56), channel_id=1, source_target_pairs={{0,8},{1,9},{2,10},{3,11},{4,12},{5,13},{6,14},{7,15}} | collective-permute-start | bytes 506888 | tf_op jit(solution)/shard_map/ppermute | solution.py:232
  65.2 8.3 %collective-permute-start.6 = (f32[3,64,160]{2,1,0:T(8,128)S(1)}, f32[3,64,160]{2,1,0:T(8,128)S(1)}, u32[]{:S(2)}, u32[]{:S(2)}) collective-permute-start(f32[3,64,160]{2,1,0:T(8,128)S(1)} %fusion.88), channel_id=1, source_target_pairs={{8,16},{9,17},{10,18},{11,19},{12,20},{13,21},{14,22},{15,23}} | collective-permute-start | bytes 368648 | tf_op jit(solution)/shard_map/ppermute | solution.py:232
  76.0 4.0 %collective-permute-start.7 = (f32[3,48,144]{2,1,0:T(8,128)S(1)}, f32[3,48,144]{2,1,0:T(8,128)S(1)}, u32[]{:S(2)}, u32[]{:S(2)}) collective-permute-start(f32[3,48,144]{2,1,0:T(8,128)S(1)} %fusion.120), channel_id=1, source_target_pairs={{16,24},{17,25},{18,26},{19,27},{20,28},{21,29},{22,30},{23,31}} | collective-permute-start | bytes 248840 | tf_op jit(solution)/shard_map/ppermute | solution.py:232
  82.5 1.0 copy-start.3
  82.5 1.6 %copy-start.5 = (f32[7,16,32,128]{3,2,1,0:T(8,128)S(1)}, f32[7,16,32,128]{3,2,1,0:T(8,128)}, u32[]{:S(2)}) copy-start(f32[7,16,32,128]{3,2,1,0:T(8,128)} %copy-done.4) | copy-start | bytes 5505028
  82.5 1.8 %copy-start.10 = (f32[3,8,2,32,128]{4,3,2,1,0:T(8,128)S(1)}, f32[3,8,2,32,128]{4,3,2,1,0:T(8,128)}, u32[]{:S(2)}) copy-start(f32[3,8,2,32,128]{4,3,2,1,0:T(8,128)} %fusion.177) | copy-start | bytes 2359300
  82.6 1.8 %copy-start.12 = (f32[16,32,128]{2,1,0:T(8,128)S(1)}, f32[16,32,128]{2,1,0:T(8,128)}, u32[]{:S(2)}) copy-start(f32[16,32,128]{2,1,0:T(8,128)} %get-tuple-element.84) | copy-start | bytes 786436
  82.6 1.9 %copy-start.13 = (f32[16,32,128]{2,1,0:T(8,128)S(1)}, f32[16,32,128]{2,1,0:T(8,128)}, u32[]{:S(2)}) copy-start(f32[16,32,128]{2,1,0:T(8,128)} %fusion) | copy-start | bytes 786436
  85.0 4.6 %collective-permute-start.8 = (f32[4,2,128]{2,1,0:T(2,128)S(1)}, f32[4,2,128]{2,1,0:T(2,128)S(1)}, u32[]{:S(2)}, u32[]{:S(2)}) collective-permute-start(f32[4,2,128]{2,1,0:T(2,128)S(1)} %bitcast.374), channel_id=1, source_target_pairs={{0,2},{2,0},{4,6},{6,4},{1,3},{3,1},{5,7},{7,5},{8,10},{10,8},{12,... | collective-permute-start | bytes 12296 | tf_op jit(solution)/shard_map/ppermute | solution.py:42
  89.7 5.0 %collective-permute-start.9 = (f32[4,1,128]{2,0,1:T(4,128)S(1)}, f32[4,1,128]{2,0,1:T(4,128)S(1)}, u32[]{:S(2)}, u32[]{:S(2)}) collective-permute-start(f32[4,1,128]{2,0,1:T(4,128)S(1)} %bitcast.375), channel_id=1, source_target_pairs={{0,4},{4,0},{2,6},{6,2},{1,5},{5,1},{3,7},{7,3},{8,12},{12,8},{10,... | collective-permute-start | bytes 6152 | tf_op jit(solution)/shard_map/ppermute | solution.py:42

commit v19 on v18

--- a/solution.py
+++ b/solution.py
@@ -226,7 +226,7 @@
             starts = section_starts
         else:
             starts = jnp.where(light_idx == section_num, section_starts, starts)
-        if section_num == 0:
+        if section_num == max(0, n_light - 2):
             outgoing, density_side = lax.optimization_barrier((outgoing, density_side))
         if section_num + 1 < n_light:
             incoming = lax.ppermute(outgoing, "light", [(section_num, section_num + 1)])

time: 97.4 us -> 99.1 us (1.017)
  the two profiles are of different devices: /device:TPU:16 before, /device:TPU:0 now
where the time goes in v19:
time: 99.1 us; the launch traced here: 98.7 us
  other arithmetic  29.1 us (29%)
  starting transfers between devices  27.8 us (28%)
  local copies, waits for them, and re-layouts  15.9 us (16%)
  waiting for transfers between devices  15.5 us (16%)
  Pallas kernels  8.76 us (9%)
    mul x31, other arithmetic, propagate(): current = current * fade_here  11.7 us
    pallas_call x1, Pallas kernels, fade_rim_of(): pl.pallas_call(kernel, out_shape=jax.ShapeDtypeStruct((colours, SLABS, ri...  8.76 us
    ppermute x2, starting transfers between devices, from_partner(): return lax.ppermute(block, axis, route)  8.25 us
    ppermute x1, starting transfers between devices, padded_2(): lax.ppermute(lax.slice_in_dim(block, block.shape[dim] - width, None, axis...  7.28 us
    unnamed x71, local copies, waits for them, and re-layouts  6.5 us
    ppermute x3, starting transfers between devices, shards(): incoming = lax.ppermute(outgoing, 'light', [(section_num, section_num + 1)])  5.06 us
    ppermute x1, waiting for transfers between devices, halo(): got = lax.ppermute(send, axis, [(0, 1), (1, 0)])  4.23 us
    ppermute x1, waiting for transfers between devices, padded_2(): lax.ppermute(lax.slice_in_dim(block, 0, width, axis=dim), axis, backward)  4.17 us
  transfers between devices with their start and end apart: 10, of which 6 were waited for; matrix products, arithmetic and copies ran while one was open for 17% of the time, Pallas kernels for 0%

profile of v19, /device:TPU:0, one launch (start us, length us, event | category | flops | bytes accessed | tf_op | source)
XLA Modules:
  0.0 98.7 jit_solution(9125145211064516360)
XLA Ops:
  0.0 1.0 %convert_element_type.39 = f32[16,32,128]{2,1,0:T(8,128)S(1)} convert(s32[16,32,128]{2,1,0:T(8,128)} %param.7) | non-fusion elementwise | flops 65536 | bytes 524288 | tf_op jit(solution)/shard_map/convert_element_type | solution.py:199
  1.1 1.1 %pad_maximum_fusion.4 = f32[35,32,128]{2,1,0:T(8,128)S(1)} fusion(f32[3,32,128]{2,1,0:T(8,128)} %param.8, f32[16,32,128]{2,1,0:T(8,128)S(1)} %convert_element_type.39, f32[16,32,128]{2,1,0:T(8,128)} %param.6), kind=kLoop, calls=%fused_computation.17 | loop fusion | flops 286720 | bytes 1146880 | tf_op jit(solution)/shard_map/concatenate | solution.py:199
  2.2 3.0 %collective-permute-start = (f32[35,32,128]{2,1,0:T(8,128)S(1)}, f32[35,32,128]{2,1,0:T(8,128)S(1)}, u32[]{:S(2)}, u32[]{:S(2)}) collective-permute-start(f32[35,32,128]{2,1,0:T(8,128)S(1)} %pad_maximum_fusion.4), channel_id=1, source_target_pairs={{0,1},{1,0},{2,3},{3,2},{4,5},{5,4},{6,7},{7,6},{8,9},{9,8},{10,11... | collective-permute-start | bytes 1720328 | tf_op jit(solution)/shard_map/ppermute | solution.py:87
  5.2 1.4 %constant_dynamic-update-slice_fusion.34 = f32[3,8,32,128]{3,2,0,1:T(8,128)} fusion(f32[3,32,128]{2,1,0:T(8,128)} %param.8), kind=kLoop, calls=%fused_computation.335 | loop fusion | bytes 98304
  6.6 0.6 broadcast_compare_fusion.14
  7.4 0.4 slice_reduce_fusion.15
  7.8 2.6 %select_select_fusion = f32[7,16,32,128]{3,2,1,0:T(8,128)S(1)} fusion(f32[7]{0:T(128)S(1)} %get-tuple-element.10, f32[7]{0:T(128)S(1)} %get-tuple-element.11, f32[7]{0:T(128)S(1)} %get-tuple-element.12, f32[7]{0:T(128)S(1)} %get-tuple-element.13, f32[7]{0:T(128)S(1)} %get-tuple-element.14, f32[7]{0:T(128)S(1)} %get-tuple-element.15, ...), kind=kLoop, calls=%fused_computation.1 | loop fusion | flops 6881280 | bytes 2818496 | tf_op jit(solution)/shard_map/jit(_where)/select_n | solution.py:209
  10.4 0.8 fusion.143
  11.3 0.7 broadcast_multiply_fusion.mask_ref
  12.0 1.0 %fusion = f32[16,32,128]{2,1,0:T(8,128)} fusion(f32[16,32,128]{2,1,0:T(8,128)S(1)} %copy-done.2, f32[7,16,32,128]{3,2,1,0:T(8,128)S(1)} %select_select_fusion), kind=kOutput, calls=%fused_computation.4 | convolution fusion | flops 100876288 | bytes 786432 | tf_op jit(solution)/shard_map/dot_general | solution.py:246
  13.0 1.0 slice_multiply_fusion
  14.0 4.2 %collective-permute-done = f32[35,32,128]{2,1,0:T(8,128)S(1)} collective-permute-done((f32[35,32,128]{2,1,0:T(8,128)S(1)}, f32[35,32,128]{2,1,0:T(8,128)S(1)}, u32[]{:S(2)}, u32[]{:S(2)}) %collective-permute-start) | collective-permute-done | bytes 573472 | tf_op jit(solution)/shard_map/ppermute | solution.py:87
  18.5 0.6 fusion.172
  19.3 1.3 %copy.123 = f32[35,96,32]{1,2,0:T(8,128)} copy(f32[35,96,32]{2,1,0:T(8,128)S(1)} %get-tuple-element.85) | data formatting | bytes 860160 | tf_op jit(solution)/shard_map/slice | solution.py:97
  20.7 1.4 %collective-permute-start.1 = (f32[35,96,32]{1,2,0:T(8,128)}, f32[35,96,32]{1,2,0:T(8,128)S(1)}, u32[]{:S(2)}, u32[]{:S(2)}) collective-permute-start(f32[35,96,32]{1,2,0:T(8,128)} %copy.123), channel_id=1, source_target_pairs={{0,2},{2,4},{4,6},{1,3},{3,5},{5,7},{8,10},{10,12},{12,14},{9,11},... | collective-permute-start | bytes 1290248 | tf_op jit(solution)/shard_map/ppermute | solution.py:98
  22.1 1.3 %copy.124 = f32[35,96,32]{1,2,0:T(8,128)} copy(f32[35,96,32]{2,1,0:T(8,128)S(1)} %get-tuple-element.86) | data formatting | bytes 860160 | tf_op jit(solution)/shard_map/slice | solution.py:99
  23.5 1.5 %collective-permute-start.2 = (f32[35,96,32]{1,2,0:T(8,128)}, f32[35,96,32]{1,2,0:T(8,128)S(1)}, u32[]{:S(2)}, u32[]{:S(2)}) collective-permute-start(f32[35,96,32]{1,2,0:T(8,128)} %copy.124), channel_id=1, source_target_pairs={{2,0},{4,2},{6,4},{3,1},{5,3},{7,5},{10,8},{12,10},{14,12},{11,9},... | collective-permute-start | bytes 1290248 | tf_op jit(solution)/shard_map/ppermute | solution.py:99
  25.1 1.0 %fusion.177 = f32[3,8,2,32,128]{4,3,2,1,0:T(8,128)} fusion(f32[3,8,2,32,128]{4,3,2,1,0:T(8,128)S(1)} %bitcast.367), kind=kOutput, calls=%fused_computation.428 | output fusion | flops 196608 | bytes 1572864 | tf_op jit(solution)/shard_map/jit(cumsum)/reduce_window_sum | solution.py:214
  26.1 1.8 %copy.125 = f32[35,96,32]{2,1,0:T(8,128)} copy(f32[35,96,32]{1,2,0:T(8,128)S(1)} %collective-permute-done.1) | data formatting | bytes 860160 | tf_op jit(solution)/shard_map/ppermute | solution.py:98
  27.9 1.6 %collective-permute-done.2 = f32[35,96,32]{1,2,0:T(8,128)S(1)} collective-permute-done((f32[35,96,32]{1,2,0:T(8,128)}, f32[35,96,32]{1,2,0:T(8,128)S(1)}, u32[]{:S(2)}, u32[]{:S(2)}) %collective-permute-start.2) | collective-permute-done | bytes 430112 | tf_op jit(solution)/shard_map/ppermute | solution.py:99
  29.5 1.7 %copy.126 = f32[35,96,32]{2,1,0:T(8,128)} copy(f32[35,96,32]{1,2,0:T(8,128)S(1)} %collective-permute-done.2) | data formatting | bytes 860160 | tf_op jit(solution)/shard_map/ppermute | solution.py:99
  31.2 3.9 %pad_maximum_fusion.stack_ref = f32[35,96,192]{2,1,0:T(8,128)S(1)} fusion(f32[35,96,32]{2,1,0:T(8,128)} %copy.126, f32[35,32,128]{2,1,0:T(8,128)} %copy-done.8, f32[3,32,128]{2,1,0:T(8,128)S(1)} %copy-done.15, f32[16,32,128]{2,1,0:T(8,128)} %copy-done.9, f32[16,32,128]{2,1,0:T(8,128)} %param.6, f32[35,32,128]{2,1,0:T(8,128)} %copy-done.7, f32[35,96,32]{2,1,0:T(8,128)} %copy.125), kind=kLoop, calls=%fused_computation | loop fusion | flops 3870720 | bytes 5160960 | tf_op jit(solution)/shard_map/concatenate | solution.py:100
  35.1 1.3 %slice.1273 = f32[16,36,132]{2,1,0:T(8,128)} slice(f32[35,96,192]{2,1,0:T(8,128)S(1)} %pad_maximum_fusion.stack_ref), slice={[0:16], [30:66], [30:162]} | slice | bytes 608256 | tf_op jit(solution)/shard_map/slice | solution.py:203
  36.4 0.7 copy-done.1
  37.1 8.8 %shard_map.64 = f32[3,8,96,192]{3,2,1,0:T(8,128)} custom-call(f32[3,16]{1,0:T(4,128)} %table_ref.1, f32[35,96,192]{2,1,0:T(8,128)} %copy-done.1, f32[96,192]{1,0:T(8,128)} %broadcast_multiply_fusion.mask_ref), custom_call_target="tpu_custom_call" | custom-call | tf_op jit(solution)/shard_map/pallas_call | solution.py:173
  45.8 1.2 %fusion.17 = f32[3,96,192]{2,1,0:T(8,128)S(1)} fusion(f32[3,8,96,192]{3,2,1,0:T(8,128)} %shard_map.64, f32[35,96,192]{2,1,0:T(8,128)} %copy-done.1), kind=kLoop, calls=%fused_computation.44 | loop fusion | flops 55296 | bytes 663552 | tf_op jit(solution)/shard_map/mul | solution.py:129
  47.1 1.4 %fusion.13 = (f32[3,94,190]{2,1,0:T(8,128)S(1)}, f32[3,94,190]{2,1,0:T(8,128)S(1)}) fusion(f32[3,8,96,192]{3,2,1,0:T(8,128)} %shard_map.64, f32[3,96,192]{2,1,0:T(8,128)S(1)} %fusion.17), kind=kLoop, calls=%fused_computation.36 | loop fusion | flops 428640 | bytes 1714560 | tf_op jit(solution)/shard_map/mul | solution.py:129
  48.5 0.4 fusion.9
  49.0 0.4 fusion.5
  49.4 0.4 fusion.30
  49.8 0.4 fusion.26
  50.3 0.4 fusion.22
  50.7 0.4 fusion.18
  51.1 0.3 fusion.56
  51.4 3.5 %collective-permute-start.3 = (f32[3,80,176]{2,1,0:T(8,128)S(1)}, f32[3,80,176]{2,1,0:T(8,128)S(1)}, u32[]{:S(2)}, u32[]{:S(2)}) collective-permute-start(f32[3,80,176]{2,1,0:T(8,128)S(1)} %fusion.56), channel_id=1, source_target_pairs={{0,8},{1,9},{2,10},{3,11},{4,12},{5,13},{6,14},{7,15}} | collective-permute-start | bytes 506888 | tf_op jit(solution)/shard_map/ppermute | solution.py:232
  55.5 3.1 %collective-permute-done.3 = f32[3,80,176]{2,1,0:T(8,128)S(1)} collective-permute-done((f32[3,80,176]{2,1,0:T(8,128)S(1)}, f32[3,80,176]{2,1,0:T(8,128)S(1)}, u32[]{:S(2)}, u32[]{:S(2)}) %collective-permute-start.3) | collective-permute-done | bytes 168992 | tf_op jit(solution)/shard_map/ppermute | solution.py:232
  58.8 0.4 fusion.49
  59.1 0.4 fusion.45
  59.5 0.4 fusion.41
  59.9 0.4 fusion.69
  60.3 0.4 fusion.65
  60.6 0.4 fusion.61
  61.0 0.4 fusion.57
  61.6 0.9 collective-permute-start.4
  63.3 0.3 fusion.81
  63.6 0.3 fusion.77
  64.0 0.3 fusion.73
  64.6 0.3 fusion.97
  64.9 0.3 fusion.93
  65.2 0.3 fusion.89
  66.0 7.3 %collective-permute-start.6 = (f32[2,36,132]{2,1,0:T(8,128)S(1)}, f32[2,36,132]{2,1,0:T(8,128)S(1)}, u32[]{:S(2)}, u32[]{:S(2)}) collective-permute-start(f32[2,36,132]{2,1,0:T(8,128)S(1)} %get-tuple-element.90), channel_id=1, source_target_pairs={{0,8},{8,16},{16,24},{1,9},{9,17},{17,25},{2,10},{10,18},{18,26},{... | collective-permute-start | bytes 114056 | tf_op jit(solution)/shard_map/ppermute | solution.py:21
  73.3 1.3 %collective-permute-start.5 = (f32[2,36,132]{2,1,0:T(8,128)S(1)}, f32[2,36,132]{2,1,0:T(8,128)S(1)}, u32[]{:S(2)}, u32[]{:S(2)}) collective-permute-start(f32[2,36,132]{2,1,0:T(8,128)S(1)} %get-tuple-element.89), channel_id=1, source_target_pairs={{8,0},{16,8},{24,16},{9,1},{17,9},{25,17},{10,2},{18,10},{26,18},{... | collective-permute-start | bytes 114056 | tf_op jit(solution)/shard_map/ppermute | solution.py:24
  74.6 0.7 collective-permute-start.7
  75.9 4.2 %collective-permute-done.5 = f32[2,36,132]{2,1,0:T(8,128)S(1)} collective-permute-done((f32[2,36,132]{2,1,0:T(8,128)S(1)}, f32[2,36,132]{2,1,0:T(8,128)S(1)}, u32[]{:S(2)}, u32[]{:S(2)}) %collective-permute-start.5) | collective-permute-done | bytes 38048 | tf_op jit(solution)/shard_map/ppermute | solution.py:24
  80.1 1.1 %multiply_multiply_fusion.1 = (f32[18,34,130]{2,1,0:T(8,128)S(1)}, f32[18,34,130]{2,1,0:T(8,128)S(1)}) fusion(f32[16,36,132]{2,1,0:T(8,128)S(1)} %copy-done.6, f32[2,36,132]{2,1,0:T(8,128)S(1)} %collective-permute-done.6, f32[2,36,132]{2,1,0:T(8,128)S(1)} %collective-permute-done.5, f32[130]{0:T(256)S(1)} %and_convert_fusion, ...), kind=kLoop, calls=%fused_computation.6 | loop fusion | flops 1750320 | bytes 2292568 | tf_op jit(solution)/shard_map/mul | solution.py:63
  81.2 0.9 fusion.37
  85.0 0.6 copy-done.3
  85.6 0.6 copy-done.5
  86.6 0.5 fusion.3
  87.2 4.5 %collective-permute-start.8 = (f32[4,2,128]{2,1,0:T(2,128)S(1)}, f32[4,2,128]{2,1,0:T(2,128)S(1)}, u32[]{:S(2)}, u32[]{:S(2)}) collective-permute-start(f32[4,2,128]{2,1,0:T(2,128)S(1)} %bitcast.374), channel_id=1, source_target_pairs={{0,2},{2,0},{4,6},{6,4},{1,3},{3,1},{5,7},{7,5},{8,10},{10,8},{12,... | collective-permute-start | bytes 12296 | tf_op jit(solution)/shard_map/ppermute | solution.py:42
  91.7 0.8 collective-permute-done.8
  92.6 3.7 %collective-permute-start.9 = (f32[4,1,128]{2,0,1:T(4,128)S(1)}, f32[4,1,128]{2,0,1:T(4,128)S(1)}, u32[]{:S(2)}, u32[]{:S(2)}) collective-permute-start(f32[4,1,128]{2,0,1:T(4,128)S(1)} %bitcast.375), channel_id=1, source_target_pairs={{0,4},{4,0},{2,6},{6,2},{1,5},{5,1},{3,7},{7,3},{8,12},{12,8},{10,... | collective-permute-start | bytes 6152 | tf_op jit(solution)/shard_map/ppermute | solution.py:42
  96.3 1.6 %collective-permute-done.9 = f32[4,1,128]{2,0,1:T(4,128)S(1)} collective-permute-done((f32[4,1,128]{2,0,1:T(4,128)S(1)}, f32[4,1,128]{2,0,1:T(4,128)S(1)}, u32[]{:S(2)}, u32[]{:S(2)}) %collective-permute-start.9) | collective-permute-done | bytes 2080 | tf_op jit(solution)/shard_map/ppermute | solution.py:42
  98.1 0.6 pad_maximum_fusion.5
  (119 shorter events, 7.3 us)
Async XLA Ops:
  0.0 6.6 %copy-start.14 = (s32[16,32,128]{2,1,0:T(8,128)S(1)}, s32[16,32,128]{2,1,0:T(8,128)}, u32[]{:S(2)}) copy-start(s32[16,32,128]{2,1,0:T(8,128)} %param.7) | copy-start | bytes 786436
  0.0 7.3 %copy-start.17 = (f32[3,16]{1,0:T(4,128)S(1)}, f32[3,16]{1,0:T(4,128)}, u32[]{:S(2)}) copy-start(f32[3,16]{1,0:T(4,128)} %table_ref.1) | copy-start | bytes 580
  0.0 7.3 %copy-start.19 = (f32[16]{0:T(128)S(1)}, f32[16]{0:T(128)}, u32[]{:S(2)}) copy-start(f32[16]{0:T(128)} %param.9) | copy-start | bytes 196
  0.0 7.3 %copy-start.18 = (f32[3,16]{1,0:T(4,128)S(1)}, f32[3,16]{1,0:T(4,128)}, u32[]{:S(2)}) copy-start(f32[3,16]{1,0:T(4,128)} %param.11) | copy-start | bytes 580
  1.0 17.3 %copy-start.9 = (f32[16,32,128]{2,1,0:T(8,128)}, f32[16,32,128]{2,1,0:T(8,128)S(1)}, u32[]{:S(2)}) copy-start(f32[16,32,128]{2,1,0:T(8,128)S(1)} %convert_element_type.39) | copy-start | bytes 786436
  2.2 16.0 %collective-permute-start = (f32[35,32,128]{2,1,0:T(8,128)S(1)}, f32[35,32,128]{2,1,0:T(8,128)S(1)}, u32[]{:S(2)}, u32[]{:S(2)}) collective-permute-start(f32[35,32,128]{2,1,0:T(8,128)S(1)} %pad_maximum_fusion.4), channel_id=1, source_target_pairs={{0,1},{1,0},{2,3},{3,2},{4,5},{5,4},{6,7},{7,6},{8,9},{9,8},{10,11... | collective-permute-start | bytes 1720328 | tf_op jit(solution)/shard_map/ppermute | solution.py:87
  6.6 3.8 %copy-start.2 = (f32[16,32,128]{2,1,0:T(8,128)S(1)}, f32[16,32,128]{2,1,0:T(8,128)}, u32[]{:S(2)}) copy-start(f32[16,32,128]{2,1,0:T(8,128)} %param.6) | copy-start | bytes 786436
  10.4 7.9 %copy-start.4 = (f32[7,16,32,128]{3,2,1,0:T(8,128)}, f32[7,16,32,128]{3,2,1,0:T(8,128)S(1)}, u32[]{:S(2)}) copy-start(f32[7,16,32,128]{3,2,1,0:T(8,128)S(1)} %select_select_fusion) | copy-start | bytes 5505028
  13.0 5.4 %copy-start.15 = (f32[3,32,128]{2,1,0:T(8,128)S(1)}, f32[3,32,128]{2,1,0:T(8,128)}, u32[]{:S(2)}) copy-start(f32[3,32,128]{2,1,0:T(8,128)} %param.8) | copy-start | bytes 147460
  18.3 0.8 copy-start.7
  18.3 1.0 %copy-start.8 = (f32[35,32,128]{2,1,0:T(8,128)}, f32[35,32,128]{2,1,0:T(8,128)S(1)}, u32[]{:S(2)}) copy-start(f32[35,32,128]{2,1,0:T(8,128)S(1)} %get-tuple-element.92) | copy-start | bytes 1720324
  20.7 4.4 %copy-start.11 = (f32[3,16,32,128]{3,2,1,0:T(8,128)S(1)}, f32[3,16,32,128]{3,2,1,0:T(8,128)}, u32[]{:S(2)}) copy-start(f32[3,16,32,128]{3,2,1,0:T(8,128)} %slice_multiply_fusion) | copy-start | bytes 2359300
  20.7 5.4 %collective-permute-start.1 = (f32[35,96,32]{1,2,0:T(8,128)}, f32[35,96,32]{1,2,0:T(8,128)S(1)}, u32[]{:S(2)}, u32[]{:S(2)}) collective-permute-start(f32[35,96,32]{1,2,0:T(8,128)} %copy.123), channel_id=1, source_target_pairs={{0,2},{2,4},{4,6},{1,3},{3,5},{5,7},{8,10},{10,12},{12,14},{9,11},... | collective-permute-start | bytes 1290248 | tf_op jit(solution)/shard_map/ppermute | solution.py:98
  23.5 6.0 %collective-permute-start.2 = (f32[35,96,32]{1,2,0:T(8,128)}, f32[35,96,32]{1,2,0:T(8,128)S(1)}, u32[]{:S(2)}, u32[]{:S(2)}) collective-permute-start(f32[35,96,32]{1,2,0:T(8,128)} %copy.124), channel_id=1, source_target_pairs={{2,0},{4,2},{6,4},{3,1},{5,3},{7,5},{10,8},{12,10},{14,12},{11,9},... | collective-permute-start | bytes 1290248 | tf_op jit(solution)/shard_map/ppermute | solution.py:99
  35.1 2.0 %copy-start.1 = (f32[35,96,192]{2,1,0:T(8,128)}, f32[35,96,192]{2,1,0:T(8,128)S(1)}, u32[]{:S(2)}) copy-start(f32[35,96,192]{2,1,0:T(8,128)S(1)} %pad_maximum_fusion.stack_ref) | copy-start | bytes 7741444
  45.8 2.7 %copy-start = (f32[3,8,96,192]{3,2,1,0:T(8,128)S(1)}, f32[3,8,96,192]{3,2,1,0:T(8,128)}, u32[]{:S(2)}) copy-start(f32[3,8,96,192]{3,2,1,0:T(8,128)} %shard_map.64) | copy-start | bytes 5308420
  50.7 4.3 %copy-start.16 = (f32[3,8,32,128]{3,2,0,1:T(8,128)S(1)}, f32[3,8,32,128]{3,2,0,1:T(8,128)}, u32[]{:S(2)}) copy-start(f32[3,8,32,128]{3,2,0,1:T(8,128)} %constant_dynamic-update-slice_fusion.34) | copy-start | bytes 1179652
  51.4 7.2 %collective-permute-start.3 = (f32[3,80,176]{2,1,0:T(8,128)S(1)}, f32[3,80,176]{2,1,0:T(8,128)S(1)}, u32[]{:S(2)}, u32[]{:S(2)}) collective-permute-start(f32[3,80,176]{2,1,0:T(8,128)S(1)} %fusion.56), channel_id=1, source_target_pairs={{0,8},{1,9},{2,10},{3,11},{4,12},{5,13},{6,14},{7,15}} | collective-permute-start | bytes 506888 | tf_op jit(solution)/shard_map/ppermute | solution.py:232
  61.6 1.6 %collective-permute-start.4 = (f32[3,64,160]{2,1,0:T(8,128)S(1)}, f32[3,64,160]{2,1,0:T(8,128)S(1)}, u32[]{:S(2)}, u32[]{:S(2)}) collective-permute-start(f32[3,64,160]{2,1,0:T(8,128)S(1)} %fusion.88), channel_id=1, source_target_pairs={{8,16},{9,17},{10,18},{11,19},{12,20},{13,21},{14,22},{15,23}} | collective-permute-start | bytes 368648 | tf_op jit(solution)/shard_map/ppermute | solution.py:232
  64.9 1.1 %copy-start.6 = (f32[16,36,132]{2,1,0:T(8,128)S(1)}, f32[16,36,132]{2,1,0:T(8,128)}, u32[]{:S(2)}) copy-start(f32[16,36,132]{2,1,0:T(8,128)} %slice.1273) | copy-start | bytes 912388
  66.0 9.8 %collective-permute-start.6 = (f32[2,36,132]{2,1,0:T(8,128)S(1)}, f32[2,36,132]{2,1,0:T(8,128)S(1)}, u32[]{:S(2)}, u32[]{:S(2)}) collective-permute-start(f32[2,36,132]{2,1,0:T(8,128)S(1)} %get-tuple-element.90), channel_id=1, source_target_pairs={{0,8},{8,16},{16,24},{1,9},{9,17},{17,25},{2,10},{10,18},{18,26},{... | collective-permute-start | bytes 114056 | tf_op jit(solution)/shard_map/ppermute | solution.py:21
  73.3 6.8 %collective-permute-start.5 = (f32[2,36,132]{2,1,0:T(8,128)S(1)}, f32[2,36,132]{2,1,0:T(8,128)S(1)}, u32[]{:S(2)}, u32[]{:S(2)}) collective-permute-start(f32[2,36,132]{2,1,0:T(8,128)S(1)} %get-tuple-element.89), channel_id=1, source_target_pairs={{8,0},{16,8},{24,16},{9,1},{17,9},{25,17},{10,2},{18,10},{26,18},{... | collective-permute-start | bytes 114056 | tf_op jit(solution)/shard_map/ppermute | solution.py:24
  74.6 7.6 %collective-permute-start.7 = (f32[3,48,144]{2,1,0:T(8,128)S(1)}, f32[3,48,144]{2,1,0:T(8,128)S(1)}, u32[]{:S(2)}, u32[]{:S(2)}) collective-permute-start(f32[3,48,144]{2,1,0:T(8,128)S(1)} %fusion.120), channel_id=1, source_target_pairs={{16,24},{17,25},{18,26},{19,27},{20,28},{21,29},{22,30},{23,31}} | collective-permute-start | bytes 248840 | tf_op jit(solution)/shard_map/ppermute | solution.py:232
  84.7 1.0 copy-start.3
  84.7 1.6 %copy-start.5 = (f32[7,16,32,128]{3,2,1,0:T(8,128)S(1)}, f32[7,16,32,128]{3,2,1,0:T(8,128)}, u32[]{:S(2)}) copy-start(f32[7,16,32,128]{3,2,1,0:T(8,128)} %copy-done.4) | copy-start | bytes 5505028
  84.7 1.8 %copy-start.10 = (f32[3,8,2,32,128]{4,3,2,1,0:T(8,128)S(1)}, f32[3,8,2,32,128]{4,3,2,1,0:T(8,128)}, u32[]{:S(2)}) copy-start(f32[3,8,2,32,128]{4,3,2,1,0:T(8,128)} %fusion.177) | copy-start | bytes 2359300
  84.7 1.8 %copy-start.12 = (f32[16,32,128]{2,1,0:T(8,128)S(1)}, f32[16,32,128]{2,1,0:T(8,128)}, u32[]{:S(2)}) copy-start(f32[16,32,128]{2,1,0:T(8,128)} %get-tuple-element.84) | copy-start | bytes 786436
  84.7 1.9 %copy-start.13 = (f32[16,32,128]{2,1,0:T(8,128)S(1)}, f32[16,32,128]{2,1,0:T(8,128)}, u32[]{:S(2)}) copy-start(f32[16,32,128]{2,1,0:T(8,128)} %fusion) | copy-start | bytes 786436
  87.2 5.4 %collective-permute-start.8 = (f32[4,2,128]{2,1,0:T(2,128)S(1)}, f32[4,2,128]{2,1,0:T(2,128)S(1)}, u32[]{:S(2)}, u32[]{:S(2)}) collective-permute-start(f32[4,2,128]{2,1,0:T(2,128)S(1)} %bitcast.374), channel_id=1, source_target_pairs={{0,2},{2,0},{4,6},{6,4},{1,3},{3,1},{5,7},{7,5},{8,10},{10,8},{12,... | collective-permute-start | bytes 12296 | tf_op jit(solution)/shard_map/ppermute | solution.py:42
  92.6 5.3 %collective-permute-start.9 = (f32[4,1,128]{2,0,1:T(4,128)S(1)}, f32[4,1,128]{2,0,1:T(4,128)S(1)}, u32[]{:S(2)}, u32[]{:S(2)}) collective-permute-start(f32[4,1,128]{2,0,1:T(4,128)S(1)} %bitcast.375), channel_id=1, source_target_pairs={{0,4},{4,0},{2,6},{6,2},{1,5},{5,1},{3,7},{7,3},{8,12},{12,8},{10,... | collective-permute-start | bytes 6152 | tf_op jit(solution)/shard_map/ppermute | solution.py:42

commit v20 on v19

--- a/solution.py
+++ b/solution.py
@@ -226,8 +226,6 @@
             starts = section_starts
         else:
             starts = jnp.where(light_idx == section_num, section_starts, starts)
-        if section_num == max(0, n_light - 2):
-            outgoing, density_side = lax.optimization_barrier((outgoing, density_side))
         if section_num + 1 < n_light:
             incoming = lax.ppermute(outgoing, "light", [(section_num, section_num + 1)])
     padded = padded_2(density_side, (("light", 0),), 2)

time: 99.1 us -> 96.8 us (0.977)
  the two profiles are of different devices: /device:TPU:0 before, /device:TPU:16 now
where the time goes in v20:
time: 96.8 us; the launch traced here: 94.9 us
  other arithmetic  30.9 us (32%)
  starting transfers between devices  21.8 us (23%)
  local copies, waits for them, and re-layouts  16 us (17%)
  waiting for transfers between devices  15.8 us (16%)
  Pallas kernels  8.83 us (9%)
  matrix products  0.98 us (1%)
    mul x31, other arithmetic, propagate(): current = current * fade_here  11.7 us
    pallas_call x1, Pallas kernels, fade_rim_of(): pl.pallas_call(kernel, out_shape=jax.ShapeDtypeStruct((colours, SLABS, ri...  8.83 us
    ppermute x2, starting transfers between devices, from_partner(): return lax.ppermute(block, axis, route)  7.96 us
    ppermute x3, waiting for transfers between devices, shards(): incoming = lax.ppermute(outgoing, 'light', [(section_num, section_num + 1)])  7.37 us
    unnamed x67, local copies, waits for them, and re-layouts  5.52 us
    ppermute x1, waiting for transfers between devices, halo(): got = lax.ppermute(send, axis, [(0, 1), (1, 0)])  4.47 us
    concatenate x2, other arithmetic, halo(): block = jnp.concatenate(lows + [block] + highs, axis=dim)  3.99 us
    ppermute x1, starting transfers between devices, padded_2(): lax.ppermute(lax.slice_in_dim(block, block.shape[dim] - width, None, axis...  3.67 us
  transfers between devices with their start and end apart: 10, of which 6 were waited for; matrix products, arithmetic and copies ran while one was open for 27% of the time, Pallas kernels for 9%

profile of v20, /device:TPU:16, one launch (start us, length us, event | category | flops | bytes accessed | tf_op | source)
XLA Modules:
  0.0 94.9 jit_solution(18146413374316608868)
XLA Ops:
  0.0 1.0 %convert_element_type.39 = f32[16,32,128]{2,1,0:T(8,128)S(1)} convert(s32[16,32,128]{2,1,0:T(8,128)} %param.7) | non-fusion elementwise | flops 65536 | bytes 524288 | tf_op jit(solution)/shard_map/convert_element_type | solution.py:199
  1.1 1.1 %pad_maximum_fusion.5 = f32[35,32,128]{2,1,0:T(8,128)S(1)} fusion(f32[3,32,128]{2,1,0:T(8,128)} %param.8, f32[16,32,128]{2,1,0:T(8,128)S(1)} %convert_element_type.39, f32[16,32,128]{2,1,0:T(8,128)} %param.6), kind=kLoop, calls=%fused_computation.18 | loop fusion | flops 286720 | bytes 1146880 | tf_op jit(solution)/shard_map/concatenate | solution.py:199
  2.2 1.6 %collective-permute-start = (f32[35,32,128]{2,1,0:T(8,128)S(1)}, f32[35,32,128]{2,1,0:T(8,128)S(1)}, u32[]{:S(2)}, u32[]{:S(2)}) collective-permute-start(f32[35,32,128]{2,1,0:T(8,128)S(1)} %pad_maximum_fusion.5), channel_id=1, source_target_pairs={{0,1},{1,0},{2,3},{3,2},{4,5},{5,4},{6,7},{7,6},{8,9},{9,8},{10,11... | collective-permute-start | bytes 1720328 | tf_op jit(solution)/shard_map/ppermute | solution.py:87
  3.8 1.4 %constant_dynamic-update-slice_fusion.31 = f32[3,8,32,128]{3,2,0,1:T(8,128)} fusion(f32[3,32,128]{2,1,0:T(8,128)} %param.8), kind=kLoop, calls=%fused_computation.333 | loop fusion | bytes 98304
  5.2 0.6 broadcast_compare_fusion.14
  5.9 0.4 slice_reduce_fusion.15
  6.4 2.6 %select_select_fusion = f32[7,16,32,128]{3,2,1,0:T(8,128)S(1)} fusion(f32[7]{0:T(128)S(1)} %get-tuple-element.6, f32[7]{0:T(128)S(1)} %get-tuple-element.7, f32[7]{0:T(128)S(1)} %get-tuple-element.8, f32[7]{0:T(128)S(1)} %get-tuple-element.9, f32[7]{0:T(128)S(1)} %get-tuple-element.10, f32[7]{0:T(128)S(1)} %get-tuple-element.11, f32[7]{0:T(128)S(1)} %get-tuple-element.12, ...), kind=kLoop, calls=%fused_computation.1 | loop fusion | flops 6881280 | bytes 2818496 | tf_op jit(solution)/shard_map/jit(_where)/select_n | solution.py:209
  9.0 0.8 fusion.143
  9.8 0.7 broadcast_multiply_fusion.mask_ref
  10.5 1.0 %fusion = f32[16,32,128]{2,1,0:T(8,128)} fusion(f32[16,32,128]{2,1,0:T(8,128)S(1)} %copy-done.2, f32[7,16,32,128]{3,2,1,0:T(8,128)S(1)} %select_select_fusion), kind=kOutput, calls=%fused_computation.4 | convolution fusion | flops 100876288 | bytes 786432 | tf_op jit(solution)/shard_map/dot_general | solution.py:244
  11.5 1.0 %slice_multiply_fusion = f32[3,16,32,128]{3,2,1,0:T(8,128)} fusion(f32[7,16,32,128]{3,2,1,0:T(8,128)S(1)} %select_select_fusion, f32[16,32,128]{2,1,0:T(8,128)S(1)} %copy-done.2), kind=kLoop, calls=%fused_computation.8 | loop fusion | flops 196608 | bytes 1835008 | tf_op jit(solution)/shard_map/mul | solution.py:212
  12.5 4.5 %collective-permute-done = f32[35,32,128]{2,1,0:T(8,128)S(1)} collective-permute-done((f32[35,32,128]{2,1,0:T(8,128)S(1)}, f32[35,32,128]{2,1,0:T(8,128)S(1)}, u32[]{:S(2)}, u32[]{:S(2)}) %collective-permute-start) | collective-permute-done | bytes 573472 | tf_op jit(solution)/shard_map/ppermute | solution.py:87
  17.3 0.6 fusion.173
  18.1 1.3 %copy.123 = f32[35,96,32]{1,2,0:T(8,128)} copy(f32[35,96,32]{2,1,0:T(8,128)S(1)} %get-tuple-element.83) | data formatting | bytes 860160 | tf_op jit(solution)/shard_map/slice | solution.py:97
  19.5 1.4 %collective-permute-start.1 = (f32[35,96,32]{1,2,0:T(8,128)}, f32[35,96,32]{1,2,0:T(8,128)S(1)}, u32[]{:S(2)}, u32[]{:S(2)}) collective-permute-start(f32[35,96,32]{1,2,0:T(8,128)} %copy.123), channel_id=1, source_target_pairs={{0,2},{2,4},{4,6},{1,3},{3,5},{5,7},{8,10},{10,12},{12,14},{9,11},... | collective-permute-start | bytes 1290248 | tf_op jit(solution)/shard_map/ppermute | solution.py:98
  20.9 1.3 %copy.124 = f32[35,96,32]{1,2,0:T(8,128)} copy(f32[35,96,32]{2,1,0:T(8,128)S(1)} %get-tuple-element.84) | data formatting | bytes 860160 | tf_op jit(solution)/shard_map/slice | solution.py:99
  22.2 1.3 %collective-permute-start.2 = (f32[35,96,32]{1,2,0:T(8,128)}, f32[35,96,32]{1,2,0:T(8,128)S(1)}, u32[]{:S(2)}, u32[]{:S(2)}) collective-permute-start(f32[35,96,32]{1,2,0:T(8,128)} %copy.124), channel_id=1, source_target_pairs={{2,0},{4,2},{6,4},{3,1},{5,3},{7,5},{10,8},{12,10},{14,12},{11,9},... | collective-permute-start | bytes 1290248 | tf_op jit(solution)/shard_map/ppermute | solution.py:99
  23.7 0.9 fusion.177
  24.6 1.8 %copy.125 = f32[35,96,32]{2,1,0:T(8,128)} copy(f32[35,96,32]{1,2,0:T(8,128)S(1)} %collective-permute-done.1) | data formatting | bytes 860160 | tf_op jit(solution)/shard_map/ppermute | solution.py:98
  26.4 1.6 %collective-permute-done.2 = f32[35,96,32]{1,2,0:T(8,128)S(1)} collective-permute-done((f32[35,96,32]{1,2,0:T(8,128)}, f32[35,96,32]{1,2,0:T(8,128)S(1)}, u32[]{:S(2)}, u32[]{:S(2)}) %collective-permute-start.2) | collective-permute-done | bytes 430112 | tf_op jit(solution)/shard_map/ppermute | solution.py:99
  28.0 1.8 %copy.126 = f32[35,96,32]{2,1,0:T(8,128)} copy(f32[35,96,32]{1,2,0:T(8,128)S(1)} %collective-permute-done.2) | data formatting | bytes 860160 | tf_op jit(solution)/shard_map/ppermute | solution.py:99
  29.8 3.9 %pad_maximum_fusion.stack_ref = f32[35,96,192]{2,1,0:T(8,128)S(1)} fusion(f32[35,96,32]{2,1,0:T(8,128)} %copy.126, f32[35,32,128]{2,1,0:T(8,128)} %copy-done.7, f32[3,32,128]{2,1,0:T(8,128)S(1)} %copy-done.14, f32[16,32,128]{2,1,0:T(8,128)} %copy-done.8, f32[16,32,128]{2,1,0:T(8,128)} %param.6, f32[35,32,128]{2,1,0:T(8,128)} %copy-done.6, f32[35,96,32]{2,1,0:T(8,128)} %copy.125), kind=kLoop, calls=%fused_computation | loop fusion | flops 3870720 | bytes 5160960 | tf_op jit(solution)/shard_map/concatenate | solution.py:100
  33.7 0.9 fusion.172
  34.6 2.3 %collective-permute-start.3 = (f32[2,36,132]{2,1,0:T(8,128)}, f32[2,36,132]{2,1,0:T(8,128)S(1)}, u32[]{:S(2)}, u32[]{:S(2)}) collective-permute-start(f32[2,36,132]{2,1,0:T(8,128)} %get-tuple-element.79), channel_id=1, source_target_pairs={{8,0},{16,8},{24,16},{9,1},{17,9},{25,17},{10,2},{18,10},{26,18},{... | collective-permute-start | bytes 114056 | tf_op jit(solution)/shard_map/ppermute | solution.py:24
  36.9 3.7 %collective-permute-start.4 = (f32[2,36,132]{2,1,0:T(8,128)}, f32[2,36,132]{2,1,0:T(8,128)}, u32[]{:S(2)}, u32[]{:S(2)}) collective-permute-start(f32[2,36,132]{2,1,0:T(8,128)} %get-tuple-element.80), channel_id=1, source_target_pairs={{0,8},{8,16},{16,24},{1,9},{9,17},{17,25},{2,10},{10,18},{18,26},{... | collective-permute-start | bytes 114056 | tf_op jit(solution)/shard_map/ppermute | solution.py:21
  40.6 8.8 %shard_map.64 = f32[3,8,96,192]{3,2,1,0:T(8,128)} custom-call(f32[3,16]{1,0:T(4,128)} %table_ref.1, f32[35,96,192]{2,1,0:T(8,128)} %copy-done.1, f32[96,192]{1,0:T(8,128)} %broadcast_multiply_fusion.mask_ref), custom_call_target="tpu_custom_call" | custom-call | tf_op jit(solution)/shard_map/pallas_call | solution.py:173
  49.4 1.2 %fusion.17 = f32[3,96,192]{2,1,0:T(8,128)S(1)} fusion(f32[3,8,96,192]{3,2,1,0:T(8,128)} %shard_map.64, f32[35,96,192]{2,1,0:T(8,128)} %copy-done.1), kind=kLoop, calls=%fused_computation.45 | loop fusion | flops 55296 | bytes 663552 | tf_op jit(solution)/shard_map/mul | solution.py:129
  50.7 1.4 %fusion.13 = (f32[3,94,190]{2,1,0:T(8,128)S(1)}, f32[3,94,190]{2,1,0:T(8,128)S(1)}) fusion(f32[3,8,96,192]{3,2,1,0:T(8,128)} %shard_map.64, f32[3,96,192]{2,1,0:T(8,128)S(1)} %fusion.17), kind=kLoop, calls=%fused_computation.37 | loop fusion | flops 428640 | bytes 1714560 | tf_op jit(solution)/shard_map/mul | solution.py:129
  52.1 0.4 fusion.9
  52.6 0.4 fusion.5
  53.0 0.4 fusion.30
  53.4 0.4 fusion.26
  53.9 0.4 fusion.22
  54.3 0.4 fusion.18
  54.7 0.3 fusion.56
  55.0 0.7 collective-permute-start.5
  56.3 1.4 %slice.1130 = f32[16,36,132]{2,1,0:T(8,128)S(1)} slice(f32[35,96,192]{2,1,0:T(8,128)} %copy-done.1), slice={[0:16], [30:66], [30:162]} | slice | bytes 608256 | tf_op jit(solution)/shard_map/slice | solution.py:203
  57.7 0.9 pad_maximum_fusion.2
  58.7 2.0 %multiply_multiply_fusion.1 = (f32[18,34,130]{2,1,0:T(8,128)S(1)}, f32[18,34,130]{2,1,0:T(8,128)S(1)}) fusion(f32[16,36,132]{2,1,0:T(8,128)S(1)} %slice.1130, f32[2,36,132]{2,1,0:T(8,128)} %collective-permute-done.4, f32[2,36,132]{2,1,0:T(8,128)S(1)} %collective-permute-done.3, f32[130]{0:T(256)S(1)} %and_convert_fusion.2, ...), kind=kLoop, calls=%fused_computation.6 | loop fusion | flops 1750320 | bytes 2292568 | tf_op jit(solution)/shard_map/mul | solution.py:63
  60.7 0.9 fusion.37
  61.7 0.4 fusion.49
  62.1 0.4 fusion.45
  62.5 0.4 fusion.41
  62.9 0.4 fusion.69
  63.3 0.4 fusion.65
  63.6 0.4 fusion.61
  64.0 0.4 fusion.57
  64.6 1.3 %collective-permute-start.6 = (f32[3,64,160]{2,1,0:T(8,128)S(1)}, f32[3,64,160]{2,1,0:T(8,128)S(1)}, u32[]{:S(2)}, u32[]{:S(2)}) collective-permute-start(f32[3,64,160]{2,1,0:T(8,128)S(1)} %fusion.88), channel_id=1, source_target_pairs={{8,16},{9,17},{10,18},{11,19},{12,20},{13,21},{14,22},{15,23}} | collective-permute-start | bytes 368648 | tf_op jit(solution)/shard_map/ppermute | solution.py:230
  66.6 5.6 %collective-permute-done.6 = f32[3,64,160]{2,1,0:T(8,128)S(1)} collective-permute-done((f32[3,64,160]{2,1,0:T(8,128)S(1)}, f32[3,64,160]{2,1,0:T(8,128)S(1)}, u32[]{:S(2)}, u32[]{:S(2)}) %collective-permute-start.6) | collective-permute-done | bytes 122912 | tf_op jit(solution)/shard_map/ppermute | solution.py:230
  72.3 0.3 fusion.81
  72.6 0.3 fusion.77
  72.9 0.3 fusion.73
  73.6 0.3 fusion.97
  74.2 0.3 fusion.89
  74.7 1.5 %collective-permute-start.7 = (f32[3,48,144]{2,1,0:T(8,128)S(1)}, f32[3,48,144]{2,1,0:T(8,128)S(1)}, u32[]{:S(2)}, u32[]{:S(2)}) collective-permute-start(f32[3,48,144]{2,1,0:T(8,128)S(1)} %fusion.120), channel_id=1, source_target_pairs={{16,24},{17,25},{18,26},{19,27},{20,28},{21,29},{22,30},{23,31}} | collective-permute-start | bytes 248840 | tf_op jit(solution)/shard_map/ppermute | solution.py:230
  76.9 1.8 %collective-permute-done.7 = f32[3,48,144]{2,1,0:T(8,128)S(1)} collective-permute-done((f32[3,48,144]{2,1,0:T(8,128)S(1)}, f32[3,48,144]{2,1,0:T(8,128)S(1)}, u32[]{:S(2)}, u32[]{:S(2)}) %collective-permute-start.7) | collective-permute-done | bytes 82976 | tf_op jit(solution)/shard_map/ppermute | solution.py:230
  81.5 0.6 copy-done.3
  82.1 0.6 copy-done.5
  83.1 0.5 fusion.3
  83.7 5.4 %collective-permute-start.8 = (f32[4,2,128]{2,1,0:T(2,128)S(1)}, f32[4,2,128]{2,1,0:T(2,128)S(1)}, u32[]{:S(2)}, u32[]{:S(2)}) collective-permute-start(f32[4,2,128]{2,1,0:T(2,128)S(1)} %bitcast.374), channel_id=1, source_target_pairs={{0,2},{2,0},{4,6},{6,4},{1,3},{3,1},{5,7},{7,5},{8,10},{10,8},{12,... | collective-permute-start | bytes 12296 | tf_op jit(solution)/shard_map/ppermute | solution.py:42
  89.1 0.8 collective-permute-done.8
  90.0 2.5 %collective-permute-start.9 = (f32[4,1,128]{2,0,1:T(4,128)S(1)}, f32[4,1,128]{2,0,1:T(4,128)S(1)}, u32[]{:S(2)}, u32[]{:S(2)}) collective-permute-start(f32[4,1,128]{2,0,1:T(4,128)S(1)} %bitcast.375), channel_id=1, source_target_pairs={{0,4},{4,0},{2,6},{6,2},{1,5},{5,1},{3,7},{7,3},{8,12},{12,8},{10,... | collective-permute-start | bytes 6152 | tf_op jit(solution)/shard_map/ppermute | solution.py:42
  92.5 1.6 %collective-permute-done.9 = f32[4,1,128]{2,0,1:T(4,128)S(1)} collective-permute-done((f32[4,1,128]{2,0,1:T(4,128)S(1)}, f32[4,1,128]{2,0,1:T(4,128)S(1)}, u32[]{:S(2)}, u32[]{:S(2)}) %collective-permute-start.9) | collective-permute-done | bytes 2080 | tf_op jit(solution)/shard_map/ppermute | solution.py:42
  94.3 0.6 pad_maximum_fusion.6
  (116 shorter events, 7.4 us)
Async XLA Ops:
  0.0 5.2 %copy-start.13 = (s32[16,32,128]{2,1,0:T(8,128)S(1)}, s32[16,32,128]{2,1,0:T(8,128)}, u32[]{:S(2)}) copy-start(s32[16,32,128]{2,1,0:T(8,128)} %param.7) | copy-start | bytes 786436
  0.0 5.9 %copy-start.16 = (f32[3,16]{1,0:T(4,128)S(1)}, f32[3,16]{1,0:T(4,128)}, u32[]{:S(2)}) copy-start(f32[3,16]{1,0:T(4,128)} %table_ref.1) | copy-start | bytes 580
  0.0 5.9 %copy-start.18 = (f32[16]{0:T(128)S(1)}, f32[16]{0:T(128)}, u32[]{:S(2)}) copy-start(f32[16]{0:T(128)} %param.9) | copy-start | bytes 196
  0.0 5.9 %copy-start.17 = (f32[3,16]{1,0:T(4,128)S(1)}, f32[3,16]{1,0:T(4,128)}, u32[]{:S(2)}) copy-start(f32[3,16]{1,0:T(4,128)} %param.11) | copy-start | bytes 580
  1.0 16.1 %copy-start.8 = (f32[16,32,128]{2,1,0:T(8,128)}, f32[16,32,128]{2,1,0:T(8,128)S(1)}, u32[]{:S(2)}) copy-start(f32[16,32,128]{2,1,0:T(8,128)S(1)} %convert_element_type.39) | copy-start | bytes 786436
  2.2 14.8 %collective-permute-start = (f32[35,32,128]{2,1,0:T(8,128)S(1)}, f32[35,32,128]{2,1,0:T(8,128)S(1)}, u32[]{:S(2)}, u32[]{:S(2)}) collective-permute-start(f32[35,32,128]{2,1,0:T(8,128)S(1)} %pad_maximum_fusion.5), channel_id=1, source_target_pairs={{0,1},{1,0},{2,3},{3,2},{4,5},{5,4},{6,7},{7,6},{8,9},{9,8},{10,11... | collective-permute-start | bytes 1720328 | tf_op jit(solution)/shard_map/ppermute | solution.py:87
  5.2 3.8 %copy-start.2 = (f32[16,32,128]{2,1,0:T(8,128)S(1)}, f32[16,32,128]{2,1,0:T(8,128)}, u32[]{:S(2)}) copy-start(f32[16,32,128]{2,1,0:T(8,128)} %param.6) | copy-start | bytes 786436
  8.9 8.1 %copy-start.4 = (f32[7,16,32,128]{3,2,1,0:T(8,128)}, f32[7,16,32,128]{3,2,1,0:T(8,128)S(1)}, u32[]{:S(2)}) copy-start(f32[7,16,32,128]{3,2,1,0:T(8,128)S(1)} %select_select_fusion) | copy-start | bytes 5505028
  11.5 5.6 %copy-start.14 = (f32[3,32,128]{2,1,0:T(8,128)S(1)}, f32[3,32,128]{2,1,0:T(8,128)}, u32[]{:S(2)}) copy-start(f32[3,32,128]{2,1,0:T(8,128)} %param.8) | copy-start | bytes 147460
  17.1 0.8 copy-start.6
  17.1 1.0 %copy-start.7 = (f32[35,32,128]{2,1,0:T(8,128)}, f32[35,32,128]{2,1,0:T(8,128)S(1)}, u32[]{:S(2)}) copy-start(f32[35,32,128]{2,1,0:T(8,128)S(1)} %get-tuple-element.88) | copy-start | bytes 1720324
  19.5 4.2 %copy-start.10 = (f32[3,16,32,128]{3,2,1,0:T(8,128)S(1)}, f32[3,16,32,128]{3,2,1,0:T(8,128)}, u32[]{:S(2)}) copy-start(f32[3,16,32,128]{3,2,1,0:T(8,128)} %slice_multiply_fusion) | copy-start | bytes 2359300
  19.5 5.2 %collective-permute-start.1 = (f32[35,96,32]{1,2,0:T(8,128)}, f32[35,96,32]{1,2,0:T(8,128)S(1)}, u32[]{:S(2)}, u32[]{:S(2)}) collective-permute-start(f32[35,96,32]{1,2,0:T(8,128)} %copy.123), channel_id=1, source_target_pairs={{0,2},{2,4},{4,6},{1,3},{3,5},{5,7},{8,10},{10,12},{12,14},{9,11},... | collective-permute-start | bytes 1290248 | tf_op jit(solution)/shard_map/ppermute | solution.py:98
  22.2 5.8 %collective-permute-start.2 = (f32[35,96,32]{1,2,0:T(8,128)}, f32[35,96,32]{1,2,0:T(8,128)S(1)}, u32[]{:S(2)}, u32[]{:S(2)}) collective-permute-start(f32[35,96,32]{1,2,0:T(8,128)} %copy.124), channel_id=1, source_target_pairs={{2,0},{4,2},{6,4},{3,1},{5,3},{7,5},{10,8},{12,10},{14,12},{11,9},... | collective-permute-start | bytes 1290248 | tf_op jit(solution)/shard_map/ppermute | solution.py:99
  33.7 6.9 %copy-start.1 = (f32[35,96,192]{2,1,0:T(8,128)}, f32[35,96,192]{2,1,0:T(8,128)S(1)}, u32[]{:S(2)}) copy-start(f32[35,96,192]{2,1,0:T(8,128)S(1)} %pad_maximum_fusion.stack_ref) | copy-start | bytes 7741444
  34.6 23.1 %collective-permute-start.3 = (f32[2,36,132]{2,1,0:T(8,128)}, f32[2,36,132]{2,1,0:T(8,128)S(1)}, u32[]{:S(2)}, u32[]{:S(2)}) collective-permute-start(f32[2,36,132]{2,1,0:T(8,128)} %get-tuple-element.79), channel_id=1, source_target_pairs={{8,0},{16,8},{24,16},{9,1},{17,9},{25,17},{10,2},{18,10},{26,18},{... | collective-permute-start | bytes 114056 | tf_op jit(solution)/shard_map/ppermute | solution.py:24
  36.9 20.8 %collective-permute-start.4 = (f32[2,36,132]{2,1,0:T(8,128)}, f32[2,36,132]{2,1,0:T(8,128)}, u32[]{:S(2)}, u32[]{:S(2)}) collective-permute-start(f32[2,36,132]{2,1,0:T(8,128)} %get-tuple-element.80), channel_id=1, source_target_pairs={{0,8},{8,16},{16,24},{1,9},{9,17},{17,25},{2,10},{10,18},{18,26},{... | collective-permute-start | bytes 114056 | tf_op jit(solution)/shard_map/ppermute | solution.py:21
  49.4 2.7 %copy-start = (f32[3,8,96,192]{3,2,1,0:T(8,128)S(1)}, f32[3,8,96,192]{3,2,1,0:T(8,128)}, u32[]{:S(2)}) copy-start(f32[3,8,96,192]{3,2,1,0:T(8,128)} %shard_map.64) | copy-start | bytes 5308420
  54.3 1.4 %copy-start.15 = (f32[3,8,32,128]{3,2,0,1:T(8,128)S(1)}, f32[3,8,32,128]{3,2,0,1:T(8,128)}, u32[]{:S(2)}) copy-start(f32[3,8,32,128]{3,2,0,1:T(8,128)} %constant_dynamic-update-slice_fusion.31) | copy-start | bytes 1179652
  55.0 6.6 %collective-permute-start.5 = (f32[3,80,176]{2,1,0:T(8,128)S(1)}, f32[3,80,176]{2,1,0:T(8,128)S(1)}, u32[]{:S(2)}, u32[]{:S(2)}) collective-permute-start(f32[3,80,176]{2,1,0:T(8,128)S(1)} %fusion.56), channel_id=1, source_target_pairs={{0,8},{1,9},{2,10},{3,11},{4,12},{5,13},{6,14},{7,15}} | collective-permute-start | bytes 506888 | tf_op jit(solution)/shard_map/ppermute | solution.py:230
  64.6 7.6 %collective-permute-start.6 = (f32[3,64,160]{2,1,0:T(8,128)S(1)}, f32[3,64,160]{2,1,0:T(8,128)S(1)}, u32[]{:S(2)}, u32[]{:S(2)}) collective-permute-start(f32[3,64,160]{2,1,0:T(8,128)S(1)} %fusion.88), channel_id=1, source_target_pairs={{8,16},{9,17},{10,18},{11,19},{12,20},{13,21},{14,22},{15,23}} | collective-permute-start | bytes 368648 | tf_op jit(solution)/shard_map/ppermute | solution.py:230
  74.7 4.0 %collective-permute-start.7 = (f32[3,48,144]{2,1,0:T(8,128)S(1)}, f32[3,48,144]{2,1,0:T(8,128)S(1)}, u32[]{:S(2)}, u32[]{:S(2)}) collective-permute-start(f32[3,48,144]{2,1,0:T(8,128)S(1)} %fusion.120), channel_id=1, source_target_pairs={{16,24},{17,25},{18,26},{19,27},{20,28},{21,29},{22,30},{23,31}} | collective-permute-start | bytes 248840 | tf_op jit(solution)/shard_map/ppermute | solution.py:230
  81.2 1.0 %copy-start.3 = (f32[16,32,128]{2,1,0:T(8,128)S(1)}, f32[16,32,128]{2,1,0:T(8,128)}, u32[]{:S(2)}) copy-start(f32[16,32,128]{2,1,0:T(8,128)} %param.6) | copy-start | bytes 786436
  81.2 1.6 %copy-start.5 = (f32[7,16,32,128]{3,2,1,0:T(8,128)S(1)}, f32[7,16,32,128]{3,2,1,0:T(8,128)}, u32[]{:S(2)}) copy-start(f32[7,16,32,128]{3,2,1,0:T(8,128)} %copy-done.4) | copy-start | bytes 5505028
  81.2 1.8 %copy-start.9 = (f32[3,8,2,32,128]{4,3,2,1,0:T(8,128)S(1)}, f32[3,8,2,32,128]{4,3,2,1,0:T(8,128)}, u32[]{:S(2)}) copy-start(f32[3,8,2,32,128]{4,3,2,1,0:T(8,128)} %fusion.177) | copy-start | bytes 2359300
  81.2 1.8 %copy-start.11 = (f32[16,32,128]{2,1,0:T(8,128)S(1)}, f32[16,32,128]{2,1,0:T(8,128)}, u32[]{:S(2)}) copy-start(f32[16,32,128]{2,1,0:T(8,128)} %get-tuple-element.82) | copy-start | bytes 786436
  81.2 1.9 %copy-start.12 = (f32[16,32,128]{2,1,0:T(8,128)S(1)}, f32[16,32,128]{2,1,0:T(8,128)}, u32[]{:S(2)}) copy-start(f32[16,32,128]{2,1,0:T(8,128)} %fusion) | copy-start | bytes 786436
  83.7 6.3 %collective-permute-start.8 = (f32[4,2,128]{2,1,0:T(2,128)S(1)}, f32[4,2,128]{2,1,0:T(2,128)S(1)}, u32[]{:S(2)}, u32[]{:S(2)}) collective-permute-start(f32[4,2,128]{2,1,0:T(2,128)S(1)} %bitcast.374), channel_id=1, source_target_pairs={{0,2},{2,0},{4,6},{6,4},{1,3},{3,1},{5,7},{7,5},{8,10},{10,8},{12,... | collective-permute-start | bytes 12296 | tf_op jit(solution)/shard_map/ppermute | solution.py:42
  90.0 4.1 %collective-permute-start.9 = (f32[4,1,128]{2,0,1:T(4,128)S(1)}, f32[4,1,128]{2,0,1:T(4,128)S(1)}, u32[]{:S(2)}, u32[]{:S(2)}) collective-permute-start(f32[4,1,128]{2,0,1:T(4,128)S(1)} %bitcast.375), channel_id=1, source_target_pairs={{0,4},{4,0},{2,6},{6,2},{1,5},{5,1},{3,7},{7,3},{8,12},{12,8},{10,... | collective-permute-start | bytes 6152 | tf_op jit(solution)/shard_map/ppermute | solution.py:42

commit v21 on v20

--- a/solution.py
+++ b/solution.py
@@ -251,22 +251,21 @@
     image_now = jnp.concatenate(
         [colour_sum.reshape(3, n_view, piece_len), transmit.reshape(1, n_view, piece_len)], axis=0
     )
-    bit_count = n_view.bit_length() - 1
-    for bit_num in range(bit_count):
-        kept = image_now.shape[1]
-        pairs = image_now.reshape(4, kept // 2, 2, piece_len)
-        my_bit = view_idx // 2**bit_num % 2
-        first_half = my_bit == 0
-        keep = jnp.where(first_half, pairs[:, :, 0], pairs[:, :, 1])
-        send = jnp.where(first_half, pairs[:, :, 1], pairs[:, :, 0])
-        got = from_partner(send, "view", bit_num)
-        front = jnp.where(first_half, keep, got)
-        back = jnp.where(first_half, got, keep)
-        image_now = jnp.concatenate(
-            [front[:3] + front[3:] * back[:3], keep[3:] * got[3:]], axis=0
-        )
-    final_colour = image_now[:3, 0]
-    final_transmit = image_now[3:, 0]
+    received = [image_now[:, :, None]]
+    for shift in range(1, n_view):
+        piece = lax.dynamic_slice_in_dim(image_now, (view_idx + shift) % n_view, 1, axis=1)
+        route = [(source, (source + shift) % n_view) for source in range(n_view)]
+        received.append(lax.ppermute(piece, "view", route)[:, :, None])
+    own = lax.dynamic_slice_in_dim(image_now, view_idx, 1, axis=1)
+    received[0] = own[:, :, None]
+    by_shift = jnp.concatenate(received, axis=2)[:, 0]
+    order = (view_idx - jnp.arange(n_view)) % n_view
+    segments = jnp.take(by_shift, order, axis=1)
+    final_colour = segments[:3, n_view - 1]
+    final_transmit = segments[3:, n_view - 1]
+    for segment in range(n_view - 2, -1, -1):
+        final_colour = segments[:3, segment] + segments[3:, segment] * final_colour
+        final_transmit = segments[3:, segment] * final_transmit
     rows_out = brick_l // n_view
     opacity = 1.0 - final_transmit.reshape(1, rows_out, brick_a)
     return jnp.concatenate([final_colour.reshape(3, rows_out, brick_a), opacity], axis=0)

time: 96.8 us -> 98.1 us (1.013)
  the two profiles are of different devices: /device:TPU:16 before, /device:TPU:31 now
where the time goes in v21:
time: 98.1 us; the launch traced here: 97.6 us
  other arithmetic  31 us (32%)
  starting transfers between devices  22.5 us (23%)
  local copies, waits for them, and re-layouts  17 us (17%)
  waiting for transfers between devices  16.6 us (17%)
  Pallas kernels  8.84 us (9%)
  matrix products  1 us (1%)
    mul x31, other arithmetic, propagate(): current = current * fade_here  11.7 us
    ppermute x3, starting transfers between devices, shards(): received.append(lax.ppermute(piece, 'view', route)[:, :, None])  10.3 us
    pallas_call x1, Pallas kernels, fade_rim_of(): pl.pallas_call(kernel, out_shape=jax.ShapeDtypeStruct((colours, SLABS, ri...  8.84 us
    ppermute x3, waiting for transfers between devices, shards(): incoming = lax.ppermute(outgoing, 'light', [(section_num, section_num + 1)])  8.77 us
    unnamed x66, local copies, waits for them, and re-layouts  5.52 us
    ppermute x1, waiting for transfers between devices, halo(): got = lax.ppermute(send, axis, [(0, 1), (1, 0)])  4.79 us
    ppermute x1, starting transfers between devices, halo(): lax.ppermute(lax.slice_in_dim(block, 0, need, axis=dim), axis, backward)  4.1 us
    concatenate x2, other arithmetic, halo(): block = jnp.concatenate(lows + [block] + highs, axis=dim)  3.99 us
  transfers between devices with their start and end apart: 11, of which 4 were waited for; matrix products, arithmetic and copies ran while one was open for 26% of the time, Pallas kernels for 9%

profile of v21, /device:TPU:31, one launch (start us, length us, event | category | flops | bytes accessed | tf_op | source)
XLA Modules:
  0.0 97.6 jit_solution(9759161454533105492)
XLA Ops:
  0.0 1.0 %convert_element_type.39 = f32[16,32,128]{2,1,0:T(8,128)S(1)} convert(s32[16,32,128]{2,1,0:T(8,128)} %param.7) | non-fusion elementwise | flops 65536 | bytes 524288 | tf_op jit(solution)/shard_map/convert_element_type | solution.py:199
  1.1 1.1 %pad_maximum_fusion.5 = f32[35,32,128]{2,1,0:T(8,128)S(1)} fusion(f32[3,32,128]{2,1,0:T(8,128)} %param.8, f32[16,32,128]{2,1,0:T(8,128)S(1)} %convert_element_type.39, f32[16,32,128]{2,1,0:T(8,128)} %param.6), kind=kLoop, calls=%fused_computation.19 | loop fusion | flops 286720 | bytes 1146880 | tf_op jit(solution)/shard_map/concatenate | solution.py:199
  2.2 0.3 collective-permute-start
  2.5 1.4 %constant_dynamic-update-slice_fusion.31 = f32[3,8,32,128]{3,2,0,1:T(8,128)} fusion(f32[3,32,128]{2,1,0:T(8,128)} %param.8), kind=kLoop, calls=%fused_computation.334 | loop fusion | bytes 98304
  3.9 0.6 broadcast_compare_fusion.14
  4.6 0.4 slice_reduce_fusion.15
  5.1 2.6 %select_select_fusion = f32[7,16,32,128]{3,2,1,0:T(8,128)S(1)} fusion(f32[7]{0:T(128)S(1)} %get-tuple-element.10, f32[7]{0:T(128)S(1)} %get-tuple-element.11, f32[7]{0:T(128)S(1)} %get-tuple-element.12, f32[7]{0:T(128)S(1)} %get-tuple-element.13, f32[7]{0:T(128)S(1)} %get-tuple-element.14, f32[7]{0:T(128)S(1)} %get-tuple-element.15, ...), kind=kLoop, calls=%fused_computation.2 | loop fusion | flops 6881280 | bytes 2818496 | tf_op jit(solution)/shard_map/jit(_where)/select_n | solution.py:209
  7.7 0.8 fusion.149
  8.6 0.7 broadcast_multiply_fusion.mask_ref
  9.3 1.0 %fusion = f32[16,32,128]{2,1,0:T(8,128)} fusion(f32[16,32,128]{2,1,0:T(8,128)S(1)} %copy-done.2, f32[7,16,32,128]{3,2,1,0:T(8,128)S(1)} %select_select_fusion), kind=kOutput, calls=%fused_computation.5 | convolution fusion | flops 100876288 | bytes 786432 | tf_op jit(solution)/shard_map/dot_general | solution.py:244
  10.3 1.0 slice_multiply_fusion
  11.3 4.8 %collective-permute-done = f32[35,32,128]{2,1,0:T(8,128)S(1)} collective-permute-done((f32[35,32,128]{2,1,0:T(8,128)S(1)}, f32[35,32,128]{2,1,0:T(8,128)S(1)}, u32[]{:S(2)}, u32[]{:S(2)}) %collective-permute-start) | collective-permute-done | bytes 573472 | tf_op jit(solution)/shard_map/ppermute | solution.py:87
  16.4 0.6 fusion.179
  17.3 1.3 %copy.106 = f32[35,96,32]{1,2,0:T(8,128)} copy(f32[35,96,32]{2,1,0:T(8,128)S(1)} %get-tuple-element.83) | data formatting | bytes 860160 | tf_op jit(solution)/shard_map/slice | solution.py:97
  18.6 1.4 %collective-permute-start.1 = (f32[35,96,32]{1,2,0:T(8,128)}, f32[35,96,32]{1,2,0:T(8,128)S(1)}, u32[]{:S(2)}, u32[]{:S(2)}) collective-permute-start(f32[35,96,32]{1,2,0:T(8,128)} %copy.106), channel_id=1, source_target_pairs={{0,2},{2,4},{4,6},{1,3},{3,5},{5,7},{8,10},{10,12},{12,14},{9,11},... | collective-permute-start | bytes 1290248 | tf_op jit(solution)/shard_map/ppermute | solution.py:98
  20.0 1.3 %copy.107 = f32[35,96,32]{1,2,0:T(8,128)} copy(f32[35,96,32]{2,1,0:T(8,128)S(1)} %get-tuple-element.84) | data formatting | bytes 860160 | tf_op jit(solution)/shard_map/slice | solution.py:99
  21.3 4.1 %collective-permute-start.2 = (f32[35,96,32]{1,2,0:T(8,128)}, f32[35,96,32]{1,2,0:T(8,128)S(1)}, u32[]{:S(2)}, u32[]{:S(2)}) collective-permute-start(f32[35,96,32]{1,2,0:T(8,128)} %copy.107), channel_id=1, source_target_pairs={{2,0},{4,2},{6,4},{3,1},{5,3},{7,5},{10,8},{12,10},{14,12},{11,9},... | collective-permute-start | bytes 1290248 | tf_op jit(solution)/shard_map/ppermute | solution.py:99
  25.6 0.9 fusion.182
  26.6 1.8 %copy.108 = f32[35,96,32]{2,1,0:T(8,128)} copy(f32[35,96,32]{1,2,0:T(8,128)S(1)} %collective-permute-done.1) | data formatting | bytes 860160 | tf_op jit(solution)/shard_map/ppermute | solution.py:98
  28.3 1.7 %copy.109 = f32[35,96,32]{2,1,0:T(8,128)} copy(f32[35,96,32]{1,2,0:T(8,128)S(1)} %collective-permute-done.2) | data formatting | bytes 860160 | tf_op jit(solution)/shard_map/ppermute | solution.py:99
  30.1 3.9 %pad_maximum_fusion.stack_ref = f32[35,96,192]{2,1,0:T(8,128)S(1)} fusion(f32[35,96,32]{2,1,0:T(8,128)} %copy.109, f32[35,32,128]{2,1,0:T(8,128)} %copy-done.7, f32[3,32,128]{2,1,0:T(8,128)S(1)} %copy-done.14, f32[16,32,128]{2,1,0:T(8,128)} %copy-done.8, f32[16,32,128]{2,1,0:T(8,128)} %param.6, f32[35,32,128]{2,1,0:T(8,128)} %copy-done.6, f32[35,96,32]{2,1,0:T(8,128)} %copy.108), kind=kLoop, calls=%fused_computation.1 | loop fusion | flops 3870720 | bytes 5160960 | tf_op jit(solution)/shard_map/concatenate | solution.py:100
  34.0 0.9 fusion.178
  34.9 2.1 %collective-permute-start.3 = (f32[2,36,132]{2,1,0:T(8,128)}, f32[2,36,132]{2,1,0:T(8,128)S(1)}, u32[]{:S(2)}, u32[]{:S(2)}) collective-permute-start(f32[2,36,132]{2,1,0:T(8,128)} %get-tuple-element.79), channel_id=1, source_target_pairs={{8,0},{16,8},{24,16},{9,1},{17,9},{25,17},{10,2},{18,10},{26,18},{... | collective-permute-start | bytes 114056 | tf_op jit(solution)/shard_map/ppermute | solution.py:24
  37.0 1.5 %collective-permute-start.4 = (f32[2,36,132]{2,1,0:T(8,128)}, f32[2,36,132]{2,1,0:T(8,128)}, u32[]{:S(2)}, u32[]{:S(2)}) collective-permute-start(f32[2,36,132]{2,1,0:T(8,128)} %get-tuple-element.80), channel_id=1, source_target_pairs={{0,8},{8,16},{16,24},{1,9},{9,17},{17,25},{2,10},{10,18},{18,26},{... | collective-permute-start | bytes 114056 | tf_op jit(solution)/shard_map/ppermute | solution.py:21
  38.4 8.8 %shard_map.64 = f32[3,8,96,192]{3,2,1,0:T(8,128)} custom-call(f32[3,16]{1,0:T(4,128)} %table_ref.1, f32[35,96,192]{2,1,0:T(8,128)} %copy-done.1, f32[96,192]{1,0:T(8,128)} %broadcast_multiply_fusion.mask_ref), custom_call_target="tpu_custom_call" | custom-call | tf_op jit(solution)/shard_map/pallas_call | solution.py:173
  47.3 1.2 %fusion.17 = f32[3,96,192]{2,1,0:T(8,128)S(1)} fusion(f32[3,8,96,192]{3,2,1,0:T(8,128)} %shard_map.64, f32[35,96,192]{2,1,0:T(8,128)} %copy-done.1), kind=kLoop, calls=%fused_computation.46 | loop fusion | flops 55296 | bytes 663552 | tf_op jit(solution)/shard_map/mul | solution.py:129
  48.5 1.4 %fusion.13 = (f32[3,94,190]{2,1,0:T(8,128)S(1)}, f32[3,94,190]{2,1,0:T(8,128)S(1)}) fusion(f32[3,8,96,192]{3,2,1,0:T(8,128)} %shard_map.64, f32[3,96,192]{2,1,0:T(8,128)S(1)} %fusion.17), kind=kLoop, calls=%fused_computation.38 | loop fusion | flops 428640 | bytes 1714560 | tf_op jit(solution)/shard_map/mul | solution.py:129
  50.0 0.4 fusion.9
  50.4 0.4 fusion.5
  50.9 0.4 fusion.30
  51.3 0.4 fusion.26
  51.7 0.4 fusion.22
  52.1 0.4 fusion.18
  52.6 0.3 fusion.56
  52.9 0.7 collective-permute-start.5
  54.2 1.4 %slice.1099 = f32[16,36,132]{2,1,0:T(8,128)S(1)} slice(f32[35,96,192]{2,1,0:T(8,128)} %copy-done.1), slice={[0:16], [30:66], [30:162]} | slice | bytes 608256 | tf_op jit(solution)/shard_map/slice | solution.py:203
  55.6 0.9 pad_maximum_fusion.2
  56.5 2.0 %multiply_multiply_fusion.1 = (f32[18,34,130]{2,1,0:T(8,128)S(1)}, f32[18,34,130]{2,1,0:T(8,128)S(1)}) fusion(f32[16,36,132]{2,1,0:T(8,128)S(1)} %slice.1099, f32[2,36,132]{2,1,0:T(8,128)} %collective-permute-done.4, f32[2,36,132]{2,1,0:T(8,128)S(1)} %collective-permute-done.3, f32[130]{0:T(256)S(1)} %and_convert_fusion.2, ...), kind=kLoop, calls=%fused_computation.7 | loop fusion | flops 1750320 | bytes 2292568 | tf_op jit(solution)/shard_map/mul | solution.py:63
  58.6 0.9 fusion.37
  59.6 0.4 fusion.49
  60.0 0.4 fusion.45
  60.4 0.4 fusion.41
  60.8 0.4 fusion.69
  61.1 0.4 fusion.65
  61.5 0.4 fusion.61
  61.8 0.4 fusion.57
  62.5 0.7 collective-permute-start.6
  63.9 0.3 fusion.81
  64.3 0.3 fusion.77
  64.6 0.3 fusion.73
  65.2 0.3 fusion.97
  65.5 0.3 fusion.93
  65.8 0.3 fusion.89
  66.3 1.5 %collective-permute-start.7 = (f32[3,48,144]{2,1,0:T(8,128)S(1)}, f32[3,48,144]{2,1,0:T(8,128)S(1)}, u32[]{:S(2)}, u32[]{:S(2)}) collective-permute-start(f32[3,48,144]{2,1,0:T(8,128)S(1)} %fusion.120), channel_id=1, source_target_pairs={{16,24},{17,25},{18,26},{19,27},{20,28},{21,29},{22,30},{23,31}} | collective-permute-start | bytes 248840 | tf_op jit(solution)/shard_map/ppermute | solution.py:230
  68.5 8.8 %collective-permute-done.7 = f32[3,48,144]{2,1,0:T(8,128)S(1)} collective-permute-done((f32[3,48,144]{2,1,0:T(8,128)S(1)}, f32[3,48,144]{2,1,0:T(8,128)S(1)}, u32[]{:S(2)}, u32[]{:S(2)}) %collective-permute-start.7) | collective-permute-done | bytes 82976 | tf_op jit(solution)/shard_map/ppermute | solution.py:230
  80.1 0.6 copy-done.3
  80.7 0.6 copy-done.5
  81.7 0.5 fusion.3
  82.3 3.1 %collective-permute-start.8 = (f32[4,1,128]{2,0,1:T(4,128)S(1)}, f32[4,1,128]{2,0,1:T(4,128)S(1)}, u32[]{:S(2)}, u32[]{:S(2)}) collective-permute-start(f32[4,1,128]{2,0,1:T(4,128)S(1)} %get-tuple-element.110), channel_id=1, source_target_pairs={{0,2},{2,4},{4,6},{6,0},{1,3},{3,5},{5,7},{7,1},{8,10},{10,12},{12... | collective-permute-start | bytes 6152 | tf_op jit(solution)/shard_map/ppermute | solution.py:258
  85.4 7.2 %collective-permute-start.9 = (f32[4,1,128]{2,0,1:T(4,128)S(1)}, f32[4,1,128]{2,0,1:T(4,128)S(1)}, u32[]{:S(2)}, u32[]{:S(2)}) collective-permute-start(f32[4,1,128]{2,0,1:T(4,128)S(1)} %get-tuple-element.111), channel_id=1, source_target_pairs={{0,4},{2,6},{4,0},{6,2},{1,5},{3,7},{5,1},{7,3},{8,12},{10,14},{12... | collective-permute-start | bytes 6152 | tf_op jit(solution)/shard_map/ppermute | solution.py:258
  92.6 1.2 %collective-permute-done.9 = f32[4,1,128]{2,0,1:T(4,128)S(1)} collective-permute-done((f32[4,1,128]{2,0,1:T(4,128)S(1)}, f32[4,1,128]{2,0,1:T(4,128)S(1)}, u32[]{:S(2)}, u32[]{:S(2)}) %collective-permute-start.9) | collective-permute-done | bytes 2080 | tf_op jit(solution)/shard_map/ppermute | solution.py:258
  93.9 1.7 %collective-permute-done.10 = f32[4,1,128]{2,0,1:T(4,128)S(1)} collective-permute-done((f32[4,1,128]{2,0,1:T(4,128)S(1)}, f32[4,1,128]{2,0,1:T(4,128)S(1)}, u32[]{:S(2)}, u32[]{:S(2)}) %collective-permute-start.10) | collective-permute-done | bytes 2080 | tf_op jit(solution)/shard_map/ppermute | solution.py:258
  95.6 0.6 gather_fusion
  97.0 0.6 pad_maximum_fusion.6
  (121 shorter events, 7.7 us)
Async XLA Ops:
  0.0 3.9 %copy-start.13 = (s32[16,32,128]{2,1,0:T(8,128)S(1)}, s32[16,32,128]{2,1,0:T(8,128)}, u32[]{:S(2)}) copy-start(s32[16,32,128]{2,1,0:T(8,128)} %param.7) | copy-start | bytes 786436
  0.0 4.6 %copy-start.16 = (f32[3,16]{1,0:T(4,128)S(1)}, f32[3,16]{1,0:T(4,128)}, u32[]{:S(2)}) copy-start(f32[3,16]{1,0:T(4,128)} %table_ref.1) | copy-start | bytes 580
  0.0 4.6 %copy-start.18 = (f32[16]{0:T(128)S(1)}, f32[16]{0:T(128)}, u32[]{:S(2)}) copy-start(f32[16]{0:T(128)} %param.9) | copy-start | bytes 196
  0.0 4.6 %copy-start.17 = (f32[3,16]{1,0:T(4,128)S(1)}, f32[3,16]{1,0:T(4,128)}, u32[]{:S(2)}) copy-start(f32[3,16]{1,0:T(4,128)} %param.11) | copy-start | bytes 580
  1.0 15.2 %copy-start.8 = (f32[16,32,128]{2,1,0:T(8,128)}, f32[16,32,128]{2,1,0:T(8,128)S(1)}, u32[]{:S(2)}) copy-start(f32[16,32,128]{2,1,0:T(8,128)S(1)} %convert_element_type.39) | copy-start | bytes 786436
  2.2 13.9 %collective-permute-start = (f32[35,32,128]{2,1,0:T(8,128)S(1)}, f32[35,32,128]{2,1,0:T(8,128)S(1)}, u32[]{:S(2)}, u32[]{:S(2)}) collective-permute-start(f32[35,32,128]{2,1,0:T(8,128)S(1)} %pad_maximum_fusion.5), channel_id=1, source_target_pairs={{0,1},{1,0},{2,3},{3,2},{4,5},{5,4},{6,7},{7,6},{8,9},{9,8},{10,11... | collective-permute-start | bytes 1720328 | tf_op jit(solution)/shard_map/ppermute | solution.py:87
  3.9 3.8 %copy-start.2 = (f32[16,32,128]{2,1,0:T(8,128)S(1)}, f32[16,32,128]{2,1,0:T(8,128)}, u32[]{:S(2)}) copy-start(f32[16,32,128]{2,1,0:T(8,128)} %param.6) | copy-start | bytes 786436
  7.7 8.6 %copy-start.4 = (f32[7,16,32,128]{3,2,1,0:T(8,128)}, f32[7,16,32,128]{3,2,1,0:T(8,128)S(1)}, u32[]{:S(2)}) copy-start(f32[7,16,32,128]{3,2,1,0:T(8,128)S(1)} %select_select_fusion) | copy-start | bytes 5505028
  10.3 5.9 %copy-start.14 = (f32[3,32,128]{2,1,0:T(8,128)S(1)}, f32[3,32,128]{2,1,0:T(8,128)}, u32[]{:S(2)}) copy-start(f32[3,32,128]{2,1,0:T(8,128)} %param.8) | copy-start | bytes 147460
  16.2 0.8 copy-start.6
  16.2 1.0 %copy-start.7 = (f32[35,32,128]{2,1,0:T(8,128)}, f32[35,32,128]{2,1,0:T(8,128)S(1)}, u32[]{:S(2)}) copy-start(f32[35,32,128]{2,1,0:T(8,128)S(1)} %get-tuple-element.88) | copy-start | bytes 1720324
  18.6 7.0 %copy-start.10 = (f32[3,16,32,128]{3,2,1,0:T(8,128)S(1)}, f32[3,16,32,128]{3,2,1,0:T(8,128)}, u32[]{:S(2)}) copy-start(f32[3,16,32,128]{3,2,1,0:T(8,128)} %slice_multiply_fusion) | copy-start | bytes 2359300
  18.6 8.0 %collective-permute-start.1 = (f32[35,96,32]{1,2,0:T(8,128)}, f32[35,96,32]{1,2,0:T(8,128)S(1)}, u32[]{:S(2)}, u32[]{:S(2)}) collective-permute-start(f32[35,96,32]{1,2,0:T(8,128)} %copy.106), channel_id=1, source_target_pairs={{0,2},{2,4},{4,6},{1,3},{3,5},{5,7},{8,10},{10,12},{12,14},{9,11},... | collective-permute-start | bytes 1290248 | tf_op jit(solution)/shard_map/ppermute | solution.py:98
  21.3 7.0 %collective-permute-start.2 = (f32[35,96,32]{1,2,0:T(8,128)}, f32[35,96,32]{1,2,0:T(8,128)S(1)}, u32[]{:S(2)}, u32[]{:S(2)}) collective-permute-start(f32[35,96,32]{1,2,0:T(8,128)} %copy.107), channel_id=1, source_target_pairs={{2,0},{4,2},{6,4},{3,1},{5,3},{7,5},{10,8},{12,10},{14,12},{11,9},... | collective-permute-start | bytes 1290248 | tf_op jit(solution)/shard_map/ppermute | solution.py:99
  34.0 4.5 %copy-start.1 = (f32[35,96,192]{2,1,0:T(8,128)}, f32[35,96,192]{2,1,0:T(8,128)S(1)}, u32[]{:S(2)}) copy-start(f32[35,96,192]{2,1,0:T(8,128)S(1)} %pad_maximum_fusion.stack_ref) | copy-start | bytes 7741444
  34.9 20.7 %collective-permute-start.3 = (f32[2,36,132]{2,1,0:T(8,128)}, f32[2,36,132]{2,1,0:T(8,128)S(1)}, u32[]{:S(2)}, u32[]{:S(2)}) collective-permute-start(f32[2,36,132]{2,1,0:T(8,128)} %get-tuple-element.79), channel_id=1, source_target_pairs={{8,0},{16,8},{24,16},{9,1},{17,9},{25,17},{10,2},{18,10},{26,18},{... | collective-permute-start | bytes 114056 | tf_op jit(solution)/shard_map/ppermute | solution.py:24
  37.0 18.6 %collective-permute-start.4 = (f32[2,36,132]{2,1,0:T(8,128)}, f32[2,36,132]{2,1,0:T(8,128)}, u32[]{:S(2)}, u32[]{:S(2)}) collective-permute-start(f32[2,36,132]{2,1,0:T(8,128)} %get-tuple-element.80), channel_id=1, source_target_pairs={{0,8},{8,16},{16,24},{1,9},{9,17},{17,25},{2,10},{10,18},{18,26},{... | collective-permute-start | bytes 114056 | tf_op jit(solution)/shard_map/ppermute | solution.py:21
  47.3 2.7 %copy-start = (f32[3,8,96,192]{3,2,1,0:T(8,128)S(1)}, f32[3,8,96,192]{3,2,1,0:T(8,128)}, u32[]{:S(2)}) copy-start(f32[3,8,96,192]{3,2,1,0:T(8,128)} %shard_map.64) | copy-start | bytes 5308420
  52.1 1.4 %copy-start.15 = (f32[3,8,32,128]{3,2,0,1:T(8,128)S(1)}, f32[3,8,32,128]{3,2,0,1:T(8,128)}, u32[]{:S(2)}) copy-start(f32[3,8,32,128]{3,2,0,1:T(8,128)} %constant_dynamic-update-slice_fusion.31) | copy-start | bytes 1179652
  52.9 6.6 %collective-permute-start.5 = (f32[3,80,176]{2,1,0:T(8,128)S(1)}, f32[3,80,176]{2,1,0:T(8,128)S(1)}, u32[]{:S(2)}, u32[]{:S(2)}) collective-permute-start(f32[3,80,176]{2,1,0:T(8,128)S(1)} %fusion.56), channel_id=1, source_target_pairs={{0,8},{1,9},{2,10},{3,11},{4,12},{5,13},{6,14},{7,15}} | collective-permute-start | bytes 506888 | tf_op jit(solution)/shard_map/ppermute | solution.py:230
  62.5 1.3 %collective-permute-start.6 = (f32[3,64,160]{2,1,0:T(8,128)S(1)}, f32[3,64,160]{2,1,0:T(8,128)S(1)}, u32[]{:S(2)}, u32[]{:S(2)}) collective-permute-start(f32[3,64,160]{2,1,0:T(8,128)S(1)} %fusion.88), channel_id=1, source_target_pairs={{8,16},{9,17},{10,18},{11,19},{12,20},{13,21},{14,22},{15,23}} | collective-permute-start | bytes 368648 | tf_op jit(solution)/shard_map/ppermute | solution.py:230
  66.3 10.9 %collective-permute-start.7 = (f32[3,48,144]{2,1,0:T(8,128)S(1)}, f32[3,48,144]{2,1,0:T(8,128)S(1)}, u32[]{:S(2)}, u32[]{:S(2)}) collective-permute-start(f32[3,48,144]{2,1,0:T(8,128)S(1)} %fusion.120), channel_id=1, source_target_pairs={{16,24},{17,25},{18,26},{19,27},{20,28},{21,29},{22,30},{23,31}} | collective-permute-start | bytes 248840 | tf_op jit(solution)/shard_map/ppermute | solution.py:230
  79.8 1.0 copy-start.3
  79.8 1.6 %copy-start.5 = (f32[7,16,32,128]{3,2,1,0:T(8,128)S(1)}, f32[7,16,32,128]{3,2,1,0:T(8,128)}, u32[]{:S(2)}) copy-start(f32[7,16,32,128]{3,2,1,0:T(8,128)} %copy-done.4) | copy-start | bytes 5505028
  79.8 1.8 %copy-start.9 = (f32[3,8,2,32,128]{4,3,2,1,0:T(8,128)S(1)}, f32[3,8,2,32,128]{4,3,2,1,0:T(8,128)}, u32[]{:S(2)}) copy-start(f32[3,8,2,32,128]{4,3,2,1,0:T(8,128)} %fusion.182) | copy-start | bytes 2359300
  79.8 1.8 %copy-start.11 = (f32[16,32,128]{2,1,0:T(8,128)S(1)}, f32[16,32,128]{2,1,0:T(8,128)}, u32[]{:S(2)}) copy-start(f32[16,32,128]{2,1,0:T(8,128)} %get-tuple-element.82) | copy-start | bytes 786436
  79.8 1.9 %copy-start.12 = (f32[16,32,128]{2,1,0:T(8,128)S(1)}, f32[16,32,128]{2,1,0:T(8,128)}, u32[]{:S(2)}) copy-start(f32[16,32,128]{2,1,0:T(8,128)} %fusion) | copy-start | bytes 786436
  82.3 10.3 %collective-permute-start.8 = (f32[4,1,128]{2,0,1:T(4,128)S(1)}, f32[4,1,128]{2,0,1:T(4,128)S(1)}, u32[]{:S(2)}, u32[]{:S(2)}) collective-permute-start(f32[4,1,128]{2,0,1:T(4,128)S(1)} %get-tuple-element.110), channel_id=1, source_target_pairs={{0,2},{2,4},{4,6},{6,0},{1,3},{3,5},{5,7},{7,1},{8,10},{10,12},{12... | collective-permute-start | bytes 6152 | tf_op jit(solution)/shard_map/ppermute | solution.py:258
  85.4 8.5 %collective-permute-start.9 = (f32[4,1,128]{2,0,1:T(4,128)S(1)}, f32[4,1,128]{2,0,1:T(4,128)S(1)}, u32[]{:S(2)}, u32[]{:S(2)}) collective-permute-start(f32[4,1,128]{2,0,1:T(4,128)S(1)} %get-tuple-element.111), channel_id=1, source_target_pairs={{0,4},{2,6},{4,0},{6,2},{1,5},{3,7},{5,1},{7,3},{8,12},{10,14},{12... | collective-permute-start | bytes 6152 | tf_op jit(solution)/shard_map/ppermute | solution.py:258
  92.6 3.0 %collective-permute-start.10 = (f32[4,1,128]{2,0,1:T(4,128)S(1)}, f32[4,1,128]{2,0,1:T(4,128)S(1)}, u32[]{:S(2)}, u32[]{:S(2)}) collective-permute-start(f32[4,1,128]{2,0,1:T(4,128)S(1)} %get-tuple-element.112), channel_id=1, source_target_pairs={{0,6},{2,0},{4,2},{6,4},{1,7},{3,1},{5,3},{7,5},{8,14},{10,8},{12,... | collective-permute-start | bytes 6152 | tf_op jit(solution)/shard_map/ppermute | solution.py:258

commit v22 on v20

--- a/solution.py
+++ b/solution.py
@@ -235,16 +235,21 @@
         * rim_mask(view_idx, n_view, brick_v, 1)[None, None, :]
     )
     shading = shade_from(padded, inside)
-    lighting = (starts[:, :, None] * jnp.exp(-light_step * running)).reshape(
-        3, brick_l, brick_a, brick_v
-    )
     optical = looked[0] * density * view_step
-    colour = (1.0 - jnp.exp(-optical))[None] * looked[4:7] * (shading[None] * lighting + AMBIENT)
     upper = (jnp.arange(brick_v)[:, None] < jnp.arange(brick_v)[None, :]).astype(jnp.float32)
     before = jnp.dot(optical.reshape(-1, brick_v), upper, precision=lax.Precision.HIGHEST).reshape(
         brick_l, brick_a, brick_v
     )
-    colour_sum = jnp.sum(colour * jnp.exp(-before)[None], axis=-1)
+    weight = (1.0 - jnp.exp(-optical))[None] * looked[4:7] * jnp.exp(-before)[None]
+    lit = (weight * shading[None]).reshape(3, SLABS, layer_rows, brick_a, brick_v) * jnp.exp(
+        -light_step * running
+    )
+    ambient_sum = AMBIENT * jnp.sum(weight, axis=-1)
+    lit, ambient_sum = lax.optimization_barrier((lit, ambient_sum))
+    colour_sum = (
+        jnp.sum((lit * starts[:, :, None]).reshape(3, brick_l, brick_a, brick_v), axis=-1)
+        + ambient_sum
+    )
     transmit = jnp.exp(-jnp.sum(optical, axis=-1))
     pixels = brick_l * brick_a
     piece_len = pixels // n_view

time: 96.8 us -> 104 us (1.074)
  local copies, waits for them, and re-layouts: 16 us -> 19.6 us
  other arithmetic: 30.9 us -> 34 us
    slice x2, local copies, waits for them, and re-layouts: 1.94 us -> 4.29 us  [halo(): low = lax.slice_in_dim(block, size - need, None, axis=dim)]
    ppermute x1, waiting for transfers between devices: 0.01 us -> 1.89 us  [padded_2(): lax.ppermute(lax.slice_in_dim(block, block.shape[dim] - width, None, axis...]
    convert_element_type x5, other arithmetic: 0.03 us -> 1.7 us  [rim_mask(): return ((places >= 0) & (places < devices * width)).astype(jnp.float32)]
    slice x1, local copies, waits for them, and re-layouts: 1.32 us -> 2.79 us  [halo(): lax.slice_in_dim(block, 0, need, axis=dim)]
    ppermute x1, waiting for transfers between devices: 4.47 us -> 3.25 us  [halo(): got = lax.ppermute(send, axis, [(0, 1), (1, 0)])]
    select_n x1, other arithmetic: 2.57 us -> 3.66 us  [shards(): jnp.where((labels == material)[None], table_all[:, material, None, None,...]
  transfers between devices with their start and end apart: 10 -> 10, of which waited for: 6 -> 7; matrix products, arithmetic and copies ran while one was open for 27% -> 23% of each run, Pallas kernels for 9% -> 0%
where the time goes in v22:
time: 104 us; the launch traced here: 102 us
  other arithmetic  34 us (33%)
  starting transfers between devices  21.5 us (21%)
  local copies, waits for them, and re-layouts  19.6 us (19%)
  waiting for transfers between devices  16.7 us (16%)
  Pallas kernels  8.78 us (8%)
    mul x31, other arithmetic, propagate(): current = current * fade_here  11.7 us
    pallas_call x1, Pallas kernels, fade_rim_of(): pl.pallas_call(kernel, out_shape=jax.ShapeDtypeStruct((colours, SLABS, ri...  8.78 us
    ppermute x2, starting transfers between devices, from_partner(): return lax.ppermute(block, axis, route)  7.83 us
    ppermute x3, waiting for transfers between devices, shards(): incoming = lax.ppermute(outgoing, 'light', [(section_num, section_num + 1)])  7.59 us
    unnamed x67, local copies, waits for them, and re-layouts  4.54 us
    slice x2, local copies, waits for them, and re-layouts, halo(): low = lax.slice_in_dim(block, size - need, None, axis=dim)  4.29 us
    concatenate x2, other arithmetic, halo(): block = jnp.concatenate(lows + [block] + highs, axis=dim)  3.99 us
    select_n x1, other arithmetic, shards(): jnp.where((labels == material)[None], table_all[:, material, None, None,...  3.66 us
  transfers between devices with their start and end apart: 10, of which 7 were waited for; matrix products, arithmetic and copies ran while one was open for 23% of the time, Pallas kernels for 0%

profile of v22, /device:TPU:16, one launch (start us, length us, event | category | flops | bytes accessed | tf_op | source)
XLA Modules:
  0.0 102.2 jit_solution(4828779473681372603)
XLA Ops:
  0.0 1.0 %convert_element_type.39 = f32[16,32,128]{2,1,0:T(8,128)S(1)} convert(s32[16,32,128]{2,1,0:T(8,128)} %param.7) | non-fusion elementwise | flops 65536 | bytes 524288 | tf_op jit(solution)/shard_map/convert_element_type | solution.py:199
  1.1 1.9 %pad_maximum_fusion.5 = f32[35,32,128]{2,1,0:T(8,128)} fusion(f32[3,32,128]{2,1,0:T(8,128)} %param.8, f32[16,32,128]{2,1,0:T(8,128)S(1)} %convert_element_type.39, f32[16,32,128]{2,1,0:T(8,128)} %param.6), kind=kLoop, calls=%fused_computation.23 | loop fusion | flops 286720 | bytes 1146880 | tf_op jit(solution)/shard_map/concatenate | solution.py:199
  3.0 1.5 %collective-permute-start = (f32[35,32,128]{2,1,0:T(8,128)}, f32[35,32,128]{2,1,0:T(8,128)S(1)}, u32[]{:S(2)}, u32[]{:S(2)}) collective-permute-start(f32[35,32,128]{2,1,0:T(8,128)} %pad_maximum_fusion.5), channel_id=1, source_target_pairs={{0,1},{1,0},{2,3},{3,2},{4,5},{5,4},{6,7},{7,6},{8,9},{9,8},{10,11... | collective-permute-start | bytes 1720328 | tf_op jit(solution)/shard_map/ppermute | solution.py:87
  4.5 1.3 %broadcast_compare_fusion.14 = (pred[16,32,128]{2,1,0:T(8,128)(4,1)S(1)}, pred[16,32,128]{2,1,0:T(8,128)(4,1)S(1)}, pred[16,32,128]{2,1,0:T(8,128)(4,1)S(1)}, pr...) fusion(s32[16,32,128]{2,1,0:T(8,128)S(1)} %copy-done.11), kind=kLoop, calls=%fused_computation.282 | loop fusion | flops 983040 | bytes 1245184 | tf_op jit(solution)/shard_map/eq | solution.py:210
  5.8 0.6 and_convert_fusion
  6.4 0.6 and_convert_fusion.1
  7.0 0.5 and_convert_fusion.4
  7.5 0.4 slice_reduce_fusion.15
  8.0 3.7 %select_select_fusion = f32[7,16,32,128]{3,2,1,0:T(8,128)S(1)} fusion(f32[7]{0:T(128)S(1)} %get-tuple-element.10, f32[7]{0:T(128)S(1)} %get-tuple-element.11, f32[7]{0:T(128)S(1)} %get-tuple-element.12, f32[7]{0:T(128)S(1)} %get-tuple-element.13, f32[7]{0:T(128)S(1)} %get-tuple-element.14, f32[7]{0:T(128)S(1)} %get-tuple-element.15, ...), kind=kLoop, calls=%fused_computation.1 | loop fusion | flops 6881280 | bytes 2818496 | tf_op jit(solution)/shard_map/jit(_where)/select_n | solution.py:209
  11.7 0.8 fusion.146
  12.6 0.6 constant_dynamic-update-slice_fusion.31
  13.2 1.4 %broadcast_multiply_fusion.mask_ref = f32[96,192]{1,0:T(8,128)} fusion(f32[192]{0:T(256)} %and_convert_fusion, f32[96]{0:T(128)} %and_convert_fusion.1), kind=kLoop, calls=%fused_computation.380 | loop fusion | flops 18432 | bytes 74880 | tf_op jit(solution)/shard_map/mul | solution.py:111
  14.7 3.2 %collective-permute-done = f32[35,32,128]{2,1,0:T(8,128)S(1)} collective-permute-done((f32[35,32,128]{2,1,0:T(8,128)}, f32[35,32,128]{2,1,0:T(8,128)S(1)}, u32[]{:S(2)}, u32[]{:S(2)}) %collective-permute-start) | collective-permute-done | bytes 573472 | tf_op jit(solution)/shard_map/ppermute | solution.py:87
  18.2 2.3 %fusion.176 = (f32[35,96,32]{2,1,0:T(8,128)}, f32[35,96,32]{2,1,0:T(8,128)}) fusion(f32[35,96,128]{2,1,0:T(8,128)S(1)} %pad_maximum_fusion.1), kind=kLoop, calls=%fused_computation.428 | loop fusion | bytes 1720320 | tf_op jit(solution)/shard_map/slice | solution.py:97
  20.6 1.9 %copy.123 = f32[35,96,32]{1,2,0:T(8,128)S(1)} copy(f32[35,96,32]{2,1,0:T(8,128)} %get-tuple-element.90) | data formatting | bytes 860160 | tf_op jit(solution)/shard_map/slice | solution.py:97
  22.5 1.3 %collective-permute-start.1 = (f32[35,96,32]{1,2,0:T(8,128)S(1)}, f32[35,96,32]{1,2,0:T(8,128)S(1)}, u32[]{:S(2)}, u32[]{:S(2)}) collective-permute-start(f32[35,96,32]{1,2,0:T(8,128)S(1)} %copy.123), channel_id=1, source_target_pairs={{0,2},{2,4},{4,6},{1,3},{3,5},{5,7},{8,10},{10,12},{12,14},{9,11},... | collective-permute-start | bytes 1290248 | tf_op jit(solution)/shard_map/ppermute | solution.py:98
  23.8 2.8 %copy.124 = f32[35,96,32]{1,2,0:T(8,128)} copy(f32[35,96,32]{2,1,0:T(8,128)} %get-tuple-element.91) | data formatting | bytes 860160 | tf_op jit(solution)/shard_map/slice | solution.py:99
  26.6 1.5 %collective-permute-start.2 = (f32[35,96,32]{1,2,0:T(8,128)}, f32[35,96,32]{1,2,0:T(8,128)}, u32[]{:S(2)}, u32[]{:S(2)}) collective-permute-start(f32[35,96,32]{1,2,0:T(8,128)} %copy.124), channel_id=1, source_target_pairs={{2,0},{4,2},{6,4},{3,1},{5,3},{7,5},{10,8},{12,10},{14,12},{11,9},... | collective-permute-start | bytes 1290248 | tf_op jit(solution)/shard_map/ppermute | solution.py:99
  28.2 1.0 fusion.3
  29.2 1.8 %copy.125 = f32[35,96,32]{2,1,0:T(8,128)} copy(f32[35,96,32]{1,2,0:T(8,128)S(1)} %collective-permute-done.1) | data formatting | bytes 860160 | tf_op jit(solution)/shard_map/ppermute | solution.py:98
  30.9 1.6 %collective-permute-done.2 = f32[35,96,32]{1,2,0:T(8,128)} collective-permute-done((f32[35,96,32]{1,2,0:T(8,128)}, f32[35,96,32]{1,2,0:T(8,128)}, u32[]{:S(2)}, u32[]{:S(2)}) %collective-permute-start.2) | collective-permute-done | bytes 430112 | tf_op jit(solution)/shard_map/ppermute | solution.py:99
  32.5 2.8 %copy.126 = f32[35,96,32]{2,1,0:T(8,128)} copy(f32[35,96,32]{1,2,0:T(8,128)} %collective-permute-done.2) | data formatting | bytes 860160 | tf_op jit(solution)/shard_map/ppermute | solution.py:99
  35.3 3.9 %pad_maximum_fusion.stack_ref = f32[35,96,192]{2,1,0:T(8,128)S(1)} fusion(f32[35,96,32]{2,1,0:T(8,128)} %copy.126, f32[35,32,128]{2,1,0:T(8,128)} %copy-done.7, f32[3,32,128]{2,1,0:T(8,128)S(1)} %copy-done.12, f32[16,32,128]{2,1,0:T(8,128)} %copy-done.8, f32[16,32,128]{2,1,0:T(8,128)} %param.6, f32[35,32,128]{2,1,0:T(8,128)} %copy-done.6, f32[35,96,32]{2,1,0:T(8,128)} %copy.125), kind=kLoop, calls=%fused_computation | loop fusion | flops 3870720 | bytes 5160960 | tf_op jit(solution)/shard_map/concatenate | solution.py:100
  39.2 0.9 fusion.175
  40.1 0.9 copy-done.1
  40.9 8.8 %shard_map.64 = f32[3,8,96,192]{3,2,1,0:T(8,128)} custom-call(f32[3,16]{1,0:T(4,128)} %table_ref.1, f32[35,96,192]{2,1,0:T(8,128)} %copy-done.1, f32[96,192]{1,0:T(8,128)} %broadcast_multiply_fusion.mask_ref), custom_call_target="tpu_custom_call" | custom-call | tf_op jit(solution)/shard_map/pallas_call | solution.py:173
  49.7 1.2 %fusion.20 = f32[3,96,192]{2,1,0:T(8,128)S(1)} fusion(f32[3,8,96,192]{3,2,1,0:T(8,128)} %shard_map.64, f32[35,96,192]{2,1,0:T(8,128)} %copy-done.1), kind=kLoop, calls=%fused_computation.50 | loop fusion | flops 55296 | bytes 663552 | tf_op jit(solution)/shard_map/mul | solution.py:129
  51.0 1.4 %fusion.16 = (f32[3,94,190]{2,1,0:T(8,128)S(1)}, f32[3,94,190]{2,1,0:T(8,128)S(1)}) fusion(f32[3,8,96,192]{3,2,1,0:T(8,128)} %shard_map.64, f32[3,96,192]{2,1,0:T(8,128)S(1)} %fusion.20), kind=kLoop, calls=%fused_computation.42 | loop fusion | flops 428640 | bytes 1714560 | tf_op jit(solution)/shard_map/mul | solution.py:129
  52.4 0.4 fusion.12
  52.8 0.4 fusion.8
  53.3 0.4 fusion.33
  53.7 0.4 fusion.29
  54.1 0.4 fusion.25
  54.6 0.4 fusion.21
  55.0 0.3 fusion.59
  55.3 0.7 collective-permute-start.5
  56.0 3.0 %collective-permute-start.3 = (f32[2,36,132]{2,1,0:T(8,128)S(1)}, f32[2,36,132]{2,1,0:T(8,128)S(1)}, u32[]{:S(2)}, u32[]{:S(2)}) collective-permute-start(f32[2,36,132]{2,1,0:T(8,128)S(1)} %copy-done.14), channel_id=1, source_target_pairs={{8,0},{16,8},{24,16},{9,1},{17,9},{25,17},{10,2},{18,10},{26,18},{... | collective-permute-start | bytes 114056 | tf_op jit(solution)/shard_map/ppermute | solution.py:24
  59.0 3.1 %collective-permute-start.4 = (f32[2,36,132]{2,1,0:T(8,128)S(1)}, f32[2,36,132]{2,1,0:T(8,128)S(1)}, u32[]{:S(2)}, u32[]{:S(2)}) collective-permute-start(f32[2,36,132]{2,1,0:T(8,128)S(1)} %get-tuple-element.84), channel_id=1, source_target_pairs={{0,8},{8,16},{16,24},{1,9},{9,17},{17,25},{2,10},{10,18},{18,26},{... | collective-permute-start | bytes 114056 | tf_op jit(solution)/shard_map/ppermute | solution.py:21
  62.7 1.4 %slice.1130 = f32[16,36,132]{2,1,0:T(8,128)S(1)} slice(f32[35,96,192]{2,1,0:T(8,128)} %copy-done.1), slice={[0:16], [30:66], [30:162]} | slice | bytes 608256 | tf_op jit(solution)/shard_map/slice | solution.py:203
  64.1 1.9 %collective-permute-done.4 = f32[2,36,132]{2,1,0:T(8,128)S(1)} collective-permute-done((f32[2,36,132]{2,1,0:T(8,128)S(1)}, f32[2,36,132]{2,1,0:T(8,128)S(1)}, u32[]{:S(2)}, u32[]{:S(2)}) %collective-permute-start.4) | collective-permute-done | bytes 38048 | tf_op jit(solution)/shard_map/ppermute | solution.py:21
  66.0 1.1 %multiply_multiply_fusion.1 = (f32[18,34,130]{2,1,0:T(8,128)S(1)}, f32[18,34,130]{2,1,0:T(8,128)S(1)}) fusion(f32[16,36,132]{2,1,0:T(8,128)S(1)} %slice.1130, f32[2,36,132]{2,1,0:T(8,128)S(1)} %collective-permute-done.4, f32[2,36,132]{2,1,0:T(8,128)S(1)} %collective-permute-done.3, f32[130]{0:T(256)S(1)} %and_convert_fusion.2, ...), kind=kLoop, calls=%fused_computation.10 | loop fusion | flops 1750320 | bytes 2292568 | tf_op jit(solution)/shard_map/mul | solution.py:63
  67.2 0.9 fusion.40
  68.1 0.6 copy-done.5
  68.9 0.3 fusion.6
  69.2 1.7 %fusion.2 = f32[3,8,2,32,128]{4,3,2,1,0:T(8,128)S(1)} fusion(f32[3,8,2,32,128]{4,3,2,1,0:T(8,128)S(1)} %bitcast.367, f32[3,8,2,32,128]{4,3,2,1,0:T(8,128)S(1)} %bitcast.366), kind=kOutput, calls=%fused_computation.6 | output fusion | flops 786432 | bytes 2359296 | tf_op jit(solution)/shard_map/jit(cumsum)/reduce_window_sum | solution.py:214
  71.1 0.4 fusion.52
  71.5 0.4 fusion.48
  71.9 0.4 fusion.44
  72.3 0.4 fusion.72
  72.6 0.4 fusion.68
  73.0 0.4 fusion.64
  73.4 0.4 fusion.60
  74.0 1.3 %collective-permute-start.6 = (f32[3,64,160]{2,1,0:T(8,128)S(1)}, f32[3,64,160]{2,1,0:T(8,128)S(1)}, u32[]{:S(2)}, u32[]{:S(2)}) collective-permute-start(f32[3,64,160]{2,1,0:T(8,128)S(1)} %fusion.91), channel_id=1, source_target_pairs={{8,16},{9,17},{10,18},{11,19},{12,20},{13,21},{14,22},{15,23}} | collective-permute-start | bytes 368648 | tf_op jit(solution)/shard_map/ppermute | solution.py:230
  76.0 5.6 %collective-permute-done.6 = f32[3,64,160]{2,1,0:T(8,128)S(1)} collective-permute-done((f32[3,64,160]{2,1,0:T(8,128)S(1)}, f32[3,64,160]{2,1,0:T(8,128)S(1)}, u32[]{:S(2)}, u32[]{:S(2)}) %collective-permute-start.6) | collective-permute-done | bytes 122912 | tf_op jit(solution)/shard_map/ppermute | solution.py:230
  81.7 0.3 fusion.84
  82.0 0.3 fusion.80
  84.1 1.3 %collective-permute-start.7 = (f32[3,48,144]{2,1,0:T(8,128)S(1)}, f32[3,48,144]{2,1,0:T(8,128)S(1)}, u32[]{:S(2)}, u32[]{:S(2)}) collective-permute-start(f32[3,48,144]{2,1,0:T(8,128)S(1)} %fusion.123), channel_id=1, source_target_pairs={{16,24},{17,25},{18,26},{19,27},{20,28},{21,29},{22,30},{23,31}} | collective-permute-start | bytes 248840 | tf_op jit(solution)/shard_map/ppermute | solution.py:230
  86.0 2.0 %collective-permute-done.7 = f32[3,48,144]{2,1,0:T(8,128)S(1)} collective-permute-done((f32[3,48,144]{2,1,0:T(8,128)S(1)}, f32[3,48,144]{2,1,0:T(8,128)S(1)}, u32[]{:S(2)}, u32[]{:S(2)}) %collective-permute-start.7) | collective-permute-done | bytes 82976 | tf_op jit(solution)/shard_map/ppermute | solution.py:230
  90.5 0.4 multiply_reduce_fusion
  91.1 4.5 %collective-permute-start.8 = (f32[4,2,128]{2,1,0:T(2,128)S(1)}, f32[4,2,128]{2,1,0:T(2,128)S(1)}, u32[]{:S(2)}, u32[]{:S(2)}) collective-permute-start(f32[4,2,128]{2,1,0:T(2,128)S(1)} %bitcast.374), channel_id=1, source_target_pairs={{0,2},{2,0},{4,6},{6,4},{1,3},{3,1},{5,7},{7,5},{8,10},{10,8},{12,... | collective-permute-start | bytes 12296 | tf_op jit(solution)/shard_map/ppermute | solution.py:42
  95.6 0.8 collective-permute-done.8
  96.5 3.3 %collective-permute-start.9 = (f32[4,1,128]{2,0,1:T(4,128)S(1)}, f32[4,1,128]{2,0,1:T(4,128)S(1)}, u32[]{:S(2)}, u32[]{:S(2)}) collective-permute-start(f32[4,1,128]{2,0,1:T(4,128)S(1)} %bitcast.375), channel_id=1, source_target_pairs={{0,4},{4,0},{2,6},{6,2},{1,5},{5,1},{3,7},{7,3},{8,12},{12,8},{10,... | collective-permute-start | bytes 6152 | tf_op jit(solution)/shard_map/ppermute | solution.py:42
  99.8 1.6 %collective-permute-done.9 = f32[4,1,128]{2,0,1:T(4,128)S(1)} collective-permute-done((f32[4,1,128]{2,0,1:T(4,128)S(1)}, f32[4,1,128]{2,0,1:T(4,128)S(1)}, u32[]{:S(2)}, u32[]{:S(2)}) %collective-permute-start.9) | collective-permute-done | bytes 2080 | tf_op jit(solution)/shard_map/ppermute | solution.py:42
  101.6 0.6 pad_maximum_fusion.6
  (115 shorter events, 7.6 us)
Async XLA Ops:
  0.0 4.5 %copy-start.11 = (s32[16,32,128]{2,1,0:T(8,128)S(1)}, s32[16,32,128]{2,1,0:T(8,128)}, u32[]{:S(2)}) copy-start(s32[16,32,128]{2,1,0:T(8,128)} %param.7) | copy-start | bytes 786436
  0.0 7.5 %copy-start.15 = (f32[3,16]{1,0:T(4,128)S(1)}, f32[3,16]{1,0:T(4,128)}, u32[]{:S(2)}) copy-start(f32[3,16]{1,0:T(4,128)} %table_ref.1) | copy-start | bytes 580
  0.0 7.5 %copy-start.17 = (f32[16]{0:T(128)S(1)}, f32[16]{0:T(128)}, u32[]{:S(2)}) copy-start(f32[16]{0:T(128)} %param.9) | copy-start | bytes 196
  0.0 7.5 %copy-start.16 = (f32[3,16]{1,0:T(4,128)S(1)}, f32[3,16]{1,0:T(4,128)}, u32[]{:S(2)}) copy-start(f32[3,16]{1,0:T(4,128)} %param.11) | copy-start | bytes 580
  1.0 17.0 %copy-start.8 = (f32[16,32,128]{2,1,0:T(8,128)}, f32[16,32,128]{2,1,0:T(8,128)S(1)}, u32[]{:S(2)}) copy-start(f32[16,32,128]{2,1,0:T(8,128)S(1)} %convert_element_type.39) | copy-start | bytes 786436
  3.0 14.9 %collective-permute-start = (f32[35,32,128]{2,1,0:T(8,128)}, f32[35,32,128]{2,1,0:T(8,128)S(1)}, u32[]{:S(2)}, u32[]{:S(2)}) collective-permute-start(f32[35,32,128]{2,1,0:T(8,128)} %pad_maximum_fusion.5), channel_id=1, source_target_pairs={{0,1},{1,0},{2,3},{3,2},{4,5},{5,4},{6,7},{7,6},{8,9},{9,8},{10,11... | collective-permute-start | bytes 1720328 | tf_op jit(solution)/shard_map/ppermute | solution.py:87
  4.5 7.1 %copy-start.2 = (f32[16,32,128]{2,1,0:T(8,128)S(1)}, f32[16,32,128]{2,1,0:T(8,128)}, u32[]{:S(2)}) copy-start(f32[16,32,128]{2,1,0:T(8,128)} %param.6) | copy-start | bytes 786436
  8.0 4.7 %copy-start.12 = (f32[3,32,128]{2,1,0:T(8,128)S(1)}, f32[3,32,128]{2,1,0:T(8,128)}, u32[]{:S(2)}) copy-start(f32[3,32,128]{2,1,0:T(8,128)} %param.8) | copy-start | bytes 147460
  11.6 16.5 %copy-start.4 = (f32[7,16,32,128]{3,2,1,0:T(8,128)}, f32[7,16,32,128]{3,2,1,0:T(8,128)S(1)}, u32[]{:S(2)}) copy-start(f32[7,16,32,128]{3,2,1,0:T(8,128)S(1)} %select_select_fusion) | copy-start | bytes 5505028
  18.1 2.5 %copy-start.6 = (f32[35,32,128]{2,1,0:T(8,128)}, f32[35,32,128]{2,1,0:T(8,128)S(1)}, u32[]{:S(2)}) copy-start(f32[35,32,128]{2,1,0:T(8,128)S(1)} %get-tuple-element.94) | copy-start | bytes 1720324
  18.1 2.5 %copy-start.7 = (f32[35,32,128]{2,1,0:T(8,128)}, f32[35,32,128]{2,1,0:T(8,128)S(1)}, u32[]{:S(2)}) copy-start(f32[35,32,128]{2,1,0:T(8,128)S(1)} %get-tuple-element.95) | copy-start | bytes 1720324
  20.6 7.5 %copy-start.18 = (f32[18]{0:T(128)S(1)}, f32[18]{0:T(128)}, u32[]{:S(2)}) copy-start(f32[18]{0:T(128)} %and_convert_fusion.4) | copy-start | bytes 220
  22.5 6.7 %collective-permute-start.1 = (f32[35,96,32]{1,2,0:T(8,128)S(1)}, f32[35,96,32]{1,2,0:T(8,128)S(1)}, u32[]{:S(2)}, u32[]{:S(2)}) collective-permute-start(f32[35,96,32]{1,2,0:T(8,128)S(1)} %copy.123), channel_id=1, source_target_pairs={{0,2},{2,4},{4,6},{1,3},{3,5},{5,7},{8,10},{10,12},{12,14},{9,11},... | collective-permute-start | bytes 1290248 | tf_op jit(solution)/shard_map/ppermute | solution.py:98
  26.6 5.9 %collective-permute-start.2 = (f32[35,96,32]{1,2,0:T(8,128)}, f32[35,96,32]{1,2,0:T(8,128)}, u32[]{:S(2)}, u32[]{:S(2)}) collective-permute-start(f32[35,96,32]{1,2,0:T(8,128)} %copy.124), channel_id=1, source_target_pairs={{2,0},{4,2},{6,4},{3,1},{5,3},{7,5},{10,8},{12,10},{14,12},{11,9},... | collective-permute-start | bytes 1290248 | tf_op jit(solution)/shard_map/ppermute | solution.py:99
  39.2 1.7 %copy-start.1 = (f32[35,96,192]{2,1,0:T(8,128)}, f32[35,96,192]{2,1,0:T(8,128)S(1)}, u32[]{:S(2)}) copy-start(f32[35,96,192]{2,1,0:T(8,128)S(1)} %pad_maximum_fusion.stack_ref) | copy-start | bytes 7741444
  49.7 2.7 %copy-start = (f32[3,8,96,192]{3,2,1,0:T(8,128)S(1)}, f32[3,8,96,192]{3,2,1,0:T(8,128)}, u32[]{:S(2)}) copy-start(f32[3,8,96,192]{3,2,1,0:T(8,128)} %shard_map.64) | copy-start | bytes 5308420
  54.6 1.5 %copy-start.14 = (f32[2,36,132]{2,1,0:T(8,128)S(1)}, f32[2,36,132]{2,1,0:T(8,128)}, u32[]{:S(2)}) copy-start(f32[2,36,132]{2,1,0:T(8,128)} %get-tuple-element.83) | copy-start | bytes 114052
  54.6 7.5 %copy-start.13 = (f32[3,8,32,128]{3,2,0,1:T(8,128)S(1)}, f32[3,8,32,128]{3,2,0,1:T(8,128)}, u32[]{:S(2)}) copy-start(f32[3,8,32,128]{3,2,0,1:T(8,128)} %constant_dynamic-update-slice_fusion.31) | copy-start | bytes 1179652
  55.3 15.7 %collective-permute-start.5 = (f32[3,80,176]{2,1,0:T(8,128)S(1)}, f32[3,80,176]{2,1,0:T(8,128)S(1)}, u32[]{:S(2)}, u32[]{:S(2)}) collective-permute-start(f32[3,80,176]{2,1,0:T(8,128)S(1)} %fusion.59), channel_id=1, source_target_pairs={{0,8},{1,9},{2,10},{3,11},{4,12},{5,13},{6,14},{7,15}} | collective-permute-start | bytes 506888 | tf_op jit(solution)/shard_map/ppermute | solution.py:230
  56.0 8.1 %collective-permute-start.3 = (f32[2,36,132]{2,1,0:T(8,128)S(1)}, f32[2,36,132]{2,1,0:T(8,128)S(1)}, u32[]{:S(2)}, u32[]{:S(2)}) collective-permute-start(f32[2,36,132]{2,1,0:T(8,128)S(1)} %copy-done.14), channel_id=1, source_target_pairs={{8,0},{16,8},{24,16},{9,1},{17,9},{25,17},{10,2},{18,10},{26,18},{... | collective-permute-start | bytes 114056 | tf_op jit(solution)/shard_map/ppermute | solution.py:24
  59.0 7.0 %collective-permute-start.4 = (f32[2,36,132]{2,1,0:T(8,128)S(1)}, f32[2,36,132]{2,1,0:T(8,128)S(1)}, u32[]{:S(2)}, u32[]{:S(2)}) collective-permute-start(f32[2,36,132]{2,1,0:T(8,128)S(1)} %get-tuple-element.84), channel_id=1, source_target_pairs={{0,8},{8,16},{16,24},{1,9},{9,17},{17,25},{2,10},{10,18},{18,26},{... | collective-permute-start | bytes 114056 | tf_op jit(solution)/shard_map/ppermute | solution.py:21
  67.2 1.0 copy-start.3
  67.2 1.6 %copy-start.5 = (f32[7,16,32,128]{3,2,1,0:T(8,128)S(1)}, f32[7,16,32,128]{3,2,1,0:T(8,128)}, u32[]{:S(2)}) copy-start(f32[7,16,32,128]{3,2,1,0:T(8,128)} %copy-done.4) | copy-start | bytes 5505028
  67.2 1.6 %copy-start.9 = (f32[16,32,128]{2,1,0:T(8,128)S(1)}, f32[16,32,128]{2,1,0:T(8,128)}, u32[]{:S(2)}) copy-start(f32[16,32,128]{2,1,0:T(8,128)} %get-tuple-element.88) | copy-start | bytes 786436
  67.2 1.6 %copy-start.10 = (f32[16,32,128]{2,1,0:T(8,128)S(1)}, f32[16,32,128]{2,1,0:T(8,128)}, u32[]{:S(2)}) copy-start(f32[16,32,128]{2,1,0:T(8,128)} %fusion.3) | copy-start | bytes 786436
  74.0 7.6 %collective-permute-start.6 = (f32[3,64,160]{2,1,0:T(8,128)S(1)}, f32[3,64,160]{2,1,0:T(8,128)S(1)}, u32[]{:S(2)}, u32[]{:S(2)}) collective-permute-start(f32[3,64,160]{2,1,0:T(8,128)S(1)} %fusion.91), channel_id=1, source_target_pairs={{8,16},{9,17},{10,18},{11,19},{12,20},{13,21},{14,22},{15,23}} | collective-permute-start | bytes 368648 | tf_op jit(solution)/shard_map/ppermute | solution.py:230
  84.1 4.0 %collective-permute-start.7 = (f32[3,48,144]{2,1,0:T(8,128)S(1)}, f32[3,48,144]{2,1,0:T(8,128)S(1)}, u32[]{:S(2)}, u32[]{:S(2)}) collective-permute-start(f32[3,48,144]{2,1,0:T(8,128)S(1)} %fusion.123), channel_id=1, source_target_pairs={{16,24},{17,25},{18,26},{19,27},{20,28},{21,29},{22,30},{23,31}} | collective-permute-start | bytes 248840 | tf_op jit(solution)/shard_map/ppermute | solution.py:230
  91.1 5.4 %collective-permute-start.8 = (f32[4,2,128]{2,1,0:T(2,128)S(1)}, f32[4,2,128]{2,1,0:T(2,128)S(1)}, u32[]{:S(2)}, u32[]{:S(2)}) collective-permute-start(f32[4,2,128]{2,1,0:T(2,128)S(1)} %bitcast.374), channel_id=1, source_target_pairs={{0,2},{2,0},{4,6},{6,4},{1,3},{3,1},{5,7},{7,5},{8,10},{10,8},{12,... | collective-permute-start | bytes 12296 | tf_op jit(solution)/shard_map/ppermute | solution.py:42
  96.5 4.9 %collective-permute-start.9 = (f32[4,1,128]{2,0,1:T(4,128)S(1)}, f32[4,1,128]{2,0,1:T(4,128)S(1)}, u32[]{:S(2)}, u32[]{:S(2)}) collective-permute-start(f32[4,1,128]{2,0,1:T(4,128)S(1)} %bitcast.375), channel_id=1, source_target_pairs={{0,4},{4,0},{2,6},{6,2},{1,5},{5,1},{3,7},{7,3},{8,12},{12,8},{10,... | collective-permute-start | bytes 6152 | tf_op jit(solution)/shard_map/ppermute | solution.py:42

commit v23 on v20

--- a/solution.py
+++ b/solution.py
@@ -84,7 +84,14 @@
                 lax.slice_in_dim(block, size - need, None, axis=dim),
                 lax.slice_in_dim(block, 0, need, axis=dim),
             )
-        got = lax.ppermute(send, axis, [(0, 1), (1, 0)])
+        half = send.shape[0] // 2
+        got = jnp.concatenate(
+            [
+                lax.ppermute(send[:half], axis, [(0, 1), (1, 0)]),
+                lax.ppermute(send[half:], axis, [(0, 1), (1, 0)]),
+            ],
+            axis=0,
+        )
         lows = [jnp.where(first, jnp.zeros_like(got), got)]
         highs = [jnp.where(first, got, jnp.zeros_like(got))]
         count = 0

time: 96.8 us -> 96.8 us (level)
    unnamed x67 -> x68, local copies, waits for them, and re-layouts: 5.52 us -> 4.77 us
    ppermute x1 -> x2, waiting for transfers between devices: 4.47 us -> 3.86 us  [the longest x1 3.85 us: halo(): lax.ppermute(send[half:], axis, [(0, 1), (1, 0)])]
    ppermute x1 -> x2, starting transfers between devices: 1.58 us -> 2.16 us  [the longest x1 1.58 us: halo(): lax.ppermute(send[:half], axis, [(0, 1), (1, 0)])]
  transfers between devices with their start and end apart: 10 -> 11, of which waited for: 6 -> 6; matrix products, arithmetic and copies ran while one was open for 27% -> 27% of each run, Pallas kernels for 9% -> 9%
where the time goes in v23:
time: 96.8 us; the launch traced here: 94.9 us
  other arithmetic  31.7 us (33%)
  starting transfers between devices  22.3 us (23%)
  local copies, waits for them, and re-layouts  15.2 us (16%)
  waiting for transfers between devices  15.2 us (16%)
  Pallas kernels  8.83 us (9%)
  matrix products  0.98 us (1%)
    mul x31, other arithmetic, propagate(): current = current * fade_here  11.7 us
    pallas_call x1, Pallas kernels, fade_rim_of(): pl.pallas_call(kernel, out_shape=jax.ShapeDtypeStruct((colours, SLABS, ri...  8.83 us
    ppermute x2, starting transfers between devices, from_partner(): return lax.ppermute(block, axis, route)  7.96 us
    ppermute x3, waiting for transfers between devices, shards(): incoming = lax.ppermute(outgoing, 'light', [(section_num, section_num + 1)])  7.37 us
    unnamed x68, local copies, waits for them, and re-layouts  4.77 us
    concatenate x2, other arithmetic, halo(): block = jnp.concatenate(lows + [block] + highs, axis=dim)  3.99 us
    ppermute x1, waiting for transfers between devices, halo(): lax.ppermute(send[half:], axis, [(0, 1), (1, 0)])  3.85 us
    ppermute x1, starting transfers between devices, padded_2(): lax.ppermute(lax.slice_in_dim(block, block.shape[dim] - width, None, axis...  3.67 us
  transfers between devices with their start and end apart: 11, of which 6 were waited for; matrix products, arithmetic and copies ran while one was open for 27% of the time, Pallas kernels for 9%

profile of v23, /device:TPU:16, one launch (start us, length us, event | category | flops | bytes accessed | tf_op | source)
XLA Modules:
  0.0 94.9 jit_solution(6507368549572977082)
XLA Ops:
  0.0 1.0 %convert_element_type.39 = f32[16,32,128]{2,1,0:T(8,128)S(1)} convert(s32[16,32,128]{2,1,0:T(8,128)} %param.7) | non-fusion elementwise | flops 65536 | bytes 524288 | tf_op jit(solution)/shard_map/convert_element_type | solution.py:206
  1.1 1.1 %pad_maximum_fusion.6 = f32[17,32,128]{2,1,0:T(8,128)S(1)} fusion(f32[16,32,128]{2,1,0:T(8,128)S(1)} %convert_element_type.39, f32[16,32,128]{2,1,0:T(8,128)} %param.6), kind=kLoop, calls=%fused_computation.48 | loop fusion | flops 69632 | bytes 802816 | tf_op jit(solution)/shard_map/concatenate | solution.py:206
  2.1 1.6 %collective-permute-start = (f32[17,32,128]{2,1,0:T(8,128)S(1)}, f32[17,32,128]{2,1,0:T(8,128)S(1)}, u32[]{:S(2)}, u32[]{:S(2)}) collective-permute-start(f32[17,32,128]{2,1,0:T(8,128)S(1)} %pad_maximum_fusion.6), channel_id=1, source_target_pairs={{0,1},{1,0},{2,3},{3,2},{4,5},{5,4},{6,7},{7,6},{8,9},{9,8},{10,11... | collective-permute-start | bytes 835592 | tf_op jit(solution)/shard_map/ppermute | solution.py:90
  3.7 0.8 pad_maximum_fusion.5
  4.5 0.6 collective-permute-start.1
  5.1 0.6 constant_dynamic-update-slice_fusion.33
  5.7 0.6 broadcast_compare_fusion.14
  6.4 0.4 slice_reduce_fusion.15
  6.9 2.6 %select_select_fusion = f32[7,16,32,128]{3,2,1,0:T(8,128)S(1)} fusion(f32[7]{0:T(128)S(1)} %get-tuple-element.6, f32[7]{0:T(128)S(1)} %get-tuple-element.7, f32[7]{0:T(128)S(1)} %get-tuple-element.8, f32[7]{0:T(128)S(1)} %get-tuple-element.9, f32[7]{0:T(128)S(1)} %get-tuple-element.10, f32[7]{0:T(128)S(1)} %get-tuple-element.11, f32[7]{0:T(128)S(1)} %get-tuple-element.12, ...), kind=kLoop, calls=%fused_computation.1 | loop fusion | flops 6881280 | bytes 2818496 | tf_op jit(solution)/shard_map/jit(_where)/select_n | solution.py:216
  9.5 1.1 %slice_multiply_fusion = f32[3,16,32,128]{3,2,1,0:T(8,128)} fusion(f32[7,16,32,128]{3,2,1,0:T(8,128)S(1)} %select_select_fusion, f32[16,32,128]{2,1,0:T(8,128)S(1)} %copy-done.2), kind=kLoop, calls=%fused_computation.8 | loop fusion | flops 196608 | bytes 1835008 | tf_op jit(solution)/shard_map/mul | solution.py:219
  10.5 0.8 fusion.143
  11.3 1.0 %fusion = f32[16,32,128]{2,1,0:T(8,128)} fusion(f32[16,32,128]{2,1,0:T(8,128)S(1)} %copy-done.2, f32[7,16,32,128]{3,2,1,0:T(8,128)S(1)} %select_select_fusion), kind=kOutput, calls=%fused_computation.4 | convolution fusion | flops 100876288 | bytes 786432 | tf_op jit(solution)/shard_map/dot_general | solution.py:251
  12.3 0.7 broadcast_multiply_fusion.mask_ref
  13.1 3.9 %collective-permute-done.1 = f32[18,32,128]{2,1,0:T(8,128)S(1)} collective-permute-done((f32[18,32,128]{2,1,0:T(8,128)S(1)}, f32[18,32,128]{2,1,0:T(8,128)S(1)}, u32[]{:S(2)}, u32[]{:S(2)}) %collective-permute-start.1) | collective-permute-done | bytes 294944 | tf_op jit(solution)/shard_map/ppermute | solution.py:91
  17.2 0.6 fusion.173
  18.1 1.3 %copy.123 = f32[35,96,32]{1,2,0:T(8,128)} copy(f32[35,96,32]{2,1,0:T(8,128)S(1)} %get-tuple-element.83) | data formatting | bytes 860160 | tf_op jit(solution)/shard_map/slice | solution.py:104
  19.4 1.4 %collective-permute-start.2 = (f32[35,96,32]{1,2,0:T(8,128)}, f32[35,96,32]{1,2,0:T(8,128)S(1)}, u32[]{:S(2)}, u32[]{:S(2)}) collective-permute-start(f32[35,96,32]{1,2,0:T(8,128)} %copy.123), channel_id=1, source_target_pairs={{0,2},{2,4},{4,6},{1,3},{3,5},{5,7},{8,10},{10,12},{12,14},{9,11},... | collective-permute-start | bytes 1290248 | tf_op jit(solution)/shard_map/ppermute | solution.py:105
  20.9 1.3 %copy.124 = f32[35,96,32]{1,2,0:T(8,128)} copy(f32[35,96,32]{2,1,0:T(8,128)S(1)} %get-tuple-element.84) | data formatting | bytes 860160 | tf_op jit(solution)/shard_map/slice | solution.py:106
  22.2 1.3 %collective-permute-start.3 = (f32[35,96,32]{1,2,0:T(8,128)}, f32[35,96,32]{1,2,0:T(8,128)S(1)}, u32[]{:S(2)}, u32[]{:S(2)}) collective-permute-start(f32[35,96,32]{1,2,0:T(8,128)} %copy.124), channel_id=1, source_target_pairs={{2,0},{4,2},{6,4},{3,1},{5,3},{7,5},{10,8},{12,10},{14,12},{11,9},... | collective-permute-start | bytes 1290248 | tf_op jit(solution)/shard_map/ppermute | solution.py:106
  23.7 0.9 fusion.177
  24.6 1.8 %copy.125 = f32[35,96,32]{2,1,0:T(8,128)} copy(f32[35,96,32]{1,2,0:T(8,128)S(1)} %collective-permute-done.2) | data formatting | bytes 860160 | tf_op jit(solution)/shard_map/ppermute | solution.py:105
  26.4 1.6 %collective-permute-done.3 = f32[35,96,32]{1,2,0:T(8,128)S(1)} collective-permute-done((f32[35,96,32]{1,2,0:T(8,128)}, f32[35,96,32]{1,2,0:T(8,128)S(1)}, u32[]{:S(2)}, u32[]{:S(2)}) %collective-permute-start.3) | collective-permute-done | bytes 430112 | tf_op jit(solution)/shard_map/ppermute | solution.py:106
  28.0 1.8 %copy.126 = f32[35,96,32]{2,1,0:T(8,128)} copy(f32[35,96,32]{1,2,0:T(8,128)S(1)} %collective-permute-done.3) | data formatting | bytes 860160 | tf_op jit(solution)/shard_map/ppermute | solution.py:106
  29.7 3.9 %pad_maximum_fusion.stack_ref = f32[35,96,192]{2,1,0:T(8,128)S(1)} fusion(f32[35,96,32]{2,1,0:T(8,128)} %copy.126, f32[35,32,128]{2,1,0:T(8,128)} %copy-done.8, f32[3,32,128]{2,1,0:T(8,128)S(1)} %copy-done.14, f32[16,32,128]{2,1,0:T(8,128)} %copy-done.6, f32[16,32,128]{2,1,0:T(8,128)} %param.6, f32[35,32,128]{2,1,0:T(8,128)} %copy-done.7, f32[35,96,32]{2,1,0:T(8,128)} %copy.125), kind=kLoop, calls=%fused_computation | loop fusion | flops 3870720 | bytes 5160960 | tf_op jit(solution)/shard_map/concatenate | solution.py:107
  33.6 0.9 fusion.172
  34.5 2.3 %collective-permute-start.4 = (f32[2,36,132]{2,1,0:T(8,128)}, f32[2,36,132]{2,1,0:T(8,128)S(1)}, u32[]{:S(2)}, u32[]{:S(2)}) collective-permute-start(f32[2,36,132]{2,1,0:T(8,128)} %get-tuple-element.79), channel_id=1, source_target_pairs={{8,0},{16,8},{24,16},{9,1},{17,9},{25,17},{10,2},{18,10},{26,18},{... | collective-permute-start | bytes 114056 | tf_op jit(solution)/shard_map/ppermute | solution.py:24
  36.9 3.7 %collective-permute-start.5 = (f32[2,36,132]{2,1,0:T(8,128)}, f32[2,36,132]{2,1,0:T(8,128)}, u32[]{:S(2)}, u32[]{:S(2)}) collective-permute-start(f32[2,36,132]{2,1,0:T(8,128)} %get-tuple-element.80), channel_id=1, source_target_pairs={{0,8},{8,16},{16,24},{1,9},{9,17},{17,25},{2,10},{10,18},{18,26},{... | collective-permute-start | bytes 114056 | tf_op jit(solution)/shard_map/ppermute | solution.py:21
  40.6 8.8 %shard_map.64 = f32[3,8,96,192]{3,2,1,0:T(8,128)} custom-call(f32[3,16]{1,0:T(4,128)} %table_ref.1, f32[35,96,192]{2,1,0:T(8,128)} %copy-done.1, f32[96,192]{1,0:T(8,128)} %broadcast_multiply_fusion.mask_ref), custom_call_target="tpu_custom_call" | custom-call | tf_op jit(solution)/shard_map/pallas_call | solution.py:180
  49.4 1.2 %fusion.17 = f32[3,96,192]{2,1,0:T(8,128)S(1)} fusion(f32[3,8,96,192]{3,2,1,0:T(8,128)} %shard_map.64, f32[35,96,192]{2,1,0:T(8,128)} %copy-done.1), kind=kLoop, calls=%fused_computation.44 | loop fusion | flops 55296 | bytes 663552 | tf_op jit(solution)/shard_map/mul | solution.py:136
  50.6 1.4 %fusion.13 = (f32[3,94,190]{2,1,0:T(8,128)S(1)}, f32[3,94,190]{2,1,0:T(8,128)S(1)}) fusion(f32[3,8,96,192]{3,2,1,0:T(8,128)} %shard_map.64, f32[3,96,192]{2,1,0:T(8,128)S(1)} %fusion.17), kind=kLoop, calls=%fused_computation.36 | loop fusion | flops 428640 | bytes 1714560 | tf_op jit(solution)/shard_map/mul | solution.py:136
  52.1 0.4 fusion.9
  52.5 0.4 fusion.5
  53.0 0.4 fusion.30
  53.4 0.4 fusion.26
  53.8 0.4 fusion.22
  54.2 0.4 fusion.18
  54.7 0.3 fusion.56
  55.0 0.7 collective-permute-start.6
  56.3 1.4 %slice.1140 = f32[16,36,132]{2,1,0:T(8,128)S(1)} slice(f32[35,96,192]{2,1,0:T(8,128)} %copy-done.1), slice={[0:16], [30:66], [30:162]} | slice | bytes 608256 | tf_op jit(solution)/shard_map/slice | solution.py:210
  57.7 0.9 pad_maximum_fusion.2
  58.6 2.0 %multiply_multiply_fusion.1 = (f32[18,34,130]{2,1,0:T(8,128)S(1)}, f32[18,34,130]{2,1,0:T(8,128)S(1)}) fusion(f32[16,36,132]{2,1,0:T(8,128)S(1)} %slice.1140, f32[2,36,132]{2,1,0:T(8,128)} %collective-permute-done.5, f32[2,36,132]{2,1,0:T(8,128)S(1)} %collective-permute-done.4, f32[130]{0:T(256)S(1)} %and_convert_fusion.2, ...), kind=kLoop, calls=%fused_computation.6 | loop fusion | flops 1750320 | bytes 2292568 | tf_op jit(solution)/shard_map/mul | solution.py:63
  60.7 0.9 fusion.37
  61.7 0.4 fusion.49
  62.1 0.4 fusion.45
  62.5 0.4 fusion.41
  62.9 0.4 fusion.69
  63.2 0.4 fusion.65
  63.6 0.4 fusion.61
  63.9 0.4 fusion.57
  64.6 1.3 %collective-permute-start.7 = (f32[3,64,160]{2,1,0:T(8,128)S(1)}, f32[3,64,160]{2,1,0:T(8,128)S(1)}, u32[]{:S(2)}, u32[]{:S(2)}) collective-permute-start(f32[3,64,160]{2,1,0:T(8,128)S(1)} %fusion.88), channel_id=1, source_target_pairs={{8,16},{9,17},{10,18},{11,19},{12,20},{13,21},{14,22},{15,23}} | collective-permute-start | bytes 368648 | tf_op jit(solution)/shard_map/ppermute | solution.py:237
  66.5 5.6 %collective-permute-done.7 = f32[3,64,160]{2,1,0:T(8,128)S(1)} collective-permute-done((f32[3,64,160]{2,1,0:T(8,128)S(1)}, f32[3,64,160]{2,1,0:T(8,128)S(1)}, u32[]{:S(2)}, u32[]{:S(2)}) %collective-permute-start.7) | collective-permute-done | bytes 122912 | tf_op jit(solution)/shard_map/ppermute | solution.py:237
  72.3 0.3 fusion.81
  72.6 0.3 fusion.77
  72.9 0.3 fusion.73
  74.6 1.5 %collective-permute-start.8 = (f32[3,48,144]{2,1,0:T(8,128)S(1)}, f32[3,48,144]{2,1,0:T(8,128)S(1)}, u32[]{:S(2)}, u32[]{:S(2)}) collective-permute-start(f32[3,48,144]{2,1,0:T(8,128)S(1)} %fusion.120), channel_id=1, source_target_pairs={{16,24},{17,25},{18,26},{19,27},{20,28},{21,29},{22,30},{23,31}} | collective-permute-start | bytes 248840 | tf_op jit(solution)/shard_map/ppermute | solution.py:237
  76.8 1.8 %collective-permute-done.8 = f32[3,48,144]{2,1,0:T(8,128)S(1)} collective-permute-done((f32[3,48,144]{2,1,0:T(8,128)S(1)}, f32[3,48,144]{2,1,0:T(8,128)S(1)}, u32[]{:S(2)}, u32[]{:S(2)}) %collective-permute-start.8) | collective-permute-done | bytes 82976 | tf_op jit(solution)/shard_map/ppermute | solution.py:237
  81.5 0.6 copy-done.3
  82.1 0.6 copy-done.5
  83.0 0.5 fusion.3
  83.6 5.4 %collective-permute-start.9 = (f32[4,2,128]{2,1,0:T(2,128)S(1)}, f32[4,2,128]{2,1,0:T(2,128)S(1)}, u32[]{:S(2)}, u32[]{:S(2)}) collective-permute-start(f32[4,2,128]{2,1,0:T(2,128)S(1)} %bitcast.374), channel_id=1, source_target_pairs={{0,2},{2,0},{4,6},{6,4},{1,3},{3,1},{5,7},{7,5},{8,10},{10,8},{12,... | collective-permute-start | bytes 12296 | tf_op jit(solution)/shard_map/ppermute | solution.py:42
  89.1 0.8 collective-permute-done.9
  89.9 2.5 %collective-permute-start.10 = (f32[4,1,128]{2,0,1:T(4,128)S(1)}, f32[4,1,128]{2,0,1:T(4,128)S(1)}, u32[]{:S(2)}, u32[]{:S(2)}) collective-permute-start(f32[4,1,128]{2,0,1:T(4,128)S(1)} %bitcast.375), channel_id=1, source_target_pairs={{0,4},{4,0},{2,6},{6,2},{1,5},{5,1},{3,7},{7,3},{8,12},{12,8},{10,... | collective-permute-start | bytes 6152 | tf_op jit(solution)/shard_map/ppermute | solution.py:42
  92.5 1.6 %collective-permute-done.10 = f32[4,1,128]{2,0,1:T(4,128)S(1)} collective-permute-done((f32[4,1,128]{2,0,1:T(4,128)S(1)}, f32[4,1,128]{2,0,1:T(4,128)S(1)}, u32[]{:S(2)}, u32[]{:S(2)}) %collective-permute-start.10) | collective-permute-done | bytes 2080 | tf_op jit(solution)/shard_map/ppermute | solution.py:42
  94.3 0.6 pad_maximum_fusion.7
  (121 shorter events, 8.0 us)
Async XLA Ops:
  0.0 5.7 %copy-start.13 = (s32[16,32,128]{2,1,0:T(8,128)S(1)}, s32[16,32,128]{2,1,0:T(8,128)}, u32[]{:S(2)}) copy-start(s32[16,32,128]{2,1,0:T(8,128)} %param.7) | copy-start | bytes 786436
  0.0 5.1 %copy-start.14 = (f32[3,32,128]{2,1,0:T(8,128)S(1)}, f32[3,32,128]{2,1,0:T(8,128)}, u32[]{:S(2)}) copy-start(f32[3,32,128]{2,1,0:T(8,128)} %param.8) | copy-start | bytes 147460
  0.0 6.4 %copy-start.16 = (f32[3,16]{1,0:T(4,128)S(1)}, f32[3,16]{1,0:T(4,128)}, u32[]{:S(2)}) copy-start(f32[3,16]{1,0:T(4,128)} %table_ref.1) | copy-start | bytes 580
  0.0 6.4 %copy-start.18 = (f32[16]{0:T(128)S(1)}, f32[16]{0:T(128)}, u32[]{:S(2)}) copy-start(f32[16]{0:T(128)} %param.9) | copy-start | bytes 196
  0.0 6.4 %copy-start.17 = (f32[3,16]{1,0:T(4,128)S(1)}, f32[3,16]{1,0:T(4,128)}, u32[]{:S(2)}) copy-start(f32[3,16]{1,0:T(4,128)} %param.11) | copy-start | bytes 580
  1.0 16.1 %copy-start.6 = (f32[16,32,128]{2,1,0:T(8,128)}, f32[16,32,128]{2,1,0:T(8,128)S(1)}, u32[]{:S(2)}) copy-start(f32[16,32,128]{2,1,0:T(8,128)S(1)} %convert_element_type.39) | copy-start | bytes 786436
  2.1 10.9 %collective-permute-start = (f32[17,32,128]{2,1,0:T(8,128)S(1)}, f32[17,32,128]{2,1,0:T(8,128)S(1)}, u32[]{:S(2)}, u32[]{:S(2)}) collective-permute-start(f32[17,32,128]{2,1,0:T(8,128)S(1)} %pad_maximum_fusion.6), channel_id=1, source_target_pairs={{0,1},{1,0},{2,3},{3,2},{4,5},{5,4},{6,7},{7,6},{8,9},{9,8},{10,11... | collective-permute-start | bytes 835592 | tf_op jit(solution)/shard_map/ppermute | solution.py:90
  4.5 12.4 %collective-permute-start.1 = (f32[18,32,128]{2,1,0:T(8,128)S(1)}, f32[18,32,128]{2,1,0:T(8,128)S(1)}, u32[]{:S(2)}, u32[]{:S(2)}) collective-permute-start(f32[18,32,128]{2,1,0:T(8,128)S(1)} %pad_maximum_fusion.5), channel_id=1, source_target_pairs={{0,1},{1,0},{2,3},{3,2},{4,5},{5,4},{6,7},{7,6},{8,9},{9,8},{10,11... | collective-permute-start | bytes 884744 | tf_op jit(solution)/shard_map/ppermute | solution.py:91
  5.7 3.7 %copy-start.2 = (f32[16,32,128]{2,1,0:T(8,128)S(1)}, f32[16,32,128]{2,1,0:T(8,128)}, u32[]{:S(2)}) copy-start(f32[16,32,128]{2,1,0:T(8,128)} %param.6) | copy-start | bytes 786436
  9.5 1.8 %copy-start.4 = (f32[7,16,32,128]{3,2,1,0:T(8,128)}, f32[7,16,32,128]{3,2,1,0:T(8,128)S(1)}, u32[]{:S(2)}) copy-start(f32[7,16,32,128]{3,2,1,0:T(8,128)S(1)} %select_select_fusion) | copy-start | bytes 5505028
  17.1 0.8 copy-start.7
  17.1 1.0 %copy-start.8 = (f32[35,32,128]{2,1,0:T(8,128)}, f32[35,32,128]{2,1,0:T(8,128)S(1)}, u32[]{:S(2)}) copy-start(f32[35,32,128]{2,1,0:T(8,128)S(1)} %get-tuple-element.88) | copy-start | bytes 1720324
  19.4 4.2 %copy-start.10 = (f32[3,16,32,128]{3,2,1,0:T(8,128)S(1)}, f32[3,16,32,128]{3,2,1,0:T(8,128)}, u32[]{:S(2)}) copy-start(f32[3,16,32,128]{3,2,1,0:T(8,128)} %slice_multiply_fusion) | copy-start | bytes 2359300
  19.4 5.2 %collective-permute-start.2 = (f32[35,96,32]{1,2,0:T(8,128)}, f32[35,96,32]{1,2,0:T(8,128)S(1)}, u32[]{:S(2)}, u32[]{:S(2)}) collective-permute-start(f32[35,96,32]{1,2,0:T(8,128)} %copy.123), channel_id=1, source_target_pairs={{0,2},{2,4},{4,6},{1,3},{3,5},{5,7},{8,10},{10,12},{12,14},{9,11},... | collective-permute-start | bytes 1290248 | tf_op jit(solution)/shard_map/ppermute | solution.py:105
  22.2 5.8 %collective-permute-start.3 = (f32[35,96,32]{1,2,0:T(8,128)}, f32[35,96,32]{1,2,0:T(8,128)S(1)}, u32[]{:S(2)}, u32[]{:S(2)}) collective-permute-start(f32[35,96,32]{1,2,0:T(8,128)} %copy.124), channel_id=1, source_target_pairs={{2,0},{4,2},{6,4},{3,1},{5,3},{7,5},{10,8},{12,10},{14,12},{11,9},... | collective-permute-start | bytes 1290248 | tf_op jit(solution)/shard_map/ppermute | solution.py:106
  33.6 7.0 %copy-start.1 = (f32[35,96,192]{2,1,0:T(8,128)}, f32[35,96,192]{2,1,0:T(8,128)S(1)}, u32[]{:S(2)}) copy-start(f32[35,96,192]{2,1,0:T(8,128)S(1)} %pad_maximum_fusion.stack_ref) | copy-start | bytes 7741444
  34.5 23.1 %collective-permute-start.4 = (f32[2,36,132]{2,1,0:T(8,128)}, f32[2,36,132]{2,1,0:T(8,128)S(1)}, u32[]{:S(2)}, u32[]{:S(2)}) collective-permute-start(f32[2,36,132]{2,1,0:T(8,128)} %get-tuple-element.79), channel_id=1, source_target_pairs={{8,0},{16,8},{24,16},{9,1},{17,9},{25,17},{10,2},{18,10},{26,18},{... | collective-permute-start | bytes 114056 | tf_op jit(solution)/shard_map/ppermute | solution.py:24
  36.9 20.8 %collective-permute-start.5 = (f32[2,36,132]{2,1,0:T(8,128)}, f32[2,36,132]{2,1,0:T(8,128)}, u32[]{:S(2)}, u32[]{:S(2)}) collective-permute-start(f32[2,36,132]{2,1,0:T(8,128)} %get-tuple-element.80), channel_id=1, source_target_pairs={{0,8},{8,16},{16,24},{1,9},{9,17},{17,25},{2,10},{10,18},{18,26},{... | collective-permute-start | bytes 114056 | tf_op jit(solution)/shard_map/ppermute | solution.py:21
  49.4 2.7 %copy-start = (f32[3,8,96,192]{3,2,1,0:T(8,128)S(1)}, f32[3,8,96,192]{3,2,1,0:T(8,128)}, u32[]{:S(2)}) copy-start(f32[3,8,96,192]{3,2,1,0:T(8,128)} %shard_map.64) | copy-start | bytes 5308420
  54.2 1.4 %copy-start.15 = (f32[3,8,32,128]{3,2,0,1:T(8,128)S(1)}, f32[3,8,32,128]{3,2,0,1:T(8,128)}, u32[]{:S(2)}) copy-start(f32[3,8,32,128]{3,2,0,1:T(8,128)} %constant_dynamic-update-slice_fusion.33) | copy-start | bytes 1179652
  55.0 6.6 %collective-permute-start.6 = (f32[3,80,176]{2,1,0:T(8,128)S(1)}, f32[3,80,176]{2,1,0:T(8,128)S(1)}, u32[]{:S(2)}, u32[]{:S(2)}) collective-permute-start(f32[3,80,176]{2,1,0:T(8,128)S(1)} %fusion.56), channel_id=1, source_target_pairs={{0,8},{1,9},{2,10},{3,11},{4,12},{5,13},{6,14},{7,15}} | collective-permute-start | bytes 506888 | tf_op jit(solution)/shard_map/ppermute | solution.py:237
  64.6 7.6 %collective-permute-start.7 = (f32[3,64,160]{2,1,0:T(8,128)S(1)}, f32[3,64,160]{2,1,0:T(8,128)S(1)}, u32[]{:S(2)}, u32[]{:S(2)}) collective-permute-start(f32[3,64,160]{2,1,0:T(8,128)S(1)} %fusion.88), channel_id=1, source_target_pairs={{8,16},{9,17},{10,18},{11,19},{12,20},{13,21},{14,22},{15,23}} | collective-permute-start | bytes 368648 | tf_op jit(solution)/shard_map/ppermute | solution.py:237
  74.6 4.0 %collective-permute-start.8 = (f32[3,48,144]{2,1,0:T(8,128)S(1)}, f32[3,48,144]{2,1,0:T(8,128)S(1)}, u32[]{:S(2)}, u32[]{:S(2)}) collective-permute-start(f32[3,48,144]{2,1,0:T(8,128)S(1)} %fusion.120), channel_id=1, source_target_pairs={{16,24},{17,25},{18,26},{19,27},{20,28},{21,29},{22,30},{23,31}} | collective-permute-start | bytes 248840 | tf_op jit(solution)/shard_map/ppermute | solution.py:237
  81.1 1.0 %copy-start.3 = (f32[16,32,128]{2,1,0:T(8,128)S(1)}, f32[16,32,128]{2,1,0:T(8,128)}, u32[]{:S(2)}) copy-start(f32[16,32,128]{2,1,0:T(8,128)} %param.6) | copy-start | bytes 786436
  81.1 1.6 %copy-start.5 = (f32[7,16,32,128]{3,2,1,0:T(8,128)S(1)}, f32[7,16,32,128]{3,2,1,0:T(8,128)}, u32[]{:S(2)}) copy-start(f32[7,16,32,128]{3,2,1,0:T(8,128)} %copy-done.4) | copy-start | bytes 5505028
  81.1 1.8 %copy-start.9 = (f32[3,8,2,32,128]{4,3,2,1,0:T(8,128)S(1)}, f32[3,8,2,32,128]{4,3,2,1,0:T(8,128)}, u32[]{:S(2)}) copy-start(f32[3,8,2,32,128]{4,3,2,1,0:T(8,128)} %fusion.177) | copy-start | bytes 2359300
  81.2 1.8 %copy-start.11 = (f32[16,32,128]{2,1,0:T(8,128)S(1)}, f32[16,32,128]{2,1,0:T(8,128)}, u32[]{:S(2)}) copy-start(f32[16,32,128]{2,1,0:T(8,128)} %get-tuple-element.82) | copy-start | bytes 786436
  81.2 1.9 %copy-start.12 = (f32[16,32,128]{2,1,0:T(8,128)S(1)}, f32[16,32,128]{2,1,0:T(8,128)}, u32[]{:S(2)}) copy-start(f32[16,32,128]{2,1,0:T(8,128)} %fusion) | copy-start | bytes 786436
  83.6 6.3 %collective-permute-start.9 = (f32[4,2,128]{2,1,0:T(2,128)S(1)}, f32[4,2,128]{2,1,0:T(2,128)S(1)}, u32[]{:S(2)}, u32[]{:S(2)}) collective-permute-start(f32[4,2,128]{2,1,0:T(2,128)S(1)} %bitcast.374), channel_id=1, source_target_pairs={{0,2},{2,0},{4,6},{6,4},{1,3},{3,1},{5,7},{7,5},{8,10},{10,8},{12,... | collective-permute-start | bytes 12296 | tf_op jit(solution)/shard_map/ppermute | solution.py:42
  89.9 4.1 %collective-permute-start.10 = (f32[4,1,128]{2,0,1:T(4,128)S(1)}, f32[4,1,128]{2,0,1:T(4,128)S(1)}, u32[]{:S(2)}, u32[]{:S(2)}) collective-permute-start(f32[4,1,128]{2,0,1:T(4,128)S(1)} %bitcast.375), channel_id=1, source_target_pairs={{0,4},{4,0},{2,6},{6,2},{1,5},{5,1},{3,7},{7,3},{8,12},{12,8},{10,... | collective-permute-start | bytes 6152 | tf_op jit(solution)/shard_map/ppermute | solution.py:42

commit v24 on v23

--- a/solution.py
+++ b/solution.py
@@ -235,7 +235,16 @@
             starts = jnp.where(light_idx == section_num, section_starts, starts)
         if section_num + 1 < n_light:
             incoming = lax.ppermute(outgoing, "light", [(section_num, section_num + 1)])
-    padded = padded_2(density_side, (("light", 0),), 2)
+    odd = light_idx % 2 == 1
+    first_rows = density_side[:2]
+    last_rows = density_side[brick_l - 2 :]
+    pairs_a = [(i, i ^ 1) for i in range(n_light) if i ^ 1 < n_light]
+    pairs_b = [(i, i + 1) for i in range(1, n_light - 1, 2)] + [(i + 1, i) for i in range(1, n_light - 1, 2)]
+    got_a = lax.ppermute(jnp.where(odd, first_rows, last_rows), "light", pairs_a)
+    got_b = lax.ppermute(jnp.where(odd, last_rows, first_rows), "light", pairs_b)
+    padded = jnp.concatenate(
+        [jnp.where(odd, got_a, got_b), density_side, jnp.where(odd, got_b, got_a)], axis=0
+    )
     inside = (
         rim_mask(light_idx, n_light, brick_l, 1)[:, None, None]
         * rim_mask(across_idx, n_across, brick_a, 1)[None, :, None]

time: 96.8 us -> 93.8 us (0.969)
  starting transfers between devices: 22.3 us -> 18.9 us
  waiting for transfers between devices: 15.2 us -> 16.5 us
    ppermute x2, starting transfers between devices: 6.01 us -> 2.6 us  [the longest x1 2.53 us: shards(): lax.ppermute(jnp.where(odd, last_rows, first_rows), 'light', pairs_b)]
    select_n x0 -> x2, other arithmetic: none -> 1.81 us  [the longest x1 0.91 us: shards(): jnp.where(odd, last_rows, first_rows)]
    ppermute x3, waiting for transfers between devices: 7.37 us -> 8.69 us  [shards(): incoming = lax.ppermute(outgoing, 'light', [(section_num, section_num + 1)])]
  transfers between devices with their start and end apart: 11 -> 11, of which waited for: 6 -> 6; matrix products, arithmetic and copies ran while one was open for 27% -> 27% of each run, Pallas kernels for 9% -> 10%
where the time goes in v24:
time: 93.8 us; the launch traced here: 91.9 us
  other arithmetic  31.7 us (34%)
  starting transfers between devices  18.9 us (20%)
  waiting for transfers between devices  16.5 us (18%)
  local copies, waits for them, and re-layouts  14.3 us (15%)
  Pallas kernels  8.86 us (9%)
  matrix products  1 us (1%)
    mul x31, other arithmetic, propagate(): current = current * fade_here  11.7 us
    pallas_call x1, Pallas kernels, fade_rim_of(): pl.pallas_call(kernel, out_shape=jax.ShapeDtypeStruct((colours, SLABS, ri...  8.86 us
    ppermute x3, waiting for transfers between devices, shards(): incoming = lax.ppermute(outgoing, 'light', [(section_num, section_num + 1)])  8.69 us
    ppermute x2, starting transfers between devices, from_partner(): return lax.ppermute(block, axis, route)  7.96 us
    unnamed x68, local copies, waits for them, and re-layouts  4.74 us
    concatenate x2, other arithmetic, halo(): block = jnp.concatenate(lows + [block] + highs, axis=dim)  3.99 us
    ppermute x1, waiting for transfers between devices, halo(): lax.ppermute(send[half:], axis, [(0, 1), (1, 0)])  3.83 us
    ppermute x3, starting transfers between devices, shards(): incoming = lax.ppermute(outgoing, 'light', [(section_num, section_num + 1)])  3.49 us
  transfers between devices with their start and end apart: 11, of which 6 were waited for; matrix products, arithmetic and copies ran while one was open for 27% of the time, Pallas kernels for 10%

profile of v24, /device:TPU:16, one launch (start us, length us, event | category | flops | bytes accessed | tf_op | source)
XLA Modules:
  0.0 91.9 jit_solution(5135273142291989074)
XLA Ops:
  0.0 1.0 %convert_element_type.39 = f32[16,32,128]{2,1,0:T(8,128)S(1)} convert(s32[16,32,128]{2,1,0:T(8,128)} %param.7) | non-fusion elementwise | flops 65536 | bytes 524288 | tf_op jit(solution)/shard_map/convert_element_type | solution.py:206
  1.1 1.1 %pad_maximum_fusion.6 = f32[17,32,128]{2,1,0:T(8,128)S(1)} fusion(f32[16,32,128]{2,1,0:T(8,128)S(1)} %convert_element_type.39, f32[16,32,128]{2,1,0:T(8,128)} %param.6), kind=kLoop, calls=%fused_computation.48 | loop fusion | flops 69632 | bytes 802816 | tf_op jit(solution)/shard_map/concatenate | solution.py:206
  2.1 1.6 %collective-permute-start = (f32[17,32,128]{2,1,0:T(8,128)S(1)}, f32[17,32,128]{2,1,0:T(8,128)S(1)}, u32[]{:S(2)}, u32[]{:S(2)}) collective-permute-start(f32[17,32,128]{2,1,0:T(8,128)S(1)} %pad_maximum_fusion.6), channel_id=1, source_target_pairs={{0,1},{1,0},{2,3},{3,2},{4,5},{5,4},{6,7},{7,6},{8,9},{9,8},{10,11... | collective-permute-start | bytes 835592 | tf_op jit(solution)/shard_map/ppermute | solution.py:90
  3.7 0.8 pad_maximum_fusion.5
  4.5 0.6 collective-permute-start.1
  5.1 0.6 constant_dynamic-update-slice_fusion.33
  5.7 0.6 broadcast_compare_fusion.14
  6.4 0.4 slice_reduce_fusion.15
  6.9 2.6 %select_select_fusion = f32[7,16,32,128]{3,2,1,0:T(8,128)S(1)} fusion(f32[7]{0:T(128)S(1)} %get-tuple-element.6, f32[7]{0:T(128)S(1)} %get-tuple-element.7, f32[7]{0:T(128)S(1)} %get-tuple-element.8, f32[7]{0:T(128)S(1)} %get-tuple-element.9, f32[7]{0:T(128)S(1)} %get-tuple-element.10, f32[7]{0:T(128)S(1)} %get-tuple-element.11, f32[7]{0:T(128)S(1)} %get-tuple-element.12, ...), kind=kLoop, calls=%fused_computation.1 | loop fusion | flops 6881280 | bytes 2818496 | tf_op jit(solution)/shard_map/jit(_where)/select_n | solution.py:216
  9.5 1.1 %slice_multiply_fusion = f32[3,16,32,128]{3,2,1,0:T(8,128)} fusion(f32[7,16,32,128]{3,2,1,0:T(8,128)S(1)} %select_select_fusion, f32[16,32,128]{2,1,0:T(8,128)S(1)} %copy-done.2), kind=kLoop, calls=%fused_computation.8 | loop fusion | flops 196608 | bytes 1835008 | tf_op jit(solution)/shard_map/mul | solution.py:219
  10.5 0.8 fusion.143
  11.3 1.0 %fusion = f32[16,32,128]{2,1,0:T(8,128)} fusion(f32[16,32,128]{2,1,0:T(8,128)S(1)} %copy-done.2, f32[7,16,32,128]{3,2,1,0:T(8,128)S(1)} %select_select_fusion), kind=kOutput, calls=%fused_computation.4 | convolution fusion | flops 100876288 | bytes 786432 | tf_op jit(solution)/shard_map/dot_general | solution.py:260
  12.3 0.7 broadcast_multiply_fusion.mask_ref
  13.1 3.8 %collective-permute-done.1 = f32[18,32,128]{2,1,0:T(8,128)S(1)} collective-permute-done((f32[18,32,128]{2,1,0:T(8,128)S(1)}, f32[18,32,128]{2,1,0:T(8,128)S(1)}, u32[]{:S(2)}, u32[]{:S(2)}) %collective-permute-start.1) | collective-permute-done | bytes 294944 | tf_op jit(solution)/shard_map/ppermute | solution.py:91
  17.2 0.6 fusion.172
  18.1 1.3 %copy.123 = f32[35,96,32]{1,2,0:T(8,128)} copy(f32[35,96,32]{2,1,0:T(8,128)S(1)} %get-tuple-element.83) | data formatting | bytes 860160 | tf_op jit(solution)/shard_map/slice | solution.py:104
  19.4 1.4 %collective-permute-start.2 = (f32[35,96,32]{1,2,0:T(8,128)}, f32[35,96,32]{1,2,0:T(8,128)S(1)}, u32[]{:S(2)}, u32[]{:S(2)}) collective-permute-start(f32[35,96,32]{1,2,0:T(8,128)} %copy.123), channel_id=1, source_target_pairs={{0,2},{2,4},{4,6},{1,3},{3,5},{5,7},{8,10},{10,12},{12,14},{9,11},... | collective-permute-start | bytes 1290248 | tf_op jit(solution)/shard_map/ppermute | solution.py:105
  20.9 1.3 %copy.124 = f32[35,96,32]{1,2,0:T(8,128)} copy(f32[35,96,32]{2,1,0:T(8,128)S(1)} %get-tuple-element.84) | data formatting | bytes 860160 | tf_op jit(solution)/shard_map/slice | solution.py:106
  22.2 1.3 %collective-permute-start.3 = (f32[35,96,32]{1,2,0:T(8,128)}, f32[35,96,32]{1,2,0:T(8,128)S(1)}, u32[]{:S(2)}, u32[]{:S(2)}) collective-permute-start(f32[35,96,32]{1,2,0:T(8,128)} %copy.124), channel_id=1, source_target_pairs={{2,0},{4,2},{6,4},{3,1},{5,3},{7,5},{10,8},{12,10},{14,12},{11,9},... | collective-permute-start | bytes 1290248 | tf_op jit(solution)/shard_map/ppermute | solution.py:106
  23.6 0.9 %fusion.176 = f32[3,8,2,32,128]{4,3,2,1,0:T(8,128)} fusion(f32[3,8,2,32,128]{4,3,2,1,0:T(8,128)S(1)} %bitcast.367), kind=kOutput, calls=%fused_computation.432 | output fusion | flops 196608 | bytes 1572864 | tf_op jit(solution)/shard_map/jit(cumsum)/reduce_window_sum | solution.py:221
  24.6 1.8 %copy.125 = f32[35,96,32]{2,1,0:T(8,128)} copy(f32[35,96,32]{1,2,0:T(8,128)S(1)} %collective-permute-done.2) | data formatting | bytes 860160 | tf_op jit(solution)/shard_map/ppermute | solution.py:105
  26.4 1.6 %collective-permute-done.3 = f32[35,96,32]{1,2,0:T(8,128)S(1)} collective-permute-done((f32[35,96,32]{1,2,0:T(8,128)}, f32[35,96,32]{1,2,0:T(8,128)S(1)}, u32[]{:S(2)}, u32[]{:S(2)}) %collective-permute-start.3) | collective-permute-done | bytes 430112 | tf_op jit(solution)/shard_map/ppermute | solution.py:106
  28.0 1.8 %copy.126 = f32[35,96,32]{2,1,0:T(8,128)} copy(f32[35,96,32]{1,2,0:T(8,128)S(1)} %collective-permute-done.3) | data formatting | bytes 860160 | tf_op jit(solution)/shard_map/ppermute | solution.py:106
  29.7 3.9 %pad_maximum_fusion.stack_ref = f32[35,96,192]{2,1,0:T(8,128)S(1)} fusion(f32[35,96,32]{2,1,0:T(8,128)} %copy.126, f32[35,32,128]{2,1,0:T(8,128)} %copy-done.8, f32[3,32,128]{2,1,0:T(8,128)S(1)} %copy-done.14, f32[16,32,128]{2,1,0:T(8,128)} %copy-done.6, f32[16,32,128]{2,1,0:T(8,128)} %param.6, f32[35,32,128]{2,1,0:T(8,128)} %copy-done.7, f32[35,96,32]{2,1,0:T(8,128)} %copy.125), kind=kLoop, calls=%fused_computation | loop fusion | flops 3870720 | bytes 5160960 | tf_op jit(solution)/shard_map/concatenate | solution.py:107
  33.6 0.9 slice_select_fusion.1
  34.5 2.5 %collective-permute-start.4 = (f32[2,36,132]{2,1,0:T(8,128)}, f32[2,36,132]{2,1,0:T(8,128)S(1)}, u32[]{:S(2)}, u32[]{:S(2)}) collective-permute-start(f32[2,36,132]{2,1,0:T(8,128)} %get-tuple-element.79), channel_id=1, source_target_pairs={{8,16},{16,8},{9,17},{17,9},{10,18},{18,10},{11,19},{19,11},{12,20... | collective-permute-start | bytes 114056 | tf_op jit(solution)/shard_map/ppermute | solution.py:244
  37.2 8.9 %shard_map.64 = f32[3,8,96,192]{3,2,1,0:T(8,128)} custom-call(f32[3,16]{1,0:T(4,128)} %table_ref.1, f32[35,96,192]{2,1,0:T(8,128)} %copy-done.1, f32[96,192]{1,0:T(8,128)} %broadcast_multiply_fusion.mask_ref), custom_call_target="tpu_custom_call" | custom-call | tf_op jit(solution)/shard_map/pallas_call | solution.py:180
  46.0 1.2 %fusion.17 = f32[3,96,192]{2,1,0:T(8,128)S(1)} fusion(f32[3,8,96,192]{3,2,1,0:T(8,128)} %shard_map.64, f32[35,96,192]{2,1,0:T(8,128)} %copy-done.1), kind=kLoop, calls=%fused_computation.44 | loop fusion | flops 55296 | bytes 663552 | tf_op jit(solution)/shard_map/mul | solution.py:136
  47.3 1.4 %fusion.13 = (f32[3,94,190]{2,1,0:T(8,128)S(1)}, f32[3,94,190]{2,1,0:T(8,128)S(1)}) fusion(f32[3,8,96,192]{3,2,1,0:T(8,128)} %shard_map.64, f32[3,96,192]{2,1,0:T(8,128)S(1)} %fusion.17), kind=kLoop, calls=%fused_computation.36 | loop fusion | flops 428640 | bytes 1714560 | tf_op jit(solution)/shard_map/mul | solution.py:136
  48.7 0.4 fusion.9
  49.1 0.4 fusion.5
  49.6 0.4 fusion.30
  50.0 0.4 fusion.26
  50.4 0.4 fusion.22
  50.9 0.4 fusion.18
  51.3 0.3 fusion.56
  51.6 0.7 collective-permute-start.6
  52.9 1.4 %slice.1140 = f32[16,36,132]{2,1,0:T(8,128)S(1)} slice(f32[35,96,192]{2,1,0:T(8,128)} %copy-done.1), slice={[0:16], [30:66], [30:162]} | slice | bytes 608256 | tf_op jit(solution)/shard_map/slice | solution.py:210
  54.3 0.9 broadcast_select_fusion.3
  55.3 1.1 %multiply_multiply_fusion.1 = (f32[18,34,130]{2,1,0:T(8,128)S(1)}, f32[18,34,130]{2,1,0:T(8,128)S(1)}) fusion(f32[16,36,132]{2,1,0:T(8,128)S(1)} %slice.1140, f32[2,36,132]{2,1,0:T(8,128)S(1)} %get-tuple-element.105, f32[2,36,132]{2,1,0:T(8,128)S(1)} %get-tuple-element.104, f32[130]{0:T(256)S(1)} %and_convert_fusion.2, ...), kind=kLoop, calls=%fused_computation.6 | loop fusion | flops 1750320 | bytes 2292568 | tf_op jit(solution)/shard_map/mul | solution.py:63
  56.4 0.9 fusion.37
  57.5 0.4 fusion.49
  57.8 0.4 fusion.45
  58.2 0.4 fusion.41
  58.6 0.4 fusion.69
  59.0 0.4 fusion.65
  59.3 0.4 fusion.61
  59.7 0.4 fusion.57
  60.3 1.3 %collective-permute-start.7 = (f32[3,64,160]{2,1,0:T(8,128)S(1)}, f32[3,64,160]{2,1,0:T(8,128)S(1)}, u32[]{:S(2)}, u32[]{:S(2)}) collective-permute-start(f32[3,64,160]{2,1,0:T(8,128)S(1)} %fusion.88), channel_id=1, source_target_pairs={{8,16},{9,17},{10,18},{11,19},{12,20},{13,21},{14,22},{15,23}} | collective-permute-start | bytes 368648 | tf_op jit(solution)/shard_map/ppermute | solution.py:237
  62.3 6.9 %collective-permute-done.7 = f32[3,64,160]{2,1,0:T(8,128)S(1)} collective-permute-done((f32[3,64,160]{2,1,0:T(8,128)S(1)}, f32[3,64,160]{2,1,0:T(8,128)S(1)}, u32[]{:S(2)}, u32[]{:S(2)}) %collective-permute-start.7) | collective-permute-done | bytes 122912 | tf_op jit(solution)/shard_map/ppermute | solution.py:237
  69.3 0.3 fusion.81
  69.7 0.3 fusion.77
  70.0 0.3 fusion.73
  70.6 0.3 fusion.97
  71.7 1.5 %collective-permute-start.8 = (f32[3,48,144]{2,1,0:T(8,128)S(1)}, f32[3,48,144]{2,1,0:T(8,128)S(1)}, u32[]{:S(2)}, u32[]{:S(2)}) collective-permute-start(f32[3,48,144]{2,1,0:T(8,128)S(1)} %fusion.120), channel_id=1, source_target_pairs={{16,24},{17,25},{18,26},{19,27},{20,28},{21,29},{22,30},{23,31}} | collective-permute-start | bytes 248840 | tf_op jit(solution)/shard_map/ppermute | solution.py:237
  73.9 1.8 %collective-permute-done.8 = f32[3,48,144]{2,1,0:T(8,128)S(1)} collective-permute-done((f32[3,48,144]{2,1,0:T(8,128)S(1)}, f32[3,48,144]{2,1,0:T(8,128)S(1)}, u32[]{:S(2)}, u32[]{:S(2)}) %collective-permute-start.8) | collective-permute-done | bytes 82976 | tf_op jit(solution)/shard_map/ppermute | solution.py:237
  78.5 0.6 copy-done.3
  79.1 0.6 copy-done.5
  80.1 0.5 fusion.3
  80.7 4.8 %collective-permute-start.9 = (f32[4,2,128]{2,1,0:T(2,128)S(1)}, f32[4,2,128]{2,1,0:T(2,128)S(1)}, u32[]{:S(2)}, u32[]{:S(2)}) collective-permute-start(f32[4,2,128]{2,1,0:T(2,128)S(1)} %bitcast.374), channel_id=1, source_target_pairs={{0,2},{2,0},{4,6},{6,4},{1,3},{3,1},{5,7},{7,5},{8,10},{10,8},{12,... | collective-permute-start | bytes 12296 | tf_op jit(solution)/shard_map/ppermute | solution.py:42
  85.5 0.8 collective-permute-done.9
  86.4 3.1 %collective-permute-start.10 = (f32[4,1,128]{2,0,1:T(4,128)S(1)}, f32[4,1,128]{2,0,1:T(4,128)S(1)}, u32[]{:S(2)}, u32[]{:S(2)}) collective-permute-start(f32[4,1,128]{2,0,1:T(4,128)S(1)} %bitcast.375), channel_id=1, source_target_pairs={{0,4},{4,0},{2,6},{6,2},{1,5},{5,1},{3,7},{7,3},{8,12},{12,8},{10,... | collective-permute-start | bytes 6152 | tf_op jit(solution)/shard_map/ppermute | solution.py:42
  89.5 1.6 %collective-permute-done.10 = f32[4,1,128]{2,0,1:T(4,128)S(1)} collective-permute-done((f32[4,1,128]{2,0,1:T(4,128)S(1)}, f32[4,1,128]{2,0,1:T(4,128)S(1)}, u32[]{:S(2)}, u32[]{:S(2)}) %collective-permute-start.10) | collective-permute-done | bytes 2080 | tf_op jit(solution)/shard_map/ppermute | solution.py:42
  91.3 0.6 pad_maximum_fusion.7
  (122 shorter events, 7.9 us)
Async XLA Ops:
  0.0 5.7 %copy-start.13 = (s32[16,32,128]{2,1,0:T(8,128)S(1)}, s32[16,32,128]{2,1,0:T(8,128)}, u32[]{:S(2)}) copy-start(s32[16,32,128]{2,1,0:T(8,128)} %param.7) | copy-start | bytes 786436
  0.0 5.1 %copy-start.14 = (f32[3,32,128]{2,1,0:T(8,128)S(1)}, f32[3,32,128]{2,1,0:T(8,128)}, u32[]{:S(2)}) copy-start(f32[3,32,128]{2,1,0:T(8,128)} %param.8) | copy-start | bytes 147460
  0.0 6.4 %copy-start.16 = (f32[3,16]{1,0:T(4,128)S(1)}, f32[3,16]{1,0:T(4,128)}, u32[]{:S(2)}) copy-start(f32[3,16]{1,0:T(4,128)} %table_ref.1) | copy-start | bytes 580
  0.0 6.4 %copy-start.18 = (f32[16]{0:T(128)S(1)}, f32[16]{0:T(128)}, u32[]{:S(2)}) copy-start(f32[16]{0:T(128)} %param.9) | copy-start | bytes 196
  0.0 6.4 %copy-start.17 = (f32[3,16]{1,0:T(4,128)S(1)}, f32[3,16]{1,0:T(4,128)}, u32[]{:S(2)}) copy-start(f32[3,16]{1,0:T(4,128)} %param.11) | copy-start | bytes 580
  1.0 16.1 %copy-start.6 = (f32[16,32,128]{2,1,0:T(8,128)}, f32[16,32,128]{2,1,0:T(8,128)S(1)}, u32[]{:S(2)}) copy-start(f32[16,32,128]{2,1,0:T(8,128)S(1)} %convert_element_type.39) | copy-start | bytes 786436
  2.1 10.9 %collective-permute-start = (f32[17,32,128]{2,1,0:T(8,128)S(1)}, f32[17,32,128]{2,1,0:T(8,128)S(1)}, u32[]{:S(2)}, u32[]{:S(2)}) collective-permute-start(f32[17,32,128]{2,1,0:T(8,128)S(1)} %pad_maximum_fusion.6), channel_id=1, source_target_pairs={{0,1},{1,0},{2,3},{3,2},{4,5},{5,4},{6,7},{7,6},{8,9},{9,8},{10,11... | collective-permute-start | bytes 835592 | tf_op jit(solution)/shard_map/ppermute | solution.py:90
  4.5 12.4 %collective-permute-start.1 = (f32[18,32,128]{2,1,0:T(8,128)S(1)}, f32[18,32,128]{2,1,0:T(8,128)S(1)}, u32[]{:S(2)}, u32[]{:S(2)}) collective-permute-start(f32[18,32,128]{2,1,0:T(8,128)S(1)} %pad_maximum_fusion.5), channel_id=1, source_target_pairs={{0,1},{1,0},{2,3},{3,2},{4,5},{5,4},{6,7},{7,6},{8,9},{9,8},{10,11... | collective-permute-start | bytes 884744 | tf_op jit(solution)/shard_map/ppermute | solution.py:91
  5.7 3.7 %copy-start.2 = (f32[16,32,128]{2,1,0:T(8,128)S(1)}, f32[16,32,128]{2,1,0:T(8,128)}, u32[]{:S(2)}) copy-start(f32[16,32,128]{2,1,0:T(8,128)} %param.6) | copy-start | bytes 786436
  9.4 1.8 %copy-start.4 = (f32[7,16,32,128]{3,2,1,0:T(8,128)}, f32[7,16,32,128]{3,2,1,0:T(8,128)S(1)}, u32[]{:S(2)}) copy-start(f32[7,16,32,128]{3,2,1,0:T(8,128)S(1)} %select_select_fusion) | copy-start | bytes 5505028
  17.1 0.8 copy-start.7
  17.1 1.0 %copy-start.8 = (f32[35,32,128]{2,1,0:T(8,128)}, f32[35,32,128]{2,1,0:T(8,128)S(1)}, u32[]{:S(2)}) copy-start(f32[35,32,128]{2,1,0:T(8,128)S(1)} %get-tuple-element.88) | copy-start | bytes 1720324
  19.4 4.2 %copy-start.10 = (f32[3,16,32,128]{3,2,1,0:T(8,128)S(1)}, f32[3,16,32,128]{3,2,1,0:T(8,128)}, u32[]{:S(2)}) copy-start(f32[3,16,32,128]{3,2,1,0:T(8,128)} %slice_multiply_fusion) | copy-start | bytes 2359300
  19.4 5.2 %collective-permute-start.2 = (f32[35,96,32]{1,2,0:T(8,128)}, f32[35,96,32]{1,2,0:T(8,128)S(1)}, u32[]{:S(2)}, u32[]{:S(2)}) collective-permute-start(f32[35,96,32]{1,2,0:T(8,128)} %copy.123), channel_id=1, source_target_pairs={{0,2},{2,4},{4,6},{1,3},{3,5},{5,7},{8,10},{10,12},{12,14},{9,11},... | collective-permute-start | bytes 1290248 | tf_op jit(solution)/shard_map/ppermute | solution.py:105
  22.2 5.8 %collective-permute-start.3 = (f32[35,96,32]{1,2,0:T(8,128)}, f32[35,96,32]{1,2,0:T(8,128)S(1)}, u32[]{:S(2)}, u32[]{:S(2)}) collective-permute-start(f32[35,96,32]{1,2,0:T(8,128)} %copy.124), channel_id=1, source_target_pairs={{2,0},{4,2},{6,4},{3,1},{5,3},{7,5},{10,8},{12,10},{14,12},{11,9},... | collective-permute-start | bytes 1290248 | tf_op jit(solution)/shard_map/ppermute | solution.py:106
  33.6 3.5 %copy-start.1 = (f32[35,96,192]{2,1,0:T(8,128)}, f32[35,96,192]{2,1,0:T(8,128)S(1)}, u32[]{:S(2)}) copy-start(f32[35,96,192]{2,1,0:T(8,128)S(1)} %pad_maximum_fusion.stack_ref) | copy-start | bytes 7741444
  34.5 19.7 %collective-permute-start.4 = (f32[2,36,132]{2,1,0:T(8,128)}, f32[2,36,132]{2,1,0:T(8,128)S(1)}, u32[]{:S(2)}, u32[]{:S(2)}) collective-permute-start(f32[2,36,132]{2,1,0:T(8,128)} %get-tuple-element.79), channel_id=1, source_target_pairs={{8,16},{16,8},{9,17},{17,9},{10,18},{18,10},{11,19},{19,11},{12,20... | collective-permute-start | bytes 114056 | tf_op jit(solution)/shard_map/ppermute | solution.py:244
  37.1 17.2 %collective-permute-start.5 = (f32[2,36,132]{2,1,0:T(8,128)}, f32[2,36,132]{2,1,0:T(8,128)}, u32[]{:S(2)}, u32[]{:S(2)}) collective-permute-start(f32[2,36,132]{2,1,0:T(8,128)} %get-tuple-element.80), channel_id=1, source_target_pairs={{0,8},{8,0},{16,24},{24,16},{1,9},{9,1},{17,25},{25,17},{2,10},{10... | collective-permute-start | bytes 114056 | tf_op jit(solution)/shard_map/ppermute | solution.py:243
  46.0 2.7 %copy-start = (f32[3,8,96,192]{3,2,1,0:T(8,128)S(1)}, f32[3,8,96,192]{3,2,1,0:T(8,128)}, u32[]{:S(2)}) copy-start(f32[3,8,96,192]{3,2,1,0:T(8,128)} %shard_map.64) | copy-start | bytes 5308420
  50.8 1.4 %copy-start.15 = (f32[3,8,32,128]{3,2,0,1:T(8,128)S(1)}, f32[3,8,32,128]{3,2,0,1:T(8,128)}, u32[]{:S(2)}) copy-start(f32[3,8,32,128]{3,2,0,1:T(8,128)} %constant_dynamic-update-slice_fusion.33) | copy-start | bytes 1179652
  51.6 5.7 %collective-permute-start.6 = (f32[3,80,176]{2,1,0:T(8,128)S(1)}, f32[3,80,176]{2,1,0:T(8,128)S(1)}, u32[]{:S(2)}, u32[]{:S(2)}) collective-permute-start(f32[3,80,176]{2,1,0:T(8,128)S(1)} %fusion.56), channel_id=1, source_target_pairs={{0,8},{1,9},{2,10},{3,11},{4,12},{5,13},{6,14},{7,15}} | collective-permute-start | bytes 506888 | tf_op jit(solution)/shard_map/ppermute | solution.py:237
  60.3 8.9 %collective-permute-start.7 = (f32[3,64,160]{2,1,0:T(8,128)S(1)}, f32[3,64,160]{2,1,0:T(8,128)S(1)}, u32[]{:S(2)}, u32[]{:S(2)}) collective-permute-start(f32[3,64,160]{2,1,0:T(8,128)S(1)} %fusion.88), channel_id=1, source_target_pairs={{8,16},{9,17},{10,18},{11,19},{12,20},{13,21},{14,22},{15,23}} | collective-permute-start | bytes 368648 | tf_op jit(solution)/shard_map/ppermute | solution.py:237
  71.7 4.0 %collective-permute-start.8 = (f32[3,48,144]{2,1,0:T(8,128)S(1)}, f32[3,48,144]{2,1,0:T(8,128)S(1)}, u32[]{:S(2)}, u32[]{:S(2)}) collective-permute-start(f32[3,48,144]{2,1,0:T(8,128)S(1)} %fusion.120), channel_id=1, source_target_pairs={{16,24},{17,25},{18,26},{19,27},{20,28},{21,29},{22,30},{23,31}} | collective-permute-start | bytes 248840 | tf_op jit(solution)/shard_map/ppermute | solution.py:237
  78.2 1.0 %copy-start.3 = (f32[16,32,128]{2,1,0:T(8,128)S(1)}, f32[16,32,128]{2,1,0:T(8,128)}, u32[]{:S(2)}) copy-start(f32[16,32,128]{2,1,0:T(8,128)} %param.6) | copy-start | bytes 786436
  78.2 1.6 %copy-start.5 = (f32[7,16,32,128]{3,2,1,0:T(8,128)S(1)}, f32[7,16,32,128]{3,2,1,0:T(8,128)}, u32[]{:S(2)}) copy-start(f32[7,16,32,128]{3,2,1,0:T(8,128)} %copy-done.4) | copy-start | bytes 5505028
  78.2 1.8 %copy-start.9 = (f32[3,8,2,32,128]{4,3,2,1,0:T(8,128)S(1)}, f32[3,8,2,32,128]{4,3,2,1,0:T(8,128)}, u32[]{:S(2)}) copy-start(f32[3,8,2,32,128]{4,3,2,1,0:T(8,128)} %fusion.176) | copy-start | bytes 2359300
  78.2 1.8 %copy-start.11 = (f32[16,32,128]{2,1,0:T(8,128)S(1)}, f32[16,32,128]{2,1,0:T(8,128)}, u32[]{:S(2)}) copy-start(f32[16,32,128]{2,1,0:T(8,128)} %get-tuple-element.82) | copy-start | bytes 786436
  78.2 1.9 %copy-start.12 = (f32[16,32,128]{2,1,0:T(8,128)S(1)}, f32[16,32,128]{2,1,0:T(8,128)}, u32[]{:S(2)}) copy-start(f32[16,32,128]{2,1,0:T(8,128)} %fusion) | copy-start | bytes 786436
  80.7 5.7 %collective-permute-start.9 = (f32[4,2,128]{2,1,0:T(2,128)S(1)}, f32[4,2,128]{2,1,0:T(2,128)S(1)}, u32[]{:S(2)}, u32[]{:S(2)}) collective-permute-start(f32[4,2,128]{2,1,0:T(2,128)S(1)} %bitcast.374), channel_id=1, source_target_pairs={{0,2},{2,0},{4,6},{6,4},{1,3},{3,1},{5,7},{7,5},{8,10},{10,8},{12,... | collective-permute-start | bytes 12296 | tf_op jit(solution)/shard_map/ppermute | solution.py:42
  86.4 4.7 %collective-permute-start.10 = (f32[4,1,128]{2,0,1:T(4,128)S(1)}, f32[4,1,128]{2,0,1:T(4,128)S(1)}, u32[]{:S(2)}, u32[]{:S(2)}) collective-permute-start(f32[4,1,128]{2,0,1:T(4,128)S(1)} %bitcast.375), channel_id=1, source_target_pairs={{0,4},{4,0},{2,6},{6,2},{1,5},{5,1},{3,7},{7,3},{8,12},{12,8},{10,... | collective-permute-start | bytes 6152 | tf_op jit(solution)/shard_map/ppermute | solution.py:42
